TPU v7x, 32 devices: a whole 2x2x4 slice. The times are simulated.
32 devices in a mesh: dp: 8 (over y, x, core), fsdp: 4 (over z).
Axes of the slice: x: 2, y: 2, z: 4, core: 2. Of those that a mesh axis runs over, the one named last changes fastest.
Arguments:
- tokens: bfloat16 [18432, 768], P(('dp', 'fsdp')), may hold values from -6 to 6
- image_lengths: int32 [32, 9], P(('dp', 'fsdp')), may hold values from 0 to 576, as said below
- w_qkv: bfloat16 [768, 2304], P('fsdp'), may hold values from -0.21875 to 0.21875
- w_out: bfloat16 [768, 768], P('fsdp'), may hold values from -0.875 to 0.875
- w_up: bfloat16 [768, 3072], P('fsdp'), may hold values from -0.21875 to 0.21875
- w_down: bfloat16 [3072, 768], P('fsdp'), may hold values from -0.109375 to 0.109375
- ln_gain: bfloat16 [2, 768], P(None, 'fsdp'), may hold values from 0.25 to 1.75
- ln_bias: bfloat16 [2, 768], P(None, 'fsdp'), may hold values from -3 to 3
- qk_gain: bfloat16 [2, 768], P(None, 'fsdp'), may hold values from 0.25 to 1.75
- cotangent: bfloat16 [18432, 768], P(('dp', 'fsdp')), may hold values from -6 to 6
Outputs:
- layer_out: bfloat16 [18432, 768], P(('dp', 'fsdp'))
- grad_tokens: bfloat16 [18432, 768], P(('dp', 'fsdp'))
- grad_w_qkv: float32 [768, 2304], P('fsdp')
- grad_w_out: float32 [768, 768], P('fsdp')
- grad_w_up: float32 [768, 3072], P('fsdp')
- grad_w_down: float32 [3072, 768], P('fsdp')
- grad_ln_gain: float32 [2, 768], P(None, 'fsdp')
- grad_ln_bias: float32 [2, 768], P(None, 'fsdp')
- grad_qk_gain: float32 [2, 768], P(None, 'fsdp')
Inputs may be any that keep to these rules, and one draw needn't show every extreme that they name: Each row of image_lengths is either 1 large images of 576 patches, or between 1 and 9 small images of 64 patches; used slots come first, zeros after. Exactly half of the rows hold large images. No image crosses a multiple of 576 rows, and padding lies after the last image.
All inputs are finite; a program needn't handle non-finite values.
Results may differ from a plain program's by a relative error of at most 0.02.
Values may be sent and summed in bfloat16 or wider, within the bound.
No kernel may reach another device: no remote copies, remote signals or barrier semaphores. Data moves between devices by JAX's collectives and lax.ppermute only.
A program may use at most 192 MiB of HBM per device.

v0:
```python
from functools import partial

import jax
import jax.numpy as jnp
from jax import lax
from jax.sharding import PartitionSpec as P

HEADS = 12
HEAD_DIM = 64
PATCH_BIG = 576


epsilon = 1e-06


def layer_norm(v, gain_row, bias_row):
    centre = v - jnp.mean(v, axis=-1, keepdims=True)
    spread = jnp.mean(centre * centre, axis=-1, keepdims=True)
    return centre * lax.rsqrt(spread + epsilon) * gain_row + bias_row


def head_norm(v, gain_row):
    centre = v - jnp.mean(v, axis=-1, keepdims=True)
    spread = jnp.mean(centre * centre, axis=-1, keepdims=True)
    return centre * lax.rsqrt(spread + epsilon) * gain_row


def both_norms(q_in, k_in, q_gain, k_gain):
    return (head_norm(q_in, q_gain), head_norm(k_in, k_gain))


def on_device(
    tokens, image_lengths, w_qkv, w_out, w_up, w_down, ln_gain, ln_bias, qk_gain, cotangent
):
    full_qkv, full_out, full_up, full_down, gain_all, bias_all, qk_all = (
        lax.all_gather(w_qkv, "fsdp", axis=0, tiled=True),
        lax.all_gather(w_out, "fsdp", axis=0, tiled=True),
        lax.all_gather(w_up, "fsdp", axis=0, tiled=True),
        lax.all_gather(w_down, "fsdp", axis=0, tiled=True),
        lax.all_gather(ln_gain, "fsdp", axis=1, tiled=True),
        lax.all_gather(ln_bias, "fsdp", axis=1, tiled=True),
        lax.all_gather(qk_gain, "fsdp", axis=1, tiled=True),
    )
    length = tokens.shape[0]
    model_width = tokens.shape[1]
    blocks = length // PATCH_BIG
    scaling = HEAD_DIM ** (-0.5)
    position = jnp.arange(length, dtype=jnp.int32)
    limits = jnp.cumsum(image_lengths[0])
    segment = jnp.sum((position[:, None] >= limits[None, :]).astype(jnp.int32), axis=1)
    valid_rows = (position < limits[-1]).astype(jnp.float32)[:, None]
    norm_gains = gain_all.astype(jnp.float32)
    biases = bias_all.astype(jnp.float32)
    qk_gains = qk_all.astype(jnp.float32).reshape(2, HEADS, HEAD_DIM)
    inputs = tokens.astype(jnp.float32)
    normed, first_back = jax.vjp(layer_norm, inputs, norm_gains[0], biases[0])
    normed_low = normed.astype(jnp.bfloat16)
    project = jnp.dot(normed_low, full_qkv, preferred_element_type=jnp.float32)
    queries = project[:, :model_width].reshape(length, HEADS, HEAD_DIM)
    keys_raw = project[:, model_width : 2 * model_width].reshape(length, HEADS, HEAD_DIM)
    values_raw = project[:, 2 * model_width :]
    (q_norm, k_norm), norms_back = jax.vjp(both_norms, queries, keys_raw, qk_gains[0], qk_gains[1])
    q_low = q_norm.astype(jnp.bfloat16).reshape(blocks, PATCH_BIG, HEADS, HEAD_DIM)
    k_low = k_norm.astype(jnp.bfloat16).reshape(blocks, PATCH_BIG, HEADS, HEAD_DIM)
    v_low = values_raw.astype(jnp.bfloat16).reshape(blocks, PATCH_BIG, HEADS, HEAD_DIM)
    s_blocks = segment.reshape(blocks, PATCH_BIG)

    def block_scores(q_block, k_block, s_block):
        scores = (
            jnp.einsum("qhd,khd->hqk", q_block, k_block, preferred_element_type=jnp.float32)
            * scaling
        )
        return jnp.where((s_block[:, None] == s_block[None, :])[None], scores, -1e30)

    def attend(members):
        q_block, k_block, v_block, s_block = members
        scores = block_scores(q_block, k_block, s_block)
        row_top = jnp.max(scores, axis=-1, keepdims=True)
        exp_scores = jnp.exp(scores - row_top)
        row_total = jnp.sum(exp_scores, axis=-1, keepdims=True)
        probability = (exp_scores / row_total).astype(jnp.bfloat16)
        mixed_block = jnp.einsum(
            "hqk,khd->qhd", probability, v_block, preferred_element_type=jnp.float32
        )
        return (mixed_block, row_top + jnp.log(row_total))

    mixed_heads, log_total = lax.map(attend, (q_low, k_low, v_low, s_blocks))
    mixed_low = mixed_heads.reshape(length, model_width).astype(jnp.bfloat16)
    residual = inputs + jnp.dot(mixed_low, full_out, preferred_element_type=jnp.float32)
    second, second_back = jax.vjp(layer_norm, residual, norm_gains[1], biases[1])
    second_low = second.astype(jnp.bfloat16)
    up_pre = jnp.dot(second_low, full_up, preferred_element_type=jnp.float32)
    active, gelu_back = jax.vjp(partial(jax.nn.gelu, approximate=False), up_pre)
    active_low = active.astype(jnp.bfloat16)
    output = residual + jnp.dot(active_low, full_down, preferred_element_type=jnp.float32)
    layer_out = (valid_rows * output).astype(jnp.bfloat16)
    back_qkv, back_out, back_up, back_down = (
        lax.all_gather(w_qkv, "fsdp", axis=0, tiled=True),
        lax.all_gather(w_out, "fsdp", axis=0, tiled=True),
        lax.all_gather(w_up, "fsdp", axis=0, tiled=True),
        lax.all_gather(w_down, "fsdp", axis=0, tiled=True),
    )
    upstream = cotangent.astype(jnp.float32) * valid_rows
    up_low = upstream.astype(jnp.bfloat16)
    grad_down = jnp.dot(active_low.T, up_low, preferred_element_type=jnp.float32)
    grad_active = jnp.dot(up_low, back_down.T, preferred_element_type=jnp.float32)
    (grad_pre,) = gelu_back(grad_active)
    pre_low = grad_pre.astype(jnp.bfloat16)
    grad_up = jnp.dot(second_low.T, pre_low, preferred_element_type=jnp.float32)
    grad_second = jnp.dot(pre_low, back_up.T, preferred_element_type=jnp.float32)
    grad_resid, gain_two, bias_two = second_back(grad_second)
    grad_resid = grad_resid + upstream
    resid_low = grad_resid.astype(jnp.bfloat16)
    grad_outw = jnp.dot(mixed_low.T, resid_low, preferred_element_type=jnp.float32)
    grad_mixed = jnp.dot(resid_low, back_out.T, preferred_element_type=jnp.float32)
    grad_mixed = grad_mixed.astype(jnp.bfloat16).reshape(blocks, PATCH_BIG, HEADS, HEAD_DIM)

    def attend_back(members):
        q_block, k_block, v_block, s_block, l_block, d_block = members
        scores = block_scores(q_block, k_block, s_block)
        probability = jnp.exp(scores - l_block)
        prob_low = probability.astype(jnp.bfloat16)
        grad_v = jnp.einsum("hqk,qhd->khd", prob_low, d_block, preferred_element_type=jnp.float32)
        grad_p = jnp.einsum("qhd,khd->hqk", d_block, v_block, preferred_element_type=jnp.float32)
        grad_p = lax.optimization_barrier(grad_p.astype(jnp.bfloat16)).astype(jnp.float32)
        grad_s = probability * (grad_p - jnp.sum(probability * grad_p, axis=-1, keepdims=True))
        s_low = grad_s.astype(jnp.bfloat16)
        grad_q = (
            jnp.einsum("hqk,khd->qhd", s_low, k_block, preferred_element_type=jnp.float32) * scaling
        )
        grad_k = (
            jnp.einsum("hqk,qhd->khd", s_low, q_block, preferred_element_type=jnp.float32) * scaling
        )
        return (grad_q, grad_k, grad_v)

    grad_qn, grad_kn, grad_vn = lax.map(
        attend_back, (q_low, k_low, v_low, s_blocks, log_total, grad_mixed)
    )
    grad_q, grad_k, gain_q, gain_k = norms_back(
        (grad_qn.reshape(length, HEADS, HEAD_DIM), grad_kn.reshape(length, HEADS, HEAD_DIM))
    )
    grad_project = jnp.concatenate(
        [
            grad_q.reshape(length, model_width),
            grad_k.reshape(length, model_width),
            grad_vn.reshape(length, model_width),
        ],
        axis=1,
    ).astype(jnp.bfloat16)
    grad_qkv = jnp.dot(normed_low.T, grad_project, preferred_element_type=jnp.float32)
    grad_normed = jnp.dot(grad_project, back_qkv.T, preferred_element_type=jnp.float32)
    grad_input, gain_one, bias_one = first_back(grad_normed)
    grad_tokens = (grad_input + grad_resid).astype(jnp.bfloat16)
    grad_gain = jnp.stack([gain_one, gain_two])
    grad_bias = jnp.stack([bias_one, bias_two])
    grad_qk = jnp.stack([gain_q.reshape(model_width), gain_k.reshape(model_width)])
    summands = (grad_qkv, grad_outw, grad_up, grad_down, grad_gain, grad_bias, grad_qk)
    pieces = (
        lax.psum_scatter(
            summands[0].astype(jnp.bfloat16), "fsdp", scatter_dimension=0, tiled=True
        ).astype(jnp.float32),
        lax.psum_scatter(
            summands[1].astype(jnp.bfloat16), "fsdp", scatter_dimension=0, tiled=True
        ).astype(jnp.float32),
        lax.psum_scatter(
            summands[2].astype(jnp.bfloat16), "fsdp", scatter_dimension=0, tiled=True
        ).astype(jnp.float32),
        lax.psum_scatter(
            summands[3].astype(jnp.bfloat16), "fsdp", scatter_dimension=0, tiled=True
        ).astype(jnp.float32),
        lax.psum_scatter(
            summands[4].astype(jnp.bfloat16), "fsdp", scatter_dimension=1, tiled=True
        ).astype(jnp.float32),
        lax.psum_scatter(
            summands[5].astype(jnp.bfloat16), "fsdp", scatter_dimension=1, tiled=True
        ).astype(jnp.float32),
        lax.psum_scatter(
            summands[6].astype(jnp.bfloat16), "fsdp", scatter_dimension=1, tiled=True
        ).astype(jnp.float32),
    )
    shares = (
        lax.psum(pieces[0].astype(jnp.bfloat16), "dp").astype(jnp.float32),
        lax.psum(pieces[1].astype(jnp.bfloat16), "dp").astype(jnp.float32),
        lax.psum(pieces[2].astype(jnp.bfloat16), "dp").astype(jnp.float32),
        lax.psum(pieces[3].astype(jnp.bfloat16), "dp").astype(jnp.float32),
        lax.psum(pieces[4].astype(jnp.bfloat16), "dp").astype(jnp.float32),
        lax.psum(pieces[5].astype(jnp.bfloat16), "dp").astype(jnp.float32),
        lax.psum(pieces[6].astype(jnp.bfloat16), "dp").astype(jnp.float32),
    )
    return (
        layer_out,
        grad_tokens,
        shares[0],
        shares[1],
        shares[2],
        shares[3],
        shares[4],
        shares[5],
        shares[6],
    )


def solution(mesh):
    in_specs = (
        P(("dp", "fsdp"), None),
        P(("dp", "fsdp"), None),
        P("fsdp", None),
        P("fsdp", None),
        P("fsdp", None),
        P("fsdp", None),
        P(None, "fsdp"),
        P(None, "fsdp"),
        P(None, "fsdp"),
        P(("dp", "fsdp"), None),
    )
    out_specs = (
        P(("dp", "fsdp"), None),
        P(("dp", "fsdp"), None),
        P("fsdp", None),
        P("fsdp", None),
        P("fsdp", None),
        P("fsdp", None),
        P(None, "fsdp"),
        P(None, "fsdp"),
        P(None, "fsdp"),
    )
    return jax.shard_map(
        on_device, mesh=mesh, in_specs=in_specs, out_specs=out_specs, check_vma=False
    )
```

profile of v0, /device:TPU:8, one launch (start us, length us, event | category | flops | bytes accessed | tf_op | source)
XLA Modules:
  0.0 766.4 jit_solution(16090609015939321576)
XLA Ops:
  11.6 8.2 %all-gather = bf16[4,192,2]{1,2,0:T(2,128)(2,1)S(1)} all-gather(bf16[1,192,2]{1,2,0:T(2,128)(2,1)S(1)} %bitcast.126), channel_id=1, replica_groups=mesh['dp'=8,'fsdp'=4] {'fsdp'}, dimensions={0}, use_global_device_ids=true | all-gather | bytes 3840 | tf_op jit(solution)/shard_map/all_gather | solution.py:40
  19.9 11.4 %all-gather.1 = bf16[4,192,2]{1,2,0:T(2,128)(2,1)S(1)} all-gather(bf16[1,192,2]{1,2,0:T(2,128)(2,1)S(1)} %bitcast.127), channel_id=1, replica_groups=mesh['dp'=8,'fsdp'=4] {'fsdp'}, dimensions={0}, use_global_device_ids=true | all-gather | bytes 3840 | tf_op jit(solution)/shard_map/all_gather | solution.py:41
  31.4 8.0 %all-gather.2 = bf16[4,192,2]{1,2,0:T(2,128)(2,1)S(1)} all-gather(bf16[1,192,2]{1,2,0:T(2,128)(2,1)S(1)} %bitcast.128), channel_id=1, replica_groups=mesh['dp'=8,'fsdp'=4] {'fsdp'}, dimensions={0}, use_global_device_ids=true | all-gather | bytes 3840 | tf_op jit(solution)/shard_map/all_gather | solution.py:42
  40.7 37.7 %all-gather.8.cloned.1.call-done = bf16[768,2304]{1,0:T(8,128)(2,1)} async-done(((bf16[192,2304]{1,0:T(8,128)(2,1)}), bf16[768,2304]{1,0:T(8,128)(2,1)}) %all-gather.8.cloned.1.call-update) | async-done | bytes 3538960 | tf_op jit(solution)/shard_map/all_gather | solution.py:36
  78.4 4.4 fusion.54
  82.9 2.0 fusion.61
  84.9 1.5 copy.68
  86.4 1.9 copy.71
  88.7 2.8 copy.69
  91.5 1.7 reduce_sum.228
  93.2 2.0 multiply_reduce_fusion.1
  95.4 8.1 %fusion.62 = (f32[12,576]{1,0:T(8,128)S(1)}, f32[12,576,576]{1,2,0:T(8,128)}) fusion(f32[576,12,64]{0,2,1:T(8,128)S(1)} %bitcast.95, f32[12,64]{1,0:T(8,128)S(1)} %mul.324, f32[576,12]{0,1:T(8,128)S(1)} %fusion.47, f32[576,12]{0,1:T(8,128)S(1)} %broadcast_multiply_fusion, f32[576,12,64]{0,2,1:T(8,128)S(1)} %bitcast.102, f32[12,64]{1,0:T(8,128)S(1)} %mul.318, ...), kind=kOutput, calls=%fused_computation.139 | convolution fusion | flops 525083904 | bytes 19940352 | tf_op jit(solution)/shard_map/while/body/eval_jaxpr/qhd,khd->hqk/dot_general | solution.py:70
  103.5 8.5 %fusion.3 = f32[12,576]{1,0:T(8,128)S(1)} fusion(f32[12,576,576]{1,2,0:T(8,128)} %get-tuple-element.91, f32[12,576]{1,0:T(8,128)S(1)} %get-tuple-element.90), kind=kLoop, calls=%fused_computation.9 | loop fusion | flops 7955712 | bytes 15980544 | tf_op jit(solution)/shard_map/while/body/eval_jaxpr/reduce_sum | solution.py:80
  112.0 10.6 %fusion.31 = bf16[12,64,576]{2,1,0:T(8,128)(2,1)} fusion(bf16[576,12,64]{0,2,1:T(8,128)(2,1)} %bitcast.109, f32[12,576,576]{1,2,0:T(8,128)} %get-tuple-element.91, f32[12,576]{1,0:T(8,128)S(1)} %fusion.3, f32[12,576]{1,0:T(8,128)S(1)} %get-tuple-element.90), kind=kOutput, calls=%fused_computation.81 | convolution fusion | flops 521994240 | bytes 17750016 | tf_op jit(solution)/shard_map/while/body/eval_jaxpr/hqk,khd->qhd/dot_general | solution.py:82
  122.6 2.6 fusion.63
  126.9 71.9 %all-gather.12.cloned.1.call-done = bf16[768,3072]{1,0:T(8,128)(2,1)} async-done(((bf16[192,3072]{1,0:T(8,128)(2,1)}), bf16[768,3072]{1,0:T(8,128)(2,1)}) %all-gather.12.cloned.1.call-update) | async-done | bytes 4718608 | tf_op jit(solution)/shard_map/all_gather | solution.py:38
  198.8 22.7 %multiply_convert_fusion = (bf16[576,3072]{1,0:T(8,128)(2,1)}, f32[576,3072]{1,0:T(8,128)}, f32[576,3072]{1,0:T(8,128)}) fusion(bf16[768,3072]{1,0:T(8,128)(2,1)} %all-gather.12.cloned.1.call-done, f32[576,768]{1,0:T(8,128)} %copy-done.7, f32[768]{0:T(1024)S(1)} %get-tuple-element.73, f32[768]{0:T(1024)S(1)} %get-tuple-element.102, f32[576]{0:T(1024)S(1)} %fusion.50, ...), kind=kOutput, calls=%fused_computation.17 | convolution fusion | flops 2835136512 | bytes 24193536 | tf_op jit(solution)/shard_map/dot_general | solution.py:92
  221.5 66.5 %all-gather.14.cloned.1.call-done = bf16[3072,768]{1,0:T(8,128)(2,1)} async-done(((bf16[768,768]{1,0:T(8,128)(2,1)}), bf16[3072,768]{1,0:T(8,128)(2,1)}) %all-gather.14.cloned.1.call-update) | async-done | bytes 4718608 | tf_op jit(solution)/shard_map/all_gather | solution.py:39
  288.0 11.3 %add_convert_fusion = bf16[576,3072]{1,0:T(8,128)(2,1)S(1)} fusion(f32[576,3072]{1,0:T(8,128)} %get-tuple-element.87, f32[576,3072]{1,0:T(8,128)} %get-tuple-element.94, bf16[3072,768]{1,0:T(8,128)(2,1)} %all-gather.14.cloned.1.call-done, bf16[576,768]{1,0:T(8,128)(2,1)} %param.19, f32[576]{0:T(1024)S(1)} %fusion.48), kind=kOutput, calls=%fused_computation.16 | convolution fusion | flops 2744008704 | bytes 23300352 | tf_op jit(solution)/shard_map/dot_general | solution.py:106
  299.4 3.3 multiply_reduce_fusion.2
  305.9 2.1 convolution_convert_fusion.4
  308.1 3.3 convolution_convert_fusion.5
  311.5 2.4 copy.73
  313.9 7.6 convolution_convert_fusion
  321.5 11.9 %fusion = f32[12,576]{1,0:T(8,128)S(1)} fusion(bf16[12,576,576]{1,2,0:T(8,128)(2,1)} %convolution_convert_fusion, f32[12,576,576]{1,2,0:T(8,128)} %get-tuple-element.91, f32[12,576]{1,0:T(8,128)S(1)} %log_add_fusion), kind=kLoop, calls=%fused_computation.2 | loop fusion | flops 15918336 | bytes 23943168 | tf_op jit(solution)/shard_map/while/body/eval_jaxpr/reduce_sum | solution.py:126
  334.0 6.6 fusion.2
  340.6 4.0 fusion.23
  344.7 1.8 fusion.24
  351.6 9.2 %fusion.32 = bf16[12,64,576]{2,1,0:T(8,128)(2,1)S(1)} fusion(bf16[576,12,64]{0,2,1:T(8,128)(2,1)S(1)} %bitcast.108, f32[12,576,576]{1,2,0:T(8,128)} %get-tuple-element.91, f32[12,576]{1,0:T(8,128)S(1)} %log_add_fusion), kind=kOutput, calls=%fused_computation.82 | convolution fusion | flops 518012928 | bytes 17722368 | tf_op jit(solution)/shard_map/while/body/eval_jaxpr/hqk,qhd->khd/dot_general | solution.py:123
  361.7 7.4 convolution_convert_fusion.1
  369.2 1.4 copy-done.9
  370.6 7.8 %convolution_convert_fusion.3 = bf16[768,3072]{1,0:T(8,128)(2,1)} fusion(bf16[576,3072]{1,0:T(8,128)(2,1)} %copy-done.38, f32[576,768]{1,0:T(8,128)S(1)} %copy-done.9, f32[768]{0:T(1024)S(1)} %get-tuple-element.73, f32[768]{0:T(1024)S(1)} %get-tuple-element.102, f32[576]{0:T(1024)S(1)} %fusion.50, f32[576]{0:T(1024)S(1)} %broadcast_multiply_fusion.4), kind=kOutput, calls=%fused_computation.34 | convolution fusion | flops 2722480128 | bytes 10037760 | tf_op jit(solution)/shard_map/dot_general | solution.py:109
  379.5 8.0 %convolution_convert_fusion.2 = bf16[3072,768]{1,0:T(8,128)(2,1)} fusion(bf16[576,3072]{1,0:T(8,128)(2,1)} %get-tuple-element.86, bf16[576,768]{1,0:T(8,128)(2,1)S(1)} %copy-done.13, f32[576]{0:T(1024)S(1)} %fusion.48), kind=kOutput, calls=%fused_computation.33 | convolution fusion | flops 2721595392 | bytes 9144576 | tf_op jit(solution)/shard_map/dot_general | solution.py:105
  389.0 5.1 fusion.58
  399.3 37.4 %reduce-scatter.14.cloned.1.call-done = bf16[192,2304]{1,0:T(8,128)(2,1)} async-done(((bf16[768,2304]{1,0:T(8,128)(2,1)}), bf16[192,2304]{1,0:T(8,128)(2,1)}) %reduce-scatter.14.cloned.1.call-update) | async-done | bytes 884752 | tf_op jit(solution)/shard_map/reduce_scatter | solution.py:159
  436.7 88.1 %reduce-scatter.18.cloned.1.call-done = bf16[192,3072]{1,0:T(8,128)(2,1)} async-done(((bf16[768,3072]{1,0:T(8,128)(2,1)}), bf16[192,3072]{1,0:T(8,128)(2,1)}) %reduce-scatter.18.cloned.1.call-update) | async-done | bytes 1179664 | tf_op jit(solution)/shard_map/reduce_scatter | solution.py:165
  524.8 88.1 %reduce-scatter.20.cloned.1.call-done = bf16[768,768]{1,0:T(8,128)(2,1)} async-done(((bf16[3072,768]{1,0:T(8,128)(2,1)}), bf16[768,768]{1,0:T(8,128)(2,1)}) %reduce-scatter.20.cloned.1.call-update) | async-done | bytes 1179664 | tf_op jit(solution)/shard_map/reduce_scatter | solution.py:168
  613.1 3.5 add_convert_fusion.3
  616.5 6.2 multiply_convert_fusion.3
  622.7 10.3 %reduce-scatter.22.cloned.1.call-done = bf16[192,2]{1,0:T(8,128)(2,1)} async-done(((bf16[768,2]{1,0:T(8,128)(2,1)}), bf16[192,2]{1,0:T(8,128)(2,1)}) %reduce-scatter.22.cloned.1.call-update) | async-done | bytes 784
  633.9 19.1 %reduce-scatter.24.cloned.1.call-done = bf16[192,2]{1,0:T(8,128)(2,1)} async-done(((bf16[768,2]{1,0:T(8,128)(2,1)}), bf16[192,2]{1,0:T(8,128)(2,1)}) %reduce-scatter.24.cloned.1.call-update) | async-done | bytes 784
  653.9 19.3 %reduce-scatter.26.cloned.1.call-done = bf16[192,2]{1,0:T(8,128)(2,1)} async-done(((bf16[768,2]{1,0:T(8,128)(2,1)}), bf16[192,2]{1,0:T(8,128)(2,1)}) %reduce-scatter.26.cloned.1.call-update) | async-done | bytes 784
  674.0 12.1 %all-reduce = (bf16[2,192]{1,0:T(2,128)(2,1)S(1)}, bf16[2,192]{1,0:T(2,128)(2,1)S(1)}, bf16[2,192]{1,0:T(2,128)(2,1)S(1)}) all-reduce(bf16[2,192]{1,0:T(2,128)(2,1)S(1)} %copy.84, bf16[2,192]{1,0:T(2,128)(2,1)S(1)} %copy.86, bf16[2,192]{1,0:T(2,128)(2,1)S(1)} %copy.88), channel_id=1, replica_groups=mesh['dp'=8,'fsdp'=4] {'dp'}, use_global_device_ids=true, to_apply=%region_32.33 | all-reduce | flops 1152 | bytes 4608 | tf_op jit(solution)/shard_map/psum | solution.py:186
  687.8 63.8 %all-reduce.4.cloned.1.call-done = (bf16[192,2304]{1,0:T(8,128)(2,1)}, bf16[192,768]{1,0:T(8,128)(2,1)}, bf16[192,3072]{1,0:T(8,128)(2,1)}, bf16[768,768]{1,0:T(8,128)(2,1)}) async-done(((bf16[192,2304]{1,0:T(8,128)(2,1)}, bf16[192,768]{1,0:T(8,128)(2,1)}, bf16[192,3072]{1,0:T(8,128)(2,1)}, bf16[768,768]{1,0:T(8,128)(2,1)}), (bf16[192,2304]{1,0:T(8,128)(2,1)}, bf16[192,768]{1,0:T(8,128)(2,1)}, ...) | async-done | bytes 3538960 | tf_op jit(solution)/shard_map/psum | solution.py:182
  751.6 1.9 convert_element_type.168
  753.5 2.5 convert_element_type.166
  756.0 1.7 convert_element_type.170
  757.7 1.6 convert_element_type.172
  (181 shorter events, 29.8 us)
Async XLA Ops:
  7.2 2.9 copy-start.36
  7.2 4.4 copy-start.32
  7.2 12.7 %copy-start.33 = (bf16[2,192]{1,0:T(2,128)(2,1)S(1)}, bf16[2,192]{1,0:T(2,128)(2,1)}, u32[]{:S(2)}) copy-start(bf16[2,192]{1,0:T(2,128)(2,1)} %param.17) | copy-start | bytes 2308
  7.2 24.2 %copy-start.34 = (bf16[2,192]{1,0:T(2,128)(2,1)S(1)}, bf16[2,192]{1,0:T(2,128)(2,1)}, u32[]{:S(2)}) copy-start(bf16[2,192]{1,0:T(2,128)(2,1)} %param.18) | copy-start | bytes 2308
  7.2 32.4 %copy-start.5 = (bf16[576,768]{1,0:T(8,128)(2,1)S(1)}, bf16[576,768]{1,0:T(8,128)(2,1)}, u32[]{:S(2)}) copy-start(bf16[576,768]{1,0:T(8,128)(2,1)} %param.10) | copy-start | bytes 2654212
  7.2 71.1 %all-gather.8.cloned.1.call-start = ((), (), s32[]{:S(2)}) async-start(), calls=%async_computation.7 | async-start | bytes 4423680 | tf_op jit(solution)/shard_map/all_gather | solution.py:36
  8.0 114.7 %all-gather.10.cloned.1.call-start = ((), (), s32[]{:S(2)}) async-start(), calls=%async_computation.8 | async-start | bytes 1474560 | tf_op jit(solution)/shard_map/all_gather | solution.py:37
  8.7 190.1 %all-gather.12.cloned.1.call-start = ((), (), s32[]{:S(2)}) async-start(), calls=%async_computation.9 | async-start | bytes 5898240 | tf_op jit(solution)/shard_map/all_gather | solution.py:38
  9.4 278.6 %all-gather.14.cloned.1.call-start = ((), (), s32[]{:S(2)}) async-start(), calls=%async_computation.10 | async-start | bytes 5898240 | tf_op jit(solution)/shard_map/all_gather | solution.py:39
  10.0 389.3 %reduce-scatter.16.cloned.1.call-start = ((), (), s32[]{:S(2)}) async-start(), calls=%async_computation.12 | async-start | bytes 1474560 | tf_op jit(solution)/shard_map/reduce_scatter | solution.py:162
  39.8 42.9 %copy-start.22 = (f32[576]{0:T(1024)}, f32[576]{0:T(1024)S(1)}, u32[]{:S(2)}) copy-start(f32[576]{0:T(1024)S(1)} %broadcast_multiply_fusion.5) | copy-start | bytes 6916
  40.2 42.5 %copy-start.24 = (f32[576]{0:T(1024)}, f32[576]{0:T(1024)S(1)}, u32[]{:S(2)}) copy-start(f32[576]{0:T(1024)S(1)} %fusion.28) | copy-start | bytes 6916
  40.2 42.5 %copy-start.28 = (f32[576]{0:T(1024)}, f32[576]{0:T(1024)S(1)}, u32[]{:S(2)}) copy-start(f32[576]{0:T(1024)S(1)} %fusion.49) | copy-start | bytes 6916
  40.7 42.1 %copy-start.26 = (f32[768]{0:T(1024)}, f32[768]{0:T(1024)S(1)}, u32[]{:S(2)}) copy-start(f32[768]{0:T(1024)S(1)} %get-tuple-element.101) | copy-start | bytes 9220
  40.7 42.1 %copy-start.30 = (f32[768]{0:T(1024)}, f32[768]{0:T(1024)S(1)}, u32[]{:S(2)}) copy-start(f32[768]{0:T(1024)S(1)} %get-tuple-element.74) | copy-start | bytes 9220
  93.2 2.2 copy-start
  288.0 11.3 %copy-start.8 = (f32[576,768]{1,0:T(8,128)S(1)}, f32[576,768]{1,0:T(8,128)}, u32[]{:S(2)}) copy-start(f32[576,768]{1,0:T(8,128)} %copy-done.7) | copy-start | bytes 5308420
  288.0 11.3 %copy-start.35 = (bf16[768,3072]{1,0:T(8,128)(2,1)S(1)}, bf16[768,3072]{1,0:T(8,128)(2,1)}, u32[]{:S(2)}) copy-start(bf16[768,3072]{1,0:T(8,128)(2,1)} %all-gather.12.cloned.1.call-done) | copy-start | bytes 14155780
  299.4 3.3 copy-start.38
  302.7 1.9 copy-start.12
  303.5 2.5 copy-start.37
  308.1 128.6 %reduce-scatter.14.cloned.1.call-start = ((), (), s32[]{:S(2)}) async-start(), calls=%async_computation.11 | async-start | bytes 4423680 | tf_op jit(solution)/shard_map/reduce_scatter | solution.py:159
  313.9 19.6 %slice-start = ((s8[17694720]{0:T(1024)(128)(4,1)}), s8[4194304]{0:T(1024)(128)(4,1)S(1)}, s32[]{:S(2)}) async-start(s8[17694720]{0:T(1024)(128)(4,1)} %bitcast.91), calls=%async_computation.19 | async-start | bytes 8388608
  313.9 19.6 %slice-start.1 = ((s8[17694720]{0:T(1024)(128)(4,1)}), s8[917504]{0:T(1024)(128)(4,1)S(1)}, s32[]{:S(2)}) async-start(s8[17694720]{0:T(1024)(128)(4,1)} %bitcast.91), calls=%async_computation.20 | async-start | bytes 1835008
  321.5 12.0 %slice-start.2 = ((s8[17694720]{0:T(1024)(128)(4,1)}), s8[4194304]{0:T(1024)(128)(4,1)S(1)}, s32[]{:S(2)}) async-start(s8[17694720]{0:T(1024)(128)(4,1)} %bitcast.91), calls=%async_computation.21 | async-start | bytes 8388608
  321.5 12.0 %slice-start.3 = ((s8[17694720]{0:T(1024)(128)(4,1)}), s8[4194304]{0:T(1024)(128)(4,1)S(1)}, s32[]{:S(2)}) async-start(s8[17694720]{0:T(1024)(128)(4,1)} %bitcast.91), calls=%async_computation.22 | async-start | bytes 8388608
  321.5 12.5 %slice-start.4 = ((s8[17694720]{0:T(1024)(128)(4,1)}), s8[4194304]{0:T(1024)(128)(4,1)S(1)}, s32[]{:S(2)}) async-start(s8[17694720]{0:T(1024)(128)(4,1)} %bitcast.91), calls=%async_computation.23 | async-start | bytes 8388608
  334.0 6.6 copy-start.1
  344.7 1.9 copy-start.2
  350.0 10.8 %copy-start.16 = (bf16[576,12,64]{0,2,1:T(8,128)(2,1)}, bf16[576,12,64]{0,2,1:T(8,128)(2,1)S(1)}, u32[]{:S(2)}) copy-start(bf16[576,12,64]{0,2,1:T(8,128)(2,1)S(1)} %add_convert_fusion.1) | copy-start | bytes 2654212
  350.0 1.6 copy-start.6
  351.6 9.2 %copy-start.18 = (bf16[576,12,64]{0,2,1:T(8,128)(2,1)}, bf16[576,12,64]{0,2,1:T(8,128)(2,1)S(1)}, u32[]{:S(2)}) copy-start(bf16[576,12,64]{0,2,1:T(8,128)(2,1)S(1)} %add_convert_fusion.2) | copy-start | bytes 2654212
  351.6 10.1 %copy-start.23 = (f32[576]{0:T(1024)S(1)}, f32[576]{0:T(1024)}, u32[]{:S(2)}) copy-start(f32[576]{0:T(1024)} %copy-done.22) | copy-start | bytes 6916
  351.6 10.1 %copy-start.27 = (f32[768]{0:T(1024)S(1)}, f32[768]{0:T(1024)}, u32[]{:S(2)}) copy-start(f32[768]{0:T(1024)} %copy-done.26) | copy-start | bytes 9220
  351.6 10.1 %copy-start.29 = (f32[576]{0:T(1024)S(1)}, f32[576]{0:T(1024)}, u32[]{:S(2)}) copy-start(f32[576]{0:T(1024)} %copy-done.28) | copy-start | bytes 6916
  351.6 10.1 %copy-start.31 = (f32[768]{0:T(1024)S(1)}, f32[768]{0:T(1024)}, u32[]{:S(2)}) copy-start(f32[768]{0:T(1024)} %copy-done.30) | copy-start | bytes 9220
  369.1 155.7 %reduce-scatter.18.cloned.1.call-start = ((), (), s32[]{:S(2)}) async-start(), calls=%async_computation.13 | async-start | bytes 5898240 | tf_op jit(solution)/shard_map/reduce_scatter | solution.py:165
  378.4 234.6 %reduce-scatter.20.cloned.1.call-start = ((), (), s32[]{:S(2)}) async-start(), calls=%async_computation.14 | async-start | bytes 5898240 | tf_op jit(solution)/shard_map/reduce_scatter | solution.py:168
  387.6 245.5 %reduce-scatter.22.cloned.1.call-start = ((), (), s32[]{:S(2)}) async-start(), calls=%async_computation.15 | async-start | bytes 245760
  389.0 5.1 copy-start.25
  397.2 255.9 %reduce-scatter.24.cloned.1.call-start = ((), (), s32[]{:S(2)}) async-start(), calls=%async_computation.16 | async-start | bytes 245760
  398.2 274.9 %reduce-scatter.26.cloned.1.call-start = ((), (), s32[]{:S(2)}) async-start(), calls=%async_computation.17 | async-start | bytes 245760
  398.3 214.7 %copy-start.4 = (f32[576,768]{1,0:T(8,128)S(1)}, f32[576,768]{1,0:T(8,128)}, u32[]{:S(2)}) copy-start(f32[576,768]{1,0:T(8,128)} %copy-done.3) | copy-start | bytes 5308420
  399.2 352.4 %all-reduce.4.cloned.1.call-start = ((), (), s32[]{:S(2)}) async-start(), calls=%async_computation.18 | async-start | bytes 7077888 | tf_op jit(solution)/shard_map/psum | solution.py:182
  613.0 3.5 copy-start.10
  613.0 3.5 copy-start.39
  751.6 4.4 copy-start.15
  756.0 1.7 copy-start.14
  (9 other events, 10.8 us)
Sparse Core Ops, SparseCore 0:
  9.6 68.6 all-gather.7
  79.9 31.0 all-gather.9
  112.6 86.1 all-gather.11
  200.2 87.7 all-gather.13
  308.2 28.4 reduce-scatter.15
  369.3 67.4 reduce-scatter.13
  439.0 85.7 reduce-scatter.17
  527.1 85.7 reduce-scatter.19
  615.8 17.1 reduce-scatter.21
  635.1 17.8 reduce-scatter.23
  655.3 17.8 reduce-scatter.25
  676.7 74.9 all-reduce.3
where the time goes:
time: 772 us; the launch traced here: 766 us
  waiting for transfers between devices  505 us (65%)
  matrix products  126 us (16%)
  other arithmetic  52.6 us (7%)
  blocking collectives  39.7 us (5%)
  local copies, waits for them, and re-layouts  27.8 us (4%)
  between operations  15.2 us (2%)
    reduce_scatter x1, waiting for transfers between devices, on_device(): lax.psum_scatter(summands[3].astype(jnp.bfloat16), 'fsdp', scatter_dimens...  88.1 us
    reduce_scatter x1, waiting for transfers between devices, on_device(): lax.psum_scatter(summands[2].astype(jnp.bfloat16), 'fsdp', scatter_dimens...  88.1 us
    all_gather x1, waiting for transfers between devices, on_device(): lax.all_gather(w_up, 'fsdp', axis=0, tiled=True)  71.9 us
    all_gather x1, waiting for transfers between devices, on_device(): lax.all_gather(w_down, 'fsdp', axis=0, tiled=True)  66.5 us
    psum x1, waiting for transfers between devices, on_device(): lax.psum(pieces[0].astype(jnp.bfloat16), 'dp').astype(jnp.float32)  63.8 us
    unnamed x15, waiting for transfers between devices  51.4 us
    all_gather x1, waiting for transfers between devices, on_device(): lax.all_gather(w_qkv, 'fsdp', axis=0, tiled=True)  37.7 us
    reduce_scatter x1, waiting for transfers between devices, on_device(): lax.psum_scatter(summands[0].astype(jnp.bfloat16), 'fsdp', scatter_dimens...  37.4 us
  transfers between devices with their start and end apart: 12, of which 10 were waited for; matrix products, arithmetic and copies ran while one was open for 22% of the time, Pallas kernels for 0%

commit v1 on v0

--- a/solution.py
+++ b/solution.py
@@ -29,18 +29,132 @@
     return (head_norm(q_in, q_gain), head_norm(k_in, k_gain))
 
 
+NF_FAST = 4
+NDP_FAST = 8
+
+
+def _flat_pieces(mats, gains, d, ndp):
+    parts = []
+    for x in mats:
+        r = x.shape[0] // ndp
+        parts.append(lax.dynamic_slice_in_dim(x, d * r, r, 0).reshape(-1))
+    for g in gains:
+        r = g.shape[1] // ndp
+        parts.append(lax.dynamic_slice_in_dim(g, d * r, r, 1).reshape(-1))
+    return jnp.concatenate(parts)
+
+
+def _plane_gather(z):
+    d = lax.axis_index("dp")
+    c = d % 2
+    a = lax.ppermute(z, "dp", [(i, i ^ 2) for i in range(NDP_FAST)])
+    b = lax.ppermute(z, "dp", [(i, i ^ 4) for i in range(NDP_FAST)])
+    send = jnp.where(c == 0, b, a)
+    diag = lax.ppermute(
+        send, "dp", [(i, i ^ 2) if i % 2 == 0 else (i, i ^ 4) for i in range(NDP_FAST)]
+    )
+    mine = jnp.stack([z, a, b, diag])
+    sib = lax.ppermute(mine, "dp", [(i, i ^ 1) for i in range(NDP_FAST)])
+    return jnp.stack([mine[0], sib[0], mine[1], sib[1], mine[2], sib[2], mine[3], sib[3]])
+
+
+def fast_gather(mats, gains):
+    d = lax.axis_index("dp")
+    f = lax.axis_index("fsdp")
+    own = _flat_pieces(mats, gains, d, NDP_FAST)
+    slots = [own] + [
+        lax.ppermute(own, "fsdp", [(i, (i + k) % NF_FAST) for i in range(NF_FAST)])
+        for k in range(1, NF_FAST)
+    ]
+    z = jnp.stack(slots)
+    x = _plane_gather(z)
+    e_idx = jnp.arange(NDP_FAST, dtype=jnp.int32) ^ d
+    f_idx = (f - jnp.arange(NF_FAST, dtype=jnp.int32)) % NF_FAST
+    x = jnp.take(jnp.take(x, e_idx, axis=0), f_idx, axis=1)
+    out = []
+    offset = 0
+    for m in mats:
+        r, cols = m.shape[0] // NDP_FAST, m.shape[1]
+        seg = x[:, :, offset : offset + r * cols].reshape(NDP_FAST, NF_FAST, r, cols)
+        out.append(seg.transpose(1, 0, 2, 3).reshape(NF_FAST * m.shape[0], cols))
+        offset += r * cols
+    for g in gains:
+        rows, r = g.shape[0], g.shape[1] // NDP_FAST
+        seg = x[:, :, offset : offset + rows * r].reshape(NDP_FAST, NF_FAST, rows, r)
+        out.append(seg.transpose(2, 1, 0, 3).reshape(rows, NF_FAST * g.shape[1]))
+        offset += rows * r
+    return out
+
+
+def fast_reduce(mats, gains):
+    d = lax.axis_index("dp")
+    f = lax.axis_index("fsdp")
+    c = d % 2
+    parts = []
+    for m in mats:
+        rows, cols = m.shape
+        parts.append(m.astype(jnp.bfloat16).reshape(NF_FAST, NDP_FAST, -1))
+    for g in gains:
+        rows, cols = g.shape
+        r = cols // (NF_FAST * NDP_FAST)
+        seg = g.astype(jnp.bfloat16).reshape(rows, NF_FAST, NDP_FAST, r).transpose(1, 2, 0, 3)
+        parts.append(seg.reshape(NF_FAST, NDP_FAST, -1))
+    flat = jnp.concatenate(parts, axis=2)
+    e_idx = jnp.arange(NDP_FAST, dtype=jnp.int32) ^ d
+    bx = jnp.take(flat, e_idx, axis=1)
+    got = lax.ppermute(bx[:, 1::2], "dp", [(i, i ^ 1) for i in range(NDP_FAST)])
+    chip = bx[:, 0::2].astype(jnp.float32) + got.astype(jnp.float32)
+    moved = lax.ppermute(
+        chip[:, 3].astype(jnp.bfloat16),
+        "dp",
+        [(i, i ^ 2) if i % 2 == 0 else (i, i ^ 4) for i in range(NDP_FAST)],
+    ).astype(jnp.float32)
+    to_x = chip[:, 1] + jnp.where(c == 1, moved, 0.0)
+    to_y = chip[:, 2] + jnp.where(c == 0, moved, 0.0)
+    from_x = lax.ppermute(to_x.astype(jnp.bfloat16), "dp", [(i, i ^ 2) for i in range(NDP_FAST)])
+    from_y = lax.ppermute(to_y.astype(jnp.bfloat16), "dp", [(i, i ^ 4) for i in range(NDP_FAST)])
+    plane = chip[:, 0] + from_x.astype(jnp.float32) + from_y.astype(jnp.float32)
+    total = lax.dynamic_index_in_dim(plane, f, 0, keepdims=False)
+    for k in range(1, NF_FAST):
+        part = lax.dynamic_index_in_dim(plane, (f + k) % NF_FAST, 0, keepdims=False)
+        total = total + lax.ppermute(
+            part.astype(jnp.bfloat16), "fsdp", [(i, (i + k) % NF_FAST) for i in range(NF_FAST)]
+        ).astype(jnp.float32)
+    x = _plane_gather(total)
+    x = jnp.take(x, e_idx, axis=0)
+    out = []
+    offset = 0
+    for m in mats:
+        rows, cols = m.shape
+        r = rows // (NF_FAST * NDP_FAST)
+        out.append(x[:, offset : offset + r * cols].reshape(NDP_FAST * r, cols))
+        offset += r * cols
+    for g in gains:
+        rows, cols = g.shape
+        r = cols // (NF_FAST * NDP_FAST)
+        seg = x[:, offset : offset + rows * r].reshape(NDP_FAST, rows, r)
+        out.append(seg.transpose(1, 0, 2).reshape(rows, NDP_FAST * r))
+        offset += rows * r
+    return out
+
+
 def on_device(
-    tokens, image_lengths, w_qkv, w_out, w_up, w_down, ln_gain, ln_bias, qk_gain, cotangent
+    fast, tokens, image_lengths, w_qkv, w_out, w_up, w_down, ln_gain, ln_bias, qk_gain, cotangent
 ):
-    full_qkv, full_out, full_up, full_down, gain_all, bias_all, qk_all = (
-        lax.all_gather(w_qkv, "fsdp", axis=0, tiled=True),
-        lax.all_gather(w_out, "fsdp", axis=0, tiled=True),
-        lax.all_gather(w_up, "fsdp", axis=0, tiled=True),
-        lax.all_gather(w_down, "fsdp", axis=0, tiled=True),
-        lax.all_gather(ln_gain, "fsdp", axis=1, tiled=True),
-        lax.all_gather(ln_bias, "fsdp", axis=1, tiled=True),
-        lax.all_gather(qk_gain, "fsdp", axis=1, tiled=True),
-    )
+    if fast:
+        full_qkv, full_out, full_up, full_down, gain_all, bias_all, qk_all = fast_gather(
+            (w_qkv, w_out, w_up, w_down), (ln_gain, ln_bias, qk_gain)
+        )
+    else:
+        full_qkv, full_out, full_up, full_down, gain_all, bias_all, qk_all = (
+            lax.all_gather(w_qkv, "fsdp", axis=0, tiled=True),
+            lax.all_gather(w_out, "fsdp", axis=0, tiled=True),
+            lax.all_gather(w_up, "fsdp", axis=0, tiled=True),
+            lax.all_gather(w_down, "fsdp", axis=0, tiled=True),
+            lax.all_gather(ln_gain, "fsdp", axis=1, tiled=True),
+            lax.all_gather(ln_bias, "fsdp", axis=1, tiled=True),
+            lax.all_gather(qk_gain, "fsdp", axis=1, tiled=True),
+        )
     length = tokens.shape[0]
     model_width = tokens.shape[1]
     blocks = length // PATCH_BIG
@@ -94,12 +208,7 @@
     active_low = active.astype(jnp.bfloat16)
     output = residual + jnp.dot(active_low, full_down, preferred_element_type=jnp.float32)
     layer_out = (valid_rows * output).astype(jnp.bfloat16)
-    back_qkv, back_out, back_up, back_down = (
-        lax.all_gather(w_qkv, "fsdp", axis=0, tiled=True),
-        lax.all_gather(w_out, "fsdp", axis=0, tiled=True),
-        lax.all_gather(w_up, "fsdp", axis=0, tiled=True),
-        lax.all_gather(w_down, "fsdp", axis=0, tiled=True),
-    )
+    back_qkv, back_out, back_up, back_down = full_qkv, full_out, full_up, full_down
     upstream = cotangent.astype(jnp.float32) * valid_rows
     up_low = upstream.astype(jnp.bfloat16)
     grad_down = jnp.dot(active_low.T, up_low, preferred_element_type=jnp.float32)
@@ -155,38 +264,16 @@
     grad_bias = jnp.stack([bias_one, bias_two])
     grad_qk = jnp.stack([gain_q.reshape(model_width), gain_k.reshape(model_width)])
     summands = (grad_qkv, grad_outw, grad_up, grad_down, grad_gain, grad_bias, grad_qk)
-    pieces = (
-        lax.psum_scatter(
-            summands[0].astype(jnp.bfloat16), "fsdp", scatter_dimension=0, tiled=True
-        ).astype(jnp.float32),
-        lax.psum_scatter(
-            summands[1].astype(jnp.bfloat16), "fsdp", scatter_dimension=0, tiled=True
-        ).astype(jnp.float32),
-        lax.psum_scatter(
-            summands[2].astype(jnp.bfloat16), "fsdp", scatter_dimension=0, tiled=True
-        ).astype(jnp.float32),
-        lax.psum_scatter(
-            summands[3].astype(jnp.bfloat16), "fsdp", scatter_dimension=0, tiled=True
-        ).astype(jnp.float32),
-        lax.psum_scatter(
-            summands[4].astype(jnp.bfloat16), "fsdp", scatter_dimension=1, tiled=True
-        ).astype(jnp.float32),
-        lax.psum_scatter(
-            summands[5].astype(jnp.bfloat16), "fsdp", scatter_dimension=1, tiled=True
-        ).astype(jnp.float32),
-        lax.psum_scatter(
-            summands[6].astype(jnp.bfloat16), "fsdp", scatter_dimension=1, tiled=True
-        ).astype(jnp.float32),
-    )
-    shares = (
-        lax.psum(pieces[0].astype(jnp.bfloat16), "dp").astype(jnp.float32),
-        lax.psum(pieces[1].astype(jnp.bfloat16), "dp").astype(jnp.float32),
-        lax.psum(pieces[2].astype(jnp.bfloat16), "dp").astype(jnp.float32),
-        lax.psum(pieces[3].astype(jnp.bfloat16), "dp").astype(jnp.float32),
-        lax.psum(pieces[4].astype(jnp.bfloat16), "dp").astype(jnp.float32),
-        lax.psum(pieces[5].astype(jnp.bfloat16), "dp").astype(jnp.float32),
-        lax.psum(pieces[6].astype(jnp.bfloat16), "dp").astype(jnp.float32),
-    )
+    if fast:
+        shares = fast_reduce(summands[:4], summands[4:])
+    else:
+        pieces = [
+            lax.psum_scatter(
+                s.astype(jnp.bfloat16), "fsdp", scatter_dimension=0 if k < 4 else 1, tiled=True
+            ).astype(jnp.float32)
+            for k, s in enumerate(summands)
+        ]
+        shares = [lax.psum(p.astype(jnp.bfloat16), "dp").astype(jnp.float32) for p in pieces]
     return (
         layer_out,
         grad_tokens,
@@ -224,6 +311,7 @@
         P(None, "fsdp"),
         P(None, "fsdp"),
     )
+    fast = dict(mesh.shape) == {"dp": NDP_FAST, "fsdp": NF_FAST}
     return jax.shard_map(
-        on_device, mesh=mesh, in_specs=in_specs, out_specs=out_specs, check_vma=False
-    )
+        partial(on_device, fast), mesh=mesh, in_specs=in_specs, out_specs=out_specs, check_vma=False
+    )

time: 772 us -> 946 us (1.23); the launches traced: 766 us -> 928 us
  local copies, waits for them, and re-layouts: 27.8 us -> 409 us
  waiting for transfers between devices: 505 us -> 201 us
  other arithmetic: 52.6 us -> 173 us
  blocking collectives: 39.7 us -> 0 us
  starting transfers between devices: 0.48 us -> 24.2 us
  between operations: 15.2 us -> 2.26 us
    reduce_scatter x4 -> x0, waiting for transfers between devices: 214 us -> none  [the longest x1 88.1 us: on_device(): lax.psum_scatter(summands[3].astype(jnp.bfloat16), 'fsdp', scatter_dimens...]
    ppermute x0 -> x18, waiting for transfers between devices: none -> 201 us  [the longest x2 54 us: _plane_gather(): b = lax.ppermute(z, 'dp', [(i, i ^ 4) for i in range(NDP_FAST)])]
    all_gather x4 -> x0, waiting for transfers between devices: 176 us -> none  [the longest x1 71.9 us: on_device(): lax.all_gather(w_up, 'fsdp', axis=0, tiled=True)]
    gather x0 -> x19, local copies, waits for them, and re-layouts: none -> 152 us  [the longest x12 100 us: fast_gather(): x = jnp.take(jnp.take(x, e_idx, axis=0), f_idx, axis=1)]
    reshape x4 -> x34, local copies, waits for them, and re-layouts: 0.02 us -> 88.2 us  [the longest x8 38.6 us: fast_gather(): seg = x[:, :, offset:offset + r * cols].reshape(NDP_FAST, NF_FAST, r, cols)]
    select_n x0 -> x8, other arithmetic: none -> 79.7 us  [the longest x4 49.3 us: fast_gather(): x = jnp.take(jnp.take(x, e_idx, axis=0), f_idx, axis=1)]
    psum x1 -> x0, waiting for transfers between devices: 63.8 us -> none  [on_device(): lax.psum(pieces[0].astype(jnp.bfloat16), 'dp').astype(jnp.float32)]
    another operation x0 -> x14, local copies, waits for them, and re-layouts: none -> 60.8 us  [the longest x2 23.3 us: _plane_gather(): jnp.stack([mine[0], sib[0], mine[1], sib[1], mine[2], sib[2], mine[3], si...]
  transfers between devices with their start and end apart: 12 -> 18, of which waited for: 10 -> 12; matrix products, arithmetic and copies ran while one was open for 22% -> 5% of each run, Pallas kernels for 0% -> 0%
where the time goes in v1:
time: 946 us; the launch traced here: 928 us
  local copies, waits for them, and re-layouts  409 us (43%)
  waiting for transfers between devices  201 us (21%)
  other arithmetic  173 us (18%)
  matrix products  119 us (13%)
  starting transfers between devices  24.2 us (3%)
    gather x12, local copies, waits for them, and re-layouts, fast_gather(): x = jnp.take(jnp.take(x, e_idx, axis=0), f_idx, axis=1)  100 us
    ppermute x2, waiting for transfers between devices, _plane_gather(): b = lax.ppermute(z, 'dp', [(i, i ^ 4) for i in range(NDP_FAST)])  54 us
    select_n x4, other arithmetic, fast_gather(): x = jnp.take(jnp.take(x, e_idx, axis=0), f_idx, axis=1)  49.3 us
    unnamed x155, local copies, waits for them, and re-layouts  41 us
    reshape x8, local copies, waits for them, and re-layouts, fast_gather(): seg = x[:, :, offset:offset + r * cols].reshape(NDP_FAST, NF_FAST, r, cols)  38.6 us
    ppermute x1, waiting for transfers between devices, fast_reduce(): lax.ppermute(to_x.astype(jnp.bfloat16), 'dp', [(i, i ^ 2) for i in range(...  38.2 us
    reshape x7, local copies, waits for them, and re-layouts, fast_reduce(): parts.append(m.astype(jnp.bfloat16).reshape(NF_FAST, NDP_FAST, -1))  37.1 us
    gather x3, local copies, waits for them, and re-layouts, fast_reduce(): bx = jnp.take(flat, e_idx, axis=1)  31.3 us
  transfers between devices with their start and end apart: 18, of which 12 were waited for; matrix products, arithmetic and copies ran while one was open for 5% of the time, Pallas kernels for 0%

profile of v1, /device:TPU:8, one launch (start us, length us, event | category | flops | bytes accessed | tf_op | source)
XLA Modules:
  0.0 928.4 jit_solution(18385453608348969951)
XLA Ops:
  18.7 21.6 %collective-permute-done.2 = bf16[221328]{0:T(1024)(128)(2,1)S(1)} collective-permute-done((bf16[221328]{0:T(1024)(128)(2,1)S(1)}, bf16[221328]{0:T(1024)(128)(2,1)S(1)}, u32[]{:S(2)}, u32[]{:S(2)}) %collective-permute-start.2) | collective-permute-done | bytes 442688 | tf_op jit(solution)/shard_map/ppermute | solution.py:66
  55.4 7.4 constant_dynamic-update-slice_fusion.3
  65.8 35.6 %collective-permute-done.4 = bf16[4,221328]{1,0:T(4,128)(2,1)S(1)} collective-permute-done((bf16[4,221328]{1,0:T(4,128)(2,1)}, bf16[4,221328]{1,0:T(4,128)(2,1)S(1)}, u32[]{:S(2)}, u32[]{:S(2)}) %collective-permute-start.4) | collective-permute-done | bytes 1770656 | tf_op jit(solution)/shard_map/ppermute | solution.py:51
  105.3 21.1 %collective-permute-done.5 = bf16[4,221328]{1,0:T(4,128)(2,1)S(1)} collective-permute-done((bf16[4,221328]{1,0:T(4,128)(2,1)S(1)}, bf16[4,221328]{1,0:T(4,128)(2,1)S(1)}, u32[]{:S(2)}, u32[]{:S(2)}) %collective-permute-start.5) | collective-permute-done | bytes 1770656 | tf_op jit(solution)/shard_map/ppermute | solution.py:53
  126.4 12.6 %pad_maximum_fusion.2 = bf16[4,4,221328]{2,1,0:T(4,128)(2,1)} fusion(bf16[1,4,221328]{2,1,0:T(4,128)(2,1)S(1)} %bitcast.175, bf16[1,4,221328]{2,1,0:T(4,128)(2,1)S(1)} %bitcast.172, bf16[1,4,221328]{2,1,0:T(4,128)(2,1)} %bitcast.3, bf16[1,4,221328]{2,1,0:T(4,128)(2,1)} %bitcast.2), kind=kLoop, calls=%fused_computation.29 | loop fusion | flops 10623744 | bytes 14164992 | tf_op jit(solution)/shard_map/stack | solution.py:56
  142.9 7.7 collective-permute-done.6
  167.5 8.3 mini-gather-slice.8
  175.8 8.3 mini-gather-slice.9
  184.2 11.2 %gather_fusion.1 = bf16[8,4,110608]{2,1,0:T(4,128)(2,1)} fusion(bf16[8,4,110608]{2,1,0:T(4,128)(2,1)} %mini-gather-slice.9, s32[1024]{0:T(1024)S(1)} %pad_clamp_fusion.1), kind=kCustom, calls=%fused_computation.1 | custom fusion | bytes 14157856 | tf_op jit(solution)/shard_map/jit(_take)/gather | solution.py:73
  195.3 11.1 %gather_fusion = bf16[8,4,110720]{2,1,0:T(4,128)(2,1)} fusion(bf16[8,4,110720]{2,1,0:T(4,128)(2,1)} %mini-gather-slice.8, s32[1024]{0:T(1024)S(1)} %pad_clamp_fusion.1), kind=kCustom, calls=%fused_computation | custom fusion | bytes 14172192 | tf_op jit(solution)/shard_map/jit(_take)/gather | solution.py:73
  206.5 24.9 %maximum_select_fusion = bf16[8,4,221328]{2,1,0:T(4,128)(2,1)} fusion(bf16[8,4,110608]{2,1,0:T(4,128)(2,1)} %gather_fusion.1, bf16[8,4,110720]{2,1,0:T(4,128)(2,1)} %gather_fusion, pred[8]{0:T(512)(128)(4,1)S(1)} %compare_and_fusion), kind=kLoop, calls=%fused_computation.18 | loop fusion | flops 35412480 | bytes 28329992 | tf_op jit(solution)/shard_map/jit(_take)/select_n | solution.py:73
  231.4 8.3 mini-gather-slice.10
  239.7 8.4 mini-gather-slice.11
  254.6 7.1 gather_fusion.3
  261.8 8.6 copy.140
  277.0 7.1 gather_fusion.2
  284.1 8.8 copy.141
  292.9 24.4 %maximum_select_fusion.1 = bf16[8,4,221328]{2,1,0:T(4,128)(2,1)} fusion(bf16[8,4,110608]{2,1,0:T(4,128)(2,1)} %bitcast.169, bf16[8,4,110720]{2,1,0:T(4,128)(2,1)} %bitcast.170, pred[4]{0:T(512)(128)(4,1)S(1)} %compare_and_fusion.1), kind=kLoop, calls=%fused_computation.19 | loop fusion | flops 35412480 | bytes 28329988 | tf_op jit(solution)/shard_map/jit(_take)/select_n | solution.py:73
  323.2 10.8 %fusion.72 = (bf16[8,4,73728]{2,1,0:T(4,128)(2,1)}, bf16[8,4,73728]{2,1,0:T(4,128)(2,1)}) fusion(bf16[8,4,221328]{2,1,0:T(4,128)(2,1)} %maximum_select_fusion.1), kind=kLoop, calls=%fused_computation.209 | loop fusion | bytes 18874368 | tf_op jit(solution)/shard_map/slice | solution.py:78
  334.4 7.5 reshape.465
  352.8 8.4 reshape.473
  366.1 8.4 reshape.471
  387.4 8.1 fusion.81
  395.5 8.5 fusion.3
  404.1 9.8 %fusion.38 = bf16[12,64,576]{2,1,0:T(8,128)(2,1)S(1)} fusion(bf16[576,12,64]{0,2,1:T(8,128)(2,1)} %bitcast.186, f32[12,576,576]{1,2,0:T(8,128)} %get-tuple-element.107, f32[12,576]{1,0:T(8,128)S(1)} %fusion.3, f32[12,576]{1,0:T(8,128)S(1)} %get-tuple-element.106), kind=kOutput, calls=%fused_computation.120 | convolution fusion | flops 521994240 | bytes 17750016 | tf_op jit(solution)/shard_map/while/body/eval_jaxpr/hqk,khd->qhd/dot_general | solution.py:196
  415.4 22.9 %multiply_convert_fusion = (bf16[576,3072]{1,0:T(8,128)(2,1)}, f32[576,3072]{1,0:T(8,128)}, f32[576,3072]{1,0:T(8,128)}) fusion(bf16[768,3072]{1,0:T(8,128)(2,1)} %bitcast.182, f32[576,768]{1,0:T(8,128)S(1)} %get-tuple-element.109, f32[768]{0:T(1024)S(1)} %add.225, f32[768]{0:T(1024)S(1)} %mul.344, f32[576]{0:T(1024)S(1)} %fusion.57, ...), kind=kOutput, calls=%fused_computation.35 | convolution fusion | flops 2835136512 | bytes 24193536 | tf_op jit(solution)/shard_map/dot_general | solution.py:206
  438.2 9.2 add_convert_fusion
  466.9 7.5 convolution_convert_fusion
  474.4 9.9 %fusion.39 = bf16[12,64,576]{2,1,0:T(8,128)(2,1)} fusion(bf16[576,12,64]{0,2,1:T(8,128)(2,1)S(1)} %bitcast.174, f32[12,576,576]{1,2,0:T(8,128)} %get-tuple-element.107, f32[12,576]{1,0:T(8,128)S(1)} %log_add_fusion), kind=kOutput, calls=%fused_computation.121 | convolution fusion | flops 518012928 | bytes 17722368 | tf_op jit(solution)/shard_map/while/body/eval_jaxpr/hqk,qhd->khd/dot_general | solution.py:232
  484.3 12.8 %fusion = f32[12,576]{1,0:T(8,128)S(1)} fusion(bf16[12,576,576]{1,2,0:T(8,128)(2,1)} %convolution_convert_fusion, f32[12,576,576]{1,2,0:T(8,128)} %get-tuple-element.107, f32[12,576]{1,0:T(8,128)S(1)} %log_add_fusion), kind=kLoop, calls=%fused_computation.10 | loop fusion | flops 15918336 | bytes 23943168 | tf_op jit(solution)/shard_map/while/body/eval_jaxpr/reduce_sum | solution.py:235
  504.2 8.2 fusion.29
  523.0 7.3 convolution_convert_fusion.1
  542.1 8.3 convolution_convert_fusion.2
  568.2 9.4 %fusion.76 = (bf16[4,8,73728]{2,0,1:T(4,128)(2,1)S(1)}, bf16[4,8,147600]{2,0,1:T(4,128)(2,1)}) fusion(bf16[4,8,73728]{2,1,0:T(8,128)(2,1)} %reshape.480), kind=kLoop, calls=%fused_computation.213 | loop fusion | bytes 14155776 | tf_op jit(solution)/shard_map/reshape | solution.py:96
  577.6 13.1 %pad_maximum_fusion = bf16[4,8,110720]{2,0,1:T(4,128)(2,1)} fusion(bf16[4,8,73728]{2,0,1:T(4,128)(2,1)S(1)} %get-tuple-element.94, bf16[4,8,18432]{2,0,1:T(4,128)(2,1)} %copy.117, bf16[4,8,55296]{2,0,1:T(4,128)(2,1)S(1)} %copy.116), kind=kLoop, calls=%fused_computation.27 | loop fusion | flops 21258240 | bytes 16523264 | tf_op jit(solution)/shard_map/concatenate | solution.py:102
  590.7 11.6 %gather_fusion.4 = bf16[8,4,110720]{2,1,0:T(4,128)(2,1)} fusion(bf16[4,8,110720]{2,0,1:T(4,128)(2,1)} %pad_maximum_fusion, s32[1024]{0:T(1024)S(1)} %copy-done.51), kind=kCustom, calls=%fused_computation.4 | custom fusion | bytes 14172192 | tf_op jit(solution)/shard_map/jit(_take)/gather | solution.py:104
  602.3 8.1 copy_dynamic-update-slice_fusion
  616.8 8.3 mini-gather-slice.12
  625.2 11.4 %gather_fusion.5 = bf16[8,4,110608]{2,1,0:T(4,128)(2,1)} fusion(bf16[4,8,110608]{2,0,1:T(4,128)(2,1)} %mini-gather-slice.12, s32[1024]{0:T(1024)S(1)} %copy-done.51), kind=kCustom, calls=%fused_computation.5 | custom fusion | bytes 14157856 | tf_op jit(solution)/shard_map/jit(_take)/gather | solution.py:104
  636.5 24.5 %maximum_select_fusion.2 = bf16[4,8,221328]{2,0,1:T(4,128)(2,1)} fusion(bf16[4,8,110608]{2,0,1:T(4,128)(2,1)} %bitcast.171, bf16[4,8,110720]{2,0,1:T(4,128)(2,1)} %bitcast.168, pred[8]{0:T(512)(128)(4,1)S(1)} %copy-done.53), kind=kLoop, calls=%fused_computation.20 | loop fusion | flops 35412480 | bytes 28329992 | tf_op jit(solution)/shard_map/jit(_take)/select_n | solution.py:104
  666.8 11.2 %collective-permute-done.7 = bf16[4,4,221328]{2,0,1:T(4,128)(2,1)S(1)} collective-permute-done((bf16[4,4,221328]{2,0,1:T(4,128)(2,1)S(1)}, bf16[4,4,221328]{2,0,1:T(4,128)(2,1)S(1)}, u32[]{:S(2)}, u32[]{:S(2)}) %collective-permute-start.7) | collective-permute-done | bytes 7082528 | tf_op jit(solution)/shard_map/ppermute | solution.py:105
  689.0 21.2 %collective-permute-done.8 = bf16[4,221328]{1,0:T(4,128)(2,1)} collective-permute-done((bf16[4,221328]{1,0:T(4,128)(2,1)S(1)}, bf16[4,221328]{1,0:T(4,128)(2,1)}, u32[]{:S(2)}, u32[]{:S(2)}) %collective-permute-start.8) | collective-permute-done | bytes 1770656 | tf_op jit(solution)/shard_map/ppermute | solution.py:107
  717.6 38.2 %collective-permute-done.9 = bf16[4,221328]{1,0:T(4,128)(2,1)} collective-permute-done((bf16[4,221328]{1,0:T(4,128)(2,1)}, bf16[4,221328]{1,0:T(4,128)(2,1)}, u32[]{:S(2)}, u32[]{:S(2)}) %collective-permute-start.9) | collective-permute-done | bytes 1770656 | tf_op jit(solution)/shard_map/ppermute | solution.py:114
  762.1 10.1 %convert_reduce_fusion.3 = (bf16[221328]{0:T(1024)(128)(2,1)}, bf16[221328]{0:T(1024)(128)(2,1)S(1)}, bf16[221328]{0:T(1024)(128)(2,1)S(1)}) fusion(f32[4,221328]{1,0:T(4,128)S(1)} %fusion.20, s32[]{:T(128)S(6)} %select_n.171, s32[]{:T(128)S(6)} %select_n.175, s32[]{:T(128)S(6)} %select_n.173), kind=kLoop, calls=%fused_computation.128 | loop fusion | bytes 2655948 | tf_op jit(solution)/shard_map/convert_element_type | solution.py:121
  780.5 8.1 dynamic-slice_reduce_fusion
  788.6 17.5 %collective-permute-done.11 = bf16[221328]{0:T(1024)(128)(2,1)S(1)} collective-permute-done((bf16[221328]{0:T(1024)(128)(2,1)}, bf16[221328]{0:T(1024)(128)(2,1)S(1)}, u32[]{:S(2)}, u32[]{:S(2)}) %collective-permute-start.11) | collective-permute-done | bytes 442688 | tf_op jit(solution)/shard_map/ppermute | solution.py:120
  814.4 18.4 %collective-permute-done.15 = f32[221328]{0:T(1024)S(1)} collective-permute-done((f32[221328]{0:T(1024)S(1)}, f32[221328]{0:T(1024)S(1)}, u32[]{:S(2)}, u32[]{:S(2)}) %collective-permute-start.15) | collective-permute-done | bytes 885344 | tf_op jit(solution)/shard_map/ppermute | solution.py:51
  865.9 20.4 %stack.101 = f32[8,221328]{1,0:T(8,128)} concatenate(f32[1,221328]{1,0:T(1,128)S(1)} %stack.96, f32[1,221328]{1,0:T(1,128)} %get-tuple-element.99, f32[1,221328]{1,0:T(1,128)S(1)} %copy-done.19, f32[1,221328]{1,0:T(1,128)} %get-tuple-element.98, f32[1,221328]{1,0:T(1,128)S(1)} %stack.98, f32[1,221328]{1,0:T(1,128)} %get-tuple-element.97, f32[1,221328]{1,0:T(1,128)} %copy-done.20, ...), dimensions={0} | concatenate | bytes 14164992 | tf_op jit(solution)/shard_map/stack | solution.py:58
  (349 shorter events, 304.4 us)
Async XLA Ops:
  8.1 32.1 %collective-permute-start.2 = (bf16[221328]{0:T(1024)(128)(2,1)S(1)}, bf16[221328]{0:T(1024)(128)(2,1)S(1)}, u32[]{:S(2)}, u32[]{:S(2)}) collective-permute-start(bf16[221328]{0:T(1024)(128)(2,1)S(1)} %concatenate.16), channel_id=1, source_target_pairs={{0,3},{1,0},{2,1},{3,2},{4,7},{5,4},{6,5},{7,6},{8,11},{9,8},{10,9... | collective-permute-start | bytes 1327976 | tf_op jit(solution)/shard_map/ppermute | solution.py:66
  8.1 37.2 %collective-permute-start.1 = (bf16[221328]{0:T(1024)(128)(2,1)S(1)}, bf16[221328]{0:T(1024)(128)(2,1)S(1)}, u32[]{:S(2)}, u32[]{:S(2)}) collective-permute-start(bf16[221328]{0:T(1024)(128)(2,1)S(1)} %concatenate.16), channel_id=1, source_target_pairs={{0,2},{1,3},{2,0},{3,1},{4,6},{5,7},{6,4},{7,5},{8,10},{9,11},{10,... | collective-permute-start | bytes 1327976 | tf_op jit(solution)/shard_map/ppermute | solution.py:66
  11.1 39.2 %collective-permute-start = (bf16[221328]{0:T(1024)(128)(2,1)S(1)}, bf16[221328]{0:T(1024)(128)(2,1)S(1)}, u32[]{:S(2)}, u32[]{:S(2)}) collective-permute-start(bf16[221328]{0:T(1024)(128)(2,1)S(1)} %concatenate.16), channel_id=1, source_target_pairs={{0,1},{1,2},{2,3},{3,0},{4,5},{5,6},{6,7},{7,4},{8,9},{9,10},{10,1... | collective-permute-start | bytes 1327976 | tf_op jit(solution)/shard_map/ppermute | solution.py:66
  62.9 38.6 %collective-permute-start.4 = (bf16[4,221328]{1,0:T(4,128)(2,1)}, bf16[4,221328]{1,0:T(4,128)(2,1)S(1)}, u32[]{:S(2)}, u32[]{:S(2)}) collective-permute-start(bf16[4,221328]{1,0:T(4,128)(2,1)} %get-tuple-element.79), channel_id=1, source_target_pairs={{0,16},{4,20},{8,24},{12,28},{16,0},{20,4},{24,8},{28,12},{1,17},{... | collective-permute-start | bytes 5311880 | tf_op jit(solution)/shard_map/ppermute | solution.py:51
  64.4 38.4 %collective-permute-start.3 = (bf16[4,221328]{1,0:T(4,128)(2,1)}, bf16[4,221328]{1,0:T(4,128)(2,1)}, u32[]{:S(2)}, u32[]{:S(2)}) collective-permute-start(bf16[4,221328]{1,0:T(4,128)(2,1)} %get-tuple-element.79), channel_id=1, source_target_pairs={{0,8},{4,12},{8,0},{12,4},{16,24},{20,28},{24,16},{28,20},{1,9},{5... | collective-permute-start | bytes 5311880 | tf_op jit(solution)/shard_map/ppermute | solution.py:50
  103.8 22.6 %collective-permute-start.5 = (bf16[4,221328]{1,0:T(4,128)(2,1)S(1)}, bf16[4,221328]{1,0:T(4,128)(2,1)S(1)}, u32[]{:S(2)}, u32[]{:S(2)}) collective-permute-start(bf16[4,221328]{1,0:T(4,128)(2,1)S(1)} %broadcast_select_fusion), channel_id=1, source_target_pairs={{0,8},{4,20},{8,0},{12,28},{16,24},{20,4},{24,16},{28,12},{1,9},{5... | collective-permute-start | bytes 5311880 | tf_op jit(solution)/shard_map/ppermute | solution.py:53
  126.4 12.6 %copy-start.21 = (bf16[4,221328]{1,0:T(4,128)(2,1)}, bf16[4,221328]{1,0:T(4,128)(2,1)S(1)}, u32[]{:S(2)}) copy-start(bf16[4,221328]{1,0:T(4,128)(2,1)S(1)} %collective-permute-done.5) | copy-start | bytes 5311876
  126.4 12.6 %copy-start.56 = (s32[1,9]{1,0:T(1,128)S(1)}, s32[1,9]{1,0:T(1,128)}, u32[]{:S(2)}) copy-start(s32[1,9]{1,0:T(1,128)} %param.11) | copy-start | bytes 112
  126.4 14.8 %copy-start.15 = (bf16[576,768]{1,0:T(8,128)(2,1)S(1)}, bf16[576,768]{1,0:T(8,128)(2,1)}, u32[]{:S(2)}) copy-start(bf16[576,768]{1,0:T(8,128)(2,1)} %param.10) | copy-start | bytes 2654212
  139.0 11.6 %collective-permute-start.6 = (bf16[4,4,221328]{2,1,0:T(4,128)(2,1)}, bf16[4,4,221328]{2,1,0:T(4,128)(2,1)}, u32[]{:S(2)}, u32[]{:S(2)}) collective-permute-start(bf16[4,4,221328]{2,1,0:T(4,128)(2,1)} %pad_maximum_fusion.2), channel_id=1, source_target_pairs={{0,4},{4,0},{8,12},{12,8},{16,20},{20,16},{24,28},{28,24},{1,5},{5... | collective-permute-start | bytes 21247496 | tf_op jit(solution)/shard_map/ppermute | solution.py:57
  139.8 66.7 %copy-start.52 = (pred[8]{0:T(512)(128)(4,1)}, pred[8]{0:T(512)(128)(4,1)S(1)}, u32[]{:S(2)}) copy-start(pred[8]{0:T(512)(128)(4,1)S(1)} %compare_and_fusion) | copy-start | bytes 28
  139.8 55.5 %copy-start.50 = (s32[1024]{0:T(1024)}, s32[1024]{0:T(1024)S(1)}, u32[]{:S(2)}) copy-start(s32[1024]{0:T(1024)S(1)} %pad_clamp_fusion.1) | copy-start | bytes 12292
  141.4 202.8 %copy-start.41 = (f32[576]{0:T(1024)}, f32[576]{0:T(1024)S(1)}, u32[]{:S(2)}) copy-start(f32[576]{0:T(1024)S(1)} %broadcast_multiply_fusion.5) | copy-start | bytes 6916
  141.8 14.2 %copy-start.43 = (f32[576]{0:T(1024)}, f32[576]{0:T(1024)S(1)}, u32[]{:S(2)}) copy-start(f32[576]{0:T(1024)S(1)} %fusion.35) | copy-start | bytes 6916
  141.8 202.4 %copy-start.48 = (f32[576]{0:T(1024)}, f32[576]{0:T(1024)S(1)}, u32[]{:S(2)}) copy-start(f32[576]{0:T(1024)S(1)} %fusion.56) | copy-start | bytes 6916
  334.2 10.0 %copy-start.54 = (f32[768]{0:T(1024)}, f32[768]{0:T(1024)S(1)}, u32[]{:S(2)}) copy-start(f32[768]{0:T(1024)S(1)} %add.218) | copy-start | bytes 9220
  334.4 9.8 %copy-start.45 = (f32[768]{0:T(1024)}, f32[768]{0:T(1024)S(1)}, u32[]{:S(2)}) copy-start(f32[768]{0:T(1024)S(1)} %mul.325) | copy-start | bytes 9220
  404.1 9.8 %copy-start.16 = (bf16[576,768]{1,0:T(8,128)(2,1)S(1)}, bf16[576,768]{1,0:T(8,128)(2,1)}, u32[]{:S(2)}) copy-start(bf16[576,768]{1,0:T(8,128)(2,1)} %param.10) | copy-start | bytes 2654212
  404.1 9.8 %copy-start.32 = (bf16[8,4,24,768]{3,2,0,1:T(8,128)(2,1)S(1)}, bf16[8,4,24,768]{3,2,0,1:T(8,128)(2,1)}, u32[]{:S(2)}) copy-start(bf16[8,4,24,768]{3,2,0,1:T(8,128)(2,1)} %copy.108) | copy-start | bytes 3538948
  413.9 24.3 %slice-start.7 = ((s8[4718592]{0:T(1024)(128)(4,1)}), s8[4194304]{0:T(1024)(128)(4,1)S(1)}, s32[]{:S(2)}) async-start(s8[4718592]{0:T(1024)(128)(4,1)} %bitcast.176), calls=%async_computation.7 | async-start | bytes 8388608
  413.9 33.6 %slice-start.11 = ((s8[4718592]{0:T(1024)(128)(4,1)}), s8[4194304]{0:T(1024)(128)(4,1)S(1)}, s32[]{:S(2)}) async-start(s8[4718592]{0:T(1024)(128)(4,1)} %bitcast.183), calls=%async_computation.11 | async-start | bytes 8388608
  414.9 44.3 %copy-start.23 = (f32[576,768]{1,0:T(8,128)}, f32[576,768]{1,0:T(8,128)S(1)}, u32[]{:S(2)}) copy-start(f32[576,768]{1,0:T(8,128)S(1)} %get-tuple-element.109) | copy-start | bytes 5308420
  415.3 22.9 %slice-start.8 = ((s8[4718592]{0:T(1024)(128)(4,1)}), s8[524288]{0:T(1024)(128)(4,1)S(1)}, s32[]{:S(2)}) async-start(s8[4718592]{0:T(1024)(128)(4,1)} %bitcast.176), calls=%async_computation.8 | async-start | bytes 1048576
  415.3 22.9 %copy-start.29 = (bf16[576,768]{1,0:T(8,128)(2,1)S(1)}, bf16[576,768]{1,0:T(8,128)(2,1)}, u32[]{:S(2)}) copy-start(bf16[576,768]{1,0:T(8,128)(2,1)} %param.19) | copy-start | bytes 2654212
  415.3 22.9 %copy-start.47 = (f32[576]{0:T(1024)S(1)}, f32[576]{0:T(1024)}, u32[]{:S(2)}) copy-start(f32[576]{0:T(1024)} %fusion.55) | copy-start | bytes 6916
  415.3 32.1 %slice-start.12 = ((s8[4718592]{0:T(1024)(128)(4,1)}), s8[524288]{0:T(1024)(128)(4,1)S(1)}, s32[]{:S(2)}) async-start(s8[4718592]{0:T(1024)(128)(4,1)} %bitcast.183), calls=%async_computation.12 | async-start | bytes 1048576
  474.4 22.7 %slice-start = ((s8[17694720]{0:T(1024)(128)(4,1)}), s8[4194304]{0:T(1024)(128)(4,1)S(1)}, s32[]{:S(2)}) async-start(s8[17694720]{0:T(1024)(128)(4,1)} %bitcast.152), calls=%async_computation | async-start | bytes 8388608
  474.4 22.7 %slice-start.1 = ((s8[17694720]{0:T(1024)(128)(4,1)}), s8[4194304]{0:T(1024)(128)(4,1)S(1)}, s32[]{:S(2)}) async-start(s8[17694720]{0:T(1024)(128)(4,1)} %bitcast.152), calls=%async_computation.1 | async-start | bytes 8388608
  474.4 22.7 %slice-start.2 = ((s8[17694720]{0:T(1024)(128)(4,1)}), s8[917504]{0:T(1024)(128)(4,1)S(1)}, s32[]{:S(2)}) async-start(s8[17694720]{0:T(1024)(128)(4,1)} %bitcast.152), calls=%async_computation.2 | async-start | bytes 1835008
  484.3 12.9 %slice-start.3 = ((s8[17694720]{0:T(1024)(128)(4,1)}), s8[4194304]{0:T(1024)(128)(4,1)S(1)}, s32[]{:S(2)}) async-start(s8[17694720]{0:T(1024)(128)(4,1)} %bitcast.152), calls=%async_computation.3 | async-start | bytes 8388608
  484.3 12.9 %slice-start.4 = ((s8[17694720]{0:T(1024)(128)(4,1)}), s8[4194304]{0:T(1024)(128)(4,1)S(1)}, s32[]{:S(2)}) async-start(s8[17694720]{0:T(1024)(128)(4,1)} %bitcast.152), calls=%async_computation.4 | async-start | bytes 8388608
  484.3 13.6 %copy-start.6 = (bf16[12,576,576]{1,2,0:T(8,128)(2,1)S(1)}, bf16[12,576,576]{1,2,0:T(8,128)(2,1)}, u32[]{:S(2)}) copy-start(bf16[12,576,576]{1,2,0:T(8,128)(2,1)} %convolution_convert_fusion) | copy-start | bytes 23887876
  522.9 34.1 %copy-start.25 = (f32[576,768]{1,0:T(8,128)}, f32[576,768]{1,0:T(8,128)S(1)}, u32[]{:S(2)}) copy-start(f32[576,768]{1,0:T(8,128)S(1)} %get-tuple-element.116) | copy-start | bytes 5308420
  577.6 13.1 %copy-start.51 = (s32[1024]{0:T(1024)S(1)}, s32[1024]{0:T(1024)}, u32[]{:S(2)}) copy-start(s32[1024]{0:T(1024)} %copy-done.50) | copy-start | bytes 12292
  625.2 11.4 %copy-start.53 = (pred[8]{0:T(512)(128)(4,1)S(1)}, pred[8]{0:T(512)(128)(4,1)}, u32[]{:S(2)}) copy-start(pred[8]{0:T(512)(128)(4,1)} %copy-done.52) | copy-start | bytes 28
  661.1 16.8 %copy-start.7 = (bf16[4,8,221328]{2,0,1:T(4,128)(2,1)S(1)}, bf16[4,8,221328]{2,0,1:T(4,128)(2,1)}, u32[]{:S(2)}) copy-start(bf16[4,8,221328]{2,0,1:T(4,128)(2,1)} %maximum_select_fusion.2) | copy-start | bytes 42494980
  666.6 11.4 %collective-permute-start.7 = (bf16[4,4,221328]{2,0,1:T(4,128)(2,1)S(1)}, bf16[4,4,221328]{2,0,1:T(4,128)(2,1)S(1)}, u32[]{:S(2)}, u32[]{:S(2)}) collective-permute-start(bf16[4,4,221328]{2,0,1:T(4,128)(2,1)S(1)} %slice.147), channel_id=1, source_target_pairs={{0,4},{4,0},{8,12},{12,8},{16,20},{20,16},{24,28},{28,24},{1,5},{5... | collective-permute-start | bytes 21247496 | tf_op jit(solution)/shard_map/ppermute | solution.py:105
  687.4 22.7 %collective-permute-start.8 = (bf16[4,221328]{1,0:T(4,128)(2,1)S(1)}, bf16[4,221328]{1,0:T(4,128)(2,1)}, u32[]{:S(2)}, u32[]{:S(2)}) collective-permute-start(bf16[4,221328]{1,0:T(4,128)(2,1)S(1)} %fusion.31), channel_id=1, source_target_pairs={{0,8},{4,20},{8,0},{12,28},{16,24},{20,4},{24,16},{28,12},{1,9},{5... | collective-permute-start | bytes 5311880 | tf_op jit(solution)/shard_map/ppermute | solution.py:107
  715.6 40.2 %collective-permute-start.9 = (bf16[4,221328]{1,0:T(4,128)(2,1)}, bf16[4,221328]{1,0:T(4,128)(2,1)}, u32[]{:S(2)}, u32[]{:S(2)}) collective-permute-start(bf16[4,221328]{1,0:T(4,128)(2,1)} %get-tuple-element.80), channel_id=1, source_target_pairs={{0,8},{4,12},{8,0},{12,4},{16,24},{20,28},{24,16},{28,20},{1,9},{5... | collective-permute-start | bytes 5311880 | tf_op jit(solution)/shard_map/ppermute | solution.py:114
  717.0 39.7 %collective-permute-start.10 = (bf16[4,221328]{1,0:T(4,128)(2,1)S(1)}, bf16[4,221328]{1,0:T(4,128)(2,1)}, u32[]{:S(2)}, u32[]{:S(2)}) collective-permute-start(bf16[4,221328]{1,0:T(4,128)(2,1)S(1)} %get-tuple-element.81), channel_id=1, source_target_pairs={{0,16},{4,20},{8,24},{12,28},{16,0},{20,4},{24,8},{28,12},{1,17},{... | collective-permute-start | bytes 5311880 | tf_op jit(solution)/shard_map/ppermute | solution.py:115
  772.2 34.0 %collective-permute-start.11 = (bf16[221328]{0:T(1024)(128)(2,1)}, bf16[221328]{0:T(1024)(128)(2,1)S(1)}, u32[]{:S(2)}, u32[]{:S(2)}) collective-permute-start(bf16[221328]{0:T(1024)(128)(2,1)} %get-tuple-element.54), channel_id=1, source_target_pairs={{0,1},{1,2},{2,3},{3,0},{4,5},{5,6},{6,7},{7,4},{8,9},{9,10},{10,1... | collective-permute-start | bytes 1327976 | tf_op jit(solution)/shard_map/ppermute | solution.py:120
  776.2 30.0 %collective-permute-start.13 = (bf16[221328]{0:T(1024)(128)(2,1)S(1)}, bf16[221328]{0:T(1024)(128)(2,1)S(1)}, u32[]{:S(2)}, u32[]{:S(2)}) collective-permute-start(bf16[221328]{0:T(1024)(128)(2,1)S(1)} %get-tuple-element.55), channel_id=1, source_target_pairs={{0,3},{1,0},{2,1},{3,2},{4,7},{5,4},{6,5},{7,6},{8,11},{9,8},{10,9... | collective-permute-start | bytes 1327976 | tf_op jit(solution)/shard_map/ppermute | solution.py:120
  778.1 34.6 %collective-permute-start.12 = (bf16[221328]{0:T(1024)(128)(2,1)S(1)}, bf16[221328]{0:T(1024)(128)(2,1)S(1)}, u32[]{:S(2)}, u32[]{:S(2)}) collective-permute-start(bf16[221328]{0:T(1024)(128)(2,1)S(1)} %get-tuple-element.56), channel_id=1, source_target_pairs={{0,2},{1,3},{2,0},{3,1},{4,6},{5,7},{6,4},{7,5},{8,10},{9,11},{10,... | collective-permute-start | bytes 1327976 | tf_op jit(solution)/shard_map/ppermute | solution.py:120
  813.0 19.8 %collective-permute-start.15 = (f32[221328]{0:T(1024)S(1)}, f32[221328]{0:T(1024)S(1)}, u32[]{:S(2)}, u32[]{:S(2)}) collective-permute-start(f32[221328]{0:T(1024)S(1)} %convert_add_fusion.2), channel_id=1, source_target_pairs={{0,16},{4,20},{8,24},{12,28},{16,0},{20,4},{24,8},{28,12},{1,17},{... | collective-permute-start | bytes 2655944 | tf_op jit(solution)/shard_map/ppermute | solution.py:51
  813.6 19.2 %collective-permute-start.14 = (f32[221328]{0:T(1024)S(1)}, f32[221328]{0:T(1024)S(1)}, u32[]{:S(2)}, u32[]{:S(2)}) collective-permute-start(f32[221328]{0:T(1024)S(1)} %convert_add_fusion.2), channel_id=1, source_target_pairs={{0,8},{4,12},{8,0},{12,4},{16,24},{20,28},{24,16},{28,20},{1,9},{5... | collective-permute-start | bytes 2655944 | tf_op jit(solution)/shard_map/ppermute | solution.py:50
  832.9 13.2 %collective-permute-start.16 = (f32[221328]{0:T(1024)S(1)}, f32[221328]{0:T(1024)S(1)}, u32[]{:S(2)}, u32[]{:S(2)}) collective-permute-start(f32[221328]{0:T(1024)S(1)} %broadcast_select_fusion.1), channel_id=1, source_target_pairs={{0,8},{4,20},{8,0},{12,28},{16,24},{20,4},{24,16},{28,12},{1,9},{5... | collective-permute-start | bytes 2655944 | tf_op jit(solution)/shard_map/ppermute | solution.py:53
  833.7 23.7 %slice-start.9 = ((s8[4718592]{0:T(1024)(128)(4,1)}), s8[4194304]{0:T(1024)(128)(4,1)S(1)}, s32[]{:S(2)}) async-start(s8[4718592]{0:T(1024)(128)(4,1)} %bitcast.179), calls=%async_computation.9 | async-start | bytes 8388608
  855.4 6.7 collective-permute-start.17
  (44 other events, 184.8 us)

commit v2 on v1

--- a/solution.py
+++ b/solution.py
@@ -33,15 +33,17 @@
 NDP_FAST = 8
 
 
-def _flat_pieces(mats, gains, d, ndp):
-    parts = []
-    for x in mats:
-        r = x.shape[0] // ndp
-        parts.append(lax.dynamic_slice_in_dim(x, d * r, r, 0).reshape(-1))
-    for g in gains:
-        r = g.shape[1] // ndp
-        parts.append(lax.dynamic_slice_in_dim(g, d * r, r, 1).reshape(-1))
-    return jnp.concatenate(parts)
+LANES = 128
+
+
+def _to_rows(v):
+    return v.reshape(-1, LANES)
+
+
+def _gain_rows(gains, pick):
+    flat = jnp.concatenate([pick(g).reshape(-1) for g in gains])
+    pad = (-flat.shape[0]) % LANES
+    return jnp.pad(flat, (0, pad)).reshape(-1, LANES)
 
 
 def _plane_gather(z):
@@ -58,31 +60,43 @@
     return jnp.stack([mine[0], sib[0], mine[1], sib[1], mine[2], sib[2], mine[3], sib[3]])
 
 
+def _take(x, idx, axis):
+    return jnp.take(x, idx, axis=axis, mode="wrap")
+
+
 def fast_gather(mats, gains):
     d = lax.axis_index("dp")
     f = lax.axis_index("fsdp")
-    own = _flat_pieces(mats, gains, d, NDP_FAST)
+    parts = []
+    for m in mats:
+        r = m.shape[0] // NDP_FAST
+        parts.append(_to_rows(lax.dynamic_slice_in_dim(m, d * r, r, 0)))
+    gr = gains[0].shape[1] // NDP_FAST
+    parts.append(_gain_rows(gains, lambda g: lax.dynamic_slice_in_dim(g, d * gr, gr, 1)))
+    own = jnp.concatenate(parts)
     slots = [own] + [
         lax.ppermute(own, "fsdp", [(i, (i + k) % NF_FAST) for i in range(NF_FAST)])
         for k in range(1, NF_FAST)
     ]
-    z = jnp.stack(slots)
-    x = _plane_gather(z)
+    x = _plane_gather(jnp.stack(slots))
     e_idx = jnp.arange(NDP_FAST, dtype=jnp.int32) ^ d
     f_idx = (f - jnp.arange(NF_FAST, dtype=jnp.int32)) % NF_FAST
-    x = jnp.take(jnp.take(x, e_idx, axis=0), f_idx, axis=1)
+    x = _take(_take(x, e_idx, 0), f_idx, 1)
     out = []
-    offset = 0
+    row = 0
     for m in mats:
         r, cols = m.shape[0] // NDP_FAST, m.shape[1]
-        seg = x[:, :, offset : offset + r * cols].reshape(NDP_FAST, NF_FAST, r, cols)
+        n_rows = r * cols // LANES
+        seg = x[:, :, row : row + n_rows].reshape(NDP_FAST, NF_FAST, r, cols)
         out.append(seg.transpose(1, 0, 2, 3).reshape(NF_FAST * m.shape[0], cols))
-        offset += r * cols
+        row += n_rows
+    flat = x[:, :, row:].reshape(NDP_FAST, NF_FAST, -1)
+    offset = 0
     for g in gains:
-        rows, r = g.shape[0], g.shape[1] // NDP_FAST
-        seg = x[:, :, offset : offset + rows * r].reshape(NDP_FAST, NF_FAST, rows, r)
+        rows = g.shape[0]
+        seg = flat[:, :, offset : offset + rows * gr].reshape(NDP_FAST, NF_FAST, rows, gr)
         out.append(seg.transpose(2, 1, 0, 3).reshape(rows, NF_FAST * g.shape[1]))
-        offset += rows * r
+        offset += rows * gr
     return out
 
 
@@ -90,20 +104,26 @@
     d = lax.axis_index("dp")
     f = lax.axis_index("fsdp")
     c = d % 2
+    n_shards = NF_FAST * NDP_FAST
     parts = []
     for m in mats:
-        rows, cols = m.shape
-        parts.append(m.astype(jnp.bfloat16).reshape(NF_FAST, NDP_FAST, -1))
-    for g in gains:
-        rows, cols = g.shape
-        r = cols // (NF_FAST * NDP_FAST)
-        seg = g.astype(jnp.bfloat16).reshape(rows, NF_FAST, NDP_FAST, r).transpose(1, 2, 0, 3)
-        parts.append(seg.reshape(NF_FAST, NDP_FAST, -1))
+        parts.append(m.astype(jnp.bfloat16).reshape(NF_FAST, NDP_FAST, -1, LANES))
+    gr = gains[0].shape[1] // n_shards
+    flat_g = jnp.concatenate(
+        [
+            g.astype(jnp.bfloat16).reshape(g.shape[0], NF_FAST, NDP_FAST, gr).transpose(1, 2, 0, 3)
+            .reshape(NF_FAST, NDP_FAST, -1)
+            for g in gains
+        ],
+        axis=2,
+    )
+    pad = (-flat_g.shape[2]) % LANES
+    parts.append(jnp.pad(flat_g, ((0, 0), (0, 0), (0, pad))).reshape(NF_FAST, NDP_FAST, -1, LANES))
     flat = jnp.concatenate(parts, axis=2)
-    e_idx = jnp.arange(NDP_FAST, dtype=jnp.int32) ^ d
-    bx = jnp.take(flat, e_idx, axis=1)
-    got = lax.ppermute(bx[:, 1::2], "dp", [(i, i ^ 1) for i in range(NDP_FAST)])
-    chip = bx[:, 0::2].astype(jnp.float32) + got.astype(jnp.float32)
+    home = _take(flat, jnp.array([0, 2, 4, 6], dtype=jnp.int32) ^ d, 1)
+    away = _take(flat, jnp.array([1, 3, 5, 7], dtype=jnp.int32) ^ d, 1)
+    got = lax.ppermute(away, "dp", [(i, i ^ 1) for i in range(NDP_FAST)])
+    chip = home.astype(jnp.float32) + got.astype(jnp.float32)
     moved = lax.ppermute(
         chip[:, 3].astype(jnp.bfloat16),
         "dp",
@@ -120,21 +140,22 @@
         total = total + lax.ppermute(
             part.astype(jnp.bfloat16), "fsdp", [(i, (i + k) % NF_FAST) for i in range(NF_FAST)]
         ).astype(jnp.float32)
-    x = _plane_gather(total)
-    x = jnp.take(x, e_idx, axis=0)
+    x = _take(_plane_gather(total), jnp.arange(NDP_FAST, dtype=jnp.int32) ^ d, 0)
     out = []
-    offset = 0
+    row = 0
     for m in mats:
         rows, cols = m.shape
-        r = rows // (NF_FAST * NDP_FAST)
-        out.append(x[:, offset : offset + r * cols].reshape(NDP_FAST * r, cols))
-        offset += r * cols
+        r = rows // n_shards
+        n_rows = r * cols // LANES
+        out.append(x[:, row : row + n_rows].reshape(NDP_FAST * r, cols))
+        row += n_rows
+    flat_out = x[:, row:].reshape(NDP_FAST, -1)
+    offset = 0
     for g in gains:
-        rows, cols = g.shape
-        r = cols // (NF_FAST * NDP_FAST)
-        seg = x[:, offset : offset + rows * r].reshape(NDP_FAST, rows, r)
-        out.append(seg.transpose(1, 0, 2).reshape(rows, NDP_FAST * r))
-        offset += rows * r
+        rows = g.shape[0]
+        seg = flat_out[:, offset : offset + rows * gr].reshape(NDP_FAST, rows, gr)
+        out.append(seg.transpose(1, 0, 2).reshape(rows, NDP_FAST * gr))
+        offset += rows * gr
     return out
 
 

time: 946 us -> 812 us (0.86)
  other arithmetic: 173 us -> 91.7 us
  local copies, waits for them, and re-layouts: 409 us -> 357 us
    select_n x6 -> x3, other arithmetic: 78.7 us -> 0.55 us  [_take(): return jnp.take(x, idx, axis=axis, mode='wrap')]
    gather x19 -> x11, local copies, waits for them, and re-layouts: 152 us -> 117 us  [_take(): return jnp.take(x, idx, axis=axis, mode='wrap')]
    another operation x2, local copies, waits for them, and re-layouts: 23.3 us -> 3.68 us  [_plane_gather(): jnp.stack([mine[0], sib[0], mine[1], sib[1], mine[2], sib[2], mine[3], si...]
    reshape x34 -> x29, local copies, waits for them, and re-layouts: 88.2 us -> 69.1 us  [the longest x4 29 us: fast_reduce(): parts.append(m.astype(jnp.bfloat16).reshape(NF_FAST, NDP_FAST, -1, LANES))]
    slice x11 -> x14, local copies, waits for them, and re-layouts: 24.3 us -> 40.8 us  [the longest x6 31.5 us: fast_gather(): seg = x[:, :, row:row + n_rows].reshape(NDP_FAST, NF_FAST, r, cols)]
    transpose x6 -> x10, local copies, waits for them, and re-layouts: 0.06 us -> 13.2 us  [the longest x4 13.2 us: fast_gather(): out.append(seg.transpose(1, 0, 2, 3).reshape(NF_FAST * m.shape[0], cols))]
    concatenate x1, other arithmetic: 13.1 us -> 0.08 us  [fast_gather(): own = jnp.concatenate(parts)]
    ppermute x2, waiting for transfers between devices: 21.1 us -> 33.6 us  [_plane_gather(): lax.ppermute(send, 'dp', [(i, i ^ 2) if i % 2 == 0 else (i, i ^ 4) for i...]
  transfers between devices with their start and end apart: 18 -> 18, of which waited for: 12 -> 13; matrix products, arithmetic and copies ran while one was open for 5% -> 6% of each run, Pallas kernels for 0% -> 0%
where the time goes in v2:
time: 812 us; the launch traced here: 800 us
  local copies, waits for them, and re-layouts  357 us (44%)
  waiting for transfers between devices  203 us (25%)
  matrix products  119 us (15%)
  other arithmetic  91.7 us (11%)
  starting transfers between devices  26.9 us (3%)
    gather x11, local copies, waits for them, and re-layouts, _take(): return jnp.take(x, idx, axis=axis, mode='wrap')  117 us
    unnamed x161, local copies, waits for them, and re-layouts  53.5 us
    ppermute x2, waiting for transfers between devices, _plane_gather(): b = lax.ppermute(z, 'dp', [(i, i ^ 4) for i in range(NDP_FAST)])  52.3 us
    ppermute x1, waiting for transfers between devices, fast_reduce(): lax.ppermute(to_x.astype(jnp.bfloat16), 'dp', [(i, i ^ 2) for i in range(...  37.2 us
    ppermute x2, waiting for transfers between devices, _plane_gather(): lax.ppermute(send, 'dp', [(i, i ^ 2) if i % 2 == 0 else (i, i ^ 4) for i...  33.6 us
    slice x6, local copies, waits for them, and re-layouts, fast_gather(): seg = x[:, :, row:row + n_rows].reshape(NDP_FAST, NF_FAST, r, cols)  31.5 us
    ppermute x3, waiting for transfers between devices, fast_reduce(): lax.ppermute(part.astype(jnp.bfloat16), 'fsdp', [(i, (i + k) % NF_FAST) f...  29.2 us
    reshape x4, local copies, waits for them, and re-layouts, fast_reduce(): parts.append(m.astype(jnp.bfloat16).reshape(NF_FAST, NDP_FAST, -1, LANES))  29 us
  transfers between devices with their start and end apart: 18, of which 13 were waited for; matrix products, arithmetic and copies ran while one was open for 6% of the time, Pallas kernels for 0%

profile of v2, /device:TPU:8, one launch (start us, length us, event | category | flops | bytes accessed | tf_op | source)
XLA Modules:
  0.0 800.1 jit_solution(13606292181812729402)
XLA Ops:
  11.3 6.8 copy.295
  18.2 19.8 %collective-permute-done.2 = bf16[1730,128]{1,0:T(8,128)(2,1)S(1)} collective-permute-done((bf16[1730,128]{1,0:T(8,128)(2,1)S(1)}, bf16[1730,128]{1,0:T(8,128)(2,1)S(1)}, u32[]{:S(2)}, u32[]{:S(2)}) %collective-permute-start.2) | collective-permute-done | bytes 442912 | tf_op jit(solution)/shard_map/ppermute | solution.py:78
  38.0 6.8 copy.298
  44.8 6.9 copy.297
  51.7 7.1 copy.296
  67.2 33.1 %collective-permute-done.4 = bf16[4,1730,128]{2,0,1:T(4,128)(2,1)S(1)} collective-permute-done((bf16[4,1730,128]{2,0,1:T(4,128)(2,1)}, bf16[4,1730,128]{2,0,1:T(4,128)(2,1)S(1)}, u32[]{:S(2)}, u32[]{:S(2)}) %collective-permute-start.4) | collective-permute-done | bytes 1771552 | tf_op jit(solution)/shard_map/ppermute | solution.py:53
  102.6 21.1 %collective-permute-done.5 = bf16[4,1730,128]{2,0,1:T(4,128)(2,1)S(1)} collective-permute-done((bf16[4,1730,128]{2,0,1:T(4,128)(2,1)S(1)}, bf16[4,1730,128]{2,0,1:T(4,128)(2,1)S(1)}, u32[]{:S(2)}, u32[]{:S(2)}) %collective-permute-start.5) | collective-permute-done | bytes 1771552 | tf_op jit(solution)/shard_map/ppermute | solution.py:55
  123.7 10.1 %pad_maximum_fusion = bf16[4,4,1730,128]{3,1,2,0:T(4,128)(2,1)} fusion(bf16[1,4,1730,128]{3,1,2,0:T(4,128)(2,1)S(1)} %bitcast.211, bf16[1,4,1730,128]{3,1,2,0:T(4,128)(2,1)S(1)} %bitcast.205, bf16[1,4,1730,128]{3,1,2,0:T(4,128)(2,1)} %bitcast.8, bf16[1,4,1730,128]{3,1,2,0:T(4,128)(2,1)} %bitcast.7), kind=kLoop, calls=%fused_computation.22 | loop fusion | flops 10629120 | bytes 14172160 | tf_op jit(solution)/shard_map/stack | solution.py:58
  162.1 19.1 %gather_fusion = bf16[8,4,1730,128]{3,1,2,0:T(4,128)(2,1)} fusion(bf16[8,4,1730,128]{3,1,2,0:T(4,128)(2,1)} %slice_dynamic-update-slice_fusion, s32[1024]{0:T(1024)S(1)} %pad_clamp_fusion.3), kind=kCustom, calls=%fused_computation.2 | custom fusion | bytes 28344352 | tf_op jit(solution)/shard_map/jit(_take)/gather | solution.py:64
  181.3 8.1 %mini-gather-slice.2 = bf16[8,4,834,128]{3,1,2,0:T(4,128)(2,1)} slice(bf16[8,4,1730,128]{3,1,2,0:T(4,128)(2,1)} %gather_fusion), slice={[0:8], [0:4], [896:1730], [0:128]} | slice | bytes 13664256 | tf_op jit(solution)/shard_map/jit(_take)/gather | solution.py:64
  189.3 8.5 %mini-gather-slice.3 = bf16[8,4,896,128]{3,1,2,0:T(4,128)(2,1)} slice(bf16[8,4,1730,128]{3,1,2,0:T(4,128)(2,1)} %gather_fusion), slice={[0:8], [0:4], [0:896], [0:128]} | slice | bytes 14680064 | tf_op jit(solution)/shard_map/jit(_take)/gather | solution.py:64
  197.9 12.2 %copy.301 = bf16[8,4,896,128]{2,3,0,1:T(8,128)(2,1)} copy(bf16[8,4,896,128]{3,1,2,0:T(4,128)(2,1)} %mini-gather-slice.3) | data formatting | bytes 14680064 | tf_op jit(solution)/shard_map/jit(_take)/gather | solution.py:64
  210.1 12.5 %copy.299 = bf16[8,4,834,128]{2,3,0,1:T(8,128)(2,1)} copy(bf16[8,4,834,128]{3,1,2,0:T(4,128)(2,1)} %mini-gather-slice.2) | data formatting | bytes 13664256 | tf_op jit(solution)/shard_map/jit(_take)/gather | solution.py:64
  222.6 7.4 gather_fusion.2
  230.0 7.5 gather_fusion.3
  243.0 11.5 %fusion.88 = (bf16[8,4,576,128]{2,3,0,1:T(8,128)(2,1)}, bf16[8,4,576,128]{2,3,0,1:T(8,128)(2,1)}) fusion(bf16[8,4,834,128]{2,3,0,1:T(8,128)(2,1)} %bitcast.196, bf16[8,4,896,128]{2,3,0,1:T(8,128)(2,1)} %bitcast.193), kind=kLoop, calls=%fused_computation.247 | loop fusion | flops 9437184 | bytes 29360128 | tf_op jit(solution)/shard_map/slice | solution.py:90
  267.7 7.6 reshape.517
  290.7 7.7 copy.312
  298.4 9.2 %reshape.525 = bf16[8,4,96,768]{3,2,1,0:T(8,128)(2,1)} reshape(bf16[8,4,576,128]{3,2,1,0:T(8,128)(2,1)} %copy.312) | data formatting | bytes 9437184 | tf_op jit(solution)/shard_map/reshape | solution.py:90
  312.5 7.7 copy.310
  320.2 8.2 %reshape.523 = bf16[8,4,24,3072]{3,2,1,0:T(8,128)(2,1)} reshape(bf16[8,4,576,128]{3,2,1,0:T(8,128)(2,1)} %copy.310) | data formatting | bytes 9437184 | tf_op jit(solution)/shard_map/reshape | solution.py:90
  341.5 8.3 %fusion.93 = (f32[12,576]{1,0:T(8,128)S(1)}, f32[12,576,576]{1,2,0:T(8,128)}) fusion(f32[576,12,64]{0,2,1:T(8,128)S(1)} %bitcast.188, f32[12,64]{1,0:T(8,128)S(1)} %mul.337, f32[576,12]{0,1:T(8,128)S(1)} %fusion.56, f32[576,12]{0,1:T(8,128)S(1)} %broadcast_multiply_fusion, f32[576,12,64]{0,2,1:T(8,128)S(1)} %bitcast.180, f32[12,64]{1,0:T(8,128)S(1)} %mul.331, ...), kind=kOutput, calls=%fused_computation.252 | convolution fusion | flops 525083904 | bytes 19940352 | tf_op jit(solution)/shard_map/while/body/eval_jaxpr/qhd,khd->hqk/dot_general | solution.py:205
  349.8 8.5 %fusion.3 = f32[12,576]{1,0:T(8,128)S(1)} fusion(f32[12,576,576]{1,2,0:T(8,128)} %get-tuple-element.107, f32[12,576]{1,0:T(8,128)S(1)} %get-tuple-element.106), kind=kLoop, calls=%fused_computation.15 | loop fusion | flops 7955712 | bytes 15980544 | tf_op jit(solution)/shard_map/while/body/eval_jaxpr/reduce_sum | solution.py:215
  358.4 9.7 %fusion.38 = bf16[12,64,576]{2,1,0:T(8,128)(2,1)S(1)} fusion(bf16[576,12,64]{0,2,1:T(8,128)(2,1)} %bitcast.223, f32[12,576,576]{1,2,0:T(8,128)} %get-tuple-element.107, f32[12,576]{1,0:T(8,128)S(1)} %fusion.3, f32[12,576]{1,0:T(8,128)S(1)} %get-tuple-element.106), kind=kOutput, calls=%fused_computation.113 | convolution fusion | flops 521994240 | bytes 17750016 | tf_op jit(solution)/shard_map/while/body/eval_jaxpr/hqk,khd->qhd/dot_general | solution.py:217
  369.6 22.7 %multiply_convert_fusion = (bf16[576,3072]{1,0:T(8,128)(2,1)}, f32[576,3072]{1,0:T(8,128)}, f32[576,3072]{1,0:T(8,128)}) fusion(bf16[768,3072]{1,0:T(8,128)(2,1)} %bitcast.218, f32[576,768]{1,0:T(8,128)S(1)} %get-tuple-element.109, f32[768]{0:T(1024)S(1)} %add.226, f32[768]{0:T(1024)S(1)} %mul.344, f32[576]{0:T(1024)S(1)} %fusion.65, ...), kind=kOutput, calls=%fused_computation.25 | convolution fusion | flops 2835136512 | bytes 24193536 | tf_op jit(solution)/shard_map/dot_general | solution.py:227
  392.3 9.3 %add_convert_fusion = bf16[576,3072]{1,0:T(8,128)(2,1)} fusion(f32[576,3072]{1,0:T(8,128)} %get-tuple-element.82, f32[576,3072]{1,0:T(8,128)} %get-tuple-element.110, bf16[3072,768]{1,0:T(8,128)(2,1)S(1)} %bitcast.214, bf16[576,768]{1,0:T(8,128)(2,1)S(1)} %copy-done.22, f32[576]{0:T(1024)S(1)} %copy-done.40), kind=kOutput, calls=%fused_computation.24 | convolution fusion | flops 2744008704 | bytes 23300352 | tf_op jit(solution)/shard_map/dot_general | solution.py:236
  421.1 7.6 convolution_convert_fusion
  428.7 9.9 %fusion.39 = bf16[12,64,576]{2,1,0:T(8,128)(2,1)} fusion(bf16[576,12,64]{0,2,1:T(8,128)(2,1)S(1)} %bitcast.208, f32[12,576,576]{1,2,0:T(8,128)} %get-tuple-element.107, f32[12,576]{1,0:T(8,128)S(1)} %log_add_fusion), kind=kOutput, calls=%fused_computation.114 | convolution fusion | flops 518012928 | bytes 17722368 | tf_op jit(solution)/shard_map/while/body/eval_jaxpr/hqk,qhd->khd/dot_general | solution.py:253
  438.6 12.9 %fusion = f32[12,576]{1,0:T(8,128)S(1)} fusion(bf16[12,576,576]{1,2,0:T(8,128)(2,1)} %convolution_convert_fusion, f32[12,576,576]{1,2,0:T(8,128)} %get-tuple-element.107, f32[12,576]{1,0:T(8,128)S(1)} %log_add_fusion), kind=kLoop, calls=%fused_computation.8 | loop fusion | flops 15918336 | bytes 23943168 | tf_op jit(solution)/shard_map/while/body/eval_jaxpr/reduce_sum | solution.py:256
  458.2 8.2 %fusion.29 = (f32[576,12]{0,1:T(8,128)S(1)}, f32[12,64,576]{2,1,0:T(8,128)}) fusion(f32[576,12,64]{0,2,1:T(8,128)} %bitcast.187, f32[12,64]{1,0:T(8,128)S(1)} %copy-done.33, f32[576,12]{0,1:T(8,128)S(1)} %broadcast_multiply_fusion, bf16[12,576,576]{1,2,0:T(8,128)(2,1)} %fusion.2, f32[576,12,64]{0,2,1:T(8,128)S(1)} %bitcast.181, f32[12,64]{1,0:T(8,128)S(1)} %mul.331, ...), kind=kOutput, calls=%fused_computation.80 | convolution fusion | flops 513139968 | bytes 13387776 | tf_op jit(solution)/shard_map/while/body/eval_jaxpr/hqk,qhd->khd/dot_general | solution.py:262
  477.0 7.4 convolution_convert_fusion.1
  484.4 8.3 %reshape.532 = bf16[4,8,576,128]{3,2,1,0:T(8,128)(2,1)} reshape(bf16[768,3072]{1,0:T(8,128)(2,1)} %convolution_convert_fusion.3) | data formatting | bytes 9437184 | tf_op jit(solution)/shard_map/reshape | solution.py:110
  496.2 8.4 %convolution_convert_fusion.2 = bf16[3072,768]{1,0:T(8,128)(2,1)} fusion(bf16[576,3072]{1,0:T(8,128)(2,1)} %get-tuple-element.81, bf16[576,768]{1,0:T(8,128)(2,1)} %param.23, f32[576]{0:T(1024)S(1)} %copy-done.40), kind=kOutput, calls=%fused_computation.42 | convolution fusion | flops 2721595392 | bytes 9144576 | tf_op jit(solution)/shard_map/dot_general | solution.py:235
  504.6 9.2 %reshape.533 = bf16[4,8,576,128]{3,2,1,0:T(8,128)(2,1)} reshape(bf16[3072,768]{1,0:T(8,128)(2,1)} %convolution_convert_fusion.2) | data formatting | bytes 9437184 | tf_op jit(solution)/shard_map/reshape | solution.py:110
  515.5 8.1 %reshape.530 = bf16[4,8,432,128]{3,2,1,0:T(8,128)(2,1)} reshape(bf16[768,2304]{1,0:T(8,128)(2,1)} %convolution_convert_fusion.1) | data formatting | bytes 7077888 | tf_op jit(solution)/shard_map/reshape | solution.py:110
  523.7 6.7 copy_dynamic-update-slice_fusion.2
  544.8 13.4 %gather_fusion.5 = bf16[4,4,1730,128]{3,1,2,0:T(4,128)(2,1)} fusion(bf16[4,8,1730,128]{3,0,2,1:T(4,128)(2,1)} %constant_dynamic-update-slice_fusion.9, s32[1024]{0:T(1024)} %pad_clamp_fusion), kind=kCustom, calls=%fused_computation.1.clone | custom fusion | bytes 14172176 | tf_op jit(solution)/shard_map/jit(_take)/gather | solution.py:64
  558.2 8.4 %copy.327 = bf16[4,4,1730,128]{3,1,2,0:T(4,128)(2,1)} copy(bf16[4,4,1730,128]{3,0,2,1:T(4,128)(2,1)} %bitcast.197) | data formatting | bytes 14172160 | tf_op jit(solution)/shard_map/jit(_take)/gather | solution.py:64
  566.8 13.2 %gather_fusion.4 = bf16[4,4,1730,128]{3,1,2,0:T(4,128)(2,1)} fusion(bf16[4,8,1730,128]{3,0,2,1:T(4,128)(2,1)} %constant_dynamic-update-slice_fusion.9, s32[1024]{0:T(1024)S(1)} %pad_clamp_fusion.1), kind=kCustom, calls=%fused_computation.clone | custom fusion | bytes 14172176 | tf_op jit(solution)/shard_map/jit(_take)/gather | solution.py:64
  579.9 9.7 %convert_add_fusion = f32[4,4,1730,128]{3,0,2,1:T(4,128)S(1)} fusion(bf16[4,4,1730,128]{3,1,2,0:T(4,128)(2,1)} %gather_fusion.4, bf16[4,4,1730,128]{3,1,2,0:T(4,128)(2,1)} %collective-permute-done.7), kind=kLoop, calls=%fused_computation.16 | loop fusion | flops 10629120 | bytes 28344320 | tf_op jit(solution)/shard_map/add | solution.py:126
  597.6 21.4 %collective-permute-done.8 = bf16[4,1730,128]{2,0,1:T(4,128)(2,1)} collective-permute-done((bf16[4,1730,128]{2,0,1:T(4,128)(2,1)}, bf16[4,1730,128]{2,0,1:T(4,128)(2,1)}, u32[]{:S(2)}, u32[]{:S(2)}) %collective-permute-start.8) | collective-permute-done | bytes 1771552 | tf_op jit(solution)/shard_map/ppermute | solution.py:127
  628.3 37.2 %collective-permute-done.9 = bf16[4,1730,128]{2,0,1:T(4,128)(2,1)} collective-permute-done((bf16[4,1730,128]{2,0,1:T(4,128)(2,1)}, bf16[4,1730,128]{2,0,1:T(4,128)(2,1)}, u32[]{:S(2)}, u32[]{:S(2)}) %collective-permute-start.9) | collective-permute-done | bytes 1771552 | tf_op jit(solution)/shard_map/ppermute | solution.py:134
  674.8 7.0 collective-permute-start.13
  685.9 19.0 %collective-permute-done.12 = bf16[1730,128]{1,0:T(8,128)(2,1)} collective-permute-done((bf16[1730,128]{1,0:T(8,128)(2,1)}, bf16[1730,128]{1,0:T(8,128)(2,1)}, u32[]{:S(2)}, u32[]{:S(2)}) %collective-permute-start.12) | collective-permute-done | bytes 442912 | tf_op jit(solution)/shard_map/ppermute | solution.py:140
  704.8 10.2 %collective-permute-done.13 = bf16[1730,128]{1,0:T(8,128)(2,1)} collective-permute-done((bf16[1730,128]{1,0:T(8,128)(2,1)}, bf16[1730,128]{1,0:T(8,128)(2,1)}, u32[]{:S(2)}, u32[]{:S(2)}) %collective-permute-start.13) | collective-permute-done | bytes 442912 | tf_op jit(solution)/shard_map/ppermute | solution.py:140
  719.5 19.2 %collective-permute-done.15 = f32[1730,128]{1,0:T(8,128)S(1)} collective-permute-done((f32[1730,128]{1,0:T(8,128)S(1)}, f32[1730,128]{1,0:T(8,128)S(1)}, u32[]{:S(2)}, u32[]{:S(2)}) %collective-permute-start.15) | collective-permute-done | bytes 885792 | tf_op jit(solution)/shard_map/ppermute | solution.py:53
  741.0 12.5 %collective-permute-done.16 = f32[1730,128]{1,0:T(8,128)S(1)} collective-permute-done((f32[1730,128]{1,0:T(8,128)S(1)}, f32[1730,128]{1,0:T(8,128)S(1)}, u32[]{:S(2)}, u32[]{:S(2)}) %collective-permute-start.16) | collective-permute-done | bytes 885792 | tf_op jit(solution)/shard_map/ppermute | solution.py:55
  775.5 7.1 gather_fusion.1
  (344 shorter events, 235.7 us)
Async XLA Ops:
  5.8 32.1 %collective-permute-start.2 = (bf16[1730,128]{1,0:T(8,128)(2,1)S(1)}, bf16[1730,128]{1,0:T(8,128)(2,1)S(1)}, u32[]{:S(2)}, u32[]{:S(2)}) collective-permute-start(bf16[1730,128]{1,0:T(8,128)(2,1)S(1)} %constant_dynamic-update-slice_fusion), channel_id=1, source_target_pairs={{0,3},{1,0},{2,1},{3,2},{4,7},{5,4},{6,5},{7,6},{8,11},{9,8},{10,9... | collective-permute-start | bytes 1328648 | tf_op jit(solution)/shard_map/ppermute | solution.py:78
  5.8 39.0 %collective-permute-start.1 = (bf16[1730,128]{1,0:T(8,128)(2,1)S(1)}, bf16[1730,128]{1,0:T(8,128)(2,1)S(1)}, u32[]{:S(2)}, u32[]{:S(2)}) collective-permute-start(bf16[1730,128]{1,0:T(8,128)(2,1)S(1)} %constant_dynamic-update-slice_fusion), channel_id=1, source_target_pairs={{0,2},{1,3},{2,0},{3,1},{4,6},{5,7},{6,4},{7,5},{8,10},{9,11},{10,... | collective-permute-start | bytes 1328648 | tf_op jit(solution)/shard_map/ppermute | solution.py:78
  8.9 42.8 %collective-permute-start = (bf16[1730,128]{1,0:T(8,128)(2,1)S(1)}, bf16[1730,128]{1,0:T(8,128)(2,1)S(1)}, u32[]{:S(2)}, u32[]{:S(2)}) collective-permute-start(bf16[1730,128]{1,0:T(8,128)(2,1)S(1)} %constant_dynamic-update-slice_fusion), channel_id=1, source_target_pairs={{0,1},{1,2},{2,3},{3,0},{4,5},{5,6},{6,7},{7,4},{8,9},{9,10},{10,1... | collective-permute-start | bytes 1328648 | tf_op jit(solution)/shard_map/ppermute | solution.py:78
  64.3 36.1 %collective-permute-start.4 = (bf16[4,1730,128]{2,0,1:T(4,128)(2,1)}, bf16[4,1730,128]{2,0,1:T(4,128)(2,1)S(1)}, u32[]{:S(2)}, u32[]{:S(2)}) collective-permute-start(bf16[4,1730,128]{2,0,1:T(4,128)(2,1)} %get-tuple-element.84), channel_id=1, source_target_pairs={{0,16},{4,20},{8,24},{12,28},{16,0},{20,4},{24,8},{28,12},{1,17},{... | collective-permute-start | bytes 5314568 | tf_op jit(solution)/shard_map/ppermute | solution.py:53
  65.8 34.8 %collective-permute-start.3 = (bf16[4,1730,128]{2,0,1:T(4,128)(2,1)}, bf16[4,1730,128]{2,0,1:T(4,128)(2,1)}, u32[]{:S(2)}, u32[]{:S(2)}) collective-permute-start(bf16[4,1730,128]{2,0,1:T(4,128)(2,1)} %get-tuple-element.84), channel_id=1, source_target_pairs={{0,8},{4,12},{8,0},{12,4},{16,24},{20,28},{24,16},{28,20},{1,9},{5... | collective-permute-start | bytes 5314568 | tf_op jit(solution)/shard_map/ppermute | solution.py:52
  101.0 22.6 %collective-permute-start.5 = (bf16[4,1730,128]{2,0,1:T(4,128)(2,1)S(1)}, bf16[4,1730,128]{2,0,1:T(4,128)(2,1)S(1)}, u32[]{:S(2)}, u32[]{:S(2)}) collective-permute-start(bf16[4,1730,128]{2,0,1:T(4,128)(2,1)S(1)} %bitcast.229), channel_id=1, source_target_pairs={{0,8},{4,20},{8,0},{12,28},{16,24},{20,4},{24,16},{28,12},{1,9},{5... | collective-permute-start | bytes 5314568 | tf_op jit(solution)/shard_map/ppermute | solution.py:55
  123.7 10.1 %copy-start.14 = (bf16[4,1730,128]{2,0,1:T(4,128)(2,1)}, bf16[4,1730,128]{2,0,1:T(4,128)(2,1)S(1)}, u32[]{:S(2)}) copy-start(bf16[4,1730,128]{2,0,1:T(4,128)(2,1)S(1)} %collective-permute-done.5) | copy-start | bytes 5314564
  123.7 10.1 %copy-start.48 = (s32[1,9]{1,0:T(1,128)S(1)}, s32[1,9]{1,0:T(1,128)}, u32[]{:S(2)}) copy-start(s32[1,9]{1,0:T(1,128)} %param.15) | copy-start | bytes 112
  123.7 12.2 %copy-start.47 = (s32[4]{0:T(128)S(1)}, s32[4]{0:T(128)}, u32[]{:S(2)}) copy-start(s32[4]{0:T(128)} %constant.272.clone) | copy-start | bytes 52
  123.7 13.4 %copy-start.12 = (bf16[576,768]{1,0:T(8,128)(2,1)S(1)}, bf16[576,768]{1,0:T(8,128)(2,1)}, u32[]{:S(2)}) copy-start(bf16[576,768]{1,0:T(8,128)(2,1)} %param.14) | copy-start | bytes 2654212
  133.7 11.6 %collective-permute-start.6 = (bf16[4,4,1730,128]{3,1,2,0:T(4,128)(2,1)}, bf16[4,4,1730,128]{3,1,2,0:T(4,128)(2,1)}, u32[]{:S(2)}, u32[]{:S(2)}) collective-permute-start(bf16[4,4,1730,128]{3,1,2,0:T(4,128)(2,1)} %pad_maximum_fusion), channel_id=1, source_target_pairs={{0,4},{4,0},{8,12},{12,8},{16,20},{20,16},{24,28},{28,24},{1,5},{5... | collective-permute-start | bytes 21258248 | tf_op jit(solution)/shard_map/ppermute | solution.py:59
  135.8 26.3 %copy-start.43 = (s32[1024]{0:T(1024)}, s32[1024]{0:T(1024)S(1)}, u32[]{:S(2)}) copy-start(s32[1024]{0:T(1024)S(1)} %pad_clamp_fusion.3) | copy-start | bytes 12292
  137.2 140.2 %copy-start.34 = (f32[576]{0:T(1024)}, f32[576]{0:T(1024)S(1)}, u32[]{:S(2)}) copy-start(f32[576]{0:T(1024)S(1)} %broadcast_multiply_fusion.5) | copy-start | bytes 6916
  137.7 13.2 %copy-start.36 = (f32[576]{0:T(1024)}, f32[576]{0:T(1024)S(1)}, u32[]{:S(2)}) copy-start(f32[576]{0:T(1024)S(1)} %fusion.35) | copy-start | bytes 6916
  137.7 139.8 %copy-start.41 = (f32[576]{0:T(1024)}, f32[576]{0:T(1024)S(1)}, u32[]{:S(2)}) copy-start(f32[576]{0:T(1024)S(1)} %fusion.64) | copy-start | bytes 6916
  261.1 16.4 %copy-start.44 = (f32[768]{0:T(1024)}, f32[768]{0:T(1024)S(1)}, u32[]{:S(2)}) copy-start(f32[768]{0:T(1024)S(1)} %add.219) | copy-start | bytes 9220
  261.4 16.2 %copy-start.38 = (f32[768]{0:T(1024)}, f32[768]{0:T(1024)S(1)}, u32[]{:S(2)}) copy-start(f32[768]{0:T(1024)S(1)} %mul.325) | copy-start | bytes 9220
  340.3 9.6 %copy-start.30 = (f32[576,12]{0,1:T(8,128)}, f32[576,12]{0,1:T(8,128)S(1)}, u32[]{:S(2)}) copy-start(f32[576,12]{0,1:T(8,128)S(1)} %multiply_reduce_fusion.1) | copy-start | bytes 82948
  358.4 9.8 %copy-start.25 = (bf16[4,8,24,768]{3,2,1,0:T(8,128)(2,1)S(1)}, bf16[4,8,24,768]{3,2,1,0:T(8,128)(2,1)}, u32[]{:S(2)}) copy-start(bf16[4,8,24,768]{3,2,1,0:T(8,128)(2,1)} %copy.309) | copy-start | bytes 3538948
  368.1 24.1 %slice-start.11 = ((s8[4718592]{0:T(1024)(128)(4,1)}), s8[4194304]{0:T(1024)(128)(4,1)S(1)}, s32[]{:S(2)}) async-start(s8[4718592]{0:T(1024)(128)(4,1)} %bitcast.212), calls=%async_computation.11 | async-start | bytes 8388608
  368.1 33.5 %slice-start.15 = ((s8[4718592]{0:T(1024)(128)(4,1)}), s8[4194304]{0:T(1024)(128)(4,1)S(1)}, s32[]{:S(2)}) async-start(s8[4718592]{0:T(1024)(128)(4,1)} %bitcast.219), calls=%async_computation.15 | async-start | bytes 8388608
  369.2 44.1 %copy-start.16 = (f32[576,768]{1,0:T(8,128)}, f32[576,768]{1,0:T(8,128)S(1)}, u32[]{:S(2)}) copy-start(f32[576,768]{1,0:T(8,128)S(1)} %get-tuple-element.109) | copy-start | bytes 5308420
  369.5 22.7 %slice-start.12 = ((s8[4718592]{0:T(1024)(128)(4,1)}), s8[524288]{0:T(1024)(128)(4,1)S(1)}, s32[]{:S(2)}) async-start(s8[4718592]{0:T(1024)(128)(4,1)} %bitcast.212), calls=%async_computation.12 | async-start | bytes 1048576
  369.5 22.7 %copy-start.22 = (bf16[576,768]{1,0:T(8,128)(2,1)S(1)}, bf16[576,768]{1,0:T(8,128)(2,1)}, u32[]{:S(2)}) copy-start(bf16[576,768]{1,0:T(8,128)(2,1)} %param.23) | copy-start | bytes 2654212
  369.6 22.7 %copy-start.40 = (f32[576]{0:T(1024)S(1)}, f32[576]{0:T(1024)}, u32[]{:S(2)}) copy-start(f32[576]{0:T(1024)} %fusion.63) | copy-start | bytes 6916
  369.6 32.0 %slice-start.16 = ((s8[4718592]{0:T(1024)(128)(4,1)}), s8[524288]{0:T(1024)(128)(4,1)S(1)}, s32[]{:S(2)}) async-start(s8[4718592]{0:T(1024)(128)(4,1)} %bitcast.219), calls=%async_computation.16 | async-start | bytes 1048576
  428.7 22.8 %slice-start = ((s8[17694720]{0:T(1024)(128)(4,1)}), s8[4194304]{0:T(1024)(128)(4,1)S(1)}, s32[]{:S(2)}) async-start(s8[17694720]{0:T(1024)(128)(4,1)} %bitcast.176), calls=%async_computation | async-start | bytes 8388608
  428.7 22.8 %slice-start.1 = ((s8[17694720]{0:T(1024)(128)(4,1)}), s8[4194304]{0:T(1024)(128)(4,1)S(1)}, s32[]{:S(2)}) async-start(s8[17694720]{0:T(1024)(128)(4,1)} %bitcast.176), calls=%async_computation.1 | async-start | bytes 8388608
  428.7 22.8 %slice-start.2 = ((s8[17694720]{0:T(1024)(128)(4,1)}), s8[917504]{0:T(1024)(128)(4,1)S(1)}, s32[]{:S(2)}) async-start(s8[17694720]{0:T(1024)(128)(4,1)} %bitcast.176), calls=%async_computation.2 | async-start | bytes 1835008
  438.6 12.9 %slice-start.3 = ((s8[17694720]{0:T(1024)(128)(4,1)}), s8[4194304]{0:T(1024)(128)(4,1)S(1)}, s32[]{:S(2)}) async-start(s8[17694720]{0:T(1024)(128)(4,1)} %bitcast.176), calls=%async_computation.3 | async-start | bytes 8388608
  438.6 12.9 %slice-start.4 = ((s8[17694720]{0:T(1024)(128)(4,1)}), s8[4194304]{0:T(1024)(128)(4,1)S(1)}, s32[]{:S(2)}) async-start(s8[17694720]{0:T(1024)(128)(4,1)} %bitcast.176), calls=%async_computation.4 | async-start | bytes 8388608
  438.6 13.6 %copy-start.6 = (bf16[12,576,576]{1,2,0:T(8,128)(2,1)S(1)}, bf16[12,576,576]{1,2,0:T(8,128)(2,1)}, u32[]{:S(2)}) copy-start(bf16[12,576,576]{1,2,0:T(8,128)(2,1)} %convolution_convert_fusion) | copy-start | bytes 23887876
  458.2 8.3 %copy-start.4 = (f32[576,768]{0,1:T(8,128)S(1)}, f32[576,768]{0,1:T(8,128)}, u32[]{:S(2)}) copy-start(f32[576,768]{0,1:T(8,128)} %copy-done.2) | copy-start | bytes 5308420
  504.6 9.6 %copy-start.37 = (f32[576]{0:T(1024)S(1)}, f32[576]{0:T(1024)}, u32[]{:S(2)}) copy-start(f32[576]{0:T(1024)} %copy-done.36) | copy-start | bytes 6916
  515.5 16.9 %slice-start.7 = ((s8[4718592]{0:T(1024)(128)(4,1)}), s8[524288]{0:T(1024)(128)(4,1)S(1)}, s32[]{:S(2)}) async-start(s8[4718592]{0:T(1024)(128)(4,1)} %bitcast.198), calls=%async_computation.7 | async-start | bytes 1048576
  523.7 8.7 %slice-start.8 = ((s8[4718592]{0:T(1024)(128)(4,1)}), s8[4194304]{0:T(1024)(128)(4,1)S(1)}, s32[]{:S(2)}) async-start(s8[4718592]{0:T(1024)(128)(4,1)} %bitcast.198), calls=%async_computation.8 | async-start | bytes 8388608
  558.2 8.5 %copy-start.46 = (s32[4]{0:T(128)S(1)}, s32[4]{0:T(128)}, u32[]{:S(2)}) copy-start(s32[4]{0:T(128)} %get-tuple-element.119) | copy-start | bytes 52
  566.6 13.3 %collective-permute-start.7 = (bf16[4,4,1730,128]{3,1,2,0:T(4,128)(2,1)}, bf16[4,4,1730,128]{3,1,2,0:T(4,128)(2,1)}, u32[]{:S(2)}, u32[]{:S(2)}) collective-permute-start(bf16[4,4,1730,128]{3,1,2,0:T(4,128)(2,1)} %copy.327), channel_id=1, source_target_pairs={{0,4},{4,0},{8,12},{12,8},{16,20},{20,16},{24,28},{28,24},{1,5},{5... | collective-permute-start | bytes 21258248 | tf_op jit(solution)/shard_map/ppermute | solution.py:125
  596.2 22.9 %collective-permute-start.8 = (bf16[4,1730,128]{2,0,1:T(4,128)(2,1)}, bf16[4,1730,128]{2,0,1:T(4,128)(2,1)}, u32[]{:S(2)}, u32[]{:S(2)}) collective-permute-start(bf16[4,1730,128]{2,0,1:T(4,128)(2,1)} %fusion.31), channel_id=1, source_target_pairs={{0,8},{4,20},{8,0},{12,28},{16,24},{20,4},{24,16},{28,12},{1,9},{5... | collective-permute-start | bytes 5314568 | tf_op jit(solution)/shard_map/ppermute | solution.py:127
  624.7 40.8 %collective-permute-start.9 = (bf16[4,1730,128]{2,0,1:T(4,128)(2,1)}, bf16[4,1730,128]{2,0,1:T(4,128)(2,1)}, u32[]{:S(2)}, u32[]{:S(2)}) collective-permute-start(bf16[4,1730,128]{2,0,1:T(4,128)(2,1)} %get-tuple-element.85), channel_id=1, source_target_pairs={{0,8},{4,12},{8,0},{12,4},{16,24},{20,28},{24,16},{28,20},{1,9},{5... | collective-permute-start | bytes 5314568 | tf_op jit(solution)/shard_map/ppermute | solution.py:134
  626.2 40.5 %collective-permute-start.10 = (bf16[4,1730,128]{2,0,1:T(4,128)(2,1)}, bf16[4,1730,128]{2,0,1:T(4,128)(2,1)}, u32[]{:S(2)}, u32[]{:S(2)}) collective-permute-start(bf16[4,1730,128]{2,0,1:T(4,128)(2,1)} %get-tuple-element.86), channel_id=1, source_target_pairs={{0,16},{4,20},{8,24},{12,28},{16,0},{20,4},{24,8},{28,12},{1,17},{... | collective-permute-start | bytes 5314568 | tf_op jit(solution)/shard_map/ppermute | solution.py:135
  674.4 30.4 %collective-permute-start.12 = (bf16[1730,128]{1,0:T(8,128)(2,1)}, bf16[1730,128]{1,0:T(8,128)(2,1)}, u32[]{:S(2)}, u32[]{:S(2)}) collective-permute-start(bf16[1730,128]{1,0:T(8,128)(2,1)} %bitcast.170), channel_id=1, source_target_pairs={{0,2},{1,3},{2,0},{3,1},{4,6},{5,7},{6,4},{7,5},{8,10},{9,11},{10,... | collective-permute-start | bytes 1328648 | tf_op jit(solution)/shard_map/ppermute | solution.py:140
  674.8 40.2 %collective-permute-start.13 = (bf16[1730,128]{1,0:T(8,128)(2,1)}, bf16[1730,128]{1,0:T(8,128)(2,1)}, u32[]{:S(2)}, u32[]{:S(2)}) collective-permute-start(bf16[1730,128]{1,0:T(8,128)(2,1)} %bitcast.169), channel_id=1, source_target_pairs={{0,3},{1,0},{2,1},{3,2},{4,7},{5,4},{6,5},{7,6},{8,11},{9,8},{10,9... | collective-permute-start | bytes 1328648 | tf_op jit(solution)/shard_map/ppermute | solution.py:140
  681.8 33.3 %collective-permute-start.11 = (bf16[1730,128]{1,0:T(8,128)(2,1)S(1)}, bf16[1730,128]{1,0:T(8,128)(2,1)}, u32[]{:S(2)}, u32[]{:S(2)}) collective-permute-start(bf16[1730,128]{1,0:T(8,128)(2,1)S(1)} %bitcast.239), channel_id=1, source_target_pairs={{0,1},{1,2},{2,3},{3,0},{4,5},{5,6},{6,7},{7,4},{8,9},{9,10},{10,1... | collective-permute-start | bytes 1328648 | tf_op jit(solution)/shard_map/ppermute | solution.py:140
  717.5 21.3 %collective-permute-start.15 = (f32[1730,128]{1,0:T(8,128)S(1)}, f32[1730,128]{1,0:T(8,128)S(1)}, u32[]{:S(2)}, u32[]{:S(2)}) collective-permute-start(f32[1730,128]{1,0:T(8,128)S(1)} %get-tuple-element.78), channel_id=1, source_target_pairs={{0,16},{4,20},{8,24},{12,28},{16,0},{20,4},{24,8},{28,12},{1,17},{... | collective-permute-start | bytes 2657288 | tf_op jit(solution)/shard_map/ppermute | solution.py:53
  718.9 21.3 %collective-permute-start.14 = (f32[1730,128]{1,0:T(8,128)S(1)}, f32[1730,128]{1,0:T(8,128)S(1)}, u32[]{:S(2)}, u32[]{:S(2)}) collective-permute-start(f32[1730,128]{1,0:T(8,128)S(1)} %get-tuple-element.78), channel_id=1, source_target_pairs={{0,8},{4,12},{8,0},{12,4},{16,24},{20,28},{24,16},{28,20},{1,9},{5... | collective-permute-start | bytes 2657288 | tf_op jit(solution)/shard_map/ppermute | solution.py:52
  740.3 13.2 %collective-permute-start.16 = (f32[1730,128]{1,0:T(8,128)S(1)}, f32[1730,128]{1,0:T(8,128)S(1)}, u32[]{:S(2)}, u32[]{:S(2)}) collective-permute-start(f32[1730,128]{1,0:T(8,128)S(1)} %broadcast_select_fusion.1), channel_id=1, source_target_pairs={{0,8},{4,20},{8,0},{12,28},{16,24},{20,4},{24,16},{28,12},{1,9},{5... | collective-permute-start | bytes 2657288 | tf_op jit(solution)/shard_map/ppermute | solution.py:55
  759.3 6.7 collective-permute-start.17
  (40 other events, 168.7 us)

commit v3 on v2

--- a/solution.py
+++ b/solution.py
@@ -64,39 +64,35 @@
     return jnp.take(x, idx, axis=axis, mode="wrap")
 
 
-def fast_gather(mats, gains):
-    d = lax.axis_index("dp")
+def _z_gather(piece):
     f = lax.axis_index("fsdp")
-    parts = []
-    for m in mats:
-        r = m.shape[0] // NDP_FAST
-        parts.append(_to_rows(lax.dynamic_slice_in_dim(m, d * r, r, 0)))
-    gr = gains[0].shape[1] // NDP_FAST
-    parts.append(_gain_rows(gains, lambda g: lax.dynamic_slice_in_dim(g, d * gr, gr, 1)))
-    own = jnp.concatenate(parts)
-    slots = [own] + [
-        lax.ppermute(own, "fsdp", [(i, (i + k) % NF_FAST) for i in range(NF_FAST)])
+    slots = [piece] + [
+        lax.ppermute(piece, "fsdp", [(i, (i + k) % NF_FAST) for i in range(NF_FAST)])
         for k in range(1, NF_FAST)
     ]
-    x = _plane_gather(jnp.stack(slots))
-    e_idx = jnp.arange(NDP_FAST, dtype=jnp.int32) ^ d
-    f_idx = (f - jnp.arange(NF_FAST, dtype=jnp.int32)) % NF_FAST
-    x = _take(_take(x, e_idx, 0), f_idx, 1)
-    out = []
-    row = 0
-    for m in mats:
-        r, cols = m.shape[0] // NDP_FAST, m.shape[1]
-        n_rows = r * cols // LANES
-        seg = x[:, :, row : row + n_rows].reshape(NDP_FAST, NF_FAST, r, cols)
-        out.append(seg.transpose(1, 0, 2, 3).reshape(NF_FAST * m.shape[0], cols))
-        row += n_rows
-    flat = x[:, :, row:].reshape(NDP_FAST, NF_FAST, -1)
-    offset = 0
+    return _take(jnp.stack(slots), (f - jnp.arange(NF_FAST, dtype=jnp.int32)) % NF_FAST, 0)
+
+
+def _gather_matrix(m):
+    d = lax.axis_index("dp")
+    j, c = d // 2, d % 2
+    rows, cols = m.shape[0] // (NDP_FAST // 2), m.shape[1] // 2
+    piece = lax.dynamic_slice(m, (j * rows, c * cols), (rows, cols))
+    z = _z_gather(piece)
+    x = lax.all_gather(z, "dp", axis=1, tiled=False)
+    x = x.reshape(NF_FAST, NDP_FAST // 2, 2, rows, cols).transpose(0, 1, 3, 2, 4)
+    return x.reshape(NF_FAST * m.shape[0], m.shape[1])
+
+
+def fast_gather(mats, gains):
+    out = [_gather_matrix(m) for m in mats]
+    stacked = jnp.concatenate(gains, axis=0)
+    z = _z_gather(stacked)
+    full = z.transpose(1, 0, 2).reshape(stacked.shape[0], NF_FAST * stacked.shape[1])
+    rows = 0
     for g in gains:
-        rows = g.shape[0]
-        seg = flat[:, :, offset : offset + rows * gr].reshape(NDP_FAST, NF_FAST, rows, gr)
-        out.append(seg.transpose(2, 1, 0, 3).reshape(rows, NF_FAST * g.shape[1]))
-        offset += rows * gr
+        out.append(full[rows : rows + g.shape[0]])
+        rows += g.shape[0]
     return out
 
 

time: 812 us -> 611 us (0.75)
  local copies, waits for them, and re-layouts: 357 us -> 203 us
  waiting for transfers between devices: 203 us -> 165 us
  other arithmetic: 91.7 us -> 64 us
  between operations: 2.15 us -> 15.2 us
    gather x11 -> x9, local copies, waits for them, and re-layouts: 117 us -> 47.9 us  [_take(): return jnp.take(x, idx, axis=axis, mode='wrap')]
    slice x9 -> x2, local copies, waits for them, and re-layouts: 35.7 us -> 0.01 us  [fast_reduce(): plane = chip[:, 0] + from_x.astype(jnp.float32) + from_y.astype(jnp.float32)]
    ppermute x2 -> x1, waiting for transfers between devices: 52.3 us -> 17.6 us  [_plane_gather(): b = lax.ppermute(z, 'dp', [(i, i ^ 4) for i in range(NDP_FAST)])]
    another operation x4, local copies, waits for them, and re-layouts: 27.6 us -> 3.53 us  [_z_gather(): jnp.stack(slots)]
    all_gather x0 -> x4, waiting for transfers between devices: none -> 22 us  [_gather_matrix(): x = lax.all_gather(z, 'dp', axis=1, tiled=False)]
    ppermute x2 -> x1, waiting for transfers between devices: 33.6 us -> 11.9 us  [_plane_gather(): lax.ppermute(send, 'dp', [(i, i ^ 2) if i % 2 == 0 else (i, i ^ 4) for i...]
    ppermute x3 -> x15, starting transfers between devices: 5.52 us -> 22.9 us  [_z_gather(): lax.ppermute(piece, 'fsdp', [(i, (i + k) % NF_FAST) for i in range(NF_FAS...]
    transpose x4 -> x0, local copies, waits for them, and re-layouts: 13.2 us -> none  [fast_gather(): out.append(seg.transpose(1, 0, 2, 3).reshape(NF_FAST * m.shape[0], cols))]
  transfers between devices with their start and end apart: 18 -> 30, of which waited for: 13 -> 18; matrix products, arithmetic and copies ran while one was open for 6% -> 17% of each run, Pallas kernels for 0% -> 0%
where the time goes in v3:
time: 611 us; the launch traced here: 599 us
  local copies, waits for them, and re-layouts  203 us (33%)
  waiting for transfers between devices  165 us (27%)
  matrix products  117 us (19%)
  other arithmetic  64 us (10%)
  starting transfers between devices  34.5 us (6%)
  between operations  15.2 us (2%)
    unnamed x144, local copies, waits for them, and re-layouts  53 us
    gather x9, local copies, waits for them, and re-layouts, _take(): return jnp.take(x, idx, axis=axis, mode='wrap')  47.9 us
    ppermute x1, waiting for transfers between devices, fast_reduce(): lax.ppermute(to_x.astype(jnp.bfloat16), 'dp', [(i, i ^ 2) for i in range(...  38.3 us
    ppermute x3, waiting for transfers between devices, fast_reduce(): lax.ppermute(part.astype(jnp.bfloat16), 'fsdp', [(i, (i + k) % NF_FAST) f...  33.5 us
    reshape x4, local copies, waits for them, and re-layouts, fast_reduce(): parts.append(m.astype(jnp.bfloat16).reshape(NF_FAST, NDP_FAST, -1, LANES))  29 us
    reshape x4, local copies, waits for them, and re-layouts, _gather_matrix(): x.reshape(NF_FAST, NDP_FAST // 2, 2, rows, cols).transpose(0, 1, 3, 2, 4)  26 us
    ppermute x15, starting transfers between devices, _z_gather(): lax.ppermute(piece, 'fsdp', [(i, (i + k) % NF_FAST) for i in range(NF_FAS...  22.9 us
    all_gather x4, waiting for transfers between devices, _gather_matrix(): x = lax.all_gather(z, 'dp', axis=1, tiled=False)  22 us
  transfers between devices with their start and end apart: 30, of which 18 were waited for; matrix products, arithmetic and copies ran while one was open for 17% of the time, Pallas kernels for 0%

profile of v3, /device:TPU:8, one launch (start us, length us, event | category | flops | bytes accessed | tf_op | source)
XLA Modules:
  0.0 599.4 jit_solution(13347512472433820671)
XLA Ops:
  16.9 4.7 collective-permute-start.4
  35.9 5.9 collective-permute-done.13
  72.4 7.2 %all-gather.9.cloned.1.call-done = bf16[4,384,1152]{2,1,0:T(8,128)(2,1)} async-done(((bf16[4,48,1152]{2,1,0:T(8,128)(2,1)}), bf16[4,384,1152]{2,1,0:T(8,128)(2,1)}) %all-gather.9.cloned.1.call-update) | async-done | bytes 3538960 | tf_op jit(solution)/shard_map/all_gather | solution.py:82
  79.5 5.0 copy.172
  91.4 3.4 fusion.87
  102.6 8.5 %fusion.90 = (f32[12,576]{1,0:T(8,128)S(1)}, f32[12,576,576]{1,2,0:T(8,128)}) fusion(f32[576,12,64]{0,2,1:T(8,128)S(1)} %bitcast.183, f32[12,64]{1,0:T(8,128)S(1)} %mul.344, f32[576,12]{0,1:T(8,128)S(1)} %fusion.58, f32[576,12]{0,1:T(8,128)S(1)} %broadcast_multiply_fusion, f32[576,12,64]{0,2,1:T(8,128)S(1)} %bitcast.175, f32[12,64]{1,0:T(8,128)S(1)} %mul.338, ...), kind=kOutput, calls=%fused_computation.228 | convolution fusion | flops 525083904 | bytes 19940352 | tf_op jit(solution)/shard_map/while/body/eval_jaxpr/qhd,khd->hqk/dot_general | solution.py:201
  111.2 8.6 %fusion.3 = f32[12,576]{1,0:T(8,128)S(1)} fusion(f32[12,576,576]{1,2,0:T(8,128)} %get-tuple-element.105, f32[12,576]{1,0:T(8,128)S(1)} %get-tuple-element.104), kind=kLoop, calls=%fused_computation.17 | loop fusion | flops 7955712 | bytes 15980544 | tf_op jit(solution)/shard_map/while/body/eval_jaxpr/reduce_sum | solution.py:211
  119.8 9.7 %fusion.37 = bf16[12,64,576]{2,1,0:T(8,128)(2,1)S(1)} fusion(bf16[576,12,64]{0,2,1:T(8,128)(2,1)} %bitcast.210, f32[12,576,576]{1,2,0:T(8,128)} %get-tuple-element.105, f32[12,576]{1,0:T(8,128)S(1)} %fusion.3, f32[12,576]{1,0:T(8,128)S(1)} %get-tuple-element.104), kind=kOutput, calls=%fused_computation.106 | convolution fusion | flops 521994240 | bytes 17750016 | tf_op jit(solution)/shard_map/while/body/eval_jaxpr/hqk,khd->qhd/dot_general | solution.py:213
  132.2 9.4 %copy.179 = bf16[4,4,2,192,384]{4,2,3,1,0:T(2,128)(2,1)} copy(bf16[4,4,2,192,384]{4,3,2,1,0:T(8,128)(2,1)} %bitcast.205) | data formatting | bytes 9437184 | tf_op jit(solution)/shard_map/reshape | solution.py:83
  141.5 5.7 copy.224
  147.2 14.8 %all-gather.13.cloned.1.call-done = bf16[4,384,1536]{2,1,0:T(8,128)(2,1)} async-done(((bf16[4,48,1536]{2,1,0:T(8,128)(2,1)}), bf16[4,384,1536]{2,1,0:T(8,128)(2,1)}) %all-gather.13.cloned.1.call-update) | async-done | bytes 4718608 | tf_op jit(solution)/shard_map/all_gather | solution.py:82
  162.0 9.4 %copy.178 = bf16[4,4,2,48,1536]{4,2,3,1,0:T(2,128)(2,1)} copy(bf16[4,4,2,48,1536]{4,3,2,1,0:T(8,128)(2,1)} %bitcast.206) | data formatting | bytes 9437184 | tf_op jit(solution)/shard_map/reshape | solution.py:83
  171.4 3.7 copy.223
  175.1 21.1 %multiply_convert_fusion = (bf16[576,3072]{1,0:T(8,128)(2,1)}, f32[576,3072]{1,0:T(8,128)}, f32[576,3072]{1,0:T(8,128)}) fusion(bf16[768,3072]{1,0:T(8,128)(2,1)S(1)} %bitcast.207, f32[576,768]{1,0:T(8,128)S(1)} %copy-done.12, f32[768]{0:T(1024)S(1)} %add.255, f32[768]{0:T(1024)S(1)} %mul.352, f32[576]{0:T(1024)S(1)} %fusion.67, ...), kind=kOutput, calls=%fused_computation.26 | convolution fusion | flops 2835136512 | bytes 24193536 | tf_op jit(solution)/shard_map/dot_general | solution.py:223
  196.2 9.2 %add_convert_fusion = bf16[576,3072]{1,0:T(8,128)(2,1)} fusion(f32[576,3072]{1,0:T(8,128)} %get-tuple-element.82, f32[576,3072]{1,0:T(8,128)} %get-tuple-element.108, bf16[3072,768]{1,0:T(8,128)(2,1)S(1)} %bitcast.201, bf16[576,768]{1,0:T(8,128)(2,1)S(1)} %copy-done.20, f32[576]{0:T(1024)S(1)} %fusion.65), kind=kOutput, calls=%fused_computation.25 | convolution fusion | flops 2744008704 | bytes 23300352 | tf_op jit(solution)/shard_map/dot_general | solution.py:232
  205.4 5.5 multiply_reduce_fusion.2
  210.9 6.2 %convolution_convert_fusion.3 = bf16[768,3072]{1,0:T(8,128)(2,1)} fusion(bf16[576,3072]{1,0:T(8,128)(2,1)S(1)} %copy-done.49, f32[576,768]{1,0:T(8,128)S(1)} %copy-done.12, f32[768]{0:T(1024)S(1)} %add.255, f32[768]{0:T(1024)S(1)} %mul.352, f32[576]{0:T(1024)S(1)} %fusion.67, f32[576]{0:T(1024)S(1)} %broadcast_multiply_fusion.4), kind=kOutput, calls=%fused_computation.43 | convolution fusion | flops 2722480128 | bytes 10037760 | tf_op jit(solution)/shard_map/dot_general | solution.py:235
  224.9 7.6 %convolution_convert_fusion = bf16[12,576,576]{1,2,0:T(8,128)(2,1)} fusion(bf16[576,12,64]{0,2,1:T(8,128)(2,1)} %bitcast.195, bf16[576,12,64]{0,2,1:T(8,128)(2,1)} %bitcast.211), kind=kOutput, calls=%fused_computation.40 | convolution fusion | flops 513589248 | bytes 9732096 | tf_op jit(solution)/shard_map/while/body/eval_jaxpr/qhd,khd->hqk/dot_general | solution.py:250
  232.5 9.9 %fusion.38 = bf16[12,64,576]{2,1,0:T(8,128)(2,1)} fusion(bf16[576,12,64]{0,2,1:T(8,128)(2,1)S(1)} %bitcast.196, f32[12,576,576]{1,2,0:T(8,128)} %get-tuple-element.105, f32[12,576]{1,0:T(8,128)S(1)} %log_add_fusion), kind=kOutput, calls=%fused_computation.107 | convolution fusion | flops 518012928 | bytes 17722368 | tf_op jit(solution)/shard_map/while/body/eval_jaxpr/hqk,qhd->khd/dot_general | solution.py:249
  242.4 12.0 %fusion = f32[12,576]{1,0:T(8,128)S(1)} fusion(bf16[12,576,576]{1,2,0:T(8,128)(2,1)} %convolution_convert_fusion, f32[12,576,576]{1,2,0:T(8,128)} %get-tuple-element.105, f32[12,576]{1,0:T(8,128)S(1)} %log_add_fusion), kind=kLoop, calls=%fused_computation.10 | loop fusion | flops 15918336 | bytes 23943168 | tf_op jit(solution)/shard_map/while/body/eval_jaxpr/reduce_sum | solution.py:252
  256.0 6.0 %fusion.2 = bf16[12,576,576]{1,2,0:T(8,128)(2,1)} fusion(bf16[12,576,576]{1,2,0:T(8,128)(2,1)S(1)} %copy-done.3, f32[12,576,576]{1,2,0:T(8,128)S(1)} %bitcast.172, f32[12,576]{1,0:T(8,128)S(1)} %fusion, f32[12,576]{1,0:T(8,128)S(1)} %log_add_fusion), kind=kLoop, calls=%fused_computation.12 | loop fusion | flops 19906560 | bytes 31905792 | tf_op jit(solution)/shard_map/while/body/eval_jaxpr/convert_element_type | solution.py:253
  262.0 8.2 %fusion.28 = (f32[576,12]{0,1:T(8,128)S(1)}, f32[12,64,576]{2,1,0:T(8,128)}) fusion(f32[576,12,64]{0,2,1:T(8,128)} %bitcast.182, f32[12,64]{1,0:T(8,128)S(1)} %copy-done.30, f32[576,12]{0,1:T(8,128)S(1)} %broadcast_multiply_fusion, bf16[12,576,576]{1,2,0:T(8,128)(2,1)} %fusion.2, f32[576,12,64]{0,2,1:T(8,128)S(1)} %bitcast.176, f32[12,64]{1,0:T(8,128)S(1)} %mul.338, ...), kind=kOutput, calls=%fused_computation.79 | convolution fusion | flops 513139968 | bytes 13387776 | tf_op jit(solution)/shard_map/while/body/eval_jaxpr/hqk,qhd->khd/dot_general | solution.py:258
  280.9 7.4 %convolution_convert_fusion.1 = bf16[768,2304]{1,0:T(8,128)(2,1)} fusion(bf16[576,768]{0,1:T(8,128)(2,1)S(1)} %bitcast.225, bf16[576,768]{0,1:T(8,128)(2,1)S(1)} %bitcast.221, bf16[576,768]{0,1:T(8,128)(2,1)S(1)} %bitcast.223, bf16[576,768]{1,0:T(8,128)(2,1)S(1)} %copy-done.8, f32[768]{0:T(1024)S(1)} %copy-done.40, f32[768]{0:T(1024)S(1)} %copy-done.38, ...), kind=kOutput, calls=%fused_computation.41 | convolution fusion | flops 2050818048 | bytes 7088640 | tf_op jit(solution)/shard_map/dot_general | solution.py:276
  288.3 8.3 %reshape.488 = bf16[4,8,576,128]{3,2,1,0:T(8,128)(2,1)} reshape(bf16[768,3072]{1,0:T(8,128)(2,1)} %convolution_convert_fusion.3) | data formatting | bytes 9437184 | tf_op jit(solution)/shard_map/reshape | solution.py:106
  296.8 3.4 reshape.487
  300.1 8.4 %convolution_convert_fusion.2 = bf16[3072,768]{1,0:T(8,128)(2,1)} fusion(bf16[576,3072]{1,0:T(8,128)(2,1)} %get-tuple-element.81, bf16[576,768]{1,0:T(8,128)(2,1)} %param.23, f32[576]{0:T(1024)S(1)} %fusion.65), kind=kOutput, calls=%fused_computation.42 | convolution fusion | flops 2721595392 | bytes 9144576 | tf_op jit(solution)/shard_map/dot_general | solution.py:231
  308.5 9.2 %reshape.489 = bf16[4,8,576,128]{3,2,1,0:T(8,128)(2,1)} reshape(bf16[3072,768]{1,0:T(8,128)(2,1)} %convolution_convert_fusion.2) | data formatting | bytes 9437184 | tf_op jit(solution)/shard_map/reshape | solution.py:106
  319.4 8.1 %reshape.486 = bf16[4,8,432,128]{3,2,1,0:T(8,128)(2,1)} reshape(bf16[768,2304]{1,0:T(8,128)(2,1)} %convolution_convert_fusion.1) | data formatting | bytes 7077888 | tf_op jit(solution)/shard_map/reshape | solution.py:106
  327.6 6.7 %copy_dynamic-update-slice_fusion.2 = bf16[4,8,1730,128]{3,0,2,1:T(4,128)(2,1)} fusion(bf16[4,8,432,128]{3,2,1,0:T(8,128)(2,1)} %reshape.486), kind=kLoop, calls=%fused_computation.58 | loop fusion | bytes 7077888
  336.2 5.8 copy_dynamic-update-slice_fusion.1
  342.0 5.9 copy_dynamic-update-slice_fusion
  348.6 13.4 %gather_fusion.7 = bf16[4,4,1730,128]{3,1,2,0:T(4,128)(2,1)} fusion(bf16[4,8,1730,128]{3,0,2,1:T(4,128)(2,1)} %constant_dynamic-update-slice_fusion, s32[1024]{0:T(1024)} %pad_clamp_fusion.1), kind=kCustom, calls=%fused_computation.1.clone | custom fusion | bytes 14172176 | tf_op jit(solution)/shard_map/jit(_take)/gather | solution.py:64
  362.0 8.4 %copy.193 = bf16[4,4,1730,128]{3,1,2,0:T(4,128)(2,1)} copy(bf16[4,4,1730,128]{3,0,2,1:T(4,128)(2,1)} %bitcast.187) | data formatting | bytes 14172160 | tf_op jit(solution)/shard_map/jit(_take)/gather | solution.py:64
  370.7 13.1 %gather_fusion.6 = bf16[4,4,1730,128]{3,1,2,0:T(4,128)(2,1)} fusion(bf16[4,8,1730,128]{3,0,2,1:T(4,128)(2,1)} %constant_dynamic-update-slice_fusion, s32[1024]{0:T(1024)S(1)} %pad_clamp_fusion.2), kind=kCustom, calls=%fused_computation.clone | custom fusion | bytes 14172176 | tf_op jit(solution)/shard_map/jit(_take)/gather | solution.py:64
  383.8 9.7 %convert_add_fusion = f32[4,4,1730,128]{3,0,2,1:T(4,128)S(1)} fusion(bf16[4,4,1730,128]{3,1,2,0:T(4,128)(2,1)} %gather_fusion.6, bf16[4,4,1730,128]{3,1,2,0:T(4,128)(2,1)} %collective-permute-done.15), kind=kLoop, calls=%fused_computation.18 | loop fusion | flops 10629120 | bytes 28344320 | tf_op jit(solution)/shard_map/add | solution.py:122
  393.5 5.0 copy-done.4
  400.7 21.2 %collective-permute-done.16 = bf16[4,1730,128]{2,0,1:T(4,128)(2,1)} collective-permute-done((bf16[4,1730,128]{2,0,1:T(4,128)(2,1)S(1)}, bf16[4,1730,128]{2,0,1:T(4,128)(2,1)}, u32[]{:S(2)}, u32[]{:S(2)}) %collective-permute-start.16) | collective-permute-done | bytes 1771552 | tf_op jit(solution)/shard_map/ppermute | solution.py:123
  421.9 5.4 fusion.17
  429.3 38.3 %collective-permute-done.17 = bf16[4,1730,128]{2,0,1:T(4,128)(2,1)} collective-permute-done((bf16[4,1730,128]{2,0,1:T(4,128)(2,1)}, bf16[4,1730,128]{2,0,1:T(4,128)(2,1)}, u32[]{:S(2)}, u32[]{:S(2)}) %collective-permute-start.17) | collective-permute-done | bytes 1771552 | tf_op jit(solution)/shard_map/ppermute | solution.py:130
  477.5 26.7 %collective-permute-done.19 = bf16[1730,128]{1,0:T(8,128)(2,1)S(1)} collective-permute-done((bf16[1730,128]{1,0:T(8,128)(2,1)S(1)}, bf16[1730,128]{1,0:T(8,128)(2,1)S(1)}, u32[]{:S(2)}, u32[]{:S(2)}) %collective-permute-start.19) | collective-permute-done | bytes 442912 | tf_op jit(solution)/shard_map/ppermute | solution.py:136
  504.2 6.8 %collective-permute-done.20 = bf16[1730,128]{1,0:T(8,128)(2,1)} collective-permute-done((bf16[1730,128]{1,0:T(8,128)(2,1)S(1)}, bf16[1730,128]{1,0:T(8,128)(2,1)}, u32[]{:S(2)}, u32[]{:S(2)}) %collective-permute-start.20) | collective-permute-done | bytes 442912 | tf_op jit(solution)/shard_map/ppermute | solution.py:136
  515.4 17.6 %collective-permute-done.23 = f32[1730,128]{1,0:T(8,128)S(1)} collective-permute-done((f32[1730,128]{1,0:T(8,128)S(1)}, f32[1730,128]{1,0:T(8,128)S(1)}, u32[]{:S(2)}, u32[]{:S(2)}) %collective-permute-start.23) | collective-permute-done | bytes 885792 | tf_op jit(solution)/shard_map/ppermute | solution.py:53
  534.3 11.9 %collective-permute-done.24 = f32[1730,128]{1,0:T(8,128)S(1)} collective-permute-done((f32[1730,128]{1,0:T(8,128)S(1)}, f32[1730,128]{1,0:T(8,128)S(1)}, u32[]{:S(2)}, u32[]{:S(2)}) %collective-permute-start.24) | collective-permute-done | bytes 885792 | tf_op jit(solution)/shard_map/ppermute | solution.py:55
  546.5 5.7 copy.202
  555.1 3.8 multiply_convert_fusion.3
  568.5 7.0 %gather_fusion.5 = f32[8,1730,128]{2,1,0:T(8,128)} fusion(f32[8,1730,128]{2,1,0:T(8,128)} %copy_dynamic-update-slice_fusion.4, s32[1024]{0:T(1024)S(1)} %pad_clamp_fusion), kind=kCustom, calls=%fused_computation.7 | custom fusion | bytes 14172192 | tf_op jit(solution)/shard_map/jit(_take)/gather | solution.py:64
  576.2 5.1 fusion.86
  584.6 3.4 reshape.497
  (327 shorter events, 137.0 us)
Async XLA Ops:
  7.2 61.7 %all-gather.11.cloned.1.call-start = ((), (), s32[]{:S(2)}) async-start(), calls=%async_computation.1 | async-start | bytes 1327104 | tf_op jit(solution)/shard_map/all_gather | solution.py:82
  8.0 38.9 %copy-start.42 = (bf16[2,192]{1,0:T(2,128)(2,1)S(1)}, bf16[2,192]{1,0:T(2,128)(2,1)}, u32[]{:S(2)}) copy-start(bf16[2,192]{1,0:T(2,128)(2,1)} %param.22) | copy-start | bytes 2308
  8.0 39.0 %copy-start.43 = (bf16[2,192]{1,0:T(2,128)(2,1)S(1)}, bf16[2,192]{1,0:T(2,128)(2,1)}, u32[]{:S(2)}) copy-start(bf16[2,192]{1,0:T(2,128)(2,1)} %param.21) | copy-start | bytes 2308
  8.0 39.0 %copy-start.44 = (bf16[2,192]{1,0:T(2,128)(2,1)S(1)}, bf16[2,192]{1,0:T(2,128)(2,1)}, u32[]{:S(2)}) copy-start(bf16[2,192]{1,0:T(2,128)(2,1)} %param.20) | copy-start | bytes 2308
  8.0 5.5 collective-permute-start.7
  10.7 4.0 collective-permute-start.6
  10.7 4.0 collective-permute-start.8
  14.7 41.2 %copy-start.46 = (s32[1,9]{1,0:T(1,128)S(1)}, s32[1,9]{1,0:T(1,128)}, u32[]{:S(2)}) copy-start(s32[1,9]{1,0:T(1,128)} %param.15) | copy-start | bytes 112
  14.7 42.0 %copy-start.8 = (bf16[576,768]{1,0:T(8,128)(2,1)S(1)}, bf16[576,768]{1,0:T(8,128)(2,1)}, u32[]{:S(2)}) copy-start(bf16[576,768]{1,0:T(8,128)(2,1)} %param.14) | copy-start | bytes 2654212
  16.0 63.6 %all-gather.9.cloned.1.call-start = ((), (), s32[]{:S(2)}) async-start(), calls=%async_computation | async-start | bytes 3981312 | tf_op jit(solution)/shard_map/all_gather | solution.py:82
  16.9 10.1 %collective-permute-start.4 = (bf16[48,1152]{1,0:T(8,128)(2,1)S(1)}, bf16[48,1152]{1,0:T(8,128)(2,1)S(1)}, u32[]{:S(2)}, u32[]{:S(2)}) collective-permute-start(bf16[48,1152]{1,0:T(8,128)(2,1)S(1)} %dynamic_slice.48), channel_id=1, source_target_pairs={{0,2},{1,3},{2,0},{3,1},{4,6},{5,7},{6,4},{7,5},{8,10},{9,11},{10,... | collective-permute-start | bytes 331784 | tf_op jit(solution)/shard_map/ppermute | solution.py:70
  21.6 6.6 %collective-permute-start.3 = (bf16[48,1152]{1,0:T(8,128)(2,1)S(1)}, bf16[48,1152]{1,0:T(8,128)(2,1)S(1)}, u32[]{:S(2)}, u32[]{:S(2)}) collective-permute-start(bf16[48,1152]{1,0:T(8,128)(2,1)S(1)} %dynamic_slice.48), channel_id=1, source_target_pairs={{0,1},{1,2},{2,3},{3,0},{4,5},{5,6},{6,7},{7,4},{8,9},{9,10},{10,1... | collective-permute-start | bytes 331784 | tf_op jit(solution)/shard_map/ppermute | solution.py:70
  21.6 7.6 %collective-permute-start.5 = (bf16[48,1152]{1,0:T(8,128)(2,1)S(1)}, bf16[48,1152]{1,0:T(8,128)(2,1)S(1)}, u32[]{:S(2)}, u32[]{:S(2)}) collective-permute-start(bf16[48,1152]{1,0:T(8,128)(2,1)S(1)} %dynamic_slice.48), channel_id=1, source_target_pairs={{0,3},{1,0},{2,1},{3,2},{4,7},{5,4},{6,5},{7,6},{8,11},{9,8},{10,9... | collective-permute-start | bytes 331784 | tf_op jit(solution)/shard_map/ppermute | solution.py:70
  29.2 28.1 %copy-start.45 = (s32[4]{0:T(128)S(1)}, s32[4]{0:T(128)}, u32[]{:S(2)}) copy-start(s32[4]{0:T(128)} %constant.339.clone) | copy-start | bytes 52
  30.6 101.5 %all-gather.15.cloned.1.call-start = ((), (), s32[]{:S(2)}) async-start(), calls=%async_computation.3 | async-start | bytes 5308416 | tf_op jit(solution)/shard_map/all_gather | solution.py:82
  31.6 10.2 %collective-permute-start.13 = (bf16[192,384]{1,0:T(8,128)(2,1)S(1)}, bf16[192,384]{1,0:T(8,128)(2,1)S(1)}, u32[]{:S(2)}, u32[]{:S(2)}) collective-permute-start(bf16[192,384]{1,0:T(8,128)(2,1)S(1)} %dynamic_slice.51), channel_id=1, source_target_pairs={{0,2},{1,3},{2,0},{3,1},{4,6},{5,7},{6,4},{7,5},{8,10},{9,11},{10,... | collective-permute-start | bytes 442376 | tf_op jit(solution)/shard_map/ppermute | solution.py:70
  32.9 11.0 %collective-permute-start.12 = (bf16[192,384]{1,0:T(8,128)(2,1)S(1)}, bf16[192,384]{1,0:T(8,128)(2,1)S(1)}, u32[]{:S(2)}, u32[]{:S(2)}) collective-permute-start(bf16[192,384]{1,0:T(8,128)(2,1)S(1)} %dynamic_slice.51), channel_id=1, source_target_pairs={{0,1},{1,2},{2,3},{3,0},{4,5},{5,6},{6,7},{7,4},{8,9},{9,10},{10,1... | collective-permute-start | bytes 442376 | tf_op jit(solution)/shard_map/ppermute | solution.py:70
  33.8 11.5 %collective-permute-start.14 = (bf16[192,384]{1,0:T(8,128)(2,1)S(1)}, bf16[192,384]{1,0:T(8,128)(2,1)S(1)}, u32[]{:S(2)}, u32[]{:S(2)}) collective-permute-start(bf16[192,384]{1,0:T(8,128)(2,1)S(1)} %dynamic_slice.51), channel_id=1, source_target_pairs={{0,3},{1,0},{2,1},{3,2},{4,7},{5,4},{6,5},{7,6},{8,11},{9,8},{10,9... | collective-permute-start | bytes 442376 | tf_op jit(solution)/shard_map/ppermute | solution.py:70
  46.9 115.1 %all-gather.13.cloned.1.call-start = ((), (), s32[]{:S(2)}) async-start(), calls=%async_computation.2 | async-start | bytes 5308416 | tf_op jit(solution)/shard_map/all_gather | solution.py:82
  47.0 12.7 %collective-permute-start.1 = (bf16[6,192]{1,0:T(8,128)(2,1)S(1)}, bf16[6,192]{1,0:T(8,128)(2,1)S(1)}, u32[]{:S(2)}, u32[]{:S(2)}) collective-permute-start(bf16[6,192]{1,0:T(8,128)(2,1)S(1)} %get-tuple-element.103), channel_id=1, source_target_pairs={{0,2},{1,3},{2,0},{3,1},{4,6},{5,7},{6,4},{7,5},{8,10},{9,11},{10,... | collective-permute-start | bytes 6920 | tf_op jit(solution)/shard_map/ppermute | solution.py:70
  47.1 13.5 %collective-permute-start = (bf16[6,192]{1,0:T(8,128)(2,1)S(1)}, bf16[6,192]{1,0:T(8,128)(2,1)S(1)}, u32[]{:S(2)}, u32[]{:S(2)}) collective-permute-start(bf16[6,192]{1,0:T(8,128)(2,1)S(1)} %get-tuple-element.103), channel_id=1, source_target_pairs={{0,1},{1,2},{2,3},{3,0},{4,5},{5,6},{6,7},{7,4},{8,9},{9,10},{10,1... | collective-permute-start | bytes 6920 | tf_op jit(solution)/shard_map/ppermute | solution.py:70
  48.4 12.2 %collective-permute-start.2 = (bf16[6,192]{1,0:T(8,128)(2,1)S(1)}, bf16[6,192]{1,0:T(8,128)(2,1)S(1)}, u32[]{:S(2)}, u32[]{:S(2)}) collective-permute-start(bf16[6,192]{1,0:T(8,128)(2,1)S(1)} %get-tuple-element.103), channel_id=1, source_target_pairs={{0,3},{1,0},{2,1},{3,2},{4,7},{5,4},{6,5},{7,6},{8,11},{9,8},{10,9... | collective-permute-start | bytes 6920 | tf_op jit(solution)/shard_map/ppermute | solution.py:70
  50.5 10.7 %collective-permute-start.10 = (bf16[48,1536]{1,0:T(8,128)(2,1)S(1)}, bf16[48,1536]{1,0:T(8,128)(2,1)S(1)}, u32[]{:S(2)}, u32[]{:S(2)}) collective-permute-start(bf16[48,1536]{1,0:T(8,128)(2,1)S(1)} %dynamic_slice.50), channel_id=1, source_target_pairs={{0,2},{1,3},{2,0},{3,1},{4,6},{5,7},{6,4},{7,5},{8,10},{9,11},{10,... | collective-permute-start | bytes 442376 | tf_op jit(solution)/shard_map/ppermute | solution.py:70
  53.0 9.5 %collective-permute-start.9 = (bf16[48,1536]{1,0:T(8,128)(2,1)S(1)}, bf16[48,1536]{1,0:T(8,128)(2,1)S(1)}, u32[]{:S(2)}, u32[]{:S(2)}) collective-permute-start(bf16[48,1536]{1,0:T(8,128)(2,1)S(1)} %dynamic_slice.50), channel_id=1, source_target_pairs={{0,1},{1,2},{2,3},{3,0},{4,5},{5,6},{6,7},{7,4},{8,9},{9,10},{10,1... | collective-permute-start | bytes 442376 | tf_op jit(solution)/shard_map/ppermute | solution.py:70
  56.9 28.2 %copy-start.31 = (f32[576]{0:T(1024)}, f32[576]{0:T(1024)S(1)}, u32[]{:S(2)}) copy-start(f32[576]{0:T(1024)S(1)} %broadcast_multiply_fusion.5) | copy-start | bytes 6916
  57.9 27.2 %copy-start.35 = (f32[576]{0:T(1024)}, f32[576]{0:T(1024)S(1)}, u32[]{:S(2)}) copy-start(f32[576]{0:T(1024)S(1)} %fusion.66) | copy-start | bytes 6916
  59.8 5.8 collective-permute-start.11
  67.5 17.7 %copy-start.37 = (f32[768]{0:T(1024)}, f32[768]{0:T(1024)S(1)}, u32[]{:S(2)}) copy-start(f32[768]{0:T(1024)S(1)} %mul.330) | copy-start | bytes 9220
  67.7 17.5 %copy-start.39 = (f32[768]{0:T(1024)}, f32[768]{0:T(1024)S(1)}, u32[]{:S(2)}) copy-start(f32[768]{0:T(1024)S(1)} %add.244) | copy-start | bytes 9220
  171.4 24.8 %slice-start.12 = ((s8[4718592]{0:T(1024)(128)(4,1)}), s8[4194304]{0:T(1024)(128)(4,1)S(1)}, s32[]{:S(2)}) async-start(s8[4718592]{0:T(1024)(128)(4,1)} %bitcast.199), calls=%async_computation.16 | async-start | bytes 8388608
  175.0 21.1 %slice-start.13 = ((s8[4718592]{0:T(1024)(128)(4,1)}), s8[524288]{0:T(1024)(128)(4,1)S(1)}, s32[]{:S(2)}) async-start(s8[4718592]{0:T(1024)(128)(4,1)} %bitcast.199), calls=%async_computation.17 | async-start | bytes 1048576
  175.1 21.1 %copy-start.20 = (bf16[576,768]{1,0:T(8,128)(2,1)S(1)}, bf16[576,768]{1,0:T(8,128)(2,1)}, u32[]{:S(2)}) copy-start(bf16[576,768]{1,0:T(8,128)(2,1)} %param.23) | copy-start | bytes 2654212
  232.5 21.9 %slice-start = ((s8[17694720]{0:T(1024)(128)(4,1)}), s8[4194304]{0:T(1024)(128)(4,1)S(1)}, s32[]{:S(2)}) async-start(s8[17694720]{0:T(1024)(128)(4,1)} %bitcast.171), calls=%async_computation.4 | async-start | bytes 8388608
  232.5 21.9 %slice-start.1 = ((s8[17694720]{0:T(1024)(128)(4,1)}), s8[4194304]{0:T(1024)(128)(4,1)S(1)}, s32[]{:S(2)}) async-start(s8[17694720]{0:T(1024)(128)(4,1)} %bitcast.171), calls=%async_computation.5 | async-start | bytes 8388608
  232.5 21.9 %slice-start.2 = ((s8[17694720]{0:T(1024)(128)(4,1)}), s8[917504]{0:T(1024)(128)(4,1)S(1)}, s32[]{:S(2)}) async-start(s8[17694720]{0:T(1024)(128)(4,1)} %bitcast.171), calls=%async_computation.6 | async-start | bytes 1835008
  280.9 37.2 %copy-start.14 = (f32[576,768]{1,0:T(8,128)}, f32[576,768]{1,0:T(8,128)S(1)}, u32[]{:S(2)}) copy-start(f32[576,768]{1,0:T(8,128)S(1)} %get-tuple-element.115) | copy-start | bytes 5308420
  370.4 13.4 %collective-permute-start.15 = (bf16[4,4,1730,128]{3,1,2,0:T(4,128)(2,1)}, bf16[4,4,1730,128]{3,1,2,0:T(4,128)(2,1)}, u32[]{:S(2)}, u32[]{:S(2)}) collective-permute-start(bf16[4,4,1730,128]{3,1,2,0:T(4,128)(2,1)} %copy.193), channel_id=1, source_target_pairs={{0,4},{4,0},{8,12},{12,8},{16,20},{20,16},{24,28},{28,24},{1,5},{5... | collective-permute-start | bytes 21258248 | tf_op jit(solution)/shard_map/ppermute | solution.py:121
  399.2 22.7 %collective-permute-start.16 = (bf16[4,1730,128]{2,0,1:T(4,128)(2,1)S(1)}, bf16[4,1730,128]{2,0,1:T(4,128)(2,1)}, u32[]{:S(2)}, u32[]{:S(2)}) collective-permute-start(bf16[4,1730,128]{2,0,1:T(4,128)(2,1)S(1)} %fusion.30), channel_id=1, source_target_pairs={{0,8},{4,20},{8,0},{12,28},{16,24},{20,4},{24,16},{28,12},{1,9},{5... | collective-permute-start | bytes 5314568 | tf_op jit(solution)/shard_map/ppermute | solution.py:123
  427.3 40.3 %collective-permute-start.17 = (bf16[4,1730,128]{2,0,1:T(4,128)(2,1)}, bf16[4,1730,128]{2,0,1:T(4,128)(2,1)}, u32[]{:S(2)}, u32[]{:S(2)}) collective-permute-start(bf16[4,1730,128]{2,0,1:T(4,128)(2,1)} %get-tuple-element.83), channel_id=1, source_target_pairs={{0,8},{4,12},{8,0},{12,4},{16,24},{20,28},{24,16},{28,20},{1,9},{5... | collective-permute-start | bytes 5314568 | tf_op jit(solution)/shard_map/ppermute | solution.py:130
  428.8 39.8 %collective-permute-start.18 = (bf16[4,1730,128]{2,0,1:T(4,128)(2,1)S(1)}, bf16[4,1730,128]{2,0,1:T(4,128)(2,1)}, u32[]{:S(2)}, u32[]{:S(2)}) collective-permute-start(bf16[4,1730,128]{2,0,1:T(4,128)(2,1)S(1)} %get-tuple-element.84), channel_id=1, source_target_pairs={{0,16},{4,20},{8,24},{12,28},{16,0},{20,4},{24,8},{28,12},{1,17},{... | collective-permute-start | bytes 5314568 | tf_op jit(solution)/shard_map/ppermute | solution.py:131
  429.3 39.2 %slice-start.5 = ((f32[4,4,1730,128]{3,0,2,1:T(4,128)}), f32[4,1,1730,128]{3,0,2,1:T(4,128)S(1)}, s32[]{:S(2)}) async-start(f32[4,4,1730,128]{3,0,2,1:T(4,128)} %copy-done.4), calls=%async_computation.9 | async-start | bytes 7086080 | tf_op jit(solution)/shard_map/slice | solution.py:132
  473.0 31.2 %collective-permute-start.19 = (bf16[1730,128]{1,0:T(8,128)(2,1)S(1)}, bf16[1730,128]{1,0:T(8,128)(2,1)S(1)}, u32[]{:S(2)}, u32[]{:S(2)}) collective-permute-start(bf16[1730,128]{1,0:T(8,128)(2,1)S(1)} %get-tuple-element.89), channel_id=1, source_target_pairs={{0,1},{1,2},{2,3},{3,0},{4,5},{5,6},{6,7},{7,4},{8,9},{9,10},{10,1... | collective-permute-start | bytes 1328648 | tf_op jit(solution)/shard_map/ppermute | solution.py:136
  474.6 29.7 %collective-permute-start.21 = (bf16[1730,128]{1,0:T(8,128)(2,1)S(1)}, bf16[1730,128]{1,0:T(8,128)(2,1)S(1)}, u32[]{:S(2)}, u32[]{:S(2)}) collective-permute-start(bf16[1730,128]{1,0:T(8,128)(2,1)S(1)} %get-tuple-element.90), channel_id=1, source_target_pairs={{0,3},{1,0},{2,1},{3,2},{4,7},{5,4},{6,5},{7,6},{8,11},{9,8},{10,9... | collective-permute-start | bytes 1328648 | tf_op jit(solution)/shard_map/ppermute | solution.py:136
  475.1 35.9 %collective-permute-start.20 = (bf16[1730,128]{1,0:T(8,128)(2,1)S(1)}, bf16[1730,128]{1,0:T(8,128)(2,1)}, u32[]{:S(2)}, u32[]{:S(2)}) collective-permute-start(bf16[1730,128]{1,0:T(8,128)(2,1)S(1)} %get-tuple-element.91), channel_id=1, source_target_pairs={{0,2},{1,3},{2,0},{3,1},{4,6},{5,7},{6,4},{7,5},{8,10},{9,11},{10,... | collective-permute-start | bytes 1328648 | tf_op jit(solution)/shard_map/ppermute | solution.py:136
  513.5 19.5 %collective-permute-start.23 = (f32[1730,128]{1,0:T(8,128)S(1)}, f32[1730,128]{1,0:T(8,128)S(1)}, u32[]{:S(2)}, u32[]{:S(2)}) collective-permute-start(f32[1730,128]{1,0:T(8,128)S(1)} %get-tuple-element.78), channel_id=1, source_target_pairs={{0,16},{4,20},{8,24},{12,28},{16,0},{20,4},{24,8},{28,12},{1,17},{... | collective-permute-start | bytes 2657288 | tf_op jit(solution)/shard_map/ppermute | solution.py:53
  514.1 18.9 %collective-permute-start.22 = (f32[1730,128]{1,0:T(8,128)S(1)}, f32[1730,128]{1,0:T(8,128)S(1)}, u32[]{:S(2)}, u32[]{:S(2)}) collective-permute-start(f32[1730,128]{1,0:T(8,128)S(1)} %get-tuple-element.78), channel_id=1, source_target_pairs={{0,8},{4,12},{8,0},{12,4},{16,24},{20,28},{24,16},{28,20},{1,9},{5... | collective-permute-start | bytes 2657288 | tf_op jit(solution)/shard_map/ppermute | solution.py:52
  533.1 13.2 %collective-permute-start.24 = (f32[1730,128]{1,0:T(8,128)S(1)}, f32[1730,128]{1,0:T(8,128)S(1)}, u32[]{:S(2)}, u32[]{:S(2)}) collective-permute-start(f32[1730,128]{1,0:T(8,128)S(1)} %broadcast_select_fusion), channel_id=1, source_target_pairs={{0,8},{4,20},{8,0},{12,28},{16,24},{20,4},{24,16},{28,12},{1,9},{5... | collective-permute-start | bytes 2657288 | tf_op jit(solution)/shard_map/ppermute | solution.py:55
  552.3 6.7 %collective-permute-start.25 = (f32[4,1730,128]{2,0,1:T(4,128)S(1)}, f32[4,1730,128]{2,0,1:T(4,128)S(1)}, u32[]{:S(2)}, u32[]{:S(2)}) collective-permute-start(f32[4,1730,128]{2,0,1:T(4,128)S(1)} %copy.202), channel_id=1, source_target_pairs={{0,4},{4,0},{8,12},{12,8},{16,20},{20,16},{24,28},{28,24},{1,5},{5... | collective-permute-start | bytes 10629128 | tf_op jit(solution)/shard_map/ppermute | solution.py:59
  (49 other events, 274.5 us)
Sparse Core Ops, SparseCore 0:
  16.1 27.0 all-gather.10
  45.7 33.8 all-gather.8
  82.0 38.7 all-gather.14
  123.2 38.7 all-gather.12

commit v4 on v3

--- a/solution.py
+++ b/solution.py
@@ -96,62 +96,54 @@
     return out
 
 
-def fast_reduce(mats, gains):
+def _reduce_matrix(g):
     d = lax.axis_index("dp")
     f = lax.axis_index("fsdp")
-    c = d % 2
-    n_shards = NF_FAST * NDP_FAST
-    parts = []
-    for m in mats:
-        parts.append(m.astype(jnp.bfloat16).reshape(NF_FAST, NDP_FAST, -1, LANES))
-    gr = gains[0].shape[1] // n_shards
-    flat_g = jnp.concatenate(
-        [
-            g.astype(jnp.bfloat16).reshape(g.shape[0], NF_FAST, NDP_FAST, gr).transpose(1, 2, 0, 3)
-            .reshape(NF_FAST, NDP_FAST, -1)
-            for g in gains
-        ],
-        axis=2,
-    )
-    pad = (-flat_g.shape[2]) % LANES
-    parts.append(jnp.pad(flat_g, ((0, 0), (0, 0), (0, pad))).reshape(NF_FAST, NDP_FAST, -1, LANES))
-    flat = jnp.concatenate(parts, axis=2)
-    home = _take(flat, jnp.array([0, 2, 4, 6], dtype=jnp.int32) ^ d, 1)
-    away = _take(flat, jnp.array([1, 3, 5, 7], dtype=jnp.int32) ^ d, 1)
-    got = lax.ppermute(away, "dp", [(i, i ^ 1) for i in range(NDP_FAST)])
-    chip = home.astype(jnp.float32) + got.astype(jnp.float32)
+    j, c = d // 2, d % 2
+    n_chips = NDP_FAST // 2
+    rows, cols = g.shape[0] // (NF_FAST * n_chips), g.shape[1] // 2
+
+    def half(which):
+        part = lax.dynamic_slice_in_dim(g, which * cols, cols, 1)
+        return part.reshape(NF_FAST, n_chips, rows, cols)
+
+    got = lax.ppermute(half(1 - c).astype(jnp.bfloat16), "dp", [(i, i ^ 1) for i in range(NDP_FAST)])
+    chip = half(c) + got.astype(jnp.float32)
+
+    def of_chip(k):
+        return lax.dynamic_index_in_dim(chip, k, 1, keepdims=False)
+
     moved = lax.ppermute(
-        chip[:, 3].astype(jnp.bfloat16),
+        of_chip(j ^ 3).astype(jnp.bfloat16),
         "dp",
         [(i, i ^ 2) if i % 2 == 0 else (i, i ^ 4) for i in range(NDP_FAST)],
     ).astype(jnp.float32)
-    to_x = chip[:, 1] + jnp.where(c == 1, moved, 0.0)
-    to_y = chip[:, 2] + jnp.where(c == 0, moved, 0.0)
+    to_x = of_chip(j ^ 1) + jnp.where(c == 1, moved, 0.0)
+    to_y = of_chip(j ^ 2) + jnp.where(c == 0, moved, 0.0)
     from_x = lax.ppermute(to_x.astype(jnp.bfloat16), "dp", [(i, i ^ 2) for i in range(NDP_FAST)])
     from_y = lax.ppermute(to_y.astype(jnp.bfloat16), "dp", [(i, i ^ 4) for i in range(NDP_FAST)])
-    plane = chip[:, 0] + from_x.astype(jnp.float32) + from_y.astype(jnp.float32)
+    plane = of_chip(j) + from_x.astype(jnp.float32) + from_y.astype(jnp.float32)
     total = lax.dynamic_index_in_dim(plane, f, 0, keepdims=False)
     for k in range(1, NF_FAST):
         part = lax.dynamic_index_in_dim(plane, (f + k) % NF_FAST, 0, keepdims=False)
         total = total + lax.ppermute(
             part.astype(jnp.bfloat16), "fsdp", [(i, (i + k) % NF_FAST) for i in range(NF_FAST)]
         ).astype(jnp.float32)
-    x = _take(_plane_gather(total), jnp.arange(NDP_FAST, dtype=jnp.int32) ^ d, 0)
-    out = []
-    row = 0
-    for m in mats:
-        rows, cols = m.shape
-        r = rows // n_shards
-        n_rows = r * cols // LANES
-        out.append(x[:, row : row + n_rows].reshape(NDP_FAST * r, cols))
-        row += n_rows
-    flat_out = x[:, row:].reshape(NDP_FAST, -1)
-    offset = 0
+    x = lax.all_gather(total, "dp", axis=0, tiled=False)
+    x = x.reshape(n_chips, 2, rows, cols).transpose(0, 2, 1, 3)
+    return x.reshape(n_chips * rows, 2 * cols)
+
+
+def fast_reduce(mats, gains):
+    out = [_reduce_matrix(m) for m in mats]
+    stacked = lax.psum(jnp.concatenate(gains, axis=0), ("dp", "fsdp"))
+    f = lax.axis_index("fsdp")
+    width = stacked.shape[1] // NF_FAST
+    mine = lax.dynamic_slice_in_dim(stacked, f * width, width, 1)
+    rows = 0
     for g in gains:
-        rows = g.shape[0]
-        seg = flat_out[:, offset : offset + rows * gr].reshape(NDP_FAST, rows, gr)
-        out.append(seg.transpose(1, 0, 2).reshape(rows, NDP_FAST * gr))
-        offset += rows * gr
+        out.append(mine[rows : rows + g.shape[0]])
+        rows += g.shape[0]
     return out
 
 
@@ -233,6 +225,8 @@
     (grad_pre,) = gelu_back(grad_active)
     pre_low = grad_pre.astype(jnp.bfloat16)
     grad_up = jnp.dot(second_low.T, pre_low, preferred_element_type=jnp.float32)
+    if fast:
+        early = [_reduce_matrix(grad_up), _reduce_matrix(grad_down)]
     grad_second = jnp.dot(pre_low, back_up.T, preferred_element_type=jnp.float32)
     grad_resid, gain_two, bias_two = second_back(grad_second)
     grad_resid = grad_resid + upstream
@@ -282,7 +276,8 @@
     grad_qk = jnp.stack([gain_q.reshape(model_width), gain_k.reshape(model_width)])
     summands = (grad_qkv, grad_outw, grad_up, grad_down, grad_gain, grad_bias, grad_qk)
     if fast:
-        shares = fast_reduce(summands[:4], summands[4:])
+        late = fast_reduce(summands[:2], summands[4:])
+        shares = late[:2] + early + late[2:]
     else:
         pieces = [
             lax.psum_scatter(

time: 611 us -> 536 us (0.88)
  local copies, waits for them, and re-layouts: 203 us -> 112 us
  blocking collectives: 0 us -> 52.6 us
  waiting for transfers between devices: 165 us -> 119 us
  starting transfers between devices: 34.5 us -> 52.8 us
    ppermute x11 -> x28, waiting for transfers between devices: 123 us -> 76 us  [the longest x12 26.9 us: _reduce_matrix(): lax.ppermute(part.astype(jnp.bfloat16), 'fsdp', [(i, (i + k) % NF_FAST) f...]
    gather x9 -> x5, local copies, waits for them, and re-layouts: 47.9 us -> 5.98 us  [_take(): return jnp.take(x, idx, axis=axis, mode='wrap')]
    psum x0 -> x1, blocking collectives: none -> 41.5 us  [fast_reduce(): stacked = lax.psum(jnp.concatenate(gains, axis=0), ('dp', 'fsdp'))]
    reshape x17 -> x8, local copies, waits for them, and re-layouts: 40.5 us -> 9.67 us  [the longest x4 9.66 us: _reduce_matrix(): x = x.reshape(n_chips, 2, rows, cols).transpose(0, 2, 1, 3)]
    unnamed x144 -> x128, local copies, waits for them, and re-layouts: 53 us -> 33.6 us
    ppermute x11 -> x28, starting transfers between devices: 11.5 us -> 29.6 us  [the longest x12 16.7 us: _reduce_matrix(): lax.ppermute(part.astype(jnp.bfloat16), 'fsdp', [(i, (i + k) % NF_FAST) f...]
    all_gather x0 -> x1, blocking collectives: none -> 11.1 us  [_reduce_matrix(): x = lax.all_gather(total, 'dp', axis=0, tiled=False)]
    dynamic_slice x0 -> x4, local copies, waits for them, and re-layouts: none -> 10.5 us  [half(): part = lax.dynamic_slice_in_dim(g, which * cols, cols, 1)]
  transfers between devices with their start and end apart: 30 -> 50, of which waited for: 18 -> 32; matrix products, arithmetic and copies ran while one was open for 17% -> 30% of each run, Pallas kernels for 0% -> 0%
where the time goes in v4:
time: 536 us; the launch traced here: 530 us
  waiting for transfers between devices  119 us (22%)
  matrix products  117 us (22%)
  local copies, waits for them, and re-layouts  112 us (21%)
  other arithmetic  60.8 us (11%)
  starting transfers between devices  52.8 us (10%)
  blocking collectives  52.6 us (10%)
  between operations  15.7 us (3%)
    psum x1, blocking collectives, fast_reduce(): stacked = lax.psum(jnp.concatenate(gains, axis=0), ('dp', 'fsdp'))  41.5 us
    unnamed x128, local copies, waits for them, and re-layouts  33.6 us
    ppermute x12, waiting for transfers between devices, _reduce_matrix(): lax.ppermute(part.astype(jnp.bfloat16), 'fsdp', [(i, (i + k) % NF_FAST) f...  26.9 us
    reshape x4, local copies, waits for them, and re-layouts, _gather_matrix(): x.reshape(NF_FAST, NDP_FAST // 2, 2, rows, cols).transpose(0, 1, 3, 2, 4)  26 us
    ppermute x4, waiting for transfers between devices, _reduce_matrix(): lax.ppermute(of_chip(j ^ 3).astype(jnp.bfloat16), 'dp', [(i, i ^ 2) if i...  25.1 us
    ppermute x15, starting transfers between devices, _z_gather(): lax.ppermute(piece, 'fsdp', [(i, (i + k) % NF_FAST) for i in range(NF_FAS...  22.5 us
    all_gather x4, waiting for transfers between devices, _gather_matrix(): x = lax.all_gather(z, 'dp', axis=1, tiled=False)  21.6 us
    dot_general x1, matrix products, on_device(): up_pre = jnp.dot(second_low, full_up, preferred_element_type=jnp.float32)  21.1 us
  transfers between devices with their start and end apart: 50, of which 32 were waited for; matrix products, arithmetic and copies ran while one was open for 30% of the time, Pallas kernels for 0%

profile of v4, /device:TPU:8, one launch (start us, length us, event | category | flops | bytes accessed | tf_op | source)
XLA Modules:
  0.0 529.9 jit_solution(8525581786635862067)
XLA Ops:
  16.8 4.7 collective-permute-start.4
  35.9 5.9 %collective-permute-done.13 = bf16[192,384]{1,0:T(8,128)(2,1)S(1)} collective-permute-done((bf16[192,384]{1,0:T(8,128)(2,1)S(1)}, bf16[192,384]{1,0:T(8,128)(2,1)S(1)}, u32[]{:S(2)}, u32[]{:S(2)}) %collective-permute-start.13) | collective-permute-done | bytes 147488 | tf_op jit(solution)/shard_map/ppermute | solution.py:70
  53.0 2.8 collective-permute-start.9
  59.9 4.2 collective-permute-done.9
  72.6 6.9 %all-gather.16.cloned.1.call-done = bf16[4,384,1152]{2,1,0:T(8,128)(2,1)} async-done(((bf16[4,48,1152]{2,1,0:T(8,128)(2,1)}), bf16[4,384,1152]{2,1,0:T(8,128)(2,1)}) %all-gather.16.cloned.1.call-update) | async-done | bytes 3538960 | tf_op jit(solution)/shard_map/all_gather | solution.py:82
  79.4 5.0 copy.51
  91.3 3.4 fusion.112
  102.6 8.3 %fusion.114 = (f32[12,576]{1,0:T(8,128)S(1)}, f32[12,576,576]{1,2,0:T(8,128)}) fusion(f32[576,12,64]{0,2,1:T(8,128)S(1)} %bitcast.243, f32[12,64]{1,0:T(8,128)S(1)} %mul.361, f32[576,12]{0,1:T(8,128)S(1)} %fusion.93, f32[576,12]{0,1:T(8,128)S(1)} %broadcast_multiply_fusion, f32[576,12,64]{0,2,1:T(8,128)S(1)} %bitcast.235, f32[12,64]{1,0:T(8,128)S(1)} %mul.355, ...), kind=kOutput, calls=%fused_computation.247 | convolution fusion | flops 525083904 | bytes 19940352 | tf_op jit(solution)/shard_map/while/body/eval_jaxpr/qhd,khd->hqk/dot_general | solution.py:193
  110.9 8.6 %fusion.3 = f32[12,576]{1,0:T(8,128)S(1)} fusion(f32[12,576,576]{1,2,0:T(8,128)} %get-tuple-element.112, f32[12,576]{1,0:T(8,128)S(1)} %get-tuple-element.111), kind=kLoop, calls=%fused_computation.14 | loop fusion | flops 7955712 | bytes 15980544 | tf_op jit(solution)/shard_map/while/body/eval_jaxpr/reduce_sum | solution.py:203
  119.6 9.7 %fusion.31 = bf16[12,64,576]{2,1,0:T(8,128)(2,1)S(1)} fusion(bf16[576,12,64]{0,2,1:T(8,128)(2,1)} %bitcast.268, f32[12,576,576]{1,2,0:T(8,128)} %get-tuple-element.112, f32[12,576]{1,0:T(8,128)S(1)} %fusion.3, f32[12,576]{1,0:T(8,128)S(1)} %get-tuple-element.111), kind=kOutput, calls=%fused_computation.92 | convolution fusion | flops 521994240 | bytes 17750016 | tf_op jit(solution)/shard_map/while/body/eval_jaxpr/hqk,khd->qhd/dot_general | solution.py:205
  131.9 9.4 %copy.58 = bf16[4,4,2,192,384]{4,2,3,1,0:T(2,128)(2,1)} copy(bf16[4,4,2,192,384]{4,3,2,1,0:T(8,128)(2,1)} %bitcast.262) | data formatting | bytes 9437184 | tf_op jit(solution)/shard_map/reshape | solution.py:83
  141.3 5.9 %copy.76 = bf16[384,8,2,384]{3,1,2,0:T(8,128)(2,1)} copy(bf16[384,8,2,384]{3,2,1,0:T(2,128)(2,1)} %bitcast.247) | data formatting | bytes 9437184
  147.2 14.7 %all-gather.20.cloned.1.call-done = bf16[4,384,1536]{2,1,0:T(8,128)(2,1)} async-done(((bf16[4,48,1536]{2,1,0:T(8,128)(2,1)}), bf16[4,384,1536]{2,1,0:T(8,128)(2,1)}) %all-gather.20.cloned.1.call-update) | async-done | bytes 4718608 | tf_op jit(solution)/shard_map/all_gather | solution.py:82
  161.9 9.4 %copy.57 = bf16[4,4,2,48,1536]{4,2,3,1,0:T(2,128)(2,1)} copy(bf16[4,4,2,48,1536]{4,3,2,1,0:T(8,128)(2,1)} %bitcast.263) | data formatting | bytes 9437184 | tf_op jit(solution)/shard_map/reshape | solution.py:83
  171.3 3.7 copy.75
  175.0 21.1 %multiply_convert_fusion = (bf16[576,3072]{1,0:T(8,128)(2,1)}, f32[576,3072]{1,0:T(8,128)}, f32[576,3072]{1,0:T(8,128)}) fusion(bf16[768,3072]{1,0:T(8,128)(2,1)S(1)} %bitcast.264, f32[576,768]{1,0:T(8,128)S(1)} %copy-done.9, f32[768]{0:T(1024)S(1)} %add.388, f32[768]{0:T(1024)S(1)} %mul.369, f32[576]{0:T(1024)S(1)} %fusion.96, ...), kind=kOutput, calls=%fused_computation.22 | convolution fusion | flops 2835136512 | bytes 24193536 | tf_op jit(solution)/shard_map/dot_general | solution.py:215
  196.2 9.2 %add_convert_fusion = bf16[576,3072]{1,0:T(8,128)(2,1)} fusion(f32[576,3072]{1,0:T(8,128)} %get-tuple-element.80, f32[576,3072]{1,0:T(8,128)} %get-tuple-element.115, bf16[3072,768]{1,0:T(8,128)(2,1)S(1)} %bitcast.261, bf16[576,768]{1,0:T(8,128)(2,1)S(1)} %copy-done.22, f32[576]{0:T(1024)S(1)} %fusion.94), kind=kOutput, calls=%fused_computation.21 | convolution fusion | flops 2744008704 | bytes 23300352 | tf_op jit(solution)/shard_map/dot_general | solution.py:224
  205.4 5.4 %multiply_reduce_fusion.2 = (f32[768]{0:T(1024)S(1)}, f32[576]{0:T(1024)S(1)}, f32[768]{0:T(1024)S(1)}, f32[576,768]{1,0:T(8,128)S(1)}) fusion(f32[576,768]{1,0:T(8,128)S(1)} %copy-done.9, f32[576]{0:T(1024)S(1)} %fusion.96, f32[576]{0:T(1024)S(1)} %broadcast_multiply_fusion.4, f32[768]{0:T(1024)S(1)} %mul.369, bf16[576,3072]{1,0:T(8,128)(2,1)} %add_convert_fusion, ...), kind=kOutput, calls=%fused_computation.79 | convolution fusion | flops 2721445888 | bytes 11812608 | tf_op jit(solution)/shard_map/dot_general | solution.py:230
  218.0 7.6 %convolution_convert_fusion = bf16[12,576,576]{1,2,0:T(8,128)(2,1)} fusion(bf16[576,12,64]{0,2,1:T(8,128)(2,1)} %bitcast.255, bf16[576,12,64]{0,2,1:T(8,128)(2,1)} %bitcast.269), kind=kOutput, calls=%fused_computation.36 | convolution fusion | flops 513589248 | bytes 9732096 | tf_op jit(solution)/shard_map/while/body/eval_jaxpr/qhd,khd->hqk/dot_general | solution.py:244
  225.6 9.9 %fusion.32 = bf16[12,64,576]{2,1,0:T(8,128)(2,1)} fusion(bf16[576,12,64]{0,2,1:T(8,128)(2,1)S(1)} %bitcast.256, f32[12,576,576]{1,2,0:T(8,128)} %get-tuple-element.112, f32[12,576]{1,0:T(8,128)S(1)} %log_add_fusion), kind=kOutput, calls=%fused_computation.93 | convolution fusion | flops 518012928 | bytes 17722368 | tf_op jit(solution)/shard_map/while/body/eval_jaxpr/hqk,qhd->khd/dot_general | solution.py:243
  235.5 12.0 %fusion = f32[12,576]{1,0:T(8,128)S(1)} fusion(bf16[12,576,576]{1,2,0:T(8,128)(2,1)} %convolution_convert_fusion, f32[12,576,576]{1,2,0:T(8,128)} %get-tuple-element.112, f32[12,576]{1,0:T(8,128)S(1)} %log_add_fusion), kind=kLoop, calls=%fused_computation.7 | loop fusion | flops 15918336 | bytes 23943168 | tf_op jit(solution)/shard_map/while/body/eval_jaxpr/reduce_sum | solution.py:246
  249.1 6.2 %fusion.2 = bf16[12,576,576]{1,2,0:T(8,128)(2,1)} fusion(bf16[12,576,576]{1,2,0:T(8,128)(2,1)S(1)} %copy-done.3, f32[12,576,576]{1,2,0:T(8,128)S(1)} %bitcast.232, f32[12,576]{1,0:T(8,128)S(1)} %fusion, f32[12,576]{1,0:T(8,128)S(1)} %log_add_fusion), kind=kLoop, calls=%fused_computation.9 | loop fusion | flops 19906560 | bytes 31905792 | tf_op jit(solution)/shard_map/while/body/eval_jaxpr/convert_element_type | solution.py:247
  255.4 8.2 %fusion.23 = (f32[576,12]{0,1:T(8,128)S(1)}, f32[12,64,576]{2,1,0:T(8,128)}) fusion(f32[576,12,64]{0,2,1:T(8,128)} %bitcast.242, f32[12,64]{1,0:T(8,128)S(1)} %copy-done.36, f32[576,12]{0,1:T(8,128)S(1)} %broadcast_multiply_fusion, bf16[12,576,576]{1,2,0:T(8,128)(2,1)} %fusion.2, f32[576,12,64]{0,2,1:T(8,128)S(1)} %bitcast.236, f32[12,64]{1,0:T(8,128)S(1)} %mul.355, ...), kind=kOutput, calls=%fused_computation.63 | convolution fusion | flops 513139968 | bytes 13387776 | tf_op jit(solution)/shard_map/while/body/eval_jaxpr/hqk,qhd->khd/dot_general | solution.py:252
  270.3 3.4 fusion.35
  273.7 2.8 copy-done.19
  278.7 6.3 %fusion.107 = f32[768,3072]{1,0:T(8,128)S(1)} fusion(bf16[576,3072]{1,0:T(8,128)(2,1)} %add_convert_fusion, f32[576,768]{1,0:T(8,128)S(1)} %copy-done.10, f32[768]{0:T(1024)S(1)} %add.388, f32[768]{0:T(1024)S(1)} %mul.369, f32[576]{0:T(1024)S(1)} %fusion.96, f32[576]{0:T(1024)S(1)} %broadcast_multiply_fusion.4), kind=kOutput, calls=%fused_computation.241 | convolution fusion | flops 2720120832 | bytes 14756352 | tf_op jit(solution)/shard_map/dot_general | solution.py:227
  287.3 3.9 constant_dynamic-slice_fusion.4
  296.5 2.8 constant_dynamic-slice_fusion.2
  299.4 4.1 collective-permute-done.16
  309.2 7.0 %collective-permute-done.17 = bf16[4,48,1152]{2,1,0:T(8,128)(2,1)S(1)} collective-permute-done((bf16[4,48,1152]{2,1,0:T(8,128)(2,1)S(1)}, bf16[4,48,1152]{2,1,0:T(8,128)(2,1)S(1)}, u32[]{:S(2)}, u32[]{:S(2)}) %collective-permute-start.17) | collective-permute-done | bytes 442400 | tf_op jit(solution)/shard_map/ppermute | solution.py:123
  323.5 3.1 collective-permute-done.19
  328.7 4.4 collective-permute-done.30
  336.9 6.0 %fusion.56 = f32[3072,768]{1,0:T(8,128)S(1)} fusion(bf16[576,3072]{1,0:T(8,128)(2,1)} %get-tuple-element.79, bf16[576,768]{1,0:T(8,128)(2,1)S(1)} %copy-done.23, f32[576]{0:T(1024)S(1)} %fusion.94), kind=kOutput, calls=%fused_computation.132 | convolution fusion | flops 2719236096 | bytes 13863168 | tf_op jit(solution)/shard_map/dot_general | solution.py:223
  343.0 3.6 copy-done.17
  354.3 8.6 %collective-permute-done.33 = bf16[48,1536]{1,0:T(8,128)(2,1)S(1)} collective-permute-done((bf16[48,1536]{1,0:T(8,128)(2,1)S(1)}, bf16[48,1536]{1,0:T(8,128)(2,1)S(1)}, u32[]{:S(2)}, u32[]{:S(2)}) %collective-permute-start.33) | collective-permute-done | bytes 147488 | tf_op jit(solution)/shard_map/ppermute | solution.py:129
  371.6 12.7 %collective-permute-done.37 = bf16[4,192,384]{2,1,0:T(8,128)(2,1)S(1)} collective-permute-done((bf16[4,192,384]{2,1,0:T(8,128)(2,1)S(1)}, bf16[4,192,384]{2,1,0:T(8,128)(2,1)S(1)}, u32[]{:S(2)}, u32[]{:S(2)}) %collective-permute-start.37) | collective-permute-done | bytes 589856 | tf_op jit(solution)/shard_map/ppermute | solution.py:116
  387.1 2.7 fusion.116
  389.8 13.0 %collective-permute-done.38 = bf16[4,192,384]{2,1,0:T(8,128)(2,1)} collective-permute-done((bf16[4,192,384]{2,1,0:T(8,128)(2,1)}, bf16[4,192,384]{2,1,0:T(8,128)(2,1)}, u32[]{:S(2)}, u32[]{:S(2)}) %collective-permute-start.38) | collective-permute-done | bytes 589856 | tf_op jit(solution)/shard_map/ppermute | solution.py:123
  406.2 3.1 collective-permute-start.40
  414.4 4.3 collective-permute-done.42
  418.7 4.1 collective-permute-done.41
  423.6 5.7 %fusion.109 = (f32[768]{0:T(1024)S(1)}, f32[576]{0:T(1024)S(1)}, f32[576,768]{1,0:T(8,128)S(1)}) fusion(f32[768]{0:T(1024)S(1)} %copy-done.44, f32[576]{0:T(1024)S(1)} %copy-done.38, bf16[576,768]{1,0:T(8,128)(2,1)S(1)} %copy-done.13, bf16[768,2304]{1,0:T(8,128)(2,1)} %bitcast.271, bf16[576,768]{0,1:T(8,128)(2,1)} %bitcast.288, ...), kind=kOutput, calls=%fused_computation.243 | convolution fusion | flops 2049047296 | bytes 8858112 | tf_op jit(solution)/shard_map/dot_general | solution.py:271
  430.4 6.5 %multiply_convert_fusion.3 = bf16[576,768]{1,0:T(8,128)(2,1)} fusion(f32[576,768]{1,0:T(8,128)S(1)} %copy-done.10, bf16[576,3072]{1,0:T(8,128)(2,1)S(1)} %copy-done.52, bf16[3072,768]{1,0:T(8,128)(2,1)} %bitcast.258, f32[576]{0:T(1024)S(1)} %fusion.94), kind=kOutput, calls=%fused_computation.85 | convolution fusion | flops 2719236096 | bytes 10914048 | tf_op jit(solution)/shard_map/dot_general | solution.py:218
  439.6 3.9 collective-permute-done.23
  447.8 41.5 %psum.7 = f32[6,768]{1,0:T(8,128)S(1)} all-reduce(f32[6,768]{1,0:T(8,128)S(1)} %concatenate.12), channel_id=1, replica_groups=mesh['dp'=8,'fsdp'=4] {'dp','fsdp'}, use_global_device_ids=true, to_apply=%region_27.28 | all-reduce | flops 4608 | bytes 36864 | tf_op jit(solution)/shard_map/psum | solution.py:139
  496.4 11.1 %all-gather.5 = f32[384,384]{1,0:T(8,128)S(1)} all-gather(f32[48,384]{1,0:T(8,128)S(1)} %fusion.88), channel_id=7, replica_groups=mesh['dp'=8,'fsdp'=4] {'dp'}, dimensions={0}, use_global_device_ids=true | all-gather | bytes 663552 | tf_op jit(solution)/shard_map/all_gather | solution.py:132
  512.4 3.5 copy.66
  517.7 3.5 copy.67
  (335 shorter events, 160.1 us)
Async XLA Ops:
  7.2 61.9 %all-gather.18.cloned.1.call-start = ((), (), s32[]{:S(2)}) async-start(), calls=%async_computation.1 | async-start | bytes 1327104 | tf_op jit(solution)/shard_map/all_gather | solution.py:82
  8.0 5.4 %collective-permute-start.7 = (bf16[48,384]{1,0:T(8,128)(2,1)S(1)}, bf16[48,384]{1,0:T(8,128)(2,1)S(1)}, u32[]{:S(2)}, u32[]{:S(2)}) collective-permute-start(bf16[48,384]{1,0:T(8,128)(2,1)S(1)} %dynamic_slice.167), channel_id=1, source_target_pairs={{0,2},{1,3},{2,0},{3,1},{4,6},{5,7},{6,4},{7,5},{8,10},{9,11},{10,... | collective-permute-start | bytes 110600 | tf_op jit(solution)/shard_map/ppermute | solution.py:70
  15.9 63.6 %all-gather.16.cloned.1.call-start = ((), (), s32[]{:S(2)}) async-start(), calls=%async_computation | async-start | bytes 3981312 | tf_op jit(solution)/shard_map/all_gather | solution.py:82
  16.8 10.1 %collective-permute-start.4 = (bf16[48,1152]{1,0:T(8,128)(2,1)S(1)}, bf16[48,1152]{1,0:T(8,128)(2,1)S(1)}, u32[]{:S(2)}, u32[]{:S(2)}) collective-permute-start(bf16[48,1152]{1,0:T(8,128)(2,1)S(1)} %dynamic_slice.166), channel_id=1, source_target_pairs={{0,2},{1,3},{2,0},{3,1},{4,6},{5,7},{6,4},{7,5},{8,10},{9,11},{10,... | collective-permute-start | bytes 331784 | tf_op jit(solution)/shard_map/ppermute | solution.py:70
  21.5 6.6 %collective-permute-start.3 = (bf16[48,1152]{1,0:T(8,128)(2,1)S(1)}, bf16[48,1152]{1,0:T(8,128)(2,1)S(1)}, u32[]{:S(2)}, u32[]{:S(2)}) collective-permute-start(bf16[48,1152]{1,0:T(8,128)(2,1)S(1)} %dynamic_slice.166), channel_id=1, source_target_pairs={{0,1},{1,2},{2,3},{3,0},{4,5},{5,6},{6,7},{7,4},{8,9},{9,10},{10,1... | collective-permute-start | bytes 331784 | tf_op jit(solution)/shard_map/ppermute | solution.py:70
  21.5 7.6 %collective-permute-start.5 = (bf16[48,1152]{1,0:T(8,128)(2,1)S(1)}, bf16[48,1152]{1,0:T(8,128)(2,1)S(1)}, u32[]{:S(2)}, u32[]{:S(2)}) collective-permute-start(bf16[48,1152]{1,0:T(8,128)(2,1)S(1)} %dynamic_slice.166), channel_id=1, source_target_pairs={{0,3},{1,0},{2,1},{3,2},{4,7},{5,4},{6,5},{7,6},{8,11},{9,8},{10,9... | collective-permute-start | bytes 331784 | tf_op jit(solution)/shard_map/ppermute | solution.py:70
  30.6 101.4 %all-gather.22.cloned.1.call-start = ((), (), s32[]{:S(2)}) async-start(), calls=%async_computation.3 | async-start | bytes 5308416 | tf_op jit(solution)/shard_map/all_gather | solution.py:82
  31.6 10.2 %collective-permute-start.13 = (bf16[192,384]{1,0:T(8,128)(2,1)S(1)}, bf16[192,384]{1,0:T(8,128)(2,1)S(1)}, u32[]{:S(2)}, u32[]{:S(2)}) collective-permute-start(bf16[192,384]{1,0:T(8,128)(2,1)S(1)} %dynamic_slice.169), channel_id=1, source_target_pairs={{0,2},{1,3},{2,0},{3,1},{4,6},{5,7},{6,4},{7,5},{8,10},{9,11},{10,... | collective-permute-start | bytes 442376 | tf_op jit(solution)/shard_map/ppermute | solution.py:70
  32.9 11.0 %collective-permute-start.12 = (bf16[192,384]{1,0:T(8,128)(2,1)S(1)}, bf16[192,384]{1,0:T(8,128)(2,1)S(1)}, u32[]{:S(2)}, u32[]{:S(2)}) collective-permute-start(bf16[192,384]{1,0:T(8,128)(2,1)S(1)} %dynamic_slice.169), channel_id=1, source_target_pairs={{0,1},{1,2},{2,3},{3,0},{4,5},{5,6},{6,7},{7,4},{8,9},{9,10},{10,1... | collective-permute-start | bytes 442376 | tf_op jit(solution)/shard_map/ppermute | solution.py:70
  33.8 11.5 %collective-permute-start.14 = (bf16[192,384]{1,0:T(8,128)(2,1)S(1)}, bf16[192,384]{1,0:T(8,128)(2,1)S(1)}, u32[]{:S(2)}, u32[]{:S(2)}) collective-permute-start(bf16[192,384]{1,0:T(8,128)(2,1)S(1)} %dynamic_slice.169), channel_id=1, source_target_pairs={{0,3},{1,0},{2,1},{3,2},{4,7},{5,4},{6,5},{7,6},{8,11},{9,8},{10,9... | collective-permute-start | bytes 442376 | tf_op jit(solution)/shard_map/ppermute | solution.py:70
  46.9 115.0 %all-gather.20.cloned.1.call-start = ((), (), s32[]{:S(2)}) async-start(), calls=%async_computation.2 | async-start | bytes 5308416 | tf_op jit(solution)/shard_map/all_gather | solution.py:82
  47.0 11.6 %collective-permute-start.1 = (bf16[6,192]{1,0:T(8,128)(2,1)S(1)}, bf16[6,192]{1,0:T(8,128)(2,1)S(1)}, u32[]{:S(2)}, u32[]{:S(2)}) collective-permute-start(bf16[6,192]{1,0:T(8,128)(2,1)S(1)} %get-tuple-element.110), channel_id=1, source_target_pairs={{0,2},{1,3},{2,0},{3,1},{4,6},{5,7},{6,4},{7,5},{8,10},{9,11},{10,... | collective-permute-start | bytes 6920 | tf_op jit(solution)/shard_map/ppermute | solution.py:70
  47.1 12.2 %collective-permute-start = (bf16[6,192]{1,0:T(8,128)(2,1)S(1)}, bf16[6,192]{1,0:T(8,128)(2,1)S(1)}, u32[]{:S(2)}, u32[]{:S(2)}) collective-permute-start(bf16[6,192]{1,0:T(8,128)(2,1)S(1)} %get-tuple-element.110), channel_id=1, source_target_pairs={{0,1},{1,2},{2,3},{3,0},{4,5},{5,6},{6,7},{7,4},{8,9},{9,10},{10,1... | collective-permute-start | bytes 6920 | tf_op jit(solution)/shard_map/ppermute | solution.py:70
  48.4 10.8 %collective-permute-start.2 = (bf16[6,192]{1,0:T(8,128)(2,1)S(1)}, bf16[6,192]{1,0:T(8,128)(2,1)S(1)}, u32[]{:S(2)}, u32[]{:S(2)}) collective-permute-start(bf16[6,192]{1,0:T(8,128)(2,1)S(1)} %get-tuple-element.110), channel_id=1, source_target_pairs={{0,3},{1,0},{2,1},{3,2},{4,7},{5,4},{6,5},{7,6},{8,11},{9,8},{10,9... | collective-permute-start | bytes 6920 | tf_op jit(solution)/shard_map/ppermute | solution.py:70
  50.5 9.4 %collective-permute-start.10 = (bf16[48,1536]{1,0:T(8,128)(2,1)S(1)}, bf16[48,1536]{1,0:T(8,128)(2,1)S(1)}, u32[]{:S(2)}, u32[]{:S(2)}) collective-permute-start(bf16[48,1536]{1,0:T(8,128)(2,1)S(1)} %dynamic_slice.168), channel_id=1, source_target_pairs={{0,2},{1,3},{2,0},{3,1},{4,6},{5,7},{6,4},{7,5},{8,10},{9,11},{10,... | collective-permute-start | bytes 442376 | tf_op jit(solution)/shard_map/ppermute | solution.py:70
  53.0 11.0 %collective-permute-start.9 = (bf16[48,1536]{1,0:T(8,128)(2,1)S(1)}, bf16[48,1536]{1,0:T(8,128)(2,1)S(1)}, u32[]{:S(2)}, u32[]{:S(2)}) collective-permute-start(bf16[48,1536]{1,0:T(8,128)(2,1)S(1)} %dynamic_slice.168), channel_id=1, source_target_pairs={{0,1},{1,2},{2,3},{3,0},{4,5},{5,6},{6,7},{7,4},{8,9},{9,10},{10,1... | collective-permute-start | bytes 442376 | tf_op jit(solution)/shard_map/ppermute | solution.py:70
  58.6 7.0 %collective-permute-start.11 = (bf16[48,1536]{1,0:T(8,128)(2,1)S(1)}, bf16[48,1536]{1,0:T(8,128)(2,1)S(1)}, u32[]{:S(2)}, u32[]{:S(2)}) collective-permute-start(bf16[48,1536]{1,0:T(8,128)(2,1)S(1)} %dynamic_slice.168), channel_id=1, source_target_pairs={{0,3},{1,0},{2,1},{3,2},{4,7},{5,4},{6,5},{7,6},{8,11},{9,8},{10,9... | collective-permute-start | bytes 442376 | tf_op jit(solution)/shard_map/ppermute | solution.py:70
  67.1 441.6 %all-gather.24.cloned.1.call-start = ((), (), s32[]{:S(2)}) async-start(), calls=%async_computation.4 | async-start | bytes 1990656 | tf_op jit(solution)/shard_map/all_gather | solution.py:132
  278.0 13.3 %collective-permute-start.15 = (bf16[4,4,48,1152]{3,2,1,0:T(8,128)(2,1)}, bf16[4,4,48,1152]{3,2,1,0:T(8,128)(2,1)}, u32[]{:S(2)}, u32[]{:S(2)}) collective-permute-start(bf16[4,4,48,1152]{3,2,1,0:T(8,128)(2,1)} %bitcast.46), channel_id=1, source_target_pairs={{0,4},{4,0},{8,12},{12,8},{16,20},{20,16},{24,28},{28,24},{1,5},{5... | collective-permute-start | bytes 5308424 | tf_op jit(solution)/shard_map/ppermute | solution.py:110
  287.1 19.7 %collective-permute-start.29 = (bf16[4,4,48,1536]{3,2,1,0:T(8,128)(2,1)}, bf16[4,4,48,1536]{3,2,1,0:T(8,128)(2,1)}, u32[]{:S(2)}, u32[]{:S(2)}) collective-permute-start(bf16[4,4,48,1536]{3,2,1,0:T(8,128)(2,1)} %bitcast.71), channel_id=1, source_target_pairs={{0,4},{4,0},{8,12},{12,8},{16,20},{20,16},{24,28},{28,24},{1,5},{5... | collective-permute-start | bytes 7077896 | tf_op jit(solution)/shard_map/ppermute | solution.py:110
  295.0 8.5 %collective-permute-start.16 = (bf16[4,48,1152]{2,1,0:T(8,128)(2,1)S(1)}, bf16[4,48,1152]{2,1,0:T(8,128)(2,1)}, u32[]{:S(2)}, u32[]{:S(2)}) collective-permute-start(bf16[4,48,1152]{2,1,0:T(8,128)(2,1)S(1)} %fusion.55), channel_id=1, source_target_pairs={{0,8},{4,20},{8,0},{12,28},{16,24},{20,4},{24,16},{28,12},{1,9},{5... | collective-permute-start | bytes 1327112 | tf_op jit(solution)/shard_map/ppermute | solution.py:116
  304.7 11.5 %collective-permute-start.17 = (bf16[4,48,1152]{2,1,0:T(8,128)(2,1)S(1)}, bf16[4,48,1152]{2,1,0:T(8,128)(2,1)S(1)}, u32[]{:S(2)}, u32[]{:S(2)}) collective-permute-start(bf16[4,48,1152]{2,1,0:T(8,128)(2,1)S(1)} %get-tuple-element.87), channel_id=1, source_target_pairs={{0,8},{4,12},{8,0},{12,4},{16,24},{20,28},{24,16},{28,20},{1,9},{5... | collective-permute-start | bytes 1327112 | tf_op jit(solution)/shard_map/ppermute | solution.py:123
  306.2 11.2 %collective-permute-start.18 = (bf16[4,48,1152]{2,1,0:T(8,128)(2,1)S(1)}, bf16[4,48,1152]{2,1,0:T(8,128)(2,1)S(1)}, u32[]{:S(2)}, u32[]{:S(2)}) collective-permute-start(bf16[4,48,1152]{2,1,0:T(8,128)(2,1)S(1)} %get-tuple-element.88), channel_id=1, source_target_pairs={{0,16},{4,20},{8,24},{12,28},{16,0},{20,4},{24,8},{28,12},{1,17},{... | collective-permute-start | bytes 1327112 | tf_op jit(solution)/shard_map/ppermute | solution.py:124
  317.6 9.1 %collective-permute-start.19 = (bf16[48,1152]{1,0:T(8,128)(2,1)S(1)}, bf16[48,1152]{1,0:T(8,128)(2,1)S(1)}, u32[]{:S(2)}, u32[]{:S(2)}) collective-permute-start(bf16[48,1152]{1,0:T(8,128)(2,1)S(1)} %get-tuple-element.97), channel_id=1, source_target_pairs={{0,1},{1,2},{2,3},{3,0},{4,5},{5,6},{6,7},{7,4},{8,9},{9,10},{10,1... | collective-permute-start | bytes 331784 | tf_op jit(solution)/shard_map/ppermute | solution.py:129
  319.1 8.5 %collective-permute-start.21 = (bf16[48,1152]{1,0:T(8,128)(2,1)S(1)}, bf16[48,1152]{1,0:T(8,128)(2,1)S(1)}, u32[]{:S(2)}, u32[]{:S(2)}) collective-permute-start(bf16[48,1152]{1,0:T(8,128)(2,1)S(1)} %get-tuple-element.98), channel_id=1, source_target_pairs={{0,3},{1,0},{2,1},{3,2},{4,7},{5,4},{6,5},{7,6},{8,11},{9,8},{10,9... | collective-permute-start | bytes 331784 | tf_op jit(solution)/shard_map/ppermute | solution.py:129
  319.7 8.2 %collective-permute-start.20 = (bf16[48,1152]{1,0:T(8,128)(2,1)S(1)}, bf16[48,1152]{1,0:T(8,128)(2,1)S(1)}, u32[]{:S(2)}, u32[]{:S(2)}) collective-permute-start(bf16[48,1152]{1,0:T(8,128)(2,1)S(1)} %get-tuple-element.99), channel_id=1, source_target_pairs={{0,2},{1,3},{2,0},{3,1},{4,6},{5,7},{6,4},{7,5},{8,10},{9,11},{10,... | collective-permute-start | bytes 331784 | tf_op jit(solution)/shard_map/ppermute | solution.py:129
  323.0 10.1 %collective-permute-start.30 = (bf16[4,48,1536]{2,1,0:T(8,128)(2,1)}, bf16[4,48,1536]{2,1,0:T(8,128)(2,1)S(1)}, u32[]{:S(2)}, u32[]{:S(2)}) collective-permute-start(bf16[4,48,1536]{2,1,0:T(8,128)(2,1)} %fusion.53), channel_id=1, source_target_pairs={{0,8},{4,20},{8,0},{12,28},{16,24},{20,4},{24,16},{28,12},{1,9},{5... | collective-permute-start | bytes 1769480 | tf_op jit(solution)/shard_map/ppermute | solution.py:116
  328.6 183.8 %all-gather.26.cloned.1.call-start = ((), (), s32[]{:S(2)}) async-start(), calls=%async_computation.5 | async-start | bytes 2654208 | tf_op jit(solution)/shard_map/all_gather | solution.py:132
  335.0 14.2 %collective-permute-start.31 = (bf16[4,48,1536]{2,1,0:T(8,128)(2,1)S(1)}, bf16[4,48,1536]{2,1,0:T(8,128)(2,1)S(1)}, u32[]{:S(2)}, u32[]{:S(2)}) collective-permute-start(bf16[4,48,1536]{2,1,0:T(8,128)(2,1)S(1)} %get-tuple-element.83), channel_id=1, source_target_pairs={{0,8},{4,12},{8,0},{12,4},{16,24},{20,28},{24,16},{28,20},{1,9},{5... | collective-permute-start | bytes 1769480 | tf_op jit(solution)/shard_map/ppermute | solution.py:123
  335.6 13.9 %collective-permute-start.32 = (bf16[4,48,1536]{2,1,0:T(8,128)(2,1)S(1)}, bf16[4,48,1536]{2,1,0:T(8,128)(2,1)S(1)}, u32[]{:S(2)}, u32[]{:S(2)}) collective-permute-start(bf16[4,48,1536]{2,1,0:T(8,128)(2,1)S(1)} %get-tuple-element.84), channel_id=1, source_target_pairs={{0,16},{4,20},{8,24},{12,28},{16,0},{20,4},{24,8},{28,12},{1,17},{... | collective-permute-start | bytes 1769480 | tf_op jit(solution)/shard_map/ppermute | solution.py:124
  348.3 20.0 %collective-permute-start.36 = (bf16[4,4,192,384]{3,2,1,0:T(8,128)(2,1)}, bf16[4,4,192,384]{3,2,1,0:T(8,128)(2,1)}, u32[]{:S(2)}, u32[]{:S(2)}) collective-permute-start(bf16[4,4,192,384]{3,2,1,0:T(8,128)(2,1)} %bitcast.83), channel_id=1, source_target_pairs={{0,4},{4,0},{8,12},{12,8},{16,20},{20,16},{24,28},{28,24},{1,5},{5... | collective-permute-start | bytes 7077896 | tf_op jit(solution)/shard_map/ppermute | solution.py:110
  351.3 11.7 %collective-permute-start.33 = (bf16[48,1536]{1,0:T(8,128)(2,1)S(1)}, bf16[48,1536]{1,0:T(8,128)(2,1)S(1)}, u32[]{:S(2)}, u32[]{:S(2)}) collective-permute-start(bf16[48,1536]{1,0:T(8,128)(2,1)S(1)} %get-tuple-element.94), channel_id=1, source_target_pairs={{0,1},{1,2},{2,3},{3,0},{4,5},{5,6},{6,7},{7,4},{8,9},{9,10},{10,1... | collective-permute-start | bytes 442376 | tf_op jit(solution)/shard_map/ppermute | solution.py:129
  352.8 11.1 %collective-permute-start.35 = (bf16[48,1536]{1,0:T(8,128)(2,1)S(1)}, bf16[48,1536]{1,0:T(8,128)(2,1)S(1)}, u32[]{:S(2)}, u32[]{:S(2)}) collective-permute-start(bf16[48,1536]{1,0:T(8,128)(2,1)S(1)} %get-tuple-element.95), channel_id=1, source_target_pairs={{0,3},{1,0},{2,1},{3,2},{4,7},{5,4},{6,5},{7,6},{8,11},{9,8},{10,9... | collective-permute-start | bytes 442376 | tf_op jit(solution)/shard_map/ppermute | solution.py:129
  353.3 11.2 %collective-permute-start.34 = (bf16[48,1536]{1,0:T(8,128)(2,1)S(1)}, bf16[48,1536]{1,0:T(8,128)(2,1)S(1)}, u32[]{:S(2)}, u32[]{:S(2)}) collective-permute-start(bf16[48,1536]{1,0:T(8,128)(2,1)S(1)} %get-tuple-element.96), channel_id=1, source_target_pairs={{0,2},{1,3},{2,0},{3,1},{4,6},{5,7},{6,4},{7,5},{8,10},{9,11},{10,... | collective-permute-start | bytes 442376 | tf_op jit(solution)/shard_map/ppermute | solution.py:129
  365.3 152.4 %all-gather.28.cloned.1.call-start = ((), (), s32[]{:S(2)}) async-start(), calls=%async_computation.6 | async-start | bytes 2654208 | tf_op jit(solution)/shard_map/all_gather | solution.py:132
  370.6 13.6 %collective-permute-start.37 = (bf16[4,192,384]{2,1,0:T(8,128)(2,1)S(1)}, bf16[4,192,384]{2,1,0:T(8,128)(2,1)S(1)}, u32[]{:S(2)}, u32[]{:S(2)}) collective-permute-start(bf16[4,192,384]{2,1,0:T(8,128)(2,1)S(1)} %fusion.54), channel_id=1, source_target_pairs={{0,8},{4,20},{8,0},{12,28},{16,24},{20,4},{24,16},{28,12},{1,9},{5... | collective-permute-start | bytes 1769480 | tf_op jit(solution)/shard_map/ppermute | solution.py:116
  385.4 17.4 %collective-permute-start.38 = (bf16[4,192,384]{2,1,0:T(8,128)(2,1)}, bf16[4,192,384]{2,1,0:T(8,128)(2,1)}, u32[]{:S(2)}, u32[]{:S(2)}) collective-permute-start(bf16[4,192,384]{2,1,0:T(8,128)(2,1)} %get-tuple-element.81), channel_id=1, source_target_pairs={{0,8},{4,12},{8,0},{12,4},{16,24},{20,28},{24,16},{28,20},{1,9},{5... | collective-permute-start | bytes 1769480 | tf_op jit(solution)/shard_map/ppermute | solution.py:123
  385.8 18.6 %collective-permute-start.39 = (bf16[4,192,384]{2,1,0:T(8,128)(2,1)S(1)}, bf16[4,192,384]{2,1,0:T(8,128)(2,1)}, u32[]{:S(2)}, u32[]{:S(2)}) collective-permute-start(bf16[4,192,384]{2,1,0:T(8,128)(2,1)S(1)} %get-tuple-element.82), channel_id=1, source_target_pairs={{0,16},{4,20},{8,24},{12,28},{16,0},{20,4},{24,8},{28,12},{1,17},{... | collective-permute-start | bytes 1769480 | tf_op jit(solution)/shard_map/ppermute | solution.py:124
  406.2 8.2 %collective-permute-start.40 = (bf16[192,384]{1,0:T(8,128)(2,1)S(1)}, bf16[192,384]{1,0:T(8,128)(2,1)S(1)}, u32[]{:S(2)}, u32[]{:S(2)}) collective-permute-start(bf16[192,384]{1,0:T(8,128)(2,1)S(1)} %get-tuple-element.91), channel_id=1, source_target_pairs={{0,1},{1,2},{2,3},{3,0},{4,5},{5,6},{6,7},{7,4},{8,9},{9,10},{10,1... | collective-permute-start | bytes 442376 | tf_op jit(solution)/shard_map/ppermute | solution.py:129
  409.3 9.4 %collective-permute-start.42 = (bf16[192,384]{1,0:T(8,128)(2,1)S(1)}, bf16[192,384]{1,0:T(8,128)(2,1)S(1)}, u32[]{:S(2)}, u32[]{:S(2)}) collective-permute-start(bf16[192,384]{1,0:T(8,128)(2,1)S(1)} %get-tuple-element.92), channel_id=1, source_target_pairs={{0,3},{1,0},{2,1},{3,2},{4,7},{5,4},{6,5},{7,6},{8,11},{9,8},{10,9... | collective-permute-start | bytes 442376 | tf_op jit(solution)/shard_map/ppermute | solution.py:129
  410.9 11.9 %collective-permute-start.41 = (bf16[192,384]{1,0:T(8,128)(2,1)S(1)}, bf16[192,384]{1,0:T(8,128)(2,1)S(1)}, u32[]{:S(2)}, u32[]{:S(2)}) collective-permute-start(bf16[192,384]{1,0:T(8,128)(2,1)S(1)} %get-tuple-element.93), channel_id=1, source_target_pairs={{0,2},{1,3},{2,0},{3,1},{4,6},{5,7},{6,4},{7,5},{8,10},{9,11},{10,... | collective-permute-start | bytes 442376 | tf_op jit(solution)/shard_map/ppermute | solution.py:129
  413.2 23.6 %collective-permute-start.22 = (bf16[4,4,48,384]{3,2,1,0:T(8,128)(2,1)S(1)}, bf16[4,4,48,384]{3,2,1,0:T(8,128)(2,1)}, u32[]{:S(2)}, u32[]{:S(2)}) collective-permute-start(bf16[4,4,48,384]{3,2,1,0:T(8,128)(2,1)S(1)} %bitcast.290), channel_id=1, source_target_pairs={{0,4},{4,0},{8,12},{12,8},{16,20},{20,16},{24,28},{28,24},{1,5},{5... | collective-permute-start | bytes 1769480 | tf_op jit(solution)/shard_map/ppermute | solution.py:110
  438.2 5.2 collective-permute-start.23
  443.5 45.8 %collective-permute-start.24 = (bf16[4,48,384]{2,1,0:T(8,128)(2,1)S(1)}, bf16[4,48,384]{2,1,0:T(8,128)(2,1)S(1)}, u32[]{:S(2)}, u32[]{:S(2)}) collective-permute-start(bf16[4,48,384]{2,1,0:T(8,128)(2,1)S(1)} %get-tuple-element.89), channel_id=1, source_target_pairs={{0,8},{4,12},{8,0},{12,4},{16,24},{20,28},{24,16},{28,20},{1,9},{5... | collective-permute-start | bytes 442376 | tf_op jit(solution)/shard_map/ppermute | solution.py:123
  444.9 44.5 %collective-permute-start.25 = (bf16[4,48,384]{2,1,0:T(8,128)(2,1)S(1)}, bf16[4,48,384]{2,1,0:T(8,128)(2,1)S(1)}, u32[]{:S(2)}, u32[]{:S(2)}) collective-permute-start(bf16[4,48,384]{2,1,0:T(8,128)(2,1)S(1)} %get-tuple-element.90), channel_id=1, source_target_pairs={{0,16},{4,20},{8,24},{12,28},{16,0},{20,4},{24,8},{28,12},{1,17},{... | collective-permute-start | bytes 442376 | tf_op jit(solution)/shard_map/ppermute | solution.py:124
  489.5 4.1 collective-permute-start.26
  490.2 4.3 collective-permute-start.28
  491.5 4.9 collective-permute-start.27
  (62 other events, 569.0 us)
Sparse Core Ops, SparseCore 0:
  16.0 27.0 all-gather.17
  45.6 33.8 all-gather.15
  81.9 38.7 all-gather.21
  123.1 38.7 all-gather.19
  328.7 29.4 all-gather.23
  365.5 37.2 all-gather.25
  423.7 31.7 all-gather.27

commit v5 on v4

--- a/solution.py
+++ b/solution.py
@@ -73,26 +73,41 @@
     return _take(jnp.stack(slots), (f - jnp.arange(NF_FAST, dtype=jnp.int32)) % NF_FAST, 0)
 
 
-def _gather_matrix(m):
+def _gather_full(z, rows, cols, out_rows):
+    x = lax.all_gather(z, "dp", axis=1, tiled=False)
+    x = x.reshape(NF_FAST, NDP_FAST // 2, 2, rows, cols).transpose(0, 1, 3, 2, 4)
+    return x.reshape(out_rows, 2 * cols)
+
+
+def fast_gather(mats, gains):
     d = lax.axis_index("dp")
     j, c = d // 2, d % 2
-    rows, cols = m.shape[0] // (NDP_FAST // 2), m.shape[1] // 2
-    piece = lax.dynamic_slice(m, (j * rows, c * cols), (rows, cols))
-    z = _z_gather(piece)
-    x = lax.all_gather(z, "dp", axis=1, tiled=False)
-    x = x.reshape(NF_FAST, NDP_FAST // 2, 2, rows, cols).transpose(0, 1, 3, 2, 4)
-    return x.reshape(NF_FAST * m.shape[0], m.shape[1])
-
-
-def fast_gather(mats, gains):
-    out = [_gather_matrix(m) for m in mats]
+    n_chips = NDP_FAST // 2
+    height = mats[0].shape[0] // n_chips
+    blocks, shapes = [], []
+    for m in mats:
+        rows, cols = m.shape[0] // n_chips, m.shape[1] // 2
+        piece = lax.dynamic_slice(m, (j * rows, c * cols), (rows, cols))
+        shapes.append((rows, cols))
+        blocks.append(piece.reshape(height, rows * cols // height))
     stacked = jnp.concatenate(gains, axis=0)
-    z = _z_gather(stacked)
-    full = z.transpose(1, 0, 2).reshape(stacked.shape[0], NF_FAST * stacked.shape[1])
-    rows = 0
-    for g in gains:
-        out.append(full[rows : rows + g.shape[0]])
-        rows += g.shape[0]
+    flat = stacked.reshape(-1)
+    blocks.append(jnp.pad(flat, (0, height * LANES - flat.shape[0])).reshape(height, LANES))
+    z = _z_gather(jnp.concatenate(blocks, axis=1))
+    out = []
+    offset = 0
+    for m, (rows, cols) in zip(mats, shapes):
+        width = rows * cols // height
+        part = z[:, :, offset : offset + width].reshape(NF_FAST, rows, cols)
+        out.append(_gather_full(part, rows, cols, NF_FAST * m.shape[0]))
+        offset += width
+    g = z[:, :, offset:].reshape(NF_FAST, -1)[:, : flat.shape[0]]
+    g = g.reshape(NF_FAST, stacked.shape[0], stacked.shape[1]).transpose(1, 0, 2)
+    g = g.reshape(stacked.shape[0], NF_FAST * stacked.shape[1])
+    row = 0
+    for gain in gains:
+        out.append(g[row : row + gain.shape[0]])
+        row += gain.shape[0]
     return out
 
 
@@ -135,11 +150,13 @@
 
 
 def fast_reduce(mats, gains):
-    out = [_reduce_matrix(m) for m in mats]
-    stacked = lax.psum(jnp.concatenate(gains, axis=0), ("dp", "fsdp"))
-    f = lax.axis_index("fsdp")
-    width = stacked.shape[1] // NF_FAST
-    mine = lax.dynamic_slice_in_dim(stacked, f * width, width, 1)
+    stacked = jnp.concatenate(gains, axis=0)
+    pad = 2 * LANES - stacked.shape[0]
+    first = jnp.concatenate([mats[0], jnp.pad(stacked.T, ((0, 0), (0, pad)))], axis=1)
+    shard = _reduce_matrix(first)
+    width = mats[0].shape[1]
+    out = [shard[:, :width]] + [_reduce_matrix(m) for m in mats[1:]]
+    mine = shard[:, width : width + stacked.shape[0]].T
     rows = 0
     for g in gains:
         out.append(mine[rows : rows + g.shape[0]])

time: 536 us -> 547 us (1.021)
  waiting for transfers between devices: 119 us -> 177 us
  blocking collectives: 52.6 us -> 10.9 us
  starting transfers between devices: 52.8 us -> 42.2 us
    all_gather x4, waiting for transfers between devices: 21.6 us -> 64.3 us  [_gather_full(): x = lax.all_gather(z, 'dp', axis=1, tiled=False)]
    psum x1 -> x0, blocking collectives: 41.5 us -> none  [fast_reduce(): stacked = lax.psum(jnp.concatenate(gains, axis=0), ('dp', 'fsdp'))]
    ppermute x15 -> x3, starting transfers between devices: 22.5 us -> 5.56 us  [_z_gather(): lax.ppermute(piece, 'fsdp', [(i, (i + k) % NF_FAST) for i in range(NF_FAS...]
    ppermute x15 -> x3, waiting for transfers between devices: 20.9 us -> 36.2 us  [_z_gather(): lax.ppermute(piece, 'fsdp', [(i, (i + k) % NF_FAST) for i in range(NF_FAS...]
    transpose x0 -> x3, local copies, waits for them, and re-layouts: none -> 12.5 us  [the longest x1 9.42 us: _gather_full(): x.reshape(NF_FAST, NDP_FAST // 2, 2, rows, cols).transpose(0, 1, 3, 2, 4)]
    reshape x4 -> x6, local copies, waits for them, and re-layouts: 26 us -> 16.8 us  [the longest x3 16.6 us: _gather_full(): x.reshape(NF_FAST, NDP_FAST // 2, 2, rows, cols).transpose(0, 1, 3, 2, 4)]
    ppermute x4, waiting for transfers between devices: 21 us -> 28.2 us  [_reduce_matrix(): lax.ppermute(to_x.astype(jnp.bfloat16), 'dp', [(i, i ^ 2) for i in range(...]
    unnamed x128 -> x129, local copies, waits for them, and re-layouts: 33.6 us -> 38.8 us
  transfers between devices with their start and end apart: 50 -> 38, of which waited for: 32 -> 26; matrix products, arithmetic and copies ran while one was open for 30% -> 26% of each run, Pallas kernels for 0% -> 0%
where the time goes in v5:
time: 547 us; the launch traced here: 538 us
  waiting for transfers between devices  177 us (32%)
  matrix products  117 us (21%)
  local copies, waits for them, and re-layouts  112 us (20%)
  other arithmetic  63.1 us (12%)
  starting transfers between devices  42.2 us (8%)
  between operations  15.5 us (3%)
  blocking collectives  10.9 us (2%)
    all_gather x4, waiting for transfers between devices, _gather_full(): x = lax.all_gather(z, 'dp', axis=1, tiled=False)  64.3 us
    unnamed x129, local copies, waits for them, and re-layouts  38.8 us
    ppermute x3, waiting for transfers between devices, _z_gather(): lax.ppermute(piece, 'fsdp', [(i, (i + k) % NF_FAST) for i in range(NF_FAS...  36.2 us
    ppermute x4, waiting for transfers between devices, _reduce_matrix(): lax.ppermute(to_x.astype(jnp.bfloat16), 'dp', [(i, i ^ 2) for i in range(...  28.2 us
    ppermute x12, waiting for transfers between devices, _reduce_matrix(): lax.ppermute(part.astype(jnp.bfloat16), 'fsdp', [(i, (i + k) % NF_FAST) f...  23.6 us
    ppermute x12, starting transfers between devices, _reduce_matrix(): lax.ppermute(part.astype(jnp.bfloat16), 'fsdp', [(i, (i + k) % NF_FAST) f...  21.9 us
    ppermute x4, waiting for transfers between devices, _reduce_matrix(): lax.ppermute(of_chip(j ^ 3).astype(jnp.bfloat16), 'dp', [(i, i ^ 2) if i...  21.5 us
    dot_general x1, matrix products, on_device(): up_pre = jnp.dot(second_low, full_up, preferred_element_type=jnp.float32)  21.1 us
  transfers between devices with their start and end apart: 38, of which 26 were waited for; matrix products, arithmetic and copies ran while one was open for 26% of the time, Pallas kernels for 0%

profile of v5, /device:TPU:8, one launch (start us, length us, event | category | flops | bytes accessed | tf_op | source)
XLA Modules:
  0.0 538.1 jit_solution(5992144889891665223)
XLA Ops:
  11.9 3.0 collective-permute-start.1
  17.4 27.2 %collective-permute-done.2 = bf16[48,4736]{1,0:T(8,128)(2,1)S(1)} collective-permute-done((bf16[48,4736]{1,0:T(8,128)(2,1)S(1)}, bf16[48,4736]{1,0:T(8,128)(2,1)S(1)}, u32[]{:S(2)}, u32[]{:S(2)}) %collective-permute-start.2) | collective-permute-done | bytes 454688 | tf_op jit(solution)/shard_map/ppermute | solution.py:70
  44.6 8.9 %collective-permute-done = bf16[48,4736]{1,0:T(8,128)(2,1)S(1)} collective-permute-done((bf16[48,4736]{1,0:T(8,128)(2,1)S(1)}, bf16[48,4736]{1,0:T(8,128)(2,1)S(1)}, u32[]{:S(2)}, u32[]{:S(2)}) %collective-permute-start) | collective-permute-done | bytes 454688 | tf_op jit(solution)/shard_map/ppermute | solution.py:70
  66.7 16.4 %all-gather.19.cloned.1.call-done = bf16[4,384,384]{2,1,0:T(8,128)(2,1)} async-done(((bf16[4,48,384]{2,1,0:T(8,128)(2,1)}), bf16[4,384,384]{2,1,0:T(8,128)(2,1)}) %all-gather.19.cloned.1.call-update) | async-done | bytes 1179664 | tf_op jit(solution)/shard_map/all_gather | solution.py:77
  86.7 32.8 %all-gather.17.cloned.1.call-done = bf16[4,384,1152]{2,1,0:T(8,128)(2,1)} async-done(((bf16[4,48,1152]{2,1,0:T(8,128)(2,1)}), bf16[4,384,1152]{2,1,0:T(8,128)(2,1)}) %all-gather.17.cloned.1.call-update) | async-done | bytes 3538960 | tf_op jit(solution)/shard_map/all_gather | solution.py:77
  119.5 5.0 copy.134
  131.3 3.4 fusion.111
  142.6 8.3 %fusion.114 = (f32[12,576]{1,0:T(8,128)S(1)}, f32[12,576,576]{1,2,0:T(8,128)}) fusion(f32[576,12,64]{0,2,1:T(8,128)S(1)} %bitcast.234, f32[12,64]{1,0:T(8,128)S(1)} %mul.363, f32[576,12]{0,1:T(8,128)S(1)} %fusion.93, f32[576,12]{0,1:T(8,128)S(1)} %broadcast_multiply_fusion, f32[576,12,64]{0,2,1:T(8,128)S(1)} %bitcast.226, f32[12,64]{1,0:T(8,128)S(1)} %mul.357, ...), kind=kOutput, calls=%fused_computation.248 | convolution fusion | flops 525083904 | bytes 19940352 | tf_op jit(solution)/shard_map/while/body/eval_jaxpr/qhd,khd->hqk/dot_general | solution.py:210
  150.9 8.6 %fusion.3 = f32[12,576]{1,0:T(8,128)S(1)} fusion(f32[12,576,576]{1,2,0:T(8,128)} %get-tuple-element.166, f32[12,576]{1,0:T(8,128)S(1)} %get-tuple-element.165), kind=kLoop, calls=%fused_computation.10 | loop fusion | flops 7955712 | bytes 15980544 | tf_op jit(solution)/shard_map/while/body/eval_jaxpr/reduce_sum | solution.py:220
  159.5 9.7 %fusion.31 = bf16[12,64,576]{2,1,0:T(8,128)(2,1)S(1)} fusion(bf16[576,12,64]{0,2,1:T(8,128)(2,1)} %bitcast.261, f32[12,576,576]{1,2,0:T(8,128)} %get-tuple-element.166, f32[12,576]{1,0:T(8,128)S(1)} %fusion.3, f32[12,576]{1,0:T(8,128)S(1)} %get-tuple-element.165), kind=kOutput, calls=%fused_computation.91 | convolution fusion | flops 521994240 | bytes 17750016 | tf_op jit(solution)/shard_map/while/body/eval_jaxpr/hqk,khd->qhd/dot_general | solution.py:222
  171.9 9.4 %copy.141 = bf16[4,4,192,2,384]{4,3,2,1,0:T(2,128)(2,1)} copy(bf16[4,4,192,2,384]{4,2,3,1,0:T(8,128)(2,1)} %bitcast.255) | data formatting | bytes 9437184 | tf_op jit(solution)/shard_map/transpose | solution.py:78
  181.3 5.7 %copy.164 = bf16[384,8,2,384]{3,1,2,0:T(8,128)(2,1)} copy(bf16[384,8,2,384]{3,2,1,0:T(2,128)(2,1)} %bitcast.238) | data formatting | bytes 9437184
  187.0 15.0 %all-gather.21.cloned.1.call-done = bf16[4,384,1536]{2,1,0:T(8,128)(2,1)} async-done(((bf16[4,48,1536]{2,1,0:T(8,128)(2,1)}), bf16[4,384,1536]{2,1,0:T(8,128)(2,1)}) %all-gather.21.cloned.1.call-update) | async-done | bytes 4718608 | tf_op jit(solution)/shard_map/all_gather | solution.py:77
  202.0 9.4 %copy.140 = bf16[4,4,2,48,1536]{4,2,3,1,0:T(2,128)(2,1)} copy(bf16[4,4,2,48,1536]{4,3,2,1,0:T(8,128)(2,1)} %bitcast.256) | data formatting | bytes 9437184 | tf_op jit(solution)/shard_map/reshape | solution.py:78
  211.3 3.7 copy.163
  215.0 21.1 %multiply_convert_fusion = (bf16[576,3072]{1,0:T(8,128)(2,1)}, f32[576,3072]{1,0:T(8,128)}, f32[576,3072]{1,0:T(8,128)}) fusion(bf16[768,3072]{1,0:T(8,128)(2,1)S(1)} %bitcast.257, f32[576,768]{1,0:T(8,128)S(1)} %copy-done.9, f32[768]{0:T(1024)S(1)} %add.364, f32[768]{0:T(1024)S(1)} %mul.370, f32[576]{0:T(1024)S(1)} %fusion.96, ...), kind=kOutput, calls=%fused_computation.20 | convolution fusion | flops 2835136512 | bytes 24193536 | tf_op jit(solution)/shard_map/dot_general | solution.py:232
  236.1 9.4 %add_convert_fusion = bf16[576,3072]{1,0:T(8,128)(2,1)} fusion(f32[576,3072]{1,0:T(8,128)} %get-tuple-element.134, f32[576,3072]{1,0:T(8,128)} %get-tuple-element.169, bf16[3072,768]{1,0:T(8,128)(2,1)S(1)} %bitcast.254, bf16[576,768]{1,0:T(8,128)(2,1)S(1)} %copy-done.23, f32[576]{0:T(1024)S(1)} %fusion.94), kind=kOutput, calls=%fused_computation.19 | convolution fusion | flops 2744008704 | bytes 23300352 | tf_op jit(solution)/shard_map/dot_general | solution.py:241
  245.6 5.4 %multiply_reduce_fusion.2 = (f32[768]{0:T(1024)S(1)}, f32[576]{0:T(1024)S(1)}, f32[768]{0:T(1024)S(1)}, f32[576,768]{1,0:T(8,128)S(1)}) fusion(f32[576,768]{1,0:T(8,128)S(1)} %copy-done.9, f32[576]{0:T(1024)S(1)} %fusion.96, f32[576]{0:T(1024)S(1)} %broadcast_multiply_fusion.4, f32[768]{0:T(1024)S(1)} %mul.370, bf16[576,3072]{1,0:T(8,128)(2,1)} %add_convert_fusion, ...), kind=kOutput, calls=%fused_computation.78 | convolution fusion | flops 2721445888 | bytes 11812608 | tf_op jit(solution)/shard_map/dot_general | solution.py:247
  258.2 7.6 %convolution_convert_fusion = bf16[12,576,576]{1,2,0:T(8,128)(2,1)} fusion(bf16[576,12,64]{0,2,1:T(8,128)(2,1)} %bitcast.246, bf16[576,12,64]{0,2,1:T(8,128)(2,1)} %bitcast.262), kind=kOutput, calls=%fused_computation.34 | convolution fusion | flops 513589248 | bytes 9732096 | tf_op jit(solution)/shard_map/while/body/eval_jaxpr/qhd,khd->hqk/dot_general | solution.py:261
  265.8 9.9 %fusion.32 = bf16[12,64,576]{2,1,0:T(8,128)(2,1)} fusion(bf16[576,12,64]{0,2,1:T(8,128)(2,1)S(1)} %bitcast.247, f32[12,576,576]{1,2,0:T(8,128)} %get-tuple-element.166, f32[12,576]{1,0:T(8,128)S(1)} %log_add_fusion), kind=kOutput, calls=%fused_computation.92 | convolution fusion | flops 518012928 | bytes 17722368 | tf_op jit(solution)/shard_map/while/body/eval_jaxpr/hqk,qhd->khd/dot_general | solution.py:260
  275.7 12.0 %fusion = f32[12,576]{1,0:T(8,128)S(1)} fusion(bf16[12,576,576]{1,2,0:T(8,128)(2,1)} %convolution_convert_fusion, f32[12,576,576]{1,2,0:T(8,128)} %get-tuple-element.166, f32[12,576]{1,0:T(8,128)S(1)} %log_add_fusion), kind=kLoop, calls=%fused_computation.3 | loop fusion | flops 15918336 | bytes 23943168 | tf_op jit(solution)/shard_map/while/body/eval_jaxpr/reduce_sum | solution.py:263
  289.3 6.0 %fusion.2 = bf16[12,576,576]{1,2,0:T(8,128)(2,1)} fusion(bf16[12,576,576]{1,2,0:T(8,128)(2,1)S(1)} %copy-done.3, f32[12,576,576]{1,2,0:T(8,128)S(1)} %bitcast.223, f32[12,576]{1,0:T(8,128)S(1)} %fusion, f32[12,576]{1,0:T(8,128)S(1)} %log_add_fusion), kind=kLoop, calls=%fused_computation.5 | loop fusion | flops 19906560 | bytes 31905792 | tf_op jit(solution)/shard_map/while/body/eval_jaxpr/convert_element_type | solution.py:264
  295.4 8.2 %fusion.23 = (f32[576,12]{0,1:T(8,128)S(1)}, f32[12,64,576]{2,1,0:T(8,128)}) fusion(f32[576,12,64]{0,2,1:T(8,128)} %bitcast.233, f32[12,64]{1,0:T(8,128)S(1)} %copy-done.35, f32[576,12]{0,1:T(8,128)S(1)} %broadcast_multiply_fusion, bf16[12,576,576]{1,2,0:T(8,128)(2,1)} %fusion.2, f32[576,12,64]{0,2,1:T(8,128)S(1)} %bitcast.227, f32[12,64]{1,0:T(8,128)S(1)} %mul.357, ...), kind=kOutput, calls=%fused_computation.61 | convolution fusion | flops 513139968 | bytes 13387776 | tf_op jit(solution)/shard_map/while/body/eval_jaxpr/hqk,qhd->khd/dot_general | solution.py:269
  311.4 2.8 fusion.108
  314.2 6.5 %fusion.35 = f32[768,2304]{1,0:T(8,128)} fusion(bf16[576,768]{0,1:T(8,128)(2,1)S(1)} %bitcast.282, bf16[576,768]{0,1:T(8,128)(2,1)S(1)} %bitcast.278, bf16[576,768]{0,1:T(8,128)(2,1)S(1)} %bitcast.280, bf16[576,768]{1,0:T(8,128)(2,1)S(1)} %copy-done.13, f32[768]{0:T(1024)S(1)} %copy-done.45, f32[768]{0:T(1024)S(1)} %copy-done.43, f32[576]{0:T(1024)S(1)} %copy-done.41, ...), kind=kOutput, calls=%fused_computation.96 | convolution fusion | flops 2049048576 | bytes 10627584 | tf_op jit(solution)/shard_map/dot_general | solution.py:287
  321.9 4.2 select_maximum_fusion
  326.1 3.1 copy-done.5
  331.4 6.1 %fusion.106 = f32[768,3072]{1,0:T(8,128)S(1)} fusion(bf16[576,3072]{1,0:T(8,128)(2,1)} %add_convert_fusion, f32[576,768]{1,0:T(8,128)S(1)} %copy-done.10, f32[768]{0:T(1024)S(1)} %add.364, f32[768]{0:T(1024)S(1)} %mul.370, f32[576]{0:T(1024)S(1)} %fusion.96, f32[576]{0:T(1024)S(1)} %broadcast_multiply_fusion.4), kind=kOutput, calls=%fused_computation.241 | convolution fusion | flops 2720120832 | bytes 14756352 | tf_op jit(solution)/shard_map/dot_general | solution.py:244
  339.7 4.1 constant_dynamic-slice_fusion.3
  349.4 2.8 constant_dynamic-slice_fusion.1
  352.3 4.6 collective-permute-done.4
  362.7 8.0 %collective-permute-done.5 = bf16[4,48,1280]{2,1,0:T(8,128)(2,1)S(1)} collective-permute-done((bf16[4,48,1280]{2,1,0:T(8,128)(2,1)S(1)}, bf16[4,48,1280]{2,1,0:T(8,128)(2,1)S(1)}, u32[]{:S(2)}, u32[]{:S(2)}) %collective-permute-start.5) | collective-permute-done | bytes 491552 | tf_op jit(solution)/shard_map/ppermute | solution.py:138
  378.1 3.9 collective-permute-done.7
  384.5 3.1 collective-permute-done.18
  391.4 6.1 %fusion.56 = f32[3072,768]{1,0:T(8,128)S(1)} fusion(bf16[576,3072]{1,0:T(8,128)(2,1)} %get-tuple-element.133, bf16[576,768]{1,0:T(8,128)(2,1)S(1)} %copy-done.24, f32[576]{0:T(1024)S(1)} %fusion.94), kind=kOutput, calls=%fused_computation.128 | convolution fusion | flops 2719236096 | bytes 13863168 | tf_op jit(solution)/shard_map/dot_general | solution.py:240
  397.5 3.6 copy-done.19
  410.3 7.2 %collective-permute-done.21 = bf16[48,1536]{1,0:T(8,128)(2,1)S(1)} collective-permute-done((bf16[48,1536]{1,0:T(8,128)(2,1)S(1)}, bf16[48,1536]{1,0:T(8,128)(2,1)S(1)}, u32[]{:S(2)}, u32[]{:S(2)}) %collective-permute-start.21) | collective-permute-done | bytes 147488 | tf_op jit(solution)/shard_map/ppermute | solution.py:144
  419.9 2.6 constant_dynamic-slice_fusion
  426.1 13.8 %collective-permute-done.25 = bf16[4,192,384]{2,1,0:T(8,128)(2,1)S(1)} collective-permute-done((bf16[4,192,384]{2,1,0:T(8,128)(2,1)S(1)}, bf16[4,192,384]{2,1,0:T(8,128)(2,1)S(1)}, u32[]{:S(2)}, u32[]{:S(2)}) %collective-permute-start.25) | collective-permute-done | bytes 589856 | tf_op jit(solution)/shard_map/ppermute | solution.py:131
  441.6 15.4 %collective-permute-done.26 = bf16[4,192,384]{2,1,0:T(8,128)(2,1)S(1)} collective-permute-done((bf16[4,192,384]{2,1,0:T(8,128)(2,1)S(1)}, bf16[4,192,384]{2,1,0:T(8,128)(2,1)S(1)}, u32[]{:S(2)}, u32[]{:S(2)}) %collective-permute-start.26) | collective-permute-done | bytes 589856 | tf_op jit(solution)/shard_map/ppermute | solution.py:138
  457.3 3.3 collective-permute-start.28
  466.1 5.0 collective-permute-done.30
  480.7 6.5 %multiply_convert_fusion.3 = bf16[576,768]{1,0:T(8,128)(2,1)} fusion(f32[576,768]{1,0:T(8,128)S(1)} %copy-done.10, bf16[576,3072]{1,0:T(8,128)(2,1)S(1)} %copy-done.48, bf16[3072,768]{1,0:T(8,128)(2,1)} %bitcast.251, f32[576]{0:T(1024)S(1)} %fusion.94), kind=kOutput, calls=%fused_computation.84 | convolution fusion | flops 2719236096 | bytes 10914048 | tf_op jit(solution)/shard_map/dot_general | solution.py:235
  490.2 3.7 collective-permute-done.12
  502.0 10.9 %all-gather.4 = f32[384,384]{1,0:T(8,128)S(1)} all-gather(f32[48,384]{1,0:T(8,128)S(1)} %fusion.88), channel_id=6, replica_groups=mesh['dp'=8,'fsdp'=4] {'dp'}, dimensions={0}, use_global_device_ids=true | all-gather | bytes 663552 | tf_op jit(solution)/shard_map/all_gather | solution.py:147
  514.1 3.1 copy.148
  520.7 3.5 copy.150
  526.0 3.5 copy.151
  (309 shorter events, 139.0 us)
Async XLA Ops:
  7.2 76.0 %all-gather.19.cloned.1.call-start = ((), (), s32[]{:S(2)}) async-start(), calls=%async_computation.2 | async-start | bytes 1327104 | tf_op jit(solution)/shard_map/all_gather | solution.py:77
  11.8 32.8 %collective-permute-start.2 = (bf16[48,4736]{1,0:T(8,128)(2,1)S(1)}, bf16[48,4736]{1,0:T(8,128)(2,1)S(1)}, u32[]{:S(2)}, u32[]{:S(2)}) collective-permute-start(bf16[48,4736]{1,0:T(8,128)(2,1)S(1)} %bitcast_dynamic-update-slice_fusion), channel_id=1, source_target_pairs={{0,3},{1,0},{2,1},{3,2},{4,7},{5,4},{6,5},{7,6},{8,11},{9,8},{10,9... | collective-permute-start | bytes 1363976 | tf_op jit(solution)/shard_map/ppermute | solution.py:70
  11.9 32.8 %collective-permute-start.1 = (bf16[48,4736]{1,0:T(8,128)(2,1)S(1)}, bf16[48,4736]{1,0:T(8,128)(2,1)S(1)}, u32[]{:S(2)}, u32[]{:S(2)}) collective-permute-start(bf16[48,4736]{1,0:T(8,128)(2,1)S(1)} %bitcast_dynamic-update-slice_fusion), channel_id=1, source_target_pairs={{0,2},{1,3},{2,0},{3,1},{4,6},{5,7},{6,4},{7,5},{8,10},{9,11},{10,... | collective-permute-start | bytes 1363976 | tf_op jit(solution)/shard_map/ppermute | solution.py:70
  14.9 38.7 %collective-permute-start = (bf16[48,4736]{1,0:T(8,128)(2,1)S(1)}, bf16[48,4736]{1,0:T(8,128)(2,1)S(1)}, u32[]{:S(2)}, u32[]{:S(2)}) collective-permute-start(bf16[48,4736]{1,0:T(8,128)(2,1)S(1)} %bitcast_dynamic-update-slice_fusion), channel_id=1, source_target_pairs={{0,1},{1,2},{2,3},{3,0},{4,5},{5,6},{6,7},{7,4},{8,9},{9,10},{10,1... | collective-permute-start | bytes 1363976 | tf_op jit(solution)/shard_map/ppermute | solution.py:70
  58.1 61.5 %all-gather.17.cloned.1.call-start = ((), (), s32[]{:S(2)}) async-start(), calls=%async_computation.1 | async-start | bytes 3981312 | tf_op jit(solution)/shard_map/all_gather | solution.py:77
  58.9 112.9 %all-gather.15.cloned.1.call-start = ((), (), s32[]{:S(2)}) async-start(), calls=%async_computation | async-start | bytes 5308416 | tf_op jit(solution)/shard_map/all_gather | solution.py:77
  61.1 140.9 %all-gather.21.cloned.1.call-start = ((), (), s32[]{:S(2)}) async-start(), calls=%async_computation.3 | async-start | bytes 5308416 | tf_op jit(solution)/shard_map/all_gather | solution.py:77
  62.9 62.2 %copy-start.36 = (f32[576]{0:T(1024)}, f32[576]{0:T(1024)S(1)}, u32[]{:S(2)}) copy-start(f32[576]{0:T(1024)S(1)} %broadcast_multiply_fusion.5) | copy-start | bytes 6916
  63.9 61.2 %copy-start.40 = (f32[576]{0:T(1024)}, f32[576]{0:T(1024)S(1)}, u32[]{:S(2)}) copy-start(f32[576]{0:T(1024)S(1)} %fusion.95) | copy-start | bytes 6916
  64.4 449.7 %all-gather.23.cloned.1.call-start = ((), (), s32[]{:S(2)}) async-start(), calls=%async_computation.4 | async-start | bytes 2211840 | tf_op jit(solution)/shard_map/all_gather | solution.py:147
  65.4 59.7 %copy-start.42 = (f32[768]{0:T(1024)}, f32[768]{0:T(1024)S(1)}, u32[]{:S(2)}) copy-start(f32[768]{0:T(1024)S(1)} %mul.351) | copy-start | bytes 9220
  65.5 59.6 %copy-start.44 = (f32[768]{0:T(1024)}, f32[768]{0:T(1024)S(1)}, u32[]{:S(2)}) copy-start(f32[768]{0:T(1024)S(1)} %add.357) | copy-start | bytes 9220
  211.3 24.8 %slice-start.5 = ((s8[4718592]{0:T(1024)(128)(4,1)}), s8[4194304]{0:T(1024)(128)(4,1)S(1)}, s32[]{:S(2)}) async-start(s8[4718592]{0:T(1024)(128)(4,1)} %bitcast.252), calls=%async_computation.12 | async-start | bytes 8388608
  215.0 21.1 %slice-start.6 = ((s8[4718592]{0:T(1024)(128)(4,1)}), s8[524288]{0:T(1024)(128)(4,1)S(1)}, s32[]{:S(2)}) async-start(s8[4718592]{0:T(1024)(128)(4,1)} %bitcast.252), calls=%async_computation.13 | async-start | bytes 1048576
  215.0 21.1 %copy-start.23 = (bf16[576,768]{1,0:T(8,128)(2,1)S(1)}, bf16[576,768]{1,0:T(8,128)(2,1)}, u32[]{:S(2)}) copy-start(bf16[576,768]{1,0:T(8,128)(2,1)} %param.19) | copy-start | bytes 2654212
  265.8 22.0 %slice-start = ((s8[17694720]{0:T(1024)(128)(4,1)}), s8[4194304]{0:T(1024)(128)(4,1)S(1)}, s32[]{:S(2)}) async-start(s8[17694720]{0:T(1024)(128)(4,1)} %bitcast.222), calls=%async_computation.7 | async-start | bytes 8388608
  265.8 22.0 %slice-start.1 = ((s8[17694720]{0:T(1024)(128)(4,1)}), s8[4194304]{0:T(1024)(128)(4,1)S(1)}, s32[]{:S(2)}) async-start(s8[17694720]{0:T(1024)(128)(4,1)} %bitcast.222), calls=%async_computation.8 | async-start | bytes 8388608
  265.8 22.0 %slice-start.2 = ((s8[17694720]{0:T(1024)(128)(4,1)}), s8[917504]{0:T(1024)(128)(4,1)S(1)}, s32[]{:S(2)}) async-start(s8[17694720]{0:T(1024)(128)(4,1)} %bitcast.222), calls=%async_computation.9 | async-start | bytes 1835008
  330.7 13.1 %collective-permute-start.3 = (bf16[4,4,48,1280]{3,2,1,0:T(8,128)(2,1)}, bf16[4,4,48,1280]{3,2,1,0:T(8,128)(2,1)}, u32[]{:S(2)}, u32[]{:S(2)}) collective-permute-start(bf16[4,4,48,1280]{3,2,1,0:T(8,128)(2,1)} %bitcast.34), channel_id=1, source_target_pairs={{0,4},{4,0},{8,12},{12,8},{16,20},{20,16},{24,28},{28,24},{1,5},{5... | collective-permute-start | bytes 5898248 | tf_op jit(solution)/shard_map/ppermute | solution.py:125
  339.5 20.7 %collective-permute-start.17 = (bf16[4,4,48,1536]{3,2,1,0:T(8,128)(2,1)}, bf16[4,4,48,1536]{3,2,1,0:T(8,128)(2,1)}, u32[]{:S(2)}, u32[]{:S(2)}) collective-permute-start(bf16[4,4,48,1536]{3,2,1,0:T(8,128)(2,1)} %bitcast.59), channel_id=1, source_target_pairs={{0,4},{4,0},{8,12},{12,8},{16,20},{20,16},{24,28},{28,24},{1,5},{5... | collective-permute-start | bytes 7077896 | tf_op jit(solution)/shard_map/ppermute | solution.py:125
  347.9 9.0 %collective-permute-start.4 = (bf16[4,48,1280]{2,1,0:T(8,128)(2,1)S(1)}, bf16[4,48,1280]{2,1,0:T(8,128)(2,1)}, u32[]{:S(2)}, u32[]{:S(2)}) collective-permute-start(bf16[4,48,1280]{2,1,0:T(8,128)(2,1)S(1)} %fusion.55), channel_id=1, source_target_pairs={{0,8},{4,20},{8,0},{12,28},{16,24},{20,4},{24,16},{28,12},{1,9},{5... | collective-permute-start | bytes 1474568 | tf_op jit(solution)/shard_map/ppermute | solution.py:131
  358.2 12.6 %collective-permute-start.5 = (bf16[4,48,1280]{2,1,0:T(8,128)(2,1)S(1)}, bf16[4,48,1280]{2,1,0:T(8,128)(2,1)S(1)}, u32[]{:S(2)}, u32[]{:S(2)}) collective-permute-start(bf16[4,48,1280]{2,1,0:T(8,128)(2,1)S(1)} %get-tuple-element.141), channel_id=1, source_target_pairs={{0,8},{4,12},{8,0},{12,4},{16,24},{20,28},{24,16},{28,20},{1,9},{5... | collective-permute-start | bytes 1474568 | tf_op jit(solution)/shard_map/ppermute | solution.py:138
  359.7 12.2 %collective-permute-start.6 = (bf16[4,48,1280]{2,1,0:T(8,128)(2,1)S(1)}, bf16[4,48,1280]{2,1,0:T(8,128)(2,1)S(1)}, u32[]{:S(2)}, u32[]{:S(2)}) collective-permute-start(bf16[4,48,1280]{2,1,0:T(8,128)(2,1)S(1)} %get-tuple-element.142), channel_id=1, source_target_pairs={{0,16},{4,20},{8,24},{12,28},{16,0},{20,4},{24,8},{28,12},{1,17},{... | collective-permute-start | bytes 1474568 | tf_op jit(solution)/shard_map/ppermute | solution.py:139
  372.1 9.9 %collective-permute-start.7 = (bf16[48,1280]{1,0:T(8,128)(2,1)S(1)}, bf16[48,1280]{1,0:T(8,128)(2,1)S(1)}, u32[]{:S(2)}, u32[]{:S(2)}) collective-permute-start(bf16[48,1280]{1,0:T(8,128)(2,1)S(1)} %get-tuple-element.153), channel_id=1, source_target_pairs={{0,1},{1,2},{2,3},{3,0},{4,5},{5,6},{6,7},{7,4},{8,9},{9,10},{10,1... | collective-permute-start | bytes 368648 | tf_op jit(solution)/shard_map/ppermute | solution.py:144
  373.7 9.5 %collective-permute-start.9 = (bf16[48,1280]{1,0:T(8,128)(2,1)S(1)}, bf16[48,1280]{1,0:T(8,128)(2,1)S(1)}, u32[]{:S(2)}, u32[]{:S(2)}) collective-permute-start(bf16[48,1280]{1,0:T(8,128)(2,1)S(1)} %get-tuple-element.154), channel_id=1, source_target_pairs={{0,3},{1,0},{2,1},{3,2},{4,7},{5,4},{6,5},{7,6},{8,11},{9,8},{10,9... | collective-permute-start | bytes 368648 | tf_op jit(solution)/shard_map/ppermute | solution.py:144
  374.2 9.1 %collective-permute-start.8 = (bf16[48,1280]{1,0:T(8,128)(2,1)S(1)}, bf16[48,1280]{1,0:T(8,128)(2,1)S(1)}, u32[]{:S(2)}, u32[]{:S(2)}) collective-permute-start(bf16[48,1280]{1,0:T(8,128)(2,1)S(1)} %get-tuple-element.155), channel_id=1, source_target_pairs={{0,2},{1,3},{2,0},{3,1},{4,6},{5,7},{6,4},{7,5},{8,10},{9,11},{10,... | collective-permute-start | bytes 368648 | tf_op jit(solution)/shard_map/ppermute | solution.py:144
  377.5 10.1 %collective-permute-start.18 = (bf16[4,48,1536]{2,1,0:T(8,128)(2,1)}, bf16[4,48,1536]{2,1,0:T(8,128)(2,1)S(1)}, u32[]{:S(2)}, u32[]{:S(2)}) collective-permute-start(bf16[4,48,1536]{2,1,0:T(8,128)(2,1)} %fusion.53), channel_id=1, source_target_pairs={{0,8},{4,20},{8,0},{12,28},{16,24},{20,4},{24,16},{28,12},{1,9},{5... | collective-permute-start | bytes 1769480 | tf_op jit(solution)/shard_map/ppermute | solution.py:131
  384.1 136.6 %all-gather.25.cloned.1.call-start = ((), (), s32[]{:S(2)}) async-start(), calls=%async_computation.5 | async-start | bytes 2654208 | tf_op jit(solution)/shard_map/all_gather | solution.py:147
  389.5 14.5 %collective-permute-start.19 = (bf16[4,48,1536]{2,1,0:T(8,128)(2,1)S(1)}, bf16[4,48,1536]{2,1,0:T(8,128)(2,1)S(1)}, u32[]{:S(2)}, u32[]{:S(2)}) collective-permute-start(bf16[4,48,1536]{2,1,0:T(8,128)(2,1)S(1)} %get-tuple-element.137), channel_id=1, source_target_pairs={{0,8},{4,12},{8,0},{12,4},{16,24},{20,28},{24,16},{28,20},{1,9},{5... | collective-permute-start | bytes 1769480 | tf_op jit(solution)/shard_map/ppermute | solution.py:138
  390.2 14.1 %collective-permute-start.20 = (bf16[4,48,1536]{2,1,0:T(8,128)(2,1)S(1)}, bf16[4,48,1536]{2,1,0:T(8,128)(2,1)S(1)}, u32[]{:S(2)}, u32[]{:S(2)}) collective-permute-start(bf16[4,48,1536]{2,1,0:T(8,128)(2,1)S(1)} %get-tuple-element.138), channel_id=1, source_target_pairs={{0,16},{4,20},{8,24},{12,28},{16,0},{20,4},{24,8},{28,12},{1,17},{... | collective-permute-start | bytes 1769480 | tf_op jit(solution)/shard_map/ppermute | solution.py:139
  402.8 19.8 %collective-permute-start.24 = (bf16[4,4,192,384]{3,2,1,0:T(8,128)(2,1)}, bf16[4,4,192,384]{3,2,1,0:T(8,128)(2,1)}, u32[]{:S(2)}, u32[]{:S(2)}) collective-permute-start(bf16[4,4,192,384]{3,2,1,0:T(8,128)(2,1)} %bitcast.71), channel_id=1, source_target_pairs={{0,4},{4,0},{8,12},{12,8},{16,20},{20,16},{24,28},{28,24},{1,5},{5... | collective-permute-start | bytes 7077896 | tf_op jit(solution)/shard_map/ppermute | solution.py:125
  405.8 11.7 %collective-permute-start.21 = (bf16[48,1536]{1,0:T(8,128)(2,1)S(1)}, bf16[48,1536]{1,0:T(8,128)(2,1)S(1)}, u32[]{:S(2)}, u32[]{:S(2)}) collective-permute-start(bf16[48,1536]{1,0:T(8,128)(2,1)S(1)} %get-tuple-element.150), channel_id=1, source_target_pairs={{0,1},{1,2},{2,3},{3,0},{4,5},{5,6},{6,7},{7,4},{8,9},{9,10},{10,1... | collective-permute-start | bytes 442376 | tf_op jit(solution)/shard_map/ppermute | solution.py:144
  407.3 11.5 %collective-permute-start.23 = (bf16[48,1536]{1,0:T(8,128)(2,1)S(1)}, bf16[48,1536]{1,0:T(8,128)(2,1)S(1)}, u32[]{:S(2)}, u32[]{:S(2)}) collective-permute-start(bf16[48,1536]{1,0:T(8,128)(2,1)S(1)} %get-tuple-element.151), channel_id=1, source_target_pairs={{0,3},{1,0},{2,1},{3,2},{4,7},{5,4},{6,5},{7,6},{8,11},{9,8},{10,9... | collective-permute-start | bytes 442376 | tf_op jit(solution)/shard_map/ppermute | solution.py:144
  407.9 11.2 %collective-permute-start.22 = (bf16[48,1536]{1,0:T(8,128)(2,1)S(1)}, bf16[48,1536]{1,0:T(8,128)(2,1)S(1)}, u32[]{:S(2)}, u32[]{:S(2)}) collective-permute-start(bf16[48,1536]{1,0:T(8,128)(2,1)S(1)} %get-tuple-element.152), channel_id=1, source_target_pairs={{0,2},{1,3},{2,0},{3,1},{4,6},{5,7},{6,4},{7,5},{8,10},{9,11},{10,... | collective-permute-start | bytes 442376 | tf_op jit(solution)/shard_map/ppermute | solution.py:144
  419.9 106.1 %all-gather.27.cloned.1.call-start = ((), (), s32[]{:S(2)}) async-start(), calls=%async_computation.6 | async-start | bytes 2654208 | tf_op jit(solution)/shard_map/all_gather | solution.py:147
  424.9 15.0 %collective-permute-start.25 = (bf16[4,192,384]{2,1,0:T(8,128)(2,1)S(1)}, bf16[4,192,384]{2,1,0:T(8,128)(2,1)S(1)}, u32[]{:S(2)}, u32[]{:S(2)}) collective-permute-start(bf16[4,192,384]{2,1,0:T(8,128)(2,1)S(1)} %fusion.54), channel_id=1, source_target_pairs={{0,8},{4,20},{8,0},{12,28},{16,24},{20,4},{24,16},{28,12},{1,9},{5... | collective-permute-start | bytes 1769480 | tf_op jit(solution)/shard_map/ppermute | solution.py:131
  440.3 16.7 %collective-permute-start.26 = (bf16[4,192,384]{2,1,0:T(8,128)(2,1)S(1)}, bf16[4,192,384]{2,1,0:T(8,128)(2,1)S(1)}, u32[]{:S(2)}, u32[]{:S(2)}) collective-permute-start(bf16[4,192,384]{2,1,0:T(8,128)(2,1)S(1)} %get-tuple-element.135), channel_id=1, source_target_pairs={{0,8},{4,12},{8,0},{12,4},{16,24},{20,28},{24,16},{28,20},{1,9},{5... | collective-permute-start | bytes 1769480 | tf_op jit(solution)/shard_map/ppermute | solution.py:138
  441.6 15.4 %collective-permute-start.27 = (bf16[4,192,384]{2,1,0:T(8,128)(2,1)S(1)}, bf16[4,192,384]{2,1,0:T(8,128)(2,1)S(1)}, u32[]{:S(2)}, u32[]{:S(2)}) collective-permute-start(bf16[4,192,384]{2,1,0:T(8,128)(2,1)S(1)} %get-tuple-element.136), channel_id=1, source_target_pairs={{0,16},{4,20},{8,24},{12,28},{16,0},{20,4},{24,8},{28,12},{1,17},{... | collective-permute-start | bytes 1769480 | tf_op jit(solution)/shard_map/ppermute | solution.py:139
  457.3 8.8 %collective-permute-start.28 = (bf16[192,384]{1,0:T(8,128)(2,1)S(1)}, bf16[192,384]{1,0:T(8,128)(2,1)S(1)}, u32[]{:S(2)}, u32[]{:S(2)}) collective-permute-start(bf16[192,384]{1,0:T(8,128)(2,1)S(1)} %get-tuple-element.147), channel_id=1, source_target_pairs={{0,1},{1,2},{2,3},{3,0},{4,5},{5,6},{6,7},{7,4},{8,9},{9,10},{10,1... | collective-permute-start | bytes 442376 | tf_op jit(solution)/shard_map/ppermute | solution.py:144
  460.6 10.5 %collective-permute-start.30 = (bf16[192,384]{1,0:T(8,128)(2,1)S(1)}, bf16[192,384]{1,0:T(8,128)(2,1)S(1)}, u32[]{:S(2)}, u32[]{:S(2)}) collective-permute-start(bf16[192,384]{1,0:T(8,128)(2,1)S(1)} %get-tuple-element.148), channel_id=1, source_target_pairs={{0,3},{1,0},{2,1},{3,2},{4,7},{5,4},{6,5},{7,6},{8,11},{9,8},{10,9... | collective-permute-start | bytes 442376 | tf_op jit(solution)/shard_map/ppermute | solution.py:144
  462.6 11.1 %collective-permute-start.29 = (bf16[192,384]{1,0:T(8,128)(2,1)S(1)}, bf16[192,384]{1,0:T(8,128)(2,1)S(1)}, u32[]{:S(2)}, u32[]{:S(2)}) collective-permute-start(bf16[192,384]{1,0:T(8,128)(2,1)S(1)} %get-tuple-element.149), channel_id=1, source_target_pairs={{0,2},{1,3},{2,0},{3,1},{4,6},{5,7},{6,4},{7,5},{8,10},{9,11},{10,... | collective-permute-start | bytes 442376 | tf_op jit(solution)/shard_map/ppermute | solution.py:144
  477.1 2.1 collective-permute-start.10
  479.3 7.8 %collective-permute-start.11 = (bf16[4,48,384]{2,1,0:T(8,128)(2,1)S(1)}, bf16[4,48,384]{2,1,0:T(8,128)(2,1)S(1)}, u32[]{:S(2)}, u32[]{:S(2)}) collective-permute-start(bf16[4,48,384]{2,1,0:T(8,128)(2,1)S(1)} %fusion.75), channel_id=1, source_target_pairs={{0,8},{4,20},{8,0},{12,28},{16,24},{20,4},{24,16},{28,12},{1,9},{5... | collective-permute-start | bytes 442376 | tf_op jit(solution)/shard_map/ppermute | solution.py:131
  487.2 6.6 %collective-permute-start.12 = (bf16[4,48,384]{2,1,0:T(8,128)(2,1)S(1)}, bf16[4,48,384]{2,1,0:T(8,128)(2,1)S(1)}, u32[]{:S(2)}, u32[]{:S(2)}) collective-permute-start(bf16[4,48,384]{2,1,0:T(8,128)(2,1)S(1)} %get-tuple-element.145), channel_id=1, source_target_pairs={{0,8},{4,12},{8,0},{12,4},{16,24},{20,28},{24,16},{28,20},{1,9},{5... | collective-permute-start | bytes 442376 | tf_op jit(solution)/shard_map/ppermute | solution.py:138
  488.0 5.9 %collective-permute-start.13 = (bf16[4,48,384]{2,1,0:T(8,128)(2,1)S(1)}, bf16[4,48,384]{2,1,0:T(8,128)(2,1)S(1)}, u32[]{:S(2)}, u32[]{:S(2)}) collective-permute-start(bf16[4,48,384]{2,1,0:T(8,128)(2,1)S(1)} %get-tuple-element.146), channel_id=1, source_target_pairs={{0,16},{4,20},{8,24},{12,28},{16,0},{20,4},{24,8},{28,12},{1,17},{... | collective-permute-start | bytes 442376 | tf_op jit(solution)/shard_map/ppermute | solution.py:139
  494.0 7.2 %collective-permute-start.14 = (bf16[48,384]{1,0:T(8,128)(2,1)S(1)}, bf16[48,384]{1,0:T(8,128)(2,1)S(1)}, u32[]{:S(2)}, u32[]{:S(2)}) collective-permute-start(bf16[48,384]{1,0:T(8,128)(2,1)S(1)} %get-tuple-element.156), channel_id=1, source_target_pairs={{0,1},{1,2},{2,3},{3,0},{4,5},{5,6},{6,7},{7,4},{8,9},{9,10},{10,1... | collective-permute-start | bytes 110600 | tf_op jit(solution)/shard_map/ppermute | solution.py:144
  494.7 6.5 %collective-permute-start.16 = (bf16[48,384]{1,0:T(8,128)(2,1)S(1)}, bf16[48,384]{1,0:T(8,128)(2,1)S(1)}, u32[]{:S(2)}, u32[]{:S(2)}) collective-permute-start(bf16[48,384]{1,0:T(8,128)(2,1)S(1)} %get-tuple-element.157), channel_id=1, source_target_pairs={{0,3},{1,0},{2,1},{3,2},{4,7},{5,4},{6,5},{7,6},{8,11},{9,8},{10,9... | collective-permute-start | bytes 110600 | tf_op jit(solution)/shard_map/ppermute | solution.py:144
  497.1 5.0 collective-permute-start.15
  (46 other events, 260.3 us)
Sparse Core Ops, SparseCore 0:
  58.2 24.9 all-gather.18
  85.6 33.8 all-gather.16
  122.0 38.7 all-gather.14
  163.1 38.7 all-gather.20
  384.2 30.6 all-gather.22
  420.0 35.3 all-gather.24
  474.6 29.7 all-gather.26

commit v6 on v5

--- a/solution.py
+++ b/solution.py
@@ -79,7 +79,7 @@
     return x.reshape(out_rows, 2 * cols)
 
 
-def fast_gather(mats, gains):
+def _gather_group(mats, gains):
     d = lax.axis_index("dp")
     j, c = d // 2, d % 2
     n_chips = NDP_FAST // 2
@@ -90,10 +90,11 @@
         piece = lax.dynamic_slice(m, (j * rows, c * cols), (rows, cols))
         shapes.append((rows, cols))
         blocks.append(piece.reshape(height, rows * cols // height))
-    stacked = jnp.concatenate(gains, axis=0)
-    flat = stacked.reshape(-1)
-    blocks.append(jnp.pad(flat, (0, height * LANES - flat.shape[0])).reshape(height, LANES))
-    z = _z_gather(jnp.concatenate(blocks, axis=1))
+    if gains:
+        stacked = jnp.concatenate(gains, axis=0)
+        flat = stacked.reshape(-1)
+        blocks.append(jnp.pad(flat, (0, height * LANES - flat.shape[0])).reshape(height, LANES))
+    z = _z_gather(jnp.concatenate(blocks, axis=1) if len(blocks) > 1 else blocks[0])
     out = []
     offset = 0
     for m, (rows, cols) in zip(mats, shapes):
@@ -101,14 +102,19 @@
         part = z[:, :, offset : offset + width].reshape(NF_FAST, rows, cols)
         out.append(_gather_full(part, rows, cols, NF_FAST * m.shape[0]))
         offset += width
-    g = z[:, :, offset:].reshape(NF_FAST, -1)[:, : flat.shape[0]]
-    g = g.reshape(NF_FAST, stacked.shape[0], stacked.shape[1]).transpose(1, 0, 2)
-    g = g.reshape(stacked.shape[0], NF_FAST * stacked.shape[1])
-    row = 0
-    for gain in gains:
-        out.append(g[row : row + gain.shape[0]])
-        row += gain.shape[0]
+    if gains:
+        g = z[:, :, offset:].reshape(NF_FAST, -1)[:, : flat.shape[0]]
+        g = g.reshape(NF_FAST, stacked.shape[0], stacked.shape[1]).transpose(1, 0, 2)
+        g = g.reshape(stacked.shape[0], NF_FAST * stacked.shape[1])
+        row = 0
+        for gain in gains:
+            out.append(g[row : row + gain.shape[0]])
+            row += gain.shape[0]
     return out
+
+
+def fast_gather(mats, gains):
+    return _gather_group(mats[:1], ()) + _gather_group(mats[1:], gains)
 
 
 def _reduce_matrix(g):
@@ -162,6 +168,12 @@
         out.append(mine[rows : rows + g.shape[0]])
         rows += g.shape[0]
     return out
+
+
+def map_blocks(fn, members):
+    if members[0].shape[0] == 1:
+        return jax.tree.map(lambda v: v[None], fn(tuple(m[0] for m in members)))
+    return lax.map(fn, members)
 
 
 def on_device(
@@ -224,7 +236,7 @@
         )
         return (mixed_block, row_top + jnp.log(row_total))
 
-    mixed_heads, log_total = lax.map(attend, (q_low, k_low, v_low, s_blocks))
+    mixed_heads, log_total = map_blocks(attend, (q_low, k_low, v_low, s_blocks))
     mixed_low = mixed_heads.reshape(length, model_width).astype(jnp.bfloat16)
     residual = inputs + jnp.dot(mixed_low, full_out, preferred_element_type=jnp.float32)
     second, second_back = jax.vjp(layer_norm, residual, norm_gains[1], biases[1])
@@ -249,6 +261,8 @@
     grad_resid = grad_resid + upstream
     resid_low = grad_resid.astype(jnp.bfloat16)
     grad_outw = jnp.dot(mixed_low.T, resid_low, preferred_element_type=jnp.float32)
+    if fast:
+        early = [_reduce_matrix(grad_outw)] + early
     grad_mixed = jnp.dot(resid_low, back_out.T, preferred_element_type=jnp.float32)
     grad_mixed = grad_mixed.astype(jnp.bfloat16).reshape(blocks, PATCH_BIG, HEADS, HEAD_DIM)
 
@@ -270,9 +284,13 @@
         )
         return (grad_q, grad_k, grad_v)
 
-    grad_qn, grad_kn, grad_vn = lax.map(
+    grad_qn, grad_kn, grad_vn = map_blocks(
         attend_back, (q_low, k_low, v_low, s_blocks, log_total, grad_mixed)
     )
+    if fast:
+        early, grad_qn, grad_kn, grad_vn = lax.optimization_barrier(
+            (early, grad_qn, grad_kn, grad_vn)
+        )
     grad_q, grad_k, gain_q, gain_k = norms_back(
         (grad_qn.reshape(length, HEADS, HEAD_DIM), grad_kn.reshape(length, HEADS, HEAD_DIM))
     )
@@ -293,8 +311,8 @@
     grad_qk = jnp.stack([gain_q.reshape(model_width), gain_k.reshape(model_width)])
     summands = (grad_qkv, grad_outw, grad_up, grad_down, grad_gain, grad_bias, grad_qk)
     if fast:
-        late = fast_reduce(summands[:2], summands[4:])
-        shares = late[:2] + early + late[2:]
+        late = fast_reduce(summands[:1], summands[4:])
+        shares = late[:1] + early + late[1:]
     else:
         pieces = [
             lax.psum_scatter(

time: 547 us -> 543 us (level)
  local copies, waits for them, and re-layouts: 112 us -> 132 us
  waiting for transfers between devices: 177 us -> 160 us
  other arithmetic: 63.1 us -> 72.4 us
  matrix products: 117 us -> 109 us
    all_gather x4, waiting for transfers between devices: 64.3 us -> 35.6 us  [_gather_full(): x = lax.all_gather(z, 'dp', axis=1, tiled=False)]
    all_gather x3, waiting for transfers between devices: 0.01 us -> 17.6 us  [_reduce_matrix(): x = lax.all_gather(total, 'dp', axis=0, tiled=False)]
    unnamed x129 -> x147, local copies, waits for them, and re-layouts: 38.8 us -> 28 us
    broadcast_in_dim x0 -> x8, local copies, waits for them, and re-layouts: none -> 10.2 us  [the longest x4 6.27 us: head_norm(): spread = jnp.mean(centre * centre, axis=-1, keepdims=True)]
    mul x2 -> x8, local copies, waits for them, and re-layouts: 0.15 us -> 9.87 us  [head_norm(): return centre * lax.rsqrt(spread + epsilon) * gain_row]
    sub x0 -> x4, local copies, waits for them, and re-layouts: none -> 8.6 us  [head_norm(): centre = v - jnp.mean(v, axis=-1, keepdims=True)]
    another operation x3 -> x2, other arithmetic: 1.79 us -> 8.34 us
    dynamic_slice x4, local copies, waits for them, and re-layouts: 9.66 us -> 3.23 us  [half(): part = lax.dynamic_slice_in_dim(g, which * cols, cols, 1)]
  transfers between devices with their start and end apart: 38 -> 41, of which waited for: 26 -> 28; matrix products, arithmetic and copies ran while one was open for 26% -> 37% of each run, Pallas kernels for 0% -> 0%
where the time goes in v6:
time: 543 us; the launch traced here: 537 us
  waiting for transfers between devices  160 us (29%)
  local copies, waits for them, and re-layouts  132 us (24%)
  matrix products  109 us (20%)
  other arithmetic  72.4 us (13%)
  starting transfers between devices  37.8 us (7%)
  between operations  15.8 us (3%)
  blocking collectives  9.83 us (2%)
    all_gather x4, waiting for transfers between devices, _gather_full(): x = lax.all_gather(z, 'dp', axis=1, tiled=False)  35.6 us
    ppermute x6, waiting for transfers between devices, _z_gather(): lax.ppermute(piece, 'fsdp', [(i, (i + k) % NF_FAST) for i in range(NF_FAS...  35.1 us
    ppermute x4, waiting for transfers between devices, _reduce_matrix(): lax.ppermute(to_x.astype(jnp.bfloat16), 'dp', [(i, i ^ 2) for i in range(...  31.7 us
    unnamed x147, local copies, waits for them, and re-layouts  28 us
    dot_general x1, matrix products, on_device(): up_pre = jnp.dot(second_low, full_up, preferred_element_type=jnp.float32)  21.3 us
    ppermute x12, waiting for transfers between devices, _reduce_matrix(): lax.ppermute(part.astype(jnp.bfloat16), 'fsdp', [(i, (i + k) % NF_FAST) f...  18.4 us
    all_gather x3, waiting for transfers between devices, _reduce_matrix(): x = lax.all_gather(total, 'dp', axis=0, tiled=False)  17.6 us
    reshape x3, local copies, waits for them, and re-layouts, _gather_full(): x.reshape(NF_FAST, NDP_FAST // 2, 2, rows, cols).transpose(0, 1, 3, 2, 4)  16.9 us
  transfers between devices with their start and end apart: 41, of which 28 were waited for; matrix products, arithmetic and copies ran while one was open for 37% of the time, Pallas kernels for 0%

profile of v6, /device:TPU:8, one launch (start us, length us, event | category | flops | bytes accessed | tf_op | source)
XLA Modules:
  0.0 536.9 jit_solution(10846747977222274661)
XLA Ops:
  15.6 20.1 %collective-permute-done = bf16[48,3584]{1,0:T(8,128)(2,1)S(1)} collective-permute-done((bf16[48,3584]{1,0:T(8,128)(2,1)S(1)}, bf16[48,3584]{1,0:T(8,128)(2,1)S(1)}, u32[]{:S(2)}, u32[]{:S(2)}) %collective-permute-start) | collective-permute-done | bytes 344096 | tf_op jit(solution)/shard_map/ppermute | solution.py:70
  35.7 6.2 %collective-permute-done.1 = bf16[48,3584]{1,0:T(8,128)(2,1)S(1)} collective-permute-done((bf16[48,3584]{1,0:T(8,128)(2,1)S(1)}, bf16[48,3584]{1,0:T(8,128)(2,1)S(1)}, u32[]{:S(2)}, u32[]{:S(2)}) %collective-permute-start.1) | collective-permute-done | bytes 344096 | tf_op jit(solution)/shard_map/ppermute | solution.py:70
  52.2 4.0 collective-permute-done.4
  66.7 2.8 all-gather.19.cloned.1.call-done
  73.0 32.8 %all-gather.17.cloned.1.call-done = bf16[4,384,1152]{2,1,0:T(8,128)(2,1)} async-done(((bf16[4,48,1152]{2,1,0:T(8,128)(2,1)}), bf16[4,384,1152]{2,1,0:T(8,128)(2,1)}) %all-gather.17.cloned.1.call-update) | async-done | bytes 3538960 | tf_op jit(solution)/shard_map/all_gather | solution.py:77
  105.8 5.0 copy.189
  133.9 2.8 copy.211
  138.1 2.9 copy.207
  142.3 2.9 copy.212
  145.3 11.4 %fusion.115 = (f32[12,576]{1,0:T(8,128)S(1)}, f32[12,576,576]{1,2,0:T(8,128)}) fusion(f32[576,12,64]{0,2,1:T(8,128)S(1)} %bitcast.236, f32[12,64]{1,0:T(8,128)S(1)} %mul.371, f32[576,12]{0,1:T(8,128)S(1)} %fusion.93, f32[576,12]{0,1:T(8,128)S(1)} %broadcast_multiply_fusion, f32[576,12,64]{0,2,1:T(8,128)} %bitcast.242, f32[12,64]{1,0:T(8,128)S(1)} %mul.365, ...), kind=kOutput, calls=%fused_computation.248 | convolution fusion | flops 525083904 | bytes 19940352 | tf_op jit(solution)/shard_map/qhd,khd->hqk/dot_general | solution.py:222
  156.8 8.9 %fusion.3 = f32[12,576]{1,0:T(8,128)S(1)} fusion(f32[12,576,576]{1,2,0:T(8,128)} %get-tuple-element.131, f32[12,576]{1,0:T(8,128)S(1)} %get-tuple-element.130), kind=kLoop, calls=%fused_computation.11 | loop fusion | flops 7955712 | bytes 15980544 | tf_op jit(solution)/shard_map/reduce_sum | solution.py:232
  165.7 9.4 %fusion.38 = bf16[12,64,576]{2,1,0:T(8,128)(2,1)S(1)} fusion(bf16[576,12,64]{0,2,1:T(8,128)(2,1)S(1)} %bitcast.278, f32[12,576,576]{1,2,0:T(8,128)} %get-tuple-element.131, f32[12,576]{1,0:T(8,128)S(1)} %fusion.3, f32[12,576]{1,0:T(8,128)S(1)} %get-tuple-element.130), kind=kOutput, calls=%fused_computation.98 | convolution fusion | flops 521994240 | bytes 17750016 | tf_op jit(solution)/shard_map/hqk,khd->qhd/dot_general | solution.py:234
  177.3 9.7 %copy.195 = bf16[4,4,2,48,1536]{4,2,3,1,0:T(2,128)(2,1)} copy(bf16[4,4,2,48,1536]{4,3,2,1,0:T(8,128)(2,1)} %bitcast.271) | data formatting | bytes 9437184 | tf_op jit(solution)/shard_map/reshape | solution.py:78
  187.0 5.8 %copy.229 = bf16[96,8,2,1536]{3,1,2,0:T(8,128)(2,1)} copy(bf16[96,8,2,1536]{3,2,1,0:T(2,128)(2,1)} %bitcast.248) | data formatting | bytes 9437184
  192.8 9.4 %copy.196 = bf16[4,4,192,2,384]{4,3,2,1,0:T(2,128)(2,1)} copy(bf16[4,4,192,2,384]{4,2,3,1,0:T(8,128)(2,1)} %bitcast.272) | data formatting | bytes 9437184 | tf_op jit(solution)/shard_map/transpose | solution.py:78
  202.2 5.5 %copy.230 = bf16[384,8,2,384]{3,1,2,0:T(8,128)(2,1)} copy(bf16[384,8,2,384]{3,2,1,0:T(2,128)(2,1)} %bitcast.249) | data formatting | bytes 9437184
  207.7 21.3 %multiply_convert_fusion = (bf16[576,3072]{1,0:T(8,128)(2,1)S(1)}, f32[576,3072]{1,0:T(8,128)}, f32[576,3072]{1,0:T(8,128)}) fusion(bf16[768,3072]{1,0:T(8,128)(2,1)S(1)} %bitcast.274, f32[576,768]{1,0:T(8,128)S(1)} %get-tuple-element.133, f32[768]{0:T(1024)S(1)} %add.366, f32[768]{0:T(1024)S(1)} %mul.378, f32[576]{0:T(1024)S(1)} %fusion.96, ...), kind=kOutput, calls=%fused_computation.21 | convolution fusion | flops 2835136512 | bytes 24193536 | tf_op jit(solution)/shard_map/dot_general | solution.py:244
  230.8 4.1 fusion.60
  236.6 10.3 %add_convert_fusion = bf16[576,3072]{1,0:T(8,128)(2,1)} fusion(f32[576,3072]{1,0:T(8,128)} %get-tuple-element.95, f32[576,3072]{1,0:T(8,128)} %get-tuple-element.134, bf16[3072,768]{1,0:T(8,128)(2,1)} %bitcast.269, bf16[576,768]{1,0:T(8,128)(2,1)S(1)} %copy-done.27, f32[576]{0:T(1024)S(1)} %fusion.94), kind=kOutput, calls=%fused_computation.20 | convolution fusion | flops 2744008704 | bytes 23300352 | tf_op jit(solution)/shard_map/dot_general | solution.py:253
  246.9 6.2 %fusion.107 = f32[768,3072]{1,0:T(8,128)S(1)} fusion(bf16[576,3072]{1,0:T(8,128)(2,1)} %add_convert_fusion, f32[576,768]{1,0:T(8,128)S(1)} %get-tuple-element.133, f32[768]{0:T(1024)S(1)} %add.366, f32[768]{0:T(1024)S(1)} %mul.378, f32[576]{0:T(1024)S(1)} %fusion.96, f32[576]{0:T(1024)S(1)} %broadcast_multiply_fusion.2), kind=kOutput, calls=%fused_computation.241 | convolution fusion | flops 2720120832 | bytes 14756352 | tf_op jit(solution)/shard_map/dot_general | solution.py:256
  255.9 5.6 %multiply_reduce_fusion.4 = (f32[768]{0:T(1024)S(1)}, f32[576]{0:T(1024)S(1)}, f32[768]{0:T(1024)S(1)}, f32[576,768]{1,0:T(8,128)S(1)}) fusion(f32[576,768]{1,0:T(8,128)S(1)} %get-tuple-element.133, f32[576]{0:T(1024)S(1)} %fusion.96, f32[576]{0:T(1024)S(1)} %broadcast_multiply_fusion.2, f32[768]{0:T(1024)S(1)} %mul.378, ...), kind=kOutput, calls=%fused_computation.84 | convolution fusion | flops 2721445888 | bytes 11812608 | tf_op jit(solution)/shard_map/dot_general | solution.py:259
  267.2 7.9 %collective-permute-done.21 = bf16[4,192,384]{2,1,0:T(8,128)(2,1)S(1)} collective-permute-done((bf16[4,192,384]{2,1,0:T(8,128)(2,1)S(1)}, bf16[4,192,384]{2,1,0:T(8,128)(2,1)S(1)}, u32[]{:S(2)}, u32[]{:S(2)}) %collective-permute-start.21) | collective-permute-done | bytes 589856 | tf_op jit(solution)/shard_map/ppermute | solution.py:137
  282.5 8.0 %collective-permute-done.22 = bf16[4,192,384]{2,1,0:T(8,128)(2,1)S(1)} collective-permute-done((bf16[4,192,384]{2,1,0:T(8,128)(2,1)S(1)}, bf16[4,192,384]{2,1,0:T(8,128)(2,1)S(1)}, u32[]{:S(2)}, u32[]{:S(2)}) %collective-permute-start.22) | collective-permute-done | bytes 589856 | tf_op jit(solution)/shard_map/ppermute | solution.py:144
  290.4 2.8 collective-permute-done.23
  298.3 4.7 collective-permute-done.24
  318.4 10.2 %collective-permute-done.15 = bf16[4,48,1536]{2,1,0:T(8,128)(2,1)S(1)} collective-permute-done((bf16[4,48,1536]{2,1,0:T(8,128)(2,1)S(1)}, bf16[4,48,1536]{2,1,0:T(8,128)(2,1)S(1)}, u32[]{:S(2)}, u32[]{:S(2)}) %collective-permute-start.15) | collective-permute-done | bytes 589856 | tf_op jit(solution)/shard_map/ppermute | solution.py:144
  332.8 8.1 %fusion = f32[12,576]{1,0:T(8,128)S(1)} fusion(bf16[12,576,576]{1,2,0:T(8,128)(2,1)S(1)} %convolution_convert_fusion, f32[12,576,576]{1,2,0:T(8,128)} %get-tuple-element.131, f32[12,576]{1,0:T(8,128)S(1)} %copy-done.42), kind=kLoop, calls=%fused_computation.4 | loop fusion | flops 15918336 | bytes 23943168 | tf_op jit(solution)/shard_map/reduce_sum | solution.py:277
  343.7 10.2 %fusion.2 = bf16[12,576,576]{1,2,0:T(8,128)(2,1)S(1)} fusion(bf16[12,576,576]{1,2,0:T(8,128)(2,1)} %copy-done.4, f32[12,576,576]{1,2,0:T(8,128)} %get-tuple-element.131, f32[12,576]{1,0:T(8,128)S(1)} %fusion, f32[12,576]{1,0:T(8,128)S(1)} %copy-done.42), kind=kLoop, calls=%fused_computation.6 | loop fusion | flops 19906560 | bytes 31905792 | tf_op jit(solution)/shard_map/convert_element_type | solution.py:278
  356.8 9.8 %fusion.35 = bf16[1,576,12,64]{1,3,2,0:T(8,128)(2,1)} fusion(bf16[576,12,64]{0,2,1:T(8,128)(2,1)S(1)} %bitcast.257, f32[12,576,576]{1,2,0:T(8,128)} %get-tuple-element.131, f32[12,576]{1,0:T(8,128)S(1)} %copy-done.42), kind=kOutput, calls=%fused_computation.93 | convolution fusion | flops 517570560 | bytes 17722368 | tf_op jit(solution)/shard_map/hqk,qhd->khd/dot_general | solution.py:274
  367.8 4.0 multiply_bitcast_fusion
  371.8 3.0 collective-permute-done.8
  378.7 3.0 multiply_bitcast_fusion.1
  382.1 9.8 %all-gather.3 = f32[384,384]{1,0:T(8,128)S(1)} all-gather(f32[48,384]{1,0:T(8,128)S(1)} %fusion.88), channel_id=5, replica_groups=mesh['dp'=8,'fsdp'=4] {'dp'}, dimensions={0}, use_global_device_ids=true | all-gather | bytes 663552 | tf_op jit(solution)/shard_map/all_gather | solution.py:153
  393.1 3.5 copy.199
  398.2 3.5 copy.198
  409.0 3.0 copy.213
  419.2 2.9 copy.205
  425.7 8.2 %fusion.31 = (bf16[576,768]{1,0:T(8,128)(2,1)S(1)}, bf16[576,768]{1,0:T(8,128)(2,1)S(1)}) fusion(f32[576,768]{1,0:T(8,128)} %copy.209, f32[576,768]{1,0:T(8,128)} %copy.208, f32[576,768]{1,0:T(8,128)} %copy.207, f32[576,768]{1,0:T(8,128)S(1)} %copy-done.17, f32[576,768]{1,0:T(8,128)} %copy.205, f32[768]{0:T(1024)S(1)} %copy-done.59, ...), kind=kLoop, calls=%fused_computation.80 | loop fusion | flops 7077888 | bytes 23009280 | tf_op jit(solution)/shard_map/convert
  433.9 6.1 %fusion.49 = f32[768,2304]{1,0:T(8,128)} fusion(bf16[576,768]{1,0:T(8,128)(2,1)S(1)} %copy-done.41, bf16[576,768]{1,0:T(8,128)(2,1)S(1)} %get-tuple-element.97, bf16[576,768]{1,0:T(8,128)(2,1)S(1)} %get-tuple-element.96, bf16[576,768]{1,0:T(8,128)(2,1)S(1)} %copy-done.15, f32[768]{0:T(1024)S(1)} %copy-done.62, f32[768]{0:T(1024)S(1)} %copy-done.58, ...), kind=kOutput, calls=%fused_computation.119 | convolution fusion | flops 2049048576 | bytes 10627584 | tf_op jit(solution)/shard_map/dot_general | solution.py:305
  445.0 4.2 select_maximum_fusion
  449.2 3.1 copy-done.8
  461.0 8.2 %collective-permute-done.28 = bf16[4,48,1280]{2,1,0:T(8,128)(2,1)S(1)} collective-permute-done((bf16[4,48,1280]{2,1,0:T(8,128)(2,1)S(1)}, bf16[4,48,1280]{2,1,0:T(8,128)(2,1)S(1)}, u32[]{:S(2)}, u32[]{:S(2)}) %collective-permute-start.28) | collective-permute-done | bytes 491552 | tf_op jit(solution)/shard_map/ppermute | solution.py:137
  471.5 10.6 %collective-permute-done.29 = bf16[4,48,1280]{2,1,0:T(8,128)(2,1)S(1)} collective-permute-done((bf16[4,48,1280]{2,1,0:T(8,128)(2,1)S(1)}, bf16[4,48,1280]{2,1,0:T(8,128)(2,1)S(1)}, u32[]{:S(2)}, u32[]{:S(2)}) %collective-permute-start.29) | collective-permute-done | bytes 491552 | tf_op jit(solution)/shard_map/ppermute | solution.py:144
  483.8 2.8 collective-permute-start.32
  487.6 5.2 collective-permute-done.31
  496.4 7.4 %multiply_convert_fusion.3 = bf16[576,768]{1,0:T(8,128)(2,1)} fusion(f32[576,768]{1,0:T(8,128)S(1)} %copy-done.11, bf16[576,3072]{1,0:T(8,128)(2,1)} %copy-done.66, bf16[3072,768]{1,0:T(8,128)(2,1)} %bitcast.270, f32[576]{0:T(1024)S(1)} %fusion.94), kind=kOutput, calls=%fused_computation.90 | convolution fusion | flops 2719236096 | bytes 10914048 | tf_op jit(solution)/shard_map/dot_general | solution.py:247
  505.6 17.6 %all-gather.27.cloned.1.call-done = f32[384,1280]{1,0:T(8,128)} async-done(((f32[48,1280]{1,0:T(8,128)}), f32[384,1280]{1,0:T(8,128)}) %all-gather.27.cloned.1.call-update) | async-done | bytes 1966096 | tf_op jit(solution)/shard_map/all_gather | solution.py:153
  523.2 3.1 copy.217
  (357 shorter events, 163.5 us)
Async XLA Ops:
  7.2 62.3 %all-gather.19.cloned.1.call-start = ((), (), s32[]{:S(2)}) async-start(), calls=%async_computation.2 | async-start | bytes 1327104 | tf_op jit(solution)/shard_map/all_gather | solution.py:77
  10.9 24.8 %collective-permute-start = (bf16[48,3584]{1,0:T(8,128)(2,1)S(1)}, bf16[48,3584]{1,0:T(8,128)(2,1)S(1)}, u32[]{:S(2)}, u32[]{:S(2)}) collective-permute-start(bf16[48,3584]{1,0:T(8,128)(2,1)S(1)} %get-tuple-element.120), channel_id=1, source_target_pairs={{0,1},{1,2},{2,3},{3,0},{4,5},{5,6},{6,7},{7,4},{8,9},{9,10},{10,1... | collective-permute-start | bytes 1032200 | tf_op jit(solution)/shard_map/ppermute | solution.py:70
  12.5 29.4 %collective-permute-start.1 = (bf16[48,3584]{1,0:T(8,128)(2,1)S(1)}, bf16[48,3584]{1,0:T(8,128)(2,1)S(1)}, u32[]{:S(2)}, u32[]{:S(2)}) collective-permute-start(bf16[48,3584]{1,0:T(8,128)(2,1)S(1)} %get-tuple-element.120), channel_id=1, source_target_pairs={{0,2},{1,3},{2,0},{3,1},{4,6},{5,7},{6,4},{7,5},{8,10},{9,11},{10,... | collective-permute-start | bytes 1032200 | tf_op jit(solution)/shard_map/ppermute | solution.py:70
  13.6 30.1 %collective-permute-start.2 = (bf16[48,3584]{1,0:T(8,128)(2,1)S(1)}, bf16[48,3584]{1,0:T(8,128)(2,1)S(1)}, u32[]{:S(2)}, u32[]{:S(2)}) collective-permute-start(bf16[48,3584]{1,0:T(8,128)(2,1)S(1)} %get-tuple-element.120), channel_id=1, source_target_pairs={{0,3},{1,0},{2,1},{3,2},{4,7},{5,4},{6,5},{7,6},{8,11},{9,8},{10,9... | collective-permute-start | bytes 1032200 | tf_op jit(solution)/shard_map/ppermute | solution.py:70
  45.3 60.6 %all-gather.17.cloned.1.call-start = ((), (), s32[]{:S(2)}) async-start(), calls=%async_computation.1 | async-start | bytes 3981312 | tf_op jit(solution)/shard_map/all_gather | solution.py:77
  46.2 6.0 %collective-permute-start.3 = (bf16[48,1152]{1,0:T(8,128)(2,1)S(1)}, bf16[48,1152]{1,0:T(8,128)(2,1)S(1)}, u32[]{:S(2)}, u32[]{:S(2)}) collective-permute-start(bf16[48,1152]{1,0:T(8,128)(2,1)S(1)} %dynamic_slice.143), channel_id=1, source_target_pairs={{0,1},{1,2},{2,3},{3,0},{4,5},{5,6},{6,7},{7,4},{8,9},{9,10},{10,1... | collective-permute-start | bytes 331784 | tf_op jit(solution)/shard_map/ppermute | solution.py:70
  46.3 9.9 %collective-permute-start.4 = (bf16[48,1152]{1,0:T(8,128)(2,1)S(1)}, bf16[48,1152]{1,0:T(8,128)(2,1)S(1)}, u32[]{:S(2)}, u32[]{:S(2)}) collective-permute-start(bf16[48,1152]{1,0:T(8,128)(2,1)S(1)} %dynamic_slice.143), channel_id=1, source_target_pairs={{0,2},{1,3},{2,0},{3,1},{4,6},{5,7},{6,4},{7,5},{8,10},{9,11},{10,... | collective-permute-start | bytes 331784 | tf_op jit(solution)/shard_map/ppermute | solution.py:70
  48.0 9.8 %collective-permute-start.5 = (bf16[48,1152]{1,0:T(8,128)(2,1)S(1)}, bf16[48,1152]{1,0:T(8,128)(2,1)S(1)}, u32[]{:S(2)}, u32[]{:S(2)}) collective-permute-start(bf16[48,1152]{1,0:T(8,128)(2,1)S(1)} %dynamic_slice.143), channel_id=1, source_target_pairs={{0,3},{1,0},{2,1},{3,2},{4,7},{5,4},{6,5},{7,6},{8,11},{9,8},{10,9... | collective-permute-start | bytes 331784 | tf_op jit(solution)/shard_map/ppermute | solution.py:70
  59.2 118.1 %all-gather.21.cloned.1.call-start = ((), (), s32[]{:S(2)}) async-start(), calls=%async_computation.3 | async-start | bytes 5308416 | tf_op jit(solution)/shard_map/all_gather | solution.py:77
  60.2 132.6 %all-gather.15.cloned.1.call-start = ((), (), s32[]{:S(2)}) async-start(), calls=%async_computation | async-start | bytes 5308416 | tf_op jit(solution)/shard_map/all_gather | solution.py:77
  61.4 50.0 %copy-start.51 = (f32[576]{0:T(1024)}, f32[576]{0:T(1024)S(1)}, u32[]{:S(2)}) copy-start(f32[576]{0:T(1024)S(1)} %broadcast_multiply_fusion.3) | copy-start | bytes 6916
  61.9 49.6 %copy-start.55 = (f32[576]{0:T(1024)}, f32[576]{0:T(1024)S(1)}, u32[]{:S(2)}) copy-start(f32[576]{0:T(1024)S(1)} %fusion.95) | copy-start | bytes 6916
  63.4 329.8 %all-gather.25.cloned.1.call-start = ((), (), s32[]{:S(2)}) async-start(), calls=%async_computation.5 | async-start | bytes 2654208 | tf_op jit(solution)/shard_map/all_gather | solution.py:153
  64.9 80.4 %copy-start.49 = (f32[12,64]{1,0:T(8,128)}, f32[12,64]{1,0:T(8,128)S(1)}, u32[]{:S(2)}) copy-start(f32[12,64]{1,0:T(8,128)S(1)} %mul.365) | copy-start | bytes 9220
  65.6 79.7 %copy-start.43 = (f32[12,64]{1,0:T(8,128)}, f32[12,64]{1,0:T(8,128)S(1)}, u32[]{:S(2)}) copy-start(f32[12,64]{1,0:T(8,128)S(1)} %mul.371) | copy-start | bytes 9220
  66.4 45.0 %copy-start.61 = (f32[768]{0:T(1024)}, f32[768]{0:T(1024)S(1)}, u32[]{:S(2)}) copy-start(f32[768]{0:T(1024)S(1)} %add.358) | copy-start | bytes 9220
  66.5 44.9 %copy-start.57 = (f32[768]{0:T(1024)}, f32[768]{0:T(1024)S(1)}, u32[]{:S(2)}) copy-start(f32[768]{0:T(1024)S(1)} %mul.358) | copy-start | bytes 9220
  176.1 85.4 %copy-start.10 = (f32[576,768]{1,0:T(8,128)}, f32[576,768]{1,0:T(8,128)S(1)}, u32[]{:S(2)}) copy-start(f32[576,768]{1,0:T(8,128)S(1)} %get-tuple-element.133) | copy-start | bytes 5308420
  236.6 26.0 %collective-permute-start.20 = (bf16[4,4,192,384]{3,2,1,0:T(8,128)(2,1)}, bf16[4,4,192,384]{3,2,1,0:T(8,128)(2,1)}, u32[]{:S(2)}, u32[]{:S(2)}) collective-permute-start(bf16[4,4,192,384]{3,2,1,0:T(8,128)(2,1)} %bitcast.53), channel_id=1, source_target_pairs={{0,4},{4,0},{8,12},{12,8},{16,20},{20,16},{24,28},{28,24},{1,5},{5... | collective-permute-start | bytes 7077896 | tf_op jit(solution)/shard_map/ppermute | solution.py:131
  254.8 22.9 %collective-permute-start.13 = (bf16[4,4,48,1536]{3,2,1,0:T(8,128)(2,1)}, bf16[4,4,48,1536]{3,2,1,0:T(8,128)(2,1)}, u32[]{:S(2)}, u32[]{:S(2)}) collective-permute-start(bf16[4,4,48,1536]{3,2,1,0:T(8,128)(2,1)} %bitcast.41), channel_id=1, source_target_pairs={{0,4},{4,0},{8,12},{12,8},{16,20},{20,16},{24,28},{28,24},{1,5},{5... | collective-permute-start | bytes 7077896 | tf_op jit(solution)/shard_map/ppermute | solution.py:131
  265.2 9.9 %collective-permute-start.21 = (bf16[4,192,384]{2,1,0:T(8,128)(2,1)S(1)}, bf16[4,192,384]{2,1,0:T(8,128)(2,1)S(1)}, u32[]{:S(2)}, u32[]{:S(2)}) collective-permute-start(bf16[4,192,384]{2,1,0:T(8,128)(2,1)S(1)} %fusion.58), channel_id=1, source_target_pairs={{0,8},{4,20},{8,0},{12,28},{16,24},{20,4},{24,16},{28,12},{1,9},{5... | collective-permute-start | bytes 1769480 | tf_op jit(solution)/shard_map/ppermute | solution.py:137
  275.5 14.9 %collective-permute-start.22 = (bf16[4,192,384]{2,1,0:T(8,128)(2,1)S(1)}, bf16[4,192,384]{2,1,0:T(8,128)(2,1)S(1)}, u32[]{:S(2)}, u32[]{:S(2)}) collective-permute-start(bf16[4,192,384]{2,1,0:T(8,128)(2,1)S(1)} %get-tuple-element.98), channel_id=1, source_target_pairs={{0,8},{4,12},{8,0},{12,4},{16,24},{20,28},{24,16},{28,20},{1,9},{5... | collective-permute-start | bytes 1769480 | tf_op jit(solution)/shard_map/ppermute | solution.py:144
  277.0 16.2 %collective-permute-start.23 = (bf16[4,192,384]{2,1,0:T(8,128)(2,1)S(1)}, bf16[4,192,384]{2,1,0:T(8,128)(2,1)S(1)}, u32[]{:S(2)}, u32[]{:S(2)}) collective-permute-start(bf16[4,192,384]{2,1,0:T(8,128)(2,1)S(1)} %get-tuple-element.99), channel_id=1, source_target_pairs={{0,16},{4,20},{8,24},{12,28},{16,0},{20,4},{24,8},{28,12},{1,17},{... | collective-permute-start | bytes 1769480 | tf_op jit(solution)/shard_map/ppermute | solution.py:145
  281.2 27.9 %collective-permute-start.14 = (bf16[4,48,1536]{2,1,0:T(8,128)(2,1)}, bf16[4,48,1536]{2,1,0:T(8,128)(2,1)}, u32[]{:S(2)}, u32[]{:S(2)}) collective-permute-start(bf16[4,48,1536]{2,1,0:T(8,128)(2,1)} %fusion.57), channel_id=1, source_target_pairs={{0,8},{4,20},{8,0},{12,28},{16,24},{20,4},{24,16},{28,12},{1,9},{5... | collective-permute-start | bytes 1769480 | tf_op jit(solution)/shard_map/ppermute | solution.py:137
  293.5 9.6 %collective-permute-start.24 = (bf16[192,384]{1,0:T(8,128)(2,1)S(1)}, bf16[192,384]{1,0:T(8,128)(2,1)S(1)}, u32[]{:S(2)}, u32[]{:S(2)}) collective-permute-start(bf16[192,384]{1,0:T(8,128)(2,1)S(1)} %get-tuple-element.110), channel_id=1, source_target_pairs={{0,1},{1,2},{2,3},{3,0},{4,5},{5,6},{6,7},{7,4},{8,9},{9,10},{10,1... | collective-permute-start | bytes 442376 | tf_op jit(solution)/shard_map/ppermute | solution.py:150
  295.0 9.6 %collective-permute-start.25 = (bf16[192,384]{1,0:T(8,128)(2,1)S(1)}, bf16[192,384]{1,0:T(8,128)(2,1)S(1)}, u32[]{:S(2)}, u32[]{:S(2)}) collective-permute-start(bf16[192,384]{1,0:T(8,128)(2,1)S(1)} %get-tuple-element.112), channel_id=1, source_target_pairs={{0,2},{1,3},{2,0},{3,1},{4,6},{5,7},{6,4},{7,5},{8,10},{9,11},{10,... | collective-permute-start | bytes 442376 | tf_op jit(solution)/shard_map/ppermute | solution.py:150
  296.4 10.0 %collective-permute-start.26 = (bf16[192,384]{1,0:T(8,128)(2,1)S(1)}, bf16[192,384]{1,0:T(8,128)(2,1)S(1)}, u32[]{:S(2)}, u32[]{:S(2)}) collective-permute-start(bf16[192,384]{1,0:T(8,128)(2,1)S(1)} %get-tuple-element.111), channel_id=1, source_target_pairs={{0,3},{1,0},{2,1},{3,2},{4,7},{5,4},{6,5},{7,6},{8,11},{9,8},{10,9... | collective-permute-start | bytes 442376 | tf_op jit(solution)/shard_map/ppermute | solution.py:150
  307.3 90.9 %all-gather.23.cloned.1.call-start = ((), (), s32[]{:S(2)}) async-start(), calls=%async_computation.4 | async-start | bytes 2654208 | tf_op jit(solution)/shard_map/all_gather | solution.py:153
  311.3 17.3 %collective-permute-start.15 = (bf16[4,48,1536]{2,1,0:T(8,128)(2,1)S(1)}, bf16[4,48,1536]{2,1,0:T(8,128)(2,1)S(1)}, u32[]{:S(2)}, u32[]{:S(2)}) collective-permute-start(bf16[4,48,1536]{2,1,0:T(8,128)(2,1)S(1)} %get-tuple-element.100), channel_id=1, source_target_pairs={{0,8},{4,12},{8,0},{12,4},{16,24},{20,28},{24,16},{28,20},{1,9},{5... | collective-permute-start | bytes 1769480 | tf_op jit(solution)/shard_map/ppermute | solution.py:144
  311.9 17.0 %collective-permute-start.16 = (bf16[4,48,1536]{2,1,0:T(8,128)(2,1)S(1)}, bf16[4,48,1536]{2,1,0:T(8,128)(2,1)S(1)}, u32[]{:S(2)}, u32[]{:S(2)}) collective-permute-start(bf16[4,48,1536]{2,1,0:T(8,128)(2,1)S(1)} %get-tuple-element.101), channel_id=1, source_target_pairs={{0,16},{4,20},{8,24},{12,28},{16,0},{20,4},{24,8},{28,12},{1,17},{... | collective-permute-start | bytes 1769480 | tf_op jit(solution)/shard_map/ppermute | solution.py:145
  318.4 35.6 %collective-permute-start.6 = (bf16[4,4,48,384]{3,2,1,0:T(8,128)(2,1)}, bf16[4,4,48,384]{3,2,1,0:T(8,128)(2,1)}, u32[]{:S(2)}, u32[]{:S(2)}) collective-permute-start(bf16[4,4,48,384]{3,2,1,0:T(8,128)(2,1)} %bitcast.29), channel_id=1, source_target_pairs={{0,4},{4,0},{8,12},{12,8},{16,20},{20,16},{24,28},{28,24},{1,5},{5... | collective-permute-start | bytes 1769480 | tf_op jit(solution)/shard_map/ppermute | solution.py:131
  330.4 10.5 %collective-permute-start.17 = (bf16[48,1536]{1,0:T(8,128)(2,1)S(1)}, bf16[48,1536]{1,0:T(8,128)(2,1)S(1)}, u32[]{:S(2)}, u32[]{:S(2)}) collective-permute-start(bf16[48,1536]{1,0:T(8,128)(2,1)S(1)} %get-tuple-element.113), channel_id=1, source_target_pairs={{0,1},{1,2},{2,3},{3,0},{4,5},{5,6},{6,7},{7,4},{8,9},{9,10},{10,1... | collective-permute-start | bytes 442376 | tf_op jit(solution)/shard_map/ppermute | solution.py:150
  330.5 10.8 %collective-permute-start.18 = (bf16[48,1536]{1,0:T(8,128)(2,1)S(1)}, bf16[48,1536]{1,0:T(8,128)(2,1)S(1)}, u32[]{:S(2)}, u32[]{:S(2)}) collective-permute-start(bf16[48,1536]{1,0:T(8,128)(2,1)S(1)} %get-tuple-element.115), channel_id=1, source_target_pairs={{0,2},{1,3},{2,0},{3,1},{4,6},{5,7},{6,4},{7,5},{8,10},{9,11},{10,... | collective-permute-start | bytes 442376 | tf_op jit(solution)/shard_map/ppermute | solution.py:150
  331.2 11.7 %collective-permute-start.19 = (bf16[48,1536]{1,0:T(8,128)(2,1)S(1)}, bf16[48,1536]{1,0:T(8,128)(2,1)S(1)}, u32[]{:S(2)}, u32[]{:S(2)}) collective-permute-start(bf16[48,1536]{1,0:T(8,128)(2,1)S(1)} %get-tuple-element.114), channel_id=1, source_target_pairs={{0,3},{1,0},{2,1},{3,2},{4,7},{5,4},{6,5},{7,6},{8,11},{9,8},{10,9... | collective-permute-start | bytes 442376 | tf_op jit(solution)/shard_map/ppermute | solution.py:150
  343.7 179.5 %all-gather.27.cloned.1.call-start = ((), (), s32[]{:S(2)}) async-start(), calls=%async_computation.6 | async-start | bytes 2211840 | tf_op jit(solution)/shard_map/all_gather | solution.py:153
  355.3 11.4 %collective-permute-start.7 = (bf16[4,48,384]{2,1,0:T(8,128)(2,1)S(1)}, bf16[4,48,384]{2,1,0:T(8,128)(2,1)S(1)}, u32[]{:S(2)}, u32[]{:S(2)}) collective-permute-start(bf16[4,48,384]{2,1,0:T(8,128)(2,1)S(1)} %fusion.77), channel_id=1, source_target_pairs={{0,8},{4,20},{8,0},{12,28},{16,24},{20,4},{24,16},{28,12},{1,9},{5... | collective-permute-start | bytes 442376 | tf_op jit(solution)/shard_map/ppermute | solution.py:137
  366.7 8.0 %collective-permute-start.8 = (bf16[4,48,384]{2,1,0:T(8,128)(2,1)S(1)}, bf16[4,48,384]{2,1,0:T(8,128)(2,1)S(1)}, u32[]{:S(2)}, u32[]{:S(2)}) collective-permute-start(bf16[4,48,384]{2,1,0:T(8,128)(2,1)S(1)} %get-tuple-element.108), channel_id=1, source_target_pairs={{0,8},{4,12},{8,0},{12,4},{16,24},{20,28},{24,16},{28,20},{1,9},{5... | collective-permute-start | bytes 442376 | tf_op jit(solution)/shard_map/ppermute | solution.py:144
  367.3 7.4 %collective-permute-start.9 = (bf16[4,48,384]{2,1,0:T(8,128)(2,1)S(1)}, bf16[4,48,384]{2,1,0:T(8,128)(2,1)S(1)}, u32[]{:S(2)}, u32[]{:S(2)}) collective-permute-start(bf16[4,48,384]{2,1,0:T(8,128)(2,1)S(1)} %get-tuple-element.109), channel_id=1, source_target_pairs={{0,16},{4,20},{8,24},{12,28},{16,0},{20,4},{24,8},{28,12},{1,17},{... | collective-permute-start | bytes 442376 | tf_op jit(solution)/shard_map/ppermute | solution.py:145
  374.8 6.9 %collective-permute-start.10 = (bf16[48,384]{1,0:T(8,128)(2,1)S(1)}, bf16[48,384]{1,0:T(8,128)(2,1)S(1)}, u32[]{:S(2)}, u32[]{:S(2)}) collective-permute-start(bf16[48,384]{1,0:T(8,128)(2,1)S(1)} %get-tuple-element.121), channel_id=1, source_target_pairs={{0,1},{1,2},{2,3},{3,0},{4,5},{5,6},{6,7},{7,4},{8,9},{9,10},{10,1... | collective-permute-start | bytes 110600 | tf_op jit(solution)/shard_map/ppermute | solution.py:150
  375.8 5.9 %collective-permute-start.11 = (bf16[48,384]{1,0:T(8,128)(2,1)S(1)}, bf16[48,384]{1,0:T(8,128)(2,1)S(1)}, u32[]{:S(2)}, u32[]{:S(2)}) collective-permute-start(bf16[48,384]{1,0:T(8,128)(2,1)S(1)} %get-tuple-element.123), channel_id=1, source_target_pairs={{0,2},{1,3},{2,0},{3,1},{4,6},{5,7},{6,4},{7,5},{8,10},{9,11},{10,... | collective-permute-start | bytes 110600 | tf_op jit(solution)/shard_map/ppermute | solution.py:150
  377.8 4.3 collective-permute-start.12
  453.8 4.3 collective-permute-start.27
  460.2 8.9 %collective-permute-start.28 = (bf16[4,48,1280]{2,1,0:T(8,128)(2,1)S(1)}, bf16[4,48,1280]{2,1,0:T(8,128)(2,1)S(1)}, u32[]{:S(2)}, u32[]{:S(2)}) collective-permute-start(bf16[4,48,1280]{2,1,0:T(8,128)(2,1)S(1)} %fusion.59), channel_id=1, source_target_pairs={{0,8},{4,20},{8,0},{12,28},{16,24},{20,4},{24,16},{28,12},{1,9},{5... | collective-permute-start | bytes 1474568 | tf_op jit(solution)/shard_map/ppermute | solution.py:137
  469.4 12.7 %collective-permute-start.29 = (bf16[4,48,1280]{2,1,0:T(8,128)(2,1)S(1)}, bf16[4,48,1280]{2,1,0:T(8,128)(2,1)S(1)}, u32[]{:S(2)}, u32[]{:S(2)}) collective-permute-start(bf16[4,48,1280]{2,1,0:T(8,128)(2,1)S(1)} %get-tuple-element.104), channel_id=1, source_target_pairs={{0,8},{4,12},{8,0},{12,4},{16,24},{20,28},{24,16},{28,20},{1,9},{5... | collective-permute-start | bytes 1474568 | tf_op jit(solution)/shard_map/ppermute | solution.py:144
  470.1 12.3 %collective-permute-start.30 = (bf16[4,48,1280]{2,1,0:T(8,128)(2,1)S(1)}, bf16[4,48,1280]{2,1,0:T(8,128)(2,1)S(1)}, u32[]{:S(2)}, u32[]{:S(2)}) collective-permute-start(bf16[4,48,1280]{2,1,0:T(8,128)(2,1)S(1)} %get-tuple-element.105), channel_id=1, source_target_pairs={{0,16},{4,20},{8,24},{12,28},{16,0},{20,4},{24,8},{28,12},{1,17},{... | collective-permute-start | bytes 1474568 | tf_op jit(solution)/shard_map/ppermute | solution.py:145
  482.7 10.1 %collective-permute-start.31 = (bf16[48,1280]{1,0:T(8,128)(2,1)S(1)}, bf16[48,1280]{1,0:T(8,128)(2,1)S(1)}, u32[]{:S(2)}, u32[]{:S(2)}) collective-permute-start(bf16[48,1280]{1,0:T(8,128)(2,1)S(1)} %get-tuple-element.116), channel_id=1, source_target_pairs={{0,1},{1,2},{2,3},{3,0},{4,5},{5,6},{6,7},{7,4},{8,9},{9,10},{10,1... | collective-permute-start | bytes 368648 | tf_op jit(solution)/shard_map/ppermute | solution.py:150
  483.8 10.2 %collective-permute-start.32 = (bf16[48,1280]{1,0:T(8,128)(2,1)S(1)}, bf16[48,1280]{1,0:T(8,128)(2,1)S(1)}, u32[]{:S(2)}, u32[]{:S(2)}) collective-permute-start(bf16[48,1280]{1,0:T(8,128)(2,1)S(1)} %get-tuple-element.118), channel_id=1, source_target_pairs={{0,2},{1,3},{2,0},{3,1},{4,6},{5,7},{6,4},{7,5},{8,10},{9,11},{10,... | collective-permute-start | bytes 368648 | tf_op jit(solution)/shard_map/ppermute | solution.py:150
  486.6 8.9 %collective-permute-start.33 = (bf16[48,1280]{1,0:T(8,128)(2,1)S(1)}, bf16[48,1280]{1,0:T(8,128)(2,1)S(1)}, u32[]{:S(2)}, u32[]{:S(2)}) collective-permute-start(bf16[48,1280]{1,0:T(8,128)(2,1)S(1)} %get-tuple-element.117), channel_id=1, source_target_pairs={{0,3},{1,0},{2,1},{3,2},{4,7},{5,4},{6,5},{7,6},{8,11},{9,8},{10,9... | collective-permute-start | bytes 368648 | tf_op jit(solution)/shard_map/ppermute | solution.py:150
  (60 other events, 490.9 us)
Sparse Core Ops, SparseCore 0:
  45.4 24.0 all-gather.18
  72.0 33.8 all-gather.16
  108.3 38.8 all-gather.20
  149.5 38.7 all-gather.14
  307.4 30.7 all-gather.24
  343.8 32.1 all-gather.22
  496.5 26.6 all-gather.26

commit v7 on v4

--- a/solution.py
+++ b/solution.py
@@ -135,11 +135,13 @@
 
 
 def fast_reduce(mats, gains):
-    out = [_reduce_matrix(m) for m in mats]
-    stacked = lax.psum(jnp.concatenate(gains, axis=0), ("dp", "fsdp"))
-    f = lax.axis_index("fsdp")
-    width = stacked.shape[1] // NF_FAST
-    mine = lax.dynamic_slice_in_dim(stacked, f * width, width, 1)
+    stacked = jnp.concatenate(gains, axis=0)
+    pad = 2 * LANES - stacked.shape[0]
+    first = jnp.concatenate([mats[0], jnp.pad(stacked.T, ((0, 0), (0, pad)))], axis=1)
+    shard = _reduce_matrix(first)
+    width = mats[0].shape[1]
+    out = [shard[:, :width]] + [_reduce_matrix(m) for m in mats[1:]]
+    mine = shard[:, width : width + stacked.shape[0]].T
     rows = 0
     for g in gains:
         out.append(mine[rows : rows + g.shape[0]])

time: 536 us -> 507 us (0.946)
  blocking collectives: 52.6 us -> 10.9 us
  starting transfers between devices: 52.8 us -> 59.1 us
    psum x1 -> x0, blocking collectives: 41.5 us -> none  [fast_reduce(): stacked = lax.psum(jnp.concatenate(gains, axis=0), ('dp', 'fsdp'))]
    ppermute x4, waiting for transfers between devices: 21 us -> 28.3 us  [_reduce_matrix(): lax.ppermute(to_x.astype(jnp.bfloat16), 'dp', [(i, i ^ 2) for i in range(...]
    unnamed x128 -> x129, local copies, waits for them, and re-layouts: 33.6 us -> 35.6 us
where the time goes in v7:
time: 507 us; the launch traced here: 498 us
  waiting for transfers between devices  119 us (23%)
  matrix products  117 us (23%)
  local copies, waits for them, and re-layouts  115 us (23%)
  other arithmetic  61.2 us (12%)
  starting transfers between devices  59.1 us (12%)
  between operations  15.6 us (3%)
  blocking collectives  10.9 us (2%)
    unnamed x129, local copies, waits for them, and re-layouts  35.6 us
    ppermute x4, waiting for transfers between devices, _reduce_matrix(): lax.ppermute(to_x.astype(jnp.bfloat16), 'dp', [(i, i ^ 2) for i in range(...  28.3 us
    reshape x4, local copies, waits for them, and re-layouts, _gather_matrix(): x.reshape(NF_FAST, NDP_FAST // 2, 2, rows, cols).transpose(0, 1, 3, 2, 4)  26 us
    ppermute x12, waiting for transfers between devices, _reduce_matrix(): lax.ppermute(part.astype(jnp.bfloat16), 'fsdp', [(i, (i + k) % NF_FAST) f...  23.6 us
    ppermute x15, starting transfers between devices, _z_gather(): lax.ppermute(piece, 'fsdp', [(i, (i + k) % NF_FAST) for i in range(NF_FAS...  22.5 us
    ppermute x12, starting transfers between devices, _reduce_matrix(): lax.ppermute(part.astype(jnp.bfloat16), 'fsdp', [(i, (i + k) % NF_FAST) f...  21.9 us
    all_gather x4, waiting for transfers between devices, _gather_matrix(): x = lax.all_gather(z, 'dp', axis=1, tiled=False)  21.5 us
    ppermute x4, waiting for transfers between devices, _reduce_matrix(): lax.ppermute(of_chip(j ^ 3).astype(jnp.bfloat16), 'dp', [(i, i ^ 2) if i...  21.5 us
  transfers between devices with their start and end apart: 50, of which 32 were waited for; matrix products, arithmetic and copies ran while one was open for 30% of the time, Pallas kernels for 0%

profile of v7, /device:TPU:8, one launch (start us, length us, event | category | flops | bytes accessed | tf_op | source)
XLA Modules:
  0.0 498.1 jit_solution(1561127114572154273)
XLA Ops:
  16.8 4.7 collective-permute-start.4
  35.9 5.9 %collective-permute-done.13 = bf16[192,384]{1,0:T(8,128)(2,1)S(1)} collective-permute-done((bf16[192,384]{1,0:T(8,128)(2,1)S(1)}, bf16[192,384]{1,0:T(8,128)(2,1)S(1)}, u32[]{:S(2)}, u32[]{:S(2)}) %collective-permute-start.13) | collective-permute-done | bytes 147488 | tf_op jit(solution)/shard_map/ppermute | solution.py:70
  53.0 2.8 collective-permute-start.9
  59.9 4.2 collective-permute-done.9
  72.9 6.5 %all-gather.16.cloned.1.call-done = bf16[4,384,1152]{2,1,0:T(8,128)(2,1)} async-done(((bf16[4,48,1152]{2,1,0:T(8,128)(2,1)}), bf16[4,384,1152]{2,1,0:T(8,128)(2,1)}) %all-gather.16.cloned.1.call-update) | async-done | bytes 3538960 | tf_op jit(solution)/shard_map/all_gather | solution.py:82
  79.4 5.0 copy.134
  91.3 3.4 fusion.112
  102.6 8.3 %fusion.114 = (f32[12,576]{1,0:T(8,128)S(1)}, f32[12,576,576]{1,2,0:T(8,128)}) fusion(f32[576,12,64]{0,2,1:T(8,128)S(1)} %bitcast.247, f32[12,64]{1,0:T(8,128)S(1)} %mul.360, f32[576,12]{0,1:T(8,128)S(1)} %fusion.93, f32[576,12]{0,1:T(8,128)S(1)} %broadcast_multiply_fusion, f32[576,12,64]{0,2,1:T(8,128)S(1)} %bitcast.239, f32[12,64]{1,0:T(8,128)S(1)} %mul.354, ...), kind=kOutput, calls=%fused_computation.249 | convolution fusion | flops 525083904 | bytes 19940352 | tf_op jit(solution)/shard_map/while/body/eval_jaxpr/qhd,khd->hqk/dot_general | solution.py:195
  110.9 8.6 %fusion.3 = f32[12,576]{1,0:T(8,128)S(1)} fusion(f32[12,576,576]{1,2,0:T(8,128)} %get-tuple-element.166, f32[12,576]{1,0:T(8,128)S(1)} %get-tuple-element.165), kind=kLoop, calls=%fused_computation.14 | loop fusion | flops 7955712 | bytes 15980544 | tf_op jit(solution)/shard_map/while/body/eval_jaxpr/reduce_sum | solution.py:205
  119.5 9.7 %fusion.31 = bf16[12,64,576]{2,1,0:T(8,128)(2,1)S(1)} fusion(bf16[576,12,64]{0,2,1:T(8,128)(2,1)} %bitcast.274, f32[12,576,576]{1,2,0:T(8,128)} %get-tuple-element.166, f32[12,576]{1,0:T(8,128)S(1)} %fusion.3, f32[12,576]{1,0:T(8,128)S(1)} %get-tuple-element.165), kind=kOutput, calls=%fused_computation.94 | convolution fusion | flops 521994240 | bytes 17750016 | tf_op jit(solution)/shard_map/while/body/eval_jaxpr/hqk,khd->qhd/dot_general | solution.py:207
  131.9 9.4 %copy.141 = bf16[4,4,2,192,384]{4,2,3,1,0:T(2,128)(2,1)} copy(bf16[4,4,2,192,384]{4,3,2,1,0:T(8,128)(2,1)} %bitcast.268) | data formatting | bytes 9437184 | tf_op jit(solution)/shard_map/reshape | solution.py:83
  141.3 5.7 %copy.163 = bf16[384,8,2,384]{3,1,2,0:T(8,128)(2,1)} copy(bf16[384,8,2,384]{3,2,1,0:T(2,128)(2,1)} %bitcast.251) | data formatting | bytes 9437184
  147.0 14.9 %all-gather.20.cloned.1.call-done = bf16[4,384,1536]{2,1,0:T(8,128)(2,1)} async-done(((bf16[4,48,1536]{2,1,0:T(8,128)(2,1)}), bf16[4,384,1536]{2,1,0:T(8,128)(2,1)}) %all-gather.20.cloned.1.call-update) | async-done | bytes 4718608 | tf_op jit(solution)/shard_map/all_gather | solution.py:82
  161.9 9.4 %copy.140 = bf16[4,4,2,48,1536]{4,2,3,1,0:T(2,128)(2,1)} copy(bf16[4,4,2,48,1536]{4,3,2,1,0:T(8,128)(2,1)} %bitcast.269) | data formatting | bytes 9437184 | tf_op jit(solution)/shard_map/reshape | solution.py:83
  171.3 3.7 copy.162
  175.0 21.1 %multiply_convert_fusion = (bf16[576,3072]{1,0:T(8,128)(2,1)}, f32[576,3072]{1,0:T(8,128)}, f32[576,3072]{1,0:T(8,128)}) fusion(bf16[768,3072]{1,0:T(8,128)(2,1)S(1)} %bitcast.270, f32[576,768]{1,0:T(8,128)S(1)} %copy-done.9, f32[768]{0:T(1024)S(1)} %add.387, f32[768]{0:T(1024)S(1)} %mul.368, f32[576]{0:T(1024)S(1)} %fusion.96, ...), kind=kOutput, calls=%fused_computation.24 | convolution fusion | flops 2835136512 | bytes 24193536 | tf_op jit(solution)/shard_map/dot_general | solution.py:217
  196.2 9.4 %add_convert_fusion = bf16[576,3072]{1,0:T(8,128)(2,1)} fusion(f32[576,3072]{1,0:T(8,128)} %get-tuple-element.134, f32[576,3072]{1,0:T(8,128)} %get-tuple-element.169, bf16[3072,768]{1,0:T(8,128)(2,1)S(1)} %bitcast.267, bf16[576,768]{1,0:T(8,128)(2,1)S(1)} %copy-done.23, f32[576]{0:T(1024)S(1)} %fusion.94), kind=kOutput, calls=%fused_computation.23 | convolution fusion | flops 2744008704 | bytes 23300352 | tf_op jit(solution)/shard_map/dot_general | solution.py:226
  205.6 5.4 %multiply_reduce_fusion.2 = (f32[768]{0:T(1024)S(1)}, f32[576]{0:T(1024)S(1)}, f32[768]{0:T(1024)S(1)}, f32[576,768]{1,0:T(8,128)S(1)}) fusion(f32[576,768]{1,0:T(8,128)S(1)} %copy-done.9, f32[576]{0:T(1024)S(1)} %fusion.96, f32[576]{0:T(1024)S(1)} %broadcast_multiply_fusion.4, f32[768]{0:T(1024)S(1)} %mul.368, bf16[576,3072]{1,0:T(8,128)(2,1)} %add_convert_fusion, ...), kind=kOutput, calls=%fused_computation.81 | convolution fusion | flops 2721445888 | bytes 11812608 | tf_op jit(solution)/shard_map/dot_general | solution.py:232
  218.2 7.6 %convolution_convert_fusion = bf16[12,576,576]{1,2,0:T(8,128)(2,1)} fusion(bf16[576,12,64]{0,2,1:T(8,128)(2,1)} %bitcast.259, bf16[576,12,64]{0,2,1:T(8,128)(2,1)} %bitcast.275), kind=kOutput, calls=%fused_computation.38 | convolution fusion | flops 513589248 | bytes 9732096 | tf_op jit(solution)/shard_map/while/body/eval_jaxpr/qhd,khd->hqk/dot_general | solution.py:246
  225.8 9.9 %fusion.32 = bf16[12,64,576]{2,1,0:T(8,128)(2,1)} fusion(bf16[576,12,64]{0,2,1:T(8,128)(2,1)S(1)} %bitcast.260, f32[12,576,576]{1,2,0:T(8,128)} %get-tuple-element.166, f32[12,576]{1,0:T(8,128)S(1)} %log_add_fusion), kind=kOutput, calls=%fused_computation.95 | convolution fusion | flops 518012928 | bytes 17722368 | tf_op jit(solution)/shard_map/while/body/eval_jaxpr/hqk,qhd->khd/dot_general | solution.py:245
  235.7 12.0 %fusion = f32[12,576]{1,0:T(8,128)S(1)} fusion(bf16[12,576,576]{1,2,0:T(8,128)(2,1)} %convolution_convert_fusion, f32[12,576,576]{1,2,0:T(8,128)} %get-tuple-element.166, f32[12,576]{1,0:T(8,128)S(1)} %log_add_fusion), kind=kLoop, calls=%fused_computation.7 | loop fusion | flops 15918336 | bytes 23943168 | tf_op jit(solution)/shard_map/while/body/eval_jaxpr/reduce_sum | solution.py:248
  249.3 6.0 %fusion.2 = bf16[12,576,576]{1,2,0:T(8,128)(2,1)} fusion(bf16[12,576,576]{1,2,0:T(8,128)(2,1)S(1)} %copy-done.3, f32[12,576,576]{1,2,0:T(8,128)S(1)} %bitcast.236, f32[12,576]{1,0:T(8,128)S(1)} %fusion, f32[12,576]{1,0:T(8,128)S(1)} %log_add_fusion), kind=kLoop, calls=%fused_computation.9 | loop fusion | flops 19906560 | bytes 31905792 | tf_op jit(solution)/shard_map/while/body/eval_jaxpr/convert_element_type | solution.py:249
  255.4 8.2 %fusion.23 = (f32[576,12]{0,1:T(8,128)S(1)}, f32[12,64,576]{2,1,0:T(8,128)}) fusion(f32[576,12,64]{0,2,1:T(8,128)} %bitcast.246, f32[12,64]{1,0:T(8,128)S(1)} %copy-done.35, f32[576,12]{0,1:T(8,128)S(1)} %broadcast_multiply_fusion, bf16[12,576,576]{1,2,0:T(8,128)(2,1)} %fusion.2, f32[576,12,64]{0,2,1:T(8,128)S(1)} %bitcast.240, f32[12,64]{1,0:T(8,128)S(1)} %mul.354, ...), kind=kOutput, calls=%fused_computation.65 | convolution fusion | flops 513139968 | bytes 13387776 | tf_op jit(solution)/shard_map/while/body/eval_jaxpr/hqk,qhd->khd/dot_general | solution.py:254
  271.4 2.8 fusion.109
  274.2 6.4 %fusion.35 = f32[768,2304]{1,0:T(8,128)} fusion(bf16[576,768]{0,1:T(8,128)(2,1)S(1)} %bitcast.295, bf16[576,768]{0,1:T(8,128)(2,1)S(1)} %bitcast.291, bf16[576,768]{0,1:T(8,128)(2,1)S(1)} %bitcast.293, bf16[576,768]{1,0:T(8,128)(2,1)S(1)} %copy-done.13, f32[768]{0:T(1024)S(1)} %copy-done.45, f32[768]{0:T(1024)S(1)} %copy-done.43, f32[576]{0:T(1024)S(1)} %copy-done.41, ...), kind=kOutput, calls=%fused_computation.99 | convolution fusion | flops 2049048576 | bytes 10627584 | tf_op jit(solution)/shard_map/dot_general | solution.py:272
  281.9 4.2 select_maximum_fusion
  286.1 3.1 copy-done.5
  291.4 6.1 %fusion.107 = f32[768,3072]{1,0:T(8,128)S(1)} fusion(bf16[576,3072]{1,0:T(8,128)(2,1)} %add_convert_fusion, f32[576,768]{1,0:T(8,128)S(1)} %copy-done.10, f32[768]{0:T(1024)S(1)} %add.387, f32[768]{0:T(1024)S(1)} %mul.368, f32[576]{0:T(1024)S(1)} %fusion.96, f32[576]{0:T(1024)S(1)} %broadcast_multiply_fusion.4), kind=kOutput, calls=%fused_computation.243 | convolution fusion | flops 2720120832 | bytes 14756352 | tf_op jit(solution)/shard_map/dot_general | solution.py:229
  299.8 4.1 constant_dynamic-slice_fusion.3
  309.4 2.8 constant_dynamic-slice_fusion.1
  312.3 4.6 collective-permute-done.16
  322.7 8.0 %collective-permute-done.17 = bf16[4,48,1280]{2,1,0:T(8,128)(2,1)S(1)} collective-permute-done((bf16[4,48,1280]{2,1,0:T(8,128)(2,1)S(1)}, bf16[4,48,1280]{2,1,0:T(8,128)(2,1)S(1)}, u32[]{:S(2)}, u32[]{:S(2)}) %collective-permute-start.17) | collective-permute-done | bytes 491552 | tf_op jit(solution)/shard_map/ppermute | solution.py:123
  338.1 3.9 collective-permute-done.19
  344.5 3.1 collective-permute-done.30
  351.4 6.1 %fusion.56 = f32[3072,768]{1,0:T(8,128)S(1)} fusion(bf16[576,3072]{1,0:T(8,128)(2,1)} %get-tuple-element.133, bf16[576,768]{1,0:T(8,128)(2,1)S(1)} %copy-done.24, f32[576]{0:T(1024)S(1)} %fusion.94), kind=kOutput, calls=%fused_computation.134 | convolution fusion | flops 2719236096 | bytes 13863168 | tf_op jit(solution)/shard_map/dot_general | solution.py:225
  357.5 3.6 copy-done.19
  370.3 7.2 %collective-permute-done.33 = bf16[48,1536]{1,0:T(8,128)(2,1)S(1)} collective-permute-done((bf16[48,1536]{1,0:T(8,128)(2,1)S(1)}, bf16[48,1536]{1,0:T(8,128)(2,1)S(1)}, u32[]{:S(2)}, u32[]{:S(2)}) %collective-permute-start.33) | collective-permute-done | bytes 147488 | tf_op jit(solution)/shard_map/ppermute | solution.py:129
  379.9 2.6 constant_dynamic-slice_fusion
  386.1 13.8 %collective-permute-done.37 = bf16[4,192,384]{2,1,0:T(8,128)(2,1)S(1)} collective-permute-done((bf16[4,192,384]{2,1,0:T(8,128)(2,1)S(1)}, bf16[4,192,384]{2,1,0:T(8,128)(2,1)S(1)}, u32[]{:S(2)}, u32[]{:S(2)}) %collective-permute-start.37) | collective-permute-done | bytes 589856 | tf_op jit(solution)/shard_map/ppermute | solution.py:116
  401.6 15.4 %collective-permute-done.38 = bf16[4,192,384]{2,1,0:T(8,128)(2,1)S(1)} collective-permute-done((bf16[4,192,384]{2,1,0:T(8,128)(2,1)S(1)}, bf16[4,192,384]{2,1,0:T(8,128)(2,1)S(1)}, u32[]{:S(2)}, u32[]{:S(2)}) %collective-permute-start.38) | collective-permute-done | bytes 589856 | tf_op jit(solution)/shard_map/ppermute | solution.py:123
  417.3 3.3 collective-permute-start.40
  426.1 5.1 %collective-permute-done.42 = bf16[192,384]{1,0:T(8,128)(2,1)S(1)} collective-permute-done((bf16[192,384]{1,0:T(8,128)(2,1)S(1)}, bf16[192,384]{1,0:T(8,128)(2,1)S(1)}, u32[]{:S(2)}, u32[]{:S(2)}) %collective-permute-start.42) | collective-permute-done | bytes 147488 | tf_op jit(solution)/shard_map/ppermute | solution.py:129
  440.7 6.5 %multiply_convert_fusion.3 = bf16[576,768]{1,0:T(8,128)(2,1)} fusion(f32[576,768]{1,0:T(8,128)S(1)} %copy-done.10, bf16[576,3072]{1,0:T(8,128)(2,1)S(1)} %copy-done.51, bf16[3072,768]{1,0:T(8,128)(2,1)} %bitcast.264, f32[576]{0:T(1024)S(1)} %fusion.94), kind=kOutput, calls=%fused_computation.87 | convolution fusion | flops 2719236096 | bytes 10914048 | tf_op jit(solution)/shard_map/dot_general | solution.py:220
  450.2 3.7 collective-permute-done.24
  462.1 10.9 %all-gather.5 = f32[384,384]{1,0:T(8,128)S(1)} all-gather(f32[48,384]{1,0:T(8,128)S(1)} %fusion.88), channel_id=7, replica_groups=mesh['dp'=8,'fsdp'=4] {'dp'}, dimensions={0}, use_global_device_ids=true | all-gather | bytes 663552 | tf_op jit(solution)/shard_map/all_gather | solution.py:132
  474.1 3.1 copy.148
  480.7 3.5 copy.150
  486.0 3.5 copy.151
  (339 shorter events, 163.3 us)
Async XLA Ops:
  7.2 62.2 %all-gather.18.cloned.1.call-start = ((), (), s32[]{:S(2)}) async-start(), calls=%async_computation.1 | async-start | bytes 1327104 | tf_op jit(solution)/shard_map/all_gather | solution.py:82
  8.0 5.4 %collective-permute-start.7 = (bf16[48,384]{1,0:T(8,128)(2,1)S(1)}, bf16[48,384]{1,0:T(8,128)(2,1)S(1)}, u32[]{:S(2)}, u32[]{:S(2)}) collective-permute-start(bf16[48,384]{1,0:T(8,128)(2,1)S(1)} %dynamic_slice.164), channel_id=1, source_target_pairs={{0,2},{1,3},{2,0},{3,1},{4,6},{5,7},{6,4},{7,5},{8,10},{9,11},{10,... | collective-permute-start | bytes 110600 | tf_op jit(solution)/shard_map/ppermute | solution.py:70
  10.6 4.0 collective-permute-start.6
  15.9 63.6 %all-gather.16.cloned.1.call-start = ((), (), s32[]{:S(2)}) async-start(), calls=%async_computation | async-start | bytes 3981312 | tf_op jit(solution)/shard_map/all_gather | solution.py:82
  16.8 10.1 %collective-permute-start.4 = (bf16[48,1152]{1,0:T(8,128)(2,1)S(1)}, bf16[48,1152]{1,0:T(8,128)(2,1)S(1)}, u32[]{:S(2)}, u32[]{:S(2)}) collective-permute-start(bf16[48,1152]{1,0:T(8,128)(2,1)S(1)} %dynamic_slice.163), channel_id=1, source_target_pairs={{0,2},{1,3},{2,0},{3,1},{4,6},{5,7},{6,4},{7,5},{8,10},{9,11},{10,... | collective-permute-start | bytes 331784 | tf_op jit(solution)/shard_map/ppermute | solution.py:70
  21.5 6.6 %collective-permute-start.3 = (bf16[48,1152]{1,0:T(8,128)(2,1)S(1)}, bf16[48,1152]{1,0:T(8,128)(2,1)S(1)}, u32[]{:S(2)}, u32[]{:S(2)}) collective-permute-start(bf16[48,1152]{1,0:T(8,128)(2,1)S(1)} %dynamic_slice.163), channel_id=1, source_target_pairs={{0,1},{1,2},{2,3},{3,0},{4,5},{5,6},{6,7},{7,4},{8,9},{9,10},{10,1... | collective-permute-start | bytes 331784 | tf_op jit(solution)/shard_map/ppermute | solution.py:70
  21.5 7.6 %collective-permute-start.5 = (bf16[48,1152]{1,0:T(8,128)(2,1)S(1)}, bf16[48,1152]{1,0:T(8,128)(2,1)S(1)}, u32[]{:S(2)}, u32[]{:S(2)}) collective-permute-start(bf16[48,1152]{1,0:T(8,128)(2,1)S(1)} %dynamic_slice.163), channel_id=1, source_target_pairs={{0,3},{1,0},{2,1},{3,2},{4,7},{5,4},{6,5},{7,6},{8,11},{9,8},{10,9... | collective-permute-start | bytes 331784 | tf_op jit(solution)/shard_map/ppermute | solution.py:70
  30.6 101.3 %all-gather.22.cloned.1.call-start = ((), (), s32[]{:S(2)}) async-start(), calls=%async_computation.3 | async-start | bytes 5308416 | tf_op jit(solution)/shard_map/all_gather | solution.py:82
  31.6 10.2 %collective-permute-start.13 = (bf16[192,384]{1,0:T(8,128)(2,1)S(1)}, bf16[192,384]{1,0:T(8,128)(2,1)S(1)}, u32[]{:S(2)}, u32[]{:S(2)}) collective-permute-start(bf16[192,384]{1,0:T(8,128)(2,1)S(1)} %dynamic_slice.166), channel_id=1, source_target_pairs={{0,2},{1,3},{2,0},{3,1},{4,6},{5,7},{6,4},{7,5},{8,10},{9,11},{10,... | collective-permute-start | bytes 442376 | tf_op jit(solution)/shard_map/ppermute | solution.py:70
  32.9 11.0 %collective-permute-start.12 = (bf16[192,384]{1,0:T(8,128)(2,1)S(1)}, bf16[192,384]{1,0:T(8,128)(2,1)S(1)}, u32[]{:S(2)}, u32[]{:S(2)}) collective-permute-start(bf16[192,384]{1,0:T(8,128)(2,1)S(1)} %dynamic_slice.166), channel_id=1, source_target_pairs={{0,1},{1,2},{2,3},{3,0},{4,5},{5,6},{6,7},{7,4},{8,9},{9,10},{10,1... | collective-permute-start | bytes 442376 | tf_op jit(solution)/shard_map/ppermute | solution.py:70
  33.8 11.5 %collective-permute-start.14 = (bf16[192,384]{1,0:T(8,128)(2,1)S(1)}, bf16[192,384]{1,0:T(8,128)(2,1)S(1)}, u32[]{:S(2)}, u32[]{:S(2)}) collective-permute-start(bf16[192,384]{1,0:T(8,128)(2,1)S(1)} %dynamic_slice.166), channel_id=1, source_target_pairs={{0,3},{1,0},{2,1},{3,2},{4,7},{5,4},{6,5},{7,6},{8,11},{9,8},{10,9... | collective-permute-start | bytes 442376 | tf_op jit(solution)/shard_map/ppermute | solution.py:70
  46.9 115.0 %all-gather.20.cloned.1.call-start = ((), (), s32[]{:S(2)}) async-start(), calls=%async_computation.2 | async-start | bytes 5308416 | tf_op jit(solution)/shard_map/all_gather | solution.py:82
  47.0 11.6 %collective-permute-start.1 = (bf16[6,192]{1,0:T(8,128)(2,1)S(1)}, bf16[6,192]{1,0:T(8,128)(2,1)S(1)}, u32[]{:S(2)}, u32[]{:S(2)}) collective-permute-start(bf16[6,192]{1,0:T(8,128)(2,1)S(1)} %get-tuple-element.164), channel_id=1, source_target_pairs={{0,2},{1,3},{2,0},{3,1},{4,6},{5,7},{6,4},{7,5},{8,10},{9,11},{10,... | collective-permute-start | bytes 6920 | tf_op jit(solution)/shard_map/ppermute | solution.py:70
  47.1 12.2 %collective-permute-start = (bf16[6,192]{1,0:T(8,128)(2,1)S(1)}, bf16[6,192]{1,0:T(8,128)(2,1)S(1)}, u32[]{:S(2)}, u32[]{:S(2)}) collective-permute-start(bf16[6,192]{1,0:T(8,128)(2,1)S(1)} %get-tuple-element.164), channel_id=1, source_target_pairs={{0,1},{1,2},{2,3},{3,0},{4,5},{5,6},{6,7},{7,4},{8,9},{9,10},{10,1... | collective-permute-start | bytes 6920 | tf_op jit(solution)/shard_map/ppermute | solution.py:70
  48.4 10.8 %collective-permute-start.2 = (bf16[6,192]{1,0:T(8,128)(2,1)S(1)}, bf16[6,192]{1,0:T(8,128)(2,1)S(1)}, u32[]{:S(2)}, u32[]{:S(2)}) collective-permute-start(bf16[6,192]{1,0:T(8,128)(2,1)S(1)} %get-tuple-element.164), channel_id=1, source_target_pairs={{0,3},{1,0},{2,1},{3,2},{4,7},{5,4},{6,5},{7,6},{8,11},{9,8},{10,9... | collective-permute-start | bytes 6920 | tf_op jit(solution)/shard_map/ppermute | solution.py:70
  50.5 9.4 %collective-permute-start.10 = (bf16[48,1536]{1,0:T(8,128)(2,1)S(1)}, bf16[48,1536]{1,0:T(8,128)(2,1)S(1)}, u32[]{:S(2)}, u32[]{:S(2)}) collective-permute-start(bf16[48,1536]{1,0:T(8,128)(2,1)S(1)} %dynamic_slice.165), channel_id=1, source_target_pairs={{0,2},{1,3},{2,0},{3,1},{4,6},{5,7},{6,4},{7,5},{8,10},{9,11},{10,... | collective-permute-start | bytes 442376 | tf_op jit(solution)/shard_map/ppermute | solution.py:70
  53.0 11.0 %collective-permute-start.9 = (bf16[48,1536]{1,0:T(8,128)(2,1)S(1)}, bf16[48,1536]{1,0:T(8,128)(2,1)S(1)}, u32[]{:S(2)}, u32[]{:S(2)}) collective-permute-start(bf16[48,1536]{1,0:T(8,128)(2,1)S(1)} %dynamic_slice.165), channel_id=1, source_target_pairs={{0,1},{1,2},{2,3},{3,0},{4,5},{5,6},{6,7},{7,4},{8,9},{9,10},{10,1... | collective-permute-start | bytes 442376 | tf_op jit(solution)/shard_map/ppermute | solution.py:70
  58.6 7.0 %collective-permute-start.11 = (bf16[48,1536]{1,0:T(8,128)(2,1)S(1)}, bf16[48,1536]{1,0:T(8,128)(2,1)S(1)}, u32[]{:S(2)}, u32[]{:S(2)}) collective-permute-start(bf16[48,1536]{1,0:T(8,128)(2,1)S(1)} %dynamic_slice.165), channel_id=1, source_target_pairs={{0,3},{1,0},{2,1},{3,2},{4,7},{5,4},{6,5},{7,6},{8,11},{9,8},{10,9... | collective-permute-start | bytes 442376 | tf_op jit(solution)/shard_map/ppermute | solution.py:70
  67.1 407.0 %all-gather.24.cloned.1.call-start = ((), (), s32[]{:S(2)}) async-start(), calls=%async_computation.4 | async-start | bytes 2211840 | tf_op jit(solution)/shard_map/all_gather | solution.py:132
  290.8 13.1 %collective-permute-start.15 = (bf16[4,4,48,1280]{3,2,1,0:T(8,128)(2,1)}, bf16[4,4,48,1280]{3,2,1,0:T(8,128)(2,1)}, u32[]{:S(2)}, u32[]{:S(2)}) collective-permute-start(bf16[4,4,48,1280]{3,2,1,0:T(8,128)(2,1)} %bitcast.49), channel_id=1, source_target_pairs={{0,4},{4,0},{8,12},{12,8},{16,20},{20,16},{24,28},{28,24},{1,5},{5... | collective-permute-start | bytes 5898248 | tf_op jit(solution)/shard_map/ppermute | solution.py:110
  299.6 20.7 %collective-permute-start.29 = (bf16[4,4,48,1536]{3,2,1,0:T(8,128)(2,1)}, bf16[4,4,48,1536]{3,2,1,0:T(8,128)(2,1)}, u32[]{:S(2)}, u32[]{:S(2)}) collective-permute-start(bf16[4,4,48,1536]{3,2,1,0:T(8,128)(2,1)} %bitcast.74), channel_id=1, source_target_pairs={{0,4},{4,0},{8,12},{12,8},{16,20},{20,16},{24,28},{28,24},{1,5},{5... | collective-permute-start | bytes 7077896 | tf_op jit(solution)/shard_map/ppermute | solution.py:110
  307.9 9.0 %collective-permute-start.16 = (bf16[4,48,1280]{2,1,0:T(8,128)(2,1)S(1)}, bf16[4,48,1280]{2,1,0:T(8,128)(2,1)}, u32[]{:S(2)}, u32[]{:S(2)}) collective-permute-start(bf16[4,48,1280]{2,1,0:T(8,128)(2,1)S(1)} %fusion.55), channel_id=1, source_target_pairs={{0,8},{4,20},{8,0},{12,28},{16,24},{20,4},{24,16},{28,12},{1,9},{5... | collective-permute-start | bytes 1474568 | tf_op jit(solution)/shard_map/ppermute | solution.py:116
  318.2 12.6 %collective-permute-start.17 = (bf16[4,48,1280]{2,1,0:T(8,128)(2,1)S(1)}, bf16[4,48,1280]{2,1,0:T(8,128)(2,1)S(1)}, u32[]{:S(2)}, u32[]{:S(2)}) collective-permute-start(bf16[4,48,1280]{2,1,0:T(8,128)(2,1)S(1)} %get-tuple-element.141), channel_id=1, source_target_pairs={{0,8},{4,12},{8,0},{12,4},{16,24},{20,28},{24,16},{28,20},{1,9},{5... | collective-permute-start | bytes 1474568 | tf_op jit(solution)/shard_map/ppermute | solution.py:123
  319.7 12.2 %collective-permute-start.18 = (bf16[4,48,1280]{2,1,0:T(8,128)(2,1)S(1)}, bf16[4,48,1280]{2,1,0:T(8,128)(2,1)S(1)}, u32[]{:S(2)}, u32[]{:S(2)}) collective-permute-start(bf16[4,48,1280]{2,1,0:T(8,128)(2,1)S(1)} %get-tuple-element.142), channel_id=1, source_target_pairs={{0,16},{4,20},{8,24},{12,28},{16,0},{20,4},{24,8},{28,12},{1,17},{... | collective-permute-start | bytes 1474568 | tf_op jit(solution)/shard_map/ppermute | solution.py:124
  332.1 9.9 %collective-permute-start.19 = (bf16[48,1280]{1,0:T(8,128)(2,1)S(1)}, bf16[48,1280]{1,0:T(8,128)(2,1)S(1)}, u32[]{:S(2)}, u32[]{:S(2)}) collective-permute-start(bf16[48,1280]{1,0:T(8,128)(2,1)S(1)} %get-tuple-element.151), channel_id=1, source_target_pairs={{0,1},{1,2},{2,3},{3,0},{4,5},{5,6},{6,7},{7,4},{8,9},{9,10},{10,1... | collective-permute-start | bytes 368648 | tf_op jit(solution)/shard_map/ppermute | solution.py:129
  333.7 9.5 %collective-permute-start.21 = (bf16[48,1280]{1,0:T(8,128)(2,1)S(1)}, bf16[48,1280]{1,0:T(8,128)(2,1)S(1)}, u32[]{:S(2)}, u32[]{:S(2)}) collective-permute-start(bf16[48,1280]{1,0:T(8,128)(2,1)S(1)} %get-tuple-element.152), channel_id=1, source_target_pairs={{0,3},{1,0},{2,1},{3,2},{4,7},{5,4},{6,5},{7,6},{8,11},{9,8},{10,9... | collective-permute-start | bytes 368648 | tf_op jit(solution)/shard_map/ppermute | solution.py:129
  334.2 9.1 %collective-permute-start.20 = (bf16[48,1280]{1,0:T(8,128)(2,1)S(1)}, bf16[48,1280]{1,0:T(8,128)(2,1)S(1)}, u32[]{:S(2)}, u32[]{:S(2)}) collective-permute-start(bf16[48,1280]{1,0:T(8,128)(2,1)S(1)} %get-tuple-element.153), channel_id=1, source_target_pairs={{0,2},{1,3},{2,0},{3,1},{4,6},{5,7},{6,4},{7,5},{8,10},{9,11},{10,... | collective-permute-start | bytes 368648 | tf_op jit(solution)/shard_map/ppermute | solution.py:129
  337.5 10.1 %collective-permute-start.30 = (bf16[4,48,1536]{2,1,0:T(8,128)(2,1)}, bf16[4,48,1536]{2,1,0:T(8,128)(2,1)S(1)}, u32[]{:S(2)}, u32[]{:S(2)}) collective-permute-start(bf16[4,48,1536]{2,1,0:T(8,128)(2,1)} %fusion.53), channel_id=1, source_target_pairs={{0,8},{4,20},{8,0},{12,28},{16,24},{20,4},{24,16},{28,12},{1,9},{5... | collective-permute-start | bytes 1769480 | tf_op jit(solution)/shard_map/ppermute | solution.py:116
  344.1 136.7 %all-gather.26.cloned.1.call-start = ((), (), s32[]{:S(2)}) async-start(), calls=%async_computation.5 | async-start | bytes 2654208 | tf_op jit(solution)/shard_map/all_gather | solution.py:132
  349.5 14.5 %collective-permute-start.31 = (bf16[4,48,1536]{2,1,0:T(8,128)(2,1)S(1)}, bf16[4,48,1536]{2,1,0:T(8,128)(2,1)S(1)}, u32[]{:S(2)}, u32[]{:S(2)}) collective-permute-start(bf16[4,48,1536]{2,1,0:T(8,128)(2,1)S(1)} %get-tuple-element.137), channel_id=1, source_target_pairs={{0,8},{4,12},{8,0},{12,4},{16,24},{20,28},{24,16},{28,20},{1,9},{5... | collective-permute-start | bytes 1769480 | tf_op jit(solution)/shard_map/ppermute | solution.py:123
  350.2 14.2 %collective-permute-start.32 = (bf16[4,48,1536]{2,1,0:T(8,128)(2,1)S(1)}, bf16[4,48,1536]{2,1,0:T(8,128)(2,1)S(1)}, u32[]{:S(2)}, u32[]{:S(2)}) collective-permute-start(bf16[4,48,1536]{2,1,0:T(8,128)(2,1)S(1)} %get-tuple-element.138), channel_id=1, source_target_pairs={{0,16},{4,20},{8,24},{12,28},{16,0},{20,4},{24,8},{28,12},{1,17},{... | collective-permute-start | bytes 1769480 | tf_op jit(solution)/shard_map/ppermute | solution.py:124
  362.8 19.8 %collective-permute-start.36 = (bf16[4,4,192,384]{3,2,1,0:T(8,128)(2,1)}, bf16[4,4,192,384]{3,2,1,0:T(8,128)(2,1)}, u32[]{:S(2)}, u32[]{:S(2)}) collective-permute-start(bf16[4,4,192,384]{3,2,1,0:T(8,128)(2,1)} %bitcast.86), channel_id=1, source_target_pairs={{0,4},{4,0},{8,12},{12,8},{16,20},{20,16},{24,28},{28,24},{1,5},{5... | collective-permute-start | bytes 7077896 | tf_op jit(solution)/shard_map/ppermute | solution.py:110
  365.9 11.6 %collective-permute-start.33 = (bf16[48,1536]{1,0:T(8,128)(2,1)S(1)}, bf16[48,1536]{1,0:T(8,128)(2,1)S(1)}, u32[]{:S(2)}, u32[]{:S(2)}) collective-permute-start(bf16[48,1536]{1,0:T(8,128)(2,1)S(1)} %get-tuple-element.148), channel_id=1, source_target_pairs={{0,1},{1,2},{2,3},{3,0},{4,5},{5,6},{6,7},{7,4},{8,9},{9,10},{10,1... | collective-permute-start | bytes 442376 | tf_op jit(solution)/shard_map/ppermute | solution.py:129
  367.3 11.5 %collective-permute-start.35 = (bf16[48,1536]{1,0:T(8,128)(2,1)S(1)}, bf16[48,1536]{1,0:T(8,128)(2,1)S(1)}, u32[]{:S(2)}, u32[]{:S(2)}) collective-permute-start(bf16[48,1536]{1,0:T(8,128)(2,1)S(1)} %get-tuple-element.149), channel_id=1, source_target_pairs={{0,3},{1,0},{2,1},{3,2},{4,7},{5,4},{6,5},{7,6},{8,11},{9,8},{10,9... | collective-permute-start | bytes 442376 | tf_op jit(solution)/shard_map/ppermute | solution.py:129
  368.0 11.1 %collective-permute-start.34 = (bf16[48,1536]{1,0:T(8,128)(2,1)S(1)}, bf16[48,1536]{1,0:T(8,128)(2,1)S(1)}, u32[]{:S(2)}, u32[]{:S(2)}) collective-permute-start(bf16[48,1536]{1,0:T(8,128)(2,1)S(1)} %get-tuple-element.150), channel_id=1, source_target_pairs={{0,2},{1,3},{2,0},{3,1},{4,6},{5,7},{6,4},{7,5},{8,10},{9,11},{10,... | collective-permute-start | bytes 442376 | tf_op jit(solution)/shard_map/ppermute | solution.py:129
  379.9 106.2 %all-gather.28.cloned.1.call-start = ((), (), s32[]{:S(2)}) async-start(), calls=%async_computation.6 | async-start | bytes 2654208 | tf_op jit(solution)/shard_map/all_gather | solution.py:132
  385.0 15.0 %collective-permute-start.37 = (bf16[4,192,384]{2,1,0:T(8,128)(2,1)S(1)}, bf16[4,192,384]{2,1,0:T(8,128)(2,1)S(1)}, u32[]{:S(2)}, u32[]{:S(2)}) collective-permute-start(bf16[4,192,384]{2,1,0:T(8,128)(2,1)S(1)} %fusion.54), channel_id=1, source_target_pairs={{0,8},{4,20},{8,0},{12,28},{16,24},{20,4},{24,16},{28,12},{1,9},{5... | collective-permute-start | bytes 1769480 | tf_op jit(solution)/shard_map/ppermute | solution.py:116
  400.2 16.8 %collective-permute-start.38 = (bf16[4,192,384]{2,1,0:T(8,128)(2,1)S(1)}, bf16[4,192,384]{2,1,0:T(8,128)(2,1)S(1)}, u32[]{:S(2)}, u32[]{:S(2)}) collective-permute-start(bf16[4,192,384]{2,1,0:T(8,128)(2,1)S(1)} %get-tuple-element.135), channel_id=1, source_target_pairs={{0,8},{4,12},{8,0},{12,4},{16,24},{20,28},{24,16},{28,20},{1,9},{5... | collective-permute-start | bytes 1769480 | tf_op jit(solution)/shard_map/ppermute | solution.py:123
  401.6 15.4 %collective-permute-start.39 = (bf16[4,192,384]{2,1,0:T(8,128)(2,1)S(1)}, bf16[4,192,384]{2,1,0:T(8,128)(2,1)S(1)}, u32[]{:S(2)}, u32[]{:S(2)}) collective-permute-start(bf16[4,192,384]{2,1,0:T(8,128)(2,1)S(1)} %get-tuple-element.136), channel_id=1, source_target_pairs={{0,16},{4,20},{8,24},{12,28},{16,0},{20,4},{24,8},{28,12},{1,17},{... | collective-permute-start | bytes 1769480 | tf_op jit(solution)/shard_map/ppermute | solution.py:124
  417.3 8.8 %collective-permute-start.40 = (bf16[192,384]{1,0:T(8,128)(2,1)S(1)}, bf16[192,384]{1,0:T(8,128)(2,1)S(1)}, u32[]{:S(2)}, u32[]{:S(2)}) collective-permute-start(bf16[192,384]{1,0:T(8,128)(2,1)S(1)} %get-tuple-element.145), channel_id=1, source_target_pairs={{0,1},{1,2},{2,3},{3,0},{4,5},{5,6},{6,7},{7,4},{8,9},{9,10},{10,1... | collective-permute-start | bytes 442376 | tf_op jit(solution)/shard_map/ppermute | solution.py:129
  420.7 10.5 %collective-permute-start.42 = (bf16[192,384]{1,0:T(8,128)(2,1)S(1)}, bf16[192,384]{1,0:T(8,128)(2,1)S(1)}, u32[]{:S(2)}, u32[]{:S(2)}) collective-permute-start(bf16[192,384]{1,0:T(8,128)(2,1)S(1)} %get-tuple-element.146), channel_id=1, source_target_pairs={{0,3},{1,0},{2,1},{3,2},{4,7},{5,4},{6,5},{7,6},{8,11},{9,8},{10,9... | collective-permute-start | bytes 442376 | tf_op jit(solution)/shard_map/ppermute | solution.py:129
  422.6 11.1 %collective-permute-start.41 = (bf16[192,384]{1,0:T(8,128)(2,1)S(1)}, bf16[192,384]{1,0:T(8,128)(2,1)S(1)}, u32[]{:S(2)}, u32[]{:S(2)}) collective-permute-start(bf16[192,384]{1,0:T(8,128)(2,1)S(1)} %get-tuple-element.147), channel_id=1, source_target_pairs={{0,2},{1,3},{2,0},{3,1},{4,6},{5,7},{6,4},{7,5},{8,10},{9,11},{10,... | collective-permute-start | bytes 442376 | tf_op jit(solution)/shard_map/ppermute | solution.py:129
  439.4 7.8 %collective-permute-start.23 = (bf16[4,48,384]{2,1,0:T(8,128)(2,1)S(1)}, bf16[4,48,384]{2,1,0:T(8,128)(2,1)S(1)}, u32[]{:S(2)}, u32[]{:S(2)}) collective-permute-start(bf16[4,48,384]{2,1,0:T(8,128)(2,1)S(1)} %fusion.75), channel_id=1, source_target_pairs={{0,8},{4,20},{8,0},{12,28},{16,24},{20,4},{24,16},{28,12},{1,9},{5... | collective-permute-start | bytes 442376 | tf_op jit(solution)/shard_map/ppermute | solution.py:116
  447.2 6.6 %collective-permute-start.24 = (bf16[4,48,384]{2,1,0:T(8,128)(2,1)S(1)}, bf16[4,48,384]{2,1,0:T(8,128)(2,1)S(1)}, u32[]{:S(2)}, u32[]{:S(2)}) collective-permute-start(bf16[4,48,384]{2,1,0:T(8,128)(2,1)S(1)} %get-tuple-element.143), channel_id=1, source_target_pairs={{0,8},{4,12},{8,0},{12,4},{16,24},{20,28},{24,16},{28,20},{1,9},{5... | collective-permute-start | bytes 442376 | tf_op jit(solution)/shard_map/ppermute | solution.py:123
  448.0 5.9 %collective-permute-start.25 = (bf16[4,48,384]{2,1,0:T(8,128)(2,1)S(1)}, bf16[4,48,384]{2,1,0:T(8,128)(2,1)S(1)}, u32[]{:S(2)}, u32[]{:S(2)}) collective-permute-start(bf16[4,48,384]{2,1,0:T(8,128)(2,1)S(1)} %get-tuple-element.144), channel_id=1, source_target_pairs={{0,16},{4,20},{8,24},{12,28},{16,0},{20,4},{24,8},{28,12},{1,17},{... | collective-permute-start | bytes 442376 | tf_op jit(solution)/shard_map/ppermute | solution.py:124
  454.0 7.3 %collective-permute-start.26 = (bf16[48,384]{1,0:T(8,128)(2,1)S(1)}, bf16[48,384]{1,0:T(8,128)(2,1)S(1)}, u32[]{:S(2)}, u32[]{:S(2)}) collective-permute-start(bf16[48,384]{1,0:T(8,128)(2,1)S(1)} %get-tuple-element.154), channel_id=1, source_target_pairs={{0,1},{1,2},{2,3},{3,0},{4,5},{5,6},{6,7},{7,4},{8,9},{9,10},{10,1... | collective-permute-start | bytes 110600 | tf_op jit(solution)/shard_map/ppermute | solution.py:129
  454.7 6.6 %collective-permute-start.28 = (bf16[48,384]{1,0:T(8,128)(2,1)S(1)}, bf16[48,384]{1,0:T(8,128)(2,1)S(1)}, u32[]{:S(2)}, u32[]{:S(2)}) collective-permute-start(bf16[48,384]{1,0:T(8,128)(2,1)S(1)} %get-tuple-element.155), channel_id=1, source_target_pairs={{0,3},{1,0},{2,1},{3,2},{4,7},{5,4},{6,5},{7,6},{8,11},{9,8},{10,9... | collective-permute-start | bytes 110600 | tf_op jit(solution)/shard_map/ppermute | solution.py:129
  457.1 5.0 collective-permute-start.27
  (61 other events, 585.1 us)
Sparse Core Ops, SparseCore 0:
  16.0 27.0 all-gather.17
  45.6 33.8 all-gather.15
  81.9 38.7 all-gather.21
  123.1 38.8 all-gather.19
  344.2 30.6 all-gather.23
  380.0 35.3 all-gather.25
  434.7 29.6 all-gather.27

commit v8 on v7

--- a/solution.py
+++ b/solution.py
@@ -80,7 +80,8 @@
     piece = lax.dynamic_slice(m, (j * rows, c * cols), (rows, cols))
     z = _z_gather(piece)
     x = lax.all_gather(z, "dp", axis=1, tiled=False)
-    x = x.reshape(NF_FAST, NDP_FAST // 2, 2, rows, cols).transpose(0, 1, 3, 2, 4)
+    x = x.reshape(NF_FAST, NDP_FAST // 2, 2, rows, cols)
+    x = jnp.concatenate([x[:, :, 0], x[:, :, 1]], axis=-1)
     return x.reshape(NF_FAST * m.shape[0], m.shape[1])
 
 
@@ -130,7 +131,8 @@
             part.astype(jnp.bfloat16), "fsdp", [(i, (i + k) % NF_FAST) for i in range(NF_FAST)]
         ).astype(jnp.float32)
     x = lax.all_gather(total, "dp", axis=0, tiled=False)
-    x = x.reshape(n_chips, 2, rows, cols).transpose(0, 2, 1, 3)
+    x = x.reshape(n_chips, 2, rows, cols)
+    x = jnp.concatenate([x[:, 0], x[:, 1]], axis=-1)
     return x.reshape(n_chips * rows, 2 * cols)
 
 

time: 507 us -> 486 us (0.959)
  local copies, waits for them, and re-layouts: 115 us -> 80.8 us
  waiting for transfers between devices: 119 us -> 130 us
  other arithmetic: 61.2 us -> 67.4 us
    reshape x7 -> x0, local copies, waits for them, and re-layouts: 33.3 us -> none  [the longest x4 26 us: _gather_matrix(): x.reshape(NF_FAST, NDP_FAST // 2, 2, rows, cols).transpose(0, 1, 3, 2, 4)]
    slice x1 -> x8, local copies, waits for them, and re-layouts: 1.32 us -> 18.5 us  [the longest x4 13.1 us: _gather_matrix(): x = jnp.concatenate([x[:, :, 0], x[:, :, 1]], axis=-1)]
    all_gather x4, waiting for transfers between devices: 21.5 us -> 37.1 us  [_gather_matrix(): x = lax.all_gather(z, 'dp', axis=1, tiled=False)]
    unnamed x129 -> x137, local copies, waits for them, and re-layouts: 35.6 us -> 20.3 us
    concatenate x0 -> x4, other arithmetic: none -> 5.35 us  [_reduce_matrix(): x = jnp.concatenate([x[:, 0], x[:, 1]], axis=-1)]
  transfers between devices with their start and end apart: 50 -> 50, of which waited for: 32 -> 30; matrix products, arithmetic and copies ran while one was open for 30% -> 27% of each run, Pallas kernels for 0% -> 0%
where the time goes in v8:
time: 486 us; the launch traced here: 477 us
  waiting for transfers between devices  130 us (27%)
  matrix products  115 us (24%)
  local copies, waits for them, and re-layouts  80.8 us (17%)
  other arithmetic  67.4 us (14%)
  starting transfers between devices  57.9 us (12%)
  between operations  15.7 us (3%)
  blocking collectives  11 us (2%)
    all_gather x4, waiting for transfers between devices, _gather_matrix(): x = lax.all_gather(z, 'dp', axis=1, tiled=False)  37.1 us
    ppermute x4, waiting for transfers between devices, _reduce_matrix(): lax.ppermute(to_x.astype(jnp.bfloat16), 'dp', [(i, i ^ 2) for i in range(...  29.3 us
    ppermute x15, starting transfers between devices, _z_gather(): lax.ppermute(piece, 'fsdp', [(i, (i + k) % NF_FAST) for i in range(NF_FAS...  22.6 us
    dot_general x1, matrix products, on_device(): up_pre = jnp.dot(second_low, full_up, preferred_element_type=jnp.float32)  22.1 us
    ppermute x12, starting transfers between devices, _reduce_matrix(): lax.ppermute(part.astype(jnp.bfloat16), 'fsdp', [(i, (i + k) % NF_FAST) f...  21.7 us
    ppermute x4, waiting for transfers between devices, _reduce_matrix(): lax.ppermute(of_chip(j ^ 3).astype(jnp.bfloat16), 'dp', [(i, i ^ 2) if i...  21.2 us
    ppermute x12, waiting for transfers between devices, _reduce_matrix(): lax.ppermute(part.astype(jnp.bfloat16), 'fsdp', [(i, (i + k) % NF_FAST) f...  21 us
    unnamed x137, local copies, waits for them, and re-layouts  20.3 us
  transfers between devices with their start and end apart: 50, of which 30 were waited for; matrix products, arithmetic and copies ran while one was open for 27% of the time, Pallas kernels for 0%

profile of v8, /device:TPU:8, one launch (start us, length us, event | category | flops | bytes accessed | tf_op | source)
XLA Modules:
  0.0 476.9 jit_solution(5170234894607616731)
XLA Ops:
  8.0 2.6 collective-permute-start.7
  16.8 4.7 collective-permute-start.4
  24.4 2.5 collective-permute-done.4
  35.9 5.9 %collective-permute-done.13 = bf16[192,384]{1,0:T(8,128)(2,1)S(1)} collective-permute-done((bf16[192,384]{1,0:T(8,128)(2,1)S(1)}, bf16[192,384]{1,0:T(8,128)(2,1)S(1)}, u32[]{:S(2)}, u32[]{:S(2)}) %collective-permute-start.13) | collective-permute-done | bytes 147488 | tf_op jit(solution)/shard_map/ppermute | solution.py:70
  50.5 2.5 collective-permute-start.10
  53.0 2.8 collective-permute-start.9
  62.5 3.0 collective-permute-done.11
  69.5 9.9 %all-gather.16.cloned.1.call-done = bf16[4,384,1152]{2,1,0:T(8,128)(2,1)} async-done(((bf16[4,48,1152]{2,1,0:T(8,128)(2,1)}), bf16[4,384,1152]{2,1,0:T(8,128)(2,1)}) %all-gather.16.cloned.1.call-update) | async-done | bytes 3538960 | tf_op jit(solution)/shard_map/all_gather | solution.py:82
  88.2 3.7 fusion.119
  99.8 8.4 %fusion.129 = (f32[12,576]{1,0:T(8,128)S(1)}, f32[12,576,576]{1,2,0:T(8,128)}) fusion(f32[576,12,64]{0,2,1:T(8,128)S(1)} %bitcast.234, f32[12,64]{1,0:T(8,128)S(1)} %mul.360, f32[576,12]{0,1:T(8,128)S(1)} %fusion.95, f32[576,12]{0,1:T(8,128)S(1)} %broadcast_multiply_fusion, f32[576,12,64]{0,2,1:T(8,128)S(1)} %bitcast.226, f32[12,64]{1,0:T(8,128)S(1)} %mul.354, ...), kind=kOutput, calls=%fused_computation.274 | convolution fusion | flops 525083904 | bytes 19940352 | tf_op jit(solution)/shard_map/while/body/eval_jaxpr/qhd,khd->hqk/dot_general | solution.py:197
  108.2 8.6 %fusion.3 = f32[12,576]{1,0:T(8,128)S(1)} fusion(f32[12,576,576]{1,2,0:T(8,128)} %get-tuple-element.182, f32[12,576]{1,0:T(8,128)S(1)} %get-tuple-element.181), kind=kLoop, calls=%fused_computation.14 | loop fusion | flops 7955712 | bytes 15980544 | tf_op jit(solution)/shard_map/while/body/eval_jaxpr/reduce_sum | solution.py:207
  116.8 9.8 %fusion.37 = bf16[12,64,576]{2,1,0:T(8,128)(2,1)S(1)} fusion(bf16[576,12,64]{0,2,1:T(8,128)(2,1)} %bitcast.253, f32[12,576,576]{1,2,0:T(8,128)} %get-tuple-element.182, f32[12,576]{1,0:T(8,128)S(1)} %fusion.3, f32[12,576]{1,0:T(8,128)S(1)} %get-tuple-element.181), kind=kOutput, calls=%fused_computation.106 | convolution fusion | flops 521994240 | bytes 17750016 | tf_op jit(solution)/shard_map/while/body/eval_jaxpr/hqk,khd->qhd/dot_general | solution.py:209
  129.3 5.5 %fusion.120 = (bf16[4,4,1,192,384]{4,3,2,1,0:T(8,128)(2,1)}, bf16[4,4,1,192,384]{4,3,2,1,0:T(8,128)(2,1)}) fusion(bf16[4,4,2,192,384]{4,3,2,1,0:T(8,128)(2,1)} %bitcast.243), kind=kLoop, calls=%fused_computation.265 | loop fusion | bytes 9437184 | tf_op jit(solution)/shard_map/slice | solution.py:84
  134.8 27.1 %all-gather.20.cloned.1.call-done = bf16[4,384,1536]{2,1,0:T(8,128)(2,1)} async-done(((bf16[4,48,1536]{2,1,0:T(8,128)(2,1)}), bf16[4,384,1536]{2,1,0:T(8,128)(2,1)}) %all-gather.20.cloned.1.call-update) | async-done | bytes 4718608 | tf_op jit(solution)/shard_map/all_gather | solution.py:82
  161.9 3.0 fusion.121
  164.9 22.1 %multiply_convert_fusion = (bf16[576,3072]{1,0:T(8,128)(2,1)}, f32[576,3072]{1,0:T(8,128)}, f32[576,3072]{1,0:T(8,128)}) fusion(bf16[768,1536]{1,0:T(8,128)(2,1)S(1)} %bitcast.265, bf16[768,1536]{1,0:T(8,128)(2,1)S(1)} %bitcast.263, f32[576,768]{1,0:T(8,128)S(1)} %copy-done.9, f32[768]{0:T(1024)S(1)} %add.387, f32[768]{0:T(1024)S(1)} %mul.368, ...), kind=kOutput, calls=%fused_computation.24 | convolution fusion | flops 2844573696 | bytes 24193536 | tf_op jit(solution)/shard_map/dot_general | solution.py:219
  187.1 8.3 %add_convert_fusion = bf16[576,3072]{1,0:T(8,128)(2,1)S(1)} fusion(f32[576,3072]{1,0:T(8,128)} %get-tuple-element.134, f32[576,3072]{1,0:T(8,128)} %get-tuple-element.185, bf16[3072,384]{1,0:T(8,128)(2,1)S(1)} %bitcast.262, bf16[3072,384]{1,0:T(8,128)(2,1)S(1)} %bitcast.260, bf16[576,768]{1,0:T(8,128)(2,1)S(1)} %copy-done.24, f32[576]{0:T(1024)S(1)} %fusion.96), kind=kOutput, calls=%fused_computation.23 | convolution fusion | flops 2753445888 | bytes 23300352 | tf_op jit(solution)/shard_map/dot_general | solution.py:228
  195.4 3.3 multiply_reduce_fusion.2
  205.9 7.6 %convolution_convert_fusion = bf16[12,576,576]{1,2,0:T(8,128)(2,1)} fusion(bf16[576,12,64]{0,2,1:T(8,128)(2,1)} %bitcast.241, bf16[576,12,64]{0,2,1:T(8,128)(2,1)} %bitcast.254), kind=kOutput, calls=%fused_computation.38 | convolution fusion | flops 513589248 | bytes 9732096 | tf_op jit(solution)/shard_map/while/body/eval_jaxpr/qhd,khd->hqk/dot_general | solution.py:248
  213.5 9.9 %fusion.38 = bf16[12,64,576]{2,1,0:T(8,128)(2,1)} fusion(bf16[576,12,64]{0,2,1:T(8,128)(2,1)S(1)} %bitcast.242, f32[12,576,576]{1,2,0:T(8,128)} %get-tuple-element.182, f32[12,576]{1,0:T(8,128)S(1)} %log_add_fusion), kind=kOutput, calls=%fused_computation.107 | convolution fusion | flops 518012928 | bytes 17722368 | tf_op jit(solution)/shard_map/while/body/eval_jaxpr/hqk,qhd->khd/dot_general | solution.py:247
  223.5 12.8 %fusion = f32[12,576]{1,0:T(8,128)S(1)} fusion(bf16[12,576,576]{1,2,0:T(8,128)(2,1)} %convolution_convert_fusion, f32[12,576,576]{1,2,0:T(8,128)} %get-tuple-element.182, f32[12,576]{1,0:T(8,128)S(1)} %log_add_fusion), kind=kLoop, calls=%fused_computation.7 | loop fusion | flops 15918336 | bytes 23943168 | tf_op jit(solution)/shard_map/while/body/eval_jaxpr/reduce_sum | solution.py:250
  237.1 6.0 %fusion.2 = bf16[12,576,576]{1,2,0:T(8,128)(2,1)} fusion(bf16[12,576,576]{1,2,0:T(8,128)(2,1)S(1)} %copy-done.3, f32[12,576,576]{1,2,0:T(8,128)S(1)} %bitcast.223, f32[12,576]{1,0:T(8,128)S(1)} %fusion, f32[12,576]{1,0:T(8,128)S(1)} %log_add_fusion), kind=kLoop, calls=%fused_computation.9 | loop fusion | flops 19906560 | bytes 31905792 | tf_op jit(solution)/shard_map/while/body/eval_jaxpr/convert_element_type | solution.py:251
  243.2 8.2 %fusion.29 = (f32[576,12]{0,1:T(8,128)S(1)}, f32[12,64,576]{2,1,0:T(8,128)}) fusion(f32[576,12,64]{0,2,1:T(8,128)} %bitcast.233, f32[12,64]{1,0:T(8,128)S(1)} %copy-done.45, f32[576,12]{0,1:T(8,128)S(1)} %broadcast_multiply_fusion, bf16[12,576,576]{1,2,0:T(8,128)(2,1)} %fusion.2, f32[576,12,64]{0,2,1:T(8,128)S(1)} %bitcast.227, f32[12,64]{1,0:T(8,128)S(1)} %mul.354, ...), kind=kOutput, calls=%fused_computation.76 | convolution fusion | flops 513139968 | bytes 13387776 | tf_op jit(solution)/shard_map/while/body/eval_jaxpr/hqk,qhd->khd/dot_general | solution.py:256
  259.2 2.8 fusion.116
  262.0 6.4 %fusion.41 = f32[768,2304]{1,0:T(8,128)} fusion(bf16[576,768]{0,1:T(8,128)(2,1)S(1)} %bitcast.281, bf16[576,768]{0,1:T(8,128)(2,1)S(1)} %bitcast.277, bf16[576,768]{0,1:T(8,128)(2,1)S(1)} %bitcast.279, bf16[576,768]{1,0:T(8,128)(2,1)S(1)} %copy-done.13, f32[768]{0:T(1024)S(1)} %copy-done.55, f32[768]{0:T(1024)S(1)} %copy-done.53, f32[576]{0:T(1024)S(1)} %copy-done.51, ...), kind=kOutput, calls=%fused_computation.111 | convolution fusion | flops 2049048576 | bytes 10627584 | tf_op jit(solution)/shard_map/dot_general | solution.py:274
  269.7 4.2 select_maximum_fusion
  273.9 3.2 copy-done.5
  279.2 6.1 %fusion.115 = f32[768,3072]{1,0:T(8,128)S(1)} fusion(bf16[576,3072]{1,0:T(8,128)(2,1)} %copy-done.23, f32[576,768]{1,0:T(8,128)S(1)} %copy-done.10, f32[768]{0:T(1024)S(1)} %add.387, f32[768]{0:T(1024)S(1)} %mul.368, f32[576]{0:T(1024)S(1)} %fusion.98, f32[576]{0:T(1024)S(1)} %broadcast_multiply_fusion.4), kind=kOutput, calls=%fused_computation.261 | convolution fusion | flops 2720120832 | bytes 14756352 | tf_op jit(solution)/shard_map/dot_general | solution.py:231
  287.6 4.1 constant_dynamic-slice_fusion.3
  297.2 2.8 constant_dynamic-slice_fusion.1
  300.0 4.7 collective-permute-done.16
  308.0 2.5 convert_add_fusion.1
  310.5 8.0 %collective-permute-done.17 = bf16[4,48,1280]{2,1,0:T(8,128)(2,1)S(1)} collective-permute-done((bf16[4,48,1280]{2,1,0:T(8,128)(2,1)S(1)}, bf16[4,48,1280]{2,1,0:T(8,128)(2,1)S(1)}, u32[]{:S(2)}, u32[]{:S(2)}) %collective-permute-start.17) | collective-permute-done | bytes 491552 | tf_op jit(solution)/shard_map/ppermute | solution.py:124
  325.9 3.9 collective-permute-done.19
  332.3 3.1 collective-permute-done.30
  339.2 6.1 %fusion.61 = f32[3072,768]{1,0:T(8,128)S(1)} fusion(bf16[576,3072]{1,0:T(8,128)(2,1)} %get-tuple-element.133, bf16[576,768]{1,0:T(8,128)(2,1)S(1)} %copy-done.25, f32[576]{0:T(1024)S(1)} %fusion.96), kind=kOutput, calls=%fused_computation.147 | convolution fusion | flops 2719236096 | bytes 13863168 | tf_op jit(solution)/shard_map/dot_general | solution.py:227
  345.3 3.6 copy-done.19
  358.1 7.2 %collective-permute-done.33 = bf16[48,1536]{1,0:T(8,128)(2,1)S(1)} collective-permute-done((bf16[48,1536]{1,0:T(8,128)(2,1)S(1)}, bf16[48,1536]{1,0:T(8,128)(2,1)S(1)}, u32[]{:S(2)}, u32[]{:S(2)}) %collective-permute-start.33) | collective-permute-done | bytes 147488 | tf_op jit(solution)/shard_map/ppermute | solution.py:130
  367.8 2.6 constant_dynamic-slice_fusion
  374.0 13.5 %collective-permute-done.37 = bf16[4,192,384]{2,1,0:T(8,128)(2,1)S(1)} collective-permute-done((bf16[4,192,384]{2,1,0:T(8,128)(2,1)S(1)}, bf16[4,192,384]{2,1,0:T(8,128)(2,1)S(1)}, u32[]{:S(2)}, u32[]{:S(2)}) %collective-permute-start.37) | collective-permute-done | bytes 589856 | tf_op jit(solution)/shard_map/ppermute | solution.py:117
  390.5 14.3 %collective-permute-done.38 = bf16[4,192,384]{2,1,0:T(8,128)(2,1)S(1)} collective-permute-done((bf16[4,192,384]{2,1,0:T(8,128)(2,1)S(1)}, bf16[4,192,384]{2,1,0:T(8,128)(2,1)S(1)}, u32[]{:S(2)}, u32[]{:S(2)}) %collective-permute-start.38) | collective-permute-done | bytes 589856 | tf_op jit(solution)/shard_map/ppermute | solution.py:124
  405.2 3.4 collective-permute-start.40
  415.5 3.6 collective-permute-done.42
  419.1 2.7 collective-permute-done.41
  422.7 7.4 %multiply_convert_fusion.3 = bf16[576,768]{1,0:T(8,128)(2,1)} fusion(f32[576,768]{1,0:T(8,128)S(1)} %copy-done.10, bf16[576,3072]{1,0:T(8,128)(2,1)} %get-tuple-element.133, bf16[3072,384]{1,0:T(8,128)(2,1)} %bitcast.261, bf16[3072,384]{1,0:T(8,128)(2,1)} %bitcast.259, f32[576]{0:T(1024)S(1)} %fusion.96), kind=kOutput, calls=%fused_computation.99 | convolution fusion | flops 2728673280 | bytes 10914048 | tf_op jit(solution)/shard_map/dot_general | solution.py:222
  432.4 5.7 %collective-permute-done.24 = bf16[4,48,384]{2,1,0:T(8,128)(2,1)S(1)} collective-permute-done((bf16[4,48,384]{2,1,0:T(8,128)(2,1)S(1)}, bf16[4,48,384]{2,1,0:T(8,128)(2,1)S(1)}, u32[]{:S(2)}, u32[]{:S(2)}) %collective-permute-start.24) | collective-permute-done | bytes 147488 | tf_op jit(solution)/shard_map/ppermute | solution.py:124
  440.8 2.7 collective-permute-start.27
  446.0 11.0 %all-gather.5 = f32[384,384]{1,0:T(8,128)S(1)} all-gather(f32[48,384]{1,0:T(8,128)S(1)} %fusion.90), channel_id=7, replica_groups=mesh['dp'=8,'fsdp'=4] {'dp'}, dimensions={0}, use_global_device_ids=true | all-gather | bytes 663552 | tf_op jit(solution)/shard_map/all_gather | solution.py:133
  (349 shorter events, 147.1 us)
Async XLA Ops:
  7.2 60.0 %all-gather.18.cloned.1.call-start = ((), (), s32[]{:S(2)}) async-start(), calls=%async_computation.1 | async-start | bytes 1327104 | tf_op jit(solution)/shard_map/all_gather | solution.py:82
  8.0 5.4 %collective-permute-start.7 = (bf16[48,384]{1,0:T(8,128)(2,1)S(1)}, bf16[48,384]{1,0:T(8,128)(2,1)S(1)}, u32[]{:S(2)}, u32[]{:S(2)}) collective-permute-start(bf16[48,384]{1,0:T(8,128)(2,1)S(1)} %dynamic_slice.164), channel_id=1, source_target_pairs={{0,2},{1,3},{2,0},{3,1},{4,6},{5,7},{6,4},{7,5},{8,10},{9,11},{10,... | collective-permute-start | bytes 110600 | tf_op jit(solution)/shard_map/ppermute | solution.py:70
  15.9 63.6 %all-gather.16.cloned.1.call-start = ((), (), s32[]{:S(2)}) async-start(), calls=%async_computation | async-start | bytes 3981312 | tf_op jit(solution)/shard_map/all_gather | solution.py:82
  16.8 10.1 %collective-permute-start.4 = (bf16[48,1152]{1,0:T(8,128)(2,1)S(1)}, bf16[48,1152]{1,0:T(8,128)(2,1)S(1)}, u32[]{:S(2)}, u32[]{:S(2)}) collective-permute-start(bf16[48,1152]{1,0:T(8,128)(2,1)S(1)} %dynamic_slice.163), channel_id=1, source_target_pairs={{0,2},{1,3},{2,0},{3,1},{4,6},{5,7},{6,4},{7,5},{8,10},{9,11},{10,... | collective-permute-start | bytes 331784 | tf_op jit(solution)/shard_map/ppermute | solution.py:70
  21.5 6.6 %collective-permute-start.3 = (bf16[48,1152]{1,0:T(8,128)(2,1)S(1)}, bf16[48,1152]{1,0:T(8,128)(2,1)S(1)}, u32[]{:S(2)}, u32[]{:S(2)}) collective-permute-start(bf16[48,1152]{1,0:T(8,128)(2,1)S(1)} %dynamic_slice.163), channel_id=1, source_target_pairs={{0,1},{1,2},{2,3},{3,0},{4,5},{5,6},{6,7},{7,4},{8,9},{9,10},{10,1... | collective-permute-start | bytes 331784 | tf_op jit(solution)/shard_map/ppermute | solution.py:70
  21.5 7.6 %collective-permute-start.5 = (bf16[48,1152]{1,0:T(8,128)(2,1)S(1)}, bf16[48,1152]{1,0:T(8,128)(2,1)S(1)}, u32[]{:S(2)}, u32[]{:S(2)}) collective-permute-start(bf16[48,1152]{1,0:T(8,128)(2,1)S(1)} %dynamic_slice.163), channel_id=1, source_target_pairs={{0,3},{1,0},{2,1},{3,2},{4,7},{5,4},{6,5},{7,6},{8,11},{9,8},{10,9... | collective-permute-start | bytes 331784 | tf_op jit(solution)/shard_map/ppermute | solution.py:70
  30.6 98.7 %all-gather.22.cloned.1.call-start = ((), (), s32[]{:S(2)}) async-start(), calls=%async_computation.3 | async-start | bytes 5308416 | tf_op jit(solution)/shard_map/all_gather | solution.py:82
  31.6 10.2 %collective-permute-start.13 = (bf16[192,384]{1,0:T(8,128)(2,1)S(1)}, bf16[192,384]{1,0:T(8,128)(2,1)S(1)}, u32[]{:S(2)}, u32[]{:S(2)}) collective-permute-start(bf16[192,384]{1,0:T(8,128)(2,1)S(1)} %dynamic_slice.166), channel_id=1, source_target_pairs={{0,2},{1,3},{2,0},{3,1},{4,6},{5,7},{6,4},{7,5},{8,10},{9,11},{10,... | collective-permute-start | bytes 442376 | tf_op jit(solution)/shard_map/ppermute | solution.py:70
  32.9 11.0 %collective-permute-start.12 = (bf16[192,384]{1,0:T(8,128)(2,1)S(1)}, bf16[192,384]{1,0:T(8,128)(2,1)S(1)}, u32[]{:S(2)}, u32[]{:S(2)}) collective-permute-start(bf16[192,384]{1,0:T(8,128)(2,1)S(1)} %dynamic_slice.166), channel_id=1, source_target_pairs={{0,1},{1,2},{2,3},{3,0},{4,5},{5,6},{6,7},{7,4},{8,9},{9,10},{10,1... | collective-permute-start | bytes 442376 | tf_op jit(solution)/shard_map/ppermute | solution.py:70
  33.8 11.5 %collective-permute-start.14 = (bf16[192,384]{1,0:T(8,128)(2,1)S(1)}, bf16[192,384]{1,0:T(8,128)(2,1)S(1)}, u32[]{:S(2)}, u32[]{:S(2)}) collective-permute-start(bf16[192,384]{1,0:T(8,128)(2,1)S(1)} %dynamic_slice.166), channel_id=1, source_target_pairs={{0,3},{1,0},{2,1},{3,2},{4,7},{5,4},{6,5},{7,6},{8,11},{9,8},{10,9... | collective-permute-start | bytes 442376 | tf_op jit(solution)/shard_map/ppermute | solution.py:70
  46.9 115.0 %all-gather.20.cloned.1.call-start = ((), (), s32[]{:S(2)}) async-start(), calls=%async_computation.2 | async-start | bytes 5308416 | tf_op jit(solution)/shard_map/all_gather | solution.py:82
  47.0 12.2 %collective-permute-start.1 = (bf16[6,192]{1,0:T(8,128)(2,1)S(1)}, bf16[6,192]{1,0:T(8,128)(2,1)S(1)}, u32[]{:S(2)}, u32[]{:S(2)}) collective-permute-start(bf16[6,192]{1,0:T(8,128)(2,1)S(1)} %get-tuple-element.180), channel_id=1, source_target_pairs={{0,2},{1,3},{2,0},{3,1},{4,6},{5,7},{6,4},{7,5},{8,10},{9,11},{10,... | collective-permute-start | bytes 6920 | tf_op jit(solution)/shard_map/ppermute | solution.py:70
  47.1 12.2 %collective-permute-start = (bf16[6,192]{1,0:T(8,128)(2,1)S(1)}, bf16[6,192]{1,0:T(8,128)(2,1)S(1)}, u32[]{:S(2)}, u32[]{:S(2)}) collective-permute-start(bf16[6,192]{1,0:T(8,128)(2,1)S(1)} %get-tuple-element.180), channel_id=1, source_target_pairs={{0,1},{1,2},{2,3},{3,0},{4,5},{5,6},{6,7},{7,4},{8,9},{9,10},{10,1... | collective-permute-start | bytes 6920 | tf_op jit(solution)/shard_map/ppermute | solution.py:70
  48.4 10.9 %collective-permute-start.2 = (bf16[6,192]{1,0:T(8,128)(2,1)S(1)}, bf16[6,192]{1,0:T(8,128)(2,1)S(1)}, u32[]{:S(2)}, u32[]{:S(2)}) collective-permute-start(bf16[6,192]{1,0:T(8,128)(2,1)S(1)} %get-tuple-element.180), channel_id=1, source_target_pairs={{0,3},{1,0},{2,1},{3,2},{4,7},{5,4},{6,5},{7,6},{8,11},{9,8},{10,9... | collective-permute-start | bytes 6920 | tf_op jit(solution)/shard_map/ppermute | solution.py:70
  50.5 11.2 %collective-permute-start.10 = (bf16[48,1536]{1,0:T(8,128)(2,1)S(1)}, bf16[48,1536]{1,0:T(8,128)(2,1)S(1)}, u32[]{:S(2)}, u32[]{:S(2)}) collective-permute-start(bf16[48,1536]{1,0:T(8,128)(2,1)S(1)} %dynamic_slice.165), channel_id=1, source_target_pairs={{0,2},{1,3},{2,0},{3,1},{4,6},{5,7},{6,4},{7,5},{8,10},{9,11},{10,... | collective-permute-start | bytes 442376 | tf_op jit(solution)/shard_map/ppermute | solution.py:70
  53.0 9.5 %collective-permute-start.9 = (bf16[48,1536]{1,0:T(8,128)(2,1)S(1)}, bf16[48,1536]{1,0:T(8,128)(2,1)S(1)}, u32[]{:S(2)}, u32[]{:S(2)}) collective-permute-start(bf16[48,1536]{1,0:T(8,128)(2,1)S(1)} %dynamic_slice.165), channel_id=1, source_target_pairs={{0,1},{1,2},{2,3},{3,0},{4,5},{5,6},{6,7},{7,4},{8,9},{9,10},{10,1... | collective-permute-start | bytes 442376 | tf_op jit(solution)/shard_map/ppermute | solution.py:70
  59.3 6.3 %collective-permute-start.11 = (bf16[48,1536]{1,0:T(8,128)(2,1)S(1)}, bf16[48,1536]{1,0:T(8,128)(2,1)S(1)}, u32[]{:S(2)}, u32[]{:S(2)}) collective-permute-start(bf16[48,1536]{1,0:T(8,128)(2,1)S(1)} %dynamic_slice.165), channel_id=1, source_target_pairs={{0,3},{1,0},{2,1},{3,2},{4,7},{5,4},{6,5},{7,6},{8,11},{9,8},{10,9... | collective-permute-start | bytes 442376 | tf_op jit(solution)/shard_map/ppermute | solution.py:70
  67.1 390.8 %all-gather.24.cloned.1.call-start = ((), (), s32[]{:S(2)}) async-start(), calls=%async_computation.4 | async-start | bytes 2211840 | tf_op jit(solution)/shard_map/all_gather | solution.py:133
  278.6 13.1 %collective-permute-start.15 = (bf16[4,4,48,1280]{3,2,1,0:T(8,128)(2,1)}, bf16[4,4,48,1280]{3,2,1,0:T(8,128)(2,1)}, u32[]{:S(2)}, u32[]{:S(2)}) collective-permute-start(bf16[4,4,48,1280]{3,2,1,0:T(8,128)(2,1)} %bitcast.53), channel_id=1, source_target_pairs={{0,4},{4,0},{8,12},{12,8},{16,20},{20,16},{24,28},{28,24},{1,5},{5... | collective-permute-start | bytes 5898248 | tf_op jit(solution)/shard_map/ppermute | solution.py:111
  287.4 20.7 %collective-permute-start.29 = (bf16[4,4,48,1536]{3,2,1,0:T(8,128)(2,1)}, bf16[4,4,48,1536]{3,2,1,0:T(8,128)(2,1)}, u32[]{:S(2)}, u32[]{:S(2)}) collective-permute-start(bf16[4,4,48,1536]{3,2,1,0:T(8,128)(2,1)} %bitcast.80), channel_id=1, source_target_pairs={{0,4},{4,0},{8,12},{12,8},{16,20},{20,16},{24,28},{28,24},{1,5},{5... | collective-permute-start | bytes 7077896 | tf_op jit(solution)/shard_map/ppermute | solution.py:111
  295.7 9.0 %collective-permute-start.16 = (bf16[4,48,1280]{2,1,0:T(8,128)(2,1)S(1)}, bf16[4,48,1280]{2,1,0:T(8,128)(2,1)}, u32[]{:S(2)}, u32[]{:S(2)}) collective-permute-start(bf16[4,48,1280]{2,1,0:T(8,128)(2,1)S(1)} %fusion.60), channel_id=1, source_target_pairs={{0,8},{4,20},{8,0},{12,28},{16,24},{20,4},{24,16},{28,12},{1,9},{5... | collective-permute-start | bytes 1474568 | tf_op jit(solution)/shard_map/ppermute | solution.py:117
  306.0 12.6 %collective-permute-start.17 = (bf16[4,48,1280]{2,1,0:T(8,128)(2,1)S(1)}, bf16[4,48,1280]{2,1,0:T(8,128)(2,1)S(1)}, u32[]{:S(2)}, u32[]{:S(2)}) collective-permute-start(bf16[4,48,1280]{2,1,0:T(8,128)(2,1)S(1)} %get-tuple-element.145), channel_id=1, source_target_pairs={{0,8},{4,12},{8,0},{12,4},{16,24},{20,28},{24,16},{28,20},{1,9},{5... | collective-permute-start | bytes 1474568 | tf_op jit(solution)/shard_map/ppermute | solution.py:124
  307.5 12.2 %collective-permute-start.18 = (bf16[4,48,1280]{2,1,0:T(8,128)(2,1)S(1)}, bf16[4,48,1280]{2,1,0:T(8,128)(2,1)S(1)}, u32[]{:S(2)}, u32[]{:S(2)}) collective-permute-start(bf16[4,48,1280]{2,1,0:T(8,128)(2,1)S(1)} %get-tuple-element.146), channel_id=1, source_target_pairs={{0,16},{4,20},{8,24},{12,28},{16,0},{20,4},{24,8},{28,12},{1,17},{... | collective-permute-start | bytes 1474568 | tf_op jit(solution)/shard_map/ppermute | solution.py:125
  319.9 9.9 %collective-permute-start.19 = (bf16[48,1280]{1,0:T(8,128)(2,1)S(1)}, bf16[48,1280]{1,0:T(8,128)(2,1)S(1)}, u32[]{:S(2)}, u32[]{:S(2)}) collective-permute-start(bf16[48,1280]{1,0:T(8,128)(2,1)S(1)} %get-tuple-element.165), channel_id=1, source_target_pairs={{0,1},{1,2},{2,3},{3,0},{4,5},{5,6},{6,7},{7,4},{8,9},{9,10},{10,1... | collective-permute-start | bytes 368648 | tf_op jit(solution)/shard_map/ppermute | solution.py:130
  321.5 9.4 %collective-permute-start.21 = (bf16[48,1280]{1,0:T(8,128)(2,1)S(1)}, bf16[48,1280]{1,0:T(8,128)(2,1)S(1)}, u32[]{:S(2)}, u32[]{:S(2)}) collective-permute-start(bf16[48,1280]{1,0:T(8,128)(2,1)S(1)} %get-tuple-element.166), channel_id=1, source_target_pairs={{0,3},{1,0},{2,1},{3,2},{4,7},{5,4},{6,5},{7,6},{8,11},{9,8},{10,9... | collective-permute-start | bytes 368648 | tf_op jit(solution)/shard_map/ppermute | solution.py:130
  322.0 9.1 %collective-permute-start.20 = (bf16[48,1280]{1,0:T(8,128)(2,1)S(1)}, bf16[48,1280]{1,0:T(8,128)(2,1)S(1)}, u32[]{:S(2)}, u32[]{:S(2)}) collective-permute-start(bf16[48,1280]{1,0:T(8,128)(2,1)S(1)} %get-tuple-element.167), channel_id=1, source_target_pairs={{0,2},{1,3},{2,0},{3,1},{4,6},{5,7},{6,4},{7,5},{8,10},{9,11},{10,... | collective-permute-start | bytes 368648 | tf_op jit(solution)/shard_map/ppermute | solution.py:130
  325.3 10.1 %collective-permute-start.30 = (bf16[4,48,1536]{2,1,0:T(8,128)(2,1)}, bf16[4,48,1536]{2,1,0:T(8,128)(2,1)S(1)}, u32[]{:S(2)}, u32[]{:S(2)}) collective-permute-start(bf16[4,48,1536]{2,1,0:T(8,128)(2,1)} %fusion.58), channel_id=1, source_target_pairs={{0,8},{4,20},{8,0},{12,28},{16,24},{20,4},{24,16},{28,12},{1,9},{5... | collective-permute-start | bytes 1769480 | tf_op jit(solution)/shard_map/ppermute | solution.py:117
  331.9 131.1 %all-gather.26.cloned.1.call-start = ((), (), s32[]{:S(2)}) async-start(), calls=%async_computation.5 | async-start | bytes 2654208 | tf_op jit(solution)/shard_map/all_gather | solution.py:133
  337.3 14.5 %collective-permute-start.31 = (bf16[4,48,1536]{2,1,0:T(8,128)(2,1)S(1)}, bf16[4,48,1536]{2,1,0:T(8,128)(2,1)S(1)}, u32[]{:S(2)}, u32[]{:S(2)}) collective-permute-start(bf16[4,48,1536]{2,1,0:T(8,128)(2,1)S(1)} %get-tuple-element.137), channel_id=1, source_target_pairs={{0,8},{4,12},{8,0},{12,4},{16,24},{20,28},{24,16},{28,20},{1,9},{5... | collective-permute-start | bytes 1769480 | tf_op jit(solution)/shard_map/ppermute | solution.py:124
  337.9 14.1 %collective-permute-start.32 = (bf16[4,48,1536]{2,1,0:T(8,128)(2,1)S(1)}, bf16[4,48,1536]{2,1,0:T(8,128)(2,1)S(1)}, u32[]{:S(2)}, u32[]{:S(2)}) collective-permute-start(bf16[4,48,1536]{2,1,0:T(8,128)(2,1)S(1)} %get-tuple-element.138), channel_id=1, source_target_pairs={{0,16},{4,20},{8,24},{12,28},{16,0},{20,4},{24,8},{28,12},{1,17},{... | collective-permute-start | bytes 1769480 | tf_op jit(solution)/shard_map/ppermute | solution.py:125
  350.6 19.8 %collective-permute-start.36 = (bf16[4,4,192,384]{3,2,1,0:T(8,128)(2,1)}, bf16[4,4,192,384]{3,2,1,0:T(8,128)(2,1)}, u32[]{:S(2)}, u32[]{:S(2)}) collective-permute-start(bf16[4,4,192,384]{3,2,1,0:T(8,128)(2,1)} %bitcast.93), channel_id=1, source_target_pairs={{0,4},{4,0},{8,12},{12,8},{16,20},{20,16},{24,28},{28,24},{1,5},{5... | collective-permute-start | bytes 7077896 | tf_op jit(solution)/shard_map/ppermute | solution.py:111
  353.6 11.7 %collective-permute-start.33 = (bf16[48,1536]{1,0:T(8,128)(2,1)S(1)}, bf16[48,1536]{1,0:T(8,128)(2,1)S(1)}, u32[]{:S(2)}, u32[]{:S(2)}) collective-permute-start(bf16[48,1536]{1,0:T(8,128)(2,1)S(1)} %get-tuple-element.160), channel_id=1, source_target_pairs={{0,1},{1,2},{2,3},{3,0},{4,5},{5,6},{6,7},{7,4},{8,9},{9,10},{10,1... | collective-permute-start | bytes 442376 | tf_op jit(solution)/shard_map/ppermute | solution.py:130
  355.1 11.5 %collective-permute-start.35 = (bf16[48,1536]{1,0:T(8,128)(2,1)S(1)}, bf16[48,1536]{1,0:T(8,128)(2,1)S(1)}, u32[]{:S(2)}, u32[]{:S(2)}) collective-permute-start(bf16[48,1536]{1,0:T(8,128)(2,1)S(1)} %get-tuple-element.161), channel_id=1, source_target_pairs={{0,3},{1,0},{2,1},{3,2},{4,7},{5,4},{6,5},{7,6},{8,11},{9,8},{10,9... | collective-permute-start | bytes 442376 | tf_op jit(solution)/shard_map/ppermute | solution.py:130
  355.7 11.2 %collective-permute-start.34 = (bf16[48,1536]{1,0:T(8,128)(2,1)S(1)}, bf16[48,1536]{1,0:T(8,128)(2,1)S(1)}, u32[]{:S(2)}, u32[]{:S(2)}) collective-permute-start(bf16[48,1536]{1,0:T(8,128)(2,1)S(1)} %get-tuple-element.162), channel_id=1, source_target_pairs={{0,2},{1,3},{2,0},{3,1},{4,6},{5,7},{6,4},{7,5},{8,10},{9,11},{10,... | collective-permute-start | bytes 442376 | tf_op jit(solution)/shard_map/ppermute | solution.py:130
  367.7 97.1 %all-gather.28.cloned.1.call-start = ((), (), s32[]{:S(2)}) async-start(), calls=%async_computation.6 | async-start | bytes 2654208 | tf_op jit(solution)/shard_map/all_gather | solution.py:133
  372.8 14.7 %collective-permute-start.37 = (bf16[4,192,384]{2,1,0:T(8,128)(2,1)S(1)}, bf16[4,192,384]{2,1,0:T(8,128)(2,1)S(1)}, u32[]{:S(2)}, u32[]{:S(2)}) collective-permute-start(bf16[4,192,384]{2,1,0:T(8,128)(2,1)S(1)} %fusion.59), channel_id=1, source_target_pairs={{0,8},{4,20},{8,0},{12,28},{16,24},{20,4},{24,16},{28,12},{1,9},{5... | collective-permute-start | bytes 1769480 | tf_op jit(solution)/shard_map/ppermute | solution.py:117
  387.8 17.0 %collective-permute-start.38 = (bf16[4,192,384]{2,1,0:T(8,128)(2,1)S(1)}, bf16[4,192,384]{2,1,0:T(8,128)(2,1)S(1)}, u32[]{:S(2)}, u32[]{:S(2)}) collective-permute-start(bf16[4,192,384]{2,1,0:T(8,128)(2,1)S(1)} %get-tuple-element.135), channel_id=1, source_target_pairs={{0,8},{4,12},{8,0},{12,4},{16,24},{20,28},{24,16},{28,20},{1,9},{5... | collective-permute-start | bytes 1769480 | tf_op jit(solution)/shard_map/ppermute | solution.py:124
  389.2 15.7 %collective-permute-start.39 = (bf16[4,192,384]{2,1,0:T(8,128)(2,1)S(1)}, bf16[4,192,384]{2,1,0:T(8,128)(2,1)S(1)}, u32[]{:S(2)}, u32[]{:S(2)}) collective-permute-start(bf16[4,192,384]{2,1,0:T(8,128)(2,1)S(1)} %get-tuple-element.136), channel_id=1, source_target_pairs={{0,16},{4,20},{8,24},{12,28},{16,0},{20,4},{24,8},{28,12},{1,17},{... | collective-permute-start | bytes 1769480 | tf_op jit(solution)/shard_map/ppermute | solution.py:125
  390.4 22.5 %collective-permute-start.22 = (bf16[4,4,48,384]{3,2,1,0:T(8,128)(2,1)S(1)}, bf16[4,4,48,384]{3,2,1,0:T(8,128)(2,1)S(1)}, u32[]{:S(2)}, u32[]{:S(2)}) collective-permute-start(bf16[4,4,48,384]{3,2,1,0:T(8,128)(2,1)S(1)} %bitcast.282), channel_id=1, source_target_pairs={{0,4},{4,0},{8,12},{12,8},{16,20},{20,16},{24,28},{28,24},{1,5},{5... | collective-permute-start | bytes 1769480 | tf_op jit(solution)/shard_map/ppermute | solution.py:111
  405.2 10.3 %collective-permute-start.40 = (bf16[192,384]{1,0:T(8,128)(2,1)S(1)}, bf16[192,384]{1,0:T(8,128)(2,1)S(1)}, u32[]{:S(2)}, u32[]{:S(2)}) collective-permute-start(bf16[192,384]{1,0:T(8,128)(2,1)S(1)} %get-tuple-element.157), channel_id=1, source_target_pairs={{0,1},{1,2},{2,3},{3,0},{4,5},{5,6},{6,7},{7,4},{8,9},{9,10},{10,1... | collective-permute-start | bytes 442376 | tf_op jit(solution)/shard_map/ppermute | solution.py:130
  408.6 10.5 %collective-permute-start.42 = (bf16[192,384]{1,0:T(8,128)(2,1)S(1)}, bf16[192,384]{1,0:T(8,128)(2,1)S(1)}, u32[]{:S(2)}, u32[]{:S(2)}) collective-permute-start(bf16[192,384]{1,0:T(8,128)(2,1)S(1)} %get-tuple-element.158), channel_id=1, source_target_pairs={{0,3},{1,0},{2,1},{3,2},{4,7},{5,4},{6,5},{7,6},{8,11},{9,8},{10,9... | collective-permute-start | bytes 442376 | tf_op jit(solution)/shard_map/ppermute | solution.py:130
  410.6 11.2 %collective-permute-start.41 = (bf16[192,384]{1,0:T(8,128)(2,1)S(1)}, bf16[192,384]{1,0:T(8,128)(2,1)S(1)}, u32[]{:S(2)}, u32[]{:S(2)}) collective-permute-start(bf16[192,384]{1,0:T(8,128)(2,1)S(1)} %get-tuple-element.159), channel_id=1, source_target_pairs={{0,2},{1,3},{2,0},{3,1},{4,6},{5,7},{6,4},{7,5},{8,10},{9,11},{10,... | collective-permute-start | bytes 442376 | tf_op jit(solution)/shard_map/ppermute | solution.py:130
  414.0 16.1 %collective-permute-start.23 = (bf16[4,48,384]{2,1,0:T(8,128)(2,1)S(1)}, bf16[4,48,384]{2,1,0:T(8,128)(2,1)S(1)}, u32[]{:S(2)}, u32[]{:S(2)}) collective-permute-start(bf16[4,48,384]{2,1,0:T(8,128)(2,1)S(1)} %fusion.77), channel_id=1, source_target_pairs={{0,8},{4,20},{8,0},{12,28},{16,24},{20,4},{24,16},{28,12},{1,9},{5... | collective-permute-start | bytes 442376 | tf_op jit(solution)/shard_map/ppermute | solution.py:117
  430.2 8.0 %collective-permute-start.24 = (bf16[4,48,384]{2,1,0:T(8,128)(2,1)S(1)}, bf16[4,48,384]{2,1,0:T(8,128)(2,1)S(1)}, u32[]{:S(2)}, u32[]{:S(2)}) collective-permute-start(bf16[4,48,384]{2,1,0:T(8,128)(2,1)S(1)} %get-tuple-element.155), channel_id=1, source_target_pairs={{0,8},{4,12},{8,0},{12,4},{16,24},{20,28},{24,16},{28,20},{1,9},{5... | collective-permute-start | bytes 442376 | tf_op jit(solution)/shard_map/ppermute | solution.py:124
  431.4 6.9 %collective-permute-start.25 = (bf16[4,48,384]{2,1,0:T(8,128)(2,1)S(1)}, bf16[4,48,384]{2,1,0:T(8,128)(2,1)S(1)}, u32[]{:S(2)}, u32[]{:S(2)}) collective-permute-start(bf16[4,48,384]{2,1,0:T(8,128)(2,1)S(1)} %get-tuple-element.156), channel_id=1, source_target_pairs={{0,16},{4,20},{8,24},{12,28},{16,0},{20,4},{24,8},{28,12},{1,17},{... | collective-permute-start | bytes 442376 | tf_op jit(solution)/shard_map/ppermute | solution.py:125
  438.4 6.9 %collective-permute-start.26 = (bf16[48,384]{1,0:T(8,128)(2,1)S(1)}, bf16[48,384]{1,0:T(8,128)(2,1)S(1)}, u32[]{:S(2)}, u32[]{:S(2)}) collective-permute-start(bf16[48,384]{1,0:T(8,128)(2,1)S(1)} %get-tuple-element.170), channel_id=1, source_target_pairs={{0,1},{1,2},{2,3},{3,0},{4,5},{5,6},{6,7},{7,4},{8,9},{9,10},{10,1... | collective-permute-start | bytes 110600 | tf_op jit(solution)/shard_map/ppermute | solution.py:130
  440.3 5.0 %collective-permute-start.28 = (bf16[48,384]{1,0:T(8,128)(2,1)S(1)}, bf16[48,384]{1,0:T(8,128)(2,1)S(1)}, u32[]{:S(2)}, u32[]{:S(2)}) collective-permute-start(bf16[48,384]{1,0:T(8,128)(2,1)S(1)} %get-tuple-element.171), channel_id=1, source_target_pairs={{0,3},{1,0},{2,1},{3,2},{4,7},{5,4},{6,5},{7,6},{8,11},{9,8},{10,9... | collective-permute-start | bytes 110600 | tf_op jit(solution)/shard_map/ppermute | solution.py:130
  440.8 5.1 %collective-permute-start.27 = (bf16[48,384]{1,0:T(8,128)(2,1)S(1)}, bf16[48,384]{1,0:T(8,128)(2,1)S(1)}, u32[]{:S(2)}, u32[]{:S(2)}) collective-permute-start(bf16[48,384]{1,0:T(8,128)(2,1)S(1)} %get-tuple-element.172), channel_id=1, source_target_pairs={{0,2},{1,3},{2,0},{3,1},{4,6},{5,7},{6,4},{7,5},{8,10},{9,11},{10,... | collective-permute-start | bytes 110600 | tf_op jit(solution)/shard_map/ppermute | solution.py:130
  (69 other events, 655.1 us)
Sparse Core Ops, SparseCore 0:
  16.0 27.0 all-gather.17
  45.6 33.8 all-gather.15
  81.9 38.7 all-gather.21
  123.1 38.7 all-gather.19
  332.0 30.7 all-gather.23
  367.8 35.4 all-gather.25
  422.8 32.6 all-gather.27

commit v9 on v8

--- a/solution.py
+++ b/solution.py
@@ -5,6 +5,7 @@
 from jax import lax
 from jax.sharding import PartitionSpec as P
 
+
 HEADS = 12
 HEAD_DIM = 64
 PATCH_BIG = 576
@@ -34,30 +35,6 @@
 
 
 LANES = 128
-
-
-def _to_rows(v):
-    return v.reshape(-1, LANES)
-
-
-def _gain_rows(gains, pick):
-    flat = jnp.concatenate([pick(g).reshape(-1) for g in gains])
-    pad = (-flat.shape[0]) % LANES
-    return jnp.pad(flat, (0, pad)).reshape(-1, LANES)
-
-
-def _plane_gather(z):
-    d = lax.axis_index("dp")
-    c = d % 2
-    a = lax.ppermute(z, "dp", [(i, i ^ 2) for i in range(NDP_FAST)])
-    b = lax.ppermute(z, "dp", [(i, i ^ 4) for i in range(NDP_FAST)])
-    send = jnp.where(c == 0, b, a)
-    diag = lax.ppermute(
-        send, "dp", [(i, i ^ 2) if i % 2 == 0 else (i, i ^ 4) for i in range(NDP_FAST)]
-    )
-    mine = jnp.stack([z, a, b, diag])
-    sib = lax.ppermute(mine, "dp", [(i, i ^ 1) for i in range(NDP_FAST)])
-    return jnp.stack([mine[0], sib[0], mine[1], sib[1], mine[2], sib[2], mine[3], sib[3]])
 
 
 def _take(x, idx, axis):
@@ -151,7 +128,17 @@
     return out
 
 
-def on_device(
+def map_blocks(fn, members):
+    if members[0].shape[0] == 1:
+        return jax.tree.map(lambda v: v[None], fn(tuple(m[0] for m in members)))
+    return lax.map(fn, members)
+
+
+def on_device(fast, *args):
+    return layer(fast, *args)
+
+
+def layer(
     fast, tokens, image_lengths, w_qkv, w_out, w_up, w_down, ln_gain, ln_bias, qk_gain, cotangent
 ):
     if fast:
@@ -257,7 +244,7 @@
         )
         return (grad_q, grad_k, grad_v)
 
-    grad_qn, grad_kn, grad_vn = lax.map(
+    grad_qn, grad_kn, grad_vn = map_blocks(
         attend_back, (q_low, k_low, v_low, s_blocks, log_total, grad_mixed)
     )
     grad_q, grad_k, gain_q, gain_k = norms_back(

time: 486 us -> 486 us (level)
  no operation moved by 1% of the time
where the time goes in v9:
time: 486 us; the launch traced here: 477 us
  waiting for transfers between devices  130 us (27%)
  matrix products  114 us (23%)
  local copies, waits for them, and re-layouts  81.1 us (17%)
  other arithmetic  67.7 us (14%)
  starting transfers between devices  57.4 us (12%)
  between operations  15.8 us (3%)
  blocking collectives  11.1 us (2%)
    all_gather x4, waiting for transfers between devices, _gather_matrix(): x = lax.all_gather(z, 'dp', axis=1, tiled=False)  36.7 us
    ppermute x4, waiting for transfers between devices, _reduce_matrix(): lax.ppermute(to_x.astype(jnp.bfloat16), 'dp', [(i, i ^ 2) for i in range(...  29.3 us
    ppermute x15, starting transfers between devices, _z_gather(): lax.ppermute(piece, 'fsdp', [(i, (i + k) % NF_FAST) for i in range(NF_FAS...  22.6 us
    dot_general x1, matrix products, layer(): up_pre = jnp.dot(second_low, full_up, preferred_element_type=jnp.float32)  22 us
    ppermute x12, starting transfers between devices, _reduce_matrix(): lax.ppermute(part.astype(jnp.bfloat16), 'fsdp', [(i, (i + k) % NF_FAST) f...  21.6 us
    ppermute x4, waiting for transfers between devices, _reduce_matrix(): lax.ppermute(of_chip(j ^ 3).astype(jnp.bfloat16), 'dp', [(i, i ^ 2) if i...  21.4 us
    ppermute x12, waiting for transfers between devices, _reduce_matrix(): lax.ppermute(part.astype(jnp.bfloat16), 'fsdp', [(i, (i + k) % NF_FAST) f...  21.2 us
    unnamed x137, local copies, waits for them, and re-layouts  20.3 us
  transfers between devices with their start and end apart: 50, of which 30 were waited for; matrix products, arithmetic and copies ran while one was open for 27% of the time, Pallas kernels for 0%

profile of v9, /device:TPU:8, one launch (start us, length us, event | category | flops | bytes accessed | tf_op | source)
XLA Modules:
  0.0 477.0 jit_solution(5170234894607616731)
XLA Ops:
  8.0 2.6 collective-permute-start.7
  16.8 4.7 collective-permute-start.4
  24.4 2.5 collective-permute-done.4
  35.9 5.9 %collective-permute-done.13 = bf16[192,384]{1,0:T(8,128)(2,1)S(1)} collective-permute-done((bf16[192,384]{1,0:T(8,128)(2,1)S(1)}, bf16[192,384]{1,0:T(8,128)(2,1)S(1)}, u32[]{:S(2)}, u32[]{:S(2)}) %collective-permute-start.13) | collective-permute-done | bytes 147488 | tf_op jit(solution)/shard_map/ppermute | solution.py:47
  50.5 2.5 collective-permute-start.10
  53.0 2.8 collective-permute-start.9
  62.5 3.0 collective-permute-done.11
  69.5 9.9 %all-gather.16.cloned.1.call-done = bf16[4,384,1152]{2,1,0:T(8,128)(2,1)} async-done(((bf16[4,48,1152]{2,1,0:T(8,128)(2,1)}), bf16[4,384,1152]{2,1,0:T(8,128)(2,1)}) %all-gather.16.cloned.1.call-update) | async-done | bytes 3538960 | tf_op jit(solution)/shard_map/all_gather | solution.py:59
  88.6 3.7 fusion.119
  100.1 8.4 %fusion.129 = (f32[12,576]{1,0:T(8,128)S(1)}, f32[12,576,576]{1,2,0:T(8,128)}) fusion(f32[576,12,64]{0,2,1:T(8,128)S(1)} %bitcast.234, f32[12,64]{1,0:T(8,128)S(1)} %mul.355, f32[576,12]{0,1:T(8,128)S(1)} %fusion.95, f32[576,12]{0,1:T(8,128)S(1)} %broadcast_multiply_fusion, f32[576,12,64]{0,2,1:T(8,128)S(1)} %bitcast.226, f32[12,64]{1,0:T(8,128)S(1)} %mul.349, ...), kind=kOutput, calls=%fused_computation.274 | convolution fusion | flops 525083904 | bytes 19940352 | tf_op jit(solution)/shard_map/while/body/eval_jaxpr/qhd,khd->hqk/dot_general | solution.py:184
  108.5 8.7 %fusion.3 = f32[12,576]{1,0:T(8,128)S(1)} fusion(f32[12,576,576]{1,2,0:T(8,128)} %get-tuple-element.152, f32[12,576]{1,0:T(8,128)S(1)} %get-tuple-element.151), kind=kLoop, calls=%fused_computation.14 | loop fusion | flops 7955712 | bytes 15980544 | tf_op jit(solution)/shard_map/while/body/eval_jaxpr/reduce_sum | solution.py:194
  117.2 9.8 %fusion.37 = bf16[12,64,576]{2,1,0:T(8,128)(2,1)S(1)} fusion(bf16[576,12,64]{0,2,1:T(8,128)(2,1)} %bitcast.253, f32[12,576,576]{1,2,0:T(8,128)} %get-tuple-element.152, f32[12,576]{1,0:T(8,128)S(1)} %fusion.3, f32[12,576]{1,0:T(8,128)S(1)} %get-tuple-element.151), kind=kOutput, calls=%fused_computation.106 | convolution fusion | flops 521994240 | bytes 17750016 | tf_op jit(solution)/shard_map/while/body/eval_jaxpr/hqk,khd->qhd/dot_general | solution.py:196
  129.7 5.4 %fusion.120 = (bf16[4,4,1,192,384]{4,3,2,1,0:T(8,128)(2,1)}, bf16[4,4,1,192,384]{4,3,2,1,0:T(8,128)(2,1)}) fusion(bf16[4,4,2,192,384]{4,3,2,1,0:T(8,128)(2,1)} %bitcast.243), kind=kLoop, calls=%fused_computation.265 | loop fusion | bytes 9437184 | tf_op jit(solution)/shard_map/slice | solution.py:61
  135.1 26.8 %all-gather.20.cloned.1.call-done = bf16[4,384,1536]{2,1,0:T(8,128)(2,1)} async-done(((bf16[4,48,1536]{2,1,0:T(8,128)(2,1)}), bf16[4,384,1536]{2,1,0:T(8,128)(2,1)}) %all-gather.20.cloned.1.call-update) | async-done | bytes 4718608 | tf_op jit(solution)/shard_map/all_gather | solution.py:59
  161.9 3.0 fusion.121
  164.9 22.0 %multiply_convert_fusion = (bf16[576,3072]{1,0:T(8,128)(2,1)}, f32[576,3072]{1,0:T(8,128)}, f32[576,3072]{1,0:T(8,128)}) fusion(bf16[768,1536]{1,0:T(8,128)(2,1)S(1)} %bitcast.265, bf16[768,1536]{1,0:T(8,128)(2,1)S(1)} %bitcast.263, f32[576,768]{1,0:T(8,128)S(1)} %copy-done.9, f32[768]{0:T(1024)S(1)} %add.386, f32[768]{0:T(1024)S(1)} %mul.363, ...), kind=kOutput, calls=%fused_computation.24 | convolution fusion | flops 2844573696 | bytes 24193536 | tf_op jit(solution)/shard_map/dot_general | solution.py:206
  187.0 8.1 %add_convert_fusion = bf16[576,3072]{1,0:T(8,128)(2,1)S(1)} fusion(f32[576,3072]{1,0:T(8,128)} %get-tuple-element.104, f32[576,3072]{1,0:T(8,128)} %get-tuple-element.155, bf16[3072,384]{1,0:T(8,128)(2,1)S(1)} %bitcast.262, bf16[3072,384]{1,0:T(8,128)(2,1)S(1)} %bitcast.260, bf16[576,768]{1,0:T(8,128)(2,1)S(1)} %copy-done.24, f32[576]{0:T(1024)S(1)} %fusion.96), kind=kOutput, calls=%fused_computation.23 | convolution fusion | flops 2753445888 | bytes 23300352 | tf_op jit(solution)/shard_map/dot_general | solution.py:215
  195.1 3.3 multiply_reduce_fusion.2
  205.7 7.6 %convolution_convert_fusion = bf16[12,576,576]{1,2,0:T(8,128)(2,1)} fusion(bf16[576,12,64]{0,2,1:T(8,128)(2,1)} %bitcast.241, bf16[576,12,64]{0,2,1:T(8,128)(2,1)} %bitcast.254), kind=kOutput, calls=%fused_computation.38 | convolution fusion | flops 513589248 | bytes 9732096 | tf_op jit(solution)/shard_map/qhd,khd->hqk/dot_general | solution.py:235
  213.3 9.9 %fusion.38 = bf16[12,64,576]{2,1,0:T(8,128)(2,1)} fusion(bf16[576,12,64]{0,2,1:T(8,128)(2,1)S(1)} %bitcast.242, f32[12,576,576]{1,2,0:T(8,128)} %get-tuple-element.152, f32[12,576]{1,0:T(8,128)S(1)} %log_add_fusion), kind=kOutput, calls=%fused_computation.107 | convolution fusion | flops 518012928 | bytes 17722368 | tf_op jit(solution)/shard_map/hqk,qhd->khd/dot_general | solution.py:234
  223.2 12.8 %fusion = f32[12,576]{1,0:T(8,128)S(1)} fusion(bf16[12,576,576]{1,2,0:T(8,128)(2,1)} %convolution_convert_fusion, f32[12,576,576]{1,2,0:T(8,128)} %get-tuple-element.152, f32[12,576]{1,0:T(8,128)S(1)} %log_add_fusion), kind=kLoop, calls=%fused_computation.7 | loop fusion | flops 15918336 | bytes 23943168 | tf_op jit(solution)/shard_map/reduce_sum | solution.py:237
  236.8 6.3 %fusion.2 = bf16[12,576,576]{1,2,0:T(8,128)(2,1)} fusion(bf16[12,576,576]{1,2,0:T(8,128)(2,1)S(1)} %copy-done.3, f32[12,576,576]{1,2,0:T(8,128)S(1)} %bitcast.223, f32[12,576]{1,0:T(8,128)S(1)} %fusion, f32[12,576]{1,0:T(8,128)S(1)} %log_add_fusion), kind=kLoop, calls=%fused_computation.9 | loop fusion | flops 19906560 | bytes 31905792 | tf_op jit(solution)/shard_map/convert_element_type | solution.py:238
  243.2 8.2 %fusion.29 = (f32[576,12]{0,1:T(8,128)S(1)}, f32[12,64,576]{2,1,0:T(8,128)}) fusion(f32[576,12,64]{0,2,1:T(8,128)} %bitcast.233, f32[12,64]{1,0:T(8,128)S(1)} %copy-done.45, f32[576,12]{0,1:T(8,128)S(1)} %broadcast_multiply_fusion, bf16[12,576,576]{1,2,0:T(8,128)(2,1)} %fusion.2, f32[576,12,64]{0,2,1:T(8,128)S(1)} %bitcast.227, f32[12,64]{1,0:T(8,128)S(1)} %mul.349, ...), kind=kOutput, calls=%fused_computation.76 | convolution fusion | flops 513139968 | bytes 13387776 | tf_op jit(solution)/shard_map/hqk,qhd->khd/dot_general | solution.py:243
  259.2 2.8 fusion.116
  262.0 6.4 %fusion.41 = f32[768,2304]{1,0:T(8,128)} fusion(bf16[576,768]{0,1:T(8,128)(2,1)S(1)} %bitcast.281, bf16[576,768]{0,1:T(8,128)(2,1)S(1)} %bitcast.277, bf16[576,768]{0,1:T(8,128)(2,1)S(1)} %bitcast.279, bf16[576,768]{1,0:T(8,128)(2,1)S(1)} %copy-done.13, f32[768]{0:T(1024)S(1)} %copy-done.55, f32[768]{0:T(1024)S(1)} %copy-done.53, f32[576]{0:T(1024)S(1)} %copy-done.51, ...), kind=kOutput, calls=%fused_computation.111 | convolution fusion | flops 2049048576 | bytes 10627584 | tf_op jit(solution)/shard_map/dot_general | solution.py:261
  269.6 4.2 select_maximum_fusion
  273.8 3.2 copy-done.5
  279.1 6.1 %fusion.115 = f32[768,3072]{1,0:T(8,128)S(1)} fusion(bf16[576,3072]{1,0:T(8,128)(2,1)} %copy-done.23, f32[576,768]{1,0:T(8,128)S(1)} %copy-done.10, f32[768]{0:T(1024)S(1)} %add.386, f32[768]{0:T(1024)S(1)} %mul.363, f32[576]{0:T(1024)S(1)} %fusion.98, f32[576]{0:T(1024)S(1)} %broadcast_multiply_fusion.4), kind=kOutput, calls=%fused_computation.261 | convolution fusion | flops 2720120832 | bytes 14756352 | tf_op jit(solution)/shard_map/dot_general | solution.py:218
  287.5 4.1 constant_dynamic-slice_fusion.3
  297.2 2.8 constant_dynamic-slice_fusion.1
  300.0 4.6 collective-permute-done.16
  308.0 2.5 convert_add_fusion.1
  310.5 8.0 %collective-permute-done.17 = bf16[4,48,1280]{2,1,0:T(8,128)(2,1)S(1)} collective-permute-done((bf16[4,48,1280]{2,1,0:T(8,128)(2,1)S(1)}, bf16[4,48,1280]{2,1,0:T(8,128)(2,1)S(1)}, u32[]{:S(2)}, u32[]{:S(2)}) %collective-permute-start.17) | collective-permute-done | bytes 491552 | tf_op jit(solution)/shard_map/ppermute | solution.py:101
  325.8 4.0 collective-permute-done.19
  332.1 3.2 collective-permute-done.30
  339.2 6.1 %fusion.61 = f32[3072,768]{1,0:T(8,128)S(1)} fusion(bf16[576,3072]{1,0:T(8,128)(2,1)} %get-tuple-element.103, bf16[576,768]{1,0:T(8,128)(2,1)S(1)} %copy-done.25, f32[576]{0:T(1024)S(1)} %fusion.96), kind=kOutput, calls=%fused_computation.147 | convolution fusion | flops 2719236096 | bytes 13863168 | tf_op jit(solution)/shard_map/dot_general | solution.py:214
  345.3 3.6 copy-done.19
  357.8 7.4 %collective-permute-done.33 = bf16[48,1536]{1,0:T(8,128)(2,1)S(1)} collective-permute-done((bf16[48,1536]{1,0:T(8,128)(2,1)S(1)}, bf16[48,1536]{1,0:T(8,128)(2,1)S(1)}, u32[]{:S(2)}, u32[]{:S(2)}) %collective-permute-start.33) | collective-permute-done | bytes 147488 | tf_op jit(solution)/shard_map/ppermute | solution.py:107
  367.7 2.6 constant_dynamic-slice_fusion
  373.9 13.5 %collective-permute-done.37 = bf16[4,192,384]{2,1,0:T(8,128)(2,1)S(1)} collective-permute-done((bf16[4,192,384]{2,1,0:T(8,128)(2,1)S(1)}, bf16[4,192,384]{2,1,0:T(8,128)(2,1)S(1)}, u32[]{:S(2)}, u32[]{:S(2)}) %collective-permute-start.37) | collective-permute-done | bytes 589856 | tf_op jit(solution)/shard_map/ppermute | solution.py:94
  390.4 14.5 %collective-permute-done.38 = bf16[4,192,384]{2,1,0:T(8,128)(2,1)S(1)} collective-permute-done((bf16[4,192,384]{2,1,0:T(8,128)(2,1)S(1)}, bf16[4,192,384]{2,1,0:T(8,128)(2,1)S(1)}, u32[]{:S(2)}, u32[]{:S(2)}) %collective-permute-start.38) | collective-permute-done | bytes 589856 | tf_op jit(solution)/shard_map/ppermute | solution.py:101
  405.2 3.4 collective-permute-start.40
  415.4 3.6 collective-permute-done.42
  419.1 2.8 collective-permute-done.41
  422.7 7.4 %multiply_convert_fusion.3 = bf16[576,768]{1,0:T(8,128)(2,1)} fusion(f32[576,768]{1,0:T(8,128)S(1)} %copy-done.10, bf16[576,3072]{1,0:T(8,128)(2,1)} %get-tuple-element.103, bf16[3072,384]{1,0:T(8,128)(2,1)} %bitcast.261, bf16[3072,384]{1,0:T(8,128)(2,1)} %bitcast.259, f32[576]{0:T(1024)S(1)} %fusion.96), kind=kOutput, calls=%fused_computation.99 | convolution fusion | flops 2728673280 | bytes 10914048 | tf_op jit(solution)/shard_map/dot_general | solution.py:209
  432.4 5.7 %collective-permute-done.24 = bf16[4,48,384]{2,1,0:T(8,128)(2,1)S(1)} collective-permute-done((bf16[4,48,384]{2,1,0:T(8,128)(2,1)S(1)}, bf16[4,48,384]{2,1,0:T(8,128)(2,1)S(1)}, u32[]{:S(2)}, u32[]{:S(2)}) %collective-permute-start.24) | collective-permute-done | bytes 147488 | tf_op jit(solution)/shard_map/ppermute | solution.py:101
  440.8 2.7 collective-permute-start.27
  445.9 11.1 %all-gather.5 = f32[384,384]{1,0:T(8,128)S(1)} all-gather(f32[48,384]{1,0:T(8,128)S(1)} %fusion.90), channel_id=7, replica_groups=mesh['dp'=8,'fsdp'=4] {'dp'}, dimensions={0}, use_global_device_ids=true | all-gather | bytes 663552 | tf_op jit(solution)/shard_map/all_gather | solution.py:110
  (349 shorter events, 147.0 us)
Async XLA Ops:
  7.2 60.0 %all-gather.18.cloned.1.call-start = ((), (), s32[]{:S(2)}) async-start(), calls=%async_computation.1 | async-start | bytes 1327104 | tf_op jit(solution)/shard_map/all_gather | solution.py:59
  8.0 5.4 %collective-permute-start.7 = (bf16[48,384]{1,0:T(8,128)(2,1)S(1)}, bf16[48,384]{1,0:T(8,128)(2,1)S(1)}, u32[]{:S(2)}, u32[]{:S(2)}) collective-permute-start(bf16[48,384]{1,0:T(8,128)(2,1)S(1)} %dynamic_slice.151), channel_id=1, source_target_pairs={{0,2},{1,3},{2,0},{3,1},{4,6},{5,7},{6,4},{7,5},{8,10},{9,11},{10,... | collective-permute-start | bytes 110600 | tf_op jit(solution)/shard_map/ppermute | solution.py:47
  15.9 63.6 %all-gather.16.cloned.1.call-start = ((), (), s32[]{:S(2)}) async-start(), calls=%async_computation | async-start | bytes 3981312 | tf_op jit(solution)/shard_map/all_gather | solution.py:59
  16.8 10.1 %collective-permute-start.4 = (bf16[48,1152]{1,0:T(8,128)(2,1)S(1)}, bf16[48,1152]{1,0:T(8,128)(2,1)S(1)}, u32[]{:S(2)}, u32[]{:S(2)}) collective-permute-start(bf16[48,1152]{1,0:T(8,128)(2,1)S(1)} %dynamic_slice.150), channel_id=1, source_target_pairs={{0,2},{1,3},{2,0},{3,1},{4,6},{5,7},{6,4},{7,5},{8,10},{9,11},{10,... | collective-permute-start | bytes 331784 | tf_op jit(solution)/shard_map/ppermute | solution.py:47
  21.5 6.6 %collective-permute-start.3 = (bf16[48,1152]{1,0:T(8,128)(2,1)S(1)}, bf16[48,1152]{1,0:T(8,128)(2,1)S(1)}, u32[]{:S(2)}, u32[]{:S(2)}) collective-permute-start(bf16[48,1152]{1,0:T(8,128)(2,1)S(1)} %dynamic_slice.150), channel_id=1, source_target_pairs={{0,1},{1,2},{2,3},{3,0},{4,5},{5,6},{6,7},{7,4},{8,9},{9,10},{10,1... | collective-permute-start | bytes 331784 | tf_op jit(solution)/shard_map/ppermute | solution.py:47
  21.5 7.6 %collective-permute-start.5 = (bf16[48,1152]{1,0:T(8,128)(2,1)S(1)}, bf16[48,1152]{1,0:T(8,128)(2,1)S(1)}, u32[]{:S(2)}, u32[]{:S(2)}) collective-permute-start(bf16[48,1152]{1,0:T(8,128)(2,1)S(1)} %dynamic_slice.150), channel_id=1, source_target_pairs={{0,3},{1,0},{2,1},{3,2},{4,7},{5,4},{6,5},{7,6},{8,11},{9,8},{10,9... | collective-permute-start | bytes 331784 | tf_op jit(solution)/shard_map/ppermute | solution.py:47
  30.6 99.1 %all-gather.22.cloned.1.call-start = ((), (), s32[]{:S(2)}) async-start(), calls=%async_computation.3 | async-start | bytes 5308416 | tf_op jit(solution)/shard_map/all_gather | solution.py:59
  31.6 10.2 %collective-permute-start.13 = (bf16[192,384]{1,0:T(8,128)(2,1)S(1)}, bf16[192,384]{1,0:T(8,128)(2,1)S(1)}, u32[]{:S(2)}, u32[]{:S(2)}) collective-permute-start(bf16[192,384]{1,0:T(8,128)(2,1)S(1)} %dynamic_slice.153), channel_id=1, source_target_pairs={{0,2},{1,3},{2,0},{3,1},{4,6},{5,7},{6,4},{7,5},{8,10},{9,11},{10,... | collective-permute-start | bytes 442376 | tf_op jit(solution)/shard_map/ppermute | solution.py:47
  32.9 11.0 %collective-permute-start.12 = (bf16[192,384]{1,0:T(8,128)(2,1)S(1)}, bf16[192,384]{1,0:T(8,128)(2,1)S(1)}, u32[]{:S(2)}, u32[]{:S(2)}) collective-permute-start(bf16[192,384]{1,0:T(8,128)(2,1)S(1)} %dynamic_slice.153), channel_id=1, source_target_pairs={{0,1},{1,2},{2,3},{3,0},{4,5},{5,6},{6,7},{7,4},{8,9},{9,10},{10,1... | collective-permute-start | bytes 442376 | tf_op jit(solution)/shard_map/ppermute | solution.py:47
  33.8 11.5 %collective-permute-start.14 = (bf16[192,384]{1,0:T(8,128)(2,1)S(1)}, bf16[192,384]{1,0:T(8,128)(2,1)S(1)}, u32[]{:S(2)}, u32[]{:S(2)}) collective-permute-start(bf16[192,384]{1,0:T(8,128)(2,1)S(1)} %dynamic_slice.153), channel_id=1, source_target_pairs={{0,3},{1,0},{2,1},{3,2},{4,7},{5,4},{6,5},{7,6},{8,11},{9,8},{10,9... | collective-permute-start | bytes 442376 | tf_op jit(solution)/shard_map/ppermute | solution.py:47
  46.9 115.0 %all-gather.20.cloned.1.call-start = ((), (), s32[]{:S(2)}) async-start(), calls=%async_computation.2 | async-start | bytes 5308416 | tf_op jit(solution)/shard_map/all_gather | solution.py:59
  47.0 12.2 %collective-permute-start.1 = (bf16[6,192]{1,0:T(8,128)(2,1)S(1)}, bf16[6,192]{1,0:T(8,128)(2,1)S(1)}, u32[]{:S(2)}, u32[]{:S(2)}) collective-permute-start(bf16[6,192]{1,0:T(8,128)(2,1)S(1)} %get-tuple-element.150), channel_id=1, source_target_pairs={{0,2},{1,3},{2,0},{3,1},{4,6},{5,7},{6,4},{7,5},{8,10},{9,11},{10,... | collective-permute-start | bytes 6920 | tf_op jit(solution)/shard_map/ppermute | solution.py:47
  47.1 12.2 %collective-permute-start = (bf16[6,192]{1,0:T(8,128)(2,1)S(1)}, bf16[6,192]{1,0:T(8,128)(2,1)S(1)}, u32[]{:S(2)}, u32[]{:S(2)}) collective-permute-start(bf16[6,192]{1,0:T(8,128)(2,1)S(1)} %get-tuple-element.150), channel_id=1, source_target_pairs={{0,1},{1,2},{2,3},{3,0},{4,5},{5,6},{6,7},{7,4},{8,9},{9,10},{10,1... | collective-permute-start | bytes 6920 | tf_op jit(solution)/shard_map/ppermute | solution.py:47
  48.4 10.9 %collective-permute-start.2 = (bf16[6,192]{1,0:T(8,128)(2,1)S(1)}, bf16[6,192]{1,0:T(8,128)(2,1)S(1)}, u32[]{:S(2)}, u32[]{:S(2)}) collective-permute-start(bf16[6,192]{1,0:T(8,128)(2,1)S(1)} %get-tuple-element.150), channel_id=1, source_target_pairs={{0,3},{1,0},{2,1},{3,2},{4,7},{5,4},{6,5},{7,6},{8,11},{9,8},{10,9... | collective-permute-start | bytes 6920 | tf_op jit(solution)/shard_map/ppermute | solution.py:47
  50.5 11.2 %collective-permute-start.10 = (bf16[48,1536]{1,0:T(8,128)(2,1)S(1)}, bf16[48,1536]{1,0:T(8,128)(2,1)S(1)}, u32[]{:S(2)}, u32[]{:S(2)}) collective-permute-start(bf16[48,1536]{1,0:T(8,128)(2,1)S(1)} %dynamic_slice.152), channel_id=1, source_target_pairs={{0,2},{1,3},{2,0},{3,1},{4,6},{5,7},{6,4},{7,5},{8,10},{9,11},{10,... | collective-permute-start | bytes 442376 | tf_op jit(solution)/shard_map/ppermute | solution.py:47
  53.0 9.5 %collective-permute-start.9 = (bf16[48,1536]{1,0:T(8,128)(2,1)S(1)}, bf16[48,1536]{1,0:T(8,128)(2,1)S(1)}, u32[]{:S(2)}, u32[]{:S(2)}) collective-permute-start(bf16[48,1536]{1,0:T(8,128)(2,1)S(1)} %dynamic_slice.152), channel_id=1, source_target_pairs={{0,1},{1,2},{2,3},{3,0},{4,5},{5,6},{6,7},{7,4},{8,9},{9,10},{10,1... | collective-permute-start | bytes 442376 | tf_op jit(solution)/shard_map/ppermute | solution.py:47
  59.3 6.3 %collective-permute-start.11 = (bf16[48,1536]{1,0:T(8,128)(2,1)S(1)}, bf16[48,1536]{1,0:T(8,128)(2,1)S(1)}, u32[]{:S(2)}, u32[]{:S(2)}) collective-permute-start(bf16[48,1536]{1,0:T(8,128)(2,1)S(1)} %dynamic_slice.152), channel_id=1, source_target_pairs={{0,3},{1,0},{2,1},{3,2},{4,7},{5,4},{6,5},{7,6},{8,11},{9,8},{10,9... | collective-permute-start | bytes 442376 | tf_op jit(solution)/shard_map/ppermute | solution.py:47
  67.1 390.8 %all-gather.24.cloned.1.call-start = ((), (), s32[]{:S(2)}) async-start(), calls=%async_computation.4 | async-start | bytes 2211840 | tf_op jit(solution)/shard_map/all_gather | solution.py:110
  278.5 13.1 %collective-permute-start.15 = (bf16[4,4,48,1280]{3,2,1,0:T(8,128)(2,1)}, bf16[4,4,48,1280]{3,2,1,0:T(8,128)(2,1)}, u32[]{:S(2)}, u32[]{:S(2)}) collective-permute-start(bf16[4,4,48,1280]{3,2,1,0:T(8,128)(2,1)} %bitcast.53), channel_id=1, source_target_pairs={{0,4},{4,0},{8,12},{12,8},{16,20},{20,16},{24,28},{28,24},{1,5},{5... | collective-permute-start | bytes 5898248 | tf_op jit(solution)/shard_map/ppermute | solution.py:88
  287.3 20.7 %collective-permute-start.29 = (bf16[4,4,48,1536]{3,2,1,0:T(8,128)(2,1)}, bf16[4,4,48,1536]{3,2,1,0:T(8,128)(2,1)}, u32[]{:S(2)}, u32[]{:S(2)}) collective-permute-start(bf16[4,4,48,1536]{3,2,1,0:T(8,128)(2,1)} %bitcast.80), channel_id=1, source_target_pairs={{0,4},{4,0},{8,12},{12,8},{16,20},{20,16},{24,28},{28,24},{1,5},{5... | collective-permute-start | bytes 7077896 | tf_op jit(solution)/shard_map/ppermute | solution.py:88
  295.6 9.0 %collective-permute-start.16 = (bf16[4,48,1280]{2,1,0:T(8,128)(2,1)S(1)}, bf16[4,48,1280]{2,1,0:T(8,128)(2,1)}, u32[]{:S(2)}, u32[]{:S(2)}) collective-permute-start(bf16[4,48,1280]{2,1,0:T(8,128)(2,1)S(1)} %fusion.60), channel_id=1, source_target_pairs={{0,8},{4,20},{8,0},{12,28},{16,24},{20,4},{24,16},{28,12},{1,9},{5... | collective-permute-start | bytes 1474568 | tf_op jit(solution)/shard_map/ppermute | solution.py:94
  305.9 12.6 %collective-permute-start.17 = (bf16[4,48,1280]{2,1,0:T(8,128)(2,1)S(1)}, bf16[4,48,1280]{2,1,0:T(8,128)(2,1)S(1)}, u32[]{:S(2)}, u32[]{:S(2)}) collective-permute-start(bf16[4,48,1280]{2,1,0:T(8,128)(2,1)S(1)} %get-tuple-element.115), channel_id=1, source_target_pairs={{0,8},{4,12},{8,0},{12,4},{16,24},{20,28},{24,16},{28,20},{1,9},{5... | collective-permute-start | bytes 1474568 | tf_op jit(solution)/shard_map/ppermute | solution.py:101
  307.4 12.2 %collective-permute-start.18 = (bf16[4,48,1280]{2,1,0:T(8,128)(2,1)S(1)}, bf16[4,48,1280]{2,1,0:T(8,128)(2,1)S(1)}, u32[]{:S(2)}, u32[]{:S(2)}) collective-permute-start(bf16[4,48,1280]{2,1,0:T(8,128)(2,1)S(1)} %get-tuple-element.116), channel_id=1, source_target_pairs={{0,16},{4,20},{8,24},{12,28},{16,0},{20,4},{24,8},{28,12},{1,17},{... | collective-permute-start | bytes 1474568 | tf_op jit(solution)/shard_map/ppermute | solution.py:102
  319.9 9.9 %collective-permute-start.19 = (bf16[48,1280]{1,0:T(8,128)(2,1)S(1)}, bf16[48,1280]{1,0:T(8,128)(2,1)S(1)}, u32[]{:S(2)}, u32[]{:S(2)}) collective-permute-start(bf16[48,1280]{1,0:T(8,128)(2,1)S(1)} %get-tuple-element.135), channel_id=1, source_target_pairs={{0,1},{1,2},{2,3},{3,0},{4,5},{5,6},{6,7},{7,4},{8,9},{9,10},{10,1... | collective-permute-start | bytes 368648 | tf_op jit(solution)/shard_map/ppermute | solution.py:107
  321.4 9.5 %collective-permute-start.21 = (bf16[48,1280]{1,0:T(8,128)(2,1)S(1)}, bf16[48,1280]{1,0:T(8,128)(2,1)S(1)}, u32[]{:S(2)}, u32[]{:S(2)}) collective-permute-start(bf16[48,1280]{1,0:T(8,128)(2,1)S(1)} %get-tuple-element.136), channel_id=1, source_target_pairs={{0,3},{1,0},{2,1},{3,2},{4,7},{5,4},{6,5},{7,6},{8,11},{9,8},{10,9... | collective-permute-start | bytes 368648 | tf_op jit(solution)/shard_map/ppermute | solution.py:107
  322.0 9.1 %collective-permute-start.20 = (bf16[48,1280]{1,0:T(8,128)(2,1)S(1)}, bf16[48,1280]{1,0:T(8,128)(2,1)S(1)}, u32[]{:S(2)}, u32[]{:S(2)}) collective-permute-start(bf16[48,1280]{1,0:T(8,128)(2,1)S(1)} %get-tuple-element.137), channel_id=1, source_target_pairs={{0,2},{1,3},{2,0},{3,1},{4,6},{5,7},{6,4},{7,5},{8,10},{9,11},{10,... | collective-permute-start | bytes 368648 | tf_op jit(solution)/shard_map/ppermute | solution.py:107
  325.2 10.1 %collective-permute-start.30 = (bf16[4,48,1536]{2,1,0:T(8,128)(2,1)}, bf16[4,48,1536]{2,1,0:T(8,128)(2,1)S(1)}, u32[]{:S(2)}, u32[]{:S(2)}) collective-permute-start(bf16[4,48,1536]{2,1,0:T(8,128)(2,1)} %fusion.58), channel_id=1, source_target_pairs={{0,8},{4,20},{8,0},{12,28},{16,24},{20,4},{24,16},{28,12},{1,9},{5... | collective-permute-start | bytes 1769480 | tf_op jit(solution)/shard_map/ppermute | solution.py:94
  331.8 131.2 %all-gather.26.cloned.1.call-start = ((), (), s32[]{:S(2)}) async-start(), calls=%async_computation.5 | async-start | bytes 2654208 | tf_op jit(solution)/shard_map/all_gather | solution.py:110
  337.3 14.5 %collective-permute-start.31 = (bf16[4,48,1536]{2,1,0:T(8,128)(2,1)S(1)}, bf16[4,48,1536]{2,1,0:T(8,128)(2,1)S(1)}, u32[]{:S(2)}, u32[]{:S(2)}) collective-permute-start(bf16[4,48,1536]{2,1,0:T(8,128)(2,1)S(1)} %get-tuple-element.107), channel_id=1, source_target_pairs={{0,8},{4,12},{8,0},{12,4},{16,24},{20,28},{24,16},{28,20},{1,9},{5... | collective-permute-start | bytes 1769480 | tf_op jit(solution)/shard_map/ppermute | solution.py:101
  337.9 14.1 %collective-permute-start.32 = (bf16[4,48,1536]{2,1,0:T(8,128)(2,1)S(1)}, bf16[4,48,1536]{2,1,0:T(8,128)(2,1)S(1)}, u32[]{:S(2)}, u32[]{:S(2)}) collective-permute-start(bf16[4,48,1536]{2,1,0:T(8,128)(2,1)S(1)} %get-tuple-element.108), channel_id=1, source_target_pairs={{0,16},{4,20},{8,24},{12,28},{16,0},{20,4},{24,8},{28,12},{1,17},{... | collective-permute-start | bytes 1769480 | tf_op jit(solution)/shard_map/ppermute | solution.py:102
  350.6 19.8 %collective-permute-start.36 = (bf16[4,4,192,384]{3,2,1,0:T(8,128)(2,1)}, bf16[4,4,192,384]{3,2,1,0:T(8,128)(2,1)}, u32[]{:S(2)}, u32[]{:S(2)}) collective-permute-start(bf16[4,4,192,384]{3,2,1,0:T(8,128)(2,1)} %bitcast.93), channel_id=1, source_target_pairs={{0,4},{4,0},{8,12},{12,8},{16,20},{20,16},{24,28},{28,24},{1,5},{5... | collective-permute-start | bytes 7077896 | tf_op jit(solution)/shard_map/ppermute | solution.py:88
  353.6 11.7 %collective-permute-start.33 = (bf16[48,1536]{1,0:T(8,128)(2,1)S(1)}, bf16[48,1536]{1,0:T(8,128)(2,1)S(1)}, u32[]{:S(2)}, u32[]{:S(2)}) collective-permute-start(bf16[48,1536]{1,0:T(8,128)(2,1)S(1)} %get-tuple-element.130), channel_id=1, source_target_pairs={{0,1},{1,2},{2,3},{3,0},{4,5},{5,6},{6,7},{7,4},{8,9},{9,10},{10,1... | collective-permute-start | bytes 442376 | tf_op jit(solution)/shard_map/ppermute | solution.py:107
  355.0 11.5 %collective-permute-start.35 = (bf16[48,1536]{1,0:T(8,128)(2,1)S(1)}, bf16[48,1536]{1,0:T(8,128)(2,1)S(1)}, u32[]{:S(2)}, u32[]{:S(2)}) collective-permute-start(bf16[48,1536]{1,0:T(8,128)(2,1)S(1)} %get-tuple-element.131), channel_id=1, source_target_pairs={{0,3},{1,0},{2,1},{3,2},{4,7},{5,4},{6,5},{7,6},{8,11},{9,8},{10,9... | collective-permute-start | bytes 442376 | tf_op jit(solution)/shard_map/ppermute | solution.py:107
  355.6 11.2 %collective-permute-start.34 = (bf16[48,1536]{1,0:T(8,128)(2,1)S(1)}, bf16[48,1536]{1,0:T(8,128)(2,1)S(1)}, u32[]{:S(2)}, u32[]{:S(2)}) collective-permute-start(bf16[48,1536]{1,0:T(8,128)(2,1)S(1)} %get-tuple-element.132), channel_id=1, source_target_pairs={{0,2},{1,3},{2,0},{3,1},{4,6},{5,7},{6,4},{7,5},{8,10},{9,11},{10,... | collective-permute-start | bytes 442376 | tf_op jit(solution)/shard_map/ppermute | solution.py:107
  367.7 97.2 %all-gather.28.cloned.1.call-start = ((), (), s32[]{:S(2)}) async-start(), calls=%async_computation.6 | async-start | bytes 2654208 | tf_op jit(solution)/shard_map/all_gather | solution.py:110
  372.8 14.7 %collective-permute-start.37 = (bf16[4,192,384]{2,1,0:T(8,128)(2,1)S(1)}, bf16[4,192,384]{2,1,0:T(8,128)(2,1)S(1)}, u32[]{:S(2)}, u32[]{:S(2)}) collective-permute-start(bf16[4,192,384]{2,1,0:T(8,128)(2,1)S(1)} %fusion.59), channel_id=1, source_target_pairs={{0,8},{4,20},{8,0},{12,28},{16,24},{20,4},{24,16},{28,12},{1,9},{5... | collective-permute-start | bytes 1769480 | tf_op jit(solution)/shard_map/ppermute | solution.py:94
  387.8 17.0 %collective-permute-start.38 = (bf16[4,192,384]{2,1,0:T(8,128)(2,1)S(1)}, bf16[4,192,384]{2,1,0:T(8,128)(2,1)S(1)}, u32[]{:S(2)}, u32[]{:S(2)}) collective-permute-start(bf16[4,192,384]{2,1,0:T(8,128)(2,1)S(1)} %get-tuple-element.105), channel_id=1, source_target_pairs={{0,8},{4,12},{8,0},{12,4},{16,24},{20,28},{24,16},{28,20},{1,9},{5... | collective-permute-start | bytes 1769480 | tf_op jit(solution)/shard_map/ppermute | solution.py:101
  389.0 15.9 %collective-permute-start.39 = (bf16[4,192,384]{2,1,0:T(8,128)(2,1)S(1)}, bf16[4,192,384]{2,1,0:T(8,128)(2,1)S(1)}, u32[]{:S(2)}, u32[]{:S(2)}) collective-permute-start(bf16[4,192,384]{2,1,0:T(8,128)(2,1)S(1)} %get-tuple-element.106), channel_id=1, source_target_pairs={{0,16},{4,20},{8,24},{12,28},{16,0},{20,4},{24,8},{28,12},{1,17},{... | collective-permute-start | bytes 1769480 | tf_op jit(solution)/shard_map/ppermute | solution.py:102
  390.2 22.7 %collective-permute-start.22 = (bf16[4,4,48,384]{3,2,1,0:T(8,128)(2,1)S(1)}, bf16[4,4,48,384]{3,2,1,0:T(8,128)(2,1)S(1)}, u32[]{:S(2)}, u32[]{:S(2)}) collective-permute-start(bf16[4,4,48,384]{3,2,1,0:T(8,128)(2,1)S(1)} %bitcast.282), channel_id=1, source_target_pairs={{0,4},{4,0},{8,12},{12,8},{16,20},{20,16},{24,28},{28,24},{1,5},{5... | collective-permute-start | bytes 1769480 | tf_op jit(solution)/shard_map/ppermute | solution.py:88
  405.2 10.3 %collective-permute-start.40 = (bf16[192,384]{1,0:T(8,128)(2,1)S(1)}, bf16[192,384]{1,0:T(8,128)(2,1)S(1)}, u32[]{:S(2)}, u32[]{:S(2)}) collective-permute-start(bf16[192,384]{1,0:T(8,128)(2,1)S(1)} %get-tuple-element.127), channel_id=1, source_target_pairs={{0,1},{1,2},{2,3},{3,0},{4,5},{5,6},{6,7},{7,4},{8,9},{9,10},{10,1... | collective-permute-start | bytes 442376 | tf_op jit(solution)/shard_map/ppermute | solution.py:107
  408.6 10.5 %collective-permute-start.42 = (bf16[192,384]{1,0:T(8,128)(2,1)S(1)}, bf16[192,384]{1,0:T(8,128)(2,1)S(1)}, u32[]{:S(2)}, u32[]{:S(2)}) collective-permute-start(bf16[192,384]{1,0:T(8,128)(2,1)S(1)} %get-tuple-element.128), channel_id=1, source_target_pairs={{0,3},{1,0},{2,1},{3,2},{4,7},{5,4},{6,5},{7,6},{8,11},{9,8},{10,9... | collective-permute-start | bytes 442376 | tf_op jit(solution)/shard_map/ppermute | solution.py:107
  410.5 11.3 %collective-permute-start.41 = (bf16[192,384]{1,0:T(8,128)(2,1)S(1)}, bf16[192,384]{1,0:T(8,128)(2,1)S(1)}, u32[]{:S(2)}, u32[]{:S(2)}) collective-permute-start(bf16[192,384]{1,0:T(8,128)(2,1)S(1)} %get-tuple-element.129), channel_id=1, source_target_pairs={{0,2},{1,3},{2,0},{3,1},{4,6},{5,7},{6,4},{7,5},{8,10},{9,11},{10,... | collective-permute-start | bytes 442376 | tf_op jit(solution)/shard_map/ppermute | solution.py:107
  414.0 16.1 %collective-permute-start.23 = (bf16[4,48,384]{2,1,0:T(8,128)(2,1)S(1)}, bf16[4,48,384]{2,1,0:T(8,128)(2,1)S(1)}, u32[]{:S(2)}, u32[]{:S(2)}) collective-permute-start(bf16[4,48,384]{2,1,0:T(8,128)(2,1)S(1)} %fusion.77), channel_id=1, source_target_pairs={{0,8},{4,20},{8,0},{12,28},{16,24},{20,4},{24,16},{28,12},{1,9},{5... | collective-permute-start | bytes 442376 | tf_op jit(solution)/shard_map/ppermute | solution.py:94
  430.1 8.0 %collective-permute-start.24 = (bf16[4,48,384]{2,1,0:T(8,128)(2,1)S(1)}, bf16[4,48,384]{2,1,0:T(8,128)(2,1)S(1)}, u32[]{:S(2)}, u32[]{:S(2)}) collective-permute-start(bf16[4,48,384]{2,1,0:T(8,128)(2,1)S(1)} %get-tuple-element.125), channel_id=1, source_target_pairs={{0,8},{4,12},{8,0},{12,4},{16,24},{20,28},{24,16},{28,20},{1,9},{5... | collective-permute-start | bytes 442376 | tf_op jit(solution)/shard_map/ppermute | solution.py:101
  431.3 7.0 %collective-permute-start.25 = (bf16[4,48,384]{2,1,0:T(8,128)(2,1)S(1)}, bf16[4,48,384]{2,1,0:T(8,128)(2,1)S(1)}, u32[]{:S(2)}, u32[]{:S(2)}) collective-permute-start(bf16[4,48,384]{2,1,0:T(8,128)(2,1)S(1)} %get-tuple-element.126), channel_id=1, source_target_pairs={{0,16},{4,20},{8,24},{12,28},{16,0},{20,4},{24,8},{28,12},{1,17},{... | collective-permute-start | bytes 442376 | tf_op jit(solution)/shard_map/ppermute | solution.py:102
  438.4 7.0 %collective-permute-start.26 = (bf16[48,384]{1,0:T(8,128)(2,1)S(1)}, bf16[48,384]{1,0:T(8,128)(2,1)S(1)}, u32[]{:S(2)}, u32[]{:S(2)}) collective-permute-start(bf16[48,384]{1,0:T(8,128)(2,1)S(1)} %get-tuple-element.140), channel_id=1, source_target_pairs={{0,1},{1,2},{2,3},{3,0},{4,5},{5,6},{6,7},{7,4},{8,9},{9,10},{10,1... | collective-permute-start | bytes 110600 | tf_op jit(solution)/shard_map/ppermute | solution.py:107
  440.2 5.1 %collective-permute-start.28 = (bf16[48,384]{1,0:T(8,128)(2,1)S(1)}, bf16[48,384]{1,0:T(8,128)(2,1)S(1)}, u32[]{:S(2)}, u32[]{:S(2)}) collective-permute-start(bf16[48,384]{1,0:T(8,128)(2,1)S(1)} %get-tuple-element.141), channel_id=1, source_target_pairs={{0,3},{1,0},{2,1},{3,2},{4,7},{5,4},{6,5},{7,6},{8,11},{9,8},{10,9... | collective-permute-start | bytes 110600 | tf_op jit(solution)/shard_map/ppermute | solution.py:107
  440.8 5.0 %collective-permute-start.27 = (bf16[48,384]{1,0:T(8,128)(2,1)S(1)}, bf16[48,384]{1,0:T(8,128)(2,1)S(1)}, u32[]{:S(2)}, u32[]{:S(2)}) collective-permute-start(bf16[48,384]{1,0:T(8,128)(2,1)S(1)} %get-tuple-element.142), channel_id=1, source_target_pairs={{0,2},{1,3},{2,0},{3,1},{4,6},{5,7},{6,4},{7,5},{8,10},{9,11},{10,... | collective-permute-start | bytes 110600 | tf_op jit(solution)/shard_map/ppermute | solution.py:107
  (69 other events, 655.0 us)
Sparse Core Ops, SparseCore 0:
  16.0 27.0 all-gather.17
  45.6 33.8 all-gather.15
  81.9 38.7 all-gather.21
  123.1 38.7 all-gather.19
  331.9 30.6 all-gather.23
  367.8 35.4 all-gather.25
  422.8 32.6 all-gather.27

commit v10 on v9

--- a/solution.py
+++ b/solution.py
@@ -35,6 +35,20 @@
 
 
 LANES = 128
+
+
+def _plane_gather(z):
+    d = lax.axis_index("dp")
+    c = d % 2
+    a = lax.ppermute(z, "dp", [(i, i ^ 2) for i in range(NDP_FAST)])
+    b = lax.ppermute(z, "dp", [(i, i ^ 4) for i in range(NDP_FAST)])
+    send = jnp.where(c == 0, b, a)
+    diag = lax.ppermute(
+        send, "dp", [(i, i ^ 2) if i % 2 == 0 else (i, i ^ 4) for i in range(NDP_FAST)]
+    )
+    mine = jnp.stack([z, a, b, diag])
+    sib = lax.ppermute(mine, "dp", [(i, i ^ 1) for i in range(NDP_FAST)])
+    return jnp.stack([mine[0], sib[0], mine[1], sib[1], mine[2], sib[2], mine[3], sib[3]])
 
 
 def _take(x, idx, axis):
@@ -107,7 +121,7 @@
         total = total + lax.ppermute(
             part.astype(jnp.bfloat16), "fsdp", [(i, (i + k) % NF_FAST) for i in range(NF_FAST)]
         ).astype(jnp.float32)
-    x = lax.all_gather(total, "dp", axis=0, tiled=False)
+    x = _take(_plane_gather(total), jnp.arange(NDP_FAST, dtype=jnp.int32) ^ d, 0)
     x = x.reshape(n_chips, 2, rows, cols)
     x = jnp.concatenate([x[:, 0], x[:, 1]], axis=-1)
     return x.reshape(n_chips * rows, 2 * cols)

time: 486 us -> 493 us (1.014)
  local copies, waits for them, and re-layouts: 81.1 us -> 98.9 us
  starting transfers between devices: 57.4 us -> 71 us
  waiting for transfers between devices: 130 us -> 117 us
  blocking collectives: 11.1 us -> 0 us
  matrix products: 114 us -> 109 us
    ppermute x0 -> x16, waiting for transfers between devices: none -> 21.5 us  [the longest x4 15 us: _plane_gather(): b = lax.ppermute(z, 'dp', [(i, i ^ 4) for i in range(NDP_FAST)])]
    ppermute x4, waiting for transfers between devices: 21.4 us -> 5.43 us  [_reduce_matrix(): lax.ppermute(of_chip(j ^ 3).astype(jnp.bfloat16), 'dp', [(i, i ^ 2) if i...]
    ppermute x0 -> x16, starting transfers between devices: none -> 13.2 us  [the longest x4 5.48 us: _plane_gather(): a = lax.ppermute(z, 'dp', [(i, i ^ 2) for i in range(NDP_FAST)])]
    all_gather x1 -> x0, blocking collectives: 11.1 us -> none  [_reduce_matrix(): x = lax.all_gather(total, 'dp', axis=0, tiled=False)]
    ppermute x4, waiting for transfers between devices: 29.3 us -> 19.9 us  [_reduce_matrix(): lax.ppermute(to_x.astype(jnp.bfloat16), 'dp', [(i, i ^ 2) for i in range(...]
    unnamed x137 -> x203, local copies, waits for them, and re-layouts: 20.3 us -> 28.9 us
    ppermute x12, waiting for transfers between devices: 21.2 us -> 13.4 us  [_reduce_matrix(): lax.ppermute(part.astype(jnp.bfloat16), 'fsdp', [(i, (i + k) % NF_FAST) f...]
    gather x5 -> x9, local copies, waits for them, and re-layouts: 5.98 us -> 13.5 us  [_take(): return jnp.take(x, idx, axis=axis, mode='wrap')]
  transfers between devices with their start and end apart: 50 -> 63, of which waited for: 30 -> 32; matrix products, arithmetic and copies ran while one was open for 27% -> 40% of each run, Pallas kernels for 0% -> 0%
where the time goes in v10:
time: 493 us; the launch traced here: 483 us
  waiting for transfers between devices  117 us (24%)
  matrix products  109 us (22%)
  local copies, waits for them, and re-layouts  98.9 us (20%)
  other arithmetic  71.1 us (14%)
  starting transfers between devices  71 us (14%)
  between operations  15.9 us (3%)
    all_gather x4, waiting for transfers between devices, _gather_matrix(): x = lax.all_gather(z, 'dp', axis=1, tiled=False)  37 us
    unnamed x203, local copies, waits for them, and re-layouts  28.9 us
    ppermute x15, starting transfers between devices, _z_gather(): lax.ppermute(piece, 'fsdp', [(i, (i + k) % NF_FAST) for i in range(NF_FAS...  22.6 us
    dot_general x1, matrix products, layer(): up_pre = jnp.dot(second_low, full_up, preferred_element_type=jnp.float32)  22.2 us
    ppermute x12, starting transfers between devices, _reduce_matrix(): lax.ppermute(part.astype(jnp.bfloat16), 'fsdp', [(i, (i + k) % NF_FAST) f...  21 us
    ppermute x4, waiting for transfers between devices, _reduce_matrix(): lax.ppermute(to_x.astype(jnp.bfloat16), 'dp', [(i, i ^ 2) for i in range(...  19.9 us
    ppermute x15, waiting for transfers between devices, _z_gather(): lax.ppermute(piece, 'fsdp', [(i, (i + k) % NF_FAST) for i in range(NF_FAS...  18 us
    ppermute x4, waiting for transfers between devices, _plane_gather(): b = lax.ppermute(z, 'dp', [(i, i ^ 4) for i in range(NDP_FAST)])  15 us
  transfers between devices with their start and end apart: 63, of which 32 were waited for; matrix products, arithmetic and copies ran while one was open for 40% of the time, Pallas kernels for 0%

profile of v10, /device:TPU:8, one launch (start us, length us, event | category | flops | bytes accessed | tf_op | source)
XLA Modules:
  0.0 483.1 jit_solution(9313124266271871112)
XLA Ops:
  8.0 2.6 collective-permute-start.7
  16.8 4.7 collective-permute-start.4
  24.5 2.5 collective-permute-done.4
  35.9 5.9 %collective-permute-done.13 = bf16[192,384]{1,0:T(8,128)(2,1)S(1)} collective-permute-done((bf16[192,384]{1,0:T(8,128)(2,1)S(1)}, bf16[192,384]{1,0:T(8,128)(2,1)S(1)}, u32[]{:S(2)}, u32[]{:S(2)}) %collective-permute-start.13) | collective-permute-done | bytes 147488 | tf_op jit(solution)/shard_map/ppermute | solution.py:61
  50.5 2.5 collective-permute-start.10
  53.0 2.8 collective-permute-start.9
  62.9 2.7 collective-permute-done.11
  69.6 9.8 %all-gather.9.cloned.1.call-done = bf16[4,384,1152]{2,1,0:T(8,128)(2,1)} async-done(((bf16[4,48,1152]{2,1,0:T(8,128)(2,1)}), bf16[4,384,1152]{2,1,0:T(8,128)(2,1)}) %all-gather.9.cloned.1.call-update) | async-done | bytes 3538960 | tf_op jit(solution)/shard_map/all_gather | solution.py:73
  88.5 3.7 fusion.125
  101.2 8.4 %fusion.135 = (f32[12,576]{1,0:T(8,128)S(1)}, f32[12,576,576]{1,2,0:T(8,128)}) fusion(f32[576,12,64]{0,2,1:T(8,128)S(1)} %bitcast.271, f32[12,64]{1,0:T(8,128)S(1)} %mul.355, f32[576,12]{0,1:T(8,128)S(1)} %fusion.95, f32[576,12]{0,1:T(8,128)S(1)} %broadcast_multiply_fusion, f32[576,12,64]{0,2,1:T(8,128)S(1)} %bitcast.264, f32[12,64]{1,0:T(8,128)S(1)} %mul.349, ...), kind=kOutput, calls=%fused_computation.324 | convolution fusion | flops 525083904 | bytes 19940352 | tf_op jit(solution)/shard_map/while/body/eval_jaxpr/qhd,khd->hqk/dot_general | solution.py:198
  109.6 8.8 %fusion.3 = f32[12,576]{1,0:T(8,128)S(1)} fusion(f32[12,576,576]{1,2,0:T(8,128)} %get-tuple-element.151, f32[12,576]{1,0:T(8,128)S(1)} %get-tuple-element.150), kind=kLoop, calls=%fused_computation.18 | loop fusion | flops 7955712 | bytes 15980544 | tf_op jit(solution)/shard_map/while/body/eval_jaxpr/reduce_sum | solution.py:208
  118.4 9.5 %fusion.37 = bf16[12,64,576]{2,1,0:T(8,128)(2,1)S(1)} fusion(bf16[576,12,64]{0,2,1:T(8,128)(2,1)S(1)} %bitcast.301, f32[12,576,576]{1,2,0:T(8,128)} %get-tuple-element.151, f32[12,576]{1,0:T(8,128)S(1)} %fusion.3, f32[12,576]{1,0:T(8,128)S(1)} %get-tuple-element.150), kind=kOutput, calls=%fused_computation.110 | convolution fusion | flops 521994240 | bytes 17750016 | tf_op jit(solution)/shard_map/while/body/eval_jaxpr/hqk,khd->qhd/dot_general | solution.py:210
  129.4 5.5 %fusion.126 = (bf16[4,4,1,192,384]{4,3,2,1,0:T(8,128)(2,1)}, bf16[4,4,1,192,384]{4,3,2,1,0:T(8,128)(2,1)}) fusion(bf16[4,4,2,192,384]{4,3,2,1,0:T(8,128)(2,1)} %bitcast.290), kind=kLoop, calls=%fused_computation.315 | loop fusion | bytes 9437184 | tf_op jit(solution)/shard_map/slice | solution.py:75
  134.8 27.1 %all-gather.13.cloned.1.call-done = bf16[4,384,1536]{2,1,0:T(8,128)(2,1)} async-done(((bf16[4,48,1536]{2,1,0:T(8,128)(2,1)}), bf16[4,384,1536]{2,1,0:T(8,128)(2,1)}) %all-gather.13.cloned.1.call-update) | async-done | bytes 4718608 | tf_op jit(solution)/shard_map/all_gather | solution.py:73
  161.9 2.9 fusion.127
  164.8 22.2 %multiply_convert_fusion = (bf16[576,3072]{1,0:T(8,128)(2,1)}, f32[576,3072]{1,0:T(8,128)}, f32[576,3072]{1,0:T(8,128)}) fusion(bf16[768,1536]{1,0:T(8,128)(2,1)S(1)} %bitcast.315, bf16[768,1536]{1,0:T(8,128)(2,1)S(1)} %bitcast.313, f32[576,768]{1,0:T(8,128)S(1)} %get-tuple-element.153, f32[768]{0:T(1024)S(1)} %add.417, f32[768]{0:T(1024)S(1)} %mul.363, ...), kind=kOutput, calls=%fused_computation.28 | convolution fusion | flops 2844573696 | bytes 24193536 | tf_op jit(solution)/shard_map/dot_general | solution.py:220
  187.0 8.1 %add_convert_fusion = bf16[576,3072]{1,0:T(8,128)(2,1)S(1)} fusion(f32[576,3072]{1,0:T(8,128)} %get-tuple-element.103, f32[576,3072]{1,0:T(8,128)} %get-tuple-element.154, bf16[3072,384]{1,0:T(8,128)(2,1)S(1)} %bitcast.311, bf16[3072,384]{1,0:T(8,128)(2,1)S(1)} %bitcast.309, bf16[576,768]{1,0:T(8,128)(2,1)S(1)} %copy-done.14, f32[576]{0:T(1024)S(1)} %fusion.96), kind=kOutput, calls=%fused_computation.27 | convolution fusion | flops 2753445888 | bytes 23300352 | tf_op jit(solution)/shard_map/dot_general | solution.py:229
  195.2 3.2 multiply_reduce_fusion.2
  202.9 7.1 %fusion.117 = f32[768,3072]{1,0:T(8,128)} fusion(bf16[576,3072]{1,0:T(8,128)(2,1)S(1)} %add_convert_fusion, f32[576,768]{1,0:T(8,128)S(1)} %get-tuple-element.153, f32[768]{0:T(1024)S(1)} %add.417, f32[768]{0:T(1024)S(1)} %mul.363, f32[576]{0:T(1024)S(1)} %fusion.98, f32[576]{0:T(1024)S(1)} %broadcast_multiply_fusion.4), kind=kOutput, calls=%fused_computation.311 | convolution fusion | flops 2720120832 | bytes 14756352 | tf_op jit(solution)/shard_map/dot_general | solution.py:232
  210.0 3.9 multiply_convert_fusion.3
  213.9 4.0 fusion.61
  220.7 2.5 constant_dynamic-slice_fusion
  225.3 4.0 convolution_convert_fusion
  229.3 13.2 %fusion.38 = bf16[12,64,576]{2,1,0:T(8,128)(2,1)} fusion(bf16[576,12,64]{0,2,1:T(8,128)(2,1)} %bitcast.288, f32[12,576,576]{1,2,0:T(8,128)} %get-tuple-element.151, f32[12,576]{1,0:T(8,128)S(1)} %log_add_fusion), kind=kOutput, calls=%fused_computation.111 | convolution fusion | flops 518012928 | bytes 17722368 | tf_op jit(solution)/shard_map/hqk,qhd->khd/dot_general | solution.py:248
  242.5 4.2 dynamic-slice_convert_fusion.1
  247.2 9.3 %fusion = f32[12,576]{1,0:T(8,128)S(1)} fusion(bf16[12,576,576]{1,2,0:T(8,128)(2,1)S(1)} %convolution_convert_fusion, f32[12,576,576]{1,2,0:T(8,128)} %get-tuple-element.151, f32[12,576]{1,0:T(8,128)S(1)} %log_add_fusion), kind=kLoop, calls=%fused_computation.11 | loop fusion | flops 15918336 | bytes 23943168 | tf_op jit(solution)/shard_map/reduce_sum | solution.py:251
  256.7 9.5 %fusion.2 = bf16[12,576,576]{1,2,0:T(8,128)(2,1)} fusion(bf16[12,576,576]{1,2,0:T(8,128)(2,1)} %copy-done.4, f32[12,576,576]{1,2,0:T(8,128)S(1)} %bitcast.261, f32[12,576]{1,0:T(8,128)S(1)} %fusion, f32[12,576]{1,0:T(8,128)S(1)} %log_add_fusion), kind=kLoop, calls=%fused_computation.13 | loop fusion | flops 19906560 | bytes 31905792 | tf_op jit(solution)/shard_map/convert_element_type | solution.py:252
  266.2 6.3 %fusion.29 = (f32[576,12]{0,1:T(8,128)S(1)}, f32[12,64,576]{2,1,0:T(8,128)S(1)}) fusion(f32[576,12,64]{0,2,1:T(8,128)S(1)} %bitcast.272, f32[12,64]{1,0:T(8,128)S(1)} %copy-done.51, f32[576,12]{0,1:T(8,128)S(1)} %copy-done.19, bf16[12,576,576]{1,2,0:T(8,128)(2,1)} %fusion.2, f32[576,12,64]{0,2,1:T(8,128)S(1)} %bitcast.265, f32[12,64]{1,0:T(8,128)S(1)} %copy-done.53, ...), kind=kOutput, calls=%fused_computation.80 | convolution fusion | flops 513139968 | bytes 13387776 | tf_op jit(solution)/shard_map/hqk,qhd->khd/dot_general | solution.py:257
  272.5 5.3 %fusion.30 = (f32[576,12]{0,1:T(8,128)S(1)}, f32[12,64,576]{2,1,0:T(8,128)S(1)}) fusion(f32[576,12,64]{0,2,1:T(8,128)S(1)} %bitcast.266, f32[12,64]{1,0:T(8,128)S(1)} %copy-done.48, f32[576,12]{0,1:T(8,128)S(1)} %copy-done.17, bf16[12,576,576]{1,2,0:T(8,128)(2,1)} %fusion.2, f32[576,12,64]{0,2,1:T(8,128)S(1)} %bitcast.273, f32[12,64]{1,0:T(8,128)S(1)} %copy-done.50, ...), kind=kOutput, calls=%fused_computation.83 | convolution fusion | flops 513139968 | bytes 13387776 | tf_op jit(solution)/shard_map/hqk,khd->qhd/dot_general | solution.py:254
  284.1 2.8 fusion.118
  289.5 5.4 %fusion.41 = f32[768,2304]{1,0:T(8,128)S(1)} fusion(bf16[576,768]{0,1:T(8,128)(2,1)} %bitcast.335, bf16[576,768]{0,1:T(8,128)(2,1)} %bitcast.332, bf16[576,768]{0,1:T(8,128)(2,1)} %bitcast.334, bf16[576,768]{1,0:T(8,128)(2,1)S(1)} %copy-done.8, f32[768]{0:T(1024)S(1)} %copy-done.68, f32[768]{0:T(1024)S(1)} %copy-done.61, f32[576]{0:T(1024)S(1)} %copy-done.59, ...), kind=kOutput, calls=%fused_computation.115 | convolution fusion | flops 2049048576 | bytes 10627584 | tf_op jit(solution)/shard_map/dot_general | solution.py:275
  304.8 3.4 collective-permute-done.28
  312.5 2.4 collective-permute-start.31
  319.3 2.7 constant_dynamic-slice_fusion.1
  330.6 2.7 convert_add_fusion.2
  334.5 2.6 convert_add_fusion.1
  338.3 4.0 collective-permute-done.16
  347.9 11.3 %collective-permute-done.17 = bf16[4,48,1280]{2,1,0:T(8,128)(2,1)S(1)} collective-permute-done((bf16[4,48,1280]{2,1,0:T(8,128)(2,1)S(1)}, bf16[4,48,1280]{2,1,0:T(8,128)(2,1)S(1)}, u32[]{:S(2)}, u32[]{:S(2)}) %collective-permute-start.17) | collective-permute-done | bytes 491552 | tf_op jit(solution)/shard_map/ppermute | solution.py:115
  366.8 2.7 collective-permute-done.21
  376.1 8.3 %collective-permute-done.23 = f32[48,1280]{1,0:T(8,128)S(1)} collective-permute-done((f32[48,1280]{1,0:T(8,128)S(1)}, f32[48,1280]{1,0:T(8,128)S(1)}, u32[]{:S(2)}, u32[]{:S(2)}) %collective-permute-start.23) | collective-permute-done | bytes 245792 | tf_op jit(solution)/shard_map/ppermute | solution.py:44
  387.3 2.9 collective-permute-start.41
  391.2 5.2 %collective-permute-done.50 = bf16[4,192,384]{2,1,0:T(8,128)(2,1)S(1)} collective-permute-done((bf16[4,192,384]{2,1,0:T(8,128)(2,1)S(1)}, bf16[4,192,384]{2,1,0:T(8,128)(2,1)S(1)}, u32[]{:S(2)}, u32[]{:S(2)}) %collective-permute-start.50) | collective-permute-done | bytes 589856 | tf_op jit(solution)/shard_map/ppermute | solution.py:115
  396.4 2.4 collective-permute-start.42
  400.1 2.5 collective-permute-start.52
  405.4 5.4 %collective-permute-done.42 = bf16[48,1536]{1,0:T(8,128)(2,1)S(1)} collective-permute-done((bf16[48,1536]{1,0:T(8,128)(2,1)S(1)}, bf16[48,1536]{1,0:T(8,128)(2,1)S(1)}, u32[]{:S(2)}, u32[]{:S(2)}) %collective-permute-start.42) | collective-permute-done | bytes 147488 | tf_op jit(solution)/shard_map/ppermute | solution.py:121
  420.7 6.2 %collective-permute-done.56 = f32[192,384]{1,0:T(8,128)S(1)} collective-permute-done((f32[192,384]{1,0:T(8,128)S(1)}, f32[192,384]{1,0:T(8,128)S(1)}, u32[]{:S(2)}, u32[]{:S(2)}) %collective-permute-start.56) | collective-permute-done | bytes 294944 | tf_op jit(solution)/shard_map/ppermute | solution.py:44
  430.3 3.3 collective-permute-done.57
  445.3 2.5 pad_maximum_fusion.14
  (458 shorter events, 186.5 us)
Async XLA Ops:
  7.2 60.0 %all-gather.11.cloned.1.call-start = ((), (), s32[]{:S(2)}) async-start(), calls=%async_computation.1 | async-start | bytes 1327104 | tf_op jit(solution)/shard_map/all_gather | solution.py:73
  15.9 63.6 %all-gather.9.cloned.1.call-start = ((), (), s32[]{:S(2)}) async-start(), calls=%async_computation | async-start | bytes 3981312 | tf_op jit(solution)/shard_map/all_gather | solution.py:73
  16.8 10.1 %collective-permute-start.4 = (bf16[48,1152]{1,0:T(8,128)(2,1)S(1)}, bf16[48,1152]{1,0:T(8,128)(2,1)S(1)}, u32[]{:S(2)}, u32[]{:S(2)}) collective-permute-start(bf16[48,1152]{1,0:T(8,128)(2,1)S(1)} %dynamic_slice.150), channel_id=1, source_target_pairs={{0,2},{1,3},{2,0},{3,1},{4,6},{5,7},{6,4},{7,5},{8,10},{9,11},{10,... | collective-permute-start | bytes 331784 | tf_op jit(solution)/shard_map/ppermute | solution.py:61
  21.5 6.6 %collective-permute-start.3 = (bf16[48,1152]{1,0:T(8,128)(2,1)S(1)}, bf16[48,1152]{1,0:T(8,128)(2,1)S(1)}, u32[]{:S(2)}, u32[]{:S(2)}) collective-permute-start(bf16[48,1152]{1,0:T(8,128)(2,1)S(1)} %dynamic_slice.150), channel_id=1, source_target_pairs={{0,1},{1,2},{2,3},{3,0},{4,5},{5,6},{6,7},{7,4},{8,9},{9,10},{10,1... | collective-permute-start | bytes 331784 | tf_op jit(solution)/shard_map/ppermute | solution.py:61
  21.5 7.6 %collective-permute-start.5 = (bf16[48,1152]{1,0:T(8,128)(2,1)S(1)}, bf16[48,1152]{1,0:T(8,128)(2,1)S(1)}, u32[]{:S(2)}, u32[]{:S(2)}) collective-permute-start(bf16[48,1152]{1,0:T(8,128)(2,1)S(1)} %dynamic_slice.150), channel_id=1, source_target_pairs={{0,3},{1,0},{2,1},{3,2},{4,7},{5,4},{6,5},{7,6},{8,11},{9,8},{10,9... | collective-permute-start | bytes 331784 | tf_op jit(solution)/shard_map/ppermute | solution.py:61
  30.6 98.8 %all-gather.15.cloned.1.call-start = ((), (), s32[]{:S(2)}) async-start(), calls=%async_computation.3 | async-start | bytes 5308416 | tf_op jit(solution)/shard_map/all_gather | solution.py:73
  31.6 10.2 %collective-permute-start.13 = (bf16[192,384]{1,0:T(8,128)(2,1)S(1)}, bf16[192,384]{1,0:T(8,128)(2,1)S(1)}, u32[]{:S(2)}, u32[]{:S(2)}) collective-permute-start(bf16[192,384]{1,0:T(8,128)(2,1)S(1)} %dynamic_slice.153), channel_id=1, source_target_pairs={{0,2},{1,3},{2,0},{3,1},{4,6},{5,7},{6,4},{7,5},{8,10},{9,11},{10,... | collective-permute-start | bytes 442376 | tf_op jit(solution)/shard_map/ppermute | solution.py:61
  32.9 11.0 %collective-permute-start.12 = (bf16[192,384]{1,0:T(8,128)(2,1)S(1)}, bf16[192,384]{1,0:T(8,128)(2,1)S(1)}, u32[]{:S(2)}, u32[]{:S(2)}) collective-permute-start(bf16[192,384]{1,0:T(8,128)(2,1)S(1)} %dynamic_slice.153), channel_id=1, source_target_pairs={{0,1},{1,2},{2,3},{3,0},{4,5},{5,6},{6,7},{7,4},{8,9},{9,10},{10,1... | collective-permute-start | bytes 442376 | tf_op jit(solution)/shard_map/ppermute | solution.py:61
  33.8 11.5 %collective-permute-start.14 = (bf16[192,384]{1,0:T(8,128)(2,1)S(1)}, bf16[192,384]{1,0:T(8,128)(2,1)S(1)}, u32[]{:S(2)}, u32[]{:S(2)}) collective-permute-start(bf16[192,384]{1,0:T(8,128)(2,1)S(1)} %dynamic_slice.153), channel_id=1, source_target_pairs={{0,3},{1,0},{2,1},{3,2},{4,7},{5,4},{6,5},{7,6},{8,11},{9,8},{10,9... | collective-permute-start | bytes 442376 | tf_op jit(solution)/shard_map/ppermute | solution.py:61
  46.9 115.0 %all-gather.13.cloned.1.call-start = ((), (), s32[]{:S(2)}) async-start(), calls=%async_computation.2 | async-start | bytes 5308416 | tf_op jit(solution)/shard_map/all_gather | solution.py:73
  47.0 13.5 %collective-permute-start.1 = (bf16[6,192]{1,0:T(8,128)(2,1)S(1)}, bf16[6,192]{1,0:T(8,128)(2,1)S(1)}, u32[]{:S(2)}, u32[]{:S(2)}) collective-permute-start(bf16[6,192]{1,0:T(8,128)(2,1)S(1)} %get-tuple-element.149), channel_id=1, source_target_pairs={{0,2},{1,3},{2,0},{3,1},{4,6},{5,7},{6,4},{7,5},{8,10},{9,11},{10,... | collective-permute-start | bytes 6920 | tf_op jit(solution)/shard_map/ppermute | solution.py:61
  47.1 13.5 %collective-permute-start = (bf16[6,192]{1,0:T(8,128)(2,1)S(1)}, bf16[6,192]{1,0:T(8,128)(2,1)S(1)}, u32[]{:S(2)}, u32[]{:S(2)}) collective-permute-start(bf16[6,192]{1,0:T(8,128)(2,1)S(1)} %get-tuple-element.149), channel_id=1, source_target_pairs={{0,1},{1,2},{2,3},{3,0},{4,5},{5,6},{6,7},{7,4},{8,9},{9,10},{10,1... | collective-permute-start | bytes 6920 | tf_op jit(solution)/shard_map/ppermute | solution.py:61
  48.4 12.1 %collective-permute-start.2 = (bf16[6,192]{1,0:T(8,128)(2,1)S(1)}, bf16[6,192]{1,0:T(8,128)(2,1)S(1)}, u32[]{:S(2)}, u32[]{:S(2)}) collective-permute-start(bf16[6,192]{1,0:T(8,128)(2,1)S(1)} %get-tuple-element.149), channel_id=1, source_target_pairs={{0,3},{1,0},{2,1},{3,2},{4,7},{5,4},{6,5},{7,6},{8,11},{9,8},{10,9... | collective-permute-start | bytes 6920 | tf_op jit(solution)/shard_map/ppermute | solution.py:61
  50.5 12.5 %collective-permute-start.10 = (bf16[48,1536]{1,0:T(8,128)(2,1)S(1)}, bf16[48,1536]{1,0:T(8,128)(2,1)S(1)}, u32[]{:S(2)}, u32[]{:S(2)}) collective-permute-start(bf16[48,1536]{1,0:T(8,128)(2,1)S(1)} %dynamic_slice.152), channel_id=1, source_target_pairs={{0,2},{1,3},{2,0},{3,1},{4,6},{5,7},{6,4},{7,5},{8,10},{9,11},{10,... | collective-permute-start | bytes 442376 | tf_op jit(solution)/shard_map/ppermute | solution.py:61
  53.0 9.9 %collective-permute-start.9 = (bf16[48,1536]{1,0:T(8,128)(2,1)S(1)}, bf16[48,1536]{1,0:T(8,128)(2,1)S(1)}, u32[]{:S(2)}, u32[]{:S(2)}) collective-permute-start(bf16[48,1536]{1,0:T(8,128)(2,1)S(1)} %dynamic_slice.152), channel_id=1, source_target_pairs={{0,1},{1,2},{2,3},{3,0},{4,5},{5,6},{6,7},{7,4},{8,9},{9,10},{10,1... | collective-permute-start | bytes 442376 | tf_op jit(solution)/shard_map/ppermute | solution.py:61
  225.0 70.0 %collective-permute-start.26 = (bf16[4,4,48,384]{3,2,1,0:T(8,128)(2,1)S(1)}, bf16[4,4,48,384]{3,2,1,0:T(8,128)(2,1)}, u32[]{:S(2)}, u32[]{:S(2)}) collective-permute-start(bf16[4,4,48,384]{3,2,1,0:T(8,128)(2,1)S(1)} %bitcast.341), channel_id=1, source_target_pairs={{0,4},{4,0},{8,12},{12,8},{16,20},{20,16},{24,28},{28,24},{1,5},{5... | collective-permute-start | bytes 1769480 | tf_op jit(solution)/shard_map/ppermute | solution.py:102
  246.7 87.7 %collective-permute-start.37 = (bf16[4,4,48,1536]{3,2,1,0:T(8,128)(2,1)}, bf16[4,4,48,1536]{3,2,1,0:T(8,128)(2,1)}, u32[]{:S(2)}, u32[]{:S(2)}) collective-permute-start(bf16[4,4,48,1536]{3,2,1,0:T(8,128)(2,1)} %bitcast.89), channel_id=1, source_target_pairs={{0,4},{4,0},{8,12},{12,8},{16,20},{20,16},{24,28},{28,24},{1,5},{5... | collective-permute-start | bytes 7077896 | tf_op jit(solution)/shard_map/ppermute | solution.py:102
  247.0 97.8 %collective-permute-start.48 = (bf16[4,4,192,384]{3,2,1,0:T(8,128)(2,1)}, bf16[4,4,192,384]{3,2,1,0:T(8,128)(2,1)}, u32[]{:S(2)}, u32[]{:S(2)}) collective-permute-start(bf16[4,4,192,384]{3,2,1,0:T(8,128)(2,1)} %bitcast.307), channel_id=1, source_target_pairs={{0,4},{4,0},{8,12},{12,8},{16,20},{20,16},{24,28},{28,24},{1,5},{5... | collective-permute-start | bytes 7077896 | tf_op jit(solution)/shard_map/ppermute | solution.py:102
  310.4 6.3 %collective-permute-start.30 = (bf16[48,384]{1,0:T(8,128)(2,1)S(1)}, bf16[48,384]{1,0:T(8,128)(2,1)S(1)}, u32[]{:S(2)}, u32[]{:S(2)}) collective-permute-start(bf16[48,384]{1,0:T(8,128)(2,1)S(1)} %get-tuple-element.139), channel_id=1, source_target_pairs={{0,1},{1,2},{2,3},{3,0},{4,5},{5,6},{6,7},{7,4},{8,9},{9,10},{10,1... | collective-permute-start | bytes 110600 | tf_op jit(solution)/shard_map/ppermute | solution.py:121
  333.4 8.9 %collective-permute-start.16 = (bf16[4,48,1280]{2,1,0:T(8,128)(2,1)S(1)}, bf16[4,48,1280]{2,1,0:T(8,128)(2,1)S(1)}, u32[]{:S(2)}, u32[]{:S(2)}) collective-permute-start(bf16[4,48,1280]{2,1,0:T(8,128)(2,1)S(1)} %fusion.60), channel_id=1, source_target_pairs={{0,8},{4,20},{8,0},{12,28},{16,24},{20,4},{24,16},{28,12},{1,9},{5... | collective-permute-start | bytes 1474568 | tf_op jit(solution)/shard_map/ppermute | solution.py:108
  337.2 27.1 %collective-permute-start.38 = (bf16[4,48,1536]{2,1,0:T(8,128)(2,1)S(1)}, bf16[4,48,1536]{2,1,0:T(8,128)(2,1)S(1)}, u32[]{:S(2)}, u32[]{:S(2)}) collective-permute-start(bf16[4,48,1536]{2,1,0:T(8,128)(2,1)S(1)} %fusion.58), channel_id=1, source_target_pairs={{0,8},{4,20},{8,0},{12,28},{16,24},{20,4},{24,16},{28,12},{1,9},{5... | collective-permute-start | bytes 1769480 | tf_op jit(solution)/shard_map/ppermute | solution.py:108
  342.5 16.6 %collective-permute-start.17 = (bf16[4,48,1280]{2,1,0:T(8,128)(2,1)S(1)}, bf16[4,48,1280]{2,1,0:T(8,128)(2,1)S(1)}, u32[]{:S(2)}, u32[]{:S(2)}) collective-permute-start(bf16[4,48,1280]{2,1,0:T(8,128)(2,1)S(1)} %get-tuple-element.114), channel_id=1, source_target_pairs={{0,8},{4,12},{8,0},{12,4},{16,24},{20,28},{24,16},{28,20},{1,9},{5... | collective-permute-start | bytes 1474568 | tf_op jit(solution)/shard_map/ppermute | solution.py:115
  343.5 15.6 %collective-permute-start.18 = (bf16[4,48,1280]{2,1,0:T(8,128)(2,1)S(1)}, bf16[4,48,1280]{2,1,0:T(8,128)(2,1)S(1)}, u32[]{:S(2)}, u32[]{:S(2)}) collective-permute-start(bf16[4,48,1280]{2,1,0:T(8,128)(2,1)S(1)} %get-tuple-element.115), channel_id=1, source_target_pairs={{0,16},{4,20},{8,24},{12,28},{16,0},{20,4},{24,8},{28,12},{1,17},{... | collective-permute-start | bytes 1474568 | tf_op jit(solution)/shard_map/ppermute | solution.py:116
  347.2 27.6 %collective-permute-start.49 = (bf16[4,192,384]{2,1,0:T(8,128)(2,1)S(1)}, bf16[4,192,384]{2,1,0:T(8,128)(2,1)S(1)}, u32[]{:S(2)}, u32[]{:S(2)}) collective-permute-start(bf16[4,192,384]{2,1,0:T(8,128)(2,1)S(1)} %fusion.59), channel_id=1, source_target_pairs={{0,8},{4,20},{8,0},{12,28},{16,24},{20,4},{24,16},{28,12},{1,9},{5... | collective-permute-start | bytes 1769480 | tf_op jit(solution)/shard_map/ppermute | solution.py:108
  360.9 8.6 %collective-permute-start.21 = (bf16[48,1280]{1,0:T(8,128)(2,1)S(1)}, bf16[48,1280]{1,0:T(8,128)(2,1)S(1)}, u32[]{:S(2)}, u32[]{:S(2)}) collective-permute-start(bf16[48,1280]{1,0:T(8,128)(2,1)S(1)} %get-tuple-element.135), channel_id=1, source_target_pairs={{0,3},{1,0},{2,1},{3,2},{4,7},{5,4},{6,5},{7,6},{8,11},{9,8},{10,9... | collective-permute-start | bytes 368648 | tf_op jit(solution)/shard_map/ppermute | solution.py:121
  361.8 10.0 %collective-permute-start.20 = (bf16[48,1280]{1,0:T(8,128)(2,1)S(1)}, bf16[48,1280]{1,0:T(8,128)(2,1)S(1)}, u32[]{:S(2)}, u32[]{:S(2)}) collective-permute-start(bf16[48,1280]{1,0:T(8,128)(2,1)S(1)} %get-tuple-element.136), channel_id=1, source_target_pairs={{0,2},{1,3},{2,0},{3,1},{4,6},{5,7},{6,4},{7,5},{8,10},{9,11},{10,... | collective-permute-start | bytes 368648 | tf_op jit(solution)/shard_map/ppermute | solution.py:121
  364.5 22.5 %collective-permute-start.39 = (bf16[4,48,1536]{2,1,0:T(8,128)(2,1)S(1)}, bf16[4,48,1536]{2,1,0:T(8,128)(2,1)S(1)}, u32[]{:S(2)}, u32[]{:S(2)}) collective-permute-start(bf16[4,48,1536]{2,1,0:T(8,128)(2,1)S(1)} %get-tuple-element.106), channel_id=1, source_target_pairs={{0,8},{4,12},{8,0},{12,4},{16,24},{20,28},{24,16},{28,20},{1,9},{5... | collective-permute-start | bytes 1769480 | tf_op jit(solution)/shard_map/ppermute | solution.py:115
  365.5 21.6 %collective-permute-start.40 = (bf16[4,48,1536]{2,1,0:T(8,128)(2,1)S(1)}, bf16[4,48,1536]{2,1,0:T(8,128)(2,1)S(1)}, u32[]{:S(2)}, u32[]{:S(2)}) collective-permute-start(bf16[4,48,1536]{2,1,0:T(8,128)(2,1)S(1)} %get-tuple-element.107), channel_id=1, source_target_pairs={{0,16},{4,20},{8,24},{12,28},{16,0},{20,4},{24,8},{28,12},{1,17},{... | collective-permute-start | bytes 1769480 | tf_op jit(solution)/shard_map/ppermute | solution.py:116
  372.6 11.8 %collective-permute-start.23 = (f32[48,1280]{1,0:T(8,128)S(1)}, f32[48,1280]{1,0:T(8,128)S(1)}, u32[]{:S(2)}, u32[]{:S(2)}) collective-permute-start(f32[48,1280]{1,0:T(8,128)S(1)} %get-tuple-element.99), channel_id=1, source_target_pairs={{0,16},{4,20},{8,24},{12,28},{16,0},{20,4},{24,8},{28,12},{1,17},{... | collective-permute-start | bytes 737288 | tf_op jit(solution)/shard_map/ppermute | solution.py:44
  373.8 12.3 %collective-permute-start.22 = (f32[48,1280]{1,0:T(8,128)S(1)}, f32[48,1280]{1,0:T(8,128)S(1)}, u32[]{:S(2)}, u32[]{:S(2)}) collective-permute-start(f32[48,1280]{1,0:T(8,128)S(1)} %get-tuple-element.99), channel_id=1, source_target_pairs={{0,8},{4,12},{8,0},{12,4},{16,24},{20,28},{24,16},{28,20},{1,9},{5... | collective-permute-start | bytes 737288 | tf_op jit(solution)/shard_map/ppermute | solution.py:43
  375.1 21.2 %collective-permute-start.50 = (bf16[4,192,384]{2,1,0:T(8,128)(2,1)S(1)}, bf16[4,192,384]{2,1,0:T(8,128)(2,1)S(1)}, u32[]{:S(2)}, u32[]{:S(2)}) collective-permute-start(bf16[4,192,384]{2,1,0:T(8,128)(2,1)S(1)} %get-tuple-element.104), channel_id=1, source_target_pairs={{0,8},{4,12},{8,0},{12,4},{16,24},{20,28},{24,16},{28,20},{1,9},{5... | collective-permute-start | bytes 1769480 | tf_op jit(solution)/shard_map/ppermute | solution.py:115
  384.4 15.4 %collective-permute-start.51 = (bf16[4,192,384]{2,1,0:T(8,128)(2,1)S(1)}, bf16[4,192,384]{2,1,0:T(8,128)(2,1)S(1)}, u32[]{:S(2)}, u32[]{:S(2)}) collective-permute-start(bf16[4,192,384]{2,1,0:T(8,128)(2,1)S(1)} %get-tuple-element.105), channel_id=1, source_target_pairs={{0,16},{4,20},{8,24},{12,28},{16,0},{20,4},{24,8},{28,12},{1,17},{... | collective-permute-start | bytes 1769480 | tf_op jit(solution)/shard_map/ppermute | solution.py:116
  386.1 25.5 %collective-permute-start.24 = (f32[48,1280]{1,0:T(8,128)S(1)}, f32[48,1280]{1,0:T(8,128)S(1)}, u32[]{:S(2)}, u32[]{:S(2)}) collective-permute-start(f32[48,1280]{1,0:T(8,128)S(1)} %broadcast_select_fusion.2), channel_id=1, source_target_pairs={{0,8},{4,20},{8,0},{12,28},{16,24},{20,4},{24,16},{28,12},{1,9},{5... | collective-permute-start | bytes 737288 | tf_op jit(solution)/shard_map/ppermute | solution.py:46
  387.3 15.3 %collective-permute-start.41 = (bf16[48,1536]{1,0:T(8,128)(2,1)S(1)}, bf16[48,1536]{1,0:T(8,128)(2,1)S(1)}, u32[]{:S(2)}, u32[]{:S(2)}) collective-permute-start(bf16[48,1536]{1,0:T(8,128)(2,1)S(1)} %get-tuple-element.129), channel_id=1, source_target_pairs={{0,1},{1,2},{2,3},{3,0},{4,5},{5,6},{6,7},{7,4},{8,9},{9,10},{10,1... | collective-permute-start | bytes 442376 | tf_op jit(solution)/shard_map/ppermute | solution.py:121
  390.2 12.9 %collective-permute-start.43 = (bf16[48,1536]{1,0:T(8,128)(2,1)S(1)}, bf16[48,1536]{1,0:T(8,128)(2,1)S(1)}, u32[]{:S(2)}, u32[]{:S(2)}) collective-permute-start(bf16[48,1536]{1,0:T(8,128)(2,1)S(1)} %get-tuple-element.130), channel_id=1, source_target_pairs={{0,3},{1,0},{2,1},{3,2},{4,7},{5,4},{6,5},{7,6},{8,11},{9,8},{10,9... | collective-permute-start | bytes 442376 | tf_op jit(solution)/shard_map/ppermute | solution.py:121
  396.4 14.4 %collective-permute-start.42 = (bf16[48,1536]{1,0:T(8,128)(2,1)S(1)}, bf16[48,1536]{1,0:T(8,128)(2,1)S(1)}, u32[]{:S(2)}, u32[]{:S(2)}) collective-permute-start(bf16[48,1536]{1,0:T(8,128)(2,1)S(1)} %get-tuple-element.131), channel_id=1, source_target_pairs={{0,2},{1,3},{2,0},{3,1},{4,6},{5,7},{6,4},{7,5},{8,10},{9,11},{10,... | collective-permute-start | bytes 442376 | tf_op jit(solution)/shard_map/ppermute | solution.py:121
  400.1 14.0 %collective-permute-start.52 = (bf16[192,384]{1,0:T(8,128)(2,1)S(1)}, bf16[192,384]{1,0:T(8,128)(2,1)S(1)}, u32[]{:S(2)}, u32[]{:S(2)}) collective-permute-start(bf16[192,384]{1,0:T(8,128)(2,1)S(1)} %get-tuple-element.126), channel_id=1, source_target_pairs={{0,1},{1,2},{2,3},{3,0},{4,5},{5,6},{6,7},{7,4},{8,9},{9,10},{10,1... | collective-permute-start | bytes 442376 | tf_op jit(solution)/shard_map/ppermute | solution.py:121
  402.6 12.5 %collective-permute-start.54 = (bf16[192,384]{1,0:T(8,128)(2,1)S(1)}, bf16[192,384]{1,0:T(8,128)(2,1)S(1)}, u32[]{:S(2)}, u32[]{:S(2)}) collective-permute-start(bf16[192,384]{1,0:T(8,128)(2,1)S(1)} %get-tuple-element.127), channel_id=1, source_target_pairs={{0,3},{1,0},{2,1},{3,2},{4,7},{5,4},{6,5},{7,6},{8,11},{9,8},{10,9... | collective-permute-start | bytes 442376 | tf_op jit(solution)/shard_map/ppermute | solution.py:121
  403.1 13.1 %collective-permute-start.53 = (bf16[192,384]{1,0:T(8,128)(2,1)S(1)}, bf16[192,384]{1,0:T(8,128)(2,1)S(1)}, u32[]{:S(2)}, u32[]{:S(2)}) collective-permute-start(bf16[192,384]{1,0:T(8,128)(2,1)S(1)} %get-tuple-element.128), channel_id=1, source_target_pairs={{0,2},{1,3},{2,0},{3,1},{4,6},{5,7},{6,4},{7,5},{8,10},{9,11},{10,... | collective-permute-start | bytes 442376 | tf_op jit(solution)/shard_map/ppermute | solution.py:121
  411.6 7.6 %collective-permute-start.45 = (f32[48,1536]{1,0:T(8,128)S(1)}, f32[48,1536]{1,0:T(8,128)S(1)}, u32[]{:S(2)}, u32[]{:S(2)}) collective-permute-start(f32[48,1536]{1,0:T(8,128)S(1)} %get-tuple-element.95), channel_id=1, source_target_pairs={{0,16},{4,20},{8,24},{12,28},{16,0},{20,4},{24,8},{28,12},{1,17},{... | collective-permute-start | bytes 884744 | tf_op jit(solution)/shard_map/ppermute | solution.py:44
  411.6 7.6 %collective-permute-start.44 = (f32[48,1536]{1,0:T(8,128)S(1)}, f32[48,1536]{1,0:T(8,128)S(1)}, u32[]{:S(2)}, u32[]{:S(2)}) collective-permute-start(f32[48,1536]{1,0:T(8,128)S(1)} %get-tuple-element.95), channel_id=1, source_target_pairs={{0,8},{4,12},{8,0},{12,4},{16,24},{20,28},{24,16},{28,20},{1,9},{5... | collective-permute-start | bytes 884744 | tf_op jit(solution)/shard_map/ppermute | solution.py:43
  414.1 20.8 %collective-permute-start.25 = (f32[4,48,1280]{2,1,0:T(8,128)S(1)}, f32[4,48,1280]{2,1,0:T(8,128)S(1)}, u32[]{:S(2)}, u32[]{:S(2)}) collective-permute-start(f32[4,48,1280]{2,1,0:T(8,128)S(1)} %pad_maximum_fusion.22), channel_id=1, source_target_pairs={{0,4},{4,0},{8,12},{12,8},{16,20},{20,16},{24,28},{28,24},{1,5},{5... | collective-permute-start | bytes 2949128 | tf_op jit(solution)/shard_map/ppermute | solution.py:50
  417.0 9.9 %collective-permute-start.56 = (f32[192,384]{1,0:T(8,128)S(1)}, f32[192,384]{1,0:T(8,128)S(1)}, u32[]{:S(2)}, u32[]{:S(2)}) collective-permute-start(f32[192,384]{1,0:T(8,128)S(1)} %get-tuple-element.93), channel_id=1, source_target_pairs={{0,16},{4,20},{8,24},{12,28},{16,0},{20,4},{24,8},{28,12},{1,17},{... | collective-permute-start | bytes 884744 | tf_op jit(solution)/shard_map/ppermute | solution.py:44
  418.1 8.8 %collective-permute-start.55 = (f32[192,384]{1,0:T(8,128)S(1)}, f32[192,384]{1,0:T(8,128)S(1)}, u32[]{:S(2)}, u32[]{:S(2)}) collective-permute-start(f32[192,384]{1,0:T(8,128)S(1)} %get-tuple-element.93), channel_id=1, source_target_pairs={{0,8},{4,12},{8,0},{12,4},{16,24},{20,28},{24,16},{28,20},{1,9},{5... | collective-permute-start | bytes 884744 | tf_op jit(solution)/shard_map/ppermute | solution.py:43
  419.2 10.0 %collective-permute-start.46 = (f32[48,1536]{1,0:T(8,128)S(1)}, f32[48,1536]{1,0:T(8,128)S(1)}, u32[]{:S(2)}, u32[]{:S(2)}) collective-permute-start(f32[48,1536]{1,0:T(8,128)S(1)} %broadcast_select_fusion.1), channel_id=1, source_target_pairs={{0,8},{4,20},{8,0},{12,28},{16,24},{20,4},{24,16},{28,12},{1,9},{5... | collective-permute-start | bytes 884744 | tf_op jit(solution)/shard_map/ppermute | solution.py:46
  426.9 6.8 %collective-permute-start.57 = (f32[192,384]{1,0:T(8,128)S(1)}, f32[192,384]{1,0:T(8,128)S(1)}, u32[]{:S(2)}, u32[]{:S(2)}) collective-permute-start(f32[192,384]{1,0:T(8,128)S(1)} %broadcast_select_fusion), channel_id=1, source_target_pairs={{0,8},{4,20},{8,0},{12,28},{16,24},{20,4},{24,16},{28,12},{1,9},{5... | collective-permute-start | bytes 884744 | tf_op jit(solution)/shard_map/ppermute | solution.py:46
  430.3 17.5 %collective-permute-start.47 = (f32[4,48,1536]{2,1,0:T(8,128)}, f32[4,48,1536]{2,1,0:T(8,128)}, u32[]{:S(2)}, u32[]{:S(2)}) collective-permute-start(f32[4,48,1536]{2,1,0:T(8,128)} %pad_maximum_fusion.20), channel_id=1, source_target_pairs={{0,4},{4,0},{8,12},{12,8},{16,20},{20,16},{24,28},{28,24},{1,5},{5... | collective-permute-start | bytes 3538952 | tf_op jit(solution)/shard_map/ppermute | solution.py:50
  434.8 25.7 %collective-permute-start.58 = (f32[4,192,384]{2,1,0:T(8,128)}, f32[4,192,384]{2,1,0:T(8,128)}, u32[]{:S(2)}, u32[]{:S(2)}) collective-permute-start(f32[4,192,384]{2,1,0:T(8,128)} %pad_maximum_fusion.21), channel_id=1, source_target_pairs={{0,4},{4,0},{8,12},{12,8},{16,20},{20,16},{24,28},{28,24},{1,5},{5... | collective-permute-start | bytes 3538952 | tf_op jit(solution)/shard_map/ppermute | solution.py:50
  (103 other events, 972.9 us)
Sparse Core Ops, SparseCore 0:
  16.0 27.0 all-gather.10
  45.6 33.8 all-gather.8
  81.9 38.7 all-gather.14
  123.1 38.7 all-gather.12

commit v11 on v9

--- a/solution.py
+++ b/solution.py
@@ -223,6 +223,8 @@
     grad_resid = grad_resid + upstream
     resid_low = grad_resid.astype(jnp.bfloat16)
     grad_outw = jnp.dot(mixed_low.T, resid_low, preferred_element_type=jnp.float32)
+    if fast:
+        early = [_reduce_matrix(grad_outw)] + early
     grad_mixed = jnp.dot(resid_low, back_out.T, preferred_element_type=jnp.float32)
     grad_mixed = grad_mixed.astype(jnp.bfloat16).reshape(blocks, PATCH_BIG, HEADS, HEAD_DIM)
 
@@ -267,8 +269,8 @@
     grad_qk = jnp.stack([gain_q.reshape(model_width), gain_k.reshape(model_width)])
     summands = (grad_qkv, grad_outw, grad_up, grad_down, grad_gain, grad_bias, grad_qk)
     if fast:
-        late = fast_reduce(summands[:2], summands[4:])
-        shares = late[:2] + early + late[2:]
+        late = fast_reduce(summands[:1], summands[4:])
+        shares = late[:1] + early + late[1:]
     else:
         pieces = [
             lax.psum_scatter(

time: 486 us -> 486 us (level)
  no operation moved by 1% of the time
where the time goes in v11:
time: 486 us; the launch traced here: 477 us
  waiting for transfers between devices  130 us (27%)
  matrix products  114 us (23%)
  local copies, waits for them, and re-layouts  81.1 us (17%)
  other arithmetic  67.7 us (14%)
  starting transfers between devices  57.4 us (12%)
  between operations  15.8 us (3%)
  blocking collectives  11.1 us (2%)
    all_gather x4, waiting for transfers between devices, _gather_matrix(): x = lax.all_gather(z, 'dp', axis=1, tiled=False)  36.7 us
    ppermute x4, waiting for transfers between devices, _reduce_matrix(): lax.ppermute(to_x.astype(jnp.bfloat16), 'dp', [(i, i ^ 2) for i in range(...  29.3 us
    ppermute x15, starting transfers between devices, _z_gather(): lax.ppermute(piece, 'fsdp', [(i, (i + k) % NF_FAST) for i in range(NF_FAS...  22.6 us
    dot_general x1, matrix products, layer(): up_pre = jnp.dot(second_low, full_up, preferred_element_type=jnp.float32)  22 us
    ppermute x12, starting transfers between devices, _reduce_matrix(): lax.ppermute(part.astype(jnp.bfloat16), 'fsdp', [(i, (i + k) % NF_FAST) f...  21.6 us
    ppermute x4, waiting for transfers between devices, _reduce_matrix(): lax.ppermute(of_chip(j ^ 3).astype(jnp.bfloat16), 'dp', [(i, i ^ 2) if i...  21.4 us
    ppermute x12, waiting for transfers between devices, _reduce_matrix(): lax.ppermute(part.astype(jnp.bfloat16), 'fsdp', [(i, (i + k) % NF_FAST) f...  21.2 us
    unnamed x137, local copies, waits for them, and re-layouts  20.3 us
  transfers between devices with their start and end apart: 50, of which 30 were waited for; matrix products, arithmetic and copies ran while one was open for 27% of the time, Pallas kernels for 0%

profile of v11, /device:TPU:8, one launch (start us, length us, event | category | flops | bytes accessed | tf_op | source)
XLA Modules:
  0.0 477.0 jit_solution(5170234894607616731)
XLA Ops:
  8.0 2.6 collective-permute-start.7
  16.8 4.7 collective-permute-start.4
  24.4 2.5 collective-permute-done.4
  35.9 5.9 %collective-permute-done.13 = bf16[192,384]{1,0:T(8,128)(2,1)S(1)} collective-permute-done((bf16[192,384]{1,0:T(8,128)(2,1)S(1)}, bf16[192,384]{1,0:T(8,128)(2,1)S(1)}, u32[]{:S(2)}, u32[]{:S(2)}) %collective-permute-start.13) | collective-permute-done | bytes 147488 | tf_op jit(solution)/shard_map/ppermute | solution.py:47
  50.5 2.5 collective-permute-start.10
  53.0 2.8 collective-permute-start.9
  62.5 3.0 collective-permute-done.11
  69.5 9.9 %all-gather.16.cloned.1.call-done = bf16[4,384,1152]{2,1,0:T(8,128)(2,1)} async-done(((bf16[4,48,1152]{2,1,0:T(8,128)(2,1)}), bf16[4,384,1152]{2,1,0:T(8,128)(2,1)}) %all-gather.16.cloned.1.call-update) | async-done | bytes 3538960 | tf_op jit(solution)/shard_map/all_gather | solution.py:59
  88.6 3.7 fusion.119
  100.1 8.4 %fusion.129 = (f32[12,576]{1,0:T(8,128)S(1)}, f32[12,576,576]{1,2,0:T(8,128)}) fusion(f32[576,12,64]{0,2,1:T(8,128)S(1)} %bitcast.234, f32[12,64]{1,0:T(8,128)S(1)} %mul.355, f32[576,12]{0,1:T(8,128)S(1)} %fusion.95, f32[576,12]{0,1:T(8,128)S(1)} %broadcast_multiply_fusion, f32[576,12,64]{0,2,1:T(8,128)S(1)} %bitcast.226, f32[12,64]{1,0:T(8,128)S(1)} %mul.349, ...), kind=kOutput, calls=%fused_computation.274 | convolution fusion | flops 525083904 | bytes 19940352 | tf_op jit(solution)/shard_map/while/body/eval_jaxpr/qhd,khd->hqk/dot_general | solution.py:184
  108.5 8.7 %fusion.3 = f32[12,576]{1,0:T(8,128)S(1)} fusion(f32[12,576,576]{1,2,0:T(8,128)} %get-tuple-element.152, f32[12,576]{1,0:T(8,128)S(1)} %get-tuple-element.151), kind=kLoop, calls=%fused_computation.14 | loop fusion | flops 7955712 | bytes 15980544 | tf_op jit(solution)/shard_map/while/body/eval_jaxpr/reduce_sum | solution.py:194
  117.2 9.8 %fusion.37 = bf16[12,64,576]{2,1,0:T(8,128)(2,1)S(1)} fusion(bf16[576,12,64]{0,2,1:T(8,128)(2,1)} %bitcast.253, f32[12,576,576]{1,2,0:T(8,128)} %get-tuple-element.152, f32[12,576]{1,0:T(8,128)S(1)} %fusion.3, f32[12,576]{1,0:T(8,128)S(1)} %get-tuple-element.151), kind=kOutput, calls=%fused_computation.106 | convolution fusion | flops 521994240 | bytes 17750016 | tf_op jit(solution)/shard_map/while/body/eval_jaxpr/hqk,khd->qhd/dot_general | solution.py:196
  129.7 5.4 %fusion.120 = (bf16[4,4,1,192,384]{4,3,2,1,0:T(8,128)(2,1)}, bf16[4,4,1,192,384]{4,3,2,1,0:T(8,128)(2,1)}) fusion(bf16[4,4,2,192,384]{4,3,2,1,0:T(8,128)(2,1)} %bitcast.243), kind=kLoop, calls=%fused_computation.265 | loop fusion | bytes 9437184 | tf_op jit(solution)/shard_map/slice | solution.py:61
  135.1 26.8 %all-gather.20.cloned.1.call-done = bf16[4,384,1536]{2,1,0:T(8,128)(2,1)} async-done(((bf16[4,48,1536]{2,1,0:T(8,128)(2,1)}), bf16[4,384,1536]{2,1,0:T(8,128)(2,1)}) %all-gather.20.cloned.1.call-update) | async-done | bytes 4718608 | tf_op jit(solution)/shard_map/all_gather | solution.py:59
  161.9 3.0 fusion.121
  164.9 22.0 %multiply_convert_fusion = (bf16[576,3072]{1,0:T(8,128)(2,1)}, f32[576,3072]{1,0:T(8,128)}, f32[576,3072]{1,0:T(8,128)}) fusion(bf16[768,1536]{1,0:T(8,128)(2,1)S(1)} %bitcast.265, bf16[768,1536]{1,0:T(8,128)(2,1)S(1)} %bitcast.263, f32[576,768]{1,0:T(8,128)S(1)} %copy-done.9, f32[768]{0:T(1024)S(1)} %add.386, f32[768]{0:T(1024)S(1)} %mul.363, ...), kind=kOutput, calls=%fused_computation.24 | convolution fusion | flops 2844573696 | bytes 24193536 | tf_op jit(solution)/shard_map/dot_general | solution.py:206
  187.0 8.1 %add_convert_fusion = bf16[576,3072]{1,0:T(8,128)(2,1)S(1)} fusion(f32[576,3072]{1,0:T(8,128)} %get-tuple-element.104, f32[576,3072]{1,0:T(8,128)} %get-tuple-element.155, bf16[3072,384]{1,0:T(8,128)(2,1)S(1)} %bitcast.262, bf16[3072,384]{1,0:T(8,128)(2,1)S(1)} %bitcast.260, bf16[576,768]{1,0:T(8,128)(2,1)S(1)} %copy-done.24, f32[576]{0:T(1024)S(1)} %fusion.96), kind=kOutput, calls=%fused_computation.23 | convolution fusion | flops 2753445888 | bytes 23300352 | tf_op jit(solution)/shard_map/dot_general | solution.py:215
  195.1 3.3 multiply_reduce_fusion.2
  205.7 7.6 %convolution_convert_fusion = bf16[12,576,576]{1,2,0:T(8,128)(2,1)} fusion(bf16[576,12,64]{0,2,1:T(8,128)(2,1)} %bitcast.241, bf16[576,12,64]{0,2,1:T(8,128)(2,1)} %bitcast.254), kind=kOutput, calls=%fused_computation.38 | convolution fusion | flops 513589248 | bytes 9732096 | tf_op jit(solution)/shard_map/qhd,khd->hqk/dot_general | solution.py:237
  213.3 9.9 %fusion.38 = bf16[12,64,576]{2,1,0:T(8,128)(2,1)} fusion(bf16[576,12,64]{0,2,1:T(8,128)(2,1)S(1)} %bitcast.242, f32[12,576,576]{1,2,0:T(8,128)} %get-tuple-element.152, f32[12,576]{1,0:T(8,128)S(1)} %log_add_fusion), kind=kOutput, calls=%fused_computation.107 | convolution fusion | flops 518012928 | bytes 17722368 | tf_op jit(solution)/shard_map/hqk,qhd->khd/dot_general | solution.py:236
  223.2 12.8 %fusion = f32[12,576]{1,0:T(8,128)S(1)} fusion(bf16[12,576,576]{1,2,0:T(8,128)(2,1)} %convolution_convert_fusion, f32[12,576,576]{1,2,0:T(8,128)} %get-tuple-element.152, f32[12,576]{1,0:T(8,128)S(1)} %log_add_fusion), kind=kLoop, calls=%fused_computation.7 | loop fusion | flops 15918336 | bytes 23943168 | tf_op jit(solution)/shard_map/reduce_sum | solution.py:239
  236.8 6.3 %fusion.2 = bf16[12,576,576]{1,2,0:T(8,128)(2,1)} fusion(bf16[12,576,576]{1,2,0:T(8,128)(2,1)S(1)} %copy-done.3, f32[12,576,576]{1,2,0:T(8,128)S(1)} %bitcast.223, f32[12,576]{1,0:T(8,128)S(1)} %fusion, f32[12,576]{1,0:T(8,128)S(1)} %log_add_fusion), kind=kLoop, calls=%fused_computation.9 | loop fusion | flops 19906560 | bytes 31905792 | tf_op jit(solution)/shard_map/convert_element_type | solution.py:240
  243.2 8.2 %fusion.29 = (f32[576,12]{0,1:T(8,128)S(1)}, f32[12,64,576]{2,1,0:T(8,128)}) fusion(f32[576,12,64]{0,2,1:T(8,128)} %bitcast.233, f32[12,64]{1,0:T(8,128)S(1)} %copy-done.45, f32[576,12]{0,1:T(8,128)S(1)} %broadcast_multiply_fusion, bf16[12,576,576]{1,2,0:T(8,128)(2,1)} %fusion.2, f32[576,12,64]{0,2,1:T(8,128)S(1)} %bitcast.227, f32[12,64]{1,0:T(8,128)S(1)} %mul.349, ...), kind=kOutput, calls=%fused_computation.76 | convolution fusion | flops 513139968 | bytes 13387776 | tf_op jit(solution)/shard_map/hqk,qhd->khd/dot_general | solution.py:245
  259.2 2.8 fusion.116
  262.0 6.4 %fusion.41 = f32[768,2304]{1,0:T(8,128)} fusion(bf16[576,768]{0,1:T(8,128)(2,1)S(1)} %bitcast.281, bf16[576,768]{0,1:T(8,128)(2,1)S(1)} %bitcast.277, bf16[576,768]{0,1:T(8,128)(2,1)S(1)} %bitcast.279, bf16[576,768]{1,0:T(8,128)(2,1)S(1)} %copy-done.13, f32[768]{0:T(1024)S(1)} %copy-done.55, f32[768]{0:T(1024)S(1)} %copy-done.53, f32[576]{0:T(1024)S(1)} %copy-done.51, ...), kind=kOutput, calls=%fused_computation.111 | convolution fusion | flops 2049048576 | bytes 10627584 | tf_op jit(solution)/shard_map/dot_general | solution.py:263
  269.6 4.2 select_maximum_fusion
  273.8 3.2 copy-done.5
  279.1 6.1 %fusion.115 = f32[768,3072]{1,0:T(8,128)S(1)} fusion(bf16[576,3072]{1,0:T(8,128)(2,1)} %copy-done.23, f32[576,768]{1,0:T(8,128)S(1)} %copy-done.10, f32[768]{0:T(1024)S(1)} %add.386, f32[768]{0:T(1024)S(1)} %mul.363, f32[576]{0:T(1024)S(1)} %fusion.98, f32[576]{0:T(1024)S(1)} %broadcast_multiply_fusion.4), kind=kOutput, calls=%fused_computation.261 | convolution fusion | flops 2720120832 | bytes 14756352 | tf_op jit(solution)/shard_map/dot_general | solution.py:218
  287.5 4.1 constant_dynamic-slice_fusion.3
  297.2 2.8 constant_dynamic-slice_fusion.1
  300.0 4.6 collective-permute-done.16
  308.0 2.5 convert_add_fusion.1
  310.5 8.0 %collective-permute-done.17 = bf16[4,48,1280]{2,1,0:T(8,128)(2,1)S(1)} collective-permute-done((bf16[4,48,1280]{2,1,0:T(8,128)(2,1)S(1)}, bf16[4,48,1280]{2,1,0:T(8,128)(2,1)S(1)}, u32[]{:S(2)}, u32[]{:S(2)}) %collective-permute-start.17) | collective-permute-done | bytes 491552 | tf_op jit(solution)/shard_map/ppermute | solution.py:101
  325.8 4.0 collective-permute-done.19
  332.1 3.2 collective-permute-done.30
  339.2 6.1 %fusion.61 = f32[3072,768]{1,0:T(8,128)S(1)} fusion(bf16[576,3072]{1,0:T(8,128)(2,1)} %get-tuple-element.103, bf16[576,768]{1,0:T(8,128)(2,1)S(1)} %copy-done.25, f32[576]{0:T(1024)S(1)} %fusion.96), kind=kOutput, calls=%fused_computation.147 | convolution fusion | flops 2719236096 | bytes 13863168 | tf_op jit(solution)/shard_map/dot_general | solution.py:214
  345.3 3.6 copy-done.19
  357.8 7.4 %collective-permute-done.33 = bf16[48,1536]{1,0:T(8,128)(2,1)S(1)} collective-permute-done((bf16[48,1536]{1,0:T(8,128)(2,1)S(1)}, bf16[48,1536]{1,0:T(8,128)(2,1)S(1)}, u32[]{:S(2)}, u32[]{:S(2)}) %collective-permute-start.33) | collective-permute-done | bytes 147488 | tf_op jit(solution)/shard_map/ppermute | solution.py:107
  367.7 2.6 constant_dynamic-slice_fusion
  373.9 13.5 %collective-permute-done.37 = bf16[4,192,384]{2,1,0:T(8,128)(2,1)S(1)} collective-permute-done((bf16[4,192,384]{2,1,0:T(8,128)(2,1)S(1)}, bf16[4,192,384]{2,1,0:T(8,128)(2,1)S(1)}, u32[]{:S(2)}, u32[]{:S(2)}) %collective-permute-start.37) | collective-permute-done | bytes 589856 | tf_op jit(solution)/shard_map/ppermute | solution.py:94
  390.4 14.5 %collective-permute-done.38 = bf16[4,192,384]{2,1,0:T(8,128)(2,1)S(1)} collective-permute-done((bf16[4,192,384]{2,1,0:T(8,128)(2,1)S(1)}, bf16[4,192,384]{2,1,0:T(8,128)(2,1)S(1)}, u32[]{:S(2)}, u32[]{:S(2)}) %collective-permute-start.38) | collective-permute-done | bytes 589856 | tf_op jit(solution)/shard_map/ppermute | solution.py:101
  405.2 3.4 collective-permute-start.40
  415.4 3.6 collective-permute-done.42
  419.1 2.8 collective-permute-done.41
  422.7 7.4 %multiply_convert_fusion.3 = bf16[576,768]{1,0:T(8,128)(2,1)} fusion(f32[576,768]{1,0:T(8,128)S(1)} %copy-done.10, bf16[576,3072]{1,0:T(8,128)(2,1)} %get-tuple-element.103, bf16[3072,384]{1,0:T(8,128)(2,1)} %bitcast.261, bf16[3072,384]{1,0:T(8,128)(2,1)} %bitcast.259, f32[576]{0:T(1024)S(1)} %fusion.96), kind=kOutput, calls=%fused_computation.99 | convolution fusion | flops 2728673280 | bytes 10914048 | tf_op jit(solution)/shard_map/dot_general | solution.py:209
  432.4 5.7 %collective-permute-done.24 = bf16[4,48,384]{2,1,0:T(8,128)(2,1)S(1)} collective-permute-done((bf16[4,48,384]{2,1,0:T(8,128)(2,1)S(1)}, bf16[4,48,384]{2,1,0:T(8,128)(2,1)S(1)}, u32[]{:S(2)}, u32[]{:S(2)}) %collective-permute-start.24) | collective-permute-done | bytes 147488 | tf_op jit(solution)/shard_map/ppermute | solution.py:101
  440.8 2.7 collective-permute-start.27
  445.9 11.1 %all-gather.5 = f32[384,384]{1,0:T(8,128)S(1)} all-gather(f32[48,384]{1,0:T(8,128)S(1)} %fusion.90), channel_id=7, replica_groups=mesh['dp'=8,'fsdp'=4] {'dp'}, dimensions={0}, use_global_device_ids=true | all-gather | bytes 663552 | tf_op jit(solution)/shard_map/all_gather | solution.py:110
  (349 shorter events, 147.0 us)
Async XLA Ops:
  7.2 60.0 %all-gather.18.cloned.1.call-start = ((), (), s32[]{:S(2)}) async-start(), calls=%async_computation.1 | async-start | bytes 1327104 | tf_op jit(solution)/shard_map/all_gather | solution.py:59
  8.0 5.4 %collective-permute-start.7 = (bf16[48,384]{1,0:T(8,128)(2,1)S(1)}, bf16[48,384]{1,0:T(8,128)(2,1)S(1)}, u32[]{:S(2)}, u32[]{:S(2)}) collective-permute-start(bf16[48,384]{1,0:T(8,128)(2,1)S(1)} %dynamic_slice.151), channel_id=1, source_target_pairs={{0,2},{1,3},{2,0},{3,1},{4,6},{5,7},{6,4},{7,5},{8,10},{9,11},{10,... | collective-permute-start | bytes 110600 | tf_op jit(solution)/shard_map/ppermute | solution.py:47
  15.9 63.6 %all-gather.16.cloned.1.call-start = ((), (), s32[]{:S(2)}) async-start(), calls=%async_computation | async-start | bytes 3981312 | tf_op jit(solution)/shard_map/all_gather | solution.py:59
  16.8 10.1 %collective-permute-start.4 = (bf16[48,1152]{1,0:T(8,128)(2,1)S(1)}, bf16[48,1152]{1,0:T(8,128)(2,1)S(1)}, u32[]{:S(2)}, u32[]{:S(2)}) collective-permute-start(bf16[48,1152]{1,0:T(8,128)(2,1)S(1)} %dynamic_slice.150), channel_id=1, source_target_pairs={{0,2},{1,3},{2,0},{3,1},{4,6},{5,7},{6,4},{7,5},{8,10},{9,11},{10,... | collective-permute-start | bytes 331784 | tf_op jit(solution)/shard_map/ppermute | solution.py:47
  21.5 6.6 %collective-permute-start.3 = (bf16[48,1152]{1,0:T(8,128)(2,1)S(1)}, bf16[48,1152]{1,0:T(8,128)(2,1)S(1)}, u32[]{:S(2)}, u32[]{:S(2)}) collective-permute-start(bf16[48,1152]{1,0:T(8,128)(2,1)S(1)} %dynamic_slice.150), channel_id=1, source_target_pairs={{0,1},{1,2},{2,3},{3,0},{4,5},{5,6},{6,7},{7,4},{8,9},{9,10},{10,1... | collective-permute-start | bytes 331784 | tf_op jit(solution)/shard_map/ppermute | solution.py:47
  21.5 7.6 %collective-permute-start.5 = (bf16[48,1152]{1,0:T(8,128)(2,1)S(1)}, bf16[48,1152]{1,0:T(8,128)(2,1)S(1)}, u32[]{:S(2)}, u32[]{:S(2)}) collective-permute-start(bf16[48,1152]{1,0:T(8,128)(2,1)S(1)} %dynamic_slice.150), channel_id=1, source_target_pairs={{0,3},{1,0},{2,1},{3,2},{4,7},{5,4},{6,5},{7,6},{8,11},{9,8},{10,9... | collective-permute-start | bytes 331784 | tf_op jit(solution)/shard_map/ppermute | solution.py:47
  30.6 99.1 %all-gather.22.cloned.1.call-start = ((), (), s32[]{:S(2)}) async-start(), calls=%async_computation.3 | async-start | bytes 5308416 | tf_op jit(solution)/shard_map/all_gather | solution.py:59
  31.6 10.2 %collective-permute-start.13 = (bf16[192,384]{1,0:T(8,128)(2,1)S(1)}, bf16[192,384]{1,0:T(8,128)(2,1)S(1)}, u32[]{:S(2)}, u32[]{:S(2)}) collective-permute-start(bf16[192,384]{1,0:T(8,128)(2,1)S(1)} %dynamic_slice.153), channel_id=1, source_target_pairs={{0,2},{1,3},{2,0},{3,1},{4,6},{5,7},{6,4},{7,5},{8,10},{9,11},{10,... | collective-permute-start | bytes 442376 | tf_op jit(solution)/shard_map/ppermute | solution.py:47
  32.9 11.0 %collective-permute-start.12 = (bf16[192,384]{1,0:T(8,128)(2,1)S(1)}, bf16[192,384]{1,0:T(8,128)(2,1)S(1)}, u32[]{:S(2)}, u32[]{:S(2)}) collective-permute-start(bf16[192,384]{1,0:T(8,128)(2,1)S(1)} %dynamic_slice.153), channel_id=1, source_target_pairs={{0,1},{1,2},{2,3},{3,0},{4,5},{5,6},{6,7},{7,4},{8,9},{9,10},{10,1... | collective-permute-start | bytes 442376 | tf_op jit(solution)/shard_map/ppermute | solution.py:47
  33.8 11.5 %collective-permute-start.14 = (bf16[192,384]{1,0:T(8,128)(2,1)S(1)}, bf16[192,384]{1,0:T(8,128)(2,1)S(1)}, u32[]{:S(2)}, u32[]{:S(2)}) collective-permute-start(bf16[192,384]{1,0:T(8,128)(2,1)S(1)} %dynamic_slice.153), channel_id=1, source_target_pairs={{0,3},{1,0},{2,1},{3,2},{4,7},{5,4},{6,5},{7,6},{8,11},{9,8},{10,9... | collective-permute-start | bytes 442376 | tf_op jit(solution)/shard_map/ppermute | solution.py:47
  46.9 115.0 %all-gather.20.cloned.1.call-start = ((), (), s32[]{:S(2)}) async-start(), calls=%async_computation.2 | async-start | bytes 5308416 | tf_op jit(solution)/shard_map/all_gather | solution.py:59
  47.0 12.2 %collective-permute-start.1 = (bf16[6,192]{1,0:T(8,128)(2,1)S(1)}, bf16[6,192]{1,0:T(8,128)(2,1)S(1)}, u32[]{:S(2)}, u32[]{:S(2)}) collective-permute-start(bf16[6,192]{1,0:T(8,128)(2,1)S(1)} %get-tuple-element.150), channel_id=1, source_target_pairs={{0,2},{1,3},{2,0},{3,1},{4,6},{5,7},{6,4},{7,5},{8,10},{9,11},{10,... | collective-permute-start | bytes 6920 | tf_op jit(solution)/shard_map/ppermute | solution.py:47
  47.1 12.2 %collective-permute-start = (bf16[6,192]{1,0:T(8,128)(2,1)S(1)}, bf16[6,192]{1,0:T(8,128)(2,1)S(1)}, u32[]{:S(2)}, u32[]{:S(2)}) collective-permute-start(bf16[6,192]{1,0:T(8,128)(2,1)S(1)} %get-tuple-element.150), channel_id=1, source_target_pairs={{0,1},{1,2},{2,3},{3,0},{4,5},{5,6},{6,7},{7,4},{8,9},{9,10},{10,1... | collective-permute-start | bytes 6920 | tf_op jit(solution)/shard_map/ppermute | solution.py:47
  48.4 10.9 %collective-permute-start.2 = (bf16[6,192]{1,0:T(8,128)(2,1)S(1)}, bf16[6,192]{1,0:T(8,128)(2,1)S(1)}, u32[]{:S(2)}, u32[]{:S(2)}) collective-permute-start(bf16[6,192]{1,0:T(8,128)(2,1)S(1)} %get-tuple-element.150), channel_id=1, source_target_pairs={{0,3},{1,0},{2,1},{3,2},{4,7},{5,4},{6,5},{7,6},{8,11},{9,8},{10,9... | collective-permute-start | bytes 6920 | tf_op jit(solution)/shard_map/ppermute | solution.py:47
  50.5 11.2 %collective-permute-start.10 = (bf16[48,1536]{1,0:T(8,128)(2,1)S(1)}, bf16[48,1536]{1,0:T(8,128)(2,1)S(1)}, u32[]{:S(2)}, u32[]{:S(2)}) collective-permute-start(bf16[48,1536]{1,0:T(8,128)(2,1)S(1)} %dynamic_slice.152), channel_id=1, source_target_pairs={{0,2},{1,3},{2,0},{3,1},{4,6},{5,7},{6,4},{7,5},{8,10},{9,11},{10,... | collective-permute-start | bytes 442376 | tf_op jit(solution)/shard_map/ppermute | solution.py:47
  53.0 9.5 %collective-permute-start.9 = (bf16[48,1536]{1,0:T(8,128)(2,1)S(1)}, bf16[48,1536]{1,0:T(8,128)(2,1)S(1)}, u32[]{:S(2)}, u32[]{:S(2)}) collective-permute-start(bf16[48,1536]{1,0:T(8,128)(2,1)S(1)} %dynamic_slice.152), channel_id=1, source_target_pairs={{0,1},{1,2},{2,3},{3,0},{4,5},{5,6},{6,7},{7,4},{8,9},{9,10},{10,1... | collective-permute-start | bytes 442376 | tf_op jit(solution)/shard_map/ppermute | solution.py:47
  59.3 6.3 %collective-permute-start.11 = (bf16[48,1536]{1,0:T(8,128)(2,1)S(1)}, bf16[48,1536]{1,0:T(8,128)(2,1)S(1)}, u32[]{:S(2)}, u32[]{:S(2)}) collective-permute-start(bf16[48,1536]{1,0:T(8,128)(2,1)S(1)} %dynamic_slice.152), channel_id=1, source_target_pairs={{0,3},{1,0},{2,1},{3,2},{4,7},{5,4},{6,5},{7,6},{8,11},{9,8},{10,9... | collective-permute-start | bytes 442376 | tf_op jit(solution)/shard_map/ppermute | solution.py:47
  67.1 390.8 %all-gather.24.cloned.1.call-start = ((), (), s32[]{:S(2)}) async-start(), calls=%async_computation.4 | async-start | bytes 2211840 | tf_op jit(solution)/shard_map/all_gather | solution.py:110
  278.5 13.1 %collective-permute-start.15 = (bf16[4,4,48,1280]{3,2,1,0:T(8,128)(2,1)}, bf16[4,4,48,1280]{3,2,1,0:T(8,128)(2,1)}, u32[]{:S(2)}, u32[]{:S(2)}) collective-permute-start(bf16[4,4,48,1280]{3,2,1,0:T(8,128)(2,1)} %bitcast.53), channel_id=1, source_target_pairs={{0,4},{4,0},{8,12},{12,8},{16,20},{20,16},{24,28},{28,24},{1,5},{5... | collective-permute-start | bytes 5898248 | tf_op jit(solution)/shard_map/ppermute | solution.py:88
  287.3 20.7 %collective-permute-start.29 = (bf16[4,4,48,1536]{3,2,1,0:T(8,128)(2,1)}, bf16[4,4,48,1536]{3,2,1,0:T(8,128)(2,1)}, u32[]{:S(2)}, u32[]{:S(2)}) collective-permute-start(bf16[4,4,48,1536]{3,2,1,0:T(8,128)(2,1)} %bitcast.80), channel_id=1, source_target_pairs={{0,4},{4,0},{8,12},{12,8},{16,20},{20,16},{24,28},{28,24},{1,5},{5... | collective-permute-start | bytes 7077896 | tf_op jit(solution)/shard_map/ppermute | solution.py:88
  295.6 9.0 %collective-permute-start.16 = (bf16[4,48,1280]{2,1,0:T(8,128)(2,1)S(1)}, bf16[4,48,1280]{2,1,0:T(8,128)(2,1)}, u32[]{:S(2)}, u32[]{:S(2)}) collective-permute-start(bf16[4,48,1280]{2,1,0:T(8,128)(2,1)S(1)} %fusion.60), channel_id=1, source_target_pairs={{0,8},{4,20},{8,0},{12,28},{16,24},{20,4},{24,16},{28,12},{1,9},{5... | collective-permute-start | bytes 1474568 | tf_op jit(solution)/shard_map/ppermute | solution.py:94
  305.9 12.6 %collective-permute-start.17 = (bf16[4,48,1280]{2,1,0:T(8,128)(2,1)S(1)}, bf16[4,48,1280]{2,1,0:T(8,128)(2,1)S(1)}, u32[]{:S(2)}, u32[]{:S(2)}) collective-permute-start(bf16[4,48,1280]{2,1,0:T(8,128)(2,1)S(1)} %get-tuple-element.115), channel_id=1, source_target_pairs={{0,8},{4,12},{8,0},{12,4},{16,24},{20,28},{24,16},{28,20},{1,9},{5... | collective-permute-start | bytes 1474568 | tf_op jit(solution)/shard_map/ppermute | solution.py:101
  307.4 12.2 %collective-permute-start.18 = (bf16[4,48,1280]{2,1,0:T(8,128)(2,1)S(1)}, bf16[4,48,1280]{2,1,0:T(8,128)(2,1)S(1)}, u32[]{:S(2)}, u32[]{:S(2)}) collective-permute-start(bf16[4,48,1280]{2,1,0:T(8,128)(2,1)S(1)} %get-tuple-element.116), channel_id=1, source_target_pairs={{0,16},{4,20},{8,24},{12,28},{16,0},{20,4},{24,8},{28,12},{1,17},{... | collective-permute-start | bytes 1474568 | tf_op jit(solution)/shard_map/ppermute | solution.py:102
  319.9 9.9 %collective-permute-start.19 = (bf16[48,1280]{1,0:T(8,128)(2,1)S(1)}, bf16[48,1280]{1,0:T(8,128)(2,1)S(1)}, u32[]{:S(2)}, u32[]{:S(2)}) collective-permute-start(bf16[48,1280]{1,0:T(8,128)(2,1)S(1)} %get-tuple-element.135), channel_id=1, source_target_pairs={{0,1},{1,2},{2,3},{3,0},{4,5},{5,6},{6,7},{7,4},{8,9},{9,10},{10,1... | collective-permute-start | bytes 368648 | tf_op jit(solution)/shard_map/ppermute | solution.py:107
  321.4 9.5 %collective-permute-start.21 = (bf16[48,1280]{1,0:T(8,128)(2,1)S(1)}, bf16[48,1280]{1,0:T(8,128)(2,1)S(1)}, u32[]{:S(2)}, u32[]{:S(2)}) collective-permute-start(bf16[48,1280]{1,0:T(8,128)(2,1)S(1)} %get-tuple-element.136), channel_id=1, source_target_pairs={{0,3},{1,0},{2,1},{3,2},{4,7},{5,4},{6,5},{7,6},{8,11},{9,8},{10,9... | collective-permute-start | bytes 368648 | tf_op jit(solution)/shard_map/ppermute | solution.py:107
  322.0 9.1 %collective-permute-start.20 = (bf16[48,1280]{1,0:T(8,128)(2,1)S(1)}, bf16[48,1280]{1,0:T(8,128)(2,1)S(1)}, u32[]{:S(2)}, u32[]{:S(2)}) collective-permute-start(bf16[48,1280]{1,0:T(8,128)(2,1)S(1)} %get-tuple-element.137), channel_id=1, source_target_pairs={{0,2},{1,3},{2,0},{3,1},{4,6},{5,7},{6,4},{7,5},{8,10},{9,11},{10,... | collective-permute-start | bytes 368648 | tf_op jit(solution)/shard_map/ppermute | solution.py:107
  325.2 10.1 %collective-permute-start.30 = (bf16[4,48,1536]{2,1,0:T(8,128)(2,1)}, bf16[4,48,1536]{2,1,0:T(8,128)(2,1)S(1)}, u32[]{:S(2)}, u32[]{:S(2)}) collective-permute-start(bf16[4,48,1536]{2,1,0:T(8,128)(2,1)} %fusion.58), channel_id=1, source_target_pairs={{0,8},{4,20},{8,0},{12,28},{16,24},{20,4},{24,16},{28,12},{1,9},{5... | collective-permute-start | bytes 1769480 | tf_op jit(solution)/shard_map/ppermute | solution.py:94
  331.8 131.2 %all-gather.26.cloned.1.call-start = ((), (), s32[]{:S(2)}) async-start(), calls=%async_computation.5 | async-start | bytes 2654208 | tf_op jit(solution)/shard_map/all_gather | solution.py:110
  337.3 14.5 %collective-permute-start.31 = (bf16[4,48,1536]{2,1,0:T(8,128)(2,1)S(1)}, bf16[4,48,1536]{2,1,0:T(8,128)(2,1)S(1)}, u32[]{:S(2)}, u32[]{:S(2)}) collective-permute-start(bf16[4,48,1536]{2,1,0:T(8,128)(2,1)S(1)} %get-tuple-element.107), channel_id=1, source_target_pairs={{0,8},{4,12},{8,0},{12,4},{16,24},{20,28},{24,16},{28,20},{1,9},{5... | collective-permute-start | bytes 1769480 | tf_op jit(solution)/shard_map/ppermute | solution.py:101
  337.9 14.1 %collective-permute-start.32 = (bf16[4,48,1536]{2,1,0:T(8,128)(2,1)S(1)}, bf16[4,48,1536]{2,1,0:T(8,128)(2,1)S(1)}, u32[]{:S(2)}, u32[]{:S(2)}) collective-permute-start(bf16[4,48,1536]{2,1,0:T(8,128)(2,1)S(1)} %get-tuple-element.108), channel_id=1, source_target_pairs={{0,16},{4,20},{8,24},{12,28},{16,0},{20,4},{24,8},{28,12},{1,17},{... | collective-permute-start | bytes 1769480 | tf_op jit(solution)/shard_map/ppermute | solution.py:102
  350.6 19.8 %collective-permute-start.36 = (bf16[4,4,192,384]{3,2,1,0:T(8,128)(2,1)}, bf16[4,4,192,384]{3,2,1,0:T(8,128)(2,1)}, u32[]{:S(2)}, u32[]{:S(2)}) collective-permute-start(bf16[4,4,192,384]{3,2,1,0:T(8,128)(2,1)} %bitcast.93), channel_id=1, source_target_pairs={{0,4},{4,0},{8,12},{12,8},{16,20},{20,16},{24,28},{28,24},{1,5},{5... | collective-permute-start | bytes 7077896 | tf_op jit(solution)/shard_map/ppermute | solution.py:88
  353.6 11.7 %collective-permute-start.33 = (bf16[48,1536]{1,0:T(8,128)(2,1)S(1)}, bf16[48,1536]{1,0:T(8,128)(2,1)S(1)}, u32[]{:S(2)}, u32[]{:S(2)}) collective-permute-start(bf16[48,1536]{1,0:T(8,128)(2,1)S(1)} %get-tuple-element.130), channel_id=1, source_target_pairs={{0,1},{1,2},{2,3},{3,0},{4,5},{5,6},{6,7},{7,4},{8,9},{9,10},{10,1... | collective-permute-start | bytes 442376 | tf_op jit(solution)/shard_map/ppermute | solution.py:107
  355.0 11.5 %collective-permute-start.35 = (bf16[48,1536]{1,0:T(8,128)(2,1)S(1)}, bf16[48,1536]{1,0:T(8,128)(2,1)S(1)}, u32[]{:S(2)}, u32[]{:S(2)}) collective-permute-start(bf16[48,1536]{1,0:T(8,128)(2,1)S(1)} %get-tuple-element.131), channel_id=1, source_target_pairs={{0,3},{1,0},{2,1},{3,2},{4,7},{5,4},{6,5},{7,6},{8,11},{9,8},{10,9... | collective-permute-start | bytes 442376 | tf_op jit(solution)/shard_map/ppermute | solution.py:107
  355.6 11.2 %collective-permute-start.34 = (bf16[48,1536]{1,0:T(8,128)(2,1)S(1)}, bf16[48,1536]{1,0:T(8,128)(2,1)S(1)}, u32[]{:S(2)}, u32[]{:S(2)}) collective-permute-start(bf16[48,1536]{1,0:T(8,128)(2,1)S(1)} %get-tuple-element.132), channel_id=1, source_target_pairs={{0,2},{1,3},{2,0},{3,1},{4,6},{5,7},{6,4},{7,5},{8,10},{9,11},{10,... | collective-permute-start | bytes 442376 | tf_op jit(solution)/shard_map/ppermute | solution.py:107
  367.7 97.2 %all-gather.28.cloned.1.call-start = ((), (), s32[]{:S(2)}) async-start(), calls=%async_computation.6 | async-start | bytes 2654208 | tf_op jit(solution)/shard_map/all_gather | solution.py:110
  372.8 14.7 %collective-permute-start.37 = (bf16[4,192,384]{2,1,0:T(8,128)(2,1)S(1)}, bf16[4,192,384]{2,1,0:T(8,128)(2,1)S(1)}, u32[]{:S(2)}, u32[]{:S(2)}) collective-permute-start(bf16[4,192,384]{2,1,0:T(8,128)(2,1)S(1)} %fusion.59), channel_id=1, source_target_pairs={{0,8},{4,20},{8,0},{12,28},{16,24},{20,4},{24,16},{28,12},{1,9},{5... | collective-permute-start | bytes 1769480 | tf_op jit(solution)/shard_map/ppermute | solution.py:94
  387.8 17.0 %collective-permute-start.38 = (bf16[4,192,384]{2,1,0:T(8,128)(2,1)S(1)}, bf16[4,192,384]{2,1,0:T(8,128)(2,1)S(1)}, u32[]{:S(2)}, u32[]{:S(2)}) collective-permute-start(bf16[4,192,384]{2,1,0:T(8,128)(2,1)S(1)} %get-tuple-element.105), channel_id=1, source_target_pairs={{0,8},{4,12},{8,0},{12,4},{16,24},{20,28},{24,16},{28,20},{1,9},{5... | collective-permute-start | bytes 1769480 | tf_op jit(solution)/shard_map/ppermute | solution.py:101
  389.0 15.9 %collective-permute-start.39 = (bf16[4,192,384]{2,1,0:T(8,128)(2,1)S(1)}, bf16[4,192,384]{2,1,0:T(8,128)(2,1)S(1)}, u32[]{:S(2)}, u32[]{:S(2)}) collective-permute-start(bf16[4,192,384]{2,1,0:T(8,128)(2,1)S(1)} %get-tuple-element.106), channel_id=1, source_target_pairs={{0,16},{4,20},{8,24},{12,28},{16,0},{20,4},{24,8},{28,12},{1,17},{... | collective-permute-start | bytes 1769480 | tf_op jit(solution)/shard_map/ppermute | solution.py:102
  390.2 22.7 %collective-permute-start.22 = (bf16[4,4,48,384]{3,2,1,0:T(8,128)(2,1)S(1)}, bf16[4,4,48,384]{3,2,1,0:T(8,128)(2,1)S(1)}, u32[]{:S(2)}, u32[]{:S(2)}) collective-permute-start(bf16[4,4,48,384]{3,2,1,0:T(8,128)(2,1)S(1)} %bitcast.282), channel_id=1, source_target_pairs={{0,4},{4,0},{8,12},{12,8},{16,20},{20,16},{24,28},{28,24},{1,5},{5... | collective-permute-start | bytes 1769480 | tf_op jit(solution)/shard_map/ppermute | solution.py:88
  405.2 10.3 %collective-permute-start.40 = (bf16[192,384]{1,0:T(8,128)(2,1)S(1)}, bf16[192,384]{1,0:T(8,128)(2,1)S(1)}, u32[]{:S(2)}, u32[]{:S(2)}) collective-permute-start(bf16[192,384]{1,0:T(8,128)(2,1)S(1)} %get-tuple-element.127), channel_id=1, source_target_pairs={{0,1},{1,2},{2,3},{3,0},{4,5},{5,6},{6,7},{7,4},{8,9},{9,10},{10,1... | collective-permute-start | bytes 442376 | tf_op jit(solution)/shard_map/ppermute | solution.py:107
  408.6 10.5 %collective-permute-start.42 = (bf16[192,384]{1,0:T(8,128)(2,1)S(1)}, bf16[192,384]{1,0:T(8,128)(2,1)S(1)}, u32[]{:S(2)}, u32[]{:S(2)}) collective-permute-start(bf16[192,384]{1,0:T(8,128)(2,1)S(1)} %get-tuple-element.128), channel_id=1, source_target_pairs={{0,3},{1,0},{2,1},{3,2},{4,7},{5,4},{6,5},{7,6},{8,11},{9,8},{10,9... | collective-permute-start | bytes 442376 | tf_op jit(solution)/shard_map/ppermute | solution.py:107
  410.5 11.3 %collective-permute-start.41 = (bf16[192,384]{1,0:T(8,128)(2,1)S(1)}, bf16[192,384]{1,0:T(8,128)(2,1)S(1)}, u32[]{:S(2)}, u32[]{:S(2)}) collective-permute-start(bf16[192,384]{1,0:T(8,128)(2,1)S(1)} %get-tuple-element.129), channel_id=1, source_target_pairs={{0,2},{1,3},{2,0},{3,1},{4,6},{5,7},{6,4},{7,5},{8,10},{9,11},{10,... | collective-permute-start | bytes 442376 | tf_op jit(solution)/shard_map/ppermute | solution.py:107
  414.0 16.1 %collective-permute-start.23 = (bf16[4,48,384]{2,1,0:T(8,128)(2,1)S(1)}, bf16[4,48,384]{2,1,0:T(8,128)(2,1)S(1)}, u32[]{:S(2)}, u32[]{:S(2)}) collective-permute-start(bf16[4,48,384]{2,1,0:T(8,128)(2,1)S(1)} %fusion.77), channel_id=1, source_target_pairs={{0,8},{4,20},{8,0},{12,28},{16,24},{20,4},{24,16},{28,12},{1,9},{5... | collective-permute-start | bytes 442376 | tf_op jit(solution)/shard_map/ppermute | solution.py:94
  430.1 8.0 %collective-permute-start.24 = (bf16[4,48,384]{2,1,0:T(8,128)(2,1)S(1)}, bf16[4,48,384]{2,1,0:T(8,128)(2,1)S(1)}, u32[]{:S(2)}, u32[]{:S(2)}) collective-permute-start(bf16[4,48,384]{2,1,0:T(8,128)(2,1)S(1)} %get-tuple-element.125), channel_id=1, source_target_pairs={{0,8},{4,12},{8,0},{12,4},{16,24},{20,28},{24,16},{28,20},{1,9},{5... | collective-permute-start | bytes 442376 | tf_op jit(solution)/shard_map/ppermute | solution.py:101
  431.3 7.0 %collective-permute-start.25 = (bf16[4,48,384]{2,1,0:T(8,128)(2,1)S(1)}, bf16[4,48,384]{2,1,0:T(8,128)(2,1)S(1)}, u32[]{:S(2)}, u32[]{:S(2)}) collective-permute-start(bf16[4,48,384]{2,1,0:T(8,128)(2,1)S(1)} %get-tuple-element.126), channel_id=1, source_target_pairs={{0,16},{4,20},{8,24},{12,28},{16,0},{20,4},{24,8},{28,12},{1,17},{... | collective-permute-start | bytes 442376 | tf_op jit(solution)/shard_map/ppermute | solution.py:102
  438.4 7.0 %collective-permute-start.26 = (bf16[48,384]{1,0:T(8,128)(2,1)S(1)}, bf16[48,384]{1,0:T(8,128)(2,1)S(1)}, u32[]{:S(2)}, u32[]{:S(2)}) collective-permute-start(bf16[48,384]{1,0:T(8,128)(2,1)S(1)} %get-tuple-element.140), channel_id=1, source_target_pairs={{0,1},{1,2},{2,3},{3,0},{4,5},{5,6},{6,7},{7,4},{8,9},{9,10},{10,1... | collective-permute-start | bytes 110600 | tf_op jit(solution)/shard_map/ppermute | solution.py:107
  440.2 5.1 %collective-permute-start.28 = (bf16[48,384]{1,0:T(8,128)(2,1)S(1)}, bf16[48,384]{1,0:T(8,128)(2,1)S(1)}, u32[]{:S(2)}, u32[]{:S(2)}) collective-permute-start(bf16[48,384]{1,0:T(8,128)(2,1)S(1)} %get-tuple-element.141), channel_id=1, source_target_pairs={{0,3},{1,0},{2,1},{3,2},{4,7},{5,4},{6,5},{7,6},{8,11},{9,8},{10,9... | collective-permute-start | bytes 110600 | tf_op jit(solution)/shard_map/ppermute | solution.py:107
  440.8 5.0 %collective-permute-start.27 = (bf16[48,384]{1,0:T(8,128)(2,1)S(1)}, bf16[48,384]{1,0:T(8,128)(2,1)S(1)}, u32[]{:S(2)}, u32[]{:S(2)}) collective-permute-start(bf16[48,384]{1,0:T(8,128)(2,1)S(1)} %get-tuple-element.142), channel_id=1, source_target_pairs={{0,2},{1,3},{2,0},{3,1},{4,6},{5,7},{6,4},{7,5},{8,10},{9,11},{10,... | collective-permute-start | bytes 110600 | tf_op jit(solution)/shard_map/ppermute | solution.py:107
  (69 other events, 655.0 us)
Sparse Core Ops, SparseCore 0:
  16.0 27.0 all-gather.17
  45.6 33.8 all-gather.15
  81.9 38.7 all-gather.21
  123.1 38.7 all-gather.19
  331.9 30.6 all-gather.23
  367.8 35.4 all-gather.25
  422.8 32.6 all-gather.27

commit v12 on v10

--- a/solution.py
+++ b/solution.py
@@ -76,8 +76,16 @@
     return x.reshape(NF_FAST * m.shape[0], m.shape[1])
 
 
+def _gather_rows(m):
+    d = lax.axis_index("dp")
+    rows = m.shape[0] // NDP_FAST
+    z = _z_gather(lax.dynamic_slice_in_dim(m, d * rows, rows, 0))
+    x = _take(_plane_gather(z), jnp.arange(NDP_FAST, dtype=jnp.int32) ^ d, 0)
+    return x.transpose(1, 0, 2, 3).reshape(NF_FAST * m.shape[0], m.shape[1])
+
+
 def fast_gather(mats, gains):
-    out = [_gather_matrix(m) for m in mats]
+    out = [_gather_matrix(m) for m in mats[:-1]] + [_gather_rows(mats[-1])]
     stacked = jnp.concatenate(gains, axis=0)
     z = _z_gather(stacked)
     full = z.transpose(1, 0, 2).reshape(stacked.shape[0], NF_FAST * stacked.shape[1])
@@ -121,7 +129,7 @@
         total = total + lax.ppermute(
             part.astype(jnp.bfloat16), "fsdp", [(i, (i + k) % NF_FAST) for i in range(NF_FAST)]
         ).astype(jnp.float32)
-    x = _take(_plane_gather(total), jnp.arange(NDP_FAST, dtype=jnp.int32) ^ d, 0)
+    x = lax.all_gather(total, "dp", axis=0, tiled=False)
     x = x.reshape(n_chips, 2, rows, cols)
     x = jnp.concatenate([x[:, 0], x[:, 1]], axis=-1)
     return x.reshape(n_chips * rows, 2 * cols)

time: 493 us -> 515 us (1.045)
  the two profiles are of different devices: /device:TPU:8 before, /device:TPU:0 now
where the time goes in v12:
time: 515 us; the launch traced here: 507 us
  matrix products  117 us (23%)
  waiting for transfers between devices  110 us (21%)
  local copies, waits for them, and re-layouts  107 us (21%)
  other arithmetic  77.7 us (15%)
  starting transfers between devices  69.7 us (14%)
  between operations  15.9 us (3%)
  blocking collectives  9.94 us (2%)
    ppermute x15, starting transfers between devices, _z_gather(): lax.ppermute(piece, 'fsdp', [(i, (i + k) % NF_FAST) for i in range(NF_FAS...  36.5 us
    unnamed x166, local copies, waits for them, and re-layouts  33.5 us
    ppermute x4, waiting for transfers between devices, _reduce_matrix(): lax.ppermute(to_x.astype(jnp.bfloat16), 'dp', [(i, i ^ 2) for i in range(...  32 us
    ppermute x12, waiting for transfers between devices, _reduce_matrix(): lax.ppermute(part.astype(jnp.bfloat16), 'fsdp', [(i, (i + k) % NF_FAST) f...  27.4 us
    dot_general x1, matrix products, layer(): up_pre = jnp.dot(second_low, full_up, preferred_element_type=jnp.float32)  22.1 us
    ppermute x4, waiting for transfers between devices, _reduce_matrix(): lax.ppermute(of_chip(j ^ 3).astype(jnp.bfloat16), 'dp', [(i, i ^ 2) if i...  18.2 us
    ppermute x1, waiting for transfers between devices, _plane_gather(): lax.ppermute(send, 'dp', [(i, i ^ 2) if i % 2 == 0 else (i, i ^ 4) for i...  16.8 us
    ppermute x12, starting transfers between devices, _reduce_matrix(): lax.ppermute(part.astype(jnp.bfloat16), 'fsdp', [(i, (i + k) % NF_FAST) f...  15.7 us
  transfers between devices with their start and end apart: 53, of which 24 were waited for; matrix products, arithmetic and copies ran while one was open for 31% of the time, Pallas kernels for 0%

profile of v12, /device:TPU:0, one launch (start us, length us, event | category | flops | bytes accessed | tf_op | source)
XLA Modules:
  0.0 507.4 jit_solution(5531059308621224657)
XLA Ops:
  8.1 4.1 collective-permute-start.7
  21.2 3.4 collective-permute-start.3
  26.0 4.3 collective-permute-done.4
  35.1 3.5 collective-permute-start.14
  38.7 6.7 %collective-permute-done.13 = bf16[96,768]{1,0:T(8,128)(2,1)S(1)} collective-permute-done((bf16[96,768]{1,0:T(8,128)(2,1)S(1)}, bf16[96,768]{1,0:T(8,128)(2,1)S(1)}, u32[]{:S(2)}, u32[]{:S(2)}) %collective-permute-start.13) | collective-permute-done | bytes 147488 | tf_op jit(solution)/shard_map/ppermute | solution.py:61
  52.4 3.8 collective-permute-start.2
  60.1 7.5 %collective-permute-start.10 = (bf16[48,1536]{1,0:T(8,128)(2,1)}, bf16[48,1536]{1,0:T(8,128)(2,1)S(1)}, u32[]{:S(2)}, u32[]{:S(2)}) collective-permute-start(bf16[48,1536]{1,0:T(8,128)(2,1)} %dynamic_slice.152), channel_id=1, source_target_pairs={{0,2},{1,3},{2,0},{3,1},{4,6},{5,7},{6,4},{7,5},{8,10},{9,11},{10,... | collective-permute-start | bytes 442376 | tf_op jit(solution)/shard_map/ppermute | solution.py:61
  70.3 16.8 %collective-permute-done.17 = bf16[4,96,768]{2,1,0:T(8,128)(2,1)S(1)} collective-permute-done((bf16[4,96,768]{2,1,0:T(8,128)(2,1)S(1)}, bf16[4,96,768]{2,1,0:T(8,128)(2,1)S(1)}, u32[]{:S(2)}, u32[]{:S(2)}) %collective-permute-start.17) | collective-permute-done | bytes 589856 | tf_op jit(solution)/shard_map/ppermute | solution.py:46
  127.0 5.5 %gather_fusion.5 = bf16[8,4,96,768]{3,2,1,0:T(8,128)(2,1)} fusion(bf16[8,4,96,768]{3,2,1,0:T(8,128)(2,1)} %slice_dynamic-update-slice_fusion, s32[1024]{0:T(1024)} %pad_clamp_fusion), kind=kCustom, calls=%fused_computation.5 | custom fusion | bytes 9437216 | tf_op jit(solution)/shard_map/jit(_take)/gather | solution.py:55
  132.5 5.5 %copy.138 = bf16[4,8,96,768]{3,2,1,0:T(8,128)(2,1)} copy(bf16[4,8,96,768]{3,2,0,1:T(8,128)(2,1)} %bitcast.249) | data formatting | bytes 9437184 | tf_op jit(solution)/shard_map/transpose | solution.py:84
  147.1 3.5 fusion.120
  158.4 8.1 %fusion.129 = (f32[12,576]{1,0:T(8,128)S(1)}, f32[12,576,576]{1,2,0:T(8,128)}) fusion(f32[576,12,64]{0,2,1:T(8,128)S(1)} %bitcast.245, f32[12,64]{1,0:T(8,128)S(1)} %mul.354, f32[576,12]{0,1:T(8,128)S(1)} %fusion.96, f32[576,12]{0,1:T(8,128)S(1)} %broadcast_multiply_fusion, f32[576,12,64]{0,2,1:T(8,128)S(1)} %bitcast.237, f32[12,64]{1,0:T(8,128)S(1)} %copy-done.45, ...), kind=kOutput, calls=%fused_computation.287 | convolution fusion | flops 525083904 | bytes 19940352 | tf_op jit(solution)/shard_map/while/body/eval_jaxpr/qhd,khd->hqk/dot_general | solution.py:206
  166.6 8.5 %fusion.3 = f32[12,576]{1,0:T(8,128)S(1)} fusion(f32[12,576,576]{1,2,0:T(8,128)} %get-tuple-element.150, f32[12,576]{1,0:T(8,128)S(1)} %get-tuple-element.149), kind=kLoop, calls=%fused_computation.15 | loop fusion | flops 7955712 | bytes 15980544 | tf_op jit(solution)/shard_map/while/body/eval_jaxpr/reduce_sum | solution.py:216
  175.1 9.8 %fusion.35 = bf16[12,64,576]{2,1,0:T(8,128)(2,1)S(1)} fusion(bf16[576,12,64]{0,2,1:T(8,128)(2,1)} %bitcast.271, f32[12,576,576]{1,2,0:T(8,128)} %get-tuple-element.150, f32[12,576]{1,0:T(8,128)S(1)} %fusion.3, f32[12,576]{1,0:T(8,128)S(1)} %get-tuple-element.149), kind=kOutput, calls=%fused_computation.105 | convolution fusion | flops 521994240 | bytes 17750016 | tf_op jit(solution)/shard_map/while/body/eval_jaxpr/hqk,khd->qhd/dot_general | solution.py:218
  187.6 2.9 fusion.121
  190.5 22.1 %multiply_convert_fusion = (bf16[576,3072]{1,0:T(8,128)(2,1)}, f32[576,3072]{1,0:T(8,128)}, f32[576,3072]{1,0:T(8,128)}) fusion(bf16[768,1536]{1,0:T(8,128)(2,1)S(1)} %bitcast.280, bf16[768,1536]{1,0:T(8,128)(2,1)S(1)} %bitcast.278, f32[576,768]{1,0:T(8,128)S(1)} %copy-done.11, f32[768]{0:T(1024)S(1)} %add.400, f32[768]{0:T(1024)S(1)} %mul.362, ...), kind=kOutput, calls=%fused_computation.25 | convolution fusion | flops 2844573696 | bytes 24193536 | tf_op jit(solution)/shard_map/dot_general | solution.py:228
  212.7 8.0 %add_convert_fusion = bf16[576,3072]{1,0:T(8,128)(2,1)S(1)} fusion(f32[576,3072]{1,0:T(8,128)} %get-tuple-element.104, f32[576,3072]{1,0:T(8,128)} %get-tuple-element.153, bf16[3072,768]{1,0:T(8,128)(2,1)S(1)} %bitcast.261, bf16[576,768]{1,0:T(8,128)(2,1)S(1)} %copy-done.27, f32[576]{0:T(1024)S(1)} %copy-done.51), kind=kOutput, calls=%fused_computation.24 | convolution fusion | flops 2744008704 | bytes 23300352 | tf_op jit(solution)/shard_map/dot_general | solution.py:237
  220.7 7.0 %multiply_reduce_fusion.2 = (f32[768]{0:T(1024)S(1)}, f32[576]{0:T(1024)S(1)}, f32[768]{0:T(1024)S(1)}, f32[576,768]{1,0:T(8,128)S(1)}) fusion(f32[576,768]{1,0:T(8,128)S(1)} %copy-done.11, f32[576]{0:T(1024)S(1)} %fusion.99, f32[576]{0:T(1024)S(1)} %broadcast_multiply_fusion.4, f32[768]{0:T(1024)S(1)} %mul.362, bf16[576,3072]{1,0:T(8,128)(2,1)S(1)} %add_convert_fusion, ...), kind=kOutput, calls=%fused_computation.92 | convolution fusion | flops 2730883072 | bytes 11812608 | tf_op jit(solution)/shard_map/dot_general | solution.py:243
  235.0 7.6 %convolution_convert_fusion = bf16[12,576,576]{1,2,0:T(8,128)(2,1)} fusion(bf16[576,12,64]{0,2,1:T(8,128)(2,1)} %bitcast.253, bf16[576,12,64]{0,2,1:T(8,128)(2,1)} %bitcast.272), kind=kOutput, calls=%fused_computation.39 | convolution fusion | flops 513589248 | bytes 9732096 | tf_op jit(solution)/shard_map/qhd,khd->hqk/dot_general | solution.py:257
  242.6 9.9 %fusion.36 = bf16[12,64,576]{2,1,0:T(8,128)(2,1)} fusion(bf16[576,12,64]{0,2,1:T(8,128)(2,1)S(1)} %bitcast.254, f32[12,576,576]{1,2,0:T(8,128)} %get-tuple-element.150, f32[12,576]{1,0:T(8,128)S(1)} %log_add_fusion), kind=kOutput, calls=%fused_computation.106 | convolution fusion | flops 518012928 | bytes 17722368 | tf_op jit(solution)/shard_map/hqk,qhd->khd/dot_general | solution.py:256
  252.5 12.9 %fusion = f32[12,576]{1,0:T(8,128)S(1)} fusion(bf16[12,576,576]{1,2,0:T(8,128)(2,1)} %convolution_convert_fusion, f32[12,576,576]{1,2,0:T(8,128)} %get-tuple-element.150, f32[12,576]{1,0:T(8,128)S(1)} %log_add_fusion), kind=kLoop, calls=%fused_computation.8 | loop fusion | flops 15918336 | bytes 23943168 | tf_op jit(solution)/shard_map/reduce_sum | solution.py:259
  266.1 6.2 %fusion.2 = bf16[12,576,576]{1,2,0:T(8,128)(2,1)} fusion(bf16[12,576,576]{1,2,0:T(8,128)(2,1)S(1)} %copy-done.5, f32[12,576,576]{1,2,0:T(8,128)S(1)} %bitcast.234, f32[12,576]{1,0:T(8,128)S(1)} %fusion, f32[12,576]{1,0:T(8,128)S(1)} %log_add_fusion), kind=kLoop, calls=%fused_computation.10 | loop fusion | flops 19906560 | bytes 31905792 | tf_op jit(solution)/shard_map/convert_element_type | solution.py:260
  272.4 8.2 %fusion.27 = (f32[576,12]{0,1:T(8,128)S(1)}, f32[12,64,576]{2,1,0:T(8,128)}) fusion(f32[576,12,64]{0,2,1:T(8,128)} %bitcast.244, f32[12,64]{1,0:T(8,128)S(1)} %copy-done.44, f32[576,12]{0,1:T(8,128)S(1)} %broadcast_multiply_fusion, bf16[12,576,576]{1,2,0:T(8,128)(2,1)} %fusion.2, f32[576,12,64]{0,2,1:T(8,128)S(1)} %bitcast.238, ...), kind=kOutput, calls=%fused_computation.75 | convolution fusion | flops 513139968 | bytes 13387776 | tf_op jit(solution)/shard_map/hqk,qhd->khd/dot_general | solution.py:265
  291.1 6.4 %fusion.39 = f32[768,2304]{1,0:T(8,128)} fusion(bf16[576,768]{0,1:T(8,128)(2,1)S(1)} %bitcast.296, bf16[576,768]{0,1:T(8,128)(2,1)S(1)} %bitcast.292, bf16[576,768]{0,1:T(8,128)(2,1)S(1)} %bitcast.294, bf16[576,768]{1,0:T(8,128)(2,1)S(1)} %copy-done.16, f32[768]{0:T(1024)S(1)} %copy-done.62, f32[768]{0:T(1024)S(1)} %copy-done.55, f32[576]{0:T(1024)S(1)} %copy-done.53, ...), kind=kOutput, calls=%fused_computation.110 | convolution fusion | flops 2049048576 | bytes 10627584 | tf_op jit(solution)/shard_map/dot_general | solution.py:283
  299.4 4.2 select_maximum_fusion
  303.6 3.2 copy-done.7
  308.9 6.1 %fusion.116 = f32[768,3072]{1,0:T(8,128)S(1)} fusion(bf16[576,3072]{1,0:T(8,128)(2,1)} %copy-done.26, f32[576,768]{1,0:T(8,128)S(1)} %copy-done.12, f32[768]{0:T(1024)S(1)} %add.400, f32[768]{0:T(1024)S(1)} %mul.362, f32[576]{0:T(1024)S(1)} %fusion.99, f32[576]{0:T(1024)S(1)} %broadcast_multiply_fusion.4), kind=kOutput, calls=%fused_computation.275 | convolution fusion | flops 2720120832 | bytes 14756352 | tf_op jit(solution)/shard_map/dot_general | solution.py:240
  315.0 3.7 copy-done.6
  331.0 4.9 collective-permute-done.20
  342.5 7.5 %collective-permute-done.21 = bf16[4,48,1280]{2,1,0:T(8,128)(2,1)S(1)} collective-permute-done((bf16[4,48,1280]{2,1,0:T(8,128)(2,1)S(1)}, bf16[4,48,1280]{2,1,0:T(8,128)(2,1)S(1)}, u32[]{:S(2)}, u32[]{:S(2)}) %collective-permute-start.21) | collective-permute-done | bytes 491552 | tf_op jit(solution)/shard_map/ppermute | solution.py:123
  351.2 3.8 collective-permute-start.25
  359.3 4.0 collective-permute-done.24
  370.1 5.1 %fusion.59 = f32[3072,768]{1,0:T(8,128)S(1)} fusion(bf16[576,3072]{1,0:T(8,128)(2,1)S(1)} %copy-done.70, bf16[576,768]{1,0:T(8,128)(2,1)} %param.19, f32[576]{0:T(1024)S(1)} %copy-done.51), kind=kOutput, calls=%fused_computation.151 | convolution fusion | flops 2719236096 | bytes 13863168 | tf_op jit(solution)/shard_map/dot_general | solution.py:236
  375.3 3.7 copy-done.22
  380.6 3.7 collective-permute-done.35
  386.4 3.8 collective-permute-start.39
  390.2 4.3 collective-permute-done.37
  394.5 6.1 %collective-permute-done.38 = bf16[48,1536]{1,0:T(8,128)(2,1)S(1)} collective-permute-done((bf16[48,1536]{1,0:T(8,128)(2,1)S(1)}, bf16[48,1536]{1,0:T(8,128)(2,1)S(1)}, u32[]{:S(2)}, u32[]{:S(2)}) %collective-permute-start.38) | collective-permute-done | bytes 147488 | tf_op jit(solution)/shard_map/ppermute | solution.py:129
  407.9 11.7 %collective-permute-done.41 = bf16[4,192,384]{2,1,0:T(8,128)(2,1)S(1)} collective-permute-done((bf16[4,192,384]{2,1,0:T(8,128)(2,1)S(1)}, bf16[4,192,384]{2,1,0:T(8,128)(2,1)S(1)}, u32[]{:S(2)}, u32[]{:S(2)}) %collective-permute-start.41) | collective-permute-done | bytes 589856 | tf_op jit(solution)/shard_map/ppermute | solution.py:116
  423.6 15.0 %collective-permute-done.42 = bf16[4,192,384]{2,1,0:T(8,128)(2,1)S(1)} collective-permute-done((bf16[4,192,384]{2,1,0:T(8,128)(2,1)S(1)}, bf16[4,192,384]{2,1,0:T(8,128)(2,1)S(1)}, u32[]{:S(2)}, u32[]{:S(2)}) %collective-permute-start.42) | collective-permute-done | bytes 589856 | tf_op jit(solution)/shard_map/ppermute | solution.py:123
  440.2 3.8 collective-permute-start.46
  445.8 3.1 collective-permute-done.44
  448.8 4.4 collective-permute-done.45
  454.1 7.4 %multiply_convert_fusion.3 = bf16[576,768]{1,0:T(8,128)(2,1)} fusion(f32[576,768]{1,0:T(8,128)S(1)} %copy-done.12, bf16[576,3072]{1,0:T(8,128)(2,1)} %get-tuple-element.103, bf16[3072,768]{1,0:T(8,128)(2,1)} %bitcast.258, f32[576]{0:T(1024)S(1)} %copy-done.51), kind=kOutput, calls=%fused_computation.98 | convolution fusion | flops 2719236096 | bytes 10914048 | tf_op jit(solution)/shard_map/dot_general | solution.py:231
  462.4 5.7 %collective-permute-done.28 = bf16[4,48,384]{2,1,0:T(8,128)(2,1)S(1)} collective-permute-done((bf16[4,48,384]{2,1,0:T(8,128)(2,1)S(1)}, bf16[4,48,384]{2,1,0:T(8,128)(2,1)S(1)}, u32[]{:S(2)}, u32[]{:S(2)}) %collective-permute-start.28) | collective-permute-done | bytes 147488 | tf_op jit(solution)/shard_map/ppermute | solution.py:123
  468.5 4.0 collective-permute-start.32
  474.4 3.0 collective-permute-done.31
  477.4 9.9 %all-gather.4 = f32[384,384]{1,0:T(8,128)S(1)} all-gather(f32[48,384]{1,0:T(8,128)S(1)} %fusion.91), channel_id=6, replica_groups=mesh['dp'=8,'fsdp'=4] {'dp'}, dimensions={0}, use_global_device_ids=true | all-gather | bytes 663552 | tf_op jit(solution)/shard_map/all_gather | solution.py:132
  (390 shorter events, 177.0 us)
Async XLA Ops:
  7.2 107.1 %all-gather.16.cloned.1.call-start = ((), (), s32[]{:S(2)}) async-start(), calls=%async_computation.1 | async-start | bytes 1327104 | tf_op jit(solution)/shard_map/all_gather | solution.py:73
  8.1 8.7 %collective-permute-start.7 = (bf16[48,384]{1,0:T(8,128)(2,1)S(1)}, bf16[48,384]{1,0:T(8,128)(2,1)S(1)}, u32[]{:S(2)}, u32[]{:S(2)}) collective-permute-start(bf16[48,384]{1,0:T(8,128)(2,1)S(1)} %dynamic_slice.151), channel_id=1, source_target_pairs={{0,2},{1,3},{2,0},{3,1},{4,6},{5,7},{6,4},{7,5},{8,10},{9,11},{10,... | collective-permute-start | bytes 110600 | tf_op jit(solution)/shard_map/ppermute | solution.py:61
  19.4 118.6 %all-gather.14.cloned.1.call-start = ((), (), s32[]{:S(2)}) async-start(), calls=%async_computation | async-start | bytes 3981312 | tf_op jit(solution)/shard_map/all_gather | solution.py:73
  20.4 9.9 %collective-permute-start.4 = (bf16[48,1152]{1,0:T(8,128)(2,1)S(1)}, bf16[48,1152]{1,0:T(8,128)(2,1)S(1)}, u32[]{:S(2)}, u32[]{:S(2)}) collective-permute-start(bf16[48,1152]{1,0:T(8,128)(2,1)S(1)} %dynamic_slice.150), channel_id=1, source_target_pairs={{0,2},{1,3},{2,0},{3,1},{4,6},{5,7},{6,4},{7,5},{8,10},{9,11},{10,... | collective-permute-start | bytes 331784 | tf_op jit(solution)/shard_map/ppermute | solution.py:61
  21.2 9.1 %collective-permute-start.3 = (bf16[48,1152]{1,0:T(8,128)(2,1)S(1)}, bf16[48,1152]{1,0:T(8,128)(2,1)S(1)}, u32[]{:S(2)}, u32[]{:S(2)}) collective-permute-start(bf16[48,1152]{1,0:T(8,128)(2,1)S(1)} %dynamic_slice.150), channel_id=1, source_target_pairs={{0,1},{1,2},{2,3},{3,0},{4,5},{5,6},{6,7},{7,4},{8,9},{9,10},{10,1... | collective-permute-start | bytes 331784 | tf_op jit(solution)/shard_map/ppermute | solution.py:61
  24.7 6.2 %collective-permute-start.5 = (bf16[48,1152]{1,0:T(8,128)(2,1)S(1)}, bf16[48,1152]{1,0:T(8,128)(2,1)S(1)}, u32[]{:S(2)}, u32[]{:S(2)}) collective-permute-start(bf16[48,1152]{1,0:T(8,128)(2,1)S(1)} %dynamic_slice.150), channel_id=1, source_target_pairs={{0,3},{1,0},{2,1},{3,2},{4,7},{5,4},{6,5},{7,6},{8,11},{9,8},{10,9... | collective-permute-start | bytes 331784 | tf_op jit(solution)/shard_map/ppermute | solution.py:61
  32.4 155.2 %all-gather.18.cloned.1.call-start = ((), (), s32[]{:S(2)}) async-start(), calls=%async_computation.2 | async-start | bytes 5308416 | tf_op jit(solution)/shard_map/all_gather | solution.py:73
  32.5 12.9 %collective-permute-start.13 = (bf16[96,768]{1,0:T(8,128)(2,1)S(1)}, bf16[96,768]{1,0:T(8,128)(2,1)S(1)}, u32[]{:S(2)}, u32[]{:S(2)}) collective-permute-start(bf16[96,768]{1,0:T(8,128)(2,1)S(1)} %constant_dynamic-slice_fusion.4), channel_id=1, source_target_pairs={{0,2},{1,3},{2,0},{3,1},{4,6},{5,7},{6,4},{7,5},{8,10},{9,11},{10,... | collective-permute-start | bytes 442376 | tf_op jit(solution)/shard_map/ppermute | solution.py:61
  34.8 10.6 %collective-permute-start.12 = (bf16[96,768]{1,0:T(8,128)(2,1)S(1)}, bf16[96,768]{1,0:T(8,128)(2,1)S(1)}, u32[]{:S(2)}, u32[]{:S(2)}) collective-permute-start(bf16[96,768]{1,0:T(8,128)(2,1)S(1)} %constant_dynamic-slice_fusion.4), channel_id=1, source_target_pairs={{0,1},{1,2},{2,3},{3,0},{4,5},{5,6},{6,7},{7,4},{8,9},{9,10},{10,1... | collective-permute-start | bytes 442376 | tf_op jit(solution)/shard_map/ppermute | solution.py:61
  35.1 10.3 %collective-permute-start.14 = (bf16[96,768]{1,0:T(8,128)(2,1)S(1)}, bf16[96,768]{1,0:T(8,128)(2,1)S(1)}, u32[]{:S(2)}, u32[]{:S(2)}) collective-permute-start(bf16[96,768]{1,0:T(8,128)(2,1)S(1)} %constant_dynamic-slice_fusion.4), channel_id=1, source_target_pairs={{0,3},{1,0},{2,1},{3,2},{4,7},{5,4},{6,5},{7,6},{8,11},{9,8},{10,9... | collective-permute-start | bytes 442376 | tf_op jit(solution)/shard_map/ppermute | solution.py:61
  46.1 14.0 %collective-permute-start.15 = (bf16[4,96,768]{2,1,0:T(8,128)(2,1)S(1)}, bf16[4,96,768]{2,1,0:T(8,128)(2,1)S(1)}, u32[]{:S(2)}, u32[]{:S(2)}) collective-permute-start(bf16[4,96,768]{2,1,0:T(8,128)(2,1)S(1)} %gather_fusion.4), channel_id=1, source_target_pairs={{0,8},{4,12},{8,0},{12,4},{16,24},{20,28},{24,16},{28,20},{1,9},{5... | collective-permute-start | bytes 1769480 | tf_op jit(solution)/shard_map/ppermute | solution.py:43
  47.7 20.0 %collective-permute-start.16 = (bf16[4,96,768]{2,1,0:T(8,128)(2,1)S(1)}, bf16[4,96,768]{2,1,0:T(8,128)(2,1)S(1)}, u32[]{:S(2)}, u32[]{:S(2)}) collective-permute-start(bf16[4,96,768]{2,1,0:T(8,128)(2,1)S(1)} %gather_fusion.4), channel_id=1, source_target_pairs={{0,16},{4,20},{8,24},{12,28},{16,0},{20,4},{24,8},{28,12},{1,17},{... | collective-permute-start | bytes 1769480 | tf_op jit(solution)/shard_map/ppermute | solution.py:44
  49.8 41.6 %collective-permute-start.1 = (bf16[6,192]{1,0:T(8,128)(2,1)S(1)}, bf16[6,192]{1,0:T(8,128)(2,1)S(1)}, u32[]{:S(2)}, u32[]{:S(2)}) collective-permute-start(bf16[6,192]{1,0:T(8,128)(2,1)S(1)} %get-tuple-element.148), channel_id=1, source_target_pairs={{0,2},{1,3},{2,0},{3,1},{4,6},{5,7},{6,4},{7,5},{8,10},{9,11},{10,... | collective-permute-start | bytes 6920 | tf_op jit(solution)/shard_map/ppermute | solution.py:61
  52.4 40.9 %collective-permute-start = (bf16[6,192]{1,0:T(8,128)(2,1)S(1)}, bf16[6,192]{1,0:T(8,128)(2,1)}, u32[]{:S(2)}, u32[]{:S(2)}) collective-permute-start(bf16[6,192]{1,0:T(8,128)(2,1)S(1)} %get-tuple-element.148), channel_id=1, source_target_pairs={{0,1},{1,2},{2,3},{3,0},{4,5},{5,6},{6,7},{7,4},{8,9},{9,10},{10,1... | collective-permute-start | bytes 6920 | tf_op jit(solution)/shard_map/ppermute | solution.py:61
  52.4 42.8 %collective-permute-start.2 = (bf16[6,192]{1,0:T(8,128)(2,1)S(1)}, bf16[6,192]{1,0:T(8,128)(2,1)}, u32[]{:S(2)}, u32[]{:S(2)}) collective-permute-start(bf16[6,192]{1,0:T(8,128)(2,1)S(1)} %get-tuple-element.148), channel_id=1, source_target_pairs={{0,3},{1,0},{2,1},{3,2},{4,7},{5,4},{6,5},{7,6},{8,11},{9,8},{10,9... | collective-permute-start | bytes 6920 | tf_op jit(solution)/shard_map/ppermute | solution.py:61
  60.1 48.8 %collective-permute-start.10 = (bf16[48,1536]{1,0:T(8,128)(2,1)}, bf16[48,1536]{1,0:T(8,128)(2,1)S(1)}, u32[]{:S(2)}, u32[]{:S(2)}) collective-permute-start(bf16[48,1536]{1,0:T(8,128)(2,1)} %dynamic_slice.152), channel_id=1, source_target_pairs={{0,2},{1,3},{2,0},{3,1},{4,6},{5,7},{6,4},{7,5},{8,10},{9,11},{10,... | collective-permute-start | bytes 442376 | tf_op jit(solution)/shard_map/ppermute | solution.py:61
  67.7 19.4 %collective-permute-start.17 = (bf16[4,96,768]{2,1,0:T(8,128)(2,1)S(1)}, bf16[4,96,768]{2,1,0:T(8,128)(2,1)S(1)}, u32[]{:S(2)}, u32[]{:S(2)}) collective-permute-start(bf16[4,96,768]{2,1,0:T(8,128)(2,1)S(1)} %broadcast_select_fusion), channel_id=1, source_target_pairs={{0,8},{4,20},{8,0},{12,28},{16,24},{20,4},{24,16},{28,12},{1,9},{5... | collective-permute-start | bytes 1769480 | tf_op jit(solution)/shard_map/ppermute | solution.py:46
  88.8 27.9 %collective-permute-start.18 = (bf16[4,4,96,768]{3,2,1,0:T(8,128)(2,1)}, bf16[4,4,96,768]{3,2,1,0:T(8,128)(2,1)}, u32[]{:S(2)}, u32[]{:S(2)}) collective-permute-start(bf16[4,4,96,768]{3,2,1,0:T(8,128)(2,1)} %pad_maximum_fusion.5), channel_id=1, source_target_pairs={{0,4},{4,0},{8,12},{12,8},{16,20},{20,16},{24,28},{28,24},{1,5},{5... | collective-permute-start | bytes 7077896 | tf_op jit(solution)/shard_map/ppermute | solution.py:50
  91.3 17.5 %collective-permute-start.9 = (bf16[48,1536]{1,0:T(8,128)(2,1)}, bf16[48,1536]{1,0:T(8,128)(2,1)}, u32[]{:S(2)}, u32[]{:S(2)}) collective-permute-start(bf16[48,1536]{1,0:T(8,128)(2,1)} %dynamic_slice.152), channel_id=1, source_target_pairs={{0,1},{1,2},{2,3},{3,0},{4,5},{5,6},{6,7},{7,4},{8,9},{9,10},{10,1... | collective-permute-start | bytes 442376 | tf_op jit(solution)/shard_map/ppermute | solution.py:61
  93.3 15.6 %collective-permute-start.11 = (bf16[48,1536]{1,0:T(8,128)(2,1)}, bf16[48,1536]{1,0:T(8,128)(2,1)}, u32[]{:S(2)}, u32[]{:S(2)}) collective-permute-start(bf16[48,1536]{1,0:T(8,128)(2,1)} %dynamic_slice.152), channel_id=1, source_target_pairs={{0,3},{1,0},{2,1},{3,2},{4,7},{5,4},{6,5},{7,6},{8,11},{9,8},{10,9... | collective-permute-start | bytes 442376 | tf_op jit(solution)/shard_map/ppermute | solution.py:61
  113.4 374.9 %all-gather.20.cloned.1.call-start = ((), (), s32[]{:S(2)}) async-start(), calls=%async_computation.3 | async-start | bytes 2211840 | tf_op jit(solution)/shard_map/all_gather | solution.py:132
  308.3 14.6 %collective-permute-start.19 = (bf16[4,4,48,1280]{3,2,1,0:T(8,128)(2,1)}, bf16[4,4,48,1280]{3,2,1,0:T(8,128)(2,1)}, u32[]{:S(2)}, u32[]{:S(2)}) collective-permute-start(bf16[4,4,48,1280]{3,2,1,0:T(8,128)(2,1)} %bitcast.57), channel_id=1, source_target_pairs={{0,4},{4,0},{8,12},{12,8},{16,20},{20,16},{24,28},{28,24},{1,5},{5... | collective-permute-start | bytes 5898248 | tf_op jit(solution)/shard_map/ppermute | solution.py:110
  320.5 19.6 %collective-permute-start.33 = (bf16[4,4,48,1536]{3,2,1,0:T(8,128)(2,1)}, bf16[4,4,48,1536]{3,2,1,0:T(8,128)(2,1)}, u32[]{:S(2)}, u32[]{:S(2)}) collective-permute-start(bf16[4,4,48,1536]{3,2,1,0:T(8,128)(2,1)} %bitcast.84), channel_id=1, source_target_pairs={{0,4},{4,0},{8,12},{12,8},{16,20},{20,16},{24,28},{28,24},{1,5},{5... | collective-permute-start | bytes 7077896 | tf_op jit(solution)/shard_map/ppermute | solution.py:110
  326.9 9.0 %collective-permute-start.20 = (bf16[4,48,1280]{2,1,0:T(8,128)(2,1)S(1)}, bf16[4,48,1280]{2,1,0:T(8,128)(2,1)}, u32[]{:S(2)}, u32[]{:S(2)}) collective-permute-start(bf16[4,48,1280]{2,1,0:T(8,128)(2,1)S(1)} %fusion.58), channel_id=1, source_target_pairs={{0,8},{4,20},{8,0},{12,28},{16,24},{20,4},{24,16},{28,12},{1,9},{5... | collective-permute-start | bytes 1474568 | tf_op jit(solution)/shard_map/ppermute | solution.py:116
  337.2 12.8 %collective-permute-start.21 = (bf16[4,48,1280]{2,1,0:T(8,128)(2,1)S(1)}, bf16[4,48,1280]{2,1,0:T(8,128)(2,1)S(1)}, u32[]{:S(2)}, u32[]{:S(2)}) collective-permute-start(bf16[4,48,1280]{2,1,0:T(8,128)(2,1)S(1)} %get-tuple-element.113), channel_id=1, source_target_pairs={{0,8},{4,12},{8,0},{12,4},{16,24},{20,28},{24,16},{28,20},{1,9},{5... | collective-permute-start | bytes 1474568 | tf_op jit(solution)/shard_map/ppermute | solution.py:123
  338.5 12.5 %collective-permute-start.22 = (bf16[4,48,1280]{2,1,0:T(8,128)(2,1)S(1)}, bf16[4,48,1280]{2,1,0:T(8,128)(2,1)S(1)}, u32[]{:S(2)}, u32[]{:S(2)}) collective-permute-start(bf16[4,48,1280]{2,1,0:T(8,128)(2,1)S(1)} %get-tuple-element.114), channel_id=1, source_target_pairs={{0,16},{4,20},{8,24},{12,28},{16,0},{20,4},{24,8},{28,12},{1,17},{... | collective-permute-start | bytes 1474568 | tf_op jit(solution)/shard_map/ppermute | solution.py:124
  351.2 8.1 %collective-permute-start.23 = (bf16[48,1280]{1,0:T(8,128)(2,1)S(1)}, bf16[48,1280]{1,0:T(8,128)(2,1)S(1)}, u32[]{:S(2)}, u32[]{:S(2)}) collective-permute-start(bf16[48,1280]{1,0:T(8,128)(2,1)S(1)} %get-tuple-element.133), channel_id=1, source_target_pairs={{0,1},{1,2},{2,3},{3,0},{4,5},{5,6},{6,7},{7,4},{8,9},{9,10},{10,1... | collective-permute-start | bytes 368648 | tf_op jit(solution)/shard_map/ppermute | solution.py:129
  351.2 8.1 %collective-permute-start.25 = (bf16[48,1280]{1,0:T(8,128)(2,1)S(1)}, bf16[48,1280]{1,0:T(8,128)(2,1)S(1)}, u32[]{:S(2)}, u32[]{:S(2)}) collective-permute-start(bf16[48,1280]{1,0:T(8,128)(2,1)S(1)} %get-tuple-element.134), channel_id=1, source_target_pairs={{0,3},{1,0},{2,1},{3,2},{4,7},{5,4},{6,5},{7,6},{8,11},{9,8},{10,9... | collective-permute-start | bytes 368648 | tf_op jit(solution)/shard_map/ppermute | solution.py:129
  355.0 8.3 %collective-permute-start.24 = (bf16[48,1280]{1,0:T(8,128)(2,1)S(1)}, bf16[48,1280]{1,0:T(8,128)(2,1)S(1)}, u32[]{:S(2)}, u32[]{:S(2)}) collective-permute-start(bf16[48,1280]{1,0:T(8,128)(2,1)S(1)} %get-tuple-element.135), channel_id=1, source_target_pairs={{0,2},{1,3},{2,0},{3,1},{4,6},{5,7},{6,4},{7,5},{8,10},{9,11},{10,... | collective-permute-start | bytes 368648 | tf_op jit(solution)/shard_map/ppermute | solution.py:129
  355.9 10.1 %collective-permute-start.34 = (bf16[4,48,1536]{2,1,0:T(8,128)(2,1)}, bf16[4,48,1536]{2,1,0:T(8,128)(2,1)S(1)}, u32[]{:S(2)}, u32[]{:S(2)}) collective-permute-start(bf16[4,48,1536]{2,1,0:T(8,128)(2,1)} %fusion.56), channel_id=1, source_target_pairs={{0,8},{4,20},{8,0},{12,28},{16,24},{20,4},{24,16},{28,12},{1,9},{5... | collective-permute-start | bytes 1769480 | tf_op jit(solution)/shard_map/ppermute | solution.py:116
  364.1 129.2 %all-gather.22.cloned.1.call-start = ((), (), s32[]{:S(2)}) async-start(), calls=%async_computation.4 | async-start | bytes 2654208 | tf_op jit(solution)/shard_map/all_gather | solution.py:132
  367.9 16.3 %collective-permute-start.35 = (bf16[4,48,1536]{2,1,0:T(8,128)(2,1)S(1)}, bf16[4,48,1536]{2,1,0:T(8,128)(2,1)S(1)}, u32[]{:S(2)}, u32[]{:S(2)}) collective-permute-start(bf16[4,48,1536]{2,1,0:T(8,128)(2,1)S(1)} %get-tuple-element.107), channel_id=1, source_target_pairs={{0,8},{4,12},{8,0},{12,4},{16,24},{20,28},{24,16},{28,20},{1,9},{5... | collective-permute-start | bytes 1769480 | tf_op jit(solution)/shard_map/ppermute | solution.py:123
  368.8 16.0 %collective-permute-start.36 = (bf16[4,48,1536]{2,1,0:T(8,128)(2,1)S(1)}, bf16[4,48,1536]{2,1,0:T(8,128)(2,1)S(1)}, u32[]{:S(2)}, u32[]{:S(2)}) collective-permute-start(bf16[4,48,1536]{2,1,0:T(8,128)(2,1)S(1)} %get-tuple-element.108), channel_id=1, source_target_pairs={{0,16},{4,20},{8,24},{12,28},{16,0},{20,4},{24,8},{28,12},{1,17},{... | collective-permute-start | bytes 1769480 | tf_op jit(solution)/shard_map/ppermute | solution.py:124
  380.6 23.5 %collective-permute-start.40 = (bf16[4,4,192,384]{3,2,1,0:T(8,128)(2,1)}, bf16[4,4,192,384]{3,2,1,0:T(8,128)(2,1)}, u32[]{:S(2)}, u32[]{:S(2)}) collective-permute-start(bf16[4,4,192,384]{3,2,1,0:T(8,128)(2,1)} %bitcast.97), channel_id=1, source_target_pairs={{0,4},{4,0},{8,12},{12,8},{16,20},{20,16},{24,28},{28,24},{1,5},{5... | collective-permute-start | bytes 7077896 | tf_op jit(solution)/shard_map/ppermute | solution.py:110
  386.3 8.2 %collective-permute-start.37 = (bf16[48,1536]{1,0:T(8,128)(2,1)S(1)}, bf16[48,1536]{1,0:T(8,128)(2,1)S(1)}, u32[]{:S(2)}, u32[]{:S(2)}) collective-permute-start(bf16[48,1536]{1,0:T(8,128)(2,1)S(1)} %get-tuple-element.128), channel_id=1, source_target_pairs={{0,1},{1,2},{2,3},{3,0},{4,5},{5,6},{6,7},{7,4},{8,9},{9,10},{10,1... | collective-permute-start | bytes 442376 | tf_op jit(solution)/shard_map/ppermute | solution.py:129
  386.4 8.1 %collective-permute-start.39 = (bf16[48,1536]{1,0:T(8,128)(2,1)S(1)}, bf16[48,1536]{1,0:T(8,128)(2,1)S(1)}, u32[]{:S(2)}, u32[]{:S(2)}) collective-permute-start(bf16[48,1536]{1,0:T(8,128)(2,1)S(1)} %get-tuple-element.129), channel_id=1, source_target_pairs={{0,3},{1,0},{2,1},{3,2},{4,7},{5,4},{6,5},{7,6},{8,11},{9,8},{10,9... | collective-permute-start | bytes 442376 | tf_op jit(solution)/shard_map/ppermute | solution.py:129
  390.2 10.4 %collective-permute-start.38 = (bf16[48,1536]{1,0:T(8,128)(2,1)S(1)}, bf16[48,1536]{1,0:T(8,128)(2,1)S(1)}, u32[]{:S(2)}, u32[]{:S(2)}) collective-permute-start(bf16[48,1536]{1,0:T(8,128)(2,1)S(1)} %get-tuple-element.130), channel_id=1, source_target_pairs={{0,2},{1,3},{2,0},{3,1},{4,6},{5,7},{6,4},{7,5},{8,10},{9,11},{10,... | collective-permute-start | bytes 442376 | tf_op jit(solution)/shard_map/ppermute | solution.py:129
  401.4 93.8 %all-gather.24.cloned.1.call-start = ((), (), s32[]{:S(2)}) async-start(), calls=%async_computation.5 | async-start | bytes 2654208 | tf_op jit(solution)/shard_map/all_gather | solution.py:132
  406.5 13.1 %collective-permute-start.41 = (bf16[4,192,384]{2,1,0:T(8,128)(2,1)S(1)}, bf16[4,192,384]{2,1,0:T(8,128)(2,1)S(1)}, u32[]{:S(2)}, u32[]{:S(2)}) collective-permute-start(bf16[4,192,384]{2,1,0:T(8,128)(2,1)S(1)} %fusion.57), channel_id=1, source_target_pairs={{0,8},{4,20},{8,0},{12,28},{16,24},{20,4},{24,16},{28,12},{1,9},{5... | collective-permute-start | bytes 1769480 | tf_op jit(solution)/shard_map/ppermute | solution.py:116
  419.9 18.7 %collective-permute-start.42 = (bf16[4,192,384]{2,1,0:T(8,128)(2,1)S(1)}, bf16[4,192,384]{2,1,0:T(8,128)(2,1)S(1)}, u32[]{:S(2)}, u32[]{:S(2)}) collective-permute-start(bf16[4,192,384]{2,1,0:T(8,128)(2,1)S(1)} %get-tuple-element.105), channel_id=1, source_target_pairs={{0,8},{4,12},{8,0},{12,4},{16,24},{20,28},{24,16},{28,20},{1,9},{5... | collective-permute-start | bytes 1769480 | tf_op jit(solution)/shard_map/ppermute | solution.py:123
  420.4 19.5 %collective-permute-start.43 = (bf16[4,192,384]{2,1,0:T(8,128)(2,1)S(1)}, bf16[4,192,384]{2,1,0:T(8,128)(2,1)S(1)}, u32[]{:S(2)}, u32[]{:S(2)}) collective-permute-start(bf16[4,192,384]{2,1,0:T(8,128)(2,1)S(1)} %get-tuple-element.106), channel_id=1, source_target_pairs={{0,16},{4,20},{8,24},{12,28},{16,0},{20,4},{24,8},{28,12},{1,17},{... | collective-permute-start | bytes 1769480 | tf_op jit(solution)/shard_map/ppermute | solution.py:124
  423.5 20.6 %collective-permute-start.26 = (bf16[4,4,48,384]{3,2,1,0:T(8,128)(2,1)S(1)}, bf16[4,4,48,384]{3,2,1,0:T(8,128)(2,1)S(1)}, u32[]{:S(2)}, u32[]{:S(2)}) collective-permute-start(bf16[4,4,48,384]{3,2,1,0:T(8,128)(2,1)S(1)} %bitcast.297), channel_id=1, source_target_pairs={{0,4},{4,0},{8,12},{12,8},{16,20},{20,16},{24,28},{28,24},{1,5},{5... | collective-permute-start | bytes 1769480 | tf_op jit(solution)/shard_map/ppermute | solution.py:110
  440.2 8.7 %collective-permute-start.44 = (bf16[192,384]{1,0:T(8,128)(2,1)S(1)}, bf16[192,384]{1,0:T(8,128)(2,1)S(1)}, u32[]{:S(2)}, u32[]{:S(2)}) collective-permute-start(bf16[192,384]{1,0:T(8,128)(2,1)S(1)} %get-tuple-element.125), channel_id=1, source_target_pairs={{0,1},{1,2},{2,3},{3,0},{4,5},{5,6},{6,7},{7,4},{8,9},{9,10},{10,1... | collective-permute-start | bytes 442376 | tf_op jit(solution)/shard_map/ppermute | solution.py:129
  440.2 8.6 %collective-permute-start.46 = (bf16[192,384]{1,0:T(8,128)(2,1)S(1)}, bf16[192,384]{1,0:T(8,128)(2,1)S(1)}, u32[]{:S(2)}, u32[]{:S(2)}) collective-permute-start(bf16[192,384]{1,0:T(8,128)(2,1)S(1)} %get-tuple-element.126), channel_id=1, source_target_pairs={{0,3},{1,0},{2,1},{3,2},{4,7},{5,4},{6,5},{7,6},{8,11},{9,8},{10,9... | collective-permute-start | bytes 442376 | tf_op jit(solution)/shard_map/ppermute | solution.py:129
  444.0 9.2 %collective-permute-start.45 = (bf16[192,384]{1,0:T(8,128)(2,1)S(1)}, bf16[192,384]{1,0:T(8,128)(2,1)S(1)}, u32[]{:S(2)}, u32[]{:S(2)}) collective-permute-start(bf16[192,384]{1,0:T(8,128)(2,1)S(1)} %get-tuple-element.127), channel_id=1, source_target_pairs={{0,2},{1,3},{2,0},{3,1},{4,6},{5,7},{6,4},{7,5},{8,10},{9,11},{10,... | collective-permute-start | bytes 442376 | tf_op jit(solution)/shard_map/ppermute | solution.py:129
  445.2 16.3 %collective-permute-start.27 = (bf16[4,48,384]{2,1,0:T(8,128)(2,1)S(1)}, bf16[4,48,384]{2,1,0:T(8,128)(2,1)S(1)}, u32[]{:S(2)}, u32[]{:S(2)}) collective-permute-start(bf16[4,48,384]{2,1,0:T(8,128)(2,1)S(1)} %fusion.78), channel_id=1, source_target_pairs={{0,8},{4,20},{8,0},{12,28},{16,24},{20,4},{24,16},{28,12},{1,9},{5... | collective-permute-start | bytes 442376 | tf_op jit(solution)/shard_map/ppermute | solution.py:116
  461.6 6.6 %collective-permute-start.28 = (bf16[4,48,384]{2,1,0:T(8,128)(2,1)S(1)}, bf16[4,48,384]{2,1,0:T(8,128)(2,1)S(1)}, u32[]{:S(2)}, u32[]{:S(2)}) collective-permute-start(bf16[4,48,384]{2,1,0:T(8,128)(2,1)S(1)} %get-tuple-element.123), channel_id=1, source_target_pairs={{0,8},{4,12},{8,0},{12,4},{16,24},{20,28},{24,16},{28,20},{1,9},{5... | collective-permute-start | bytes 442376 | tf_op jit(solution)/shard_map/ppermute | solution.py:123
  462.4 6.0 %collective-permute-start.29 = (bf16[4,48,384]{2,1,0:T(8,128)(2,1)S(1)}, bf16[4,48,384]{2,1,0:T(8,128)(2,1)S(1)}, u32[]{:S(2)}, u32[]{:S(2)}) collective-permute-start(bf16[4,48,384]{2,1,0:T(8,128)(2,1)S(1)} %get-tuple-element.124), channel_id=1, source_target_pairs={{0,16},{4,20},{8,24},{12,28},{16,0},{20,4},{24,8},{28,12},{1,17},{... | collective-permute-start | bytes 442376 | tf_op jit(solution)/shard_map/ppermute | solution.py:124
  (83 other events, 798.7 us)
Sparse Core Ops, SparseCore 0:
  19.5 25.1 all-gather.15
  47.2 41.3 all-gather.13
  113.5 37.0 all-gather.17
  364.2 28.8 all-gather.19
  401.5 35.2 all-gather.21
  454.2 27.9 all-gather.23

commit v13 on v9

--- a/solution.py
+++ b/solution.py
@@ -62,8 +62,29 @@
     return x.reshape(NF_FAST * m.shape[0], m.shape[1])
 
 
+def _gather_side_by_side(mats):
+    d = lax.axis_index("dp")
+    j, c = d // 2, d % 2
+    n_chips = NDP_FAST // 2
+    rows = mats[0].shape[0] // n_chips
+    halves = [m.shape[1] // 2 for m in mats]
+    piece = jnp.concatenate(
+        [lax.dynamic_slice(m, (j * rows, c * h), (rows, h)) for m, h in zip(mats, halves)], axis=1
+    )
+    x = lax.all_gather(_z_gather(piece), "dp", axis=1, tiled=False)
+    x = x.reshape(NF_FAST, n_chips, 2, rows, sum(halves))
+    out = []
+    offset = 0
+    for m, h in zip(mats, halves):
+        part = x[..., offset : offset + h]
+        full = jnp.concatenate([part[:, :, 0], part[:, :, 1]], axis=-1)
+        out.append(full.reshape(NF_FAST * m.shape[0], m.shape[1]))
+        offset += h
+    return out
+
+
 def fast_gather(mats, gains):
-    out = [_gather_matrix(m) for m in mats]
+    out = _gather_side_by_side(mats[:2]) + [_gather_matrix(m) for m in mats[2:]]
     stacked = jnp.concatenate(gains, axis=0)
     z = _z_gather(stacked)
     full = z.transpose(1, 0, 2).reshape(stacked.shape[0], NF_FAST * stacked.shape[1])

time: 486 us -> 512 us (1.053)
  waiting for transfers between devices: 130 us -> 170 us
  starting transfers between devices: 57.4 us -> 48.4 us
    all_gather x4 -> x2, waiting for transfers between devices: 36.7 us -> 64.8 us  [_gather_matrix(): x = lax.all_gather(z, 'dp', axis=1, tiled=False)]
    ppermute x15 -> x12, waiting for transfers between devices: 19.1 us -> 31.7 us  [_z_gather(): lax.ppermute(piece, 'fsdp', [(i, (i + k) % NF_FAST) for i in range(NF_FAS...]
    ppermute x15 -> x12, starting transfers between devices: 22.6 us -> 14.7 us  [_z_gather(): lax.ppermute(piece, 'fsdp', [(i, (i + k) % NF_FAST) for i in range(NF_FAS...]
    unnamed x137 -> x135, local copies, waits for them, and re-layouts: 20.3 us -> 24.4 us
    slice x4 -> x2, local copies, waits for them, and re-layouts: 13.1 us -> 9.99 us  [_gather_matrix(): x = jnp.concatenate([x[:, :, 0], x[:, :, 1]], axis=-1)]
  transfers between devices with their start and end apart: 50 -> 46, of which waited for: 30 -> 28; matrix products, arithmetic and copies ran while one was open for 27% -> 16% of each run, Pallas kernels for 0% -> 0%
where the time goes in v13:
time: 512 us; the launch traced here: 502 us
  waiting for transfers between devices  170 us (33%)
  matrix products  113 us (22%)
  local copies, waits for them, and re-layouts  80.4 us (16%)
  other arithmetic  64.4 us (13%)
  starting transfers between devices  48.4 us (9%)
  between operations  15.7 us (3%)
  blocking collectives  10.9 us (2%)
    all_gather x2, waiting for transfers between devices, _gather_matrix(): x = lax.all_gather(z, 'dp', axis=1, tiled=False)  64.8 us
    ppermute x12, waiting for transfers between devices, _z_gather(): lax.ppermute(piece, 'fsdp', [(i, (i + k) % NF_FAST) for i in range(NF_FAS...  31.7 us
    ppermute x4, waiting for transfers between devices, _reduce_matrix(): lax.ppermute(to_x.astype(jnp.bfloat16), 'dp', [(i, i ^ 2) for i in range(...  28.3 us
    unnamed x135, local copies, waits for them, and re-layouts  24.4 us
    ppermute x4, waiting for transfers between devices, _reduce_matrix(): lax.ppermute(of_chip(j ^ 3).astype(jnp.bfloat16), 'dp', [(i, i ^ 2) if i...  22.8 us
    dot_general x1, matrix products, layer(): up_pre = jnp.dot(second_low, full_up, preferred_element_type=jnp.float32)  22 us
    ppermute x12, starting transfers between devices, _reduce_matrix(): lax.ppermute(part.astype(jnp.bfloat16), 'fsdp', [(i, (i + k) % NF_FAST) f...  19.8 us
    ppermute x12, waiting for transfers between devices, _reduce_matrix(): lax.ppermute(part.astype(jnp.bfloat16), 'fsdp', [(i, (i + k) % NF_FAST) f...  19.7 us
  transfers between devices with their start and end apart: 46, of which 28 were waited for; matrix products, arithmetic and copies ran while one was open for 16% of the time, Pallas kernels for 0%

profile of v13, /device:TPU:8, one launch (start us, length us, event | category | flops | bytes accessed | tf_op | source)
XLA Modules:
  0.0 502.1 jit_solution(6710251223803954450)
XLA Ops:
  9.0 2.7 collective-permute-start.4
  13.7 5.0 %collective-permute-done.4 = bf16[48,1536]{1,0:T(8,128)(2,1)S(1)} collective-permute-done((bf16[48,1536]{1,0:T(8,128)(2,1)S(1)}, bf16[48,1536]{1,0:T(8,128)(2,1)S(1)}, u32[]{:S(2)}, u32[]{:S(2)}) %collective-permute-start.4) | collective-permute-done | bytes 147488 | tf_op jit(solution)/shard_map/ppermute | solution.py:47
  18.7 5.4 %collective-permute-done.3 = bf16[48,1536]{1,0:T(8,128)(2,1)S(1)} collective-permute-done((bf16[48,1536]{1,0:T(8,128)(2,1)S(1)}, bf16[48,1536]{1,0:T(8,128)(2,1)S(1)}, u32[]{:S(2)}, u32[]{:S(2)}) %collective-permute-start.3) | collective-permute-done | bytes 147488 | tf_op jit(solution)/shard_map/ppermute | solution.py:47
  33.8 4.7 collective-permute-done.9
  38.5 4.2 collective-permute-done.11
  48.8 4.3 collective-permute-done.7
  53.1 5.4 %collective-permute-done.6 = bf16[48,1536]{1,0:T(8,128)(2,1)S(1)} collective-permute-done((bf16[48,1536]{1,0:T(8,128)(2,1)S(1)}, bf16[48,1536]{1,0:T(8,128)(2,1)S(1)}, u32[]{:S(2)}, u32[]{:S(2)}) %collective-permute-start.6) | collective-permute-done | bytes 147488 | tf_op jit(solution)/shard_map/ppermute | solution.py:47
  71.3 2.4 fusion.24
  73.9 2.5 fusion.125
  78.4 28.5 %all-gather.18.cloned.1.call-done = bf16[4,1536,384]{2,1,0:T(8,128)(2,1)} async-done(((bf16[4,192,384]{2,1,0:T(8,128)(2,1)}), bf16[4,1536,384]{2,1,0:T(8,128)(2,1)}) %all-gather.18.cloned.1.call-update) | async-done | bytes 4718608 | tf_op jit(solution)/shard_map/all_gather | solution.py:59
  106.9 5.1 %fusion.123 = (bf16[4,4,1,192,384]{4,3,2,1,0:T(8,128)(2,1)}, bf16[4,4,1,192,384]{4,3,2,1,0:T(8,128)(2,1)}) fusion(bf16[4,4,2,192,384]{4,3,2,1,0:T(8,128)(2,1)} %bitcast.239), kind=kLoop, calls=%fused_computation.274 | loop fusion | bytes 9437184 | tf_op jit(solution)/shard_map/slice | solution.py:61
  112.0 36.2 %all-gather.16.cloned.1.call-done = bf16[4,384,1536]{2,1,0:T(8,128)(2,1)} async-done(((bf16[4,48,1536]{2,1,0:T(8,128)(2,1)}), bf16[4,384,1536]{2,1,0:T(8,128)(2,1)}) %all-gather.16.cloned.1.call-update) | async-done | bytes 4718608 | tf_op jit(solution)/shard_map/all_gather | solution.py:59
  148.2 4.9 fusion.124
  161.7 8.1 %fusion.132 = (f32[12,576]{1,0:T(8,128)S(1)}, f32[12,576,576]{1,2,0:T(8,128)}) fusion(f32[576,12,64]{0,2,1:T(8,128)S(1)} %bitcast.228, f32[12,64]{1,0:T(8,128)S(1)} %mul.356, f32[576,12]{0,1:T(8,128)S(1)} %fusion.95, f32[576,12]{0,1:T(8,128)S(1)} %broadcast_multiply_fusion, f32[576,12,64]{0,2,1:T(8,128)S(1)} %bitcast.220, f32[12,64]{1,0:T(8,128)S(1)} %mul.350, ...), kind=kOutput, calls=%fused_computation.283 | convolution fusion | flops 525083904 | bytes 19940352 | tf_op jit(solution)/shard_map/while/body/eval_jaxpr/qhd,khd->hqk/dot_general | solution.py:205
  169.8 8.5 %fusion.3 = f32[12,576]{1,0:T(8,128)S(1)} fusion(f32[12,576,576]{1,2,0:T(8,128)} %get-tuple-element.155, f32[12,576]{1,0:T(8,128)S(1)} %get-tuple-element.154), kind=kLoop, calls=%fused_computation.13 | loop fusion | flops 7955712 | bytes 15980544 | tf_op jit(solution)/shard_map/while/body/eval_jaxpr/reduce_sum | solution.py:215
  178.3 9.7 %fusion.37 = bf16[12,64,576]{2,1,0:T(8,128)(2,1)S(1)} fusion(bf16[576,12,64]{0,2,1:T(8,128)(2,1)} %bitcast.249, f32[12,576,576]{1,2,0:T(8,128)} %get-tuple-element.155, f32[12,576]{1,0:T(8,128)S(1)} %fusion.3, f32[12,576]{1,0:T(8,128)S(1)} %get-tuple-element.154), kind=kOutput, calls=%fused_computation.105 | convolution fusion | flops 521994240 | bytes 17750016 | tf_op jit(solution)/shard_map/while/body/eval_jaxpr/hqk,khd->qhd/dot_general | solution.py:217
  191.5 22.0 %multiply_convert_fusion = (bf16[576,3072]{1,0:T(8,128)(2,1)}, f32[576,3072]{1,0:T(8,128)}, f32[576,3072]{1,0:T(8,128)}) fusion(bf16[768,1536]{1,0:T(8,128)(2,1)S(1)} %bitcast.260, bf16[768,1536]{1,0:T(8,128)(2,1)S(1)} %bitcast.258, f32[576,768]{1,0:T(8,128)S(1)} %get-tuple-element.157, f32[768]{0:T(1024)S(1)} %add.378, f32[768]{0:T(1024)S(1)} %mul.363, ...), kind=kOutput, calls=%fused_computation.23 | convolution fusion | flops 2844573696 | bytes 24193536 | tf_op jit(solution)/shard_map/dot_general | solution.py:227
  213.5 8.1 %add_convert_fusion = bf16[576,3072]{1,0:T(8,128)(2,1)S(1)} fusion(f32[576,3072]{1,0:T(8,128)} %get-tuple-element.105, f32[576,3072]{1,0:T(8,128)} %get-tuple-element.158, bf16[3072,384]{1,0:T(8,128)(2,1)S(1)} %bitcast.257, bf16[3072,384]{1,0:T(8,128)(2,1)S(1)} %bitcast.255, bf16[576,768]{1,0:T(8,128)(2,1)S(1)} %copy-done.23, f32[576]{0:T(1024)S(1)} %fusion.96), kind=kOutput, calls=%fused_computation.22 | convolution fusion | flops 2753445888 | bytes 23300352 | tf_op jit(solution)/shard_map/dot_general | solution.py:236
  221.6 3.3 multiply_reduce_fusion.2
  232.2 7.6 %convolution_convert_fusion = bf16[12,576,576]{1,2,0:T(8,128)(2,1)} fusion(bf16[576,12,64]{0,2,1:T(8,128)(2,1)} %bitcast.235, bf16[576,12,64]{0,2,1:T(8,128)(2,1)} %bitcast.250), kind=kOutput, calls=%fused_computation.37 | convolution fusion | flops 513589248 | bytes 9732096 | tf_op jit(solution)/shard_map/qhd,khd->hqk/dot_general | solution.py:256
  239.7 9.9 %fusion.38 = bf16[12,64,576]{2,1,0:T(8,128)(2,1)} fusion(bf16[576,12,64]{0,2,1:T(8,128)(2,1)S(1)} %bitcast.236, f32[12,576,576]{1,2,0:T(8,128)} %get-tuple-element.155, f32[12,576]{1,0:T(8,128)S(1)} %log_add_fusion), kind=kOutput, calls=%fused_computation.106 | convolution fusion | flops 518012928 | bytes 17722368 | tf_op jit(solution)/shard_map/hqk,qhd->khd/dot_general | solution.py:255
  249.6 12.8 %fusion = f32[12,576]{1,0:T(8,128)S(1)} fusion(bf16[12,576,576]{1,2,0:T(8,128)(2,1)} %convolution_convert_fusion, f32[12,576,576]{1,2,0:T(8,128)} %get-tuple-element.155, f32[12,576]{1,0:T(8,128)S(1)} %log_add_fusion), kind=kLoop, calls=%fused_computation.6 | loop fusion | flops 15918336 | bytes 23943168 | tf_op jit(solution)/shard_map/reduce_sum | solution.py:258
  263.2 6.3 %fusion.2 = bf16[12,576,576]{1,2,0:T(8,128)(2,1)} fusion(bf16[12,576,576]{1,2,0:T(8,128)(2,1)S(1)} %copy-done.4, f32[12,576,576]{1,2,0:T(8,128)S(1)} %bitcast.217, f32[12,576]{1,0:T(8,128)S(1)} %fusion, f32[12,576]{1,0:T(8,128)S(1)} %log_add_fusion), kind=kLoop, calls=%fused_computation.8 | loop fusion | flops 19906560 | bytes 31905792 | tf_op jit(solution)/shard_map/convert_element_type | solution.py:259
  269.5 8.2 %fusion.29 = (f32[576,12]{0,1:T(8,128)S(1)}, f32[12,64,576]{2,1,0:T(8,128)}) fusion(f32[576,12,64]{0,2,1:T(8,128)} %bitcast.227, f32[12,64]{1,0:T(8,128)S(1)} %copy-done.43, f32[576,12]{0,1:T(8,128)S(1)} %broadcast_multiply_fusion, bf16[12,576,576]{1,2,0:T(8,128)(2,1)} %fusion.2, f32[576,12,64]{0,2,1:T(8,128)S(1)} %bitcast.221, f32[12,64]{1,0:T(8,128)S(1)} %mul.350, ...), kind=kOutput, calls=%fused_computation.75 | convolution fusion | flops 513139968 | bytes 13387776 | tf_op jit(solution)/shard_map/hqk,qhd->khd/dot_general | solution.py:264
  285.5 2.8 fusion.119
  288.3 6.4 %fusion.41 = f32[768,2304]{1,0:T(8,128)} fusion(bf16[576,768]{0,1:T(8,128)(2,1)S(1)} %bitcast.275, bf16[576,768]{0,1:T(8,128)(2,1)S(1)} %bitcast.271, bf16[576,768]{0,1:T(8,128)(2,1)S(1)} %bitcast.273, bf16[576,768]{1,0:T(8,128)(2,1)S(1)} %copy-done.13, f32[768]{0:T(1024)S(1)} %copy-done.53, f32[768]{0:T(1024)S(1)} %copy-done.51, f32[576]{0:T(1024)S(1)} %copy-done.49, ...), kind=kOutput, calls=%fused_computation.110 | convolution fusion | flops 2049048576 | bytes 10627584 | tf_op jit(solution)/shard_map/dot_general | solution.py:282
  296.0 4.2 select_maximum_fusion
  300.2 3.1 copy-done.6
  305.5 6.1 %fusion.118 = f32[768,3072]{1,0:T(8,128)S(1)} fusion(bf16[576,3072]{1,0:T(8,128)(2,1)} %copy-done.22, f32[576,768]{1,0:T(8,128)S(1)} %copy-done.10, f32[768]{0:T(1024)S(1)} %add.378, f32[768]{0:T(1024)S(1)} %mul.363, f32[576]{0:T(1024)S(1)} %fusion.98, f32[576]{0:T(1024)S(1)} %broadcast_multiply_fusion.4), kind=kOutput, calls=%fused_computation.270 | convolution fusion | flops 2720120832 | bytes 14756352 | tf_op jit(solution)/shard_map/dot_general | solution.py:239
  311.6 3.7 copy-done.5
  325.3 2.8 constant_dynamic-slice_fusion.1
  328.1 4.6 collective-permute-done.13
  336.1 2.5 convert_add_fusion.1
  338.6 8.0 %collective-permute-done.14 = bf16[4,48,1280]{2,1,0:T(8,128)(2,1)S(1)} collective-permute-done((bf16[4,48,1280]{2,1,0:T(8,128)(2,1)S(1)}, bf16[4,48,1280]{2,1,0:T(8,128)(2,1)S(1)}, u32[]{:S(2)}, u32[]{:S(2)}) %collective-permute-start.14) | collective-permute-done | bytes 491552 | tf_op jit(solution)/shard_map/ppermute | solution.py:122
  350.1 2.4 collective-permute-start.17
  353.9 4.0 collective-permute-done.16
  360.2 3.2 collective-permute-done.27
  367.3 5.2 %fusion.61 = f32[3072,768]{1,0:T(8,128)S(1)} fusion(bf16[576,3072]{1,0:T(8,128)(2,1)S(1)} %copy-done.60, bf16[576,768]{1,0:T(8,128)(2,1)} %param.21, f32[576]{0:T(1024)S(1)} %fusion.96), kind=kOutput, calls=%fused_computation.146 | convolution fusion | flops 2719236096 | bytes 13863168 | tf_op jit(solution)/shard_map/dot_general | solution.py:235
  372.5 3.7 copy-done.19
  386.0 6.4 %collective-permute-done.30 = bf16[48,1536]{1,0:T(8,128)(2,1)S(1)} collective-permute-done((bf16[48,1536]{1,0:T(8,128)(2,1)S(1)}, bf16[48,1536]{1,0:T(8,128)(2,1)S(1)}, u32[]{:S(2)}, u32[]{:S(2)}) %collective-permute-start.30) | collective-permute-done | bytes 147488 | tf_op jit(solution)/shard_map/ppermute | solution.py:128
  395.3 2.6 constant_dynamic-slice_fusion
  401.1 14.9 %collective-permute-done.34 = bf16[4,192,384]{2,1,0:T(8,128)(2,1)S(1)} collective-permute-done((bf16[4,192,384]{2,1,0:T(8,128)(2,1)S(1)}, bf16[4,192,384]{2,1,0:T(8,128)(2,1)S(1)}, u32[]{:S(2)}, u32[]{:S(2)}) %collective-permute-start.34) | collective-permute-done | bytes 589856 | tf_op jit(solution)/shard_map/ppermute | solution.py:115
  419.8 12.7 %collective-permute-done.35 = bf16[4,192,384]{2,1,0:T(8,128)(2,1)S(1)} collective-permute-done((bf16[4,192,384]{2,1,0:T(8,128)(2,1)S(1)}, bf16[4,192,384]{2,1,0:T(8,128)(2,1)S(1)}, u32[]{:S(2)}, u32[]{:S(2)}) %collective-permute-start.35) | collective-permute-done | bytes 589856 | tf_op jit(solution)/shard_map/ppermute | solution.py:122
  441.5 2.8 collective-permute-done.39
  444.3 2.5 collective-permute-done.38
  447.7 7.4 %multiply_convert_fusion.3 = bf16[576,768]{1,0:T(8,128)(2,1)} fusion(f32[576,768]{1,0:T(8,128)S(1)} %copy-done.10, bf16[576,3072]{1,0:T(8,128)(2,1)} %get-tuple-element.104, bf16[3072,384]{1,0:T(8,128)(2,1)} %bitcast.256, bf16[3072,384]{1,0:T(8,128)(2,1)} %bitcast.254, f32[576]{0:T(1024)S(1)} %fusion.96), kind=kOutput, calls=%fused_computation.98 | convolution fusion | flops 2728673280 | bytes 10914048 | tf_op jit(solution)/shard_map/dot_general | solution.py:230
  457.7 5.5 %collective-permute-done.21 = bf16[4,48,384]{2,1,0:T(8,128)(2,1)S(1)} collective-permute-done((bf16[4,48,384]{2,1,0:T(8,128)(2,1)S(1)}, bf16[4,48,384]{2,1,0:T(8,128)(2,1)S(1)}, u32[]{:S(2)}, u32[]{:S(2)}) %collective-permute-start.21) | collective-permute-done | bytes 147488 | tf_op jit(solution)/shard_map/ppermute | solution.py:122
  471.2 10.9 %all-gather.4 = f32[384,384]{1,0:T(8,128)S(1)} all-gather(f32[48,384]{1,0:T(8,128)S(1)} %fusion.90), channel_id=6, replica_groups=mesh['dp'=8,'fsdp'=4] {'dp'}, dimensions={0}, use_global_device_ids=true | all-gather | bytes 663552 | tf_op jit(solution)/shard_map/all_gather | solution.py:131
  (337 shorter events, 142.3 us)
Async XLA Ops:
  7.2 61.8 %all-gather.14.cloned.1.call-start = ((), (), s32[]{:S(2)}) async-start(), calls=%async_computation | async-start | bytes 5308416 | tf_op jit(solution)/shard_map/all_gather | solution.py:74
  9.0 9.8 %collective-permute-start.4 = (bf16[48,1536]{1,0:T(8,128)(2,1)S(1)}, bf16[48,1536]{1,0:T(8,128)(2,1)S(1)}, u32[]{:S(2)}, u32[]{:S(2)}) collective-permute-start(bf16[48,1536]{1,0:T(8,128)(2,1)S(1)} %get-tuple-element.145), channel_id=1, source_target_pairs={{0,2},{1,3},{2,0},{3,1},{4,6},{5,7},{6,4},{7,5},{8,10},{9,11},{10,... | collective-permute-start | bytes 442376 | tf_op jit(solution)/shard_map/ppermute | solution.py:47
  11.6 12.5 %collective-permute-start.3 = (bf16[48,1536]{1,0:T(8,128)(2,1)S(1)}, bf16[48,1536]{1,0:T(8,128)(2,1)S(1)}, u32[]{:S(2)}, u32[]{:S(2)}) collective-permute-start(bf16[48,1536]{1,0:T(8,128)(2,1)S(1)} %get-tuple-element.145), channel_id=1, source_target_pairs={{0,1},{1,2},{2,3},{3,0},{4,5},{5,6},{6,7},{7,4},{8,9},{9,10},{10,1... | collective-permute-start | bytes 442376 | tf_op jit(solution)/shard_map/ppermute | solution.py:47
  11.6 12.5 %collective-permute-start.5 = (bf16[48,1536]{1,0:T(8,128)(2,1)S(1)}, bf16[48,1536]{1,0:T(8,128)(2,1)S(1)}, u32[]{:S(2)}, u32[]{:S(2)}) collective-permute-start(bf16[48,1536]{1,0:T(8,128)(2,1)S(1)} %get-tuple-element.145), channel_id=1, source_target_pairs={{0,3},{1,0},{2,1},{3,2},{4,7},{5,4},{6,5},{7,6},{8,11},{9,8},{10,9... | collective-permute-start | bytes 442376 | tf_op jit(solution)/shard_map/ppermute | solution.py:47
  25.6 81.3 %all-gather.18.cloned.1.call-start = ((), (), s32[]{:S(2)}) async-start(), calls=%async_computation.2 | async-start | bytes 5308416 | tf_op jit(solution)/shard_map/all_gather | solution.py:59
  26.6 7.2 %collective-permute-start.10 = (bf16[192,384]{1,0:T(8,128)(2,1)S(1)}, bf16[192,384]{1,0:T(8,128)(2,1)S(1)}, u32[]{:S(2)}, u32[]{:S(2)}) collective-permute-start(bf16[192,384]{1,0:T(8,128)(2,1)S(1)} %dynamic_slice.153), channel_id=1, source_target_pairs={{0,2},{1,3},{2,0},{3,1},{4,6},{5,7},{6,4},{7,5},{8,10},{9,11},{10,... | collective-permute-start | bytes 442376 | tf_op jit(solution)/shard_map/ppermute | solution.py:47
  27.0 11.5 %collective-permute-start.9 = (bf16[192,384]{1,0:T(8,128)(2,1)S(1)}, bf16[192,384]{1,0:T(8,128)(2,1)S(1)}, u32[]{:S(2)}, u32[]{:S(2)}) collective-permute-start(bf16[192,384]{1,0:T(8,128)(2,1)S(1)} %dynamic_slice.153), channel_id=1, source_target_pairs={{0,1},{1,2},{2,3},{3,0},{4,5},{5,6},{6,7},{7,4},{8,9},{9,10},{10,1... | collective-permute-start | bytes 442376 | tf_op jit(solution)/shard_map/ppermute | solution.py:47
  29.2 13.5 %collective-permute-start.11 = (bf16[192,384]{1,0:T(8,128)(2,1)S(1)}, bf16[192,384]{1,0:T(8,128)(2,1)S(1)}, u32[]{:S(2)}, u32[]{:S(2)}) collective-permute-start(bf16[192,384]{1,0:T(8,128)(2,1)S(1)} %dynamic_slice.153), channel_id=1, source_target_pairs={{0,3},{1,0},{2,1},{3,2},{4,7},{5,4},{6,5},{7,6},{8,11},{9,8},{10,9... | collective-permute-start | bytes 442376 | tf_op jit(solution)/shard_map/ppermute | solution.py:47
  44.3 103.9 %all-gather.16.cloned.1.call-start = ((), (), s32[]{:S(2)}) async-start(), calls=%async_computation.1 | async-start | bytes 5308416 | tf_op jit(solution)/shard_map/all_gather | solution.py:59
  45.4 7.7 %collective-permute-start.7 = (bf16[48,1536]{1,0:T(8,128)(2,1)S(1)}, bf16[48,1536]{1,0:T(8,128)(2,1)S(1)}, u32[]{:S(2)}, u32[]{:S(2)}) collective-permute-start(bf16[48,1536]{1,0:T(8,128)(2,1)S(1)} %dynamic_slice.152), channel_id=1, source_target_pairs={{0,2},{1,3},{2,0},{3,1},{4,6},{5,7},{6,4},{7,5},{8,10},{9,11},{10,... | collective-permute-start | bytes 442376 | tf_op jit(solution)/shard_map/ppermute | solution.py:47
  45.9 12.6 %collective-permute-start.6 = (bf16[48,1536]{1,0:T(8,128)(2,1)S(1)}, bf16[48,1536]{1,0:T(8,128)(2,1)S(1)}, u32[]{:S(2)}, u32[]{:S(2)}) collective-permute-start(bf16[48,1536]{1,0:T(8,128)(2,1)S(1)} %dynamic_slice.152), channel_id=1, source_target_pairs={{0,1},{1,2},{2,3},{3,0},{4,5},{5,6},{6,7},{7,4},{8,9},{9,10},{10,1... | collective-permute-start | bytes 442376 | tf_op jit(solution)/shard_map/ppermute | solution.py:47
  46.4 12.6 %collective-permute-start.8 = (bf16[48,1536]{1,0:T(8,128)(2,1)S(1)}, bf16[48,1536]{1,0:T(8,128)(2,1)S(1)}, u32[]{:S(2)}, u32[]{:S(2)}) collective-permute-start(bf16[48,1536]{1,0:T(8,128)(2,1)S(1)} %dynamic_slice.152), channel_id=1, source_target_pairs={{0,3},{1,0},{2,1},{3,2},{4,7},{5,4},{6,5},{7,6},{8,11},{9,8},{10,9... | collective-permute-start | bytes 442376 | tf_op jit(solution)/shard_map/ppermute | solution.py:47
  60.5 422.6 %all-gather.20.cloned.1.call-start = ((), (), s32[]{:S(2)}) async-start(), calls=%async_computation.3 | async-start | bytes 2211840 | tf_op jit(solution)/shard_map/all_gather | solution.py:131
  60.6 6.0 %collective-permute-start.1 = (bf16[6,192]{1,0:T(8,128)(2,1)S(1)}, bf16[6,192]{1,0:T(8,128)(2,1)S(1)}, u32[]{:S(2)}, u32[]{:S(2)}) collective-permute-start(bf16[6,192]{1,0:T(8,128)(2,1)S(1)} %get-tuple-element.153), channel_id=1, source_target_pairs={{0,2},{1,3},{2,0},{3,1},{4,6},{5,7},{6,4},{7,5},{8,10},{9,11},{10,... | collective-permute-start | bytes 6920 | tf_op jit(solution)/shard_map/ppermute | solution.py:47
  61.7 4.9 collective-permute-start
  62.7 3.9 collective-permute-start.2
  189.1 35.8 %copy-start.9 = (f32[576,768]{1,0:T(8,128)}, f32[576,768]{1,0:T(8,128)S(1)}, u32[]{:S(2)}) copy-start(f32[576,768]{1,0:T(8,128)S(1)} %get-tuple-element.157) | copy-start | bytes 5308420
  239.7 22.7 %slice-start.2 = ((s8[17694720]{0:T(1024)(128)(4,1)}), s8[917504]{0:T(1024)(128)(4,1)S(1)}, s32[]{:S(2)}) async-start(s8[17694720]{0:T(1024)(128)(4,1)} %bitcast.216), calls=%async_computation.8 | async-start | bytes 1835008
  304.8 14.8 %collective-permute-start.12 = (bf16[4,4,48,1280]{3,2,1,0:T(8,128)(2,1)}, bf16[4,4,48,1280]{3,2,1,0:T(8,128)(2,1)}, u32[]{:S(2)}, u32[]{:S(2)}) collective-permute-start(bf16[4,4,48,1280]{3,2,1,0:T(8,128)(2,1)} %bitcast.48), channel_id=1, source_target_pairs={{0,4},{4,0},{8,12},{12,8},{16,20},{20,16},{24,28},{28,24},{1,5},{5... | collective-permute-start | bytes 5898248 | tf_op jit(solution)/shard_map/ppermute | solution.py:109
  317.0 19.1 %collective-permute-start.26 = (bf16[4,4,48,1536]{3,2,1,0:T(8,128)(2,1)}, bf16[4,4,48,1536]{3,2,1,0:T(8,128)(2,1)}, u32[]{:S(2)}, u32[]{:S(2)}) collective-permute-start(bf16[4,4,48,1536]{3,2,1,0:T(8,128)(2,1)} %bitcast.75), channel_id=1, source_target_pairs={{0,4},{4,0},{8,12},{12,8},{16,20},{20,16},{24,28},{28,24},{1,5},{5... | collective-permute-start | bytes 7077896 | tf_op jit(solution)/shard_map/ppermute | solution.py:109
  323.8 9.0 %collective-permute-start.13 = (bf16[4,48,1280]{2,1,0:T(8,128)(2,1)S(1)}, bf16[4,48,1280]{2,1,0:T(8,128)(2,1)}, u32[]{:S(2)}, u32[]{:S(2)}) collective-permute-start(bf16[4,48,1280]{2,1,0:T(8,128)(2,1)S(1)} %fusion.60), channel_id=1, source_target_pairs={{0,8},{4,20},{8,0},{12,28},{16,24},{20,4},{24,16},{28,12},{1,9},{5... | collective-permute-start | bytes 1474568 | tf_op jit(solution)/shard_map/ppermute | solution.py:115
  334.0 12.6 %collective-permute-start.14 = (bf16[4,48,1280]{2,1,0:T(8,128)(2,1)S(1)}, bf16[4,48,1280]{2,1,0:T(8,128)(2,1)S(1)}, u32[]{:S(2)}, u32[]{:S(2)}) collective-permute-start(bf16[4,48,1280]{2,1,0:T(8,128)(2,1)S(1)} %get-tuple-element.120), channel_id=1, source_target_pairs={{0,8},{4,12},{8,0},{12,4},{16,24},{20,28},{24,16},{28,20},{1,9},{5... | collective-permute-start | bytes 1474568 | tf_op jit(solution)/shard_map/ppermute | solution.py:122
  335.6 12.3 %collective-permute-start.15 = (bf16[4,48,1280]{2,1,0:T(8,128)(2,1)S(1)}, bf16[4,48,1280]{2,1,0:T(8,128)(2,1)S(1)}, u32[]{:S(2)}, u32[]{:S(2)}) collective-permute-start(bf16[4,48,1280]{2,1,0:T(8,128)(2,1)S(1)} %get-tuple-element.121), channel_id=1, source_target_pairs={{0,16},{4,20},{8,24},{12,28},{16,0},{20,4},{24,8},{28,12},{1,17},{... | collective-permute-start | bytes 1474568 | tf_op jit(solution)/shard_map/ppermute | solution.py:123
  348.0 9.9 %collective-permute-start.16 = (bf16[48,1280]{1,0:T(8,128)(2,1)S(1)}, bf16[48,1280]{1,0:T(8,128)(2,1)S(1)}, u32[]{:S(2)}, u32[]{:S(2)}) collective-permute-start(bf16[48,1280]{1,0:T(8,128)(2,1)S(1)} %get-tuple-element.136), channel_id=1, source_target_pairs={{0,1},{1,2},{2,3},{3,0},{4,5},{5,6},{6,7},{7,4},{8,9},{9,10},{10,1... | collective-permute-start | bytes 368648 | tf_op jit(solution)/shard_map/ppermute | solution.py:128
  349.5 9.5 %collective-permute-start.18 = (bf16[48,1280]{1,0:T(8,128)(2,1)S(1)}, bf16[48,1280]{1,0:T(8,128)(2,1)S(1)}, u32[]{:S(2)}, u32[]{:S(2)}) collective-permute-start(bf16[48,1280]{1,0:T(8,128)(2,1)S(1)} %get-tuple-element.137), channel_id=1, source_target_pairs={{0,3},{1,0},{2,1},{3,2},{4,7},{5,4},{6,5},{7,6},{8,11},{9,8},{10,9... | collective-permute-start | bytes 368648 | tf_op jit(solution)/shard_map/ppermute | solution.py:128
  350.1 9.1 %collective-permute-start.17 = (bf16[48,1280]{1,0:T(8,128)(2,1)S(1)}, bf16[48,1280]{1,0:T(8,128)(2,1)S(1)}, u32[]{:S(2)}, u32[]{:S(2)}) collective-permute-start(bf16[48,1280]{1,0:T(8,128)(2,1)S(1)} %get-tuple-element.138), channel_id=1, source_target_pairs={{0,2},{1,3},{2,0},{3,1},{4,6},{5,7},{6,4},{7,5},{8,10},{9,11},{10,... | collective-permute-start | bytes 368648 | tf_op jit(solution)/shard_map/ppermute | solution.py:128
  353.4 10.1 %collective-permute-start.27 = (bf16[4,48,1536]{2,1,0:T(8,128)(2,1)}, bf16[4,48,1536]{2,1,0:T(8,128)(2,1)S(1)}, u32[]{:S(2)}, u32[]{:S(2)}) collective-permute-start(bf16[4,48,1536]{2,1,0:T(8,128)(2,1)} %fusion.58), channel_id=1, source_target_pairs={{0,8},{4,20},{8,0},{12,28},{16,24},{20,4},{24,16},{28,12},{1,9},{5... | collective-permute-start | bytes 1769480 | tf_op jit(solution)/shard_map/ppermute | solution.py:115
  360.0 128.1 %all-gather.22.cloned.1.call-start = ((), (), s32[]{:S(2)}) async-start(), calls=%async_computation.4 | async-start | bytes 2654208 | tf_op jit(solution)/shard_map/all_gather | solution.py:131
  365.4 14.5 %collective-permute-start.28 = (bf16[4,48,1536]{2,1,0:T(8,128)(2,1)S(1)}, bf16[4,48,1536]{2,1,0:T(8,128)(2,1)S(1)}, u32[]{:S(2)}, u32[]{:S(2)}) collective-permute-start(bf16[4,48,1536]{2,1,0:T(8,128)(2,1)S(1)} %get-tuple-element.108), channel_id=1, source_target_pairs={{0,8},{4,12},{8,0},{12,4},{16,24},{20,28},{24,16},{28,20},{1,9},{5... | collective-permute-start | bytes 1769480 | tf_op jit(solution)/shard_map/ppermute | solution.py:122
  366.0 14.2 %collective-permute-start.29 = (bf16[4,48,1536]{2,1,0:T(8,128)(2,1)S(1)}, bf16[4,48,1536]{2,1,0:T(8,128)(2,1)S(1)}, u32[]{:S(2)}, u32[]{:S(2)}) collective-permute-start(bf16[4,48,1536]{2,1,0:T(8,128)(2,1)S(1)} %get-tuple-element.109), channel_id=1, source_target_pairs={{0,16},{4,20},{8,24},{12,28},{16,0},{20,4},{24,8},{28,12},{1,17},{... | collective-permute-start | bytes 1769480 | tf_op jit(solution)/shard_map/ppermute | solution.py:123
  377.8 20.1 %collective-permute-start.33 = (bf16[4,4,192,384]{3,2,1,0:T(8,128)(2,1)}, bf16[4,4,192,384]{3,2,1,0:T(8,128)(2,1)}, u32[]{:S(2)}, u32[]{:S(2)}) collective-permute-start(bf16[4,4,192,384]{3,2,1,0:T(8,128)(2,1)} %bitcast.88), channel_id=1, source_target_pairs={{0,4},{4,0},{8,12},{12,8},{16,20},{20,16},{24,28},{28,24},{1,5},{5... | collective-permute-start | bytes 7077896 | tf_op jit(solution)/shard_map/ppermute | solution.py:109
  381.7 10.7 %collective-permute-start.30 = (bf16[48,1536]{1,0:T(8,128)(2,1)S(1)}, bf16[48,1536]{1,0:T(8,128)(2,1)S(1)}, u32[]{:S(2)}, u32[]{:S(2)}) collective-permute-start(bf16[48,1536]{1,0:T(8,128)(2,1)S(1)} %get-tuple-element.133), channel_id=1, source_target_pairs={{0,1},{1,2},{2,3},{3,0},{4,5},{5,6},{6,7},{7,4},{8,9},{9,10},{10,1... | collective-permute-start | bytes 442376 | tf_op jit(solution)/shard_map/ppermute | solution.py:128
  383.2 11.3 %collective-permute-start.32 = (bf16[48,1536]{1,0:T(8,128)(2,1)S(1)}, bf16[48,1536]{1,0:T(8,128)(2,1)S(1)}, u32[]{:S(2)}, u32[]{:S(2)}) collective-permute-start(bf16[48,1536]{1,0:T(8,128)(2,1)S(1)} %get-tuple-element.134), channel_id=1, source_target_pairs={{0,3},{1,0},{2,1},{3,2},{4,7},{5,4},{6,5},{7,6},{8,11},{9,8},{10,9... | collective-permute-start | bytes 442376 | tf_op jit(solution)/shard_map/ppermute | solution.py:128
  383.8 10.6 %collective-permute-start.31 = (bf16[48,1536]{1,0:T(8,128)(2,1)S(1)}, bf16[48,1536]{1,0:T(8,128)(2,1)S(1)}, u32[]{:S(2)}, u32[]{:S(2)}) collective-permute-start(bf16[48,1536]{1,0:T(8,128)(2,1)S(1)} %get-tuple-element.135), channel_id=1, source_target_pairs={{0,2},{1,3},{2,0},{3,1},{4,6},{5,7},{6,4},{7,5},{8,10},{9,11},{10,... | collective-permute-start | bytes 442376 | tf_op jit(solution)/shard_map/ppermute | solution.py:128
  395.3 94.7 %all-gather.24.cloned.1.call-start = ((), (), s32[]{:S(2)}) async-start(), calls=%async_computation.5 | async-start | bytes 2654208 | tf_op jit(solution)/shard_map/all_gather | solution.py:131
  400.4 15.7 %collective-permute-start.34 = (bf16[4,192,384]{2,1,0:T(8,128)(2,1)S(1)}, bf16[4,192,384]{2,1,0:T(8,128)(2,1)S(1)}, u32[]{:S(2)}, u32[]{:S(2)}) collective-permute-start(bf16[4,192,384]{2,1,0:T(8,128)(2,1)S(1)} %fusion.59), channel_id=1, source_target_pairs={{0,8},{4,20},{8,0},{12,28},{16,24},{20,4},{24,16},{28,12},{1,9},{5... | collective-permute-start | bytes 1769480 | tf_op jit(solution)/shard_map/ppermute | solution.py:115
  416.4 16.1 %collective-permute-start.35 = (bf16[4,192,384]{2,1,0:T(8,128)(2,1)S(1)}, bf16[4,192,384]{2,1,0:T(8,128)(2,1)S(1)}, u32[]{:S(2)}, u32[]{:S(2)}) collective-permute-start(bf16[4,192,384]{2,1,0:T(8,128)(2,1)S(1)} %get-tuple-element.106), channel_id=1, source_target_pairs={{0,8},{4,12},{8,0},{12,4},{16,24},{20,28},{24,16},{28,20},{1,9},{5... | collective-permute-start | bytes 1769480 | tf_op jit(solution)/shard_map/ppermute | solution.py:122
  416.5 16.0 %collective-permute-start.36 = (bf16[4,192,384]{2,1,0:T(8,128)(2,1)S(1)}, bf16[4,192,384]{2,1,0:T(8,128)(2,1)S(1)}, u32[]{:S(2)}, u32[]{:S(2)}) collective-permute-start(bf16[4,192,384]{2,1,0:T(8,128)(2,1)S(1)} %get-tuple-element.107), channel_id=1, source_target_pairs={{0,16},{4,20},{8,24},{12,28},{16,0},{20,4},{24,8},{28,12},{1,17},{... | collective-permute-start | bytes 1769480 | tf_op jit(solution)/shard_map/ppermute | solution.py:123
  419.6 19.4 %collective-permute-start.19 = (bf16[4,4,48,384]{3,2,1,0:T(8,128)(2,1)S(1)}, bf16[4,4,48,384]{3,2,1,0:T(8,128)(2,1)S(1)}, u32[]{:S(2)}, u32[]{:S(2)}) collective-permute-start(bf16[4,4,48,384]{3,2,1,0:T(8,128)(2,1)S(1)} %bitcast.276), channel_id=1, source_target_pairs={{0,4},{4,0},{8,12},{12,8},{16,20},{20,16},{24,28},{28,24},{1,5},{5... | collective-permute-start | bytes 1769480 | tf_op jit(solution)/shard_map/ppermute | solution.py:109
  432.7 8.8 %collective-permute-start.37 = (bf16[192,384]{1,0:T(8,128)(2,1)S(1)}, bf16[192,384]{1,0:T(8,128)(2,1)S(1)}, u32[]{:S(2)}, u32[]{:S(2)}) collective-permute-start(bf16[192,384]{1,0:T(8,128)(2,1)S(1)} %get-tuple-element.130), channel_id=1, source_target_pairs={{0,1},{1,2},{2,3},{3,0},{4,5},{5,6},{6,7},{7,4},{8,9},{9,10},{10,1... | collective-permute-start | bytes 442376 | tf_op jit(solution)/shard_map/ppermute | solution.py:128
  434.3 10.0 %collective-permute-start.39 = (bf16[192,384]{1,0:T(8,128)(2,1)S(1)}, bf16[192,384]{1,0:T(8,128)(2,1)S(1)}, u32[]{:S(2)}, u32[]{:S(2)}) collective-permute-start(bf16[192,384]{1,0:T(8,128)(2,1)S(1)} %get-tuple-element.131), channel_id=1, source_target_pairs={{0,3},{1,0},{2,1},{3,2},{4,7},{5,4},{6,5},{7,6},{8,11},{9,8},{10,9... | collective-permute-start | bytes 442376 | tf_op jit(solution)/shard_map/ppermute | solution.py:128
  436.6 10.2 %collective-permute-start.38 = (bf16[192,384]{1,0:T(8,128)(2,1)S(1)}, bf16[192,384]{1,0:T(8,128)(2,1)S(1)}, u32[]{:S(2)}, u32[]{:S(2)}) collective-permute-start(bf16[192,384]{1,0:T(8,128)(2,1)S(1)} %get-tuple-element.132), channel_id=1, source_target_pairs={{0,2},{1,3},{2,0},{3,1},{4,6},{5,7},{6,4},{7,5},{8,10},{9,11},{10,... | collective-permute-start | bytes 442376 | tf_op jit(solution)/shard_map/ppermute | solution.py:128
  440.1 15.0 %collective-permute-start.20 = (bf16[4,48,384]{2,1,0:T(8,128)(2,1)S(1)}, bf16[4,48,384]{2,1,0:T(8,128)(2,1)S(1)}, u32[]{:S(2)}, u32[]{:S(2)}) collective-permute-start(bf16[4,48,384]{2,1,0:T(8,128)(2,1)S(1)} %fusion.77), channel_id=1, source_target_pairs={{0,8},{4,20},{8,0},{12,28},{16,24},{20,4},{24,16},{28,12},{1,9},{5... | collective-permute-start | bytes 442376 | tf_op jit(solution)/shard_map/ppermute | solution.py:115
  455.1 8.0 %collective-permute-start.21 = (bf16[4,48,384]{2,1,0:T(8,128)(2,1)S(1)}, bf16[4,48,384]{2,1,0:T(8,128)(2,1)S(1)}, u32[]{:S(2)}, u32[]{:S(2)}) collective-permute-start(bf16[4,48,384]{2,1,0:T(8,128)(2,1)S(1)} %get-tuple-element.128), channel_id=1, source_target_pairs={{0,8},{4,12},{8,0},{12,4},{16,24},{20,28},{24,16},{28,20},{1,9},{5... | collective-permute-start | bytes 442376 | tf_op jit(solution)/shard_map/ppermute | solution.py:122
  456.4 7.4 %collective-permute-start.22 = (bf16[4,48,384]{2,1,0:T(8,128)(2,1)S(1)}, bf16[4,48,384]{2,1,0:T(8,128)(2,1)S(1)}, u32[]{:S(2)}, u32[]{:S(2)}) collective-permute-start(bf16[4,48,384]{2,1,0:T(8,128)(2,1)S(1)} %get-tuple-element.129), channel_id=1, source_target_pairs={{0,16},{4,20},{8,24},{12,28},{16,0},{20,4},{24,8},{28,12},{1,17},{... | collective-permute-start | bytes 442376 | tf_op jit(solution)/shard_map/ppermute | solution.py:123
  463.9 6.7 %collective-permute-start.23 = (bf16[48,384]{1,0:T(8,128)(2,1)S(1)}, bf16[48,384]{1,0:T(8,128)(2,1)S(1)}, u32[]{:S(2)}, u32[]{:S(2)}) collective-permute-start(bf16[48,384]{1,0:T(8,128)(2,1)S(1)} %get-tuple-element.141), channel_id=1, source_target_pairs={{0,1},{1,2},{2,3},{3,0},{4,5},{5,6},{6,7},{7,4},{8,9},{9,10},{10,1... | collective-permute-start | bytes 110600 | tf_op jit(solution)/shard_map/ppermute | solution.py:128
  465.4 5.1 %collective-permute-start.25 = (bf16[48,384]{1,0:T(8,128)(2,1)S(1)}, bf16[48,384]{1,0:T(8,128)(2,1)S(1)}, u32[]{:S(2)}, u32[]{:S(2)}) collective-permute-start(bf16[48,384]{1,0:T(8,128)(2,1)S(1)} %get-tuple-element.142), channel_id=1, source_target_pairs={{0,3},{1,0},{2,1},{3,2},{4,7},{5,4},{6,5},{7,6},{8,11},{9,8},{10,9... | collective-permute-start | bytes 110600 | tf_op jit(solution)/shard_map/ppermute | solution.py:128
  466.4 4.9 collective-permute-start.24
  (64 other events, 522.7 us)
Sparse Core Ops, SparseCore 0:
  25.7 39.8 all-gather.13
  68.1 38.7 all-gather.17
  109.4 38.7 all-gather.15
  360.1 30.7 all-gather.19
  395.4 35.0 all-gather.21
  447.8 32.7 all-gather.23

commit v14 on v9

--- a/solution.py
+++ b/solution.py
@@ -107,19 +107,36 @@
         total = total + lax.ppermute(
             part.astype(jnp.bfloat16), "fsdp", [(i, (i + k) % NF_FAST) for i in range(NF_FAST)]
         ).astype(jnp.float32)
-    x = lax.all_gather(total, "dp", axis=0, tiled=False)
-    x = x.reshape(n_chips, 2, rows, cols)
-    x = jnp.concatenate([x[:, 0], x[:, 1]], axis=-1)
-    return x.reshape(n_chips * rows, 2 * cols)
+    return total
+
+
+def _finish(totals):
+    x = lax.all_gather(jnp.concatenate(totals, axis=1), "dp", axis=0, tiled=False)
+    n_chips = NDP_FAST // 2
+    rows = totals[0].shape[0]
+    x = x.reshape(n_chips, 2, rows, x.shape[-1])
+    out = []
+    offset = 0
+    for t in totals:
+        part = x[..., offset : offset + t.shape[1]]
+        full = jnp.concatenate([part[:, 0], part[:, 1]], axis=-1)
+        out.append(full.reshape(n_chips * rows, 2 * t.shape[1]))
+        offset += t.shape[1]
+    return out
+
+
+def _reduce_one(g):
+    return _finish([_reduce_matrix(g)])[0]
 
 
 def fast_reduce(mats, gains):
     stacked = jnp.concatenate(gains, axis=0)
     pad = 2 * LANES - stacked.shape[0]
     first = jnp.concatenate([mats[0], jnp.pad(stacked.T, ((0, 0), (0, pad)))], axis=1)
-    shard = _reduce_matrix(first)
+    shards = _finish([_reduce_matrix(first)] + [_reduce_matrix(m) for m in mats[1:]])
+    shard = shards[0]
     width = mats[0].shape[1]
-    out = [shard[:, :width]] + [_reduce_matrix(m) for m in mats[1:]]
+    out = [shard[:, :width]] + shards[1:]
     mine = shard[:, width : width + stacked.shape[0]].T
     rows = 0
     for g in gains:
@@ -217,7 +234,7 @@
     pre_low = grad_pre.astype(jnp.bfloat16)
     grad_up = jnp.dot(second_low.T, pre_low, preferred_element_type=jnp.float32)
     if fast:
-        early = [_reduce_matrix(grad_up), _reduce_matrix(grad_down)]
+        early = [_reduce_one(grad_up), _reduce_one(grad_down)]
     grad_second = jnp.dot(pre_low, back_up.T, preferred_element_type=jnp.float32)
     grad_resid, gain_two, bias_two = second_back(grad_second)
     grad_resid = grad_resid + upstream

time: 486 us -> 479 us (0.986)
  waiting for transfers between devices: 130 us -> 155 us
  local copies, waits for them, and re-layouts: 81.1 us -> 69.2 us
  blocking collectives: 11.1 us -> 0 us
  matrix products: 114 us -> 109 us
    ppermute x4, waiting for transfers between devices: 21.4 us -> 36.4 us  [_reduce_matrix(): lax.ppermute(of_chip(j ^ 3).astype(jnp.bfloat16), 'dp', [(i, i ^ 2) if i...]
    all_gather x3, waiting for transfers between devices: 0.02 us -> 11.1 us  [_finish(): lax.all_gather(jnp.concatenate(totals, axis=1), 'dp', axis=0, tiled=False)]
    all_gather x1 -> x0, blocking collectives: 11.1 us -> none  [_reduce_matrix(): x = lax.all_gather(total, 'dp', axis=0, tiled=False)]
    unnamed x137 -> x129, local copies, waits for them, and re-layouts: 20.3 us -> 13.4 us
  transfers between devices with their start and end apart: 50 -> 50, of which waited for: 30 -> 30; matrix products, arithmetic and copies ran while one was open for 27% -> 25% of each run, Pallas kernels for 0% -> 0%
where the time goes in v14:
time: 479 us; the launch traced here: 471 us
  waiting for transfers between devices  155 us (32%)
  matrix products  109 us (23%)
  local copies, waits for them, and re-layouts  69.2 us (14%)
  other arithmetic  66.5 us (14%)
  starting transfers between devices  55.7 us (12%)
  between operations  15.8 us (3%)
    all_gather x4, waiting for transfers between devices, _gather_matrix(): x = lax.all_gather(z, 'dp', axis=1, tiled=False)  36.7 us
    ppermute x4, waiting for transfers between devices, _reduce_matrix(): lax.ppermute(of_chip(j ^ 3).astype(jnp.bfloat16), 'dp', [(i, i ^ 2) if i...  36.4 us
    ppermute x4, waiting for transfers between devices, _reduce_matrix(): lax.ppermute(to_x.astype(jnp.bfloat16), 'dp', [(i, i ^ 2) for i in range(...  28.5 us
    ppermute x12, waiting for transfers between devices, _reduce_matrix(): lax.ppermute(part.astype(jnp.bfloat16), 'fsdp', [(i, (i + k) % NF_FAST) f...  23.4 us
    ppermute x15, starting transfers between devices, _z_gather(): lax.ppermute(piece, 'fsdp', [(i, (i + k) % NF_FAST) for i in range(NF_FAS...  22.6 us
    dot_general x1, matrix products, layer(): up_pre = jnp.dot(second_low, full_up, preferred_element_type=jnp.float32)  22.1 us
    ppermute x12, starting transfers between devices, _reduce_matrix(): lax.ppermute(part.astype(jnp.bfloat16), 'fsdp', [(i, (i + k) % NF_FAST) f...  21.2 us
    ppermute x15, waiting for transfers between devices, _z_gather(): lax.ppermute(piece, 'fsdp', [(i, (i + k) % NF_FAST) for i in range(NF_FAS...  19 us
  transfers between devices with their start and end apart: 50, of which 30 were waited for; matrix products, arithmetic and copies ran while one was open for 25% of the time, Pallas kernels for 0%

profile of v14, /device:TPU:8, one launch (start us, length us, event | category | flops | bytes accessed | tf_op | source)
XLA Modules:
  0.0 471.5 jit_solution(15841785811063014717)
XLA Ops:
  8.0 2.6 collective-permute-start.7
  16.8 4.7 collective-permute-start.4
  24.4 2.5 collective-permute-done.4
  35.9 5.9 %collective-permute-done.13 = bf16[192,384]{1,0:T(8,128)(2,1)S(1)} collective-permute-done((bf16[192,384]{1,0:T(8,128)(2,1)S(1)}, bf16[192,384]{1,0:T(8,128)(2,1)S(1)}, u32[]{:S(2)}, u32[]{:S(2)}) %collective-permute-start.13) | collective-permute-done | bytes 147488 | tf_op jit(solution)/shard_map/ppermute | solution.py:47
  50.5 2.5 collective-permute-start.10
  53.0 2.8 collective-permute-start.9
  62.5 3.0 collective-permute-done.11
  69.5 9.9 %all-gather.15.cloned.1.call-done = bf16[4,384,1152]{2,1,0:T(8,128)(2,1)} async-done(((bf16[4,48,1152]{2,1,0:T(8,128)(2,1)}), bf16[4,384,1152]{2,1,0:T(8,128)(2,1)}) %all-gather.15.cloned.1.call-update) | async-done | bytes 3538960 | tf_op jit(solution)/shard_map/all_gather | solution.py:59
  88.6 3.7 fusion.119
  100.1 8.4 %fusion.129 = (f32[12,576]{1,0:T(8,128)S(1)}, f32[12,576,576]{1,2,0:T(8,128)}) fusion(f32[576,12,64]{0,2,1:T(8,128)S(1)} %bitcast.229, f32[12,64]{1,0:T(8,128)S(1)} %mul.355, f32[576,12]{0,1:T(8,128)S(1)} %fusion.95, f32[576,12]{0,1:T(8,128)S(1)} %broadcast_multiply_fusion, f32[576,12,64]{0,2,1:T(8,128)S(1)} %bitcast.221, f32[12,64]{1,0:T(8,128)S(1)} %mul.349, ...), kind=kOutput, calls=%fused_computation.275 | convolution fusion | flops 525083904 | bytes 19940352 | tf_op jit(solution)/shard_map/while/body/eval_jaxpr/qhd,khd->hqk/dot_general | solution.py:201
  108.5 8.7 %fusion.3 = f32[12,576]{1,0:T(8,128)S(1)} fusion(f32[12,576,576]{1,2,0:T(8,128)} %get-tuple-element.152, f32[12,576]{1,0:T(8,128)S(1)} %get-tuple-element.151), kind=kLoop, calls=%fused_computation.14 | loop fusion | flops 7955712 | bytes 15980544 | tf_op jit(solution)/shard_map/while/body/eval_jaxpr/reduce_sum | solution.py:211
  117.2 9.8 %fusion.37 = bf16[12,64,576]{2,1,0:T(8,128)(2,1)S(1)} fusion(bf16[576,12,64]{0,2,1:T(8,128)(2,1)} %bitcast.248, f32[12,576,576]{1,2,0:T(8,128)} %get-tuple-element.152, f32[12,576]{1,0:T(8,128)S(1)} %fusion.3, f32[12,576]{1,0:T(8,128)S(1)} %get-tuple-element.151), kind=kOutput, calls=%fused_computation.106 | convolution fusion | flops 521994240 | bytes 17750016 | tf_op jit(solution)/shard_map/while/body/eval_jaxpr/hqk,khd->qhd/dot_general | solution.py:213
  129.7 5.4 %fusion.120 = (bf16[4,4,1,192,384]{4,3,2,1,0:T(8,128)(2,1)}, bf16[4,4,1,192,384]{4,3,2,1,0:T(8,128)(2,1)}) fusion(bf16[4,4,2,192,384]{4,3,2,1,0:T(8,128)(2,1)} %bitcast.238), kind=kLoop, calls=%fused_computation.266 | loop fusion | bytes 9437184 | tf_op jit(solution)/shard_map/slice | solution.py:61
  135.1 26.8 %all-gather.19.cloned.1.call-done = bf16[4,384,1536]{2,1,0:T(8,128)(2,1)} async-done(((bf16[4,48,1536]{2,1,0:T(8,128)(2,1)}), bf16[4,384,1536]{2,1,0:T(8,128)(2,1)}) %all-gather.19.cloned.1.call-update) | async-done | bytes 4718608 | tf_op jit(solution)/shard_map/all_gather | solution.py:59
  161.9 3.0 fusion.121
  165.0 22.1 %multiply_convert_fusion = (bf16[576,3072]{1,0:T(8,128)(2,1)}, f32[576,3072]{1,0:T(8,128)}, f32[576,3072]{1,0:T(8,128)}) fusion(bf16[768,1536]{1,0:T(8,128)(2,1)S(1)} %bitcast.262, bf16[768,1536]{1,0:T(8,128)(2,1)S(1)} %bitcast.260, f32[576,768]{1,0:T(8,128)S(1)} %copy-done.6, f32[768]{0:T(1024)S(1)} %add.386, f32[768]{0:T(1024)S(1)} %mul.363, ...), kind=kOutput, calls=%fused_computation.24 | convolution fusion | flops 2844573696 | bytes 24193536 | tf_op jit(solution)/shard_map/dot_general | solution.py:223
  187.0 8.1 %add_convert_fusion = bf16[576,3072]{1,0:T(8,128)(2,1)S(1)} fusion(f32[576,3072]{1,0:T(8,128)} %get-tuple-element.104, f32[576,3072]{1,0:T(8,128)} %get-tuple-element.155, bf16[3072,384]{1,0:T(8,128)(2,1)S(1)} %bitcast.258, bf16[3072,384]{1,0:T(8,128)(2,1)S(1)} %bitcast.256, bf16[576,768]{1,0:T(8,128)(2,1)S(1)} %copy-done.17, f32[576]{0:T(1024)S(1)} %fusion.96), kind=kOutput, calls=%fused_computation.23 | convolution fusion | flops 2753445888 | bytes 23300352 | tf_op jit(solution)/shard_map/dot_general | solution.py:232
  195.2 3.3 multiply_reduce_fusion.2
  205.7 7.6 %convolution_convert_fusion = bf16[12,576,576]{1,2,0:T(8,128)(2,1)} fusion(bf16[576,12,64]{0,2,1:T(8,128)(2,1)} %bitcast.236, bf16[576,12,64]{0,2,1:T(8,128)(2,1)} %bitcast.249), kind=kOutput, calls=%fused_computation.38 | convolution fusion | flops 513589248 | bytes 9732096 | tf_op jit(solution)/shard_map/qhd,khd->hqk/dot_general | solution.py:252
  213.3 9.9 %fusion.38 = bf16[12,64,576]{2,1,0:T(8,128)(2,1)} fusion(bf16[576,12,64]{0,2,1:T(8,128)(2,1)S(1)} %bitcast.237, f32[12,576,576]{1,2,0:T(8,128)} %get-tuple-element.152, f32[12,576]{1,0:T(8,128)S(1)} %log_add_fusion), kind=kOutput, calls=%fused_computation.107 | convolution fusion | flops 518012928 | bytes 17722368 | tf_op jit(solution)/shard_map/hqk,qhd->khd/dot_general | solution.py:251
  223.2 12.8 %fusion = f32[12,576]{1,0:T(8,128)S(1)} fusion(bf16[12,576,576]{1,2,0:T(8,128)(2,1)} %convolution_convert_fusion, f32[12,576,576]{1,2,0:T(8,128)} %get-tuple-element.152, f32[12,576]{1,0:T(8,128)S(1)} %log_add_fusion), kind=kLoop, calls=%fused_computation.7 | loop fusion | flops 15918336 | bytes 23943168 | tf_op jit(solution)/shard_map/reduce_sum | solution.py:254
  236.8 6.3 %fusion.2 = bf16[12,576,576]{1,2,0:T(8,128)(2,1)} fusion(bf16[12,576,576]{1,2,0:T(8,128)(2,1)S(1)} %copy-done.3, f32[12,576,576]{1,2,0:T(8,128)S(1)} %bitcast.218, f32[12,576]{1,0:T(8,128)S(1)} %fusion, f32[12,576]{1,0:T(8,128)S(1)} %log_add_fusion), kind=kLoop, calls=%fused_computation.9 | loop fusion | flops 19906560 | bytes 31905792 | tf_op jit(solution)/shard_map/convert_element_type | solution.py:255
  243.1 8.2 %fusion.29 = (f32[576,12]{0,1:T(8,128)S(1)}, f32[12,64,576]{2,1,0:T(8,128)}) fusion(f32[576,12,64]{0,2,1:T(8,128)} %bitcast.228, f32[12,64]{1,0:T(8,128)S(1)} %copy-done.39, f32[576,12]{0,1:T(8,128)S(1)} %broadcast_multiply_fusion, bf16[12,576,576]{1,2,0:T(8,128)(2,1)} %fusion.2, f32[576,12,64]{0,2,1:T(8,128)S(1)} %bitcast.222, f32[12,64]{1,0:T(8,128)S(1)} %mul.349, ...), kind=kOutput, calls=%fused_computation.76 | convolution fusion | flops 513139968 | bytes 13387776 | tf_op jit(solution)/shard_map/hqk,qhd->khd/dot_general | solution.py:260
  259.1 2.7 fusion.116
  261.9 6.4 %fusion.41 = f32[768,2304]{1,0:T(8,128)} fusion(bf16[576,768]{0,1:T(8,128)(2,1)S(1)} %bitcast.278, bf16[576,768]{0,1:T(8,128)(2,1)S(1)} %bitcast.274, bf16[576,768]{0,1:T(8,128)(2,1)S(1)} %bitcast.276, bf16[576,768]{1,0:T(8,128)(2,1)S(1)} %copy-done.10, f32[768]{0:T(1024)S(1)} %copy-done.50, f32[768]{0:T(1024)S(1)} %copy-done.47, f32[576]{0:T(1024)S(1)} %copy-done.45, ...), kind=kOutput, calls=%fused_computation.111 | convolution fusion | flops 2049048576 | bytes 10627584 | tf_op jit(solution)/shard_map/dot_general | solution.py:278
  270.2 4.2 select_maximum_fusion
  280.0 4.2 fusion.115
  291.7 5.1 %collective-permute-done.16 = bf16[4,48,1280]{2,1,0:T(8,128)(2,1)S(1)} collective-permute-done((bf16[4,48,1280]{2,1,0:T(8,128)(2,1)S(1)}, bf16[4,48,1280]{2,1,0:T(8,128)(2,1)S(1)}, u32[]{:S(2)}, u32[]{:S(2)}) %collective-permute-start.16) | collective-permute-done | bytes 491552 | tf_op jit(solution)/shard_map/ppermute | solution.py:94
  299.0 2.6 constant_dynamic-slice_fusion.1
  303.8 5.2 %collective-permute-done.17 = bf16[4,48,1280]{2,1,0:T(8,128)(2,1)S(1)} collective-permute-done((bf16[4,48,1280]{2,1,0:T(8,128)(2,1)S(1)}, bf16[4,48,1280]{2,1,0:T(8,128)(2,1)S(1)}, u32[]{:S(2)}, u32[]{:S(2)}) %collective-permute-start.17) | collective-permute-done | bytes 491552 | tf_op jit(solution)/shard_map/ppermute | solution.py:101
  308.9 2.4 collective-permute-start.27
  315.2 5.5 %collective-permute-done.19 = bf16[48,1280]{1,0:T(8,128)(2,1)S(1)} collective-permute-done((bf16[48,1280]{1,0:T(8,128)(2,1)S(1)}, bf16[48,1280]{1,0:T(8,128)(2,1)S(1)}, u32[]{:S(2)}, u32[]{:S(2)}) %collective-permute-start.19) | collective-permute-done | bytes 122912 | tf_op jit(solution)/shard_map/ppermute | solution.py:107
  323.1 3.8 convert_add_fusion.1
  328.1 14.3 %collective-permute-done.30 = bf16[4,48,1536]{2,1,0:T(8,128)(2,1)S(1)} collective-permute-done((bf16[4,48,1536]{2,1,0:T(8,128)(2,1)S(1)}, bf16[4,48,1536]{2,1,0:T(8,128)(2,1)S(1)}, u32[]{:S(2)}, u32[]{:S(2)}) %collective-permute-start.30) | collective-permute-done | bytes 589856 | tf_op jit(solution)/shard_map/ppermute | solution.py:94
  344.5 4.0 fusion.61
  350.5 9.4 %collective-permute-done.31 = bf16[4,48,1536]{2,1,0:T(8,128)(2,1)S(1)} collective-permute-done((bf16[4,48,1536]{2,1,0:T(8,128)(2,1)S(1)}, bf16[4,48,1536]{2,1,0:T(8,128)(2,1)S(1)}, u32[]{:S(2)}, u32[]{:S(2)}) %collective-permute-start.31) | collective-permute-done | bytes 589856 | tf_op jit(solution)/shard_map/ppermute | solution.py:101
  361.9 2.7 collective-permute-start.35
  369.3 2.7 collective-permute-done.35
  372.0 2.5 collective-permute-done.34
  375.3 2.6 constant_dynamic-slice_fusion
  380.8 16.1 %collective-permute-done.37 = bf16[4,192,384]{2,1,0:T(8,128)(2,1)S(1)} collective-permute-done((bf16[4,192,384]{2,1,0:T(8,128)(2,1)S(1)}, bf16[4,192,384]{2,1,0:T(8,128)(2,1)S(1)}, u32[]{:S(2)}, u32[]{:S(2)}) %collective-permute-start.37) | collective-permute-done | bytes 589856 | tf_op jit(solution)/shard_map/ppermute | solution.py:94
  398.5 13.9 %collective-permute-done.38 = bf16[4,192,384]{2,1,0:T(8,128)(2,1)S(1)} collective-permute-done((bf16[4,192,384]{2,1,0:T(8,128)(2,1)S(1)}, bf16[4,192,384]{2,1,0:T(8,128)(2,1)S(1)}, u32[]{:S(2)}, u32[]{:S(2)}) %collective-permute-start.38) | collective-permute-done | bytes 589856 | tf_op jit(solution)/shard_map/ppermute | solution.py:101
  412.7 2.4 collective-permute-start.40
  420.5 5.1 %collective-permute-done.42 = bf16[192,384]{1,0:T(8,128)(2,1)S(1)} collective-permute-done((bf16[192,384]{1,0:T(8,128)(2,1)S(1)}, bf16[192,384]{1,0:T(8,128)(2,1)S(1)}, u32[]{:S(2)}, u32[]{:S(2)}) %collective-permute-start.42) | collective-permute-done | bytes 147488 | tf_op jit(solution)/shard_map/ppermute | solution.py:107
  425.6 2.8 collective-permute-done.41
  429.9 3.4 add_convert_fusion.3
  433.5 5.9 %multiply_convert_fusion.3 = bf16[576,768]{1,0:T(8,128)(2,1)} fusion(f32[576,768]{1,0:T(8,128)S(1)} %copy-done.7, bf16[576,3072]{1,0:T(8,128)(2,1)} %get-tuple-element.103, bf16[3072,384]{1,0:T(8,128)(2,1)S(1)} %bitcast.259, bf16[3072,384]{1,0:T(8,128)(2,1)S(1)} %bitcast.257, f32[576]{0:T(1024)S(1)} %fusion.96), kind=kOutput, calls=%fused_computation.99 | convolution fusion | flops 2728673280 | bytes 10914048 | tf_op jit(solution)/shard_map/dot_general | solution.py:226
  448.2 11.1 %all-gather.27.cloned.1.call-done = f32[1536,384]{1,0:T(8,128)} async-done(((f32[192,384]{1,0:T(8,128)}), f32[1536,384]{1,0:T(8,128)}) %all-gather.27.cloned.1.call-update) | async-done | bytes 2359312 | tf_op jit(solution)/shard_map/all_gather | solution.py:114
  (342 shorter events, 136.5 us)
Async XLA Ops:
  7.2 60.0 %all-gather.17.cloned.1.call-start = ((), (), s32[]{:S(2)}) async-start(), calls=%async_computation.1 | async-start | bytes 1327104 | tf_op jit(solution)/shard_map/all_gather | solution.py:59
  8.0 5.4 %collective-permute-start.7 = (bf16[48,384]{1,0:T(8,128)(2,1)S(1)}, bf16[48,384]{1,0:T(8,128)(2,1)S(1)}, u32[]{:S(2)}, u32[]{:S(2)}) collective-permute-start(bf16[48,384]{1,0:T(8,128)(2,1)S(1)} %dynamic_slice.151), channel_id=1, source_target_pairs={{0,2},{1,3},{2,0},{3,1},{4,6},{5,7},{6,4},{7,5},{8,10},{9,11},{10,... | collective-permute-start | bytes 110600 | tf_op jit(solution)/shard_map/ppermute | solution.py:47
  15.9 63.6 %all-gather.15.cloned.1.call-start = ((), (), s32[]{:S(2)}) async-start(), calls=%async_computation | async-start | bytes 3981312 | tf_op jit(solution)/shard_map/all_gather | solution.py:59
  16.8 10.1 %collective-permute-start.4 = (bf16[48,1152]{1,0:T(8,128)(2,1)S(1)}, bf16[48,1152]{1,0:T(8,128)(2,1)S(1)}, u32[]{:S(2)}, u32[]{:S(2)}) collective-permute-start(bf16[48,1152]{1,0:T(8,128)(2,1)S(1)} %dynamic_slice.150), channel_id=1, source_target_pairs={{0,2},{1,3},{2,0},{3,1},{4,6},{5,7},{6,4},{7,5},{8,10},{9,11},{10,... | collective-permute-start | bytes 331784 | tf_op jit(solution)/shard_map/ppermute | solution.py:47
  21.5 6.6 %collective-permute-start.3 = (bf16[48,1152]{1,0:T(8,128)(2,1)S(1)}, bf16[48,1152]{1,0:T(8,128)(2,1)S(1)}, u32[]{:S(2)}, u32[]{:S(2)}) collective-permute-start(bf16[48,1152]{1,0:T(8,128)(2,1)S(1)} %dynamic_slice.150), channel_id=1, source_target_pairs={{0,1},{1,2},{2,3},{3,0},{4,5},{5,6},{6,7},{7,4},{8,9},{9,10},{10,1... | collective-permute-start | bytes 331784 | tf_op jit(solution)/shard_map/ppermute | solution.py:47
  21.5 7.6 %collective-permute-start.5 = (bf16[48,1152]{1,0:T(8,128)(2,1)S(1)}, bf16[48,1152]{1,0:T(8,128)(2,1)S(1)}, u32[]{:S(2)}, u32[]{:S(2)}) collective-permute-start(bf16[48,1152]{1,0:T(8,128)(2,1)S(1)} %dynamic_slice.150), channel_id=1, source_target_pairs={{0,3},{1,0},{2,1},{3,2},{4,7},{5,4},{6,5},{7,6},{8,11},{9,8},{10,9... | collective-permute-start | bytes 331784 | tf_op jit(solution)/shard_map/ppermute | solution.py:47
  30.6 99.1 %all-gather.21.cloned.1.call-start = ((), (), s32[]{:S(2)}) async-start(), calls=%async_computation.3 | async-start | bytes 5308416 | tf_op jit(solution)/shard_map/all_gather | solution.py:59
  31.6 10.2 %collective-permute-start.13 = (bf16[192,384]{1,0:T(8,128)(2,1)S(1)}, bf16[192,384]{1,0:T(8,128)(2,1)S(1)}, u32[]{:S(2)}, u32[]{:S(2)}) collective-permute-start(bf16[192,384]{1,0:T(8,128)(2,1)S(1)} %dynamic_slice.153), channel_id=1, source_target_pairs={{0,2},{1,3},{2,0},{3,1},{4,6},{5,7},{6,4},{7,5},{8,10},{9,11},{10,... | collective-permute-start | bytes 442376 | tf_op jit(solution)/shard_map/ppermute | solution.py:47
  32.9 11.0 %collective-permute-start.12 = (bf16[192,384]{1,0:T(8,128)(2,1)S(1)}, bf16[192,384]{1,0:T(8,128)(2,1)S(1)}, u32[]{:S(2)}, u32[]{:S(2)}) collective-permute-start(bf16[192,384]{1,0:T(8,128)(2,1)S(1)} %dynamic_slice.153), channel_id=1, source_target_pairs={{0,1},{1,2},{2,3},{3,0},{4,5},{5,6},{6,7},{7,4},{8,9},{9,10},{10,1... | collective-permute-start | bytes 442376 | tf_op jit(solution)/shard_map/ppermute | solution.py:47
  33.8 11.5 %collective-permute-start.14 = (bf16[192,384]{1,0:T(8,128)(2,1)S(1)}, bf16[192,384]{1,0:T(8,128)(2,1)S(1)}, u32[]{:S(2)}, u32[]{:S(2)}) collective-permute-start(bf16[192,384]{1,0:T(8,128)(2,1)S(1)} %dynamic_slice.153), channel_id=1, source_target_pairs={{0,3},{1,0},{2,1},{3,2},{4,7},{5,4},{6,5},{7,6},{8,11},{9,8},{10,9... | collective-permute-start | bytes 442376 | tf_op jit(solution)/shard_map/ppermute | solution.py:47
  46.9 115.0 %all-gather.19.cloned.1.call-start = ((), (), s32[]{:S(2)}) async-start(), calls=%async_computation.2 | async-start | bytes 5308416 | tf_op jit(solution)/shard_map/all_gather | solution.py:59
  47.0 12.3 %collective-permute-start.1 = (bf16[6,192]{1,0:T(8,128)(2,1)S(1)}, bf16[6,192]{1,0:T(8,128)(2,1)S(1)}, u32[]{:S(2)}, u32[]{:S(2)}) collective-permute-start(bf16[6,192]{1,0:T(8,128)(2,1)S(1)} %get-tuple-element.150), channel_id=1, source_target_pairs={{0,2},{1,3},{2,0},{3,1},{4,6},{5,7},{6,4},{7,5},{8,10},{9,11},{10,... | collective-permute-start | bytes 6920 | tf_op jit(solution)/shard_map/ppermute | solution.py:47
  47.1 12.3 %collective-permute-start = (bf16[6,192]{1,0:T(8,128)(2,1)S(1)}, bf16[6,192]{1,0:T(8,128)(2,1)S(1)}, u32[]{:S(2)}, u32[]{:S(2)}) collective-permute-start(bf16[6,192]{1,0:T(8,128)(2,1)S(1)} %get-tuple-element.150), channel_id=1, source_target_pairs={{0,1},{1,2},{2,3},{3,0},{4,5},{5,6},{6,7},{7,4},{8,9},{9,10},{10,1... | collective-permute-start | bytes 6920 | tf_op jit(solution)/shard_map/ppermute | solution.py:47
  48.4 11.0 %collective-permute-start.2 = (bf16[6,192]{1,0:T(8,128)(2,1)S(1)}, bf16[6,192]{1,0:T(8,128)(2,1)S(1)}, u32[]{:S(2)}, u32[]{:S(2)}) collective-permute-start(bf16[6,192]{1,0:T(8,128)(2,1)S(1)} %get-tuple-element.150), channel_id=1, source_target_pairs={{0,3},{1,0},{2,1},{3,2},{4,7},{5,4},{6,5},{7,6},{8,11},{9,8},{10,9... | collective-permute-start | bytes 6920 | tf_op jit(solution)/shard_map/ppermute | solution.py:47
  50.5 11.3 %collective-permute-start.10 = (bf16[48,1536]{1,0:T(8,128)(2,1)S(1)}, bf16[48,1536]{1,0:T(8,128)(2,1)S(1)}, u32[]{:S(2)}, u32[]{:S(2)}) collective-permute-start(bf16[48,1536]{1,0:T(8,128)(2,1)S(1)} %dynamic_slice.152), channel_id=1, source_target_pairs={{0,2},{1,3},{2,0},{3,1},{4,6},{5,7},{6,4},{7,5},{8,10},{9,11},{10,... | collective-permute-start | bytes 442376 | tf_op jit(solution)/shard_map/ppermute | solution.py:47
  53.0 9.5 %collective-permute-start.9 = (bf16[48,1536]{1,0:T(8,128)(2,1)S(1)}, bf16[48,1536]{1,0:T(8,128)(2,1)S(1)}, u32[]{:S(2)}, u32[]{:S(2)}) collective-permute-start(bf16[48,1536]{1,0:T(8,128)(2,1)S(1)} %dynamic_slice.152), channel_id=1, source_target_pairs={{0,1},{1,2},{2,3},{3,0},{4,5},{5,6},{6,7},{7,4},{8,9},{9,10},{10,1... | collective-permute-start | bytes 442376 | tf_op jit(solution)/shard_map/ppermute | solution.py:47
  59.3 6.2 %collective-permute-start.11 = (bf16[48,1536]{1,0:T(8,128)(2,1)S(1)}, bf16[48,1536]{1,0:T(8,128)(2,1)S(1)}, u32[]{:S(2)}, u32[]{:S(2)}) collective-permute-start(bf16[48,1536]{1,0:T(8,128)(2,1)S(1)} %dynamic_slice.152), channel_id=1, source_target_pairs={{0,3},{1,0},{2,1},{3,2},{4,7},{5,4},{6,5},{7,6},{8,11},{9,8},{10,9... | collective-permute-start | bytes 442376 | tf_op jit(solution)/shard_map/ppermute | solution.py:47
  67.1 372.3 %all-gather.23.cloned.1.call-start = ((), (), s32[]{:S(2)}) async-start(), calls=%async_computation.4 | async-start | bytes 2875392 | tf_op jit(solution)/shard_map/all_gather | solution.py:114
  274.6 11.3 %collective-permute-start.15 = (bf16[4,4,48,1280]{3,2,1,0:T(8,128)(2,1)S(1)}, bf16[4,4,48,1280]{3,2,1,0:T(8,128)(2,1)S(1)}, u32[]{:S(2)}, u32[]{:S(2)}) collective-permute-start(bf16[4,4,48,1280]{3,2,1,0:T(8,128)(2,1)S(1)} %bitcast.264), channel_id=1, source_target_pairs={{0,4},{4,0},{8,12},{12,8},{16,20},{20,16},{24,28},{28,24},{1,5},{5... | collective-permute-start | bytes 5898248 | tf_op jit(solution)/shard_map/ppermute | solution.py:88
  277.1 7.1 %collective-permute-start.22 = (bf16[4,4,48,384]{3,2,0,1:T(8,128)(2,1)S(1)}, bf16[4,4,48,384]{3,2,0,1:T(8,128)(2,1)S(1)}, u32[]{:S(2)}, u32[]{:S(2)}) collective-permute-start(bf16[4,4,48,384]{3,2,0,1:T(8,128)(2,1)S(1)} %copy.138), channel_id=1, source_target_pairs={{0,4},{4,0},{8,12},{12,8},{16,20},{20,16},{24,28},{28,24},{1,5},{5... | collective-permute-start | bytes 1769480 | tf_op jit(solution)/shard_map/ppermute | solution.py:88
  284.4 5.2 %collective-permute-start.23 = (bf16[4,48,384]{2,1,0:T(8,128)(2,1)S(1)}, bf16[4,48,384]{2,1,0:T(8,128)(2,1)S(1)}, u32[]{:S(2)}, u32[]{:S(2)}) collective-permute-start(bf16[4,48,384]{2,1,0:T(8,128)(2,1)S(1)} %fusion.77), channel_id=1, source_target_pairs={{0,8},{4,20},{8,0},{12,28},{16,24},{20,4},{24,16},{28,12},{1,9},{5... | collective-permute-start | bytes 442376 | tf_op jit(solution)/shard_map/ppermute | solution.py:94
  286.4 10.5 %collective-permute-start.16 = (bf16[4,48,1280]{2,1,0:T(8,128)(2,1)S(1)}, bf16[4,48,1280]{2,1,0:T(8,128)(2,1)S(1)}, u32[]{:S(2)}, u32[]{:S(2)}) collective-permute-start(bf16[4,48,1280]{2,1,0:T(8,128)(2,1)S(1)} %fusion.60), channel_id=1, source_target_pairs={{0,8},{4,20},{8,0},{12,28},{16,24},{20,4},{24,16},{28,12},{1,9},{5... | collective-permute-start | bytes 1474568 | tf_op jit(solution)/shard_map/ppermute | solution.py:94
  288.7 34.4 %collective-permute-start.29 = (bf16[4,4,48,1536]{3,2,1,0:T(8,128)(2,1)}, bf16[4,4,48,1536]{3,2,1,0:T(8,128)(2,1)}, u32[]{:S(2)}, u32[]{:S(2)}) collective-permute-start(bf16[4,4,48,1536]{3,2,1,0:T(8,128)(2,1)} %bitcast.79), channel_id=1, source_target_pairs={{0,4},{4,0},{8,12},{12,8},{16,20},{20,16},{24,28},{28,24},{1,5},{5... | collective-permute-start | bytes 7077896 | tf_op jit(solution)/shard_map/ppermute | solution.py:88
  289.6 12.0 %collective-permute-start.24 = (bf16[4,48,384]{2,1,0:T(8,128)(2,1)S(1)}, bf16[4,48,384]{2,1,0:T(8,128)(2,1)S(1)}, u32[]{:S(2)}, u32[]{:S(2)}) collective-permute-start(bf16[4,48,384]{2,1,0:T(8,128)(2,1)S(1)} %get-tuple-element.127), channel_id=1, source_target_pairs={{0,8},{4,12},{8,0},{12,4},{16,24},{20,28},{24,16},{28,20},{1,9},{5... | collective-permute-start | bytes 442376 | tf_op jit(solution)/shard_map/ppermute | solution.py:101
  291.2 10.5 %collective-permute-start.25 = (bf16[4,48,384]{2,1,0:T(8,128)(2,1)S(1)}, bf16[4,48,384]{2,1,0:T(8,128)(2,1)S(1)}, u32[]{:S(2)}, u32[]{:S(2)}) collective-permute-start(bf16[4,48,384]{2,1,0:T(8,128)(2,1)S(1)} %get-tuple-element.128), channel_id=1, source_target_pairs={{0,16},{4,20},{8,24},{12,28},{16,0},{20,4},{24,8},{28,12},{1,17},{... | collective-permute-start | bytes 442376 | tf_op jit(solution)/shard_map/ppermute | solution.py:102
  297.1 11.9 %collective-permute-start.17 = (bf16[4,48,1280]{2,1,0:T(8,128)(2,1)S(1)}, bf16[4,48,1280]{2,1,0:T(8,128)(2,1)S(1)}, u32[]{:S(2)}, u32[]{:S(2)}) collective-permute-start(bf16[4,48,1280]{2,1,0:T(8,128)(2,1)S(1)} %get-tuple-element.115), channel_id=1, source_target_pairs={{0,8},{4,12},{8,0},{12,4},{16,24},{20,28},{24,16},{28,20},{1,9},{5... | collective-permute-start | bytes 1474568 | tf_op jit(solution)/shard_map/ppermute | solution.py:101
  298.2 13.2 %collective-permute-start.18 = (bf16[4,48,1280]{2,1,0:T(8,128)(2,1)S(1)}, bf16[4,48,1280]{2,1,0:T(8,128)(2,1)S(1)}, u32[]{:S(2)}, u32[]{:S(2)}) collective-permute-start(bf16[4,48,1280]{2,1,0:T(8,128)(2,1)S(1)} %get-tuple-element.116), channel_id=1, source_target_pairs={{0,16},{4,20},{8,24},{12,28},{16,0},{20,4},{24,8},{28,12},{1,17},{... | collective-permute-start | bytes 1474568 | tf_op jit(solution)/shard_map/ppermute | solution.py:102
  301.7 9.9 %collective-permute-start.26 = (bf16[48,384]{1,0:T(8,128)(2,1)S(1)}, bf16[48,384]{1,0:T(8,128)(2,1)S(1)}, u32[]{:S(2)}, u32[]{:S(2)}) collective-permute-start(bf16[48,384]{1,0:T(8,128)(2,1)S(1)} %get-tuple-element.140), channel_id=1, source_target_pairs={{0,1},{1,2},{2,3},{3,0},{4,5},{5,6},{6,7},{7,4},{8,9},{9,10},{10,1... | collective-permute-start | bytes 110600 | tf_op jit(solution)/shard_map/ppermute | solution.py:107
  303.2 10.4 %collective-permute-start.28 = (bf16[48,384]{1,0:T(8,128)(2,1)S(1)}, bf16[48,384]{1,0:T(8,128)(2,1)S(1)}, u32[]{:S(2)}, u32[]{:S(2)}) collective-permute-start(bf16[48,384]{1,0:T(8,128)(2,1)S(1)} %get-tuple-element.141), channel_id=1, source_target_pairs={{0,3},{1,0},{2,1},{3,2},{4,7},{5,4},{6,5},{7,6},{8,11},{9,8},{10,9... | collective-permute-start | bytes 110600 | tf_op jit(solution)/shard_map/ppermute | solution.py:107
  308.9 6.2 %collective-permute-start.27 = (bf16[48,384]{1,0:T(8,128)(2,1)S(1)}, bf16[48,384]{1,0:T(8,128)(2,1)S(1)}, u32[]{:S(2)}, u32[]{:S(2)}) collective-permute-start(bf16[48,384]{1,0:T(8,128)(2,1)S(1)} %get-tuple-element.142), channel_id=1, source_target_pairs={{0,2},{1,3},{2,0},{3,1},{4,6},{5,7},{6,4},{7,5},{8,10},{9,11},{10,... | collective-permute-start | bytes 110600 | tf_op jit(solution)/shard_map/ppermute | solution.py:107
  311.6 9.1 %collective-permute-start.19 = (bf16[48,1280]{1,0:T(8,128)(2,1)S(1)}, bf16[48,1280]{1,0:T(8,128)(2,1)S(1)}, u32[]{:S(2)}, u32[]{:S(2)}) collective-permute-start(bf16[48,1280]{1,0:T(8,128)(2,1)S(1)} %get-tuple-element.137), channel_id=1, source_target_pairs={{0,1},{1,2},{2,3},{3,0},{4,5},{5,6},{6,7},{7,4},{8,9},{9,10},{10,1... | collective-permute-start | bytes 368648 | tf_op jit(solution)/shard_map/ppermute | solution.py:107
  311.7 10.2 %collective-permute-start.21 = (bf16[48,1280]{1,0:T(8,128)(2,1)S(1)}, bf16[48,1280]{1,0:T(8,128)(2,1)S(1)}, u32[]{:S(2)}, u32[]{:S(2)}) collective-permute-start(bf16[48,1280]{1,0:T(8,128)(2,1)S(1)} %get-tuple-element.138), channel_id=1, source_target_pairs={{0,3},{1,0},{2,1},{3,2},{4,7},{5,4},{6,5},{7,6},{8,11},{9,8},{10,9... | collective-permute-start | bytes 368648 | tf_op jit(solution)/shard_map/ppermute | solution.py:107
  313.7 8.3 %collective-permute-start.20 = (bf16[48,1280]{1,0:T(8,128)(2,1)S(1)}, bf16[48,1280]{1,0:T(8,128)(2,1)S(1)}, u32[]{:S(2)}, u32[]{:S(2)}) collective-permute-start(bf16[48,1280]{1,0:T(8,128)(2,1)S(1)} %get-tuple-element.139), channel_id=1, source_target_pairs={{0,2},{1,3},{2,0},{3,1},{4,6},{5,7},{6,4},{7,5},{8,10},{9,11},{10,... | collective-permute-start | bytes 368648 | tf_op jit(solution)/shard_map/ppermute | solution.py:107
  322.8 123.5 %all-gather.25.cloned.1.call-start = ((), (), s32[]{:S(2)}) async-start(), calls=%async_computation.5 | async-start | bytes 2654208 | tf_op jit(solution)/shard_map/all_gather | solution.py:114
  327.0 15.4 %collective-permute-start.30 = (bf16[4,48,1536]{2,1,0:T(8,128)(2,1)S(1)}, bf16[4,48,1536]{2,1,0:T(8,128)(2,1)S(1)}, u32[]{:S(2)}, u32[]{:S(2)}) collective-permute-start(bf16[4,48,1536]{2,1,0:T(8,128)(2,1)S(1)} %fusion.58), channel_id=1, source_target_pairs={{0,8},{4,20},{8,0},{12,28},{16,24},{20,4},{24,16},{28,12},{1,9},{5... | collective-permute-start | bytes 1769480 | tf_op jit(solution)/shard_map/ppermute | solution.py:94
  342.7 17.1 %collective-permute-start.31 = (bf16[4,48,1536]{2,1,0:T(8,128)(2,1)S(1)}, bf16[4,48,1536]{2,1,0:T(8,128)(2,1)S(1)}, u32[]{:S(2)}, u32[]{:S(2)}) collective-permute-start(bf16[4,48,1536]{2,1,0:T(8,128)(2,1)S(1)} %get-tuple-element.107), channel_id=1, source_target_pairs={{0,8},{4,12},{8,0},{12,4},{16,24},{20,28},{24,16},{28,20},{1,9},{5... | collective-permute-start | bytes 1769480 | tf_op jit(solution)/shard_map/ppermute | solution.py:101
  344.2 15.9 %collective-permute-start.32 = (bf16[4,48,1536]{2,1,0:T(8,128)(2,1)S(1)}, bf16[4,48,1536]{2,1,0:T(8,128)(2,1)S(1)}, u32[]{:S(2)}, u32[]{:S(2)}) collective-permute-start(bf16[4,48,1536]{2,1,0:T(8,128)(2,1)S(1)} %get-tuple-element.108), channel_id=1, source_target_pairs={{0,16},{4,20},{8,24},{12,28},{16,0},{20,4},{24,8},{28,12},{1,17},{... | collective-permute-start | bytes 1769480 | tf_op jit(solution)/shard_map/ppermute | solution.py:102
  350.5 27.5 %collective-permute-start.36 = (bf16[4,4,192,384]{3,2,1,0:T(8,128)(2,1)}, bf16[4,4,192,384]{3,2,1,0:T(8,128)(2,1)}, u32[]{:S(2)}, u32[]{:S(2)}) collective-permute-start(bf16[4,4,192,384]{3,2,1,0:T(8,128)(2,1)} %bitcast.92), channel_id=1, source_target_pairs={{0,4},{4,0},{8,12},{12,8},{16,20},{20,16},{24,28},{28,24},{1,5},{5... | collective-permute-start | bytes 7077896 | tf_op jit(solution)/shard_map/ppermute | solution.py:88
  360.4 8.9 %collective-permute-start.33 = (bf16[48,1536]{1,0:T(8,128)(2,1)S(1)}, bf16[48,1536]{1,0:T(8,128)(2,1)S(1)}, u32[]{:S(2)}, u32[]{:S(2)}) collective-permute-start(bf16[48,1536]{1,0:T(8,128)(2,1)S(1)} %get-tuple-element.132), channel_id=1, source_target_pairs={{0,1},{1,2},{2,3},{3,0},{4,5},{5,6},{6,7},{7,4},{8,9},{9,10},{10,1... | collective-permute-start | bytes 442376 | tf_op jit(solution)/shard_map/ppermute | solution.py:107
  361.9 10.1 %collective-permute-start.35 = (bf16[48,1536]{1,0:T(8,128)(2,1)S(1)}, bf16[48,1536]{1,0:T(8,128)(2,1)S(1)}, u32[]{:S(2)}, u32[]{:S(2)}) collective-permute-start(bf16[48,1536]{1,0:T(8,128)(2,1)S(1)} %get-tuple-element.133), channel_id=1, source_target_pairs={{0,3},{1,0},{2,1},{3,2},{4,7},{5,4},{6,5},{7,6},{8,11},{9,8},{10,9... | collective-permute-start | bytes 442376 | tf_op jit(solution)/shard_map/ppermute | solution.py:107
  364.6 9.8 %collective-permute-start.34 = (bf16[48,1536]{1,0:T(8,128)(2,1)S(1)}, bf16[48,1536]{1,0:T(8,128)(2,1)S(1)}, u32[]{:S(2)}, u32[]{:S(2)}) collective-permute-start(bf16[48,1536]{1,0:T(8,128)(2,1)S(1)} %get-tuple-element.134), channel_id=1, source_target_pairs={{0,2},{1,3},{2,0},{3,1},{4,6},{5,7},{6,4},{7,5},{8,10},{9,11},{10,... | collective-permute-start | bytes 442376 | tf_op jit(solution)/shard_map/ppermute | solution.py:107
  375.3 84.1 %all-gather.27.cloned.1.call-start = ((), (), s32[]{:S(2)}) async-start(), calls=%async_computation.6 | async-start | bytes 2654208 | tf_op jit(solution)/shard_map/all_gather | solution.py:114
  380.3 16.6 %collective-permute-start.37 = (bf16[4,192,384]{2,1,0:T(8,128)(2,1)S(1)}, bf16[4,192,384]{2,1,0:T(8,128)(2,1)S(1)}, u32[]{:S(2)}, u32[]{:S(2)}) collective-permute-start(bf16[4,192,384]{2,1,0:T(8,128)(2,1)S(1)} %fusion.59), channel_id=1, source_target_pairs={{0,8},{4,20},{8,0},{12,28},{16,24},{20,4},{24,16},{28,12},{1,9},{5... | collective-permute-start | bytes 1769480 | tf_op jit(solution)/shard_map/ppermute | solution.py:94
  397.3 15.1 %collective-permute-start.38 = (bf16[4,192,384]{2,1,0:T(8,128)(2,1)S(1)}, bf16[4,192,384]{2,1,0:T(8,128)(2,1)S(1)}, u32[]{:S(2)}, u32[]{:S(2)}) collective-permute-start(bf16[4,192,384]{2,1,0:T(8,128)(2,1)S(1)} %get-tuple-element.105), channel_id=1, source_target_pairs={{0,8},{4,12},{8,0},{12,4},{16,24},{20,28},{24,16},{28,20},{1,9},{5... | collective-permute-start | bytes 1769480 | tf_op jit(solution)/shard_map/ppermute | solution.py:101
  397.7 14.7 %collective-permute-start.39 = (bf16[4,192,384]{2,1,0:T(8,128)(2,1)S(1)}, bf16[4,192,384]{2,1,0:T(8,128)(2,1)S(1)}, u32[]{:S(2)}, u32[]{:S(2)}) collective-permute-start(bf16[4,192,384]{2,1,0:T(8,128)(2,1)S(1)} %get-tuple-element.106), channel_id=1, source_target_pairs={{0,16},{4,20},{8,24},{12,28},{16,0},{20,4},{24,8},{28,12},{1,17},{... | collective-permute-start | bytes 1769480 | tf_op jit(solution)/shard_map/ppermute | solution.py:102
  412.7 7.8 %collective-permute-start.40 = (bf16[192,384]{1,0:T(8,128)(2,1)S(1)}, bf16[192,384]{1,0:T(8,128)(2,1)S(1)}, u32[]{:S(2)}, u32[]{:S(2)}) collective-permute-start(bf16[192,384]{1,0:T(8,128)(2,1)S(1)} %get-tuple-element.129), channel_id=1, source_target_pairs={{0,1},{1,2},{2,3},{3,0},{4,5},{5,6},{6,7},{7,4},{8,9},{9,10},{10,1... | collective-permute-start | bytes 442376 | tf_op jit(solution)/shard_map/ppermute | solution.py:107
  415.1 10.4 %collective-permute-start.42 = (bf16[192,384]{1,0:T(8,128)(2,1)S(1)}, bf16[192,384]{1,0:T(8,128)(2,1)S(1)}, u32[]{:S(2)}, u32[]{:S(2)}) collective-permute-start(bf16[192,384]{1,0:T(8,128)(2,1)S(1)} %get-tuple-element.130), channel_id=1, source_target_pairs={{0,3},{1,0},{2,1},{3,2},{4,7},{5,4},{6,5},{7,6},{8,11},{9,8},{10,9... | collective-permute-start | bytes 442376 | tf_op jit(solution)/shard_map/ppermute | solution.py:107
  417.5 10.8 %collective-permute-start.41 = (bf16[192,384]{1,0:T(8,128)(2,1)S(1)}, bf16[192,384]{1,0:T(8,128)(2,1)S(1)}, u32[]{:S(2)}, u32[]{:S(2)}) collective-permute-start(bf16[192,384]{1,0:T(8,128)(2,1)S(1)} %get-tuple-element.131), channel_id=1, source_target_pairs={{0,2},{1,3},{2,0},{3,1},{4,6},{5,7},{6,4},{7,5},{8,10},{9,11},{10,... | collective-permute-start | bytes 442376 | tf_op jit(solution)/shard_map/ppermute | solution.py:107
  (65 other events, 611.7 us)
Sparse Core Ops, SparseCore 0:
  16.0 27.0 all-gather.16
  45.6 33.8 all-gather.14
  81.9 38.7 all-gather.20
  123.1 38.7 all-gather.18
  322.9 35.8 all-gather.22
  375.4 34.5 all-gather.24
  429.3 30.0 all-gather.26

commit v15 on v5

--- a/solution.py
+++ b/solution.py
@@ -5,6 +5,7 @@
 from jax import lax
 from jax.sharding import PartitionSpec as P
 
+
 HEADS = 12
 HEAD_DIM = 64
 PATCH_BIG = 576
@@ -34,16 +35,6 @@
 
 
 LANES = 128
-
-
-def _to_rows(v):
-    return v.reshape(-1, LANES)
-
-
-def _gain_rows(gains, pick):
-    flat = jnp.concatenate([pick(g).reshape(-1) for g in gains])
-    pad = (-flat.shape[0]) % LANES
-    return jnp.pad(flat, (0, pad)).reshape(-1, LANES)
 
 
 def _plane_gather(z):
@@ -73,13 +64,19 @@
     return _take(jnp.stack(slots), (f - jnp.arange(NF_FAST, dtype=jnp.int32)) % NF_FAST, 0)
 
 
-def _gather_full(z, rows, cols, out_rows):
-    x = lax.all_gather(z, "dp", axis=1, tiled=False)
-    x = x.reshape(NF_FAST, NDP_FAST // 2, 2, rows, cols).transpose(0, 1, 3, 2, 4)
-    return x.reshape(out_rows, 2 * cols)
-
-
-def fast_gather(mats, gains):
+def _gather_matrix_pp(m):
+    d = lax.axis_index("dp")
+    j, c = d // 2, d % 2
+    n_chips = NDP_FAST // 2
+    rows, cols = m.shape[0] // n_chips, m.shape[1] // 2
+    z = _z_gather(lax.dynamic_slice(m, (j * rows, c * cols), (rows, cols)))
+    x = _take(_plane_gather(z), jnp.arange(NDP_FAST, dtype=jnp.int32) ^ d, 0)
+    x = x.reshape(n_chips, 2, NF_FAST, rows, cols)
+    x = jnp.concatenate([x[:, 0], x[:, 1]], axis=-1).transpose(1, 0, 2, 3)
+    return x.reshape(NF_FAST * m.shape[0], m.shape[1])
+
+
+def _gather_group(mats, gains):
     d = lax.axis_index("dp")
     j, c = d // 2, d % 2
     n_chips = NDP_FAST // 2
@@ -99,7 +96,10 @@
     for m, (rows, cols) in zip(mats, shapes):
         width = rows * cols // height
         part = z[:, :, offset : offset + width].reshape(NF_FAST, rows, cols)
-        out.append(_gather_full(part, rows, cols, NF_FAST * m.shape[0]))
+        x = lax.all_gather(part, "dp", axis=1, tiled=False)
+        x = x.reshape(NF_FAST, n_chips, 2, rows, cols)
+        x = jnp.concatenate([x[:, :, 0], x[:, :, 1]], axis=-1)
+        out.append(x.reshape(NF_FAST * m.shape[0], m.shape[1]))
         offset += width
     g = z[:, :, offset:].reshape(NF_FAST, -1)[:, : flat.shape[0]]
     g = g.reshape(NF_FAST, stacked.shape[0], stacked.shape[1]).transpose(1, 0, 2)
@@ -109,6 +109,10 @@
         out.append(g[row : row + gain.shape[0]])
         row += gain.shape[0]
     return out
+
+
+def fast_gather(mats, gains):
+    return [_gather_matrix_pp(mats[0])] + _gather_group(mats[1:], gains)
 
 
 def _reduce_matrix(g):
@@ -145,7 +149,8 @@
             part.astype(jnp.bfloat16), "fsdp", [(i, (i + k) % NF_FAST) for i in range(NF_FAST)]
         ).astype(jnp.float32)
     x = lax.all_gather(total, "dp", axis=0, tiled=False)
-    x = x.reshape(n_chips, 2, rows, cols).transpose(0, 2, 1, 3)
+    x = x.reshape(n_chips, 2, rows, cols)
+    x = jnp.concatenate([x[:, 0], x[:, 1]], axis=-1)
     return x.reshape(n_chips * rows, 2 * cols)
 
 
@@ -164,7 +169,17 @@
     return out
 
 
-def on_device(
+def map_blocks(fn, members):
+    if members[0].shape[0] == 1:
+        return jax.tree.map(lambda v: v[None], fn(tuple(m[0] for m in members)))
+    return lax.map(fn, members)
+
+
+def on_device(fast, *args):
+    return layer(fast, *args)
+
+
+def layer(
     fast, tokens, image_lengths, w_qkv, w_out, w_up, w_down, ln_gain, ln_bias, qk_gain, cotangent
 ):
     if fast:
@@ -270,7 +285,7 @@
         )
         return (grad_q, grad_k, grad_v)
 
-    grad_qn, grad_kn, grad_vn = lax.map(
+    grad_qn, grad_kn, grad_vn = map_blocks(
         attend_back, (q_low, k_low, v_low, s_blocks, log_total, grad_mixed)
     )
     grad_q, grad_k, gain_q, gain_k = norms_back(

time: 547 us -> 493 us (0.901)
  the two profiles are of different devices: /device:TPU:8 before, /device:TPU:0 now
where the time goes in v15:
time: 493 us; the launch traced here: 485 us
  waiting for transfers between devices  120 us (24%)
  matrix products  113 us (23%)
  local copies, waits for them, and re-layouts  94.6 us (19%)
  other arithmetic  75.8 us (15%)
  starting transfers between devices  55.6 us (11%)
  between operations  15.7 us (3%)
  blocking collectives  9.94 us (2%)
    unnamed x148, local copies, waits for them, and re-layouts  34.2 us
    ppermute x4, waiting for transfers between devices, _reduce_matrix(): lax.ppermute(to_x.astype(jnp.bfloat16), 'dp', [(i, i ^ 2) for i in range(...  31.2 us
    ppermute x12, waiting for transfers between devices, _reduce_matrix(): lax.ppermute(part.astype(jnp.bfloat16), 'fsdp', [(i, (i + k) % NF_FAST) f...  27.1 us
    ppermute x6, waiting for transfers between devices, _z_gather(): lax.ppermute(piece, 'fsdp', [(i, (i + k) % NF_FAST) for i in range(NF_FAS...  22.7 us
    dot_general x1, matrix products, layer(): up_pre = jnp.dot(second_low, full_up, preferred_element_type=jnp.float32)  22 us
    ppermute x6, starting transfers between devices, _z_gather(): lax.ppermute(piece, 'fsdp', [(i, (i + k) % NF_FAST) for i in range(NF_FAS...  20.3 us
    ppermute x4, waiting for transfers between devices, _reduce_matrix(): lax.ppermute(of_chip(j ^ 3).astype(jnp.bfloat16), 'dp', [(i, i ^ 2) if i...  19.3 us
    ppermute x12, starting transfers between devices, _reduce_matrix(): lax.ppermute(part.astype(jnp.bfloat16), 'fsdp', [(i, (i + k) % NF_FAST) f...  18.2 us
  transfers between devices with their start and end apart: 44, of which 26 were waited for; matrix products, arithmetic and copies ran while one was open for 29% of the time, Pallas kernels for 0%

profile of v15, /device:TPU:0, one launch (start us, length us, event | category | flops | bytes accessed | tf_op | source)
XLA Modules:
  0.0 485.2 jit_solution(11052043787324474855)
XLA Ops:
  10.9 4.1 collective-permute-start.1
  18.9 19.9 %collective-permute-done.1 = bf16[48,3584]{1,0:T(8,128)(2,1)S(1)} collective-permute-done((bf16[48,3584]{1,0:T(8,128)(2,1)S(1)}, bf16[48,3584]{1,0:T(8,128)(2,1)S(1)}, u32[]{:S(2)}, u32[]{:S(2)}) %collective-permute-start.1) | collective-permute-done | bytes 344096 | tf_op jit(solution)/shard_map/ppermute | solution.py:61
  46.5 8.5 %collective-permute-start.4 = (bf16[48,1152]{1,0:T(8,128)(2,1)S(1)}, bf16[48,1152]{1,0:T(8,128)(2,1)S(1)}, u32[]{:S(2)}, u32[]{:S(2)}) collective-permute-start(bf16[48,1152]{1,0:T(8,128)(2,1)S(1)} %dynamic_slice.153), channel_id=1, source_target_pairs={{0,2},{1,3},{2,0},{3,1},{4,6},{5,7},{6,4},{7,5},{8,10},{9,11},{10,... | collective-permute-start | bytes 331784 | tf_op jit(solution)/shard_map/ppermute | solution.py:61
  55.0 3.8 collective-permute-start.5
  69.6 10.1 %collective-permute-done.6 = bf16[4,48,1152]{2,1,0:T(8,128)(2,1)S(1)} collective-permute-done((bf16[4,48,1152]{2,1,0:T(8,128)(2,1)}, bf16[4,48,1152]{2,1,0:T(8,128)(2,1)S(1)}, u32[]{:S(2)}, u32[]{:S(2)}) %collective-permute-start.6) | collective-permute-done | bytes 442400 | tf_op jit(solution)/shard_map/ppermute | solution.py:43
  83.2 6.2 %collective-permute-done.8 = bf16[4,48,1152]{2,1,0:T(8,128)(2,1)S(1)} collective-permute-done((bf16[4,48,1152]{2,1,0:T(8,128)(2,1)S(1)}, bf16[4,48,1152]{2,1,0:T(8,128)(2,1)S(1)}, u32[]{:S(2)}, u32[]{:S(2)}) %collective-permute-start.8) | collective-permute-done | bytes 442400 | tf_op jit(solution)/shard_map/ppermute | solution.py:46
  109.0 3.3 gather_fusion.2
  120.7 3.4 fusion.120
  132.2 8.1 %fusion.130 = (f32[12,576]{1,0:T(8,128)S(1)}, f32[12,576,576]{1,2,0:T(8,128)}) fusion(f32[576,12,64]{0,2,1:T(8,128)S(1)} %bitcast.245, f32[12,64]{1,0:T(8,128)S(1)} %mul.358, f32[576,12]{0,1:T(8,128)S(1)} %fusion.94, f32[576,12]{0,1:T(8,128)S(1)} %broadcast_multiply_fusion, f32[576,12,64]{0,2,1:T(8,128)S(1)} %bitcast.237, f32[12,64]{1,0:T(8,128)S(1)} %copy-done.46, ...), kind=kOutput, calls=%fused_computation.290 | convolution fusion | flops 525083904 | bytes 19940352 | tf_op jit(solution)/shard_map/while/body/eval_jaxpr/qhd,khd->hqk/dot_general | solution.py:225
  140.3 9.3 %fusion.3 = f32[12,576]{1,0:T(8,128)S(1)} fusion(f32[12,576,576]{1,2,0:T(8,128)} %get-tuple-element.154, f32[12,576]{1,0:T(8,128)S(1)} %get-tuple-element.153), kind=kLoop, calls=%fused_computation.12 | loop fusion | flops 7955712 | bytes 15980544 | tf_op jit(solution)/shard_map/while/body/eval_jaxpr/reduce_sum | solution.py:235
  149.6 9.9 %fusion.35 = bf16[12,64,576]{2,1,0:T(8,128)(2,1)S(1)} fusion(bf16[576,12,64]{0,2,1:T(8,128)(2,1)} %bitcast.267, f32[12,576,576]{1,2,0:T(8,128)} %get-tuple-element.154, f32[12,576]{1,0:T(8,128)S(1)} %fusion.3, f32[12,576]{1,0:T(8,128)S(1)} %get-tuple-element.153), kind=kOutput, calls=%fused_computation.105 | convolution fusion | flops 521994240 | bytes 17750016 | tf_op jit(solution)/shard_map/while/body/eval_jaxpr/hqk,khd->qhd/dot_general | solution.py:237
  162.1 5.1 %fusion.121 = (bf16[4,4,1,192,384]{4,3,2,1,0:T(8,128)(2,1)}, bf16[4,4,1,192,384]{4,3,2,1,0:T(8,128)(2,1)}) fusion(bf16[4,4,2,192,384]{4,3,2,1,0:T(8,128)(2,1)} %bitcast.255), kind=kLoop, calls=%fused_computation.281 | loop fusion | bytes 9437184 | tf_op jit(solution)/shard_map/slice | solution.py:101
  167.3 3.0 fusion.122
  170.3 22.0 %multiply_convert_fusion = (bf16[576,3072]{1,0:T(8,128)(2,1)}, f32[576,3072]{1,0:T(8,128)}, f32[576,3072]{1,0:T(8,128)}) fusion(bf16[768,1536]{1,0:T(8,128)(2,1)S(1)} %bitcast.280, bf16[768,1536]{1,0:T(8,128)(2,1)S(1)} %bitcast.278, f32[576,768]{1,0:T(8,128)S(1)} %copy-done.9, f32[768]{0:T(1024)S(1)} %add.387, f32[768]{0:T(1024)S(1)} %mul.365, ...), kind=kOutput, calls=%fused_computation.22 | convolution fusion | flops 2844573696 | bytes 24193536 | tf_op jit(solution)/shard_map/dot_general | solution.py:247
  192.4 8.1 %add_convert_fusion = bf16[576,3072]{1,0:T(8,128)(2,1)S(1)} fusion(f32[576,3072]{1,0:T(8,128)} %get-tuple-element.104, f32[576,3072]{1,0:T(8,128)} %get-tuple-element.157, bf16[3072,384]{1,0:T(8,128)(2,1)S(1)} %bitcast.277, bf16[3072,384]{1,0:T(8,128)(2,1)S(1)} %bitcast.275, bf16[576,768]{1,0:T(8,128)(2,1)S(1)} %copy-done.27, f32[576]{0:T(1024)S(1)} %copy-done.52), kind=kOutput, calls=%fused_computation.21 | convolution fusion | flops 2753445888 | bytes 23300352 | tf_op jit(solution)/shard_map/dot_general | solution.py:256
  200.5 3.3 multiply_reduce_fusion.2
  211.0 7.6 %convolution_convert_fusion = bf16[12,576,576]{1,2,0:T(8,128)(2,1)} fusion(bf16[576,12,64]{0,2,1:T(8,128)(2,1)} %bitcast.253, bf16[576,12,64]{0,2,1:T(8,128)(2,1)} %bitcast.268), kind=kOutput, calls=%fused_computation.36 | convolution fusion | flops 513589248 | bytes 9732096 | tf_op jit(solution)/shard_map/qhd,khd->hqk/dot_general | solution.py:276
  218.6 9.9 %fusion.36 = bf16[12,64,576]{2,1,0:T(8,128)(2,1)} fusion(bf16[576,12,64]{0,2,1:T(8,128)(2,1)S(1)} %bitcast.254, f32[12,576,576]{1,2,0:T(8,128)} %get-tuple-element.154, f32[12,576]{1,0:T(8,128)S(1)} %log_add_fusion), kind=kOutput, calls=%fused_computation.106 | convolution fusion | flops 518012928 | bytes 17722368 | tf_op jit(solution)/shard_map/hqk,qhd->khd/dot_general | solution.py:275
  228.5 12.8 %fusion = f32[12,576]{1,0:T(8,128)S(1)} fusion(bf16[12,576,576]{1,2,0:T(8,128)(2,1)} %convolution_convert_fusion, f32[12,576,576]{1,2,0:T(8,128)} %get-tuple-element.154, f32[12,576]{1,0:T(8,128)S(1)} %log_add_fusion), kind=kLoop, calls=%fused_computation.5 | loop fusion | flops 15918336 | bytes 23943168 | tf_op jit(solution)/shard_map/reduce_sum | solution.py:278
  242.1 6.3 %fusion.2 = bf16[12,576,576]{1,2,0:T(8,128)(2,1)} fusion(bf16[12,576,576]{1,2,0:T(8,128)(2,1)S(1)} %copy-done.3, f32[12,576,576]{1,2,0:T(8,128)S(1)} %bitcast.234, f32[12,576]{1,0:T(8,128)S(1)} %fusion, f32[12,576]{1,0:T(8,128)S(1)} %log_add_fusion), kind=kLoop, calls=%fused_computation.7 | loop fusion | flops 19906560 | bytes 31905792 | tf_op jit(solution)/shard_map/convert_element_type | solution.py:279
  248.5 8.2 %fusion.27 = (f32[576,12]{0,1:T(8,128)S(1)}, f32[12,64,576]{2,1,0:T(8,128)}) fusion(f32[576,12,64]{0,2,1:T(8,128)} %bitcast.244, f32[12,64]{1,0:T(8,128)S(1)} %copy-done.44, f32[576,12]{0,1:T(8,128)S(1)} %broadcast_multiply_fusion, bf16[12,576,576]{1,2,0:T(8,128)(2,1)} %fusion.2, f32[576,12,64]{0,2,1:T(8,128)S(1)} %bitcast.238, ...), kind=kOutput, calls=%fused_computation.72 | convolution fusion | flops 513139968 | bytes 13387776 | tf_op jit(solution)/shard_map/hqk,qhd->khd/dot_general | solution.py:284
  264.5 2.8 fusion.117
  267.3 6.4 %fusion.39 = f32[768,2304]{1,0:T(8,128)} fusion(bf16[576,768]{0,1:T(8,128)(2,1)S(1)} %bitcast.293, bf16[576,768]{0,1:T(8,128)(2,1)S(1)} %bitcast.289, bf16[576,768]{0,1:T(8,128)(2,1)S(1)} %bitcast.291, bf16[576,768]{1,0:T(8,128)(2,1)S(1)} %copy-done.14, f32[768]{0:T(1024)S(1)} %copy-done.58, f32[768]{0:T(1024)S(1)} %copy-done.56, f32[576]{0:T(1024)S(1)} %copy-done.54, ...), kind=kOutput, calls=%fused_computation.111 | convolution fusion | flops 2049048576 | bytes 10627584 | tf_op jit(solution)/shard_map/dot_general | solution.py:302
  275.0 4.2 select_maximum_fusion
  279.2 3.1 copy-done.5
  284.6 6.1 %fusion.116 = f32[768,3072]{1,0:T(8,128)S(1)} fusion(bf16[576,3072]{1,0:T(8,128)(2,1)} %copy-done.24, f32[576,768]{1,0:T(8,128)S(1)} %copy-done.10, f32[768]{0:T(1024)S(1)} %add.387, f32[768]{0:T(1024)S(1)} %mul.365, f32[576]{0:T(1024)S(1)} %fusion.97, f32[576]{0:T(1024)S(1)} %broadcast_multiply_fusion.4), kind=kOutput, calls=%fused_computation.277 | convolution fusion | flops 2720120832 | bytes 14756352 | tf_op jit(solution)/shard_map/dot_general | solution.py:259
  290.7 3.7 copy-done.4
  304.0 2.8 constant_dynamic-slice_fusion.1
  306.8 5.4 %collective-permute-done.11 = bf16[4,48,1280]{2,1,0:T(8,128)(2,1)} collective-permute-done((bf16[4,48,1280]{2,1,0:T(8,128)(2,1)S(1)}, bf16[4,48,1280]{2,1,0:T(8,128)(2,1)}, u32[]{:S(2)}, u32[]{:S(2)}) %collective-permute-start.11) | collective-permute-done | bytes 491552 | tf_op jit(solution)/shard_map/ppermute | solution.py:135
  318.2 7.6 %collective-permute-done.12 = bf16[4,48,1280]{2,1,0:T(8,128)(2,1)S(1)} collective-permute-done((bf16[4,48,1280]{2,1,0:T(8,128)(2,1)S(1)}, bf16[4,48,1280]{2,1,0:T(8,128)(2,1)S(1)}, u32[]{:S(2)}, u32[]{:S(2)}) %collective-permute-start.12) | collective-permute-done | bytes 491552 | tf_op jit(solution)/shard_map/ppermute | solution.py:142
  326.4 4.8 collective-permute-start.14
  336.7 3.9 collective-permute-done.15
  346.5 5.2 %fusion.60 = f32[3072,768]{1,0:T(8,128)S(1)} fusion(bf16[576,3072]{1,0:T(8,128)(2,1)S(1)} %copy-done.62, bf16[576,768]{1,0:T(8,128)(2,1)} %param.19, f32[576]{0:T(1024)S(1)} %copy-done.52), kind=kOutput, calls=%fused_computation.151 | convolution fusion | flops 2719236096 | bytes 13863168 | tf_op jit(solution)/shard_map/dot_general | solution.py:255
  351.6 3.7 copy-done.20
  356.9 3.4 collective-permute-done.26
  362.6 3.8 collective-permute-start.30
  366.4 3.5 collective-permute-done.28
  369.9 6.1 %collective-permute-done.29 = bf16[48,1536]{1,0:T(8,128)(2,1)S(1)} collective-permute-done((bf16[48,1536]{1,0:T(8,128)(2,1)S(1)}, bf16[48,1536]{1,0:T(8,128)(2,1)S(1)}, u32[]{:S(2)}, u32[]{:S(2)}) %collective-permute-start.29) | collective-permute-done | bytes 147488 | tf_op jit(solution)/shard_map/ppermute | solution.py:148
  383.2 11.7 %collective-permute-done.32 = bf16[4,192,384]{2,1,0:T(8,128)(2,1)S(1)} collective-permute-done((bf16[4,192,384]{2,1,0:T(8,128)(2,1)S(1)}, bf16[4,192,384]{2,1,0:T(8,128)(2,1)S(1)}, u32[]{:S(2)}, u32[]{:S(2)}) %collective-permute-start.32) | collective-permute-done | bytes 589856 | tf_op jit(solution)/shard_map/ppermute | solution.py:135
  399.8 15.0 %collective-permute-done.33 = bf16[4,192,384]{2,1,0:T(8,128)(2,1)S(1)} collective-permute-done((bf16[4,192,384]{2,1,0:T(8,128)(2,1)S(1)}, bf16[4,192,384]{2,1,0:T(8,128)(2,1)S(1)}, u32[]{:S(2)}, u32[]{:S(2)}) %collective-permute-start.33) | collective-permute-done | bytes 589856 | tf_op jit(solution)/shard_map/ppermute | solution.py:142
  416.5 3.8 collective-permute-start.37
  421.9 3.2 collective-permute-done.35
  425.1 4.7 collective-permute-done.36
  430.7 7.4 %multiply_convert_fusion.3 = bf16[576,768]{1,0:T(8,128)(2,1)} fusion(f32[576,768]{1,0:T(8,128)S(1)} %copy-done.10, bf16[576,3072]{1,0:T(8,128)(2,1)} %get-tuple-element.103, bf16[3072,384]{1,0:T(8,128)(2,1)} %bitcast.276, bf16[3072,384]{1,0:T(8,128)(2,1)} %bitcast.274, f32[576]{0:T(1024)S(1)} %copy-done.52), kind=kOutput, calls=%fused_computation.98 | convolution fusion | flops 2728673280 | bytes 10914048 | tf_op jit(solution)/shard_map/dot_general | solution.py:250
  440.8 5.2 %collective-permute-done.19 = bf16[4,48,384]{2,1,0:T(8,128)(2,1)S(1)} collective-permute-done((bf16[4,48,384]{2,1,0:T(8,128)(2,1)S(1)}, bf16[4,48,384]{2,1,0:T(8,128)(2,1)S(1)}, u32[]{:S(2)}, u32[]{:S(2)}) %collective-permute-start.19) | collective-permute-done | bytes 147488 | tf_op jit(solution)/shard_map/ppermute | solution.py:142
  446.3 4.0 collective-permute-start.23
  452.2 3.0 collective-permute-done.22
  455.3 9.9 %all-gather.3 = f32[384,384]{1,0:T(8,128)S(1)} all-gather(f32[48,384]{1,0:T(8,128)S(1)} %fusion.89), channel_id=5, replica_groups=mesh['dp'=8,'fsdp'=4] {'dp'}, dimensions={0}, use_global_device_ids=true | all-gather | bytes 663552 | tf_op jit(solution)/shard_map/all_gather | solution.py:151
  (355 shorter events, 152.2 us)
Async XLA Ops:
  7.2 89.7 %all-gather.15.cloned.1.call-start = ((), (), s32[]{:S(2)}) async-start(), calls=%async_computation.1 | async-start | bytes 1327104 | tf_op jit(solution)/shard_map/all_gather | solution.py:99
  10.9 27.8 %collective-permute-start.1 = (bf16[48,3584]{1,0:T(8,128)(2,1)S(1)}, bf16[48,3584]{1,0:T(8,128)(2,1)S(1)}, u32[]{:S(2)}, u32[]{:S(2)}) collective-permute-start(bf16[48,3584]{1,0:T(8,128)(2,1)S(1)} %get-tuple-element.143), channel_id=1, source_target_pairs={{0,2},{1,3},{2,0},{3,1},{4,6},{5,7},{6,4},{7,5},{8,10},{9,11},{10,... | collective-permute-start | bytes 1032200 | tf_op jit(solution)/shard_map/ppermute | solution.py:61
  15.0 23.7 %collective-permute-start = (bf16[48,3584]{1,0:T(8,128)(2,1)S(1)}, bf16[48,3584]{1,0:T(8,128)(2,1)S(1)}, u32[]{:S(2)}, u32[]{:S(2)}) collective-permute-start(bf16[48,3584]{1,0:T(8,128)(2,1)S(1)} %get-tuple-element.143), channel_id=1, source_target_pairs={{0,1},{1,2},{2,3},{3,0},{4,5},{5,6},{6,7},{7,4},{8,9},{9,10},{10,1... | collective-permute-start | bytes 1032200 | tf_op jit(solution)/shard_map/ppermute | solution.py:61
  16.6 22.8 %collective-permute-start.2 = (bf16[48,3584]{1,0:T(8,128)(2,1)S(1)}, bf16[48,3584]{1,0:T(8,128)(2,1)S(1)}, u32[]{:S(2)}, u32[]{:S(2)}) collective-permute-start(bf16[48,3584]{1,0:T(8,128)(2,1)S(1)} %get-tuple-element.143), channel_id=1, source_target_pairs={{0,3},{1,0},{2,1},{3,2},{4,7},{5,4},{6,5},{7,6},{8,11},{9,8},{10,9... | collective-permute-start | bytes 1032200 | tf_op jit(solution)/shard_map/ppermute | solution.py:61
  43.4 118.8 %all-gather.13.cloned.1.call-start = ((), (), s32[]{:S(2)}) async-start(), calls=%async_computation | async-start | bytes 5308416 | tf_op jit(solution)/shard_map/all_gather | solution.py:99
  45.5 121.7 %all-gather.17.cloned.1.call-start = ((), (), s32[]{:S(2)}) async-start(), calls=%async_computation.2 | async-start | bytes 5308416 | tf_op jit(solution)/shard_map/all_gather | solution.py:99
  46.5 16.8 %collective-permute-start.4 = (bf16[48,1152]{1,0:T(8,128)(2,1)S(1)}, bf16[48,1152]{1,0:T(8,128)(2,1)S(1)}, u32[]{:S(2)}, u32[]{:S(2)}) collective-permute-start(bf16[48,1152]{1,0:T(8,128)(2,1)S(1)} %dynamic_slice.153), channel_id=1, source_target_pairs={{0,2},{1,3},{2,0},{3,1},{4,6},{5,7},{6,4},{7,5},{8,10},{9,11},{10,... | collective-permute-start | bytes 331784 | tf_op jit(solution)/shard_map/ppermute | solution.py:61
  55.0 8.3 %collective-permute-start.3 = (bf16[48,1152]{1,0:T(8,128)(2,1)S(1)}, bf16[48,1152]{1,0:T(8,128)(2,1)S(1)}, u32[]{:S(2)}, u32[]{:S(2)}) collective-permute-start(bf16[48,1152]{1,0:T(8,128)(2,1)S(1)} %dynamic_slice.153), channel_id=1, source_target_pairs={{0,1},{1,2},{2,3},{3,0},{4,5},{5,6},{6,7},{7,4},{8,9},{9,10},{10,1... | collective-permute-start | bytes 331784 | tf_op jit(solution)/shard_map/ppermute | solution.py:61
  55.0 9.2 %collective-permute-start.5 = (bf16[48,1152]{1,0:T(8,128)(2,1)S(1)}, bf16[48,1152]{1,0:T(8,128)(2,1)S(1)}, u32[]{:S(2)}, u32[]{:S(2)}) collective-permute-start(bf16[48,1152]{1,0:T(8,128)(2,1)S(1)} %dynamic_slice.153), channel_id=1, source_target_pairs={{0,3},{1,0},{2,1},{3,2},{4,7},{5,4},{6,5},{7,6},{8,11},{9,8},{10,9... | collective-permute-start | bytes 331784 | tf_op jit(solution)/shard_map/ppermute | solution.py:61
  65.6 14.2 %collective-permute-start.6 = (bf16[4,48,1152]{2,1,0:T(8,128)(2,1)}, bf16[4,48,1152]{2,1,0:T(8,128)(2,1)S(1)}, u32[]{:S(2)}, u32[]{:S(2)}) collective-permute-start(bf16[4,48,1152]{2,1,0:T(8,128)(2,1)} %gather_fusion.1), channel_id=1, source_target_pairs={{0,8},{4,12},{8,0},{12,4},{16,24},{20,28},{24,16},{28,20},{1,9},{5... | collective-permute-start | bytes 1327112 | tf_op jit(solution)/shard_map/ppermute | solution.py:43
  67.1 13.9 %collective-permute-start.7 = (bf16[4,48,1152]{2,1,0:T(8,128)(2,1)}, bf16[4,48,1152]{2,1,0:T(8,128)(2,1)S(1)}, u32[]{:S(2)}, u32[]{:S(2)}) collective-permute-start(bf16[4,48,1152]{2,1,0:T(8,128)(2,1)} %gather_fusion.1), channel_id=1, source_target_pairs={{0,16},{4,20},{8,24},{12,28},{16,0},{20,4},{24,8},{28,12},{1,17},{... | collective-permute-start | bytes 1327112 | tf_op jit(solution)/shard_map/ppermute | solution.py:44
  81.0 8.4 %collective-permute-start.8 = (bf16[4,48,1152]{2,1,0:T(8,128)(2,1)S(1)}, bf16[4,48,1152]{2,1,0:T(8,128)(2,1)S(1)}, u32[]{:S(2)}, u32[]{:S(2)}) collective-permute-start(bf16[4,48,1152]{2,1,0:T(8,128)(2,1)S(1)} %broadcast_select_fusion), channel_id=1, source_target_pairs={{0,8},{4,20},{8,0},{12,28},{16,24},{20,4},{24,16},{28,12},{1,9},{5... | collective-permute-start | bytes 1327112 | tf_op jit(solution)/shard_map/ppermute | solution.py:46
  91.9 7.4 %collective-permute-start.9 = (bf16[4,4,48,1152]{3,2,1,0:T(8,128)(2,1)}, bf16[4,4,48,1152]{3,2,1,0:T(8,128)(2,1)}, u32[]{:S(2)}, u32[]{:S(2)}) collective-permute-start(bf16[4,4,48,1152]{3,2,1,0:T(8,128)(2,1)} %pad_maximum_fusion.12), channel_id=1, source_target_pairs={{0,4},{4,0},{8,12},{12,8},{16,20},{20,16},{24,28},{28,24},{1,5},{5... | collective-permute-start | bytes 5308424 | tf_op jit(solution)/shard_map/ppermute | solution.py:50
  95.6 370.5 %all-gather.19.cloned.1.call-start = ((), (), s32[]{:S(2)}) async-start(), calls=%async_computation.3 | async-start | bytes 2211840 | tf_op jit(solution)/shard_map/all_gather | solution.py:151
  170.3 22.1 %copy-start.27 = (bf16[576,768]{1,0:T(8,128)(2,1)S(1)}, bf16[576,768]{1,0:T(8,128)(2,1)}, u32[]{:S(2)}) copy-start(bf16[576,768]{1,0:T(8,128)(2,1)} %param.19) | copy-start | bytes 2654212
  218.6 22.7 %slice-start = ((s8[17694720]{0:T(1024)(128)(4,1)}), s8[4194304]{0:T(1024)(128)(4,1)S(1)}, s32[]{:S(2)}) async-start(s8[17694720]{0:T(1024)(128)(4,1)} %bitcast.233), calls=%async_computation.6 | async-start | bytes 8388608
  218.6 22.7 %slice-start.1 = ((s8[17694720]{0:T(1024)(128)(4,1)}), s8[4194304]{0:T(1024)(128)(4,1)S(1)}, s32[]{:S(2)}) async-start(s8[17694720]{0:T(1024)(128)(4,1)} %bitcast.233), calls=%async_computation.7 | async-start | bytes 8388608
  218.6 22.7 %slice-start.2 = ((s8[17694720]{0:T(1024)(128)(4,1)}), s8[917504]{0:T(1024)(128)(4,1)S(1)}, s32[]{:S(2)}) async-start(s8[17694720]{0:T(1024)(128)(4,1)} %bitcast.233), calls=%async_computation.8 | async-start | bytes 1835008
  283.8 15.3 %collective-permute-start.10 = (bf16[4,4,48,1280]{3,2,1,0:T(8,128)(2,1)}, bf16[4,4,48,1280]{3,2,1,0:T(8,128)(2,1)}, u32[]{:S(2)}, u32[]{:S(2)}) collective-permute-start(bf16[4,4,48,1280]{3,2,1,0:T(8,128)(2,1)} %bitcast.49), channel_id=1, source_target_pairs={{0,4},{4,0},{8,12},{12,8},{16,20},{20,16},{24,28},{28,24},{1,5},{5... | collective-permute-start | bytes 5898248 | tf_op jit(solution)/shard_map/ppermute | solution.py:129
  296.1 19.6 %collective-permute-start.24 = (bf16[4,4,48,1536]{3,2,1,0:T(8,128)(2,1)}, bf16[4,4,48,1536]{3,2,1,0:T(8,128)(2,1)}, u32[]{:S(2)}, u32[]{:S(2)}) collective-permute-start(bf16[4,4,48,1536]{3,2,1,0:T(8,128)(2,1)} %bitcast.76), channel_id=1, source_target_pairs={{0,4},{4,0},{8,12},{12,8},{16,20},{20,16},{24,28},{28,24},{1,5},{5... | collective-permute-start | bytes 7077896 | tf_op jit(solution)/shard_map/ppermute | solution.py:129
  303.2 9.0 %collective-permute-start.11 = (bf16[4,48,1280]{2,1,0:T(8,128)(2,1)S(1)}, bf16[4,48,1280]{2,1,0:T(8,128)(2,1)}, u32[]{:S(2)}, u32[]{:S(2)}) collective-permute-start(bf16[4,48,1280]{2,1,0:T(8,128)(2,1)S(1)} %fusion.59), channel_id=1, source_target_pairs={{0,8},{4,20},{8,0},{12,28},{16,24},{20,4},{24,16},{28,12},{1,9},{5... | collective-permute-start | bytes 1474568 | tf_op jit(solution)/shard_map/ppermute | solution.py:135
  313.5 12.3 %collective-permute-start.12 = (bf16[4,48,1280]{2,1,0:T(8,128)(2,1)S(1)}, bf16[4,48,1280]{2,1,0:T(8,128)(2,1)S(1)}, u32[]{:S(2)}, u32[]{:S(2)}) collective-permute-start(bf16[4,48,1280]{2,1,0:T(8,128)(2,1)S(1)} %get-tuple-element.115), channel_id=1, source_target_pairs={{0,8},{4,12},{8,0},{12,4},{16,24},{20,28},{24,16},{28,20},{1,9},{5... | collective-permute-start | bytes 1474568 | tf_op jit(solution)/shard_map/ppermute | solution.py:142
  314.2 12.0 %collective-permute-start.13 = (bf16[4,48,1280]{2,1,0:T(8,128)(2,1)S(1)}, bf16[4,48,1280]{2,1,0:T(8,128)(2,1)S(1)}, u32[]{:S(2)}, u32[]{:S(2)}) collective-permute-start(bf16[4,48,1280]{2,1,0:T(8,128)(2,1)S(1)} %get-tuple-element.116), channel_id=1, source_target_pairs={{0,16},{4,20},{8,24},{12,28},{16,0},{20,4},{24,8},{28,12},{1,17},{... | collective-permute-start | bytes 1474568 | tf_op jit(solution)/shard_map/ppermute | solution.py:143
  326.4 8.3 %collective-permute-start.14 = (bf16[48,1280]{1,0:T(8,128)(2,1)S(1)}, bf16[48,1280]{1,0:T(8,128)(2,1)S(1)}, u32[]{:S(2)}, u32[]{:S(2)}) collective-permute-start(bf16[48,1280]{1,0:T(8,128)(2,1)S(1)} %get-tuple-element.137), channel_id=1, source_target_pairs={{0,1},{1,2},{2,3},{3,0},{4,5},{5,6},{6,7},{7,4},{8,9},{9,10},{10,1... | collective-permute-start | bytes 368648 | tf_op jit(solution)/shard_map/ppermute | solution.py:148
  331.2 5.5 %collective-permute-start.16 = (bf16[48,1280]{1,0:T(8,128)(2,1)S(1)}, bf16[48,1280]{1,0:T(8,128)(2,1)S(1)}, u32[]{:S(2)}, u32[]{:S(2)}) collective-permute-start(bf16[48,1280]{1,0:T(8,128)(2,1)S(1)} %get-tuple-element.138), channel_id=1, source_target_pairs={{0,3},{1,0},{2,1},{3,2},{4,7},{5,4},{6,5},{7,6},{8,11},{9,8},{10,9... | collective-permute-start | bytes 368648 | tf_op jit(solution)/shard_map/ppermute | solution.py:148
  331.2 9.3 %collective-permute-start.15 = (bf16[48,1280]{1,0:T(8,128)(2,1)S(1)}, bf16[48,1280]{1,0:T(8,128)(2,1)S(1)}, u32[]{:S(2)}, u32[]{:S(2)}) collective-permute-start(bf16[48,1280]{1,0:T(8,128)(2,1)S(1)} %get-tuple-element.139), channel_id=1, source_target_pairs={{0,2},{1,3},{2,0},{3,1},{4,6},{5,7},{6,4},{7,5},{8,10},{9,11},{10,... | collective-permute-start | bytes 368648 | tf_op jit(solution)/shard_map/ppermute | solution.py:148
  333.7 10.1 %collective-permute-start.25 = (bf16[4,48,1536]{2,1,0:T(8,128)(2,1)}, bf16[4,48,1536]{2,1,0:T(8,128)(2,1)S(1)}, u32[]{:S(2)}, u32[]{:S(2)}) collective-permute-start(bf16[4,48,1536]{2,1,0:T(8,128)(2,1)} %fusion.57), channel_id=1, source_target_pairs={{0,8},{4,20},{8,0},{12,28},{16,24},{20,4},{24,16},{28,12},{1,9},{5... | collective-permute-start | bytes 1769480 | tf_op jit(solution)/shard_map/ppermute | solution.py:135
  341.3 129.9 %all-gather.21.cloned.1.call-start = ((), (), s32[]{:S(2)}) async-start(), calls=%async_computation.4 | async-start | bytes 2654208 | tf_op jit(solution)/shard_map/all_gather | solution.py:151
  345.7 14.7 %collective-permute-start.26 = (bf16[4,48,1536]{2,1,0:T(8,128)(2,1)S(1)}, bf16[4,48,1536]{2,1,0:T(8,128)(2,1)S(1)}, u32[]{:S(2)}, u32[]{:S(2)}) collective-permute-start(bf16[4,48,1536]{2,1,0:T(8,128)(2,1)S(1)} %get-tuple-element.107), channel_id=1, source_target_pairs={{0,8},{4,12},{8,0},{12,4},{16,24},{20,28},{24,16},{28,20},{1,9},{5... | collective-permute-start | bytes 1769480 | tf_op jit(solution)/shard_map/ppermute | solution.py:142
  346.1 14.7 %collective-permute-start.27 = (bf16[4,48,1536]{2,1,0:T(8,128)(2,1)S(1)}, bf16[4,48,1536]{2,1,0:T(8,128)(2,1)S(1)}, u32[]{:S(2)}, u32[]{:S(2)}) collective-permute-start(bf16[4,48,1536]{2,1,0:T(8,128)(2,1)S(1)} %get-tuple-element.108), channel_id=1, source_target_pairs={{0,16},{4,20},{8,24},{12,28},{16,0},{20,4},{24,8},{28,12},{1,17},{... | collective-permute-start | bytes 1769480 | tf_op jit(solution)/shard_map/ppermute | solution.py:143
  356.9 22.5 %collective-permute-start.31 = (bf16[4,4,192,384]{3,2,1,0:T(8,128)(2,1)}, bf16[4,4,192,384]{3,2,1,0:T(8,128)(2,1)}, u32[]{:S(2)}, u32[]{:S(2)}) collective-permute-start(bf16[4,4,192,384]{3,2,1,0:T(8,128)(2,1)} %bitcast.89), channel_id=1, source_target_pairs={{0,4},{4,0},{8,12},{12,8},{16,20},{20,16},{24,28},{28,24},{1,5},{5... | collective-permute-start | bytes 7077896 | tf_op jit(solution)/shard_map/ppermute | solution.py:129
  362.5 7.4 %collective-permute-start.28 = (bf16[48,1536]{1,0:T(8,128)(2,1)S(1)}, bf16[48,1536]{1,0:T(8,128)(2,1)S(1)}, u32[]{:S(2)}, u32[]{:S(2)}) collective-permute-start(bf16[48,1536]{1,0:T(8,128)(2,1)S(1)} %get-tuple-element.132), channel_id=1, source_target_pairs={{0,1},{1,2},{2,3},{3,0},{4,5},{5,6},{6,7},{7,4},{8,9},{9,10},{10,1... | collective-permute-start | bytes 442376 | tf_op jit(solution)/shard_map/ppermute | solution.py:148
  362.6 7.2 %collective-permute-start.30 = (bf16[48,1536]{1,0:T(8,128)(2,1)S(1)}, bf16[48,1536]{1,0:T(8,128)(2,1)S(1)}, u32[]{:S(2)}, u32[]{:S(2)}) collective-permute-start(bf16[48,1536]{1,0:T(8,128)(2,1)S(1)} %get-tuple-element.133), channel_id=1, source_target_pairs={{0,3},{1,0},{2,1},{3,2},{4,7},{5,4},{6,5},{7,6},{8,11},{9,8},{10,9... | collective-permute-start | bytes 442376 | tf_op jit(solution)/shard_map/ppermute | solution.py:148
  366.4 9.5 %collective-permute-start.29 = (bf16[48,1536]{1,0:T(8,128)(2,1)S(1)}, bf16[48,1536]{1,0:T(8,128)(2,1)S(1)}, u32[]{:S(2)}, u32[]{:S(2)}) collective-permute-start(bf16[48,1536]{1,0:T(8,128)(2,1)S(1)} %get-tuple-element.134), channel_id=1, source_target_pairs={{0,2},{1,3},{2,0},{3,1},{4,6},{5,7},{6,4},{7,5},{8,10},{9,11},{10,... | collective-permute-start | bytes 442376 | tf_op jit(solution)/shard_map/ppermute | solution.py:148
  376.8 96.3 %all-gather.23.cloned.1.call-start = ((), (), s32[]{:S(2)}) async-start(), calls=%async_computation.5 | async-start | bytes 2654208 | tf_op jit(solution)/shard_map/all_gather | solution.py:151
  381.9 13.1 %collective-permute-start.32 = (bf16[4,192,384]{2,1,0:T(8,128)(2,1)S(1)}, bf16[4,192,384]{2,1,0:T(8,128)(2,1)S(1)}, u32[]{:S(2)}, u32[]{:S(2)}) collective-permute-start(bf16[4,192,384]{2,1,0:T(8,128)(2,1)S(1)} %fusion.58), channel_id=1, source_target_pairs={{0,8},{4,20},{8,0},{12,28},{16,24},{20,4},{24,16},{28,12},{1,9},{5... | collective-permute-start | bytes 1769480 | tf_op jit(solution)/shard_map/ppermute | solution.py:135
  395.3 19.4 %collective-permute-start.33 = (bf16[4,192,384]{2,1,0:T(8,128)(2,1)S(1)}, bf16[4,192,384]{2,1,0:T(8,128)(2,1)S(1)}, u32[]{:S(2)}, u32[]{:S(2)}) collective-permute-start(bf16[4,192,384]{2,1,0:T(8,128)(2,1)S(1)} %get-tuple-element.105), channel_id=1, source_target_pairs={{0,8},{4,12},{8,0},{12,4},{16,24},{20,28},{24,16},{28,20},{1,9},{5... | collective-permute-start | bytes 1769480 | tf_op jit(solution)/shard_map/ppermute | solution.py:142
  396.6 19.5 %collective-permute-start.34 = (bf16[4,192,384]{2,1,0:T(8,128)(2,1)S(1)}, bf16[4,192,384]{2,1,0:T(8,128)(2,1)S(1)}, u32[]{:S(2)}, u32[]{:S(2)}) collective-permute-start(bf16[4,192,384]{2,1,0:T(8,128)(2,1)S(1)} %get-tuple-element.106), channel_id=1, source_target_pairs={{0,16},{4,20},{8,24},{12,28},{16,0},{20,4},{24,8},{28,12},{1,17},{... | collective-permute-start | bytes 1769480 | tf_op jit(solution)/shard_map/ppermute | solution.py:143
  399.6 20.8 %collective-permute-start.17 = (bf16[4,4,48,384]{3,2,1,0:T(8,128)(2,1)S(1)}, bf16[4,4,48,384]{3,2,1,0:T(8,128)(2,1)S(1)}, u32[]{:S(2)}, u32[]{:S(2)}) collective-permute-start(bf16[4,4,48,384]{3,2,1,0:T(8,128)(2,1)S(1)} %bitcast.294), channel_id=1, source_target_pairs={{0,4},{4,0},{8,12},{12,8},{16,20},{20,16},{24,28},{28,24},{1,5},{5... | collective-permute-start | bytes 1769480 | tf_op jit(solution)/shard_map/ppermute | solution.py:129
  416.5 8.7 %collective-permute-start.35 = (bf16[192,384]{1,0:T(8,128)(2,1)S(1)}, bf16[192,384]{1,0:T(8,128)(2,1)S(1)}, u32[]{:S(2)}, u32[]{:S(2)}) collective-permute-start(bf16[192,384]{1,0:T(8,128)(2,1)S(1)} %get-tuple-element.129), channel_id=1, source_target_pairs={{0,1},{1,2},{2,3},{3,0},{4,5},{5,6},{6,7},{7,4},{8,9},{9,10},{10,1... | collective-permute-start | bytes 442376 | tf_op jit(solution)/shard_map/ppermute | solution.py:148
  416.5 8.6 %collective-permute-start.37 = (bf16[192,384]{1,0:T(8,128)(2,1)S(1)}, bf16[192,384]{1,0:T(8,128)(2,1)S(1)}, u32[]{:S(2)}, u32[]{:S(2)}) collective-permute-start(bf16[192,384]{1,0:T(8,128)(2,1)S(1)} %get-tuple-element.130), channel_id=1, source_target_pairs={{0,3},{1,0},{2,1},{3,2},{4,7},{5,4},{6,5},{7,6},{8,11},{9,8},{10,9... | collective-permute-start | bytes 442376 | tf_op jit(solution)/shard_map/ppermute | solution.py:148
  420.3 9.5 %collective-permute-start.36 = (bf16[192,384]{1,0:T(8,128)(2,1)S(1)}, bf16[192,384]{1,0:T(8,128)(2,1)S(1)}, u32[]{:S(2)}, u32[]{:S(2)}) collective-permute-start(bf16[192,384]{1,0:T(8,128)(2,1)S(1)} %get-tuple-element.131), channel_id=1, source_target_pairs={{0,2},{1,3},{2,0},{3,1},{4,6},{5,7},{6,4},{7,5},{8,10},{9,11},{10,... | collective-permute-start | bytes 442376 | tf_op jit(solution)/shard_map/ppermute | solution.py:148
  421.5 16.6 %collective-permute-start.18 = (bf16[4,48,384]{2,1,0:T(8,128)(2,1)S(1)}, bf16[4,48,384]{2,1,0:T(8,128)(2,1)S(1)}, u32[]{:S(2)}, u32[]{:S(2)}) collective-permute-start(bf16[4,48,384]{2,1,0:T(8,128)(2,1)S(1)} %fusion.76), channel_id=1, source_target_pairs={{0,8},{4,20},{8,0},{12,28},{16,24},{20,4},{24,16},{28,12},{1,9},{5... | collective-permute-start | bytes 442376 | tf_op jit(solution)/shard_map/ppermute | solution.py:135
  438.2 7.8 %collective-permute-start.19 = (bf16[4,48,384]{2,1,0:T(8,128)(2,1)S(1)}, bf16[4,48,384]{2,1,0:T(8,128)(2,1)S(1)}, u32[]{:S(2)}, u32[]{:S(2)}) collective-permute-start(bf16[4,48,384]{2,1,0:T(8,128)(2,1)S(1)} %get-tuple-element.127), channel_id=1, source_target_pairs={{0,8},{4,12},{8,0},{12,4},{16,24},{20,28},{24,16},{28,20},{1,9},{5... | collective-permute-start | bytes 442376 | tf_op jit(solution)/shard_map/ppermute | solution.py:142
  438.6 7.5 %collective-permute-start.20 = (bf16[4,48,384]{2,1,0:T(8,128)(2,1)S(1)}, bf16[4,48,384]{2,1,0:T(8,128)(2,1)S(1)}, u32[]{:S(2)}, u32[]{:S(2)}) collective-permute-start(bf16[4,48,384]{2,1,0:T(8,128)(2,1)S(1)} %get-tuple-element.128), channel_id=1, source_target_pairs={{0,16},{4,20},{8,24},{12,28},{16,0},{20,4},{24,8},{28,12},{1,17},{... | collective-permute-start | bytes 442376 | tf_op jit(solution)/shard_map/ppermute | solution.py:143
  446.3 5.9 %collective-permute-start.21 = (bf16[48,384]{1,0:T(8,128)(2,1)S(1)}, bf16[48,384]{1,0:T(8,128)(2,1)S(1)}, u32[]{:S(2)}, u32[]{:S(2)}) collective-permute-start(bf16[48,384]{1,0:T(8,128)(2,1)S(1)} %get-tuple-element.144), channel_id=1, source_target_pairs={{0,1},{1,2},{2,3},{3,0},{4,5},{5,6},{6,7},{7,4},{8,9},{9,10},{10,1... | collective-permute-start | bytes 110600 | tf_op jit(solution)/shard_map/ppermute | solution.py:148
  446.3 5.9 %collective-permute-start.23 = (bf16[48,384]{1,0:T(8,128)(2,1)S(1)}, bf16[48,384]{1,0:T(8,128)(2,1)S(1)}, u32[]{:S(2)}, u32[]{:S(2)}) collective-permute-start(bf16[48,384]{1,0:T(8,128)(2,1)S(1)} %get-tuple-element.145), channel_id=1, source_target_pairs={{0,3},{1,0},{2,1},{3,2},{4,7},{5,4},{6,5},{7,6},{8,11},{9,8},{10,9... | collective-permute-start | bytes 110600 | tf_op jit(solution)/shard_map/ppermute | solution.py:148
  450.4 4.9 %collective-permute-start.22 = (bf16[48,384]{1,0:T(8,128)(2,1)S(1)}, bf16[48,384]{1,0:T(8,128)(2,1)S(1)}, u32[]{:S(2)}, u32[]{:S(2)}) collective-permute-start(bf16[48,384]{1,0:T(8,128)(2,1)S(1)} %get-tuple-element.146), channel_id=1, source_target_pairs={{0,2},{1,3},{2,0},{3,1},{4,6},{5,7},{6,4},{7,5},{8,10},{9,11},{10,... | collective-permute-start | bytes 110600 | tf_op jit(solution)/shard_map/ppermute | solution.py:148
  (64 other events, 466.8 us)
Sparse Core Ops, SparseCore 0:
  43.5 33.2 all-gather.14
  79.2 38.7 all-gather.12
  120.5 38.7 all-gather.16
  341.4 28.8 all-gather.18
  376.9 36.6 all-gather.20
  430.8 29.9 all-gather.22

commit v16 on v10

--- a/solution.py
+++ b/solution.py
@@ -76,8 +76,20 @@
     return x.reshape(NF_FAST * m.shape[0], m.shape[1])
 
 
+def _gather_matrix_pp(m):
+    d = lax.axis_index("dp")
+    j, c = d // 2, d % 2
+    n_chips = NDP_FAST // 2
+    rows, cols = m.shape[0] // n_chips, m.shape[1] // 2
+    z = _z_gather(lax.dynamic_slice(m, (j * rows, c * cols), (rows, cols)))
+    x = _take(_plane_gather(z), jnp.arange(NDP_FAST, dtype=jnp.int32) ^ d, 0)
+    x = x.reshape(n_chips, 2, NF_FAST, rows, cols)
+    x = jnp.concatenate([x[:, 0], x[:, 1]], axis=-1).transpose(1, 0, 2, 3)
+    return x.reshape(NF_FAST * m.shape[0], m.shape[1])
+
+
 def fast_gather(mats, gains):
-    out = [_gather_matrix(m) for m in mats]
+    out = [_gather_matrix_pp(mats[0])] + [_gather_matrix(m) for m in mats[1:]]
     stacked = jnp.concatenate(gains, axis=0)
     z = _z_gather(stacked)
     full = z.transpose(1, 0, 2).reshape(stacked.shape[0], NF_FAST * stacked.shape[1])
@@ -121,7 +133,7 @@
         total = total + lax.ppermute(
             part.astype(jnp.bfloat16), "fsdp", [(i, (i + k) % NF_FAST) for i in range(NF_FAST)]
         ).astype(jnp.float32)
-    x = _take(_plane_gather(total), jnp.arange(NDP_FAST, dtype=jnp.int32) ^ d, 0)
+    x = lax.all_gather(total.astype(jnp.bfloat16), "dp", axis=0, tiled=False).astype(jnp.float32)
     x = x.reshape(n_chips, 2, rows, cols)
     x = jnp.concatenate([x[:, 0], x[:, 1]], axis=-1)
     return x.reshape(n_chips * rows, 2 * cols)

time: 493 us -> 456 us (0.925)
  local copies, waits for them, and re-layouts: 98.9 us -> 74.7 us
  waiting for transfers between devices: 117 us -> 95.9 us
  blocking collectives: 0 us -> 20.6 us
  starting transfers between devices: 71 us -> 61.6 us
    all_gather x4 -> x3, waiting for transfers between devices: 37 us -> 0.04 us  [_gather_matrix(): x = lax.all_gather(z, 'dp', axis=1, tiled=False)]
    all_gather x0 -> x2, blocking collectives: none -> 20.6 us  [_reduce_matrix(): lax.all_gather(total.astype(jnp.bfloat16), 'dp', axis=0, tiled=False)]
    ppermute x4 -> x1, waiting for transfers between devices: 15 us -> 3.85 us  [_plane_gather(): b = lax.ppermute(z, 'dp', [(i, i ^ 4) for i in range(NDP_FAST)])]
    ppermute x4 -> x1, waiting for transfers between devices: 0.45 us -> 11.2 us  [_plane_gather(): a = lax.ppermute(z, 'dp', [(i, i ^ 2) for i in range(NDP_FAST)])]
    unnamed x203 -> x178, local copies, waits for them, and re-layouts: 28.9 us -> 19.5 us
    all_gather x0 -> x2, waiting for transfers between devices: none -> 9.32 us  [_reduce_matrix(): lax.all_gather(total.astype(jnp.bfloat16), 'dp', axis=0, tiled=False)]
    ppermute x15, waiting for transfers between devices: 18 us -> 8.9 us  [_z_gather(): lax.ppermute(piece, 'fsdp', [(i, (i + k) % NF_FAST) for i in range(NF_FAS...]
    ppermute x4, waiting for transfers between devices: 5.43 us -> 12 us  [_reduce_matrix(): lax.ppermute(of_chip(j ^ 3).astype(jnp.bfloat16), 'dp', [(i, i ^ 2) if i...]
  transfers between devices with their start and end apart: 63 -> 52, of which waited for: 32 -> 25; matrix products, arithmetic and copies ran while one was open for 40% -> 26% of each run, Pallas kernels for 0% -> 0%
where the time goes in v16:
time: 456 us; the launch traced here: 447 us
  matrix products  109 us (24%)
  waiting for transfers between devices  95.9 us (21%)
  local copies, waits for them, and re-layouts  74.7 us (16%)
  other arithmetic  68.8 us (15%)
  starting transfers between devices  61.6 us (14%)
  blocking collectives  20.6 us (5%)
  between operations  15.6 us (3%)
    ppermute x15, starting transfers between devices, _z_gather(): lax.ppermute(piece, 'fsdp', [(i, (i + k) % NF_FAST) for i in range(NF_FAS...  22.3 us
    dot_general x1, matrix products, layer(): up_pre = jnp.dot(second_low, full_up, preferred_element_type=jnp.float32)  22 us
    ppermute x4, waiting for transfers between devices, _reduce_matrix(): lax.ppermute(to_x.astype(jnp.bfloat16), 'dp', [(i, i ^ 2) for i in range(...  21.5 us
    ppermute x12, starting transfers between devices, _reduce_matrix(): lax.ppermute(part.astype(jnp.bfloat16), 'fsdp', [(i, (i + k) % NF_FAST) f...  20.9 us
    all_gather x2, blocking collectives, _reduce_matrix(): lax.all_gather(total.astype(jnp.bfloat16), 'dp', axis=0, tiled=False)  20.6 us
    unnamed x178, local copies, waits for them, and re-layouts  19.5 us
    ppermute x12, waiting for transfers between devices, _reduce_matrix(): lax.ppermute(part.astype(jnp.bfloat16), 'fsdp', [(i, (i + k) % NF_FAST) f...  17.8 us
    ppermute x4, waiting for transfers between devices, _reduce_matrix(): lax.ppermute(of_chip(j ^ 3).astype(jnp.bfloat16), 'dp', [(i, i ^ 2) if i...  12 us
  transfers between devices with their start and end apart: 52, of which 25 were waited for; matrix products, arithmetic and copies ran while one was open for 26% of the time, Pallas kernels for 0%

profile of v16, /device:TPU:8, one launch (start us, length us, event | category | flops | bytes accessed | tf_op | source)
XLA Modules:
  0.0 446.7 jit_solution(2239646625177142256)
XLA Ops:
  8.1 2.6 collective-permute-start.11
  16.9 4.7 %collective-permute-start.17 = (bf16[192,384]{1,0:T(8,128)(2,1)S(1)}, bf16[192,384]{1,0:T(8,128)(2,1)S(1)}, u32[]{:S(2)}, u32[]{:S(2)}) collective-permute-start(bf16[192,384]{1,0:T(8,128)(2,1)S(1)} %dynamic_slice.153), channel_id=1, source_target_pairs={{0,2},{1,3},{2,0},{3,1},{4,6},{5,7},{6,4},{7,5},{8,10},{9,11},{10,... | collective-permute-start | bytes 442376 | tf_op jit(solution)/shard_map/ppermute | solution.py:61
  24.5 4.8 %collective-permute-done.17 = bf16[192,384]{1,0:T(8,128)(2,1)S(1)} collective-permute-done((bf16[192,384]{1,0:T(8,128)(2,1)S(1)}, bf16[192,384]{1,0:T(8,128)(2,1)S(1)}, u32[]{:S(2)}, u32[]{:S(2)}) %collective-permute-start.17) | collective-permute-done | bytes 147488 | tf_op jit(solution)/shard_map/ppermute | solution.py:61
  36.3 3.6 collective-permute-start.4
  54.5 11.2 %collective-permute-done.6 = bf16[4,48,1152]{2,1,0:T(8,128)(2,1)S(1)} collective-permute-done((bf16[4,48,1152]{2,1,0:T(8,128)(2,1)S(1)}, bf16[4,48,1152]{2,1,0:T(8,128)(2,1)S(1)}, u32[]{:S(2)}, u32[]{:S(2)}) %collective-permute-start.6) | collective-permute-done | bytes 442400 | tf_op jit(solution)/shard_map/ppermute | solution.py:43
  65.7 3.9 collective-permute-done.7
  74.1 10.5 %collective-permute-done.8 = bf16[4,48,1152]{2,1,0:T(8,128)(2,1)S(1)} collective-permute-done((bf16[4,48,1152]{2,1,0:T(8,128)(2,1)S(1)}, bf16[4,48,1152]{2,1,0:T(8,128)(2,1)S(1)}, u32[]{:S(2)}, u32[]{:S(2)}) %collective-permute-start.8) | collective-permute-done | bytes 442400 | tf_op jit(solution)/shard_map/ppermute | solution.py:46
  101.4 3.4 gather_fusion.2
  106.5 2.4 fusion.117
  113.2 3.4 fusion.124
  125.7 8.2 %fusion.133 = (f32[12,576]{1,0:T(8,128)S(1)}, f32[12,576,576]{1,2,0:T(8,128)}) fusion(f32[576,12,64]{0,2,1:T(8,128)S(1)} %bitcast.264, f32[12,64]{1,0:T(8,128)S(1)} %mul.355, f32[576,12]{0,1:T(8,128)S(1)} %fusion.98, f32[576,12]{0,1:T(8,128)S(1)} %broadcast_multiply_fusion, f32[576,12,64]{0,2,1:T(8,128)S(1)} %bitcast.257, f32[12,64]{1,0:T(8,128)S(1)} %copy-done.49, ...), kind=kOutput, calls=%fused_computation.295 | convolution fusion | flops 525083904 | bytes 19940352 | tf_op jit(solution)/shard_map/while/body/eval_jaxpr/qhd,khd->hqk/dot_general | solution.py:210
  133.9 8.6 %fusion.3 = f32[12,576]{1,0:T(8,128)S(1)} fusion(f32[12,576,576]{1,2,0:T(8,128)} %get-tuple-element.152, f32[12,576]{1,0:T(8,128)S(1)} %get-tuple-element.151), kind=kLoop, calls=%fused_computation.15 | loop fusion | flops 7955712 | bytes 15980544 | tf_op jit(solution)/shard_map/while/body/eval_jaxpr/reduce_sum | solution.py:220
  142.5 9.4 %fusion.35 = bf16[12,64,576]{2,1,0:T(8,128)(2,1)S(1)} fusion(bf16[576,12,64]{0,2,1:T(8,128)(2,1)S(1)} %bitcast.297, f32[12,576,576]{1,2,0:T(8,128)} %get-tuple-element.152, f32[12,576]{1,0:T(8,128)S(1)} %fusion.3, f32[12,576]{1,0:T(8,128)S(1)} %get-tuple-element.151), kind=kOutput, calls=%fused_computation.108 | convolution fusion | flops 521994240 | bytes 17750016 | tf_op jit(solution)/shard_map/while/body/eval_jaxpr/hqk,khd->qhd/dot_general | solution.py:222
  153.4 5.1 %fusion.125 = (bf16[4,4,1,192,384]{4,3,2,1,0:T(8,128)(2,1)}, bf16[4,4,1,192,384]{4,3,2,1,0:T(8,128)(2,1)}) fusion(bf16[4,4,2,192,384]{4,3,2,1,0:T(8,128)(2,1)} %bitcast.282), kind=kLoop, calls=%fused_computation.287 | loop fusion | bytes 9437184 | tf_op jit(solution)/shard_map/slice | solution.py:75
  158.5 2.9 fusion.126
  161.4 22.0 %multiply_convert_fusion = (bf16[576,3072]{1,0:T(8,128)(2,1)}, f32[576,3072]{1,0:T(8,128)}, f32[576,3072]{1,0:T(8,128)}) fusion(bf16[768,1536]{1,0:T(8,128)(2,1)S(1)} %bitcast.309, bf16[768,1536]{1,0:T(8,128)(2,1)S(1)} %bitcast.307, f32[576,768]{1,0:T(8,128)S(1)} %get-tuple-element.154, f32[768]{0:T(1024)S(1)} %add.403, f32[768]{0:T(1024)S(1)} %mul.363, ...), kind=kOutput, calls=%fused_computation.25 | convolution fusion | flops 2844573696 | bytes 24193536 | tf_op jit(solution)/shard_map/dot_general | solution.py:232
  183.5 8.3 %add_convert_fusion = bf16[576,3072]{1,0:T(8,128)(2,1)S(1)} fusion(f32[576,3072]{1,0:T(8,128)} %get-tuple-element.104, f32[576,3072]{1,0:T(8,128)} %get-tuple-element.155, bf16[3072,384]{1,0:T(8,128)(2,1)S(1)} %bitcast.305, bf16[3072,384]{1,0:T(8,128)(2,1)S(1)} %bitcast.303, bf16[576,768]{1,0:T(8,128)(2,1)S(1)} %copy-done.18, f32[576]{0:T(1024)S(1)} %copy-done.56), kind=kOutput, calls=%fused_computation.24 | convolution fusion | flops 2753445888 | bytes 23300352 | tf_op jit(solution)/shard_map/dot_general | solution.py:241
  191.8 3.2 multiply_reduce_fusion.2
  199.5 2.5 fusion.135
  202.0 6.7 %fusion.120 = f32[768,3072]{1,0:T(8,128)} fusion(bf16[576,3072]{1,0:T(8,128)(2,1)S(1)} %add_convert_fusion, f32[576,768]{1,0:T(8,128)S(1)} %get-tuple-element.154, f32[768]{0:T(1024)S(1)} %add.403, f32[768]{0:T(1024)S(1)} %mul.363, f32[576]{0:T(1024)S(1)} %fusion.101, f32[576]{0:T(1024)S(1)} %broadcast_multiply_fusion.4), kind=kOutput, calls=%fused_computation.283 | convolution fusion | flops 2720120832 | bytes 14756352 | tf_op jit(solution)/shard_map/dot_general | solution.py:244
  208.7 3.8 multiply_convert_fusion.3
  212.5 6.6 %fusion.60 = f32[3072,768]{1,0:T(8,128)} fusion(bf16[576,3072]{1,0:T(8,128)(2,1)S(1)} %copy-done.70, bf16[576,768]{1,0:T(8,128)(2,1)S(1)} %copy-done.18, f32[576]{0:T(1024)S(1)} %copy-done.56), kind=kOutput, calls=%fused_computation.155 | convolution fusion | flops 2719236096 | bytes 13863168 | tf_op jit(solution)/shard_map/dot_general | solution.py:240
  220.7 4.8 %convolution_convert_fusion = bf16[12,576,576]{1,2,0:T(8,128)(2,1)} fusion(bf16[576,12,64]{0,2,1:T(8,128)(2,1)S(1)} %bitcast.278, bf16[576,12,64]{0,2,1:T(8,128)(2,1)S(1)} %bitcast.298), kind=kOutput, calls=%fused_computation.39 | convolution fusion | flops 513589248 | bytes 9732096 | tf_op jit(solution)/shard_map/qhd,khd->hqk/dot_general | solution.py:261
  225.5 9.9 %fusion.36 = bf16[12,64,576]{2,1,0:T(8,128)(2,1)} fusion(bf16[576,12,64]{0,2,1:T(8,128)(2,1)S(1)} %bitcast.279, f32[12,576,576]{1,2,0:T(8,128)} %get-tuple-element.152, f32[12,576]{1,0:T(8,128)S(1)} %log_add_fusion), kind=kOutput, calls=%fused_computation.109 | convolution fusion | flops 518012928 | bytes 17722368 | tf_op jit(solution)/shard_map/hqk,qhd->khd/dot_general | solution.py:260
  235.4 10.7 %fusion = f32[12,576]{1,0:T(8,128)S(1)} fusion(bf16[12,576,576]{1,2,0:T(8,128)(2,1)} %convolution_convert_fusion, f32[12,576,576]{1,2,0:T(8,128)} %get-tuple-element.152, f32[12,576]{1,0:T(8,128)S(1)} %log_add_fusion), kind=kLoop, calls=%fused_computation.8 | loop fusion | flops 15918336 | bytes 23943168 | tf_op jit(solution)/shard_map/reduce_sum | solution.py:263
  246.5 2.5 copy-done.5
  249.0 6.0 %fusion.2 = bf16[12,576,576]{1,2,0:T(8,128)(2,1)} fusion(bf16[12,576,576]{1,2,0:T(8,128)(2,1)S(1)} %copy-done.5, f32[12,576,576]{1,2,0:T(8,128)S(1)} %bitcast.254, f32[12,576]{1,0:T(8,128)S(1)} %fusion, f32[12,576]{1,0:T(8,128)S(1)} %log_add_fusion), kind=kLoop, calls=%fused_computation.10 | loop fusion | flops 19906560 | bytes 31905792 | tf_op jit(solution)/shard_map/convert_element_type | solution.py:264
  255.1 7.7 %fusion.27 = (f32[576,12]{0,1:T(8,128)S(1)}, f32[12,64,576]{2,1,0:T(8,128)}) fusion(f32[576,12,64]{0,2,1:T(8,128)S(1)} %bitcast.265, f32[12,64]{1,0:T(8,128)S(1)} %copy-done.47, f32[576,12]{0,1:T(8,128)S(1)} %copy-done.23, bf16[12,576,576]{1,2,0:T(8,128)(2,1)} %fusion.2, f32[576,12,64]{0,2,1:T(8,128)S(1)} %bitcast.258, f32[12,64]{1,0:T(8,128)S(1)} %copy-done.50, ...), kind=kOutput, calls=%fused_computation.75 | convolution fusion | flops 513139968 | bytes 13387776 | tf_op jit(solution)/shard_map/hqk,qhd->khd/dot_general | solution.py:269
  270.6 2.8 fusion.121
  273.4 6.4 %fusion.39 = f32[768,2304]{1,0:T(8,128)} fusion(bf16[576,768]{0,1:T(8,128)(2,1)S(1)} %bitcast.322, bf16[576,768]{0,1:T(8,128)(2,1)S(1)} %bitcast.318, bf16[576,768]{0,1:T(8,128)(2,1)S(1)} %bitcast.320, bf16[576,768]{1,0:T(8,128)(2,1)S(1)} %copy-done.11, f32[768]{0:T(1024)S(1)} %copy-done.63, f32[768]{0:T(1024)S(1)} %copy-done.60, f32[576]{0:T(1024)S(1)} %copy-done.58, ...), kind=kOutput, calls=%fused_computation.113 | convolution fusion | flops 2049048576 | bytes 10627584 | tf_op jit(solution)/shard_map/dot_general | solution.py:287
  279.8 2.5 constant_dynamic-slice_fusion
  286.2 4.0 dynamic-slice_convert_fusion.1
  294.2 4.3 select_maximum_fusion
  300.6 4.8 %collective-permute-done.27 = bf16[4,48,384]{2,1,0:T(8,128)(2,1)S(1)} collective-permute-done((bf16[4,48,384]{2,1,0:T(8,128)(2,1)S(1)}, bf16[4,48,384]{2,1,0:T(8,128)(2,1)S(1)}, u32[]{:S(2)}, u32[]{:S(2)}) %collective-permute-start.27) | collective-permute-done | bytes 147488 | tf_op jit(solution)/shard_map/ppermute | solution.py:120
  305.5 2.5 collective-permute-start.29
  308.3 2.6 collective-permute-done.28
  318.2 10.0 %all-gather.4 = bf16[384,384]{1,0:T(8,128)(2,1)S(1)} all-gather(bf16[48,384]{1,0:T(8,128)(2,1)S(1)} %fusion.93), channel_id=6, replica_groups=mesh['dp'=8,'fsdp'=4] {'dp'}, dimensions={0}, use_global_device_ids=true | all-gather | bytes 331776 | tf_op jit(solution)/shard_map/all_gather | solution.py:136
  329.1 2.5 convert_add_fusion.1
  334.4 7.2 %collective-permute-done.34 = bf16[4,48,1536]{2,1,0:T(8,128)(2,1)S(1)} collective-permute-done((bf16[4,48,1536]{2,1,0:T(8,128)(2,1)S(1)}, bf16[4,48,1536]{2,1,0:T(8,128)(2,1)S(1)}, u32[]{:S(2)}, u32[]{:S(2)}) %collective-permute-start.34) | collective-permute-done | bytes 589856 | tf_op jit(solution)/shard_map/ppermute | solution.py:120
  346.3 13.2 %collective-permute-done.35 = bf16[4,48,1536]{2,1,0:T(8,128)(2,1)S(1)} collective-permute-done((bf16[4,48,1536]{2,1,0:T(8,128)(2,1)S(1)}, bf16[4,48,1536]{2,1,0:T(8,128)(2,1)S(1)}, u32[]{:S(2)}, u32[]{:S(2)}) %collective-permute-start.35) | collective-permute-done | bytes 589856 | tf_op jit(solution)/shard_map/ppermute | solution.py:127
  365.5 2.7 collective-permute-start.22
  368.2 3.3 collective-permute-done.39
  380.1 4.8 %collective-permute-start.23 = (bf16[48,1280]{1,0:T(8,128)(2,1)S(1)}, bf16[48,1280]{1,0:T(8,128)(2,1)S(1)}, u32[]{:S(2)}, u32[]{:S(2)}) collective-permute-start(bf16[48,1280]{1,0:T(8,128)(2,1)S(1)} %get-tuple-element.135), channel_id=1, source_target_pairs={{0,1},{1,2},{2,3},{3,0},{4,5},{5,6},{6,7},{7,4},{8,9},{9,10},{10,1... | collective-permute-start | bytes 368648 | tf_op jit(solution)/shard_map/ppermute | solution.py:133
  386.4 5.7 %collective-permute-done.42 = bf16[4,192,384]{2,1,0:T(8,128)(2,1)S(1)} collective-permute-done((bf16[4,192,384]{2,1,0:T(8,128)(2,1)S(1)}, bf16[4,192,384]{2,1,0:T(8,128)(2,1)S(1)}, u32[]{:S(2)}, u32[]{:S(2)}) %collective-permute-start.42) | collective-permute-done | bytes 589856 | tf_op jit(solution)/shard_map/ppermute | solution.py:127
  393.7 3.5 collective-permute-start.44
  403.0 4.9 %collective-permute-done.46 = bf16[192,384]{1,0:T(8,128)(2,1)S(1)} collective-permute-done((bf16[192,384]{1,0:T(8,128)(2,1)S(1)}, bf16[192,384]{1,0:T(8,128)(2,1)S(1)}, u32[]{:S(2)}, u32[]{:S(2)}) %collective-permute-start.46) | collective-permute-done | bytes 147488 | tf_op jit(solution)/shard_map/ppermute | solution.py:133
  410.3 10.5 %all-gather.3 = bf16[384,1280]{1,0:T(8,128)(2,1)S(1)} all-gather(bf16[48,1280]{1,0:T(8,128)(2,1)S(1)} %fusion.76), channel_id=5, replica_groups=mesh['dp'=8,'fsdp'=4] {'dp'}, dimensions={0}, use_global_device_ids=true | all-gather | bytes 1105920 | tf_op jit(solution)/shard_map/all_gather | solution.py:136
  426.0 9.3 %all-gather.21.cloned.1.call-done = bf16[1536,384]{1,0:T(8,128)(2,1)} async-done(((bf16[192,384]{1,0:T(8,128)(2,1)}), bf16[1536,384]{1,0:T(8,128)(2,1)}) %all-gather.21.cloned.1.call-update) | async-done | bytes 1179664 | tf_op jit(solution)/shard_map/all_gather | solution.py:136
  (404 shorter events, 144.1 us)
Async XLA Ops:
  7.2 86.1 %all-gather.13.cloned.1.call-start = ((), (), s32[]{:S(2)}) async-start(), calls=%async_computation | async-start | bytes 1327104 | tf_op jit(solution)/shard_map/all_gather | solution.py:73
  8.1 5.4 %collective-permute-start.11 = (bf16[48,384]{1,0:T(8,128)(2,1)S(1)}, bf16[48,384]{1,0:T(8,128)(2,1)S(1)}, u32[]{:S(2)}, u32[]{:S(2)}) collective-permute-start(bf16[48,384]{1,0:T(8,128)(2,1)S(1)} %dynamic_slice.151), channel_id=1, source_target_pairs={{0,2},{1,3},{2,0},{3,1},{4,6},{5,7},{6,4},{7,5},{8,10},{9,11},{10,... | collective-permute-start | bytes 110600 | tf_op jit(solution)/shard_map/ppermute | solution.py:61
  15.9 137.5 %all-gather.17.cloned.1.call-start = ((), (), s32[]{:S(2)}) async-start(), calls=%async_computation.2 | async-start | bytes 5308416 | tf_op jit(solution)/shard_map/all_gather | solution.py:73
  16.9 12.4 %collective-permute-start.17 = (bf16[192,384]{1,0:T(8,128)(2,1)S(1)}, bf16[192,384]{1,0:T(8,128)(2,1)S(1)}, u32[]{:S(2)}, u32[]{:S(2)}) collective-permute-start(bf16[192,384]{1,0:T(8,128)(2,1)S(1)} %dynamic_slice.153), channel_id=1, source_target_pairs={{0,2},{1,3},{2,0},{3,1},{4,6},{5,7},{6,4},{7,5},{8,10},{9,11},{10,... | collective-permute-start | bytes 442376 | tf_op jit(solution)/shard_map/ppermute | solution.py:61
  21.6 9.3 %collective-permute-start.16 = (bf16[192,384]{1,0:T(8,128)(2,1)S(1)}, bf16[192,384]{1,0:T(8,128)(2,1)S(1)}, u32[]{:S(2)}, u32[]{:S(2)}) collective-permute-start(bf16[192,384]{1,0:T(8,128)(2,1)S(1)} %dynamic_slice.153), channel_id=1, source_target_pairs={{0,1},{1,2},{2,3},{3,0},{4,5},{5,6},{6,7},{7,4},{8,9},{9,10},{10,1... | collective-permute-start | bytes 442376 | tf_op jit(solution)/shard_map/ppermute | solution.py:61
  21.6 10.7 %collective-permute-start.18 = (bf16[192,384]{1,0:T(8,128)(2,1)S(1)}, bf16[192,384]{1,0:T(8,128)(2,1)S(1)}, u32[]{:S(2)}, u32[]{:S(2)}) collective-permute-start(bf16[192,384]{1,0:T(8,128)(2,1)S(1)} %dynamic_slice.153), channel_id=1, source_target_pairs={{0,3},{1,0},{2,1},{3,2},{4,7},{5,4},{6,5},{7,6},{8,11},{9,8},{10,9... | collective-permute-start | bytes 442376 | tf_op jit(solution)/shard_map/ppermute | solution.py:61
  33.9 124.6 %all-gather.15.cloned.1.call-start = ((), (), s32[]{:S(2)}) async-start(), calls=%async_computation.1 | async-start | bytes 5308416 | tf_op jit(solution)/shard_map/all_gather | solution.py:73
  34.0 37.5 %collective-permute-start.1 = (bf16[6,192]{1,0:T(8,128)(2,1)S(1)}, bf16[6,192]{1,0:T(8,128)(2,1)S(1)}, u32[]{:S(2)}, u32[]{:S(2)}) collective-permute-start(bf16[6,192]{1,0:T(8,128)(2,1)S(1)} %get-tuple-element.150), channel_id=1, source_target_pairs={{0,2},{1,3},{2,0},{3,1},{4,6},{5,7},{6,4},{7,5},{8,10},{9,11},{10,... | collective-permute-start | bytes 6920 | tf_op jit(solution)/shard_map/ppermute | solution.py:61
  34.4 38.0 %collective-permute-start = (bf16[6,192]{1,0:T(8,128)(2,1)S(1)}, bf16[6,192]{1,0:T(8,128)(2,1)S(1)}, u32[]{:S(2)}, u32[]{:S(2)}) collective-permute-start(bf16[6,192]{1,0:T(8,128)(2,1)S(1)} %get-tuple-element.150), channel_id=1, source_target_pairs={{0,1},{1,2},{2,3},{3,0},{4,5},{5,6},{6,7},{7,4},{8,9},{9,10},{10,1... | collective-permute-start | bytes 6920 | tf_op jit(solution)/shard_map/ppermute | solution.py:61
  36.3 10.9 %collective-permute-start.4 = (bf16[48,1152]{1,0:T(8,128)(2,1)S(1)}, bf16[48,1152]{1,0:T(8,128)(2,1)S(1)}, u32[]{:S(2)}, u32[]{:S(2)}) collective-permute-start(bf16[48,1152]{1,0:T(8,128)(2,1)S(1)} %dynamic_slice.150), channel_id=1, source_target_pairs={{0,2},{1,3},{2,0},{3,1},{4,6},{5,7},{6,4},{7,5},{8,10},{9,11},{10,... | collective-permute-start | bytes 331784 | tf_op jit(solution)/shard_map/ppermute | solution.py:61
  39.9 9.3 %collective-permute-start.3 = (bf16[48,1152]{1,0:T(8,128)(2,1)S(1)}, bf16[48,1152]{1,0:T(8,128)(2,1)S(1)}, u32[]{:S(2)}, u32[]{:S(2)}) collective-permute-start(bf16[48,1152]{1,0:T(8,128)(2,1)S(1)} %dynamic_slice.150), channel_id=1, source_target_pairs={{0,1},{1,2},{2,3},{3,0},{4,5},{5,6},{6,7},{7,4},{8,9},{9,10},{10,1... | collective-permute-start | bytes 331784 | tf_op jit(solution)/shard_map/ppermute | solution.py:61
  39.9 9.3 %collective-permute-start.5 = (bf16[48,1152]{1,0:T(8,128)(2,1)S(1)}, bf16[48,1152]{1,0:T(8,128)(2,1)S(1)}, u32[]{:S(2)}, u32[]{:S(2)}) collective-permute-start(bf16[48,1152]{1,0:T(8,128)(2,1)S(1)} %dynamic_slice.150), channel_id=1, source_target_pairs={{0,3},{1,0},{2,1},{3,2},{4,7},{5,4},{6,5},{7,6},{8,11},{9,8},{10,9... | collective-permute-start | bytes 331784 | tf_op jit(solution)/shard_map/ppermute | solution.py:61
  47.2 26.4 %collective-permute-start.2 = (bf16[6,192]{1,0:T(8,128)(2,1)S(1)}, bf16[6,192]{1,0:T(8,128)(2,1)S(1)}, u32[]{:S(2)}, u32[]{:S(2)}) collective-permute-start(bf16[6,192]{1,0:T(8,128)(2,1)S(1)} %get-tuple-element.150), channel_id=1, source_target_pairs={{0,3},{1,0},{2,1},{3,2},{4,7},{5,4},{6,5},{7,6},{8,11},{9,8},{10,9... | collective-permute-start | bytes 6920 | tf_op jit(solution)/shard_map/ppermute | solution.py:61
  49.9 15.9 %collective-permute-start.6 = (bf16[4,48,1152]{2,1,0:T(8,128)(2,1)S(1)}, bf16[4,48,1152]{2,1,0:T(8,128)(2,1)S(1)}, u32[]{:S(2)}, u32[]{:S(2)}) collective-permute-start(bf16[4,48,1152]{2,1,0:T(8,128)(2,1)S(1)} %gather_fusion.1), channel_id=1, source_target_pairs={{0,8},{4,12},{8,0},{12,4},{16,24},{20,28},{24,16},{28,20},{1,9},{5... | collective-permute-start | bytes 1327112 | tf_op jit(solution)/shard_map/ppermute | solution.py:43
  51.4 18.1 %collective-permute-start.7 = (bf16[4,48,1152]{2,1,0:T(8,128)(2,1)S(1)}, bf16[4,48,1152]{2,1,0:T(8,128)(2,1)S(1)}, u32[]{:S(2)}, u32[]{:S(2)}) collective-permute-start(bf16[4,48,1152]{2,1,0:T(8,128)(2,1)S(1)} %gather_fusion.1), channel_id=1, source_target_pairs={{0,16},{4,20},{8,24},{12,28},{16,0},{20,4},{24,8},{28,12},{1,17},{... | collective-permute-start | bytes 1327112 | tf_op jit(solution)/shard_map/ppermute | solution.py:44
  65.7 24.9 %collective-permute-start.14 = (bf16[48,1536]{1,0:T(8,128)(2,1)}, bf16[48,1536]{1,0:T(8,128)(2,1)S(1)}, u32[]{:S(2)}, u32[]{:S(2)}) collective-permute-start(bf16[48,1536]{1,0:T(8,128)(2,1)} %dynamic_slice.152), channel_id=1, source_target_pairs={{0,2},{1,3},{2,0},{3,1},{4,6},{5,7},{6,4},{7,5},{8,10},{9,11},{10,... | collective-permute-start | bytes 442376 | tf_op jit(solution)/shard_map/ppermute | solution.py:61
  69.6 15.0 %collective-permute-start.8 = (bf16[4,48,1152]{2,1,0:T(8,128)(2,1)S(1)}, bf16[4,48,1152]{2,1,0:T(8,128)(2,1)S(1)}, u32[]{:S(2)}, u32[]{:S(2)}) collective-permute-start(bf16[4,48,1152]{2,1,0:T(8,128)(2,1)S(1)} %broadcast_select_fusion), channel_id=1, source_target_pairs={{0,8},{4,20},{8,0},{12,28},{16,24},{20,4},{24,16},{28,12},{1,9},{5... | collective-permute-start | bytes 1327112 | tf_op jit(solution)/shard_map/ppermute | solution.py:46
  71.5 19.1 %collective-permute-start.13 = (bf16[48,1536]{1,0:T(8,128)(2,1)}, bf16[48,1536]{1,0:T(8,128)(2,1)}, u32[]{:S(2)}, u32[]{:S(2)}) collective-permute-start(bf16[48,1536]{1,0:T(8,128)(2,1)} %dynamic_slice.152), channel_id=1, source_target_pairs={{0,1},{1,2},{2,3},{3,0},{4,5},{5,6},{6,7},{7,4},{8,9},{9,10},{10,1... | collective-permute-start | bytes 442376 | tf_op jit(solution)/shard_map/ppermute | solution.py:61
  72.5 18.2 %collective-permute-start.15 = (bf16[48,1536]{1,0:T(8,128)(2,1)}, bf16[48,1536]{1,0:T(8,128)(2,1)}, u32[]{:S(2)}, u32[]{:S(2)}) collective-permute-start(bf16[48,1536]{1,0:T(8,128)(2,1)} %dynamic_slice.152), channel_id=1, source_target_pairs={{0,3},{1,0},{2,1},{3,2},{4,7},{5,4},{6,5},{7,6},{8,11},{9,8},{10,9... | collective-permute-start | bytes 442376 | tf_op jit(solution)/shard_map/ppermute | solution.py:61
  86.9 8.8 %collective-permute-start.9 = (bf16[4,4,48,1152]{3,2,1,0:T(8,128)(2,1)}, bf16[4,4,48,1152]{3,2,1,0:T(8,128)(2,1)S(1)}, u32[]{:S(2)}, u32[]{:S(2)}) collective-permute-start(bf16[4,4,48,1152]{3,2,1,0:T(8,128)(2,1)} %pad_maximum_fusion.12), channel_id=1, source_target_pairs={{0,4},{4,0},{8,12},{12,8},{16,20},{20,16},{24,28},{28,24},{1,5},{5... | collective-permute-start | bytes 5308424 | tf_op jit(solution)/shard_map/ppermute | solution.py:50
  93.3 331.2 %all-gather.19.cloned.1.call-start = ((), (), s32[]{:S(2)}) async-start(), calls=%async_computation.3 | async-start | bytes 1327104 | tf_op jit(solution)/shard_map/all_gather | solution.py:136
  285.7 12.8 %collective-permute-start.26 = (bf16[4,4,48,384]{3,2,1,0:T(8,128)(2,1)}, bf16[4,4,48,384]{3,2,1,0:T(8,128)(2,1)}, u32[]{:S(2)}, u32[]{:S(2)}) collective-permute-start(bf16[4,4,48,384]{3,2,1,0:T(8,128)(2,1)} %bitcast.75), channel_id=1, source_target_pairs={{0,4},{4,0},{8,12},{12,8},{16,20},{20,16},{24,28},{28,24},{1,5},{5... | collective-permute-start | bytes 1769480 | tf_op jit(solution)/shard_map/ppermute | solution.py:114
  290.2 39.0 %collective-permute-start.33 = (bf16[4,4,48,1536]{3,2,1,0:T(8,128)(2,1)}, bf16[4,4,48,1536]{3,2,1,0:T(8,128)(2,1)}, u32[]{:S(2)}, u32[]{:S(2)}) collective-permute-start(bf16[4,4,48,1536]{3,2,1,0:T(8,128)(2,1)} %bitcast.89), channel_id=1, source_target_pairs={{0,4},{4,0},{8,12},{12,8},{16,20},{20,16},{24,28},{28,24},{1,5},{5... | collective-permute-start | bytes 7077896 | tf_op jit(solution)/shard_map/ppermute | solution.py:114
  300.1 5.2 %collective-permute-start.27 = (bf16[4,48,384]{2,1,0:T(8,128)(2,1)S(1)}, bf16[4,48,384]{2,1,0:T(8,128)(2,1)S(1)}, u32[]{:S(2)}, u32[]{:S(2)}) collective-permute-start(bf16[4,48,384]{2,1,0:T(8,128)(2,1)S(1)} %fusion.79), channel_id=1, source_target_pairs={{0,8},{4,20},{8,0},{12,28},{16,24},{20,4},{24,16},{28,12},{1,9},{5... | collective-permute-start | bytes 442376 | tf_op jit(solution)/shard_map/ppermute | solution.py:120
  305.4 5.5 %collective-permute-start.28 = (bf16[4,48,384]{2,1,0:T(8,128)(2,1)S(1)}, bf16[4,48,384]{2,1,0:T(8,128)(2,1)S(1)}, u32[]{:S(2)}, u32[]{:S(2)}) collective-permute-start(bf16[4,48,384]{2,1,0:T(8,128)(2,1)S(1)} %get-tuple-element.119), channel_id=1, source_target_pairs={{0,8},{4,12},{8,0},{12,4},{16,24},{20,28},{24,16},{28,20},{1,9},{5... | collective-permute-start | bytes 442376 | tf_op jit(solution)/shard_map/ppermute | solution.py:127
  305.5 5.6 %collective-permute-start.29 = (bf16[4,48,384]{2,1,0:T(8,128)(2,1)S(1)}, bf16[4,48,384]{2,1,0:T(8,128)(2,1)S(1)}, u32[]{:S(2)}, u32[]{:S(2)}) collective-permute-start(bf16[4,48,384]{2,1,0:T(8,128)(2,1)S(1)} %get-tuple-element.120), channel_id=1, source_target_pairs={{0,16},{4,20},{8,24},{12,28},{16,0},{20,4},{24,8},{28,12},{1,17},{... | collective-permute-start | bytes 442376 | tf_op jit(solution)/shard_map/ppermute | solution.py:128
  308.3 25.1 %collective-permute-start.19 = (bf16[4,4,48,1280]{3,2,1,0:T(8,128)(2,1)S(1)}, bf16[4,4,48,1280]{3,2,1,0:T(8,128)(2,1)S(1)}, u32[]{:S(2)}, u32[]{:S(2)}) collective-permute-start(bf16[4,4,48,1280]{3,2,1,0:T(8,128)(2,1)S(1)} %bitcast.311), channel_id=1, source_target_pairs={{0,4},{4,0},{8,12},{12,8},{16,20},{20,16},{24,28},{28,24},{1,5},{5... | collective-permute-start | bytes 5898248 | tf_op jit(solution)/shard_map/ppermute | solution.py:114
  311.3 5.1 %collective-permute-start.32 = (bf16[48,384]{1,0:T(8,128)(2,1)S(1)}, bf16[48,384]{1,0:T(8,128)(2,1)S(1)}, u32[]{:S(2)}, u32[]{:S(2)}) collective-permute-start(bf16[48,384]{1,0:T(8,128)(2,1)S(1)} %get-tuple-element.141), channel_id=1, source_target_pairs={{0,3},{1,0},{2,1},{3,2},{4,7},{5,4},{6,5},{7,6},{8,11},{9,8},{10,9... | collective-permute-start | bytes 110600 | tf_op jit(solution)/shard_map/ppermute | solution.py:133
  315.2 28.8 %collective-permute-start.40 = (bf16[4,4,192,384]{3,2,1,0:T(8,128)(2,1)S(1)}, bf16[4,4,192,384]{3,2,1,0:T(8,128)(2,1)S(1)}, u32[]{:S(2)}, u32[]{:S(2)}) collective-permute-start(bf16[4,4,192,384]{3,2,1,0:T(8,128)(2,1)S(1)} %bitcast.302), channel_id=1, source_target_pairs={{0,4},{4,0},{8,12},{12,8},{16,20},{20,16},{24,28},{28,24},{1,5},{5... | collective-permute-start | bytes 7077896 | tf_op jit(solution)/shard_map/ppermute | solution.py:114
  331.7 9.9 %collective-permute-start.34 = (bf16[4,48,1536]{2,1,0:T(8,128)(2,1)S(1)}, bf16[4,48,1536]{2,1,0:T(8,128)(2,1)S(1)}, u32[]{:S(2)}, u32[]{:S(2)}) collective-permute-start(bf16[4,48,1536]{2,1,0:T(8,128)(2,1)S(1)} %fusion.57), channel_id=1, source_target_pairs={{0,8},{4,20},{8,0},{12,28},{16,24},{20,4},{24,16},{28,12},{1,9},{5... | collective-permute-start | bytes 1769480 | tf_op jit(solution)/shard_map/ppermute | solution.py:120
  333.9 30.4 %collective-permute-start.20 = (bf16[4,48,1280]{2,1,0:T(8,128)(2,1)S(1)}, bf16[4,48,1280]{2,1,0:T(8,128)(2,1)S(1)}, u32[]{:S(2)}, u32[]{:S(2)}) collective-permute-start(bf16[4,48,1280]{2,1,0:T(8,128)(2,1)S(1)} %fusion.59), channel_id=1, source_target_pairs={{0,8},{4,20},{8,0},{12,28},{16,24},{20,4},{24,16},{28,12},{1,9},{5... | collective-permute-start | bytes 1474568 | tf_op jit(solution)/shard_map/ppermute | solution.py:120
  341.9 17.6 %collective-permute-start.35 = (bf16[4,48,1536]{2,1,0:T(8,128)(2,1)S(1)}, bf16[4,48,1536]{2,1,0:T(8,128)(2,1)S(1)}, u32[]{:S(2)}, u32[]{:S(2)}) collective-permute-start(bf16[4,48,1536]{2,1,0:T(8,128)(2,1)S(1)} %get-tuple-element.107), channel_id=1, source_target_pairs={{0,8},{4,12},{8,0},{12,4},{16,24},{20,28},{24,16},{28,20},{1,9},{5... | collective-permute-start | bytes 1769480 | tf_op jit(solution)/shard_map/ppermute | solution.py:127
  343.6 16.2 %collective-permute-start.36 = (bf16[4,48,1536]{2,1,0:T(8,128)(2,1)S(1)}, bf16[4,48,1536]{2,1,0:T(8,128)(2,1)S(1)}, u32[]{:S(2)}, u32[]{:S(2)}) collective-permute-start(bf16[4,48,1536]{2,1,0:T(8,128)(2,1)S(1)} %get-tuple-element.108), channel_id=1, source_target_pairs={{0,16},{4,20},{8,24},{12,28},{16,0},{20,4},{24,8},{28,12},{1,17},{... | collective-permute-start | bytes 1769480 | tf_op jit(solution)/shard_map/ppermute | solution.py:128
  344.6 30.0 %collective-permute-start.41 = (bf16[4,192,384]{2,1,0:T(8,128)(2,1)S(1)}, bf16[4,192,384]{2,1,0:T(8,128)(2,1)S(1)}, u32[]{:S(2)}, u32[]{:S(2)}) collective-permute-start(bf16[4,192,384]{2,1,0:T(8,128)(2,1)S(1)} %fusion.58), channel_id=1, source_target_pairs={{0,8},{4,20},{8,0},{12,28},{16,24},{20,4},{24,16},{28,12},{1,9},{5... | collective-permute-start | bytes 1769480 | tf_op jit(solution)/shard_map/ppermute | solution.py:120
  360.1 5.4 %collective-permute-start.37 = (bf16[48,1536]{1,0:T(8,128)(2,1)S(1)}, bf16[48,1536]{1,0:T(8,128)(2,1)S(1)}, u32[]{:S(2)}, u32[]{:S(2)}) collective-permute-start(bf16[48,1536]{1,0:T(8,128)(2,1)S(1)} %get-tuple-element.128), channel_id=1, source_target_pairs={{0,1},{1,2},{2,3},{3,0},{4,5},{5,6},{6,7},{7,4},{8,9},{9,10},{10,1... | collective-permute-start | bytes 442376 | tf_op jit(solution)/shard_map/ppermute | solution.py:133
  360.9 10.6 %collective-permute-start.39 = (bf16[48,1536]{1,0:T(8,128)(2,1)S(1)}, bf16[48,1536]{1,0:T(8,128)(2,1)S(1)}, u32[]{:S(2)}, u32[]{:S(2)}) collective-permute-start(bf16[48,1536]{1,0:T(8,128)(2,1)S(1)} %get-tuple-element.129), channel_id=1, source_target_pairs={{0,3},{1,0},{2,1},{3,2},{4,7},{5,4},{6,5},{7,6},{8,11},{9,8},{10,9... | collective-permute-start | bytes 442376 | tf_op jit(solution)/shard_map/ppermute | solution.py:133
  362.2 11.7 %collective-permute-start.38 = (bf16[48,1536]{1,0:T(8,128)(2,1)S(1)}, bf16[48,1536]{1,0:T(8,128)(2,1)S(1)}, u32[]{:S(2)}, u32[]{:S(2)}) collective-permute-start(bf16[48,1536]{1,0:T(8,128)(2,1)S(1)} %get-tuple-element.130), channel_id=1, source_target_pairs={{0,2},{1,3},{2,0},{3,1},{4,6},{5,7},{6,4},{7,5},{8,10},{9,11},{10,... | collective-permute-start | bytes 442376 | tf_op jit(solution)/shard_map/ppermute | solution.py:133
  364.5 14.2 %collective-permute-start.21 = (bf16[4,48,1280]{2,1,0:T(8,128)(2,1)S(1)}, bf16[4,48,1280]{2,1,0:T(8,128)(2,1)S(1)}, u32[]{:S(2)}, u32[]{:S(2)}) collective-permute-start(bf16[4,48,1280]{2,1,0:T(8,128)(2,1)S(1)} %get-tuple-element.115), channel_id=1, source_target_pairs={{0,8},{4,12},{8,0},{12,4},{16,24},{20,28},{24,16},{28,20},{1,9},{5... | collective-permute-start | bytes 1474568 | tf_op jit(solution)/shard_map/ppermute | solution.py:127
  365.5 13.3 %collective-permute-start.22 = (bf16[4,48,1280]{2,1,0:T(8,128)(2,1)S(1)}, bf16[4,48,1280]{2,1,0:T(8,128)(2,1)S(1)}, u32[]{:S(2)}, u32[]{:S(2)}) collective-permute-start(bf16[4,48,1280]{2,1,0:T(8,128)(2,1)S(1)} %get-tuple-element.116), channel_id=1, source_target_pairs={{0,16},{4,20},{8,24},{12,28},{16,0},{20,4},{24,8},{28,12},{1,17},{... | collective-permute-start | bytes 1474568 | tf_op jit(solution)/shard_map/ppermute | solution.py:128
  374.6 60.7 %all-gather.21.cloned.1.call-start = ((), (), s32[]{:S(2)}) async-start(), calls=%async_computation.4 | async-start | bytes 1327104 | tf_op jit(solution)/shard_map/all_gather | solution.py:136
  376.6 15.5 %collective-permute-start.42 = (bf16[4,192,384]{2,1,0:T(8,128)(2,1)S(1)}, bf16[4,192,384]{2,1,0:T(8,128)(2,1)S(1)}, u32[]{:S(2)}, u32[]{:S(2)}) collective-permute-start(bf16[4,192,384]{2,1,0:T(8,128)(2,1)S(1)} %get-tuple-element.105), channel_id=1, source_target_pairs={{0,8},{4,12},{8,0},{12,4},{16,24},{20,28},{24,16},{28,20},{1,9},{5... | collective-permute-start | bytes 1769480 | tf_op jit(solution)/shard_map/ppermute | solution.py:127
  376.8 15.4 %collective-permute-start.43 = (bf16[4,192,384]{2,1,0:T(8,128)(2,1)S(1)}, bf16[4,192,384]{2,1,0:T(8,128)(2,1)S(1)}, u32[]{:S(2)}, u32[]{:S(2)}) collective-permute-start(bf16[4,192,384]{2,1,0:T(8,128)(2,1)S(1)} %get-tuple-element.106), channel_id=1, source_target_pairs={{0,16},{4,20},{8,24},{12,28},{16,0},{20,4},{24,8},{28,12},{1,17},{... | collective-permute-start | bytes 1769480 | tf_op jit(solution)/shard_map/ppermute | solution.py:128
  380.1 18.9 %collective-permute-start.23 = (bf16[48,1280]{1,0:T(8,128)(2,1)S(1)}, bf16[48,1280]{1,0:T(8,128)(2,1)S(1)}, u32[]{:S(2)}, u32[]{:S(2)}) collective-permute-start(bf16[48,1280]{1,0:T(8,128)(2,1)S(1)} %get-tuple-element.135), channel_id=1, source_target_pairs={{0,1},{1,2},{2,3},{3,0},{4,5},{5,6},{6,7},{7,4},{8,9},{9,10},{10,1... | collective-permute-start | bytes 368648 | tf_op jit(solution)/shard_map/ppermute | solution.py:133
  384.9 16.4 %collective-permute-start.25 = (bf16[48,1280]{1,0:T(8,128)(2,1)S(1)}, bf16[48,1280]{1,0:T(8,128)(2,1)S(1)}, u32[]{:S(2)}, u32[]{:S(2)}) collective-permute-start(bf16[48,1280]{1,0:T(8,128)(2,1)S(1)} %get-tuple-element.136), channel_id=1, source_target_pairs={{0,3},{1,0},{2,1},{3,2},{4,7},{5,4},{6,5},{7,6},{8,11},{9,8},{10,9... | collective-permute-start | bytes 368648 | tf_op jit(solution)/shard_map/ppermute | solution.py:133
  384.9 16.4 %collective-permute-start.24 = (bf16[48,1280]{1,0:T(8,128)(2,1)S(1)}, bf16[48,1280]{1,0:T(8,128)(2,1)S(1)}, u32[]{:S(2)}, u32[]{:S(2)}) collective-permute-start(bf16[48,1280]{1,0:T(8,128)(2,1)S(1)} %get-tuple-element.137), channel_id=1, source_target_pairs={{0,2},{1,3},{2,0},{3,1},{4,6},{5,7},{6,4},{7,5},{8,10},{9,11},{10,... | collective-permute-start | bytes 368648 | tf_op jit(solution)/shard_map/ppermute | solution.py:133
  393.7 9.3 %collective-permute-start.44 = (bf16[192,384]{1,0:T(8,128)(2,1)S(1)}, bf16[192,384]{1,0:T(8,128)(2,1)S(1)}, u32[]{:S(2)}, u32[]{:S(2)}) collective-permute-start(bf16[192,384]{1,0:T(8,128)(2,1)S(1)} %get-tuple-element.123), channel_id=1, source_target_pairs={{0,1},{1,2},{2,3},{3,0},{4,5},{5,6},{6,7},{7,4},{8,9},{9,10},{10,1... | collective-permute-start | bytes 442376 | tf_op jit(solution)/shard_map/ppermute | solution.py:133
  397.3 10.7 %collective-permute-start.46 = (bf16[192,384]{1,0:T(8,128)(2,1)S(1)}, bf16[192,384]{1,0:T(8,128)(2,1)S(1)}, u32[]{:S(2)}, u32[]{:S(2)}) collective-permute-start(bf16[192,384]{1,0:T(8,128)(2,1)S(1)} %get-tuple-element.124), channel_id=1, source_target_pairs={{0,3},{1,0},{2,1},{3,2},{4,7},{5,4},{6,5},{7,6},{8,11},{9,8},{10,9... | collective-permute-start | bytes 442376 | tf_op jit(solution)/shard_map/ppermute | solution.py:133
  399.0 10.6 %collective-permute-start.45 = (bf16[192,384]{1,0:T(8,128)(2,1)S(1)}, bf16[192,384]{1,0:T(8,128)(2,1)S(1)}, u32[]{:S(2)}, u32[]{:S(2)}) collective-permute-start(bf16[192,384]{1,0:T(8,128)(2,1)S(1)} %get-tuple-element.125), channel_id=1, source_target_pairs={{0,2},{1,3},{2,0},{3,1},{4,6},{5,7},{6,4},{7,5},{8,10},{9,11},{10,... | collective-permute-start | bytes 442376 | tf_op jit(solution)/shard_map/ppermute | solution.py:133
  (88 other events, 813.3 us)
Sparse Core Ops, SparseCore 0:
  16.0 27.1 all-gather.12
  45.7 46.4 all-gather.16
  94.7 37.4 all-gather.14
  374.7 25.8 all-gather.18
  410.5 24.8 all-gather.20

commit v17 on v16

--- a/solution.py
+++ b/solution.py
@@ -100,7 +100,7 @@
     return out
 
 
-def _reduce_matrix(g):
+def _reduce_matrix(g, hold=None):
     d = lax.axis_index("dp")
     f = lax.axis_index("fsdp")
     j, c = d // 2, d % 2
@@ -133,17 +133,20 @@
         total = total + lax.ppermute(
             part.astype(jnp.bfloat16), "fsdp", [(i, (i + k) % NF_FAST) for i in range(NF_FAST)]
         ).astype(jnp.float32)
-    x = lax.all_gather(total.astype(jnp.bfloat16), "dp", axis=0, tiled=False).astype(jnp.float32)
+    if hold is not None:
+        total, hold = lax.optimization_barrier((total, hold))
+    x = lax.all_gather(total, "dp", axis=0, tiled=False)
     x = x.reshape(n_chips, 2, rows, cols)
     x = jnp.concatenate([x[:, 0], x[:, 1]], axis=-1)
-    return x.reshape(n_chips * rows, 2 * cols)
-
-
-def fast_reduce(mats, gains):
+    shard = x.reshape(n_chips * rows, 2 * cols)
+    return shard if hold is None else (shard, hold)
+
+
+def fast_reduce(mats, gains, hold):
     stacked = jnp.concatenate(gains, axis=0)
     pad = 2 * LANES - stacked.shape[0]
     first = jnp.concatenate([mats[0], jnp.pad(stacked.T, ((0, 0), (0, pad)))], axis=1)
-    shard = _reduce_matrix(first)
+    shard, hold = _reduce_matrix(first, hold)
     width = mats[0].shape[1]
     out = [shard[:, :width]] + [_reduce_matrix(m) for m in mats[1:]]
     mine = shard[:, width : width + stacked.shape[0]].T
@@ -151,7 +154,7 @@
     for g in gains:
         out.append(mine[rows : rows + g.shape[0]])
         rows += g.shape[0]
-    return out
+    return out, hold
 
 
 def map_blocks(fn, members):
@@ -293,8 +296,8 @@
     grad_qk = jnp.stack([gain_q.reshape(model_width), gain_k.reshape(model_width)])
     summands = (grad_qkv, grad_outw, grad_up, grad_down, grad_gain, grad_bias, grad_qk)
     if fast:
-        late = fast_reduce(summands[:2], summands[4:])
-        shares = late[:2] + early + late[2:]
+        late, early = fast_reduce(summands[:2], summands[4:], early)
+        shares = late[:2] + list(early) + late[2:]
     else:
         pieces = [
             lax.psum_scatter(

time: 456 us -> 479 us (1.050)
  the two profiles are of different devices: /device:TPU:8 before, /device:TPU:0 now
where the time goes in v17:
time: 479 us; the launch traced here: 472 us
  waiting for transfers between devices  120 us (25%)
  matrix products  111 us (23%)
  local copies, waits for them, and re-layouts  85.7 us (18%)
  other arithmetic  65.9 us (14%)
  starting transfers between devices  62.9 us (13%)
  between operations  16 us (3%)
  blocking collectives  10.2 us (2%)
    ppermute x4, waiting for transfers between devices, _reduce_matrix(): lax.ppermute(to_x.astype(jnp.bfloat16), 'dp', [(i, i ^ 2) for i in range(...  36.8 us
    ppermute x15, starting transfers between devices, _z_gather(): lax.ppermute(piece, 'fsdp', [(i, (i + k) % NF_FAST) for i in range(NF_FAS...  29.8 us
    ppermute x12, waiting for transfers between devices, _reduce_matrix(): lax.ppermute(part.astype(jnp.bfloat16), 'fsdp', [(i, (i + k) % NF_FAST) f...  28.2 us
    ppermute x4, waiting for transfers between devices, _reduce_matrix(): lax.ppermute(of_chip(j ^ 3).astype(jnp.bfloat16), 'dp', [(i, i ^ 2) if i...  23.7 us
    dot_general x1, matrix products, layer(): up_pre = jnp.dot(second_low, full_up, preferred_element_type=jnp.float32)  22.2 us
    unnamed x180, local copies, waits for them, and re-layouts  21.6 us
    ppermute x12, starting transfers between devices, _reduce_matrix(): lax.ppermute(part.astype(jnp.bfloat16), 'fsdp', [(i, (i + k) % NF_FAST) f...  15.7 us
    slice x3, local copies, waits for them, and re-layouts, _gather_matrix(): x = jnp.concatenate([x[:, :, 0], x[:, :, 1]], axis=-1)  10.4 us
  transfers between devices with their start and end apart: 53, of which 27 were waited for; matrix products, arithmetic and copies ran while one was open for 40% of the time, Pallas kernels for 0%

profile of v17, /device:TPU:0, one launch (start us, length us, event | category | flops | bytes accessed | tf_op | source)
XLA Modules:
  0.0 472.1 jit_solution(12563591716987884824)
XLA Ops:
  8.1 4.1 collective-permute-start.11
  21.2 3.4 collective-permute-start.16
  26.0 6.7 %collective-permute-done.17 = bf16[192,384]{1,0:T(8,128)(2,1)S(1)} collective-permute-done((bf16[192,384]{1,0:T(8,128)(2,1)S(1)}, bf16[192,384]{1,0:T(8,128)(2,1)S(1)}, u32[]{:S(2)}, u32[]{:S(2)}) %collective-permute-start.17) | collective-permute-done | bytes 147488 | tf_op jit(solution)/shard_map/ppermute | solution.py:61
  34.9 2.7 collective-permute-start.1
  57.3 10.2 %collective-permute-done.6 = bf16[4,48,1152]{2,1,0:T(8,128)(2,1)S(1)} collective-permute-done((bf16[4,48,1152]{2,1,0:T(8,128)(2,1)S(1)}, bf16[4,48,1152]{2,1,0:T(8,128)(2,1)S(1)}, u32[]{:S(2)}, u32[]{:S(2)}) %collective-permute-start.6) | collective-permute-done | bytes 442400 | tf_op jit(solution)/shard_map/ppermute | solution.py:43
  77.6 9.1 %collective-permute-done.8 = bf16[4,48,1152]{2,1,0:T(8,128)(2,1)S(1)} collective-permute-done((bf16[4,48,1152]{2,1,0:T(8,128)(2,1)S(1)}, bf16[4,48,1152]{2,1,0:T(8,128)(2,1)S(1)}, u32[]{:S(2)}, u32[]{:S(2)}) %collective-permute-start.8) | collective-permute-done | bytes 442400 | tf_op jit(solution)/shard_map/ppermute | solution.py:46
  103.4 3.2 gather_fusion.2
  114.7 3.4 fusion.120
  126.1 8.2 %fusion.129 = (f32[12,576]{1,0:T(8,128)S(1)}, f32[12,576,576]{1,2,0:T(8,128)}) fusion(f32[576,12,64]{0,2,1:T(8,128)S(1)} %bitcast.253, f32[12,64]{1,0:T(8,128)S(1)} %mul.355, f32[576,12]{0,1:T(8,128)S(1)} %fusion.94, f32[576,12]{0,1:T(8,128)S(1)} %broadcast_multiply_fusion, f32[576,12,64]{0,2,1:T(8,128)S(1)} %bitcast.245, f32[12,64]{1,0:T(8,128)S(1)} %copy-done.51, ...), kind=kOutput, calls=%fused_computation.291 | convolution fusion | flops 525083904 | bytes 19940352 | tf_op jit(solution)/shard_map/while/body/eval_jaxpr/qhd,khd->hqk/dot_general | solution.py:213
  134.3 8.5 %fusion.3 = f32[12,576]{1,0:T(8,128)S(1)} fusion(f32[12,576,576]{1,2,0:T(8,128)} %get-tuple-element.158, f32[12,576]{1,0:T(8,128)S(1)} %get-tuple-element.157), kind=kLoop, calls=%fused_computation.15 | loop fusion | flops 7955712 | bytes 15980544 | tf_op jit(solution)/shard_map/while/body/eval_jaxpr/reduce_sum | solution.py:223
  142.8 9.7 %fusion.35 = bf16[12,64,576]{2,1,0:T(8,128)(2,1)S(1)} fusion(bf16[576,12,64]{0,2,1:T(8,128)(2,1)} %bitcast.282, f32[12,576,576]{1,2,0:T(8,128)} %get-tuple-element.158, f32[12,576]{1,0:T(8,128)S(1)} %fusion.3, f32[12,576]{1,0:T(8,128)S(1)} %get-tuple-element.157), kind=kOutput, calls=%fused_computation.108 | convolution fusion | flops 521994240 | bytes 17750016 | tf_op jit(solution)/shard_map/while/body/eval_jaxpr/hqk,khd->qhd/dot_general | solution.py:225
  155.2 5.1 %fusion.121 = (bf16[4,4,1,192,384]{4,3,2,1,0:T(8,128)(2,1)}, bf16[4,4,1,192,384]{4,3,2,1,0:T(8,128)(2,1)}) fusion(bf16[4,4,2,192,384]{4,3,2,1,0:T(8,128)(2,1)} %bitcast.269), kind=kLoop, calls=%fused_computation.283 | loop fusion | bytes 9437184 | tf_op jit(solution)/shard_map/slice | solution.py:75
  160.3 3.0 fusion.122
  163.3 22.2 %multiply_convert_fusion = (bf16[576,3072]{1,0:T(8,128)(2,1)}, f32[576,3072]{1,0:T(8,128)}, f32[576,3072]{1,0:T(8,128)}) fusion(bf16[768,1536]{1,0:T(8,128)(2,1)S(1)} %bitcast.295, bf16[768,1536]{1,0:T(8,128)(2,1)S(1)} %bitcast.293, f32[576,768]{1,0:T(8,128)S(1)} %copy-done.11, f32[768]{0:T(1024)S(1)} %add.403, f32[768]{0:T(1024)S(1)} %mul.363, ...), kind=kOutput, calls=%fused_computation.25 | convolution fusion | flops 2844573696 | bytes 24193536 | tf_op jit(solution)/shard_map/dot_general | solution.py:235
  185.6 8.1 %add_convert_fusion = bf16[576,3072]{1,0:T(8,128)(2,1)S(1)} fusion(f32[576,3072]{1,0:T(8,128)} %get-tuple-element.110, f32[576,3072]{1,0:T(8,128)} %get-tuple-element.161, bf16[3072,384]{1,0:T(8,128)(2,1)S(1)} %bitcast.292, bf16[3072,384]{1,0:T(8,128)(2,1)S(1)} %bitcast.289, bf16[576,768]{1,0:T(8,128)(2,1)S(1)} %copy-done.25, f32[576]{0:T(1024)S(1)} %copy-done.57), kind=kOutput, calls=%fused_computation.24 | convolution fusion | flops 2753445888 | bytes 23300352 | tf_op jit(solution)/shard_map/dot_general | solution.py:244
  193.7 3.3 multiply_reduce_fusion.2
  196.9 6.8 %fusion.116 = f32[768,3072]{1,0:T(8,128)} fusion(bf16[576,3072]{1,0:T(8,128)(2,1)S(1)} %add_convert_fusion, f32[576,768]{1,0:T(8,128)S(1)} %copy-done.11, f32[768]{0:T(1024)S(1)} %add.403, f32[768]{0:T(1024)S(1)} %mul.363, f32[576]{0:T(1024)S(1)} %fusion.97, f32[576]{0:T(1024)S(1)} %broadcast_multiply_fusion.4), kind=kOutput, calls=%fused_computation.279 | convolution fusion | flops 2720120832 | bytes 14756352 | tf_op jit(solution)/shard_map/dot_general | solution.py:247
  211.0 4.2 dynamic-slice_convert_fusion.1
  215.7 4.0 fusion.60
  219.8 3.7 copy-done.21
  225.1 7.5 %convolution_convert_fusion = bf16[12,576,576]{1,2,0:T(8,128)(2,1)} fusion(bf16[576,12,64]{0,2,1:T(8,128)(2,1)S(1)} %bitcast.265, bf16[576,12,64]{0,2,1:T(8,128)(2,1)} %bitcast.283), kind=kOutput, calls=%fused_computation.39 | convolution fusion | flops 513589248 | bytes 9732096 | tf_op jit(solution)/shard_map/qhd,khd->hqk/dot_general | solution.py:264
  232.7 6.7 %fusion = f32[12,576]{1,0:T(8,128)S(1)} fusion(bf16[12,576,576]{1,2,0:T(8,128)(2,1)} %convolution_convert_fusion, f32[12,576,576]{1,2,0:T(8,128)S(1)} %bitcast.242, f32[12,576]{1,0:T(8,128)S(1)} %log_add_fusion), kind=kLoop, calls=%fused_computation.8 | loop fusion | flops 15918336 | bytes 23943168 | tf_op jit(solution)/shard_map/reduce_sum | solution.py:266
  239.4 6.4 %fusion.2 = bf16[12,576,576]{1,2,0:T(8,128)(2,1)} fusion(bf16[12,576,576]{1,2,0:T(8,128)(2,1)S(1)} %copy-done.3, f32[12,576,576]{1,2,0:T(8,128)S(1)} %bitcast.242, f32[12,576]{1,0:T(8,128)S(1)} %fusion, f32[12,576]{1,0:T(8,128)S(1)} %log_add_fusion), kind=kLoop, calls=%fused_computation.10 | loop fusion | flops 19906560 | bytes 31905792 | tf_op jit(solution)/shard_map/convert_element_type | solution.py:267
  245.9 6.9 %fusion.27 = (f32[576,12]{0,1:T(8,128)S(1)}, f32[12,64,576]{2,1,0:T(8,128)S(1)}) fusion(f32[576,12,64]{0,2,1:T(8,128)} %bitcast.252, f32[12,64]{1,0:T(8,128)S(1)} %copy-done.49, f32[576,12]{0,1:T(8,128)S(1)} %broadcast_multiply_fusion, bf16[12,576,576]{1,2,0:T(8,128)(2,1)} %fusion.2, f32[576,12,64]{0,2,1:T(8,128)S(1)} %bitcast.246, ...), kind=kOutput, calls=%fused_computation.75 | convolution fusion | flops 513139968 | bytes 13387776 | tf_op jit(solution)/shard_map/hqk,qhd->khd/dot_general | solution.py:272
  259.9 8.7 %fusion.36 = bf16[12,64,576]{2,1,0:T(8,128)(2,1)S(1)} fusion(bf16[576,12,64]{0,2,1:T(8,128)(2,1)S(1)} %bitcast.266, f32[12,576,576]{1,2,0:T(8,128)} %get-tuple-element.158, f32[12,576]{1,0:T(8,128)S(1)} %log_add_fusion), kind=kOutput, calls=%fused_computation.109 | convolution fusion | flops 518012928 | bytes 17722368 | tf_op jit(solution)/shard_map/hqk,qhd->khd/dot_general | solution.py:263
  268.7 2.7 convert_add_fusion.1
  273.9 7.6 %collective-permute-done.27 = bf16[4,48,1536]{2,1,0:T(8,128)(2,1)S(1)} collective-permute-done((bf16[4,48,1536]{2,1,0:T(8,128)(2,1)S(1)}, bf16[4,48,1536]{2,1,0:T(8,128)(2,1)S(1)}, u32[]{:S(2)}, u32[]{:S(2)}) %collective-permute-start.27) | collective-permute-done | bytes 589856 | tf_op jit(solution)/shard_map/ppermute | solution.py:120
  283.1 3.0 fusion.117
  286.1 2.7 constant_dynamic-slice_fusion.1
  288.8 7.6 %collective-permute-done.28 = bf16[4,48,1536]{2,1,0:T(8,128)(2,1)S(1)} collective-permute-done((bf16[4,48,1536]{2,1,0:T(8,128)(2,1)S(1)}, bf16[4,48,1536]{2,1,0:T(8,128)(2,1)S(1)}, u32[]{:S(2)}, u32[]{:S(2)}) %collective-permute-start.28) | collective-permute-done | bytes 589856 | tf_op jit(solution)/shard_map/ppermute | solution.py:127
  300.7 4.8 %collective-permute-done.30 = bf16[48,1536]{1,0:T(8,128)(2,1)S(1)} collective-permute-done((bf16[48,1536]{1,0:T(8,128)(2,1)S(1)}, bf16[48,1536]{1,0:T(8,128)(2,1)S(1)}, u32[]{:S(2)}, u32[]{:S(2)}) %collective-permute-start.30) | collective-permute-done | bytes 147488 | tf_op jit(solution)/shard_map/ppermute | solution.py:133
  305.9 6.1 %collective-permute-done.31 = bf16[48,1536]{1,0:T(8,128)(2,1)S(1)} collective-permute-done((bf16[48,1536]{1,0:T(8,128)(2,1)S(1)}, bf16[48,1536]{1,0:T(8,128)(2,1)S(1)}, u32[]{:S(2)}, u32[]{:S(2)}) %collective-permute-start.31) | collective-permute-done | bytes 147488 | tf_op jit(solution)/shard_map/ppermute | solution.py:133
  314.2 8.1 %fusion.39 = f32[768,2304]{1,0:T(8,128)} fusion(bf16[576,768]{0,1:T(8,128)(2,1)} %bitcast.308, bf16[576,768]{0,1:T(8,128)(2,1)} %bitcast.304, bf16[576,768]{0,1:T(8,128)(2,1)} %bitcast.306, bf16[576,768]{1,0:T(8,128)(2,1)S(1)} %copy-done.16, f32[768]{0:T(1024)S(1)} %copy-done.64, f32[768]{0:T(1024)S(1)} %copy-done.61, f32[576]{0:T(1024)S(1)} %copy-done.59, ...), kind=kOutput, calls=%fused_computation.113 | convolution fusion | flops 2049048576 | bytes 10627584 | tf_op jit(solution)/shard_map/dot_general | solution.py:290
  326.0 4.2 select_maximum_fusion
  331.9 5.4 %collective-permute-done.34 = bf16[4,192,384]{2,1,0:T(8,128)(2,1)S(1)} collective-permute-done((bf16[4,192,384]{2,1,0:T(8,128)(2,1)S(1)}, bf16[4,192,384]{2,1,0:T(8,128)(2,1)S(1)}, u32[]{:S(2)}, u32[]{:S(2)}) %collective-permute-start.34) | collective-permute-done | bytes 589856 | tf_op jit(solution)/shard_map/ppermute | solution.py:120
  340.9 12.6 %collective-permute-done.35 = bf16[4,192,384]{2,1,0:T(8,128)(2,1)} collective-permute-done((bf16[4,192,384]{2,1,0:T(8,128)(2,1)}, bf16[4,192,384]{2,1,0:T(8,128)(2,1)}, u32[]{:S(2)}, u32[]{:S(2)}) %collective-permute-start.35) | collective-permute-done | bytes 589856 | tf_op jit(solution)/shard_map/ppermute | solution.py:127
  356.2 3.1 collective-permute-start.39
  359.3 4.3 constant_dynamic-slice_fusion.3
  364.5 6.4 %collective-permute-done.38 = bf16[192,384]{1,0:T(8,128)(2,1)S(1)} collective-permute-done((bf16[192,384]{1,0:T(8,128)(2,1)S(1)}, bf16[192,384]{1,0:T(8,128)(2,1)S(1)}, u32[]{:S(2)}, u32[]{:S(2)}) %collective-permute-start.38) | collective-permute-done | bytes 147488 | tf_op jit(solution)/shard_map/ppermute | solution.py:133
  375.8 10.6 %collective-permute-done.20 = bf16[4,48,1280]{2,1,0:T(8,128)(2,1)S(1)} collective-permute-done((bf16[4,48,1280]{2,1,0:T(8,128)(2,1)S(1)}, bf16[4,48,1280]{2,1,0:T(8,128)(2,1)S(1)}, u32[]{:S(2)}, u32[]{:S(2)}) %collective-permute-start.20) | collective-permute-done | bytes 491552 | tf_op jit(solution)/shard_map/ppermute | solution.py:120
  390.2 13.9 %collective-permute-done.21 = bf16[4,48,1280]{2,1,0:T(8,128)(2,1)S(1)} collective-permute-done((bf16[4,48,1280]{2,1,0:T(8,128)(2,1)S(1)}, bf16[4,48,1280]{2,1,0:T(8,128)(2,1)S(1)}, u32[]{:S(2)}, u32[]{:S(2)}) %collective-permute-start.21) | collective-permute-done | bytes 491552 | tf_op jit(solution)/shard_map/ppermute | solution.py:127
  405.5 3.8 collective-permute-start.25
  409.5 2.7 collective-permute-done.23
  412.2 3.9 collective-permute-done.24
  427.1 6.8 %multiply_convert_fusion.3 = bf16[576,768]{1,0:T(8,128)(2,1)} fusion(f32[576,768]{1,0:T(8,128)S(1)} %copy-done.12, bf16[576,3072]{1,0:T(8,128)(2,1)} %get-tuple-element.109, bf16[3072,384]{1,0:T(8,128)(2,1)} %bitcast.291, bf16[3072,384]{1,0:T(8,128)(2,1)S(1)} %bitcast.290, f32[576]{0:T(1024)S(1)} %copy-done.57), kind=kOutput, calls=%fused_computation.101 | convolution fusion | flops 2728673280 | bytes 10914048 | tf_op jit(solution)/shard_map/dot_general | solution.py:238
  440.1 3.8 collective-permute-start.46
  445.9 2.9 collective-permute-done.45
  448.8 10.2 %all-gather.6 = f32[384,384]{1,0:T(8,128)S(1)} all-gather(f32[48,384]{1,0:T(8,128)S(1)} %fusion.89), channel_id=8, replica_groups=mesh['dp'=8,'fsdp'=4] {'dp'}, dimensions={0}, use_global_device_ids=true | all-gather | bytes 663552 | tf_op jit(solution)/shard_map/all_gather | solution.py:138
  (408 shorter events, 152.6 us)
Async XLA Ops:
  7.2 88.1 %all-gather.14.cloned.1.call-start = ((), (), s32[]{:S(2)}) async-start(), calls=%async_computation | async-start | bytes 1327104 | tf_op jit(solution)/shard_map/all_gather | solution.py:73
  8.1 8.7 %collective-permute-start.11 = (bf16[48,384]{1,0:T(8,128)(2,1)S(1)}, bf16[48,384]{1,0:T(8,128)(2,1)S(1)}, u32[]{:S(2)}, u32[]{:S(2)}) collective-permute-start(bf16[48,384]{1,0:T(8,128)(2,1)S(1)} %dynamic_slice.151), channel_id=1, source_target_pairs={{0,2},{1,3},{2,0},{3,1},{4,6},{5,7},{6,4},{7,5},{8,10},{9,11},{10,... | collective-permute-start | bytes 110600 | tf_op jit(solution)/shard_map/ppermute | solution.py:61
  12.1 5.9 %collective-permute-start.10 = (bf16[48,384]{1,0:T(8,128)(2,1)S(1)}, bf16[48,384]{1,0:T(8,128)(2,1)S(1)}, u32[]{:S(2)}, u32[]{:S(2)}) collective-permute-start(bf16[48,384]{1,0:T(8,128)(2,1)S(1)} %dynamic_slice.151), channel_id=1, source_target_pairs={{0,1},{1,2},{2,3},{3,0},{4,5},{5,6},{6,7},{7,4},{8,9},{9,10},{10,1... | collective-permute-start | bytes 110600 | tf_op jit(solution)/shard_map/ppermute | solution.py:61
  19.4 135.8 %all-gather.18.cloned.1.call-start = ((), (), s32[]{:S(2)}) async-start(), calls=%async_computation.2 | async-start | bytes 5308416 | tf_op jit(solution)/shard_map/all_gather | solution.py:73
  20.4 12.3 %collective-permute-start.17 = (bf16[192,384]{1,0:T(8,128)(2,1)S(1)}, bf16[192,384]{1,0:T(8,128)(2,1)S(1)}, u32[]{:S(2)}, u32[]{:S(2)}) collective-permute-start(bf16[192,384]{1,0:T(8,128)(2,1)S(1)} %dynamic_slice.153), channel_id=1, source_target_pairs={{0,2},{1,3},{2,0},{3,1},{4,6},{5,7},{6,4},{7,5},{8,10},{9,11},{10,... | collective-permute-start | bytes 442376 | tf_op jit(solution)/shard_map/ppermute | solution.py:61
  21.2 11.4 %collective-permute-start.16 = (bf16[192,384]{1,0:T(8,128)(2,1)S(1)}, bf16[192,384]{1,0:T(8,128)(2,1)S(1)}, u32[]{:S(2)}, u32[]{:S(2)}) collective-permute-start(bf16[192,384]{1,0:T(8,128)(2,1)S(1)} %dynamic_slice.153), channel_id=1, source_target_pairs={{0,1},{1,2},{2,3},{3,0},{4,5},{5,6},{6,7},{7,4},{8,9},{9,10},{10,1... | collective-permute-start | bytes 442376 | tf_op jit(solution)/shard_map/ppermute | solution.py:61
  24.6 8.6 %collective-permute-start.18 = (bf16[192,384]{1,0:T(8,128)(2,1)S(1)}, bf16[192,384]{1,0:T(8,128)(2,1)S(1)}, u32[]{:S(2)}, u32[]{:S(2)}) collective-permute-start(bf16[192,384]{1,0:T(8,128)(2,1)S(1)} %dynamic_slice.153), channel_id=1, source_target_pairs={{0,3},{1,0},{2,1},{3,2},{4,7},{5,4},{6,5},{7,6},{8,11},{9,8},{10,9... | collective-permute-start | bytes 442376 | tf_op jit(solution)/shard_map/ppermute | solution.py:61
  34.8 125.5 %all-gather.16.cloned.1.call-start = ((), (), s32[]{:S(2)}) async-start(), calls=%async_computation.1 | async-start | bytes 5308416 | tf_op jit(solution)/shard_map/all_gather | solution.py:73
  34.9 38.3 %collective-permute-start.1 = (bf16[6,192]{1,0:T(8,128)(2,1)S(1)}, bf16[6,192]{1,0:T(8,128)(2,1)S(1)}, u32[]{:S(2)}, u32[]{:S(2)}) collective-permute-start(bf16[6,192]{1,0:T(8,128)(2,1)S(1)} %get-tuple-element.156), channel_id=1, source_target_pairs={{0,2},{1,3},{2,0},{3,1},{4,6},{5,7},{6,4},{7,5},{8,10},{9,11},{10,... | collective-permute-start | bytes 6920 | tf_op jit(solution)/shard_map/ppermute | solution.py:61
  37.6 37.0 %collective-permute-start = (bf16[6,192]{1,0:T(8,128)(2,1)S(1)}, bf16[6,192]{1,0:T(8,128)(2,1)S(1)}, u32[]{:S(2)}, u32[]{:S(2)}) collective-permute-start(bf16[6,192]{1,0:T(8,128)(2,1)S(1)} %get-tuple-element.156), channel_id=1, source_target_pairs={{0,1},{1,2},{2,3},{3,0},{4,5},{5,6},{6,7},{7,4},{8,9},{9,10},{10,1... | collective-permute-start | bytes 6920 | tf_op jit(solution)/shard_map/ppermute | solution.py:61
  38.5 11.6 %collective-permute-start.4 = (bf16[48,1152]{1,0:T(8,128)(2,1)S(1)}, bf16[48,1152]{1,0:T(8,128)(2,1)S(1)}, u32[]{:S(2)}, u32[]{:S(2)}) collective-permute-start(bf16[48,1152]{1,0:T(8,128)(2,1)S(1)} %dynamic_slice.150), channel_id=1, source_target_pairs={{0,2},{1,3},{2,0},{3,1},{4,6},{5,7},{6,4},{7,5},{8,10},{9,11},{10,... | collective-permute-start | bytes 331784 | tf_op jit(solution)/shard_map/ppermute | solution.py:61
  41.0 11.1 %collective-permute-start.3 = (bf16[48,1152]{1,0:T(8,128)(2,1)S(1)}, bf16[48,1152]{1,0:T(8,128)(2,1)S(1)}, u32[]{:S(2)}, u32[]{:S(2)}) collective-permute-start(bf16[48,1152]{1,0:T(8,128)(2,1)S(1)} %dynamic_slice.150), channel_id=1, source_target_pairs={{0,1},{1,2},{2,3},{3,0},{4,5},{5,6},{6,7},{7,4},{8,9},{9,10},{10,1... | collective-permute-start | bytes 331784 | tf_op jit(solution)/shard_map/ppermute | solution.py:61
  42.9 9.2 %collective-permute-start.5 = (bf16[48,1152]{1,0:T(8,128)(2,1)S(1)}, bf16[48,1152]{1,0:T(8,128)(2,1)S(1)}, u32[]{:S(2)}, u32[]{:S(2)}) collective-permute-start(bf16[48,1152]{1,0:T(8,128)(2,1)S(1)} %dynamic_slice.150), channel_id=1, source_target_pairs={{0,3},{1,0},{2,1},{3,2},{4,7},{5,4},{6,5},{7,6},{8,11},{9,8},{10,9... | collective-permute-start | bytes 331784 | tf_op jit(solution)/shard_map/ppermute | solution.py:61
  50.1 26.9 %collective-permute-start.2 = (bf16[6,192]{1,0:T(8,128)(2,1)S(1)}, bf16[6,192]{1,0:T(8,128)(2,1)S(1)}, u32[]{:S(2)}, u32[]{:S(2)}) collective-permute-start(bf16[6,192]{1,0:T(8,128)(2,1)S(1)} %get-tuple-element.156), channel_id=1, source_target_pairs={{0,3},{1,0},{2,1},{3,2},{4,7},{5,4},{6,5},{7,6},{8,11},{9,8},{10,9... | collective-permute-start | bytes 6920 | tf_op jit(solution)/shard_map/ppermute | solution.py:61
  52.8 14.7 %collective-permute-start.6 = (bf16[4,48,1152]{2,1,0:T(8,128)(2,1)S(1)}, bf16[4,48,1152]{2,1,0:T(8,128)(2,1)S(1)}, u32[]{:S(2)}, u32[]{:S(2)}) collective-permute-start(bf16[4,48,1152]{2,1,0:T(8,128)(2,1)S(1)} %gather_fusion.1), channel_id=1, source_target_pairs={{0,8},{4,12},{8,0},{12,4},{16,24},{20,28},{24,16},{28,20},{1,9},{5... | collective-permute-start | bytes 1327112 | tf_op jit(solution)/shard_map/ppermute | solution.py:43
  54.4 16.9 %collective-permute-start.7 = (bf16[4,48,1152]{2,1,0:T(8,128)(2,1)S(1)}, bf16[4,48,1152]{2,1,0:T(8,128)(2,1)S(1)}, u32[]{:S(2)}, u32[]{:S(2)}) collective-permute-start(bf16[4,48,1152]{2,1,0:T(8,128)(2,1)S(1)} %gather_fusion.1), channel_id=1, source_target_pairs={{0,16},{4,20},{8,24},{12,28},{16,0},{20,4},{24,8},{28,12},{1,17},{... | collective-permute-start | bytes 1327112 | tf_op jit(solution)/shard_map/ppermute | solution.py:44
  67.5 25.1 %collective-permute-start.14 = (bf16[48,1536]{1,0:T(8,128)(2,1)}, bf16[48,1536]{1,0:T(8,128)(2,1)S(1)}, u32[]{:S(2)}, u32[]{:S(2)}) collective-permute-start(bf16[48,1536]{1,0:T(8,128)(2,1)} %dynamic_slice.152), channel_id=1, source_target_pairs={{0,2},{1,3},{2,0},{3,1},{4,6},{5,7},{6,4},{7,5},{8,10},{9,11},{10,... | collective-permute-start | bytes 442376 | tf_op jit(solution)/shard_map/ppermute | solution.py:61
  71.3 15.3 %collective-permute-start.8 = (bf16[4,48,1152]{2,1,0:T(8,128)(2,1)S(1)}, bf16[4,48,1152]{2,1,0:T(8,128)(2,1)S(1)}, u32[]{:S(2)}, u32[]{:S(2)}) collective-permute-start(bf16[4,48,1152]{2,1,0:T(8,128)(2,1)S(1)} %broadcast_select_fusion), channel_id=1, source_target_pairs={{0,8},{4,20},{8,0},{12,28},{16,24},{20,4},{24,16},{28,12},{1,9},{5... | collective-permute-start | bytes 1327112 | tf_op jit(solution)/shard_map/ppermute | solution.py:46
  73.1 19.5 %collective-permute-start.13 = (bf16[48,1536]{1,0:T(8,128)(2,1)}, bf16[48,1536]{1,0:T(8,128)(2,1)}, u32[]{:S(2)}, u32[]{:S(2)}) collective-permute-start(bf16[48,1536]{1,0:T(8,128)(2,1)} %dynamic_slice.152), channel_id=1, source_target_pairs={{0,1},{1,2},{2,3},{3,0},{4,5},{5,6},{6,7},{7,4},{8,9},{9,10},{10,1... | collective-permute-start | bytes 442376 | tf_op jit(solution)/shard_map/ppermute | solution.py:61
  74.6 18.0 %collective-permute-start.15 = (bf16[48,1536]{1,0:T(8,128)(2,1)}, bf16[48,1536]{1,0:T(8,128)(2,1)}, u32[]{:S(2)}, u32[]{:S(2)}) collective-permute-start(bf16[48,1536]{1,0:T(8,128)(2,1)} %dynamic_slice.152), channel_id=1, source_target_pairs={{0,3},{1,0},{2,1},{3,2},{4,7},{5,4},{6,5},{7,6},{8,11},{9,8},{10,9... | collective-permute-start | bytes 442376 | tf_op jit(solution)/shard_map/ppermute | solution.py:61
  88.9 8.8 %collective-permute-start.9 = (bf16[4,4,48,1152]{3,2,1,0:T(8,128)(2,1)}, bf16[4,4,48,1152]{3,2,1,0:T(8,128)(2,1)S(1)}, u32[]{:S(2)}, u32[]{:S(2)}) collective-permute-start(bf16[4,4,48,1152]{3,2,1,0:T(8,128)(2,1)} %pad_maximum_fusion.12), channel_id=1, source_target_pairs={{0,4},{4,0},{8,12},{12,8},{16,20},{20,16},{24,28},{28,24},{1,5},{5... | collective-permute-start | bytes 5308424 | tf_op jit(solution)/shard_map/ppermute | solution.py:50
  95.3 321.7 %all-gather.20.cloned.1.call-start = ((), (), s32[]{:S(2)}) async-start(), calls=%async_computation.3 | async-start | bytes 2654208 | tf_op jit(solution)/shard_map/all_gather | solution.py:138
  215.1 53.6 %collective-permute-start.26 = (bf16[4,4,48,1536]{3,2,1,0:T(8,128)(2,1)}, bf16[4,4,48,1536]{3,2,1,0:T(8,128)(2,1)}, u32[]{:S(2)}, u32[]{:S(2)}) collective-permute-start(bf16[4,4,48,1536]{3,2,1,0:T(8,128)(2,1)} %bitcast.70), channel_id=1, source_target_pairs={{0,4},{4,0},{8,12},{12,8},{16,20},{20,16},{24,28},{28,24},{1,5},{5... | collective-permute-start | bytes 7077896 | tf_op jit(solution)/shard_map/ppermute | solution.py:114
  225.1 97.1 %collective-permute-start.33 = (bf16[4,4,192,384]{3,2,1,0:T(8,128)(2,1)}, bf16[4,4,192,384]{3,2,1,0:T(8,128)(2,1)}, u32[]{:S(2)}, u32[]{:S(2)}) collective-permute-start(bf16[4,4,192,384]{3,2,1,0:T(8,128)(2,1)} %bitcast.83), channel_id=1, source_target_pairs={{0,4},{4,0},{8,12},{12,8},{16,20},{20,16},{24,28},{28,24},{1,5},{5... | collective-permute-start | bytes 7077896 | tf_op jit(solution)/shard_map/ppermute | solution.py:114
  271.6 9.9 %collective-permute-start.27 = (bf16[4,48,1536]{2,1,0:T(8,128)(2,1)S(1)}, bf16[4,48,1536]{2,1,0:T(8,128)(2,1)S(1)}, u32[]{:S(2)}, u32[]{:S(2)}) collective-permute-start(bf16[4,48,1536]{2,1,0:T(8,128)(2,1)S(1)} %fusion.57), channel_id=1, source_target_pairs={{0,8},{4,20},{8,0},{12,28},{16,24},{20,4},{24,16},{28,12},{1,9},{5... | collective-permute-start | bytes 1769480 | tf_op jit(solution)/shard_map/ppermute | solution.py:120
  281.9 14.6 %collective-permute-start.28 = (bf16[4,48,1536]{2,1,0:T(8,128)(2,1)S(1)}, bf16[4,48,1536]{2,1,0:T(8,128)(2,1)S(1)}, u32[]{:S(2)}, u32[]{:S(2)}) collective-permute-start(bf16[4,48,1536]{2,1,0:T(8,128)(2,1)S(1)} %get-tuple-element.113), channel_id=1, source_target_pairs={{0,8},{4,12},{8,0},{12,4},{16,24},{20,28},{24,16},{28,20},{1,9},{5... | collective-permute-start | bytes 1769480 | tf_op jit(solution)/shard_map/ppermute | solution.py:127
  281.9 14.6 %collective-permute-start.29 = (bf16[4,48,1536]{2,1,0:T(8,128)(2,1)S(1)}, bf16[4,48,1536]{2,1,0:T(8,128)(2,1)S(1)}, u32[]{:S(2)}, u32[]{:S(2)}) collective-permute-start(bf16[4,48,1536]{2,1,0:T(8,128)(2,1)S(1)} %get-tuple-element.114), channel_id=1, source_target_pairs={{0,16},{4,20},{8,24},{12,28},{16,0},{20,4},{24,8},{28,12},{1,17},{... | collective-permute-start | bytes 1769480 | tf_op jit(solution)/shard_map/ppermute | solution.py:128
  296.8 8.7 %collective-permute-start.30 = (bf16[48,1536]{1,0:T(8,128)(2,1)S(1)}, bf16[48,1536]{1,0:T(8,128)(2,1)S(1)}, u32[]{:S(2)}, u32[]{:S(2)}) collective-permute-start(bf16[48,1536]{1,0:T(8,128)(2,1)S(1)} %get-tuple-element.136), channel_id=1, source_target_pairs={{0,1},{1,2},{2,3},{3,0},{4,5},{5,6},{6,7},{7,4},{8,9},{9,10},{10,1... | collective-permute-start | bytes 442376 | tf_op jit(solution)/shard_map/ppermute | solution.py:133
  298.5 7.4 %collective-permute-start.32 = (bf16[48,1536]{1,0:T(8,128)(2,1)S(1)}, bf16[48,1536]{1,0:T(8,128)(2,1)S(1)}, u32[]{:S(2)}, u32[]{:S(2)}) collective-permute-start(bf16[48,1536]{1,0:T(8,128)(2,1)S(1)} %get-tuple-element.137), channel_id=1, source_target_pairs={{0,3},{1,0},{2,1},{3,2},{4,7},{5,4},{6,5},{7,6},{8,11},{9,8},{10,9... | collective-permute-start | bytes 442376 | tf_op jit(solution)/shard_map/ppermute | solution.py:133
  300.7 11.3 %collective-permute-start.31 = (bf16[48,1536]{1,0:T(8,128)(2,1)S(1)}, bf16[48,1536]{1,0:T(8,128)(2,1)S(1)}, u32[]{:S(2)}, u32[]{:S(2)}) collective-permute-start(bf16[48,1536]{1,0:T(8,128)(2,1)S(1)} %get-tuple-element.138), channel_id=1, source_target_pairs={{0,2},{1,3},{2,0},{3,1},{4,6},{5,7},{6,4},{7,5},{8,10},{9,11},{10,... | collective-permute-start | bytes 442376 | tf_op jit(solution)/shard_map/ppermute | solution.py:133
  312.8 107.5 %all-gather.22.cloned.1.call-start = ((), (), s32[]{:S(2)}) async-start(), calls=%async_computation.4 | async-start | bytes 2654208 | tf_op jit(solution)/shard_map/all_gather | solution.py:138
  324.5 12.8 %collective-permute-start.34 = (bf16[4,192,384]{2,1,0:T(8,128)(2,1)S(1)}, bf16[4,192,384]{2,1,0:T(8,128)(2,1)S(1)}, u32[]{:S(2)}, u32[]{:S(2)}) collective-permute-start(bf16[4,192,384]{2,1,0:T(8,128)(2,1)S(1)} %fusion.58), channel_id=1, source_target_pairs={{0,8},{4,20},{8,0},{12,28},{16,24},{20,4},{24,16},{28,12},{1,9},{5... | collective-permute-start | bytes 1769480 | tf_op jit(solution)/shard_map/ppermute | solution.py:120
  331.9 39.8 %collective-permute-start.19 = (bf16[4,4,48,1280]{3,2,1,0:T(8,128)(2,1)}, bf16[4,4,48,1280]{3,2,1,0:T(8,128)(2,1)S(1)}, u32[]{:S(2)}, u32[]{:S(2)}) collective-permute-start(bf16[4,4,48,1280]{3,2,1,0:T(8,128)(2,1)} %bitcast.60), channel_id=1, source_target_pairs={{0,4},{4,0},{8,12},{12,8},{16,20},{20,16},{24,28},{28,24},{1,5},{5... | collective-permute-start | bytes 5898248 | tf_op jit(solution)/shard_map/ppermute | solution.py:114
  338.4 15.1 %collective-permute-start.35 = (bf16[4,192,384]{2,1,0:T(8,128)(2,1)}, bf16[4,192,384]{2,1,0:T(8,128)(2,1)}, u32[]{:S(2)}, u32[]{:S(2)}) collective-permute-start(bf16[4,192,384]{2,1,0:T(8,128)(2,1)} %get-tuple-element.111), channel_id=1, source_target_pairs={{0,8},{4,12},{8,0},{12,4},{16,24},{20,28},{24,16},{28,20},{1,9},{5... | collective-permute-start | bytes 1769480 | tf_op jit(solution)/shard_map/ppermute | solution.py:127
  340.9 12.6 %collective-permute-start.36 = (bf16[4,192,384]{2,1,0:T(8,128)(2,1)S(1)}, bf16[4,192,384]{2,1,0:T(8,128)(2,1)}, u32[]{:S(2)}, u32[]{:S(2)}) collective-permute-start(bf16[4,192,384]{2,1,0:T(8,128)(2,1)S(1)} %get-tuple-element.112), channel_id=1, source_target_pairs={{0,16},{4,20},{8,24},{12,28},{16,0},{20,4},{24,8},{28,12},{1,17},{... | collective-permute-start | bytes 1769480 | tf_op jit(solution)/shard_map/ppermute | solution.py:128
  355.4 8.7 %collective-permute-start.37 = (bf16[192,384]{1,0:T(8,128)(2,1)S(1)}, bf16[192,384]{1,0:T(8,128)(2,1)S(1)}, u32[]{:S(2)}, u32[]{:S(2)}) collective-permute-start(bf16[192,384]{1,0:T(8,128)(2,1)S(1)} %get-tuple-element.133), channel_id=1, source_target_pairs={{0,1},{1,2},{2,3},{3,0},{4,5},{5,6},{6,7},{7,4},{8,9},{9,10},{10,1... | collective-permute-start | bytes 442376 | tf_op jit(solution)/shard_map/ppermute | solution.py:133
  356.2 8.3 %collective-permute-start.39 = (bf16[192,384]{1,0:T(8,128)(2,1)S(1)}, bf16[192,384]{1,0:T(8,128)(2,1)S(1)}, u32[]{:S(2)}, u32[]{:S(2)}) collective-permute-start(bf16[192,384]{1,0:T(8,128)(2,1)S(1)} %get-tuple-element.134), channel_id=1, source_target_pairs={{0,3},{1,0},{2,1},{3,2},{4,7},{5,4},{6,5},{7,6},{8,11},{9,8},{10,9... | collective-permute-start | bytes 442376 | tf_op jit(solution)/shard_map/ppermute | solution.py:133
  359.3 11.6 %collective-permute-start.38 = (bf16[192,384]{1,0:T(8,128)(2,1)S(1)}, bf16[192,384]{1,0:T(8,128)(2,1)S(1)}, u32[]{:S(2)}, u32[]{:S(2)}) collective-permute-start(bf16[192,384]{1,0:T(8,128)(2,1)S(1)} %get-tuple-element.135), channel_id=1, source_target_pairs={{0,2},{1,3},{2,0},{3,1},{4,6},{5,7},{6,4},{7,5},{8,10},{9,11},{10,... | collective-permute-start | bytes 442376 | tf_op jit(solution)/shard_map/ppermute | solution.py:133
  371.7 88.2 %all-gather.24.cloned.1.call-start = ((), (), s32[]{:S(2)}) async-start(), calls=%async_computation.5 | async-start | bytes 2211840 | tf_op jit(solution)/shard_map/all_gather | solution.py:138
  374.4 12.1 %collective-permute-start.20 = (bf16[4,48,1280]{2,1,0:T(8,128)(2,1)S(1)}, bf16[4,48,1280]{2,1,0:T(8,128)(2,1)S(1)}, u32[]{:S(2)}, u32[]{:S(2)}) collective-permute-start(bf16[4,48,1280]{2,1,0:T(8,128)(2,1)S(1)} %fusion.59), channel_id=1, source_target_pairs={{0,8},{4,20},{8,0},{12,28},{16,24},{20,4},{24,16},{28,12},{1,9},{5... | collective-permute-start | bytes 1474568 | tf_op jit(solution)/shard_map/ppermute | solution.py:120
  386.7 17.5 %collective-permute-start.21 = (bf16[4,48,1280]{2,1,0:T(8,128)(2,1)S(1)}, bf16[4,48,1280]{2,1,0:T(8,128)(2,1)S(1)}, u32[]{:S(2)}, u32[]{:S(2)}) collective-permute-start(bf16[4,48,1280]{2,1,0:T(8,128)(2,1)S(1)} %get-tuple-element.121), channel_id=1, source_target_pairs={{0,8},{4,12},{8,0},{12,4},{16,24},{20,28},{24,16},{28,20},{1,9},{5... | collective-permute-start | bytes 1474568 | tf_op jit(solution)/shard_map/ppermute | solution.py:127
  388.3 16.7 %collective-permute-start.22 = (bf16[4,48,1280]{2,1,0:T(8,128)(2,1)S(1)}, bf16[4,48,1280]{2,1,0:T(8,128)(2,1)S(1)}, u32[]{:S(2)}, u32[]{:S(2)}) collective-permute-start(bf16[4,48,1280]{2,1,0:T(8,128)(2,1)S(1)} %get-tuple-element.122), channel_id=1, source_target_pairs={{0,16},{4,20},{8,24},{12,28},{16,0},{20,4},{24,8},{28,12},{1,17},{... | collective-permute-start | bytes 1474568 | tf_op jit(solution)/shard_map/ppermute | solution.py:128
  405.2 6.9 %collective-permute-start.23 = (bf16[48,1280]{1,0:T(8,128)(2,1)S(1)}, bf16[48,1280]{1,0:T(8,128)(2,1)S(1)}, u32[]{:S(2)}, u32[]{:S(2)}) collective-permute-start(bf16[48,1280]{1,0:T(8,128)(2,1)S(1)} %get-tuple-element.141), channel_id=1, source_target_pairs={{0,1},{1,2},{2,3},{3,0},{4,5},{5,6},{6,7},{7,4},{8,9},{9,10},{10,1... | collective-permute-start | bytes 368648 | tf_op jit(solution)/shard_map/ppermute | solution.py:133
  405.5 6.7 %collective-permute-start.25 = (bf16[48,1280]{1,0:T(8,128)(2,1)S(1)}, bf16[48,1280]{1,0:T(8,128)(2,1)S(1)}, u32[]{:S(2)}, u32[]{:S(2)}) collective-permute-start(bf16[48,1280]{1,0:T(8,128)(2,1)S(1)} %get-tuple-element.142), channel_id=1, source_target_pairs={{0,3},{1,0},{2,1},{3,2},{4,7},{5,4},{6,5},{7,6},{8,11},{9,8},{10,9... | collective-permute-start | bytes 368648 | tf_op jit(solution)/shard_map/ppermute | solution.py:133
  409.3 6.8 %collective-permute-start.24 = (bf16[48,1280]{1,0:T(8,128)(2,1)S(1)}, bf16[48,1280]{1,0:T(8,128)(2,1)S(1)}, u32[]{:S(2)}, u32[]{:S(2)}) collective-permute-start(bf16[48,1280]{1,0:T(8,128)(2,1)S(1)} %get-tuple-element.143), channel_id=1, source_target_pairs={{0,2},{1,3},{2,0},{3,1},{4,6},{5,7},{6,4},{7,5},{8,10},{9,11},{10,... | collective-permute-start | bytes 368648 | tf_op jit(solution)/shard_map/ppermute | solution.py:133
  409.4 15.8 %collective-permute-start.40 = (bf16[4,4,48,384]{3,2,1,0:T(8,128)(2,1)S(1)}, bf16[4,4,48,384]{3,2,1,0:T(8,128)(2,1)S(1)}, u32[]{:S(2)}, u32[]{:S(2)}) collective-permute-start(bf16[4,4,48,384]{3,2,1,0:T(8,128)(2,1)S(1)} %bitcast.309), channel_id=1, source_target_pairs={{0,4},{4,0},{8,12},{12,8},{16,20},{20,16},{24,28},{28,24},{1,5},{5... | collective-permute-start | bytes 1769480 | tf_op jit(solution)/shard_map/ppermute | solution.py:114
  425.4 8.5 %collective-permute-start.41 = (bf16[4,48,384]{2,1,0:T(8,128)(2,1)S(1)}, bf16[4,48,384]{2,1,0:T(8,128)(2,1)S(1)}, u32[]{:S(2)}, u32[]{:S(2)}) collective-permute-start(bf16[4,48,384]{2,1,0:T(8,128)(2,1)S(1)} %fusion.82), channel_id=1, source_target_pairs={{0,8},{4,20},{8,0},{12,28},{16,24},{20,4},{24,16},{28,12},{1,9},{5... | collective-permute-start | bytes 442376 | tf_op jit(solution)/shard_map/ppermute | solution.py:120
  440.0 5.8 %collective-permute-start.44 = (bf16[48,384]{1,0:T(8,128)(2,1)S(1)}, bf16[48,384]{1,0:T(8,128)(2,1)S(1)}, u32[]{:S(2)}, u32[]{:S(2)}) collective-permute-start(bf16[48,384]{1,0:T(8,128)(2,1)S(1)} %get-tuple-element.146), channel_id=1, source_target_pairs={{0,1},{1,2},{2,3},{3,0},{4,5},{5,6},{6,7},{7,4},{8,9},{9,10},{10,1... | collective-permute-start | bytes 110600 | tf_op jit(solution)/shard_map/ppermute | solution.py:133
  (90 other events, 870.5 us)
Sparse Core Ops, SparseCore 0:
  19.5 25.1 all-gather.13
  47.2 46.6 all-gather.17
  96.4 37.2 all-gather.15
  312.9 31.2 all-gather.19
  371.8 33.5 all-gather.21
  423.8 26.8 all-gather.23

commit v18 on v16

--- a/solution.py
+++ b/solution.py
@@ -89,7 +89,8 @@
 
 
 def fast_gather(mats, gains):
-    out = [_gather_matrix_pp(mats[0])] + [_gather_matrix(m) for m in mats[1:]]
+    out = [_gather_matrix_pp(mats[0])]
+    out += [_gather_matrix(m) for m in mats[1:]]
     stacked = jnp.concatenate(gains, axis=0)
     z = _z_gather(stacked)
     full = z.transpose(1, 0, 2).reshape(stacked.shape[0], NF_FAST * stacked.shape[1])
@@ -133,7 +134,7 @@
         total = total + lax.ppermute(
             part.astype(jnp.bfloat16), "fsdp", [(i, (i + k) % NF_FAST) for i in range(NF_FAST)]
         ).astype(jnp.float32)
-    x = lax.all_gather(total.astype(jnp.bfloat16), "dp", axis=0, tiled=False).astype(jnp.float32)
+    x = lax.all_gather(total, "dp", axis=0, tiled=False)
     x = x.reshape(n_chips, 2, rows, cols)
     x = jnp.concatenate([x[:, 0], x[:, 1]], axis=-1)
     return x.reshape(n_chips * rows, 2 * cols)

time: 456 us -> 484 us (1.061)
  the two profiles are of different devices: /device:TPU:8 before, /device:TPU:0 now
where the time goes in v18:
time: 484 us; the launch traced here: 476 us
  matrix products  113 us (23%)
  waiting for transfers between devices  109 us (23%)
  local copies, waits for them, and re-layouts  92.6 us (19%)
  other arithmetic  73.4 us (15%)
  starting transfers between devices  61.7 us (13%)
  between operations  15.9 us (3%)
  blocking collectives  9.94 us (2%)
    ppermute x4, waiting for transfers between devices, _reduce_matrix(): lax.ppermute(to_x.astype(jnp.bfloat16), 'dp', [(i, i ^ 2) for i in range(...  32.5 us
    unnamed x158, local copies, waits for them, and re-layouts  30.8 us
    ppermute x15, starting transfers between devices, _z_gather(): lax.ppermute(piece, 'fsdp', [(i, (i + k) % NF_FAST) for i in range(NF_FAS...  29.8 us
    ppermute x12, waiting for transfers between devices, _reduce_matrix(): lax.ppermute(part.astype(jnp.bfloat16), 'fsdp', [(i, (i + k) % NF_FAST) f...  27.7 us
    dot_general x1, matrix products, layer(): up_pre = jnp.dot(second_low, full_up, preferred_element_type=jnp.float32)  22.1 us
    ppermute x4, waiting for transfers between devices, _reduce_matrix(): lax.ppermute(of_chip(j ^ 3).astype(jnp.bfloat16), 'dp', [(i, i ^ 2) if i...  18.2 us
    ppermute x12, starting transfers between devices, _reduce_matrix(): lax.ppermute(part.astype(jnp.bfloat16), 'fsdp', [(i, (i + k) % NF_FAST) f...  15.8 us
    reduce_sum x1, other arithmetic, attend_back(): jnp.sum(probability * grad_p, axis=-1, keepdims=True)  12.9 us
  transfers between devices with their start and end apart: 53, of which 25 were waited for; matrix products, arithmetic and copies ran while one was open for 29% of the time, Pallas kernels for 0%

profile of v18, /device:TPU:0, one launch (start us, length us, event | category | flops | bytes accessed | tf_op | source)
XLA Modules:
  0.0 476.2 jit_solution(8652507965094845775)
XLA Ops:
  8.1 4.1 collective-permute-start.11
  21.2 3.4 collective-permute-start.16
  26.0 6.7 %collective-permute-done.17 = bf16[192,384]{1,0:T(8,128)(2,1)S(1)} collective-permute-done((bf16[192,384]{1,0:T(8,128)(2,1)S(1)}, bf16[192,384]{1,0:T(8,128)(2,1)S(1)}, u32[]{:S(2)}, u32[]{:S(2)}) %collective-permute-start.17) | collective-permute-done | bytes 147488 | tf_op jit(solution)/shard_map/ppermute | solution.py:61
  34.9 2.7 collective-permute-start.1
  57.7 9.8 %collective-permute-done.6 = bf16[4,48,1152]{2,1,0:T(8,128)(2,1)S(1)} collective-permute-done((bf16[4,48,1152]{2,1,0:T(8,128)(2,1)S(1)}, bf16[4,48,1152]{2,1,0:T(8,128)(2,1)S(1)}, u32[]{:S(2)}, u32[]{:S(2)}) %collective-permute-start.6) | collective-permute-done | bytes 442400 | tf_op jit(solution)/shard_map/ppermute | solution.py:43
  77.1 9.5 %collective-permute-done.8 = bf16[4,48,1152]{2,1,0:T(8,128)(2,1)S(1)} collective-permute-done((bf16[4,48,1152]{2,1,0:T(8,128)(2,1)S(1)}, bf16[4,48,1152]{2,1,0:T(8,128)(2,1)S(1)}, u32[]{:S(2)}, u32[]{:S(2)}) %collective-permute-start.8) | collective-permute-done | bytes 442400 | tf_op jit(solution)/shard_map/ppermute | solution.py:46
  103.4 3.2 gather_fusion.2
  115.1 3.4 fusion.120
  126.5 8.2 %fusion.129 = (f32[12,576]{1,0:T(8,128)S(1)}, f32[12,576,576]{1,2,0:T(8,128)}) fusion(f32[576,12,64]{0,2,1:T(8,128)S(1)} %bitcast.253, f32[12,64]{1,0:T(8,128)S(1)} %mul.355, f32[576,12]{0,1:T(8,128)S(1)} %fusion.94, f32[576,12]{0,1:T(8,128)S(1)} %broadcast_multiply_fusion, f32[576,12,64]{0,2,1:T(8,128)S(1)} %bitcast.245, f32[12,64]{1,0:T(8,128)S(1)} %copy-done.48, ...), kind=kOutput, calls=%fused_computation.291 | convolution fusion | flops 525083904 | bytes 19940352 | tf_op jit(solution)/shard_map/while/body/eval_jaxpr/qhd,khd->hqk/dot_general | solution.py:211
  134.7 8.5 %fusion.3 = f32[12,576]{1,0:T(8,128)S(1)} fusion(f32[12,576,576]{1,2,0:T(8,128)} %get-tuple-element.152, f32[12,576]{1,0:T(8,128)S(1)} %get-tuple-element.151), kind=kLoop, calls=%fused_computation.15 | loop fusion | flops 7955712 | bytes 15980544 | tf_op jit(solution)/shard_map/while/body/eval_jaxpr/reduce_sum | solution.py:221
  143.3 9.7 %fusion.35 = bf16[12,64,576]{2,1,0:T(8,128)(2,1)S(1)} fusion(bf16[576,12,64]{0,2,1:T(8,128)(2,1)} %bitcast.276, f32[12,576,576]{1,2,0:T(8,128)} %get-tuple-element.152, f32[12,576]{1,0:T(8,128)S(1)} %fusion.3, f32[12,576]{1,0:T(8,128)S(1)} %get-tuple-element.151), kind=kOutput, calls=%fused_computation.108 | convolution fusion | flops 521994240 | bytes 17750016 | tf_op jit(solution)/shard_map/while/body/eval_jaxpr/hqk,khd->qhd/dot_general | solution.py:223
  155.7 5.1 %fusion.121 = (bf16[4,4,1,192,384]{4,3,2,1,0:T(8,128)(2,1)}, bf16[4,4,1,192,384]{4,3,2,1,0:T(8,128)(2,1)}) fusion(bf16[4,4,2,192,384]{4,3,2,1,0:T(8,128)(2,1)} %bitcast.263), kind=kLoop, calls=%fused_computation.283 | loop fusion | bytes 9437184 | tf_op jit(solution)/shard_map/slice | solution.py:75
  160.8 3.0 fusion.122
  163.9 22.1 %multiply_convert_fusion = (bf16[576,3072]{1,0:T(8,128)(2,1)}, f32[576,3072]{1,0:T(8,128)}, f32[576,3072]{1,0:T(8,128)}) fusion(bf16[768,1536]{1,0:T(8,128)(2,1)S(1)} %bitcast.289, bf16[768,1536]{1,0:T(8,128)(2,1)S(1)} %bitcast.287, f32[576,768]{1,0:T(8,128)S(1)} %copy-done.9, f32[768]{0:T(1024)S(1)} %add.403, f32[768]{0:T(1024)S(1)} %mul.363, ...), kind=kOutput, calls=%fused_computation.25 | convolution fusion | flops 2844573696 | bytes 24193536 | tf_op jit(solution)/shard_map/dot_general | solution.py:233
  185.9 8.1 %add_convert_fusion = bf16[576,3072]{1,0:T(8,128)(2,1)S(1)} fusion(f32[576,3072]{1,0:T(8,128)} %get-tuple-element.104, f32[576,3072]{1,0:T(8,128)} %get-tuple-element.155, bf16[3072,384]{1,0:T(8,128)(2,1)S(1)} %bitcast.286, bf16[3072,384]{1,0:T(8,128)(2,1)S(1)} %bitcast.284, bf16[576,768]{1,0:T(8,128)(2,1)S(1)} %copy-done.27, f32[576]{0:T(1024)S(1)} %copy-done.54), kind=kOutput, calls=%fused_computation.24 | convolution fusion | flops 2753445888 | bytes 23300352 | tf_op jit(solution)/shard_map/dot_general | solution.py:242
  194.1 3.3 multiply_reduce_fusion.2
  204.6 7.6 %convolution_convert_fusion = bf16[12,576,576]{1,2,0:T(8,128)(2,1)} fusion(bf16[576,12,64]{0,2,1:T(8,128)(2,1)} %bitcast.261, bf16[576,12,64]{0,2,1:T(8,128)(2,1)} %bitcast.277), kind=kOutput, calls=%fused_computation.39 | convolution fusion | flops 513589248 | bytes 9732096 | tf_op jit(solution)/shard_map/qhd,khd->hqk/dot_general | solution.py:262
  212.2 9.9 %fusion.36 = bf16[12,64,576]{2,1,0:T(8,128)(2,1)} fusion(bf16[576,12,64]{0,2,1:T(8,128)(2,1)S(1)} %bitcast.262, f32[12,576,576]{1,2,0:T(8,128)} %get-tuple-element.152, f32[12,576]{1,0:T(8,128)S(1)} %log_add_fusion), kind=kOutput, calls=%fused_computation.109 | convolution fusion | flops 518012928 | bytes 17722368 | tf_op jit(solution)/shard_map/hqk,qhd->khd/dot_general | solution.py:261
  222.1 12.9 %fusion = f32[12,576]{1,0:T(8,128)S(1)} fusion(bf16[12,576,576]{1,2,0:T(8,128)(2,1)} %convolution_convert_fusion, f32[12,576,576]{1,2,0:T(8,128)} %get-tuple-element.152, f32[12,576]{1,0:T(8,128)S(1)} %log_add_fusion), kind=kLoop, calls=%fused_computation.8 | loop fusion | flops 15918336 | bytes 23943168 | tf_op jit(solution)/shard_map/reduce_sum | solution.py:264
  235.7 6.2 %fusion.2 = bf16[12,576,576]{1,2,0:T(8,128)(2,1)} fusion(bf16[12,576,576]{1,2,0:T(8,128)(2,1)S(1)} %copy-done.3, f32[12,576,576]{1,2,0:T(8,128)S(1)} %bitcast.242, f32[12,576]{1,0:T(8,128)S(1)} %fusion, f32[12,576]{1,0:T(8,128)S(1)} %log_add_fusion), kind=kLoop, calls=%fused_computation.10 | loop fusion | flops 19906560 | bytes 31905792 | tf_op jit(solution)/shard_map/convert_element_type | solution.py:265
  242.0 8.2 %fusion.27 = (f32[576,12]{0,1:T(8,128)S(1)}, f32[12,64,576]{2,1,0:T(8,128)}) fusion(f32[576,12,64]{0,2,1:T(8,128)} %bitcast.252, f32[12,64]{1,0:T(8,128)S(1)} %copy-done.46, f32[576,12]{0,1:T(8,128)S(1)} %broadcast_multiply_fusion, bf16[12,576,576]{1,2,0:T(8,128)(2,1)} %fusion.2, f32[576,12,64]{0,2,1:T(8,128)S(1)} %bitcast.246, ...), kind=kOutput, calls=%fused_computation.75 | convolution fusion | flops 513139968 | bytes 13387776 | tf_op jit(solution)/shard_map/hqk,qhd->khd/dot_general | solution.py:270
  258.1 2.8 fusion.117
  260.9 6.4 %fusion.39 = f32[768,2304]{1,0:T(8,128)} fusion(bf16[576,768]{0,1:T(8,128)(2,1)S(1)} %bitcast.302, bf16[576,768]{0,1:T(8,128)(2,1)S(1)} %bitcast.298, bf16[576,768]{0,1:T(8,128)(2,1)S(1)} %bitcast.300, bf16[576,768]{1,0:T(8,128)(2,1)S(1)} %copy-done.14, f32[768]{0:T(1024)S(1)} %copy-done.61, f32[768]{0:T(1024)S(1)} %copy-done.58, f32[576]{0:T(1024)S(1)} %copy-done.56, ...), kind=kOutput, calls=%fused_computation.113 | convolution fusion | flops 2049048576 | bytes 10627584 | tf_op jit(solution)/shard_map/dot_general | solution.py:288
  268.6 4.2 select_maximum_fusion
  272.8 3.2 copy-done.5
  278.1 6.1 %fusion.116 = f32[768,3072]{1,0:T(8,128)S(1)} fusion(bf16[576,3072]{1,0:T(8,128)(2,1)} %copy-done.24, f32[576,768]{1,0:T(8,128)S(1)} %copy-done.10, f32[768]{0:T(1024)S(1)} %add.403, f32[768]{0:T(1024)S(1)} %mul.363, f32[576]{0:T(1024)S(1)} %fusion.97, f32[576]{0:T(1024)S(1)} %broadcast_multiply_fusion.4), kind=kOutput, calls=%fused_computation.279 | convolution fusion | flops 2720120832 | bytes 14756352 | tf_op jit(solution)/shard_map/dot_general | solution.py:245
  284.2 3.7 copy-done.4
  296.7 2.8 constant_dynamic-slice_fusion.1
  299.5 6.0 %collective-permute-done.20 = bf16[4,48,1280]{2,1,0:T(8,128)(2,1)} collective-permute-done((bf16[4,48,1280]{2,1,0:T(8,128)(2,1)S(1)}, bf16[4,48,1280]{2,1,0:T(8,128)(2,1)}, u32[]{:S(2)}, u32[]{:S(2)}) %collective-permute-start.20) | collective-permute-done | bytes 491552 | tf_op jit(solution)/shard_map/ppermute | solution.py:121
  310.5 8.6 %collective-permute-done.21 = bf16[4,48,1280]{2,1,0:T(8,128)(2,1)S(1)} collective-permute-done((bf16[4,48,1280]{2,1,0:T(8,128)(2,1)S(1)}, bf16[4,48,1280]{2,1,0:T(8,128)(2,1)S(1)}, u32[]{:S(2)}, u32[]{:S(2)}) %collective-permute-start.21) | collective-permute-done | bytes 491552 | tf_op jit(solution)/shard_map/ppermute | solution.py:128
  327.6 5.0 %collective-permute-done.24 = bf16[48,1280]{1,0:T(8,128)(2,1)S(1)} collective-permute-done((bf16[48,1280]{1,0:T(8,128)(2,1)S(1)}, bf16[48,1280]{1,0:T(8,128)(2,1)S(1)}, u32[]{:S(2)}, u32[]{:S(2)}) %collective-permute-start.24) | collective-permute-done | bytes 122912 | tf_op jit(solution)/shard_map/ppermute | solution.py:134
  339.2 5.1 %fusion.60 = f32[3072,768]{1,0:T(8,128)S(1)} fusion(bf16[576,3072]{1,0:T(8,128)(2,1)S(1)} %copy-done.68, bf16[576,768]{1,0:T(8,128)(2,1)} %param.19, f32[576]{0:T(1024)S(1)} %copy-done.54), kind=kOutput, calls=%fused_computation.155 | convolution fusion | flops 2719236096 | bytes 13863168 | tf_op jit(solution)/shard_map/dot_general | solution.py:241
  344.3 3.7 copy-done.20
  349.6 3.3 collective-permute-done.35
  354.8 3.8 collective-permute-start.39
  358.6 4.4 collective-permute-done.37
  363.1 5.8 %collective-permute-done.38 = bf16[48,1536]{1,0:T(8,128)(2,1)S(1)} collective-permute-done((bf16[48,1536]{1,0:T(8,128)(2,1)S(1)}, bf16[48,1536]{1,0:T(8,128)(2,1)S(1)}, u32[]{:S(2)}, u32[]{:S(2)}) %collective-permute-start.38) | collective-permute-done | bytes 147488 | tf_op jit(solution)/shard_map/ppermute | solution.py:134
  369.7 2.6 constant_dynamic-slice_fusion
  375.9 11.6 %collective-permute-done.41 = bf16[4,192,384]{2,1,0:T(8,128)(2,1)S(1)} collective-permute-done((bf16[4,192,384]{2,1,0:T(8,128)(2,1)S(1)}, bf16[4,192,384]{2,1,0:T(8,128)(2,1)S(1)}, u32[]{:S(2)}, u32[]{:S(2)}) %collective-permute-start.41) | collective-permute-done | bytes 589856 | tf_op jit(solution)/shard_map/ppermute | solution.py:121
  391.1 15.6 %collective-permute-done.42 = bf16[4,192,384]{2,1,0:T(8,128)(2,1)S(1)} collective-permute-done((bf16[4,192,384]{2,1,0:T(8,128)(2,1)S(1)}, bf16[4,192,384]{2,1,0:T(8,128)(2,1)S(1)}, u32[]{:S(2)}, u32[]{:S(2)}) %collective-permute-start.42) | collective-permute-done | bytes 589856 | tf_op jit(solution)/shard_map/ppermute | solution.py:128
  408.1 3.8 collective-permute-start.46
  413.9 2.9 collective-permute-done.44
  416.7 4.8 %collective-permute-done.45 = bf16[192,384]{1,0:T(8,128)(2,1)S(1)} collective-permute-done((bf16[192,384]{1,0:T(8,128)(2,1)S(1)}, bf16[192,384]{1,0:T(8,128)(2,1)S(1)}, u32[]{:S(2)}, u32[]{:S(2)}) %collective-permute-start.45) | collective-permute-done | bytes 147488 | tf_op jit(solution)/shard_map/ppermute | solution.py:134
  422.4 7.4 %multiply_convert_fusion.3 = bf16[576,768]{1,0:T(8,128)(2,1)} fusion(f32[576,768]{1,0:T(8,128)S(1)} %copy-done.10, bf16[576,3072]{1,0:T(8,128)(2,1)} %get-tuple-element.103, bf16[3072,384]{1,0:T(8,128)(2,1)} %bitcast.285, bf16[3072,384]{1,0:T(8,128)(2,1)} %bitcast.283, f32[576]{0:T(1024)S(1)} %copy-done.54), kind=kOutput, calls=%fused_computation.101 | convolution fusion | flops 2728673280 | bytes 10914048 | tf_op jit(solution)/shard_map/dot_general | solution.py:236
  432.0 5.0 %collective-permute-done.28 = bf16[4,48,384]{2,1,0:T(8,128)(2,1)S(1)} collective-permute-done((bf16[4,48,384]{2,1,0:T(8,128)(2,1)S(1)}, bf16[4,48,384]{2,1,0:T(8,128)(2,1)S(1)}, u32[]{:S(2)}, u32[]{:S(2)}) %collective-permute-start.28) | collective-permute-done | bytes 147488 | tf_op jit(solution)/shard_map/ppermute | solution.py:128
  437.3 4.0 collective-permute-start.32
  443.2 3.0 collective-permute-done.31
  446.2 9.9 %all-gather.4 = f32[384,384]{1,0:T(8,128)S(1)} all-gather(f32[48,384]{1,0:T(8,128)S(1)} %fusion.89), channel_id=6, replica_groups=mesh['dp'=8,'fsdp'=4] {'dp'}, dimensions={0}, use_global_device_ids=true | all-gather | bytes 663552 | tf_op jit(solution)/shard_map/all_gather | solution.py:137
  (383 shorter events, 158.8 us)
Async XLA Ops:
  7.2 88.1 %all-gather.14.cloned.1.call-start = ((), (), s32[]{:S(2)}) async-start(), calls=%async_computation | async-start | bytes 1327104 | tf_op jit(solution)/shard_map/all_gather | solution.py:73
  8.1 8.7 %collective-permute-start.11 = (bf16[48,384]{1,0:T(8,128)(2,1)S(1)}, bf16[48,384]{1,0:T(8,128)(2,1)S(1)}, u32[]{:S(2)}, u32[]{:S(2)}) collective-permute-start(bf16[48,384]{1,0:T(8,128)(2,1)S(1)} %dynamic_slice.151), channel_id=1, source_target_pairs={{0,2},{1,3},{2,0},{3,1},{4,6},{5,7},{6,4},{7,5},{8,10},{9,11},{10,... | collective-permute-start | bytes 110600 | tf_op jit(solution)/shard_map/ppermute | solution.py:61
  19.4 136.3 %all-gather.18.cloned.1.call-start = ((), (), s32[]{:S(2)}) async-start(), calls=%async_computation.2 | async-start | bytes 5308416 | tf_op jit(solution)/shard_map/all_gather | solution.py:73
  20.4 12.3 %collective-permute-start.17 = (bf16[192,384]{1,0:T(8,128)(2,1)S(1)}, bf16[192,384]{1,0:T(8,128)(2,1)S(1)}, u32[]{:S(2)}, u32[]{:S(2)}) collective-permute-start(bf16[192,384]{1,0:T(8,128)(2,1)S(1)} %dynamic_slice.153), channel_id=1, source_target_pairs={{0,2},{1,3},{2,0},{3,1},{4,6},{5,7},{6,4},{7,5},{8,10},{9,11},{10,... | collective-permute-start | bytes 442376 | tf_op jit(solution)/shard_map/ppermute | solution.py:61
  21.2 11.4 %collective-permute-start.16 = (bf16[192,384]{1,0:T(8,128)(2,1)S(1)}, bf16[192,384]{1,0:T(8,128)(2,1)S(1)}, u32[]{:S(2)}, u32[]{:S(2)}) collective-permute-start(bf16[192,384]{1,0:T(8,128)(2,1)S(1)} %dynamic_slice.153), channel_id=1, source_target_pairs={{0,1},{1,2},{2,3},{3,0},{4,5},{5,6},{6,7},{7,4},{8,9},{9,10},{10,1... | collective-permute-start | bytes 442376 | tf_op jit(solution)/shard_map/ppermute | solution.py:61
  24.6 8.6 %collective-permute-start.18 = (bf16[192,384]{1,0:T(8,128)(2,1)S(1)}, bf16[192,384]{1,0:T(8,128)(2,1)S(1)}, u32[]{:S(2)}, u32[]{:S(2)}) collective-permute-start(bf16[192,384]{1,0:T(8,128)(2,1)S(1)} %dynamic_slice.153), channel_id=1, source_target_pairs={{0,3},{1,0},{2,1},{3,2},{4,7},{5,4},{6,5},{7,6},{8,11},{9,8},{10,9... | collective-permute-start | bytes 442376 | tf_op jit(solution)/shard_map/ppermute | solution.py:61
  34.8 126.0 %all-gather.16.cloned.1.call-start = ((), (), s32[]{:S(2)}) async-start(), calls=%async_computation.1 | async-start | bytes 5308416 | tf_op jit(solution)/shard_map/all_gather | solution.py:73
  34.9 37.8 %collective-permute-start.1 = (bf16[6,192]{1,0:T(8,128)(2,1)S(1)}, bf16[6,192]{1,0:T(8,128)(2,1)S(1)}, u32[]{:S(2)}, u32[]{:S(2)}) collective-permute-start(bf16[6,192]{1,0:T(8,128)(2,1)S(1)} %get-tuple-element.150), channel_id=1, source_target_pairs={{0,2},{1,3},{2,0},{3,1},{4,6},{5,7},{6,4},{7,5},{8,10},{9,11},{10,... | collective-permute-start | bytes 6920 | tf_op jit(solution)/shard_map/ppermute | solution.py:61
  37.6 36.6 %collective-permute-start = (bf16[6,192]{1,0:T(8,128)(2,1)S(1)}, bf16[6,192]{1,0:T(8,128)(2,1)S(1)}, u32[]{:S(2)}, u32[]{:S(2)}) collective-permute-start(bf16[6,192]{1,0:T(8,128)(2,1)S(1)} %get-tuple-element.150), channel_id=1, source_target_pairs={{0,1},{1,2},{2,3},{3,0},{4,5},{5,6},{6,7},{7,4},{8,9},{9,10},{10,1... | collective-permute-start | bytes 6920 | tf_op jit(solution)/shard_map/ppermute | solution.py:61
  38.5 11.6 %collective-permute-start.4 = (bf16[48,1152]{1,0:T(8,128)(2,1)S(1)}, bf16[48,1152]{1,0:T(8,128)(2,1)S(1)}, u32[]{:S(2)}, u32[]{:S(2)}) collective-permute-start(bf16[48,1152]{1,0:T(8,128)(2,1)S(1)} %dynamic_slice.150), channel_id=1, source_target_pairs={{0,2},{1,3},{2,0},{3,1},{4,6},{5,7},{6,4},{7,5},{8,10},{9,11},{10,... | collective-permute-start | bytes 331784 | tf_op jit(solution)/shard_map/ppermute | solution.py:61
  41.0 11.1 %collective-permute-start.3 = (bf16[48,1152]{1,0:T(8,128)(2,1)S(1)}, bf16[48,1152]{1,0:T(8,128)(2,1)S(1)}, u32[]{:S(2)}, u32[]{:S(2)}) collective-permute-start(bf16[48,1152]{1,0:T(8,128)(2,1)S(1)} %dynamic_slice.150), channel_id=1, source_target_pairs={{0,1},{1,2},{2,3},{3,0},{4,5},{5,6},{6,7},{7,4},{8,9},{9,10},{10,1... | collective-permute-start | bytes 331784 | tf_op jit(solution)/shard_map/ppermute | solution.py:61
  43.0 9.2 %collective-permute-start.5 = (bf16[48,1152]{1,0:T(8,128)(2,1)S(1)}, bf16[48,1152]{1,0:T(8,128)(2,1)S(1)}, u32[]{:S(2)}, u32[]{:S(2)}) collective-permute-start(bf16[48,1152]{1,0:T(8,128)(2,1)S(1)} %dynamic_slice.150), channel_id=1, source_target_pairs={{0,3},{1,0},{2,1},{3,2},{4,7},{5,4},{6,5},{7,6},{8,11},{9,8},{10,9... | collective-permute-start | bytes 331784 | tf_op jit(solution)/shard_map/ppermute | solution.py:61
  50.1 26.4 %collective-permute-start.2 = (bf16[6,192]{1,0:T(8,128)(2,1)S(1)}, bf16[6,192]{1,0:T(8,128)(2,1)S(1)}, u32[]{:S(2)}, u32[]{:S(2)}) collective-permute-start(bf16[6,192]{1,0:T(8,128)(2,1)S(1)} %get-tuple-element.150), channel_id=1, source_target_pairs={{0,3},{1,0},{2,1},{3,2},{4,7},{5,4},{6,5},{7,6},{8,11},{9,8},{10,9... | collective-permute-start | bytes 6920 | tf_op jit(solution)/shard_map/ppermute | solution.py:61
  52.8 14.7 %collective-permute-start.6 = (bf16[4,48,1152]{2,1,0:T(8,128)(2,1)S(1)}, bf16[4,48,1152]{2,1,0:T(8,128)(2,1)S(1)}, u32[]{:S(2)}, u32[]{:S(2)}) collective-permute-start(bf16[4,48,1152]{2,1,0:T(8,128)(2,1)S(1)} %gather_fusion.1), channel_id=1, source_target_pairs={{0,8},{4,12},{8,0},{12,4},{16,24},{20,28},{24,16},{28,20},{1,9},{5... | collective-permute-start | bytes 1327112 | tf_op jit(solution)/shard_map/ppermute | solution.py:43
  54.4 16.9 %collective-permute-start.7 = (bf16[4,48,1152]{2,1,0:T(8,128)(2,1)S(1)}, bf16[4,48,1152]{2,1,0:T(8,128)(2,1)S(1)}, u32[]{:S(2)}, u32[]{:S(2)}) collective-permute-start(bf16[4,48,1152]{2,1,0:T(8,128)(2,1)S(1)} %gather_fusion.1), channel_id=1, source_target_pairs={{0,16},{4,20},{8,24},{12,28},{16,0},{20,4},{24,8},{28,12},{1,17},{... | collective-permute-start | bytes 1327112 | tf_op jit(solution)/shard_map/ppermute | solution.py:44
  67.5 25.1 %collective-permute-start.14 = (bf16[48,1536]{1,0:T(8,128)(2,1)}, bf16[48,1536]{1,0:T(8,128)(2,1)S(1)}, u32[]{:S(2)}, u32[]{:S(2)}) collective-permute-start(bf16[48,1536]{1,0:T(8,128)(2,1)} %dynamic_slice.152), channel_id=1, source_target_pairs={{0,2},{1,3},{2,0},{3,1},{4,6},{5,7},{6,4},{7,5},{8,10},{9,11},{10,... | collective-permute-start | bytes 442376 | tf_op jit(solution)/shard_map/ppermute | solution.py:61
  71.3 15.3 %collective-permute-start.8 = (bf16[4,48,1152]{2,1,0:T(8,128)(2,1)S(1)}, bf16[4,48,1152]{2,1,0:T(8,128)(2,1)S(1)}, u32[]{:S(2)}, u32[]{:S(2)}) collective-permute-start(bf16[4,48,1152]{2,1,0:T(8,128)(2,1)S(1)} %broadcast_select_fusion), channel_id=1, source_target_pairs={{0,8},{4,20},{8,0},{12,28},{16,24},{20,4},{24,16},{28,12},{1,9},{5... | collective-permute-start | bytes 1327112 | tf_op jit(solution)/shard_map/ppermute | solution.py:46
  72.7 19.9 %collective-permute-start.13 = (bf16[48,1536]{1,0:T(8,128)(2,1)}, bf16[48,1536]{1,0:T(8,128)(2,1)}, u32[]{:S(2)}, u32[]{:S(2)}) collective-permute-start(bf16[48,1536]{1,0:T(8,128)(2,1)} %dynamic_slice.152), channel_id=1, source_target_pairs={{0,1},{1,2},{2,3},{3,0},{4,5},{5,6},{6,7},{7,4},{8,9},{9,10},{10,1... | collective-permute-start | bytes 442376 | tf_op jit(solution)/shard_map/ppermute | solution.py:61
  74.2 18.5 %collective-permute-start.15 = (bf16[48,1536]{1,0:T(8,128)(2,1)}, bf16[48,1536]{1,0:T(8,128)(2,1)}, u32[]{:S(2)}, u32[]{:S(2)}) collective-permute-start(bf16[48,1536]{1,0:T(8,128)(2,1)} %dynamic_slice.152), channel_id=1, source_target_pairs={{0,3},{1,0},{2,1},{3,2},{4,7},{5,4},{6,5},{7,6},{8,11},{9,8},{10,9... | collective-permute-start | bytes 442376 | tf_op jit(solution)/shard_map/ppermute | solution.py:61
  88.9 8.9 %collective-permute-start.9 = (bf16[4,4,48,1152]{3,2,1,0:T(8,128)(2,1)}, bf16[4,4,48,1152]{3,2,1,0:T(8,128)(2,1)S(1)}, u32[]{:S(2)}, u32[]{:S(2)}) collective-permute-start(bf16[4,4,48,1152]{3,2,1,0:T(8,128)(2,1)} %pad_maximum_fusion.12), channel_id=1, source_target_pairs={{0,4},{4,0},{8,12},{12,8},{16,20},{20,16},{24,28},{28,24},{1,5},{5... | collective-permute-start | bytes 5308424 | tf_op jit(solution)/shard_map/ppermute | solution.py:50
  95.3 361.8 %all-gather.20.cloned.1.call-start = ((), (), s32[]{:S(2)}) async-start(), calls=%async_computation.3 | async-start | bytes 2211840 | tf_op jit(solution)/shard_map/all_gather | solution.py:137
  277.5 15.0 %collective-permute-start.19 = (bf16[4,4,48,1280]{3,2,1,0:T(8,128)(2,1)}, bf16[4,4,48,1280]{3,2,1,0:T(8,128)(2,1)}, u32[]{:S(2)}, u32[]{:S(2)}) collective-permute-start(bf16[4,4,48,1280]{3,2,1,0:T(8,128)(2,1)} %bitcast.60), channel_id=1, source_target_pairs={{0,4},{4,0},{8,12},{12,8},{16,20},{20,16},{24,28},{28,24},{1,5},{5... | collective-permute-start | bytes 5898248 | tf_op jit(solution)/shard_map/ppermute | solution.py:115
  289.6 18.5 %collective-permute-start.33 = (bf16[4,4,48,1536]{3,2,1,0:T(8,128)(2,1)}, bf16[4,4,48,1536]{3,2,1,0:T(8,128)(2,1)}, u32[]{:S(2)}, u32[]{:S(2)}) collective-permute-start(bf16[4,4,48,1536]{3,2,1,0:T(8,128)(2,1)} %bitcast.87), channel_id=1, source_target_pairs={{0,4},{4,0},{8,12},{12,8},{16,20},{20,16},{24,28},{28,24},{1,5},{5... | collective-permute-start | bytes 7077896 | tf_op jit(solution)/shard_map/ppermute | solution.py:115
  296.5 9.0 %collective-permute-start.20 = (bf16[4,48,1280]{2,1,0:T(8,128)(2,1)S(1)}, bf16[4,48,1280]{2,1,0:T(8,128)(2,1)}, u32[]{:S(2)}, u32[]{:S(2)}) collective-permute-start(bf16[4,48,1280]{2,1,0:T(8,128)(2,1)S(1)} %fusion.59), channel_id=1, source_target_pairs={{0,8},{4,20},{8,0},{12,28},{16,24},{20,4},{24,16},{28,12},{1,9},{5... | collective-permute-start | bytes 1474568 | tf_op jit(solution)/shard_map/ppermute | solution.py:121
  306.8 12.4 %collective-permute-start.21 = (bf16[4,48,1280]{2,1,0:T(8,128)(2,1)S(1)}, bf16[4,48,1280]{2,1,0:T(8,128)(2,1)S(1)}, u32[]{:S(2)}, u32[]{:S(2)}) collective-permute-start(bf16[4,48,1280]{2,1,0:T(8,128)(2,1)S(1)} %get-tuple-element.115), channel_id=1, source_target_pairs={{0,8},{4,12},{8,0},{12,4},{16,24},{20,28},{24,16},{28,20},{1,9},{5... | collective-permute-start | bytes 1474568 | tf_op jit(solution)/shard_map/ppermute | solution.py:128
  306.9 12.4 %collective-permute-start.22 = (bf16[4,48,1280]{2,1,0:T(8,128)(2,1)S(1)}, bf16[4,48,1280]{2,1,0:T(8,128)(2,1)S(1)}, u32[]{:S(2)}, u32[]{:S(2)}) collective-permute-start(bf16[4,48,1280]{2,1,0:T(8,128)(2,1)S(1)} %get-tuple-element.116), channel_id=1, source_target_pairs={{0,16},{4,20},{8,24},{12,28},{16,0},{20,4},{24,8},{28,12},{1,17},{... | collective-permute-start | bytes 1474568 | tf_op jit(solution)/shard_map/ppermute | solution.py:129
  319.5 8.1 %collective-permute-start.23 = (bf16[48,1280]{1,0:T(8,128)(2,1)S(1)}, bf16[48,1280]{1,0:T(8,128)(2,1)S(1)}, u32[]{:S(2)}, u32[]{:S(2)}) collective-permute-start(bf16[48,1280]{1,0:T(8,128)(2,1)S(1)} %get-tuple-element.135), channel_id=1, source_target_pairs={{0,1},{1,2},{2,3},{3,0},{4,5},{5,6},{6,7},{7,4},{8,9},{9,10},{10,1... | collective-permute-start | bytes 368648 | tf_op jit(solution)/shard_map/ppermute | solution.py:134
  321.3 6.3 %collective-permute-start.25 = (bf16[48,1280]{1,0:T(8,128)(2,1)S(1)}, bf16[48,1280]{1,0:T(8,128)(2,1)S(1)}, u32[]{:S(2)}, u32[]{:S(2)}) collective-permute-start(bf16[48,1280]{1,0:T(8,128)(2,1)S(1)} %get-tuple-element.136), channel_id=1, source_target_pairs={{0,3},{1,0},{2,1},{3,2},{4,7},{5,4},{6,5},{7,6},{8,11},{9,8},{10,9... | collective-permute-start | bytes 368648 | tf_op jit(solution)/shard_map/ppermute | solution.py:134
  323.3 9.3 %collective-permute-start.24 = (bf16[48,1280]{1,0:T(8,128)(2,1)S(1)}, bf16[48,1280]{1,0:T(8,128)(2,1)S(1)}, u32[]{:S(2)}, u32[]{:S(2)}) collective-permute-start(bf16[48,1280]{1,0:T(8,128)(2,1)S(1)} %get-tuple-element.137), channel_id=1, source_target_pairs={{0,2},{1,3},{2,0},{3,1},{4,6},{5,7},{6,4},{7,5},{8,10},{9,11},{10,... | collective-permute-start | bytes 368648 | tf_op jit(solution)/shard_map/ppermute | solution.py:134
  324.2 10.1 %collective-permute-start.34 = (bf16[4,48,1536]{2,1,0:T(8,128)(2,1)}, bf16[4,48,1536]{2,1,0:T(8,128)(2,1)S(1)}, u32[]{:S(2)}, u32[]{:S(2)}) collective-permute-start(bf16[4,48,1536]{2,1,0:T(8,128)(2,1)} %fusion.57), channel_id=1, source_target_pairs={{0,8},{4,20},{8,0},{12,28},{16,24},{20,4},{24,16},{28,12},{1,9},{5... | collective-permute-start | bytes 1769480 | tf_op jit(solution)/shard_map/ppermute | solution.py:121
  333.4 128.7 %all-gather.22.cloned.1.call-start = ((), (), s32[]{:S(2)}) async-start(), calls=%async_computation.4 | async-start | bytes 2654208 | tf_op jit(solution)/shard_map/all_gather | solution.py:137
  336.5 16.4 %collective-permute-start.35 = (bf16[4,48,1536]{2,1,0:T(8,128)(2,1)S(1)}, bf16[4,48,1536]{2,1,0:T(8,128)(2,1)S(1)}, u32[]{:S(2)}, u32[]{:S(2)}) collective-permute-start(bf16[4,48,1536]{2,1,0:T(8,128)(2,1)S(1)} %get-tuple-element.107), channel_id=1, source_target_pairs={{0,8},{4,12},{8,0},{12,4},{16,24},{20,28},{24,16},{28,20},{1,9},{5... | collective-permute-start | bytes 1769480 | tf_op jit(solution)/shard_map/ppermute | solution.py:128
  338.0 15.2 %collective-permute-start.36 = (bf16[4,48,1536]{2,1,0:T(8,128)(2,1)S(1)}, bf16[4,48,1536]{2,1,0:T(8,128)(2,1)S(1)}, u32[]{:S(2)}, u32[]{:S(2)}) collective-permute-start(bf16[4,48,1536]{2,1,0:T(8,128)(2,1)S(1)} %get-tuple-element.108), channel_id=1, source_target_pairs={{0,16},{4,20},{8,24},{12,28},{16,0},{20,4},{24,8},{28,12},{1,17},{... | collective-permute-start | bytes 1769480 | tf_op jit(solution)/shard_map/ppermute | solution.py:129
  349.6 22.8 %collective-permute-start.40 = (bf16[4,4,192,384]{3,2,1,0:T(8,128)(2,1)}, bf16[4,4,192,384]{3,2,1,0:T(8,128)(2,1)}, u32[]{:S(2)}, u32[]{:S(2)}) collective-permute-start(bf16[4,4,192,384]{3,2,1,0:T(8,128)(2,1)} %bitcast.100), channel_id=1, source_target_pairs={{0,4},{4,0},{8,12},{12,8},{16,20},{20,16},{24,28},{28,24},{1,5},{5... | collective-permute-start | bytes 7077896 | tf_op jit(solution)/shard_map/ppermute | solution.py:115
  354.7 8.3 %collective-permute-start.37 = (bf16[48,1536]{1,0:T(8,128)(2,1)S(1)}, bf16[48,1536]{1,0:T(8,128)(2,1)S(1)}, u32[]{:S(2)}, u32[]{:S(2)}) collective-permute-start(bf16[48,1536]{1,0:T(8,128)(2,1)S(1)} %get-tuple-element.130), channel_id=1, source_target_pairs={{0,1},{1,2},{2,3},{3,0},{4,5},{5,6},{6,7},{7,4},{8,9},{9,10},{10,1... | collective-permute-start | bytes 442376 | tf_op jit(solution)/shard_map/ppermute | solution.py:134
  354.8 8.3 %collective-permute-start.39 = (bf16[48,1536]{1,0:T(8,128)(2,1)S(1)}, bf16[48,1536]{1,0:T(8,128)(2,1)S(1)}, u32[]{:S(2)}, u32[]{:S(2)}) collective-permute-start(bf16[48,1536]{1,0:T(8,128)(2,1)S(1)} %get-tuple-element.131), channel_id=1, source_target_pairs={{0,3},{1,0},{2,1},{3,2},{4,7},{5,4},{6,5},{7,6},{8,11},{9,8},{10,9... | collective-permute-start | bytes 442376 | tf_op jit(solution)/shard_map/ppermute | solution.py:134
  358.6 10.2 %collective-permute-start.38 = (bf16[48,1536]{1,0:T(8,128)(2,1)S(1)}, bf16[48,1536]{1,0:T(8,128)(2,1)S(1)}, u32[]{:S(2)}, u32[]{:S(2)}) collective-permute-start(bf16[48,1536]{1,0:T(8,128)(2,1)S(1)} %get-tuple-element.132), channel_id=1, source_target_pairs={{0,2},{1,3},{2,0},{3,1},{4,6},{5,7},{6,4},{7,5},{8,10},{9,11},{10,... | collective-permute-start | bytes 442376 | tf_op jit(solution)/shard_map/ppermute | solution.py:134
  369.7 94.3 %all-gather.24.cloned.1.call-start = ((), (), s32[]{:S(2)}) async-start(), calls=%async_computation.5 | async-start | bytes 2654208 | tf_op jit(solution)/shard_map/all_gather | solution.py:137
  374.8 12.7 %collective-permute-start.41 = (bf16[4,192,384]{2,1,0:T(8,128)(2,1)S(1)}, bf16[4,192,384]{2,1,0:T(8,128)(2,1)S(1)}, u32[]{:S(2)}, u32[]{:S(2)}) collective-permute-start(bf16[4,192,384]{2,1,0:T(8,128)(2,1)S(1)} %fusion.58), channel_id=1, source_target_pairs={{0,8},{4,20},{8,0},{12,28},{16,24},{20,4},{24,16},{28,12},{1,9},{5... | collective-permute-start | bytes 1769480 | tf_op jit(solution)/shard_map/ppermute | solution.py:121
  387.8 18.9 %collective-permute-start.42 = (bf16[4,192,384]{2,1,0:T(8,128)(2,1)S(1)}, bf16[4,192,384]{2,1,0:T(8,128)(2,1)S(1)}, u32[]{:S(2)}, u32[]{:S(2)}) collective-permute-start(bf16[4,192,384]{2,1,0:T(8,128)(2,1)S(1)} %get-tuple-element.105), channel_id=1, source_target_pairs={{0,8},{4,12},{8,0},{12,4},{16,24},{20,28},{24,16},{28,20},{1,9},{5... | collective-permute-start | bytes 1769480 | tf_op jit(solution)/shard_map/ppermute | solution.py:128
  388.2 19.5 %collective-permute-start.43 = (bf16[4,192,384]{2,1,0:T(8,128)(2,1)S(1)}, bf16[4,192,384]{2,1,0:T(8,128)(2,1)S(1)}, u32[]{:S(2)}, u32[]{:S(2)}) collective-permute-start(bf16[4,192,384]{2,1,0:T(8,128)(2,1)S(1)} %get-tuple-element.106), channel_id=1, source_target_pairs={{0,16},{4,20},{8,24},{12,28},{16,0},{20,4},{24,8},{28,12},{1,17},{... | collective-permute-start | bytes 1769480 | tf_op jit(solution)/shard_map/ppermute | solution.py:129
  391.0 21.0 %collective-permute-start.26 = (bf16[4,4,48,384]{3,2,1,0:T(8,128)(2,1)S(1)}, bf16[4,4,48,384]{3,2,1,0:T(8,128)(2,1)S(1)}, u32[]{:S(2)}, u32[]{:S(2)}) collective-permute-start(bf16[4,4,48,384]{3,2,1,0:T(8,128)(2,1)S(1)} %bitcast.303), channel_id=1, source_target_pairs={{0,4},{4,0},{8,12},{12,8},{16,20},{20,16},{24,28},{28,24},{1,5},{5... | collective-permute-start | bytes 1769480 | tf_op jit(solution)/shard_map/ppermute | solution.py:115
  408.1 8.7 %collective-permute-start.44 = (bf16[192,384]{1,0:T(8,128)(2,1)S(1)}, bf16[192,384]{1,0:T(8,128)(2,1)S(1)}, u32[]{:S(2)}, u32[]{:S(2)}) collective-permute-start(bf16[192,384]{1,0:T(8,128)(2,1)S(1)} %get-tuple-element.127), channel_id=1, source_target_pairs={{0,1},{1,2},{2,3},{3,0},{4,5},{5,6},{6,7},{7,4},{8,9},{9,10},{10,1... | collective-permute-start | bytes 442376 | tf_op jit(solution)/shard_map/ppermute | solution.py:134
  408.1 8.6 %collective-permute-start.46 = (bf16[192,384]{1,0:T(8,128)(2,1)S(1)}, bf16[192,384]{1,0:T(8,128)(2,1)S(1)}, u32[]{:S(2)}, u32[]{:S(2)}) collective-permute-start(bf16[192,384]{1,0:T(8,128)(2,1)S(1)} %get-tuple-element.128), channel_id=1, source_target_pairs={{0,3},{1,0},{2,1},{3,2},{4,7},{5,4},{6,5},{7,6},{8,11},{9,8},{10,9... | collective-permute-start | bytes 442376 | tf_op jit(solution)/shard_map/ppermute | solution.py:134
  411.9 9.6 %collective-permute-start.45 = (bf16[192,384]{1,0:T(8,128)(2,1)S(1)}, bf16[192,384]{1,0:T(8,128)(2,1)S(1)}, u32[]{:S(2)}, u32[]{:S(2)}) collective-permute-start(bf16[192,384]{1,0:T(8,128)(2,1)S(1)} %get-tuple-element.129), channel_id=1, source_target_pairs={{0,2},{1,3},{2,0},{3,1},{4,6},{5,7},{6,4},{7,5},{8,10},{9,11},{10,... | collective-permute-start | bytes 442376 | tf_op jit(solution)/shard_map/ppermute | solution.py:134
  413.1 16.7 %collective-permute-start.27 = (bf16[4,48,384]{2,1,0:T(8,128)(2,1)S(1)}, bf16[4,48,384]{2,1,0:T(8,128)(2,1)S(1)}, u32[]{:S(2)}, u32[]{:S(2)}) collective-permute-start(bf16[4,48,384]{2,1,0:T(8,128)(2,1)S(1)} %fusion.76), channel_id=1, source_target_pairs={{0,8},{4,20},{8,0},{12,28},{16,24},{20,4},{24,16},{28,12},{1,9},{5... | collective-permute-start | bytes 442376 | tf_op jit(solution)/shard_map/ppermute | solution.py:121
  429.9 7.1 %collective-permute-start.28 = (bf16[4,48,384]{2,1,0:T(8,128)(2,1)S(1)}, bf16[4,48,384]{2,1,0:T(8,128)(2,1)S(1)}, u32[]{:S(2)}, u32[]{:S(2)}) collective-permute-start(bf16[4,48,384]{2,1,0:T(8,128)(2,1)S(1)} %get-tuple-element.125), channel_id=1, source_target_pairs={{0,8},{4,12},{8,0},{12,4},{16,24},{20,28},{24,16},{28,20},{1,9},{5... | collective-permute-start | bytes 442376 | tf_op jit(solution)/shard_map/ppermute | solution.py:128
  430.3 6.8 %collective-permute-start.29 = (bf16[4,48,384]{2,1,0:T(8,128)(2,1)S(1)}, bf16[4,48,384]{2,1,0:T(8,128)(2,1)S(1)}, u32[]{:S(2)}, u32[]{:S(2)}) collective-permute-start(bf16[4,48,384]{2,1,0:T(8,128)(2,1)S(1)} %get-tuple-element.126), channel_id=1, source_target_pairs={{0,16},{4,20},{8,24},{12,28},{16,0},{20,4},{24,8},{28,12},{1,17},{... | collective-permute-start | bytes 442376 | tf_op jit(solution)/shard_map/ppermute | solution.py:129
  (79 other events, 746.7 us)
Sparse Core Ops, SparseCore 0:
  19.5 25.1 all-gather.13
  47.2 46.6 all-gather.17
  96.4 37.2 all-gather.15
  333.6 27.9 all-gather.19
  369.8 34.7 all-gather.21
  422.5 28.4 all-gather.23

commit v19 on v16

--- a/solution.py
+++ b/solution.py
@@ -133,7 +133,7 @@
         total = total + lax.ppermute(
             part.astype(jnp.bfloat16), "fsdp", [(i, (i + k) % NF_FAST) for i in range(NF_FAST)]
         ).astype(jnp.float32)
-    x = lax.all_gather(total.astype(jnp.bfloat16), "dp", axis=0, tiled=False).astype(jnp.float32)
+    x = lax.all_gather(total, "dp", axis=0, tiled=False)
     x = x.reshape(n_chips, 2, rows, cols)
     x = jnp.concatenate([x[:, 0], x[:, 1]], axis=-1)
     return x.reshape(n_chips * rows, 2 * cols)
@@ -142,10 +142,11 @@
 def fast_reduce(mats, gains):
     stacked = jnp.concatenate(gains, axis=0)
     pad = 2 * LANES - stacked.shape[0]
-    first = jnp.concatenate([mats[0], jnp.pad(stacked.T, ((0, 0), (0, pad)))], axis=1)
-    shard = _reduce_matrix(first)
-    width = mats[0].shape[1]
-    out = [shard[:, :width]] + [_reduce_matrix(m) for m in mats[1:]]
+    last = jnp.concatenate([mats[-1], jnp.pad(stacked.T, ((0, 0), (0, pad)))], axis=1)
+    out = [_reduce_matrix(m) for m in mats[:-1]]
+    shard = _reduce_matrix(last)
+    width = mats[-1].shape[1]
+    out.append(shard[:, :width])
     mine = shard[:, width : width + stacked.shape[0]].T
     rows = 0
     for g in gains:

time: 456 us -> 485 us (1.064)
  the two profiles are of different devices: /device:TPU:8 before, /device:TPU:0 now
where the time goes in v19:
time: 485 us; the launch traced here: 477 us
  matrix products  116 us (24%)
  local copies, waits for them, and re-layouts  103 us (21%)
  waiting for transfers between devices  92.4 us (19%)
  other arithmetic  75.6 us (16%)
  starting transfers between devices  63.3 us (13%)
  between operations  15.8 us (3%)
  blocking collectives  10.4 us (2%)
    unnamed x164, local copies, waits for them, and re-layouts  30.7 us
    ppermute x15, starting transfers between devices, _z_gather(): lax.ppermute(piece, 'fsdp', [(i, (i + k) % NF_FAST) for i in range(NF_FAS...  29.8 us
    ppermute x12, waiting for transfers between devices, _reduce_matrix(): lax.ppermute(part.astype(jnp.bfloat16), 'fsdp', [(i, (i + k) % NF_FAST) f...  27.6 us
    dot_general x1, matrix products, layer(): up_pre = jnp.dot(second_low, full_up, preferred_element_type=jnp.float32)  22 us
    ppermute x4, waiting for transfers between devices, _reduce_matrix(): lax.ppermute(of_chip(j ^ 3).astype(jnp.bfloat16), 'dp', [(i, i ^ 2) if i...  18.6 us
    ppermute x12, starting transfers between devices, _reduce_matrix(): lax.ppermute(part.astype(jnp.bfloat16), 'fsdp', [(i, (i + k) % NF_FAST) f...  16 us
    ppermute x4, waiting for transfers between devices, _reduce_matrix(): lax.ppermute(to_x.astype(jnp.bfloat16), 'dp', [(i, i ^ 2) for i in range(...  15.8 us
    dynamic_slice x5, local copies, waits for them, and re-layouts, half(): part = lax.dynamic_slice_in_dim(g, which * cols, cols, 1)  14.8 us
  transfers between devices with their start and end apart: 53, of which 26 were waited for; matrix products, arithmetic and copies ran while one was open for 35% of the time, Pallas kernels for 0%

profile of v19, /device:TPU:0, one launch (start us, length us, event | category | flops | bytes accessed | tf_op | source)
XLA Modules:
  0.0 476.8 jit_solution(3594875064787522727)
XLA Ops:
  8.1 4.1 collective-permute-start.11
  21.2 3.4 collective-permute-start.16
  26.0 6.7 %collective-permute-done.17 = bf16[192,384]{1,0:T(8,128)(2,1)S(1)} collective-permute-done((bf16[192,384]{1,0:T(8,128)(2,1)S(1)}, bf16[192,384]{1,0:T(8,128)(2,1)S(1)}, u32[]{:S(2)}, u32[]{:S(2)}) %collective-permute-start.17) | collective-permute-done | bytes 147488 | tf_op jit(solution)/shard_map/ppermute | solution.py:61
  34.9 2.7 collective-permute-start.1
  57.7 9.8 %collective-permute-done.6 = bf16[4,48,1152]{2,1,0:T(8,128)(2,1)S(1)} collective-permute-done((bf16[4,48,1152]{2,1,0:T(8,128)(2,1)S(1)}, bf16[4,48,1152]{2,1,0:T(8,128)(2,1)S(1)}, u32[]{:S(2)}, u32[]{:S(2)}) %collective-permute-start.6) | collective-permute-done | bytes 442400 | tf_op jit(solution)/shard_map/ppermute | solution.py:43
  77.1 9.5 %collective-permute-done.8 = bf16[4,48,1152]{2,1,0:T(8,128)(2,1)S(1)} collective-permute-done((bf16[4,48,1152]{2,1,0:T(8,128)(2,1)S(1)}, bf16[4,48,1152]{2,1,0:T(8,128)(2,1)S(1)}, u32[]{:S(2)}, u32[]{:S(2)}) %collective-permute-start.8) | collective-permute-done | bytes 442400 | tf_op jit(solution)/shard_map/ppermute | solution.py:46
  103.3 3.2 gather_fusion.2
  115.0 3.4 fusion.120
  126.4 8.3 %fusion.129 = (f32[12,576]{1,0:T(8,128)S(1)}, f32[12,576,576]{1,2,0:T(8,128)}) fusion(f32[576,12,64]{0,2,1:T(8,128)S(1)} %bitcast.249, f32[12,64]{1,0:T(8,128)S(1)} %mul.357, f32[576,12]{0,1:T(8,128)S(1)} %fusion.94, f32[576,12]{0,1:T(8,128)S(1)} %broadcast_multiply_fusion, f32[576,12,64]{0,2,1:T(8,128)S(1)} %bitcast.241, f32[12,64]{1,0:T(8,128)S(1)} %copy-done.52, ...), kind=kOutput, calls=%fused_computation.291 | convolution fusion | flops 525083904 | bytes 19940352 | tf_op jit(solution)/shard_map/while/body/eval_jaxpr/qhd,khd->hqk/dot_general | solution.py:211
  134.7 8.5 %fusion.3 = f32[12,576]{1,0:T(8,128)S(1)} fusion(f32[12,576,576]{1,2,0:T(8,128)} %get-tuple-element.134, f32[12,576]{1,0:T(8,128)S(1)} %get-tuple-element.133), kind=kLoop, calls=%fused_computation.15 | loop fusion | flops 7955712 | bytes 15980544 | tf_op jit(solution)/shard_map/while/body/eval_jaxpr/reduce_sum | solution.py:221
  143.2 9.7 %fusion.35 = bf16[12,64,576]{2,1,0:T(8,128)(2,1)S(1)} fusion(bf16[576,12,64]{0,2,1:T(8,128)(2,1)} %bitcast.269, f32[12,576,576]{1,2,0:T(8,128)} %get-tuple-element.134, f32[12,576]{1,0:T(8,128)S(1)} %fusion.3, f32[12,576]{1,0:T(8,128)S(1)} %get-tuple-element.133), kind=kOutput, calls=%fused_computation.110 | convolution fusion | flops 521994240 | bytes 17750016 | tf_op jit(solution)/shard_map/while/body/eval_jaxpr/hqk,khd->qhd/dot_general | solution.py:223
  155.6 5.1 %fusion.121 = (bf16[4,4,1,192,384]{4,3,2,1,0:T(8,128)(2,1)}, bf16[4,4,1,192,384]{4,3,2,1,0:T(8,128)(2,1)}) fusion(bf16[4,4,2,192,384]{4,3,2,1,0:T(8,128)(2,1)} %bitcast.260), kind=kLoop, calls=%fused_computation.283 | loop fusion | bytes 9437184 | tf_op jit(solution)/shard_map/slice | solution.py:75
  160.7 3.0 fusion.122
  163.8 22.0 %multiply_convert_fusion = (bf16[576,3072]{1,0:T(8,128)(2,1)}, f32[576,3072]{1,0:T(8,128)}, f32[576,3072]{1,0:T(8,128)}) fusion(bf16[768,1536]{1,0:T(8,128)(2,1)S(1)} %bitcast.284, bf16[768,1536]{1,0:T(8,128)(2,1)S(1)} %bitcast.282, f32[576,768]{1,0:T(8,128)S(1)} %copy-done.9, f32[768]{0:T(1024)S(1)} %add.405, f32[768]{0:T(1024)S(1)} %mul.365, ...), kind=kOutput, calls=%fused_computation.23 | convolution fusion | flops 2844573696 | bytes 24193536 | tf_op jit(solution)/shard_map/dot_general | solution.py:233
  185.8 8.1 %add_convert_fusion = bf16[576,3072]{1,0:T(8,128)(2,1)S(1)} fusion(f32[576,3072]{1,0:T(8,128)} %get-tuple-element.86, f32[576,3072]{1,0:T(8,128)} %get-tuple-element.137, bf16[3072,384]{1,0:T(8,128)(2,1)S(1)} %bitcast.281, bf16[3072,384]{1,0:T(8,128)(2,1)S(1)} %bitcast.279, bf16[576,768]{1,0:T(8,128)(2,1)S(1)} %copy-done.29, f32[576]{0:T(1024)S(1)} %copy-done.58), kind=kOutput, calls=%fused_computation.22 | convolution fusion | flops 2753445888 | bytes 23300352 | tf_op jit(solution)/shard_map/dot_general | solution.py:242
  194.0 3.3 multiply_reduce_fusion.2
  204.5 7.6 %convolution_convert_fusion = bf16[12,576,576]{1,2,0:T(8,128)(2,1)} fusion(bf16[576,12,64]{0,2,1:T(8,128)(2,1)} %bitcast.257, bf16[576,12,64]{0,2,1:T(8,128)(2,1)} %bitcast.270), kind=kOutput, calls=%fused_computation.37 | convolution fusion | flops 513589248 | bytes 9732096 | tf_op jit(solution)/shard_map/qhd,khd->hqk/dot_general | solution.py:262
  212.1 9.9 %fusion.36 = bf16[12,64,576]{2,1,0:T(8,128)(2,1)} fusion(bf16[576,12,64]{0,2,1:T(8,128)(2,1)S(1)} %bitcast.258, f32[12,576,576]{1,2,0:T(8,128)} %get-tuple-element.134, f32[12,576]{1,0:T(8,128)S(1)} %log_add_fusion), kind=kOutput, calls=%fused_computation.111 | convolution fusion | flops 518012928 | bytes 17722368 | tf_op jit(solution)/shard_map/hqk,qhd->khd/dot_general | solution.py:261
  222.0 12.9 %fusion = f32[12,576]{1,0:T(8,128)S(1)} fusion(bf16[12,576,576]{1,2,0:T(8,128)(2,1)} %convolution_convert_fusion, f32[12,576,576]{1,2,0:T(8,128)} %get-tuple-element.134, f32[12,576]{1,0:T(8,128)S(1)} %log_add_fusion), kind=kLoop, calls=%fused_computation.8 | loop fusion | flops 15918336 | bytes 23943168 | tf_op jit(solution)/shard_map/reduce_sum | solution.py:264
  235.6 6.2 %fusion.2 = bf16[12,576,576]{1,2,0:T(8,128)(2,1)} fusion(bf16[12,576,576]{1,2,0:T(8,128)(2,1)S(1)} %copy-done.3, f32[12,576,576]{1,2,0:T(8,128)S(1)} %bitcast.238, f32[12,576]{1,0:T(8,128)S(1)} %fusion, f32[12,576]{1,0:T(8,128)S(1)} %log_add_fusion), kind=kLoop, calls=%fused_computation.10 | loop fusion | flops 19906560 | bytes 31905792 | tf_op jit(solution)/shard_map/convert_element_type | solution.py:265
  241.9 8.2 %fusion.27 = (f32[576,12]{0,1:T(8,128)S(1)}, f32[12,64,576]{2,1,0:T(8,128)}) fusion(f32[576,12,64]{0,2,1:T(8,128)} %bitcast.248, f32[12,64]{1,0:T(8,128)S(1)} %copy-done.50, f32[576,12]{0,1:T(8,128)S(1)} %broadcast_multiply_fusion, bf16[12,576,576]{1,2,0:T(8,128)(2,1)} %fusion.2, f32[576,12,64]{0,2,1:T(8,128)S(1)} %bitcast.242, ...), kind=kOutput, calls=%fused_computation.75 | convolution fusion | flops 513139968 | bytes 13387776 | tf_op jit(solution)/shard_map/hqk,qhd->khd/dot_general | solution.py:270
  256.9 3.4 fusion.39
  260.3 2.9 copy-done.25
  265.3 6.3 %fusion.116 = f32[768,3072]{1,0:T(8,128)S(1)} fusion(bf16[576,3072]{1,0:T(8,128)(2,1)} %copy-done.27, f32[576,768]{1,0:T(8,128)S(1)} %copy-done.10, f32[768]{0:T(1024)S(1)} %add.405, f32[768]{0:T(1024)S(1)} %mul.365, f32[576]{0:T(1024)S(1)} %fusion.97, f32[576]{0:T(1024)S(1)} %broadcast_multiply_fusion.4), kind=kOutput, calls=%fused_computation.279 | convolution fusion | flops 2720120832 | bytes 14756352 | tf_op jit(solution)/shard_map/dot_general | solution.py:245
  274.2 3.6 constant_dynamic-slice_fusion.3
  281.7 2.8 constant_dynamic-slice_fusion.1
  284.5 5.4 %collective-permute-done.20 = bf16[4,48,1152]{2,1,0:T(8,128)(2,1)} collective-permute-done((bf16[4,48,1152]{2,1,0:T(8,128)(2,1)S(1)}, bf16[4,48,1152]{2,1,0:T(8,128)(2,1)}, u32[]{:S(2)}, u32[]{:S(2)}) %collective-permute-start.20) | collective-permute-done | bytes 442400 | tf_op jit(solution)/shard_map/ppermute | solution.py:120
  294.9 8.0 %collective-permute-done.21 = bf16[4,48,1152]{2,1,0:T(8,128)(2,1)S(1)} collective-permute-done((bf16[4,48,1152]{2,1,0:T(8,128)(2,1)S(1)}, bf16[4,48,1152]{2,1,0:T(8,128)(2,1)S(1)}, u32[]{:S(2)}, u32[]{:S(2)}) %collective-permute-start.21) | collective-permute-done | bytes 442400 | tf_op jit(solution)/shard_map/ppermute | solution.py:127
  311.2 4.5 collective-permute-done.24
  322.9 5.2 %fusion.65 = f32[3072,768]{1,0:T(8,128)S(1)} fusion(bf16[576,3072]{1,0:T(8,128)(2,1)S(1)} %copy-done.71, bf16[576,768]{1,0:T(8,128)(2,1)} %param.19, f32[576]{0:T(1024)S(1)} %copy-done.58), kind=kOutput, calls=%fused_computation.162 | convolution fusion | flops 2719236096 | bytes 13863168 | tf_op jit(solution)/shard_map/dot_general | solution.py:241
  328.1 3.7 copy-done.24
  339.9 3.7 collective-permute-start.39
  344.0 4.1 collective-permute-done.37
  348.2 6.1 %collective-permute-done.38 = bf16[48,1536]{1,0:T(8,128)(2,1)S(1)} collective-permute-done((bf16[48,1536]{1,0:T(8,128)(2,1)S(1)}, bf16[48,1536]{1,0:T(8,128)(2,1)S(1)}, u32[]{:S(2)}, u32[]{:S(2)}) %collective-permute-start.38) | collective-permute-done | bytes 147488 | tf_op jit(solution)/shard_map/ppermute | solution.py:133
  356.3 6.7 %fusion.117 = (f32[768]{0:T(1024)S(1)}, f32[576]{0:T(1024)S(1)}, f32[576,768]{1,0:T(8,128)}) fusion(f32[768]{0:T(1024)S(1)} %copy-done.62, f32[576]{0:T(1024)S(1)} %copy-done.55, bf16[576,768]{1,0:T(8,128)(2,1)S(1)} %copy-done.14, bf16[768,2304]{1,0:T(8,128)(2,1)} %bitcast.274, bf16[576,768]{0,1:T(8,128)(2,1)} %bitcast.296, ...), kind=kOutput, calls=%fused_computation.280 | convolution fusion | flops 2049047296 | bytes 8858112 | tf_op jit(solution)/shard_map/dot_general | solution.py:289
  363.2 2.6 constant_dynamic-slice_fusion
  372.3 3.0 fusion.131
  375.3 11.6 %collective-permute-done.41 = bf16[4,192,384]{2,1,0:T(8,128)(2,1)} collective-permute-done((bf16[4,192,384]{2,1,0:T(8,128)(2,1)S(1)}, bf16[4,192,384]{2,1,0:T(8,128)(2,1)}, u32[]{:S(2)}, u32[]{:S(2)}) %collective-permute-start.41) | collective-permute-done | bytes 589856 | tf_op jit(solution)/shard_map/ppermute | solution.py:120
  386.9 2.9 fusion.46
  396.4 2.7 constant_dynamic-slice_fusion.2
  399.0 3.1 copy.92
  404.2 3.8 collective-permute-start.46
  413.6 7.0 %collective-permute-done.45 = bf16[192,384]{1,0:T(8,128)(2,1)S(1)} collective-permute-done((bf16[192,384]{1,0:T(8,128)(2,1)S(1)}, bf16[192,384]{1,0:T(8,128)(2,1)S(1)}, u32[]{:S(2)}, u32[]{:S(2)}) %collective-permute-start.45) | collective-permute-done | bytes 147488 | tf_op jit(solution)/shard_map/ppermute | solution.py:133
  421.5 7.4 %multiply_convert_fusion.3 = bf16[576,768]{1,0:T(8,128)(2,1)} fusion(f32[576,768]{1,0:T(8,128)S(1)} %copy-done.10, bf16[576,3072]{1,0:T(8,128)(2,1)} %get-tuple-element.85, bf16[3072,384]{1,0:T(8,128)(2,1)} %bitcast.280, bf16[3072,384]{1,0:T(8,128)(2,1)} %bitcast.278, f32[576]{0:T(1024)S(1)} %copy-done.58), kind=kOutput, calls=%fused_computation.101 | convolution fusion | flops 2728673280 | bytes 10914048 | tf_op jit(solution)/shard_map/dot_general | solution.py:236
  432.1 5.3 %collective-permute-done.28 = bf16[4,48,512]{2,1,0:T(8,128)(2,1)S(1)} collective-permute-done((bf16[4,48,512]{2,1,0:T(8,128)(2,1)S(1)}, bf16[4,48,512]{2,1,0:T(8,128)(2,1)S(1)}, u32[]{:S(2)}, u32[]{:S(2)}) %collective-permute-start.28) | collective-permute-done | bytes 196640 | tf_op jit(solution)/shard_map/ppermute | solution.py:127
  438.7 2.9 collective-permute-start.32
  443.7 2.8 collective-permute-done.31
  446.6 10.4 %all-gather.4 = f32[384,512]{1,0:T(8,128)S(1)} all-gather(f32[48,512]{1,0:T(8,128)S(1)} %fusion.87), channel_id=6, replica_groups=mesh['dp'=8,'fsdp'=4] {'dp'}, dimensions={0}, use_global_device_ids=true | all-gather | bytes 884736 | tf_op jit(solution)/shard_map/all_gather | solution.py:136
  (390 shorter events, 173.4 us)
Async XLA Ops:
  7.2 88.1 %all-gather.14.cloned.1.call-start = ((), (), s32[]{:S(2)}) async-start(), calls=%async_computation | async-start | bytes 1327104 | tf_op jit(solution)/shard_map/all_gather | solution.py:73
  8.1 8.7 %collective-permute-start.11 = (bf16[48,384]{1,0:T(8,128)(2,1)S(1)}, bf16[48,384]{1,0:T(8,128)(2,1)S(1)}, u32[]{:S(2)}, u32[]{:S(2)}) collective-permute-start(bf16[48,384]{1,0:T(8,128)(2,1)S(1)} %dynamic_slice.151), channel_id=1, source_target_pairs={{0,2},{1,3},{2,0},{3,1},{4,6},{5,7},{6,4},{7,5},{8,10},{9,11},{10,... | collective-permute-start | bytes 110600 | tf_op jit(solution)/shard_map/ppermute | solution.py:61
  19.4 136.2 %all-gather.18.cloned.1.call-start = ((), (), s32[]{:S(2)}) async-start(), calls=%async_computation.2 | async-start | bytes 5308416 | tf_op jit(solution)/shard_map/all_gather | solution.py:73
  20.4 12.3 %collective-permute-start.17 = (bf16[192,384]{1,0:T(8,128)(2,1)S(1)}, bf16[192,384]{1,0:T(8,128)(2,1)S(1)}, u32[]{:S(2)}, u32[]{:S(2)}) collective-permute-start(bf16[192,384]{1,0:T(8,128)(2,1)S(1)} %dynamic_slice.153), channel_id=1, source_target_pairs={{0,2},{1,3},{2,0},{3,1},{4,6},{5,7},{6,4},{7,5},{8,10},{9,11},{10,... | collective-permute-start | bytes 442376 | tf_op jit(solution)/shard_map/ppermute | solution.py:61
  21.2 11.4 %collective-permute-start.16 = (bf16[192,384]{1,0:T(8,128)(2,1)S(1)}, bf16[192,384]{1,0:T(8,128)(2,1)S(1)}, u32[]{:S(2)}, u32[]{:S(2)}) collective-permute-start(bf16[192,384]{1,0:T(8,128)(2,1)S(1)} %dynamic_slice.153), channel_id=1, source_target_pairs={{0,1},{1,2},{2,3},{3,0},{4,5},{5,6},{6,7},{7,4},{8,9},{9,10},{10,1... | collective-permute-start | bytes 442376 | tf_op jit(solution)/shard_map/ppermute | solution.py:61
  24.6 8.6 %collective-permute-start.18 = (bf16[192,384]{1,0:T(8,128)(2,1)S(1)}, bf16[192,384]{1,0:T(8,128)(2,1)S(1)}, u32[]{:S(2)}, u32[]{:S(2)}) collective-permute-start(bf16[192,384]{1,0:T(8,128)(2,1)S(1)} %dynamic_slice.153), channel_id=1, source_target_pairs={{0,3},{1,0},{2,1},{3,2},{4,7},{5,4},{6,5},{7,6},{8,11},{9,8},{10,9... | collective-permute-start | bytes 442376 | tf_op jit(solution)/shard_map/ppermute | solution.py:61
  34.8 125.9 %all-gather.16.cloned.1.call-start = ((), (), s32[]{:S(2)}) async-start(), calls=%async_computation.1 | async-start | bytes 5308416 | tf_op jit(solution)/shard_map/all_gather | solution.py:73
  34.9 37.8 %collective-permute-start.1 = (bf16[6,192]{1,0:T(8,128)(2,1)S(1)}, bf16[6,192]{1,0:T(8,128)(2,1)S(1)}, u32[]{:S(2)}, u32[]{:S(2)}) collective-permute-start(bf16[6,192]{1,0:T(8,128)(2,1)S(1)} %get-tuple-element.132), channel_id=1, source_target_pairs={{0,2},{1,3},{2,0},{3,1},{4,6},{5,7},{6,4},{7,5},{8,10},{9,11},{10,... | collective-permute-start | bytes 6920 | tf_op jit(solution)/shard_map/ppermute | solution.py:61
  37.6 36.6 %collective-permute-start = (bf16[6,192]{1,0:T(8,128)(2,1)S(1)}, bf16[6,192]{1,0:T(8,128)(2,1)S(1)}, u32[]{:S(2)}, u32[]{:S(2)}) collective-permute-start(bf16[6,192]{1,0:T(8,128)(2,1)S(1)} %get-tuple-element.132), channel_id=1, source_target_pairs={{0,1},{1,2},{2,3},{3,0},{4,5},{5,6},{6,7},{7,4},{8,9},{9,10},{10,1... | collective-permute-start | bytes 6920 | tf_op jit(solution)/shard_map/ppermute | solution.py:61
  38.5 11.6 %collective-permute-start.4 = (bf16[48,1152]{1,0:T(8,128)(2,1)S(1)}, bf16[48,1152]{1,0:T(8,128)(2,1)S(1)}, u32[]{:S(2)}, u32[]{:S(2)}) collective-permute-start(bf16[48,1152]{1,0:T(8,128)(2,1)S(1)} %dynamic_slice.150), channel_id=1, source_target_pairs={{0,2},{1,3},{2,0},{3,1},{4,6},{5,7},{6,4},{7,5},{8,10},{9,11},{10,... | collective-permute-start | bytes 331784 | tf_op jit(solution)/shard_map/ppermute | solution.py:61
  41.0 11.1 %collective-permute-start.3 = (bf16[48,1152]{1,0:T(8,128)(2,1)S(1)}, bf16[48,1152]{1,0:T(8,128)(2,1)S(1)}, u32[]{:S(2)}, u32[]{:S(2)}) collective-permute-start(bf16[48,1152]{1,0:T(8,128)(2,1)S(1)} %dynamic_slice.150), channel_id=1, source_target_pairs={{0,1},{1,2},{2,3},{3,0},{4,5},{5,6},{6,7},{7,4},{8,9},{9,10},{10,1... | collective-permute-start | bytes 331784 | tf_op jit(solution)/shard_map/ppermute | solution.py:61
  43.0 9.2 %collective-permute-start.5 = (bf16[48,1152]{1,0:T(8,128)(2,1)S(1)}, bf16[48,1152]{1,0:T(8,128)(2,1)S(1)}, u32[]{:S(2)}, u32[]{:S(2)}) collective-permute-start(bf16[48,1152]{1,0:T(8,128)(2,1)S(1)} %dynamic_slice.150), channel_id=1, source_target_pairs={{0,3},{1,0},{2,1},{3,2},{4,7},{5,4},{6,5},{7,6},{8,11},{9,8},{10,9... | collective-permute-start | bytes 331784 | tf_op jit(solution)/shard_map/ppermute | solution.py:61
  50.1 26.4 %collective-permute-start.2 = (bf16[6,192]{1,0:T(8,128)(2,1)S(1)}, bf16[6,192]{1,0:T(8,128)(2,1)S(1)}, u32[]{:S(2)}, u32[]{:S(2)}) collective-permute-start(bf16[6,192]{1,0:T(8,128)(2,1)S(1)} %get-tuple-element.132), channel_id=1, source_target_pairs={{0,3},{1,0},{2,1},{3,2},{4,7},{5,4},{6,5},{7,6},{8,11},{9,8},{10,9... | collective-permute-start | bytes 6920 | tf_op jit(solution)/shard_map/ppermute | solution.py:61
  52.8 14.7 %collective-permute-start.6 = (bf16[4,48,1152]{2,1,0:T(8,128)(2,1)S(1)}, bf16[4,48,1152]{2,1,0:T(8,128)(2,1)S(1)}, u32[]{:S(2)}, u32[]{:S(2)}) collective-permute-start(bf16[4,48,1152]{2,1,0:T(8,128)(2,1)S(1)} %gather_fusion.1), channel_id=1, source_target_pairs={{0,8},{4,12},{8,0},{12,4},{16,24},{20,28},{24,16},{28,20},{1,9},{5... | collective-permute-start | bytes 1327112 | tf_op jit(solution)/shard_map/ppermute | solution.py:43
  54.4 16.9 %collective-permute-start.7 = (bf16[4,48,1152]{2,1,0:T(8,128)(2,1)S(1)}, bf16[4,48,1152]{2,1,0:T(8,128)(2,1)S(1)}, u32[]{:S(2)}, u32[]{:S(2)}) collective-permute-start(bf16[4,48,1152]{2,1,0:T(8,128)(2,1)S(1)} %gather_fusion.1), channel_id=1, source_target_pairs={{0,16},{4,20},{8,24},{12,28},{16,0},{20,4},{24,8},{28,12},{1,17},{... | collective-permute-start | bytes 1327112 | tf_op jit(solution)/shard_map/ppermute | solution.py:44
  67.5 25.1 %collective-permute-start.14 = (bf16[48,1536]{1,0:T(8,128)(2,1)}, bf16[48,1536]{1,0:T(8,128)(2,1)S(1)}, u32[]{:S(2)}, u32[]{:S(2)}) collective-permute-start(bf16[48,1536]{1,0:T(8,128)(2,1)} %dynamic_slice.152), channel_id=1, source_target_pairs={{0,2},{1,3},{2,0},{3,1},{4,6},{5,7},{6,4},{7,5},{8,10},{9,11},{10,... | collective-permute-start | bytes 442376 | tf_op jit(solution)/shard_map/ppermute | solution.py:61
  71.3 15.3 %collective-permute-start.8 = (bf16[4,48,1152]{2,1,0:T(8,128)(2,1)S(1)}, bf16[4,48,1152]{2,1,0:T(8,128)(2,1)S(1)}, u32[]{:S(2)}, u32[]{:S(2)}) collective-permute-start(bf16[4,48,1152]{2,1,0:T(8,128)(2,1)S(1)} %broadcast_select_fusion), channel_id=1, source_target_pairs={{0,8},{4,20},{8,0},{12,28},{16,24},{20,4},{24,16},{28,12},{1,9},{5... | collective-permute-start | bytes 1327112 | tf_op jit(solution)/shard_map/ppermute | solution.py:46
  72.7 19.9 %collective-permute-start.13 = (bf16[48,1536]{1,0:T(8,128)(2,1)}, bf16[48,1536]{1,0:T(8,128)(2,1)}, u32[]{:S(2)}, u32[]{:S(2)}) collective-permute-start(bf16[48,1536]{1,0:T(8,128)(2,1)} %dynamic_slice.152), channel_id=1, source_target_pairs={{0,1},{1,2},{2,3},{3,0},{4,5},{5,6},{6,7},{7,4},{8,9},{9,10},{10,1... | collective-permute-start | bytes 442376 | tf_op jit(solution)/shard_map/ppermute | solution.py:61
  74.2 18.5 %collective-permute-start.15 = (bf16[48,1536]{1,0:T(8,128)(2,1)}, bf16[48,1536]{1,0:T(8,128)(2,1)}, u32[]{:S(2)}, u32[]{:S(2)}) collective-permute-start(bf16[48,1536]{1,0:T(8,128)(2,1)} %dynamic_slice.152), channel_id=1, source_target_pairs={{0,3},{1,0},{2,1},{3,2},{4,7},{5,4},{6,5},{7,6},{8,11},{9,8},{10,9... | collective-permute-start | bytes 442376 | tf_op jit(solution)/shard_map/ppermute | solution.py:61
  88.9 8.8 %collective-permute-start.9 = (bf16[4,4,48,1152]{3,2,1,0:T(8,128)(2,1)}, bf16[4,4,48,1152]{3,2,1,0:T(8,128)(2,1)S(1)}, u32[]{:S(2)}, u32[]{:S(2)}) collective-permute-start(bf16[4,4,48,1152]{3,2,1,0:T(8,128)(2,1)} %pad_maximum_fusion.11), channel_id=1, source_target_pairs={{0,4},{4,0},{8,12},{12,8},{16,20},{20,16},{24,28},{28,24},{1,5},{5... | collective-permute-start | bytes 5308424 | tf_op jit(solution)/shard_map/ppermute | solution.py:50
  95.3 364.7 %all-gather.20.cloned.1.call-start = ((), (), s32[]{:S(2)}) async-start(), calls=%async_computation.3 | async-start | bytes 1990656 | tf_op jit(solution)/shard_map/all_gather | solution.py:136
  264.6 13.2 %collective-permute-start.19 = (bf16[4,4,48,1152]{3,2,1,0:T(8,128)(2,1)}, bf16[4,4,48,1152]{3,2,1,0:T(8,128)(2,1)}, u32[]{:S(2)}, u32[]{:S(2)}) collective-permute-start(bf16[4,4,48,1152]{3,2,1,0:T(8,128)(2,1)} %bitcast.57), channel_id=1, source_target_pairs={{0,4},{4,0},{8,12},{12,8},{16,20},{20,16},{24,28},{28,24},{1,5},{5... | collective-permute-start | bytes 5308424 | tf_op jit(solution)/shard_map/ppermute | solution.py:114
  273.8 18.7 %collective-permute-start.33 = (bf16[4,4,48,1536]{3,2,1,0:T(8,128)(2,1)}, bf16[4,4,48,1536]{3,2,1,0:T(8,128)(2,1)}, u32[]{:S(2)}, u32[]{:S(2)}) collective-permute-start(bf16[4,4,48,1536]{3,2,1,0:T(8,128)(2,1)} %bitcast.87), channel_id=1, source_target_pairs={{0,4},{4,0},{8,12},{12,8},{16,20},{20,16},{24,28},{28,24},{1,5},{5... | collective-permute-start | bytes 7077896 | tf_op jit(solution)/shard_map/ppermute | solution.py:114
  281.5 8.4 %collective-permute-start.20 = (bf16[4,48,1152]{2,1,0:T(8,128)(2,1)S(1)}, bf16[4,48,1152]{2,1,0:T(8,128)(2,1)}, u32[]{:S(2)}, u32[]{:S(2)}) collective-permute-start(bf16[4,48,1152]{2,1,0:T(8,128)(2,1)S(1)} %fusion.59), channel_id=1, source_target_pairs={{0,8},{4,20},{8,0},{12,28},{16,24},{20,4},{24,16},{28,12},{1,9},{5... | collective-permute-start | bytes 1327112 | tf_op jit(solution)/shard_map/ppermute | solution.py:120
  291.2 11.8 %collective-permute-start.21 = (bf16[4,48,1152]{2,1,0:T(8,128)(2,1)S(1)}, bf16[4,48,1152]{2,1,0:T(8,128)(2,1)S(1)}, u32[]{:S(2)}, u32[]{:S(2)}) collective-permute-start(bf16[4,48,1152]{2,1,0:T(8,128)(2,1)S(1)} %get-tuple-element.97), channel_id=1, source_target_pairs={{0,8},{4,12},{8,0},{12,4},{16,24},{20,28},{24,16},{28,20},{1,9},{5... | collective-permute-start | bytes 1327112 | tf_op jit(solution)/shard_map/ppermute | solution.py:127
  291.4 11.7 %collective-permute-start.22 = (bf16[4,48,1152]{2,1,0:T(8,128)(2,1)S(1)}, bf16[4,48,1152]{2,1,0:T(8,128)(2,1)S(1)}, u32[]{:S(2)}, u32[]{:S(2)}) collective-permute-start(bf16[4,48,1152]{2,1,0:T(8,128)(2,1)S(1)} %get-tuple-element.98), channel_id=1, source_target_pairs={{0,16},{4,20},{8,24},{12,28},{16,0},{20,4},{24,8},{28,12},{1,17},{... | collective-permute-start | bytes 1327112 | tf_op jit(solution)/shard_map/ppermute | solution.py:128
  303.2 7.9 %collective-permute-start.23 = (bf16[48,1152]{1,0:T(8,128)(2,1)S(1)}, bf16[48,1152]{1,0:T(8,128)(2,1)S(1)}, u32[]{:S(2)}, u32[]{:S(2)}) collective-permute-start(bf16[48,1152]{1,0:T(8,128)(2,1)S(1)} %get-tuple-element.117), channel_id=1, source_target_pairs={{0,1},{1,2},{2,3},{3,0},{4,5},{5,6},{6,7},{7,4},{8,9},{9,10},{10,1... | collective-permute-start | bytes 331784 | tf_op jit(solution)/shard_map/ppermute | solution.py:133
  305.0 6.2 %collective-permute-start.25 = (bf16[48,1152]{1,0:T(8,128)(2,1)S(1)}, bf16[48,1152]{1,0:T(8,128)(2,1)S(1)}, u32[]{:S(2)}, u32[]{:S(2)}) collective-permute-start(bf16[48,1152]{1,0:T(8,128)(2,1)S(1)} %get-tuple-element.118), channel_id=1, source_target_pairs={{0,3},{1,0},{2,1},{3,2},{4,7},{5,4},{6,5},{7,6},{8,11},{9,8},{10,9... | collective-permute-start | bytes 331784 | tf_op jit(solution)/shard_map/ppermute | solution.py:133
  307.1 8.6 %collective-permute-start.24 = (bf16[48,1152]{1,0:T(8,128)(2,1)S(1)}, bf16[48,1152]{1,0:T(8,128)(2,1)S(1)}, u32[]{:S(2)}, u32[]{:S(2)}) collective-permute-start(bf16[48,1152]{1,0:T(8,128)(2,1)S(1)} %get-tuple-element.119), channel_id=1, source_target_pairs={{0,2},{1,3},{2,0},{3,1},{4,6},{5,7},{6,4},{7,5},{8,10},{9,11},{10,... | collective-permute-start | bytes 331784 | tf_op jit(solution)/shard_map/ppermute | solution.py:133
  308.0 10.1 %collective-permute-start.34 = (bf16[4,48,1536]{2,1,0:T(8,128)(2,1)}, bf16[4,48,1536]{2,1,0:T(8,128)(2,1)S(1)}, u32[]{:S(2)}, u32[]{:S(2)}) collective-permute-start(bf16[4,48,1536]{2,1,0:T(8,128)(2,1)} %fusion.57), channel_id=1, source_target_pairs={{0,8},{4,20},{8,0},{12,28},{16,24},{20,4},{24,16},{28,12},{1,9},{5... | collective-permute-start | bytes 1769480 | tf_op jit(solution)/shard_map/ppermute | solution.py:120
  316.5 146.4 %all-gather.22.cloned.1.call-start = ((), (), s32[]{:S(2)}) async-start(), calls=%async_computation.4 | async-start | bytes 2654208 | tf_op jit(solution)/shard_map/all_gather | solution.py:136
  320.0 15.8 %collective-permute-start.35 = (bf16[4,48,1536]{2,1,0:T(8,128)(2,1)S(1)}, bf16[4,48,1536]{2,1,0:T(8,128)(2,1)S(1)}, u32[]{:S(2)}, u32[]{:S(2)}) collective-permute-start(bf16[4,48,1536]{2,1,0:T(8,128)(2,1)S(1)} %get-tuple-element.89), channel_id=1, source_target_pairs={{0,8},{4,12},{8,0},{12,4},{16,24},{20,28},{24,16},{28,20},{1,9},{5... | collective-permute-start | bytes 1769480 | tf_op jit(solution)/shard_map/ppermute | solution.py:127
  321.8 14.9 %collective-permute-start.36 = (bf16[4,48,1536]{2,1,0:T(8,128)(2,1)S(1)}, bf16[4,48,1536]{2,1,0:T(8,128)(2,1)S(1)}, u32[]{:S(2)}, u32[]{:S(2)}) collective-permute-start(bf16[4,48,1536]{2,1,0:T(8,128)(2,1)S(1)} %get-tuple-element.90), channel_id=1, source_target_pairs={{0,16},{4,20},{8,24},{12,28},{16,0},{20,4},{24,8},{28,12},{1,17},{... | collective-permute-start | bytes 1769480 | tf_op jit(solution)/shard_map/ppermute | solution.py:128
  333.4 32.4 %collective-permute-start.40 = (bf16[4,4,192,384]{3,2,1,0:T(8,128)(2,1)}, bf16[4,4,192,384]{3,2,1,0:T(8,128)(2,1)}, u32[]{:S(2)}, u32[]{:S(2)}) collective-permute-start(bf16[4,4,192,384]{3,2,1,0:T(8,128)(2,1)} %bitcast.100), channel_id=1, source_target_pairs={{0,4},{4,0},{8,12},{12,8},{16,20},{20,16},{24,28},{28,24},{1,5},{5... | collective-permute-start | bytes 7077896 | tf_op jit(solution)/shard_map/ppermute | solution.py:114
  339.8 8.4 %collective-permute-start.37 = (bf16[48,1536]{1,0:T(8,128)(2,1)}, bf16[48,1536]{1,0:T(8,128)(2,1)S(1)}, u32[]{:S(2)}, u32[]{:S(2)}) collective-permute-start(bf16[48,1536]{1,0:T(8,128)(2,1)} %get-tuple-element.112), channel_id=1, source_target_pairs={{0,1},{1,2},{2,3},{3,0},{4,5},{5,6},{6,7},{7,4},{8,9},{9,10},{10,1... | collective-permute-start | bytes 442376 | tf_op jit(solution)/shard_map/ppermute | solution.py:133
  339.9 8.2 %collective-permute-start.39 = (bf16[48,1536]{1,0:T(8,128)(2,1)S(1)}, bf16[48,1536]{1,0:T(8,128)(2,1)S(1)}, u32[]{:S(2)}, u32[]{:S(2)}) collective-permute-start(bf16[48,1536]{1,0:T(8,128)(2,1)S(1)} %get-tuple-element.113), channel_id=1, source_target_pairs={{0,3},{1,0},{2,1},{3,2},{4,7},{5,4},{6,5},{7,6},{8,11},{9,8},{10,9... | collective-permute-start | bytes 442376 | tf_op jit(solution)/shard_map/ppermute | solution.py:133
  343.6 10.6 %collective-permute-start.38 = (bf16[48,1536]{1,0:T(8,128)(2,1)S(1)}, bf16[48,1536]{1,0:T(8,128)(2,1)S(1)}, u32[]{:S(2)}, u32[]{:S(2)}) collective-permute-start(bf16[48,1536]{1,0:T(8,128)(2,1)S(1)} %get-tuple-element.114), channel_id=1, source_target_pairs={{0,2},{1,3},{2,0},{3,1},{4,6},{5,7},{6,4},{7,5},{8,10},{9,11},{10,... | collective-permute-start | bytes 442376 | tf_op jit(solution)/shard_map/ppermute | solution.py:133
  356.0 108.7 %all-gather.24.cloned.1.call-start = ((), (), s32[]{:S(2)}) async-start(), calls=%async_computation.5 | async-start | bytes 2654208 | tf_op jit(solution)/shard_map/all_gather | solution.py:136
  370.5 16.4 %collective-permute-start.41 = (bf16[4,192,384]{2,1,0:T(8,128)(2,1)S(1)}, bf16[4,192,384]{2,1,0:T(8,128)(2,1)}, u32[]{:S(2)}, u32[]{:S(2)}) collective-permute-start(bf16[4,192,384]{2,1,0:T(8,128)(2,1)S(1)} %fusion.58), channel_id=1, source_target_pairs={{0,8},{4,20},{8,0},{12,28},{16,24},{20,4},{24,16},{28,12},{1,9},{5... | collective-permute-start | bytes 1769480 | tf_op jit(solution)/shard_map/ppermute | solution.py:120
  389.8 12.3 %collective-permute-start.42 = (bf16[4,192,384]{2,1,0:T(8,128)(2,1)}, bf16[4,192,384]{2,1,0:T(8,128)(2,1)}, u32[]{:S(2)}, u32[]{:S(2)}) collective-permute-start(bf16[4,192,384]{2,1,0:T(8,128)(2,1)} %get-tuple-element.87), channel_id=1, source_target_pairs={{0,8},{4,12},{8,0},{12,4},{16,24},{20,28},{24,16},{28,20},{1,9},{5... | collective-permute-start | bytes 1769480 | tf_op jit(solution)/shard_map/ppermute | solution.py:127
  390.5 11.6 %collective-permute-start.43 = (bf16[4,192,384]{2,1,0:T(8,128)(2,1)S(1)}, bf16[4,192,384]{2,1,0:T(8,128)(2,1)}, u32[]{:S(2)}, u32[]{:S(2)}) collective-permute-start(bf16[4,192,384]{2,1,0:T(8,128)(2,1)S(1)} %get-tuple-element.88), channel_id=1, source_target_pairs={{0,16},{4,20},{8,24},{12,28},{16,0},{20,4},{24,8},{28,12},{1,17},{... | collective-permute-start | bytes 1769480 | tf_op jit(solution)/shard_map/ppermute | solution.py:128
  396.4 11.6 %collective-permute-start.26 = (bf16[4,4,48,512]{3,2,1,0:T(8,128)(2,1)}, bf16[4,4,48,512]{3,2,1,0:T(8,128)(2,1)}, u32[]{:S(2)}, u32[]{:S(2)}) collective-permute-start(bf16[4,4,48,512]{3,2,1,0:T(8,128)(2,1)} %bitcast.298), channel_id=1, source_target_pairs={{0,4},{4,0},{8,12},{12,8},{16,20},{20,16},{24,28},{28,24},{1,5},{5... | collective-permute-start | bytes 2359304 | tf_op jit(solution)/shard_map/ppermute | solution.py:114
  404.1 8.6 %collective-permute-start.44 = (bf16[192,384]{1,0:T(8,128)(2,1)S(1)}, bf16[192,384]{1,0:T(8,128)(2,1)S(1)}, u32[]{:S(2)}, u32[]{:S(2)}) collective-permute-start(bf16[192,384]{1,0:T(8,128)(2,1)S(1)} %get-tuple-element.109), channel_id=1, source_target_pairs={{0,1},{1,2},{2,3},{3,0},{4,5},{5,6},{6,7},{7,4},{8,9},{9,10},{10,1... | collective-permute-start | bytes 442376 | tf_op jit(solution)/shard_map/ppermute | solution.py:133
  404.2 9.5 %collective-permute-start.46 = (bf16[192,384]{1,0:T(8,128)(2,1)S(1)}, bf16[192,384]{1,0:T(8,128)(2,1)S(1)}, u32[]{:S(2)}, u32[]{:S(2)}) collective-permute-start(bf16[192,384]{1,0:T(8,128)(2,1)S(1)} %get-tuple-element.110), channel_id=1, source_target_pairs={{0,3},{1,0},{2,1},{3,2},{4,7},{5,4},{6,5},{7,6},{8,11},{9,8},{10,9... | collective-permute-start | bytes 442376 | tf_op jit(solution)/shard_map/ppermute | solution.py:133
  408.0 12.6 %collective-permute-start.45 = (bf16[192,384]{1,0:T(8,128)(2,1)S(1)}, bf16[192,384]{1,0:T(8,128)(2,1)S(1)}, u32[]{:S(2)}, u32[]{:S(2)}) collective-permute-start(bf16[192,384]{1,0:T(8,128)(2,1)S(1)} %get-tuple-element.111), channel_id=1, source_target_pairs={{0,2},{1,3},{2,0},{3,1},{4,6},{5,7},{6,4},{7,5},{8,10},{9,11},{10,... | collective-permute-start | bytes 442376 | tf_op jit(solution)/shard_map/ppermute | solution.py:133
  410.6 18.2 %collective-permute-start.27 = (bf16[4,48,512]{2,1,0:T(8,128)(2,1)S(1)}, bf16[4,48,512]{2,1,0:T(8,128)(2,1)S(1)}, u32[]{:S(2)}, u32[]{:S(2)}) collective-permute-start(bf16[4,48,512]{2,1,0:T(8,128)(2,1)S(1)} %fusion.76), channel_id=1, source_target_pairs={{0,8},{4,20},{8,0},{12,28},{16,24},{20,4},{24,16},{28,12},{1,9},{5... | collective-permute-start | bytes 589832 | tf_op jit(solution)/shard_map/ppermute | solution.py:120
  429.0 8.4 %collective-permute-start.28 = (bf16[4,48,512]{2,1,0:T(8,128)(2,1)S(1)}, bf16[4,48,512]{2,1,0:T(8,128)(2,1)S(1)}, u32[]{:S(2)}, u32[]{:S(2)}) collective-permute-start(bf16[4,48,512]{2,1,0:T(8,128)(2,1)S(1)} %get-tuple-element.105), channel_id=1, source_target_pairs={{0,8},{4,12},{8,0},{12,4},{16,24},{20,28},{24,16},{28,20},{1,9},{5... | collective-permute-start | bytes 589832 | tf_op jit(solution)/shard_map/ppermute | solution.py:127
  430.6 6.9 %collective-permute-start.29 = (bf16[4,48,512]{2,1,0:T(8,128)(2,1)S(1)}, bf16[4,48,512]{2,1,0:T(8,128)(2,1)S(1)}, u32[]{:S(2)}, u32[]{:S(2)}) collective-permute-start(bf16[4,48,512]{2,1,0:T(8,128)(2,1)S(1)} %get-tuple-element.106), channel_id=1, source_target_pairs={{0,16},{4,20},{8,24},{12,28},{16,0},{20,4},{24,8},{28,12},{1,17},{... | collective-permute-start | bytes 589832 | tf_op jit(solution)/shard_map/ppermute | solution.py:128
  (82 other events, 723.1 us)
Sparse Core Ops, SparseCore 0:
  19.5 25.1 all-gather.13
  47.2 46.6 all-gather.17
  96.4 37.2 all-gather.15
  316.6 27.7 all-gather.19
  356.1 30.2 all-gather.21
  421.6 30.2 all-gather.23
